TPU v7x, 512 devices: a whole 4x8x8 slice. The times are simulated.
512 devices in a mesh: segment: 8 (over z), gy: 64 (over x, y, core).
Axes of the slice: x: 4, y: 8, z: 8, core: 2. Of those that a mesh axis runs over, the one named last changes fastest.
Arguments:
- acts: bfloat16 [8, 8, 128, 32, 256], P('segment', None, 'gy'), may hold values from -6 to 6
- grad_out: bfloat16 [8, 128, 32, 256], P('segment', 'gy'), may hold values from -6 to 6
- w_plane: bfloat16 [8, 3, 3, 32, 32], P('segment'), may hold values from -0.375 to 0.375
- w_depth: bfloat16 [8, 3, 32, 32], P('segment'), may hold values from -0.625 to 0.625
- tiles: int32 [64, 12], P('gy'), may hold values from -1 to 15, as said below
Outputs:
- grad_in: bfloat16 [8, 128, 32, 256], P('segment', 'gy')
- grad_plane: float32 [8, 3, 3, 32, 32], P('segment')
- grad_depth: float32 [8, 3, 32, 32], P('segment')
Inputs may be any that keep to these rules, and one draw needn't show every extreme that they name: Row s lists distinct tiles z * 2 + x-tile of slab s in its first entries and -1 after them; each row lists 1 to 12 tiles, and some row lists exactly 12.
All inputs are finite; a program needn't handle non-finite values.
Results may differ from a plain program's by a relative error of at most 0.02.
Values may be sent and summed in bfloat16 or wider, within the bound.
No kernel may reach another device: no remote copies, remote signals or barrier semaphores. Data moves between devices by JAX's collectives and lax.ppermute only.
A program may use at most 64 MiB of HBM per device.

v0:
```python
import math

import jax
import jax.numpy as jnp
from jax import lax
from jax.sharding import PartitionSpec as P

TILE = 128


def padded_2(block, sides, width):
    for axis, dim in sides:
        count = lax.axis_size(axis)
        forward = [(i, i + 1) for i in range(count - 1)]
        backward = [(target, source) for source, target in forward]
        low = lax.ppermute(
            lax.slice_in_dim(block, block.shape[dim] - width, None, axis=dim), axis, forward
        )
        high = lax.ppermute(lax.slice_in_dim(block, 0, width, axis=dim), axis, backward)
        block = jnp.concatenate([low, block, high], axis=dim)
    return block


def passed_along(block, axis, distance):
    devices = range(lax.axis_size(axis))
    route = [(i - distance, i) for i in devices if i - distance in devices]
    return lax.ppermute(block, axis, route)


def spread(value, axis, root):
    mine = lax.axis_index(axis) == root
    return lax.psum(jnp.where(mine, value, jnp.zeros_like(value)), axis)


def width_pad(field):
    return jnp.pad(field, [(0, 0)] * (field.ndim - 1) + [(1, 1)])


def depth_pad(field):
    return jnp.pad(field, [(1, 1)] + [(0, 0)] * (field.ndim - 1))


def plane_conv(rows_in, kernel, height, width):
    padded = width_pad(rows_in)
    total = None
    for i in range(3):
        for j in range(3):
            term = jnp.einsum(
                "oc,...ycx->...yox",
                kernel[i, j],
                padded[..., i : i + height, :, j : j + width],
                preferred_element_type=jnp.float32,
            )
            total = term if total is None else total + term
    return total


def plane_back(rows_grad, kernel, height, width):
    padded = width_pad(rows_grad)
    total = None
    for i in range(3):
        for j in range(3):
            term = jnp.einsum(
                "oc,...yox->...ycx",
                kernel[i, j],
                padded[..., 2 - i : 2 - i + height, :, 2 - j : 2 - j + width],
                preferred_element_type=jnp.float32,
            )
            total = term if total is None else total + term
    return total


def plane_taps(grad_mid, rows_in, height, width):
    padded = width_pad(rows_in)
    rows_out = []
    for i in range(3):
        row_taps = []
        for j in range(3):
            row_taps.append(
                jnp.einsum(
                    "...yox,...ycx->oc",
                    grad_mid,
                    padded[..., i : i + height, :, j : j + width],
                    preferred_element_type=jnp.float32,
                )
            )
        rows_out.append(jnp.stack(row_taps))
    return jnp.stack(rows_out)


def depth_conv(deep, kernel, depth):
    total = None
    for k in range(3):
        term = jnp.einsum(
            "oc,zycx->zyox", kernel[k], deep[k : k + depth], preferred_element_type=jnp.float32
        )
        total = term if total is None else total + term
    return total


def depth_back(mix_deep, kernel, depth):
    total = None
    for k in range(3):
        term = jnp.einsum(
            "oc,zyox->zycx",
            kernel[k],
            mix_deep[2 - k : 2 - k + depth],
            preferred_element_type=jnp.float32,
        )
        total = term if total is None else total + term
    return total


def depth_taps(grad_mix, deep, depth):
    return jnp.stack(
        [
            jnp.einsum(
                "zyox,zycx->oc", grad_mix, deep[k : k + depth], preferred_element_type=jnp.float32
            )
            for k in range(3)
        ]
    )


def silu_slope(value):
    sig = jax.nn.sigmoid(value)
    return sig * (1.0 + value * (1.0 - sig))


def local(acts, grad_out, w_plane, w_depth, tiles):
    sections = acts.shape[1]
    height = acts.shape[2]
    width = acts.shape[4]
    chans = w_plane.shape[3]
    tile_total = sections * (width // TILE)
    scale = 1.0 / math.sqrt(sections * height * lax.axis_size("gy") * width)
    segment = lax.axis_index("segment")
    hit = jnp.any(tiles[0][:, None] == jnp.arange(tile_total, dtype=jnp.int32)[None, :], axis=0)
    mask_full = jnp.repeat(hit.astype(jnp.float32).reshape(sections, width // TILE), TILE, axis=1)[
        :, None, None, :
    ]
    count = lax.axis_size("segment")
    seed = lax.all_gather(grad_out, "segment", axis=0, tiled=True)
    rows_own = padded_2(acts[0], (("gy", 1),), 1)

    def front(grad):
        mid = plane_conv(rows_own, w_plane[0], height, width).astype(jnp.bfloat16)
        deep = depth_pad(mid)
        value = depth_conv(deep, w_depth[0], sections)
        grad_mix = (grad.astype(jnp.float32) * mask_full * silu_slope(value)).astype(jnp.bfloat16)
        grad_mid = depth_back(depth_pad(grad_mix), w_depth[0], sections).astype(jnp.bfloat16)
        depth_grad = depth_taps(grad_mix, deep, sections) * scale
        return (grad_mid, depth_grad)

    def front_skip(grad):
        return (jnp.zeros(grad.shape, jnp.bfloat16), jnp.zeros((3, chans, chans), jnp.float32))

    def rear(operands):
        grad, grad_mid, rows_grad = operands
        fresh = (
            grad.astype(jnp.float32) + plane_back(rows_grad, w_plane[0], height, width)
        ).astype(jnp.bfloat16)
        plane_grad = plane_taps(grad_mid, rows_own, height, width) * scale
        return (fresh, plane_grad)

    def rear_skip(operands):
        return (operands[0], jnp.zeros((3, 3, chans, chans), jnp.float32))

    def backward(keep, grad):
        grad_mid, depth_grad = lax.cond(keep, front, front_skip, grad)
        rows_grad = padded_2(grad_mid, (("gy", 1),), 1)
        fresh, plane_grad = lax.cond(keep, rear, rear_skip, (grad, grad_mid, rows_grad))
        return (fresh, plane_grad, depth_grad)

    def turn(index, carry):
        grad, plane_sum, depth_sum = carry
        keep = segment == count - 1 - index
        fresh, plane_grad, depth_grad = backward(keep, grad)
        plane_sum = jnp.where(keep, plane_grad, plane_sum)
        depth_sum = jnp.where(keep, depth_grad, depth_sum)
        passed = passed_along(fresh, "segment", -1)
        return (passed, plane_sum, depth_sum)

    start = (
        seed,
        jnp.zeros((3, 3, chans, chans), jnp.float32),
        jnp.zeros((3, chans, chans), jnp.float32),
    )
    grad, plane_sum, depth_sum = lax.fori_loop(0, count - 1, turn, start)
    first = segment == 0
    fresh, plane_grad, depth_grad = backward(first, grad)
    plane_sum = jnp.where(first, plane_grad, plane_sum)
    depth_sum = jnp.where(first, depth_grad, depth_sum)
    whole = spread(fresh, "segment", 0)
    planes = grad_out.shape[0]
    grad_in = lax.dynamic_slice_in_dim(whole, segment * planes, planes, 0)
    plane_sum, depth_sum = lax.psum((plane_sum, depth_sum), "gy")
    return (grad_in, plane_sum[None], depth_sum[None])


def solution(mesh):
    placed = (
        P("segment", None, "gy", None, None),
        P("segment", "gy", None, None),
        P("segment", None, None, None, None),
        P("segment", None, None, None),
        P("gy", None),
    )
    return jax.shard_map(
        local,
        mesh=mesh,
        in_specs=placed,
        out_specs=(
            P("segment", "gy", None, None),
            P("segment", None, None, None, None),
            P("segment", None, None, None),
        ),
        check_vma=False,
    )
```

profile of v0, /device:TPU:1, one launch (start us, length us, event | category | flops | bytes accessed | tf_op | source)
XLA Modules:
  0.0 510.5 jit_solution(11133507370020270652)
XLA Ops:
  7.2 1.0 fusion.119
  8.3 4.7 collective-permute-start.3
  13.0 5.5 %collective-permute-start.4 = (bf16[8,1,32,256]{3,2,1,0:T(8,128)(2,1)S(1)}, bf16[8,1,32,256]{3,2,1,0:T(8,128)(2,1)S(1)}, u32[]{:S(2)}, u32[]{:S(2)}) collective-permute-start(bf16[8,1,32,256]{3,2,1,0:T(8,128)(2,1)S(1)} %get-tuple-element.383), channel_id=1, source_target_pairs={{1,0},{2,1},{3,2},{4,3},{5,4},{6,5},{7,6},{8,7},{9,8},{10,9},{11,1... | collective-permute-start | bytes 393224 | tf_op jit(solution)/shard_map/ppermute | solution.py:19
  19.0 21.5 %all_gather.3 = bf16[8,2,32,256]{3,2,1,0:T(8,128)(2,1)S(1)} all-gather(bf16[1,2,32,256]{3,2,1,0:T(8,128)(2,1)S(1)} %copy-done.3), channel_id=1, replica_groups=mesh['segment'=8,'gy'=64] {'segment'}, dimensions={0}, use_global_device_ids=true | all-gather | bytes 294912 | tf_op jit(solution)/shard_map/all_gather | solution.py:143
  41.2 194.3 %while.24 = (s32[]{:T(128)}, bf16[8,2,32,256]{3,2,1,0:T(8,128)(2,1)S(1)}, f32[3,3,32,32]{2,3,1,0:T(8,128)S(1)}, f32[3,32,32]{2,1,0:T(8,128)S(1)}, s32[]{:T(128)}...) while((s32[]{:T(128)}, ...), condition=%wide.region_6.7_spmd.clone, body=%wide.region_1.6_spmd.clone.sunk | while | flops 305215488 | bytes 45445568 | solution.py:189
  41.4 6.0 %collective-permute-start = (bf16[8,1,32,256]{3,2,1,0:T(8,128)(2,1)S(1)}, bf16[8,1,32,256]{3,2,1,0:T(8,128)(2,1)S(1)}, u32[]{:S(2)}, u32[]{:S(2)}) collective-permute-start(bf16[8,1,32,256]{3,2,1,0:T(8,128)(2,1)S(1)} %get-tuple-element.446), channel_id=1, source_target_pairs={{1,0},{2,1},{3,2},{4,3},{5,4},{6,5},{7,6},{8,7},{9,8},{10,9},{11,1... | collective-permute-start | bytes 393224 | tf_op jit(solution)/shard_map/while/body/eval_jaxpr/ppermute | solution.py:19
  47.4 5.6 %collective-permute-start.1 = (bf16[8,1,32,256]{3,2,1,0:T(8,128)(2,1)S(1)}, bf16[8,1,32,256]{3,2,1,0:T(8,128)(2,1)S(1)}, u32[]{:S(2)}, u32[]{:S(2)}) collective-permute-start(bf16[8,1,32,256]{3,2,1,0:T(8,128)(2,1)S(1)} %get-tuple-element.447), channel_id=1, source_target_pairs={{0,1},{1,2},{2,3},{3,4},{4,5},{5,6},{6,7},{7,8},{8,9},{9,10},{10,1... | collective-permute-start | bytes 393224 | tf_op jit(solution)/shard_map/while/body/eval_jaxpr/ppermute | solution.py:16
  53.8 1.2 collective-permute-done.1
  55.1 1.3 collective-permute-start.2
  56.5 5.7 %collective-permute-done.2 = bf16[8,2,32,256]{3,2,1,0:T(8,128)(2,1)S(1)} collective-permute-done((bf16[8,2,32,256]{3,2,1,0:T(8,128)(2,1)S(1)}, bf16[8,2,32,256]{3,2,1,0:T(8,128)(2,1)S(1)}, u32[]{:S(2)}, u32[]{:S(2)}) %collective-permute-start.2) | collective-permute-done | bytes 262176 | tf_op jit(solution)/shard_map/while/body/eval_jaxpr/ppermute | solution.py:27
  62.4 1.9 collective-permute-start
  64.3 6.6 %collective-permute-start.1 = (bf16[8,1,32,256]{3,2,1,0:T(8,128)(2,1)S(1)}, bf16[8,1,32,256]{3,2,1,0:T(8,128)(2,1)S(1)}, u32[]{:S(2)}, u32[]{:S(2)}) collective-permute-start(bf16[8,1,32,256]{3,2,1,0:T(8,128)(2,1)S(1)} %get-tuple-element.447), channel_id=1, source_target_pairs={{0,1},{1,2},{2,3},{3,4},{4,5},{5,6},{6,7},{7,8},{8,9},{9,10},{10,1... | collective-permute-start | bytes 393224 | tf_op jit(solution)/shard_map/while/body/eval_jaxpr/ppermute | solution.py:16
  71.6 1.2 collective-permute-done.1
  72.9 1.3 collective-permute-start.2
  74.3 5.7 %collective-permute-done.2 = bf16[8,2,32,256]{3,2,1,0:T(8,128)(2,1)S(1)} collective-permute-done((bf16[8,2,32,256]{3,2,1,0:T(8,128)(2,1)S(1)}, bf16[8,2,32,256]{3,2,1,0:T(8,128)(2,1)S(1)}, u32[]{:S(2)}, u32[]{:S(2)}) %collective-permute-start.2) | collective-permute-done | bytes 262176 | tf_op jit(solution)/shard_map/while/body/eval_jaxpr/ppermute | solution.py:27
  80.2 1.9 collective-permute-start
  82.2 6.6 %collective-permute-start.1 = (bf16[8,1,32,256]{3,2,1,0:T(8,128)(2,1)S(1)}, bf16[8,1,32,256]{3,2,1,0:T(8,128)(2,1)S(1)}, u32[]{:S(2)}, u32[]{:S(2)}) collective-permute-start(bf16[8,1,32,256]{3,2,1,0:T(8,128)(2,1)S(1)} %get-tuple-element.447), channel_id=1, source_target_pairs={{0,1},{1,2},{2,3},{3,4},{4,5},{5,6},{6,7},{7,8},{8,9},{9,10},{10,1... | collective-permute-start | bytes 393224 | tf_op jit(solution)/shard_map/while/body/eval_jaxpr/ppermute | solution.py:16
  89.5 1.2 collective-permute-done.1
  90.8 1.3 collective-permute-start.2
  92.2 5.7 %collective-permute-done.2 = bf16[8,2,32,256]{3,2,1,0:T(8,128)(2,1)S(1)} collective-permute-done((bf16[8,2,32,256]{3,2,1,0:T(8,128)(2,1)S(1)}, bf16[8,2,32,256]{3,2,1,0:T(8,128)(2,1)S(1)}, u32[]{:S(2)}, u32[]{:S(2)}) %collective-permute-start.2) | collective-permute-done | bytes 262176 | tf_op jit(solution)/shard_map/while/body/eval_jaxpr/ppermute | solution.py:27
  98.1 1.9 collective-permute-start
  100.0 7.7 %collective-permute-start.1 = (bf16[8,1,32,256]{3,2,1,0:T(8,128)(2,1)S(1)}, bf16[8,1,32,256]{3,2,1,0:T(8,128)(2,1)S(1)}, u32[]{:S(2)}, u32[]{:S(2)}) collective-permute-start(bf16[8,1,32,256]{3,2,1,0:T(8,128)(2,1)S(1)} %get-tuple-element.447), channel_id=1, source_target_pairs={{0,1},{1,2},{2,3},{3,4},{4,5},{5,6},{6,7},{7,8},{8,9},{9,10},{10,1... | collective-permute-start | bytes 393224 | tf_op jit(solution)/shard_map/while/body/eval_jaxpr/ppermute | solution.py:16
  107.7 1.0 collective-permute-done
  108.7 0.9 collective-permute-done.1
  109.7 1.3 collective-permute-start.2
  111.1 5.7 %collective-permute-done.2 = bf16[8,2,32,256]{3,2,1,0:T(8,128)(2,1)S(1)} collective-permute-done((bf16[8,2,32,256]{3,2,1,0:T(8,128)(2,1)S(1)}, bf16[8,2,32,256]{3,2,1,0:T(8,128)(2,1)S(1)}, u32[]{:S(2)}, u32[]{:S(2)}) %collective-permute-start.2) | collective-permute-done | bytes 262176 | tf_op jit(solution)/shard_map/while/body/eval_jaxpr/ppermute | solution.py:27
  117.0 1.9 collective-permute-start
  119.0 8.3 %collective-permute-start.1 = (bf16[8,1,32,256]{3,2,1,0:T(8,128)(2,1)S(1)}, bf16[8,1,32,256]{3,2,1,0:T(8,128)(2,1)S(1)}, u32[]{:S(2)}, u32[]{:S(2)}) collective-permute-start(bf16[8,1,32,256]{3,2,1,0:T(8,128)(2,1)S(1)} %get-tuple-element.447), channel_id=1, source_target_pairs={{0,1},{1,2},{2,3},{3,4},{4,5},{5,6},{6,7},{7,8},{8,9},{9,10},{10,1... | collective-permute-start | bytes 393224 | tf_op jit(solution)/shard_map/while/body/eval_jaxpr/ppermute | solution.py:16
  127.3 1.0 collective-permute-done
  129.3 1.3 collective-permute-start.2
  130.7 5.7 %collective-permute-done.2 = bf16[8,2,32,256]{3,2,1,0:T(8,128)(2,1)S(1)} collective-permute-done((bf16[8,2,32,256]{3,2,1,0:T(8,128)(2,1)S(1)}, bf16[8,2,32,256]{3,2,1,0:T(8,128)(2,1)S(1)}, u32[]{:S(2)}, u32[]{:S(2)}) %collective-permute-start.2) | collective-permute-done | bytes 262176 | tf_op jit(solution)/shard_map/while/body/eval_jaxpr/ppermute | solution.py:27
  136.6 1.9 collective-permute-start
  138.5 8.0 %collective-permute-start.1 = (bf16[8,1,32,256]{3,2,1,0:T(8,128)(2,1)S(1)}, bf16[8,1,32,256]{3,2,1,0:T(8,128)(2,1)S(1)}, u32[]{:S(2)}, u32[]{:S(2)}) collective-permute-start(bf16[8,1,32,256]{3,2,1,0:T(8,128)(2,1)S(1)} %get-tuple-element.447), channel_id=1, source_target_pairs={{0,1},{1,2},{2,3},{3,4},{4,5},{5,6},{6,7},{7,8},{8,9},{9,10},{10,1... | collective-permute-start | bytes 393224 | tf_op jit(solution)/shard_map/while/body/eval_jaxpr/ppermute | solution.py:16
  146.5 1.0 collective-permute-done
  148.5 1.3 collective-permute-start.2
  149.9 5.9 %collective-permute-done.2 = bf16[8,2,32,256]{3,2,1,0:T(8,128)(2,1)S(1)} collective-permute-done((bf16[8,2,32,256]{3,2,1,0:T(8,128)(2,1)S(1)}, bf16[8,2,32,256]{3,2,1,0:T(8,128)(2,1)S(1)}, u32[]{:S(2)}, u32[]{:S(2)}) %collective-permute-start.2) | collective-permute-done | bytes 262176 | tf_op jit(solution)/shard_map/while/body/eval_jaxpr/ppermute | solution.py:27
  156.0 1.9 collective-permute-start
  157.9 7.9 %collective-permute-start.1 = (bf16[8,1,32,256]{3,2,1,0:T(8,128)(2,1)S(1)}, bf16[8,1,32,256]{3,2,1,0:T(8,128)(2,1)S(1)}, u32[]{:S(2)}, u32[]{:S(2)}) collective-permute-start(bf16[8,1,32,256]{3,2,1,0:T(8,128)(2,1)S(1)} %get-tuple-element.447), channel_id=1, source_target_pairs={{0,1},{1,2},{2,3},{3,4},{4,5},{5,6},{6,7},{7,8},{8,9},{9,10},{10,1... | collective-permute-start | bytes 393224 | tf_op jit(solution)/shard_map/while/body/eval_jaxpr/ppermute | solution.py:16
  166.5 1.2 collective-permute-done.1
  167.8 1.3 collective-permute-start.2
  169.2 66.4 %collective-permute-done.2 = bf16[8,2,32,256]{3,2,1,0:T(8,128)(2,1)S(1)} collective-permute-done((bf16[8,2,32,256]{3,2,1,0:T(8,128)(2,1)S(1)}, bf16[8,2,32,256]{3,2,1,0:T(8,128)(2,1)S(1)}, u32[]{:S(2)}, u32[]{:S(2)}) %collective-permute-start.2) | collective-permute-done | bytes 262176 | tf_op jit(solution)/shard_map/while/body/eval_jaxpr/ppermute | solution.py:27
  235.6 4.7 conditional.4
  240.3 7.9 %collective-permute-start.5 = (bf16[8,1,32,256]{3,2,1,0:T(8,128)(2,1)S(1)}, bf16[8,1,32,256]{3,2,1,0:T(8,128)(2,1)S(1)}, u32[]{:S(2)}, u32[]{:S(2)}) collective-permute-start(bf16[8,1,32,256]{3,2,1,0:T(8,128)(2,1)S(1)} %get-tuple-element.380), channel_id=1, source_target_pairs={{0,1},{1,2},{2,3},{3,4},{4,5},{5,6},{6,7},{7,8},{8,9},{9,10},{10,1... | collective-permute-start | bytes 393224 | tf_op jit(solution)/shard_map/ppermute | solution.py:16
  248.1 1.9 collective-permute-start.6
  250.1 4.3 collective-permute-done.6
  254.5 5.2 %conditional.5 = (bf16[8,2,32,256]{3,2,1,0:T(8,128)(2,1)S(1)}, f32[3,3,32,32]{3,2,1,0:T(8,128)S(1)}) conditional(s32[]{:T(128)} %convert_element_type.73, bf16[8,2,32,256]{3,2,1,0:T(8,128)(2,1)S(1)} %get-tuple-element.229, (bf16[8,2,32,256]{3,2,1,0:T(8,128)(2,1)S(1)}, bf16[8,4,32,256]{3,2,1,0:T(8,128)(2,1)S(1)}, ...), branch_computations={%region_9.10_spmd, %region_10.11_spmd} | conditional | flops 152482816 | bytes 19505168 | solution.py:172
  260.6 241.7 %all-reduce.10 = (f32[1,3,3,32,32]{4,3,2,1,0:T(8,128)}, f32[1,3,32,32]{3,2,1,0:T(8,128)}) all-reduce(f32[1,3,3,32,32]{4,3,2,1,0:T(8,128)S(1)} %select_bitcast_fusion, f32[1,3,32,32]{3,2,1,0:T(8,128)S(1)} %select_bitcast_fusion.1), channel_id=1, replica_groups=mesh['segment'=8,'gy'=64] {'gy'}, use_global_device_ids=true, to_apply=%region_12.13 | all-reduce | flops 12288 | bytes 98304 | tf_op jit(solution)/shard_map/psum | solution.py:197
  502.3 1.4 constant_dynamic-slice_fusion
  (157 shorter events, 18.7 us)
Async XLA Ops:
  7.2 495.1 %all-reduce.13.cloned.1.call-start = ((), (), s32[]{:S(2)}) async-start(), calls=%async_computation | async-start | bytes 524288 | tf_op jit(solution)/shard_map/psum | solution.py:32
  7.2 11.3 %copy-start.4 = (s32[1,12]{1,0:T(1,128)S(1)}, s32[1,12]{1,0:T(1,128)}, u32[]{:S(2)}) copy-start(s32[1,12]{1,0:T(1,128)} %param.19) | copy-start | bytes 148
  7.2 11.6 %copy-start.2 = (bf16[1,3,3,32,32]{4,3,2,1,0:T(8,128)(2,1)S(1)}, bf16[1,3,3,32,32]{4,3,2,1,0:T(8,128)(2,1)}, u32[]{:S(2)}) copy-start(bf16[1,3,3,32,32]{4,3,2,1,0:T(8,128)(2,1)} %param.17) | copy-start | bytes 55300
  7.2 11.8 %copy-start.3 = (bf16[1,2,32,256]{3,2,1,0:T(8,128)(2,1)S(1)}, bf16[1,2,32,256]{3,2,1,0:T(8,128)(2,1)}, u32[]{:S(2)}) copy-start(bf16[1,2,32,256]{3,2,1,0:T(8,128)(2,1)} %param.16) | copy-start | bytes 98308
  8.3 32.2 %copy-start.1 = (bf16[1,8,2,32,256]{4,3,2,1,0:T(8,128)(2,1)S(1)}, bf16[1,8,2,32,256]{4,3,2,1,0:T(8,128)(2,1)}, u32[]{:S(2)}) copy-start(bf16[1,8,2,32,256]{4,3,2,1,0:T(8,128)(2,1)} %param.15) | copy-start | bytes 786436
  8.3 32.2 %collective-permute-start.3 = (bf16[8,1,32,256]{3,2,1,0:T(8,128)(2,1)S(1)}, bf16[8,1,32,256]{3,2,1,0:T(8,128)(2,1)S(1)}, u32[]{:S(2)}, u32[]{:S(2)}) collective-permute-start(bf16[8,1,32,256]{3,2,1,0:T(8,128)(2,1)S(1)} %get-tuple-element.382), channel_id=1, source_target_pairs={{0,1},{1,2},{2,3},{3,4},{4,5},{5,6},{6,7},{7,8},{8,9},{9,10},{10,1... | collective-permute-start | bytes 393224 | tf_op jit(solution)/shard_map/ppermute | solution.py:16
  13.0 27.5 %collective-permute-start.4 = (bf16[8,1,32,256]{3,2,1,0:T(8,128)(2,1)S(1)}, bf16[8,1,32,256]{3,2,1,0:T(8,128)(2,1)S(1)}, u32[]{:S(2)}, u32[]{:S(2)}) collective-permute-start(bf16[8,1,32,256]{3,2,1,0:T(8,128)(2,1)S(1)} %get-tuple-element.383), channel_id=1, source_target_pairs={{1,0},{2,1},{3,2},{4,3},{5,4},{6,5},{7,6},{8,7},{9,8},{10,9},{11,1... | collective-permute-start | bytes 393224 | tf_op jit(solution)/shard_map/ppermute | solution.py:19
  40.5 0.7 copy-start
  41.4 12.4 %collective-permute-start = (bf16[8,1,32,256]{3,2,1,0:T(8,128)(2,1)S(1)}, bf16[8,1,32,256]{3,2,1,0:T(8,128)(2,1)S(1)}, u32[]{:S(2)}, u32[]{:S(2)}) collective-permute-start(bf16[8,1,32,256]{3,2,1,0:T(8,128)(2,1)S(1)} %get-tuple-element.446), channel_id=1, source_target_pairs={{1,0},{2,1},{3,2},{4,3},{5,4},{6,5},{7,6},{8,7},{9,8},{10,9},{11,1... | collective-permute-start | bytes 393224 | tf_op jit(solution)/shard_map/while/body/eval_jaxpr/ppermute | solution.py:19
  47.4 7.6 %collective-permute-start.1 = (bf16[8,1,32,256]{3,2,1,0:T(8,128)(2,1)S(1)}, bf16[8,1,32,256]{3,2,1,0:T(8,128)(2,1)S(1)}, u32[]{:S(2)}, u32[]{:S(2)}) collective-permute-start(bf16[8,1,32,256]{3,2,1,0:T(8,128)(2,1)S(1)} %get-tuple-element.447), channel_id=1, source_target_pairs={{0,1},{1,2},{2,3},{3,4},{4,5},{5,6},{6,7},{7,8},{8,9},{9,10},{10,1... | collective-permute-start | bytes 393224 | tf_op jit(solution)/shard_map/while/body/eval_jaxpr/ppermute | solution.py:16
  55.1 7.1 %collective-permute-start.2 = (bf16[8,2,32,256]{3,2,1,0:T(8,128)(2,1)S(1)}, bf16[8,2,32,256]{3,2,1,0:T(8,128)(2,1)S(1)}, u32[]{:S(2)}, u32[]{:S(2)}) collective-permute-start(bf16[8,2,32,256]{3,2,1,0:T(8,128)(2,1)S(1)} %get-tuple-element.448), channel_id=1, source_target_pairs={{64,0},{128,64},{192,128},{256,192},{320,256},{384,320},{448,384},... | collective-permute-start | bytes 786440 | tf_op jit(solution)/shard_map/while/body/eval_jaxpr/ppermute | solution.py:27
  62.4 9.2 %collective-permute-start = (bf16[8,1,32,256]{3,2,1,0:T(8,128)(2,1)S(1)}, bf16[8,1,32,256]{3,2,1,0:T(8,128)(2,1)S(1)}, u32[]{:S(2)}, u32[]{:S(2)}) collective-permute-start(bf16[8,1,32,256]{3,2,1,0:T(8,128)(2,1)S(1)} %get-tuple-element.446), channel_id=1, source_target_pairs={{1,0},{2,1},{3,2},{4,3},{5,4},{6,5},{7,6},{8,7},{9,8},{10,9},{11,1... | collective-permute-start | bytes 393224 | tf_op jit(solution)/shard_map/while/body/eval_jaxpr/ppermute | solution.py:19
  64.3 8.5 %collective-permute-start.1 = (bf16[8,1,32,256]{3,2,1,0:T(8,128)(2,1)S(1)}, bf16[8,1,32,256]{3,2,1,0:T(8,128)(2,1)S(1)}, u32[]{:S(2)}, u32[]{:S(2)}) collective-permute-start(bf16[8,1,32,256]{3,2,1,0:T(8,128)(2,1)S(1)} %get-tuple-element.447), channel_id=1, source_target_pairs={{0,1},{1,2},{2,3},{3,4},{4,5},{5,6},{6,7},{7,8},{8,9},{9,10},{10,1... | collective-permute-start | bytes 393224 | tf_op jit(solution)/shard_map/while/body/eval_jaxpr/ppermute | solution.py:16
  72.9 7.1 %collective-permute-start.2 = (bf16[8,2,32,256]{3,2,1,0:T(8,128)(2,1)S(1)}, bf16[8,2,32,256]{3,2,1,0:T(8,128)(2,1)S(1)}, u32[]{:S(2)}, u32[]{:S(2)}) collective-permute-start(bf16[8,2,32,256]{3,2,1,0:T(8,128)(2,1)S(1)} %get-tuple-element.448), channel_id=1, source_target_pairs={{64,0},{128,64},{192,128},{256,192},{320,256},{384,320},{448,384},... | collective-permute-start | bytes 786440 | tf_op jit(solution)/shard_map/while/body/eval_jaxpr/ppermute | solution.py:27
  80.2 9.2 %collective-permute-start = (bf16[8,1,32,256]{3,2,1,0:T(8,128)(2,1)S(1)}, bf16[8,1,32,256]{3,2,1,0:T(8,128)(2,1)S(1)}, u32[]{:S(2)}, u32[]{:S(2)}) collective-permute-start(bf16[8,1,32,256]{3,2,1,0:T(8,128)(2,1)S(1)} %get-tuple-element.446), channel_id=1, source_target_pairs={{1,0},{2,1},{3,2},{4,3},{5,4},{6,5},{7,6},{8,7},{9,8},{10,9},{11,1... | collective-permute-start | bytes 393224 | tf_op jit(solution)/shard_map/while/body/eval_jaxpr/ppermute | solution.py:19
  82.2 8.5 %collective-permute-start.1 = (bf16[8,1,32,256]{3,2,1,0:T(8,128)(2,1)S(1)}, bf16[8,1,32,256]{3,2,1,0:T(8,128)(2,1)S(1)}, u32[]{:S(2)}, u32[]{:S(2)}) collective-permute-start(bf16[8,1,32,256]{3,2,1,0:T(8,128)(2,1)S(1)} %get-tuple-element.447), channel_id=1, source_target_pairs={{0,1},{1,2},{2,3},{3,4},{4,5},{5,6},{6,7},{7,8},{8,9},{9,10},{10,1... | collective-permute-start | bytes 393224 | tf_op jit(solution)/shard_map/while/body/eval_jaxpr/ppermute | solution.py:16
  90.8 7.1 %collective-permute-start.2 = (bf16[8,2,32,256]{3,2,1,0:T(8,128)(2,1)S(1)}, bf16[8,2,32,256]{3,2,1,0:T(8,128)(2,1)S(1)}, u32[]{:S(2)}, u32[]{:S(2)}) collective-permute-start(bf16[8,2,32,256]{3,2,1,0:T(8,128)(2,1)S(1)} %get-tuple-element.448), channel_id=1, source_target_pairs={{64,0},{128,64},{192,128},{256,192},{320,256},{384,320},{448,384},... | collective-permute-start | bytes 786440 | tf_op jit(solution)/shard_map/while/body/eval_jaxpr/ppermute | solution.py:27
  98.1 10.6 %collective-permute-start = (bf16[8,1,32,256]{3,2,1,0:T(8,128)(2,1)S(1)}, bf16[8,1,32,256]{3,2,1,0:T(8,128)(2,1)S(1)}, u32[]{:S(2)}, u32[]{:S(2)}) collective-permute-start(bf16[8,1,32,256]{3,2,1,0:T(8,128)(2,1)S(1)} %get-tuple-element.446), channel_id=1, source_target_pairs={{1,0},{2,1},{3,2},{4,3},{5,4},{6,5},{7,6},{8,7},{9,8},{10,9},{11,1... | collective-permute-start | bytes 393224 | tf_op jit(solution)/shard_map/while/body/eval_jaxpr/ppermute | solution.py:19
  100.0 9.6 %collective-permute-start.1 = (bf16[8,1,32,256]{3,2,1,0:T(8,128)(2,1)S(1)}, bf16[8,1,32,256]{3,2,1,0:T(8,128)(2,1)S(1)}, u32[]{:S(2)}, u32[]{:S(2)}) collective-permute-start(bf16[8,1,32,256]{3,2,1,0:T(8,128)(2,1)S(1)} %get-tuple-element.447), channel_id=1, source_target_pairs={{0,1},{1,2},{2,3},{3,4},{4,5},{5,6},{6,7},{7,8},{8,9},{9,10},{10,1... | collective-permute-start | bytes 393224 | tf_op jit(solution)/shard_map/while/body/eval_jaxpr/ppermute | solution.py:16
  109.7 7.1 %collective-permute-start.2 = (bf16[8,2,32,256]{3,2,1,0:T(8,128)(2,1)S(1)}, bf16[8,2,32,256]{3,2,1,0:T(8,128)(2,1)S(1)}, u32[]{:S(2)}, u32[]{:S(2)}) collective-permute-start(bf16[8,2,32,256]{3,2,1,0:T(8,128)(2,1)S(1)} %get-tuple-element.448), channel_id=1, source_target_pairs={{64,0},{128,64},{192,128},{256,192},{320,256},{384,320},{448,384},... | collective-permute-start | bytes 786440 | tf_op jit(solution)/shard_map/while/body/eval_jaxpr/ppermute | solution.py:27
  117.0 11.2 %collective-permute-start = (bf16[8,1,32,256]{3,2,1,0:T(8,128)(2,1)S(1)}, bf16[8,1,32,256]{3,2,1,0:T(8,128)(2,1)S(1)}, u32[]{:S(2)}, u32[]{:S(2)}) collective-permute-start(bf16[8,1,32,256]{3,2,1,0:T(8,128)(2,1)S(1)} %get-tuple-element.446), channel_id=1, source_target_pairs={{1,0},{2,1},{3,2},{4,3},{5,4},{6,5},{7,6},{8,7},{9,8},{10,9},{11,1... | collective-permute-start | bytes 393224 | tf_op jit(solution)/shard_map/while/body/eval_jaxpr/ppermute | solution.py:19
  119.0 10.2 %collective-permute-start.1 = (bf16[8,1,32,256]{3,2,1,0:T(8,128)(2,1)S(1)}, bf16[8,1,32,256]{3,2,1,0:T(8,128)(2,1)S(1)}, u32[]{:S(2)}, u32[]{:S(2)}) collective-permute-start(bf16[8,1,32,256]{3,2,1,0:T(8,128)(2,1)S(1)} %get-tuple-element.447), channel_id=1, source_target_pairs={{0,1},{1,2},{2,3},{3,4},{4,5},{5,6},{6,7},{7,8},{8,9},{9,10},{10,1... | collective-permute-start | bytes 393224 | tf_op jit(solution)/shard_map/while/body/eval_jaxpr/ppermute | solution.py:16
  129.3 7.1 %collective-permute-start.2 = (bf16[8,2,32,256]{3,2,1,0:T(8,128)(2,1)S(1)}, bf16[8,2,32,256]{3,2,1,0:T(8,128)(2,1)S(1)}, u32[]{:S(2)}, u32[]{:S(2)}) collective-permute-start(bf16[8,2,32,256]{3,2,1,0:T(8,128)(2,1)S(1)} %get-tuple-element.448), channel_id=1, source_target_pairs={{64,0},{128,64},{192,128},{256,192},{320,256},{384,320},{448,384},... | collective-permute-start | bytes 786440 | tf_op jit(solution)/shard_map/while/body/eval_jaxpr/ppermute | solution.py:27
  136.6 10.9 %collective-permute-start = (bf16[8,1,32,256]{3,2,1,0:T(8,128)(2,1)S(1)}, bf16[8,1,32,256]{3,2,1,0:T(8,128)(2,1)S(1)}, u32[]{:S(2)}, u32[]{:S(2)}) collective-permute-start(bf16[8,1,32,256]{3,2,1,0:T(8,128)(2,1)S(1)} %get-tuple-element.446), channel_id=1, source_target_pairs={{1,0},{2,1},{3,2},{4,3},{5,4},{6,5},{7,6},{8,7},{9,8},{10,9},{11,1... | collective-permute-start | bytes 393224 | tf_op jit(solution)/shard_map/while/body/eval_jaxpr/ppermute | solution.py:19
  138.5 9.9 %collective-permute-start.1 = (bf16[8,1,32,256]{3,2,1,0:T(8,128)(2,1)S(1)}, bf16[8,1,32,256]{3,2,1,0:T(8,128)(2,1)S(1)}, u32[]{:S(2)}, u32[]{:S(2)}) collective-permute-start(bf16[8,1,32,256]{3,2,1,0:T(8,128)(2,1)S(1)} %get-tuple-element.447), channel_id=1, source_target_pairs={{0,1},{1,2},{2,3},{3,4},{4,5},{5,6},{6,7},{7,8},{8,9},{9,10},{10,1... | collective-permute-start | bytes 393224 | tf_op jit(solution)/shard_map/while/body/eval_jaxpr/ppermute | solution.py:16
  148.5 7.3 %collective-permute-start.2 = (bf16[8,2,32,256]{3,2,1,0:T(8,128)(2,1)S(1)}, bf16[8,2,32,256]{3,2,1,0:T(8,128)(2,1)S(1)}, u32[]{:S(2)}, u32[]{:S(2)}) collective-permute-start(bf16[8,2,32,256]{3,2,1,0:T(8,128)(2,1)S(1)} %get-tuple-element.448), channel_id=1, source_target_pairs={{64,0},{128,64},{192,128},{256,192},{320,256},{384,320},{448,384},... | collective-permute-start | bytes 786440 | tf_op jit(solution)/shard_map/while/body/eval_jaxpr/ppermute | solution.py:27
  156.0 10.5 %collective-permute-start = (bf16[8,1,32,256]{3,2,1,0:T(8,128)(2,1)S(1)}, bf16[8,1,32,256]{3,2,1,0:T(8,128)(2,1)S(1)}, u32[]{:S(2)}, u32[]{:S(2)}) collective-permute-start(bf16[8,1,32,256]{3,2,1,0:T(8,128)(2,1)S(1)} %get-tuple-element.446), channel_id=1, source_target_pairs={{1,0},{2,1},{3,2},{4,3},{5,4},{6,5},{7,6},{8,7},{9,8},{10,9},{11,1... | collective-permute-start | bytes 393224 | tf_op jit(solution)/shard_map/while/body/eval_jaxpr/ppermute | solution.py:19
  157.9 9.8 %collective-permute-start.1 = (bf16[8,1,32,256]{3,2,1,0:T(8,128)(2,1)S(1)}, bf16[8,1,32,256]{3,2,1,0:T(8,128)(2,1)S(1)}, u32[]{:S(2)}, u32[]{:S(2)}) collective-permute-start(bf16[8,1,32,256]{3,2,1,0:T(8,128)(2,1)S(1)} %get-tuple-element.447), channel_id=1, source_target_pairs={{0,1},{1,2},{2,3},{3,4},{4,5},{5,6},{6,7},{7,8},{8,9},{9,10},{10,1... | collective-permute-start | bytes 393224 | tf_op jit(solution)/shard_map/while/body/eval_jaxpr/ppermute | solution.py:16
  167.8 67.7 %collective-permute-start.2 = (bf16[8,2,32,256]{3,2,1,0:T(8,128)(2,1)S(1)}, bf16[8,2,32,256]{3,2,1,0:T(8,128)(2,1)S(1)}, u32[]{:S(2)}, u32[]{:S(2)}) collective-permute-start(bf16[8,2,32,256]{3,2,1,0:T(8,128)(2,1)S(1)} %get-tuple-element.448), channel_id=1, source_target_pairs={{64,0},{128,64},{192,128},{256,192},{320,256},{384,320},{448,384},... | collective-permute-start | bytes 786440 | tf_op jit(solution)/shard_map/while/body/eval_jaxpr/ppermute | solution.py:27
  240.3 9.8 %collective-permute-start.5 = (bf16[8,1,32,256]{3,2,1,0:T(8,128)(2,1)S(1)}, bf16[8,1,32,256]{3,2,1,0:T(8,128)(2,1)S(1)}, u32[]{:S(2)}, u32[]{:S(2)}) collective-permute-start(bf16[8,1,32,256]{3,2,1,0:T(8,128)(2,1)S(1)} %get-tuple-element.380), channel_id=1, source_target_pairs={{0,1},{1,2},{2,3},{3,4},{4,5},{5,6},{6,7},{7,8},{8,9},{9,10},{10,1... | collective-permute-start | bytes 393224 | tf_op jit(solution)/shard_map/ppermute | solution.py:16
  248.1 6.3 %collective-permute-start.6 = (bf16[8,1,32,256]{3,2,1,0:T(8,128)(2,1)S(1)}, bf16[8,1,32,256]{3,2,1,0:T(8,128)(2,1)S(1)}, u32[]{:S(2)}, u32[]{:S(2)}) collective-permute-start(bf16[8,1,32,256]{3,2,1,0:T(8,128)(2,1)S(1)} %get-tuple-element.381), channel_id=1, source_target_pairs={{1,0},{2,1},{3,2},{4,3},{5,4},{6,5},{7,6},{8,7},{9,8},{10,9},{11,1... | collective-permute-start | bytes 393224 | tf_op jit(solution)/shard_map/ppermute | solution.py:19
Sparse Core Ops, SparseCore 0:
  260.5 72.9 all-reduce.12
where the time goes:
time: 511 us; the launch traced here: 510 us
  blocking collectives  263 us (51%)
  waiting for transfers between devices  119 us (23%)
  starting transfers between devices  97.2 us (19%)
  between operations  14.2 us (3%)
  matrix products  9.16 us (2%)
    psum x1, blocking collectives, local(): plane_sum, depth_sum = lax.psum((plane_sum, depth_sum), 'gy')  242 us
    ppermute x7, waiting for transfers between devices, passed_along(): return lax.ppermute(block, axis, route)  101 us
    ppermute x9, starting transfers between devices, padded_2(): lax.ppermute(lax.slice_in_dim(block, block.shape[dim] - width, None, axis...  63.2 us
    ppermute x9, starting transfers between devices, padded_2(): lax.ppermute(lax.slice_in_dim(block, 0, width, axis=dim), axis, backward)  25 us
    all_gather x1, blocking collectives, local(): seed = lax.all_gather(grad_out, 'segment', axis=0, tiled=True)  21.5 us
  transfers between devices with their start and end apart: 26, of which 22 were waited for; matrix products, arithmetic and copies ran while one was open for 0% of the time, Pallas kernels for 0%

commit v1 on v0

v1 whole, which is shorter than its diff:
```python
import math

import jax
import jax.numpy as jnp
from jax import lax
from jax.sharding import PartitionSpec as P

TILE = 128


def padded_2(block, sides, width):
    for axis, dim in sides:
        count = lax.axis_size(axis)
        forward = [(i, i + 1) for i in range(count - 1)]
        backward = [(target, source) for source, target in forward]
        low = lax.ppermute(
            lax.slice_in_dim(block, block.shape[dim] - width, None, axis=dim), axis, forward
        )
        high = lax.ppermute(lax.slice_in_dim(block, 0, width, axis=dim), axis, backward)
        block = jnp.concatenate([low, block, high], axis=dim)
    return block


def width_pad(field):
    return jnp.pad(field, [(0, 0)] * (field.ndim - 1) + [(1, 1)])


def plane_conv_all(rows_in, kernel, height, width):
    padded = width_pad(rows_in)
    total = None
    for i in range(3):
        for j in range(3):
            term = jnp.einsum(
                "loc,lzycx->lzyox",
                kernel[:, i, j],
                padded[:, :, i : i + height, :, j : j + width],
                preferred_element_type=jnp.float32,
            )
            total = term if total is None else total + term
    return total


def depth_conv_all(deep, kernel, depth):
    total = None
    for k in range(3):
        term = jnp.einsum(
            "loc,lzycx->lzyox", kernel[:, k], deep[:, k : k + depth], preferred_element_type=jnp.float32
        )
        total = term if total is None else total + term
    return total


def plane_back(rows_grad, kernel, height, width):
    padded = width_pad(rows_grad)
    total = None
    for i in range(3):
        for j in range(3):
            term = jnp.einsum(
                "oc,...yox->...ycx",
                kernel[i, j],
                padded[..., 2 - i : 2 - i + height, :, 2 - j : 2 - j + width],
                preferred_element_type=jnp.float32,
            )
            total = term if total is None else total + term
    return total


def plane_taps(grad_mid, rows_in, height, width):
    padded = width_pad(rows_in)
    rows_out = []
    for i in range(3):
        row_taps = []
        for j in range(3):
            row_taps.append(
                jnp.einsum(
                    "...yox,...ycx->oc",
                    grad_mid,
                    padded[..., i : i + height, :, j : j + width],
                    preferred_element_type=jnp.float32,
                )
            )
        rows_out.append(jnp.stack(row_taps))
    return jnp.stack(rows_out)


def depth_back(mix_deep, kernel, depth):
    total = None
    for k in range(3):
        term = jnp.einsum(
            "oc,zyox->zycx",
            kernel[k],
            mix_deep[2 - k : 2 - k + depth],
            preferred_element_type=jnp.float32,
        )
        total = term if total is None else total + term
    return total


def depth_taps(grad_mix, deep, depth):
    return jnp.stack(
        [
            jnp.einsum(
                "zyox,zycx->oc", grad_mix, deep[k : k + depth], preferred_element_type=jnp.float32
            )
            for k in range(3)
        ]
    )


def silu_slope(value):
    sig = jax.nn.sigmoid(value)
    return sig * (1.0 + value * (1.0 - sig))


def local(acts, grad_out, w_plane, w_depth, tiles):
    sections = acts.shape[1]
    height = acts.shape[2]
    width = acts.shape[4]
    chans = w_plane.shape[3]
    count = lax.axis_size("segment")
    layers = count * acts.shape[0]
    zs = grad_out.shape[0]
    scale = 1.0 / math.sqrt(sections * height * lax.axis_size("gy") * width)
    segment = lax.axis_index("segment")

    mine = lax.all_to_all(acts, "segment", 1, 0, tiled=True)
    plane_w = lax.all_gather(w_plane, "segment", axis=0, tiled=True)
    depth_w = lax.all_gather(w_depth, "segment", axis=0, tiled=True)

    ids = (segment * zs + jnp.arange(zs, dtype=jnp.int32))[:, None] * (width // TILE) + jnp.arange(
        width // TILE, dtype=jnp.int32
    )[None, :]
    hit = jnp.any(tiles[0][None, None, :] == ids[:, :, None], axis=2)
    mask_full = jnp.repeat(hit.astype(jnp.float32), TILE, axis=1)[:, None, None, :]

    rows_own = padded_2(mine, (("gy", 2),), 1)
    mid = plane_conv_all(rows_own, plane_w, height, width).astype(jnp.bfloat16)
    deep = padded_2(mid, (("segment", 1),), 1)
    value = depth_conv_all(deep, depth_w, zs)
    factor = silu_slope(value) * mask_full[None]

    grad = grad_out
    plane_list = [None] * layers
    depth_list = [None] * layers
    for layer in reversed(range(layers)):
        grad_mix = (grad.astype(jnp.float32) * factor[layer]).astype(jnp.bfloat16)
        mix_deep = padded_2(grad_mix, (("segment", 0),), 1)
        grad_mid = depth_back(mix_deep, depth_w[layer], zs).astype(jnp.bfloat16)
        rows_grad = padded_2(grad_mid, (("gy", 1),), 1)
        grad = (
            grad.astype(jnp.float32) + plane_back(rows_grad, plane_w[layer], height, width)
        ).astype(jnp.bfloat16)
        depth_list[layer] = depth_taps(grad_mix, deep[layer], zs)
        plane_list[layer] = plane_taps(grad_mid, rows_own[layer], height, width)

    planes = jnp.stack(plane_list).reshape(layers, -1)
    depths = jnp.stack(depth_list).reshape(layers, -1)
    flat = jnp.concatenate([planes, depths], axis=1) * scale
    flat = lax.psum_scatter(flat, "segment", scatter_dimension=0, tiled=True)
    flat = lax.psum(flat, "gy")
    cut = planes.shape[1]
    plane_sum = flat[:, :cut].reshape(-1, 3, 3, chans, chans)
    depth_sum = flat[:, cut:].reshape(-1, 3, chans, chans)
    return (grad, plane_sum, depth_sum)


def solution(mesh):
    placed = (
        P("segment", None, "gy", None, None),
        P("segment", "gy", None, None),
        P("segment", None, None, None, None),
        P("segment", None, None, None),
        P("gy", None),
    )
    return jax.shard_map(
        local,
        mesh=mesh,
        in_specs=placed,
        out_specs=(
            P("segment", "gy", None, None),
            P("segment", None, None, None, None),
            P("segment", None, None, None),
        ),
        check_vma=False,
    )
```

time: 511 us -> 604 us (1.18)
  matrix products: 9.16 us -> 38.6 us
  blocking collectives: 263 us -> 286 us
  starting transfers between devices: 97.2 us -> 120 us
  waiting for transfers between devices: 119 us -> 131 us
    ppermute x7 -> x0, waiting for transfers between devices: 101 us -> none  [passed_along(): return lax.ppermute(block, axis, route)]
    unnamed x1 -> x2, waiting for transfers between devices: 0.02 us -> 77.7 us
    ppermute x9 -> x18, waiting for transfers between devices: 10.2 us -> 51.8 us  [padded_2(): lax.ppermute(lax.slice_in_dim(block, 0, width, axis=dim), axis, backward)]
    all_gather x1 -> x2, blocking collectives: 21.5 us -> 40.5 us  [the longest x1 21 us: local(): depth_w = lax.all_gather(w_depth, 'segment', axis=0, tiled=True)]
    ppermute x9 -> x18, starting transfers between devices: 63.2 us -> 80 us  [padded_2(): lax.ppermute(lax.slice_in_dim(block, block.shape[dim] - width, None, axis...]
    dot_general x9 -> x72, matrix products: 2.33 us -> 15 us  [plane_back(): jnp.einsum('oc,...yox->...ycx', kernel[i, j], padded[..., 2 - i:2 - i + h...]
    all_to_all x0 -> x1, starting transfers between devices: none -> 10.9 us  [local(): mine = lax.all_to_all(acts, 'segment', 1, 0, tiled=True)]
    dot_general x9 -> x72, matrix products: 2.34 us -> 12.9 us  [plane_taps(): jnp.einsum('...yox,...ycx->oc', grad_mid, padded[..., i:i + height, :, j:...]
  transfers between devices with their start and end apart: 26 -> 38, of which waited for: 22 -> 20; matrix products, arithmetic and copies ran while one was open for 0% -> 2% of each run, Pallas kernels for 0% -> 0%
where the time goes in v1:
time: 604 us; the launch traced here: 600 us
  blocking collectives  286 us (47%)
  waiting for transfers between devices  131 us (22%)
  starting transfers between devices  120 us (20%)
  matrix products  38.6 us (6%)
  between operations  15.3 us (3%)
  local copies, waits for them, and re-layouts  7.11 us (1%)
    psum x1, blocking collectives, local(): flat = lax.psum(flat, 'gy')  246 us
    ppermute x18, starting transfers between devices, padded_2(): lax.ppermute(lax.slice_in_dim(block, block.shape[dim] - width, None, axis...  80 us
    unnamed x2, waiting for transfers between devices  77.7 us
    ppermute x18, waiting for transfers between devices, padded_2(): lax.ppermute(lax.slice_in_dim(block, 0, width, axis=dim), axis, backward)  51.8 us
    ppermute x18, starting transfers between devices, padded_2(): lax.ppermute(lax.slice_in_dim(block, 0, width, axis=dim), axis, backward)  28.9 us
    all_gather x1, blocking collectives, local(): depth_w = lax.all_gather(w_depth, 'segment', axis=0, tiled=True)  21 us
    all_gather x1, blocking collectives, local(): plane_w = lax.all_gather(w_plane, 'segment', axis=0, tiled=True)  19.5 us
    dot_general x72, matrix products, plane_back(): jnp.einsum('oc,...yox->...ycx', kernel[i, j], padded[..., 2 - i:2 - i + h...  15 us
  transfers between devices with their start and end apart: 38, of which 20 were waited for; matrix products, arithmetic and copies ran while one was open for 2% of the time, Pallas kernels for 0%

profile of v1, /device:TPU:1, one launch (start us, length us, event | category | flops | bytes accessed | tf_op | source)
XLA Modules:
  0.0 600.1 jit_solution(2332710889217415071)
XLA Ops:
  7.2 10.9 %all-to-all-start = ((bf16[1,8,2,32,256]{4,3,2,0,1:T(8,128)(2,1)}), bf16[1,8,2,32,256]{4,3,2,0,1:T(8,128)(2,1)S(1)}, u32[]{:S(2)}, u32[]{:S(2)}) async-start(bf16[1,8,2,32,256]{4,3,2,0,1:T(8,128)(2,1)} %bitcast.2011), calls=%async_computation | async-start | bytes 524288 | tf_op jit(solution)/shard_map/all_to_all | solution.py:126
  19.6 21.0 %all_gather.7 = bf16[8,3,32,32]{3,2,0,1:T(8,128)(2,1)S(1)} all-gather(bf16[1,3,32,32]{3,2,0,1:T(8,128)(2,1)S(1)} %bitcast.2013), channel_id=1, replica_groups=mesh['segment'=8,'gy'=64] {'segment'}, dimensions={0}, use_global_device_ids=true | all-gather | bytes 55296 | tf_op jit(solution)/shard_map/all_gather | solution.py:128
  40.6 19.5 %all_gather.6 = bf16[8,3,3,32,32]{4,3,0,2,1:T(8,128)(2,1)S(1)} all-gather(bf16[1,3,3,32,32]{4,3,0,2,1:T(8,128)(2,1)S(1)} %bitcast.2012), channel_id=1, replica_groups=mesh['segment'=8,'gy'=64] {'segment'}, dimensions={0}, use_global_device_ids=true | all-gather | bytes 165888 | tf_op jit(solution)/shard_map/all_gather | solution.py:127
  60.2 15.3 %collective-permute-start = (bf16[8,1,1,32,256]{4,3,2,0,1:T(8,128)(2,1)S(1)}, bf16[8,1,1,32,256]{4,3,2,0,1:T(8,128)(2,1)S(1)}, u32[]{:S(2)}, u32[]{:S(2)}) collective-permute-start(bf16[8,1,1,32,256]{4,3,2,0,1:T(8,128)(2,1)S(1)} %get-tuple-element.19), channel_id=1, source_target_pairs={{0,1},{1,2},{2,3},{3,4},{4,5},{5,6},{6,7},{7,8},{8,9},{9,10},{10,1... | collective-permute-start | bytes 393224 | tf_op jit(solution)/shard_map/ppermute | solution.py:16
  75.5 1.9 collective-permute-start.1
  77.5 4.3 collective-permute-done.1
  85.5 4.5 collective-permute-start.2
  94.1 3.8 collective-permute-start.5
  99.9 2.9 collective-permute-done.4
  104.7 6.1 %collective-permute-start.6 = (bf16[1,1,32,256]{3,2,1,0:T(8,128)(2,1)S(1)}, bf16[1,1,32,256]{3,2,1,0:T(8,128)(2,1)S(1)}, u32[]{:S(2)}, u32[]{:S(2)}) collective-permute-start(bf16[1,1,32,256]{3,2,1,0:T(8,128)(2,1)S(1)} %get-tuple-element.35), channel_id=1, source_target_pairs={{0,1},{1,2},{2,3},{3,4},{4,5},{5,6},{6,7},{7,8},{8,9},{9,10},{10,1... | collective-permute-start | bytes 49160 | tf_op jit(solution)/shard_map/ppermute | solution.py:16
  110.8 1.9 collective-permute-start.7
  113.0 2.9 collective-permute-done.7
  118.0 3.6 collective-permute-start.9
  123.6 4.6 collective-permute-done.8
  130.0 3.1 collective-permute-start.10
  133.1 1.9 collective-permute-start.11
  135.3 2.9 collective-permute-done.11
  140.3 4.8 collective-permute-start.13
  147.1 2.9 collective-permute-done.12
  151.9 3.1 collective-permute-start.14
  155.0 1.9 collective-permute-start.15
  157.1 2.9 collective-permute-done.15
  162.2 3.6 collective-permute-start.17
  167.8 2.7 collective-permute-done.16
  172.3 3.4 collective-permute-start.18
  175.7 1.9 collective-permute-start.19
  177.8 2.9 collective-permute-done.19
  182.8 2.8 collective-permute-start.21
  187.7 2.7 collective-permute-done.20
  192.2 3.5 collective-permute-start.22
  195.7 1.9 collective-permute-start.23
  197.8 2.9 collective-permute-done.23
  202.9 2.8 collective-permute-start.25
  207.7 2.7 collective-permute-done.24
  212.2 4.6 collective-permute-start.26
  216.8 1.9 collective-permute-start.27
  218.9 2.9 collective-permute-done.27
  224.0 2.8 collective-permute-start.29
  228.8 2.7 collective-permute-done.28
  233.3 4.6 collective-permute-start.30
  237.9 1.9 collective-permute-start.31
  240.0 2.9 collective-permute-done.31
  245.1 2.8 collective-permute-start.33
  250.1 2.5 collective-permute-done.32
  254.6 4.6 collective-permute-start.34
  259.2 1.9 collective-permute-start.35
  266.8 77.7 %all-reduce.20.cloned.1.call-done = f32[8,12288]{1,0:T(8,128)} async-done(((f32[8,12288]{1,0:T(8,128)}), f32[8,12288]{1,0:T(8,128)}) %all-reduce.20.cloned.1.call-update) | async-done | bytes 393232
  346.1 245.5 %psum.7 = f32[1,12288]{1,0:T(1,128)S(1)} all-reduce(f32[1,12288]{1,0:T(1,128)S(1)} %constant_dynamic-slice_fusion), channel_id=1, replica_groups=mesh['segment'=8,'gy'=64] {'gy'}, use_global_device_ids=true, to_apply=%region_2.3 | all-reduce | flops 12288 | bytes 98304 | tf_op jit(solution)/shard_map/psum | solution.py:160
  (326 shorter events, 64.5 us)
Async XLA Ops:
  7.2 11.0 %copy-start.3 = (s32[1,12]{1,0:T(1,128)S(1)}, s32[1,12]{1,0:T(1,128)}, u32[]{:S(2)}) copy-start(s32[1,12]{1,0:T(1,128)} %param.9) | copy-start | bytes 148
  7.2 53.0 %all-to-all-start = ((bf16[1,8,2,32,256]{4,3,2,0,1:T(8,128)(2,1)}), bf16[1,8,2,32,256]{4,3,2,0,1:T(8,128)(2,1)S(1)}, u32[]{:S(2)}, u32[]{:S(2)}) async-start(bf16[1,8,2,32,256]{4,3,2,0,1:T(8,128)(2,1)} %bitcast.2011), calls=%async_computation | async-start | bytes 524288 | tf_op jit(solution)/shard_map/all_to_all | solution.py:126
  18.1 1.6 copy-start.2
  18.1 326.4 %all-reduce.20.cloned.1.call-start = ((), (), s32[]{:S(2)}) async-start(), calls=%async_computation.1 | async-start | bytes 786432
  19.6 21.0 %copy-start.1 = (bf16[1,3,3,32,32]{4,3,2,1,0:T(8,128)(2,1)S(1)}, bf16[1,3,3,32,32]{4,3,2,1,0:T(8,128)(2,1)}, u32[]{:S(2)}) copy-start(bf16[1,3,3,32,32]{4,3,2,1,0:T(8,128)(2,1)} %param.7) | copy-start | bytes 55300
  60.2 17.3 %collective-permute-start = (bf16[8,1,1,32,256]{4,3,2,0,1:T(8,128)(2,1)S(1)}, bf16[8,1,1,32,256]{4,3,2,0,1:T(8,128)(2,1)S(1)}, u32[]{:S(2)}, u32[]{:S(2)}) collective-permute-start(bf16[8,1,1,32,256]{4,3,2,0,1:T(8,128)(2,1)S(1)} %get-tuple-element.19), channel_id=1, source_target_pairs={{0,1},{1,2},{2,3},{3,4},{4,5},{5,6},{6,7},{7,8},{8,9},{9,10},{10,1... | collective-permute-start | bytes 393224 | tf_op jit(solution)/shard_map/ppermute | solution.py:16
  75.5 6.3 %collective-permute-start.1 = (bf16[8,1,1,32,256]{4,3,2,0,1:T(8,128)(2,1)S(1)}, bf16[8,1,1,32,256]{4,3,2,0,1:T(8,128)(2,1)S(1)}, u32[]{:S(2)}, u32[]{:S(2)}) collective-permute-start(bf16[8,1,1,32,256]{4,3,2,0,1:T(8,128)(2,1)S(1)} %get-tuple-element.20), channel_id=1, source_target_pairs={{1,0},{2,1},{3,2},{4,3},{5,4},{6,5},{7,6},{8,7},{9,8},{10,9},{11,1... | collective-permute-start | bytes 393224 | tf_op jit(solution)/shard_map/ppermute | solution.py:19
  84.2 7.6 %collective-permute-start.3 = (bf16[8,1,2,32,256]{4,3,2,0,1:T(8,128)(2,1)S(1)}, bf16[8,1,2,32,256]{4,3,2,0,1:T(8,128)(2,1)S(1)}, u32[]{:S(2)}, u32[]{:S(2)}) collective-permute-start(bf16[8,1,2,32,256]{4,3,2,0,1:T(8,128)(2,1)S(1)} %bitcast.1994), channel_id=1, source_target_pairs={{64,0},{128,64},{192,128},{256,192},{320,256},{384,320},{448,384},... | collective-permute-start | bytes 786440 | tf_op jit(solution)/shard_map/ppermute | solution.py:19
  85.5 8.0 %collective-permute-start.2 = (bf16[8,1,2,32,256]{4,3,2,0,1:T(8,128)(2,1)S(1)}, bf16[8,1,2,32,256]{4,3,2,0,1:T(8,128)(2,1)S(1)}, u32[]{:S(2)}, u32[]{:S(2)}) collective-permute-start(bf16[8,1,2,32,256]{4,3,2,0,1:T(8,128)(2,1)S(1)} %bitcast.1995), channel_id=1, source_target_pairs={{0,64},{64,128},{128,192},{192,256},{256,320},{320,384},{384,448},... | collective-permute-start | bytes 786440 | tf_op jit(solution)/shard_map/ppermute | solution.py:16
  92.0 1.9 copy-start
  94.1 5.6 collective-permute-start.5
  97.9 4.9 collective-permute-start.4
  104.7 8.3 %collective-permute-start.6 = (bf16[1,1,32,256]{3,2,1,0:T(8,128)(2,1)S(1)}, bf16[1,1,32,256]{3,2,1,0:T(8,128)(2,1)S(1)}, u32[]{:S(2)}, u32[]{:S(2)}) collective-permute-start(bf16[1,1,32,256]{3,2,1,0:T(8,128)(2,1)S(1)} %get-tuple-element.35), channel_id=1, source_target_pairs={{0,1},{1,2},{2,3},{3,4},{4,5},{5,6},{6,7},{7,8},{8,9},{9,10},{10,1... | collective-permute-start | bytes 49160 | tf_op jit(solution)/shard_map/ppermute | solution.py:16
  110.8 5.1 collective-permute-start.7
  118.0 5.4 collective-permute-start.9
  121.6 6.6 %collective-permute-start.8 = (bf16[1,2,32,256]{3,2,1,0:T(8,128)(2,1)S(1)}, bf16[1,2,32,256]{3,2,1,0:T(8,128)(2,1)S(1)}, u32[]{:S(2)}, u32[]{:S(2)}) collective-permute-start(bf16[1,2,32,256]{3,2,1,0:T(8,128)(2,1)S(1)} %get-tuple-element.37), channel_id=1, source_target_pairs={{64,0},{128,64},{192,128},{256,192},{320,256},{384,320},{448,384},... | collective-permute-start | bytes 98312 | tf_op jit(solution)/shard_map/ppermute | solution.py:19
  130.0 5.2 collective-permute-start.10
  133.1 5.1 collective-permute-start.11
  140.3 6.7 %collective-permute-start.13 = (bf16[1,2,32,256]{3,2,1,0:T(8,128)(2,1)S(1)}, bf16[1,2,32,256]{3,2,1,0:T(8,128)(2,1)S(1)}, u32[]{:S(2)}, u32[]{:S(2)}) collective-permute-start(bf16[1,2,32,256]{3,2,1,0:T(8,128)(2,1)S(1)} %get-tuple-element.39), channel_id=1, source_target_pairs={{0,64},{64,128},{128,192},{192,256},{256,320},{320,384},{384,448},... | collective-permute-start | bytes 98312 | tf_op jit(solution)/shard_map/ppermute | solution.py:16
  145.1 4.9 collective-permute-start.12
  151.9 5.2 collective-permute-start.14
  155.0 5.1 collective-permute-start.15
  162.2 5.4 collective-permute-start.17
  165.8 4.7 collective-permute-start.16
  172.3 5.5 collective-permute-start.18
  175.7 5.1 collective-permute-start.19
  182.8 4.7 collective-permute-start.21
  185.7 4.7 collective-permute-start.20
  192.2 5.6 collective-permute-start.22
  195.7 5.1 collective-permute-start.23
  202.9 4.7 collective-permute-start.25
  205.7 4.7 collective-permute-start.24
  212.2 6.7 %collective-permute-start.26 = (bf16[1,1,32,256]{3,2,1,0:T(8,128)(2,1)S(1)}, bf16[1,1,32,256]{3,2,1,0:T(8,128)(2,1)S(1)}, u32[]{:S(2)}, u32[]{:S(2)}) collective-permute-start(bf16[1,1,32,256]{3,2,1,0:T(8,128)(2,1)S(1)} %get-tuple-element.25), channel_id=1, source_target_pairs={{0,1},{1,2},{2,3},{3,4},{4,5},{5,6},{6,7},{7,8},{8,9},{9,10},{10,1... | collective-permute-start | bytes 49160 | tf_op jit(solution)/shard_map/ppermute | solution.py:16
  216.8 5.1 collective-permute-start.27
  224.0 4.7 collective-permute-start.29
  226.8 4.7 collective-permute-start.28
  233.3 6.7 %collective-permute-start.30 = (bf16[1,1,32,256]{3,2,1,0:T(8,128)(2,1)S(1)}, bf16[1,1,32,256]{3,2,1,0:T(8,128)(2,1)S(1)}, u32[]{:S(2)}, u32[]{:S(2)}) collective-permute-start(bf16[1,1,32,256]{3,2,1,0:T(8,128)(2,1)S(1)} %get-tuple-element.23), channel_id=1, source_target_pairs={{0,1},{1,2},{2,3},{3,4},{4,5},{5,6},{6,7},{7,8},{8,9},{9,10},{10,1... | collective-permute-start | bytes 49160 | tf_op jit(solution)/shard_map/ppermute | solution.py:16
  237.9 5.1 collective-permute-start.31
  245.1 4.8 collective-permute-start.33
  247.9 4.7 collective-permute-start.32
  254.6 7.8 %collective-permute-start.34 = (bf16[1,1,32,256]{3,2,1,0:T(8,128)(2,1)S(1)}, bf16[1,1,32,256]{3,2,1,0:T(8,128)(2,1)S(1)}, u32[]{:S(2)}, u32[]{:S(2)}) collective-permute-start(bf16[1,1,32,256]{3,2,1,0:T(8,128)(2,1)S(1)} %get-tuple-element.21), channel_id=1, source_target_pairs={{0,1},{1,2},{2,3},{3,4},{4,5},{5,6},{6,7},{7,8},{8,9},{9,10},{10,1... | collective-permute-start | bytes 49160 | tf_op jit(solution)/shard_map/ppermute | solution.py:16
  259.2 5.1 collective-permute-start.35
Sparse Core Ops, SparseCore 0:
  262.6 81.8 all-reduce.19

commit v2 on v1

--- a/solution.py
+++ b/solution.py
@@ -123,9 +123,15 @@
     scale = 1.0 / math.sqrt(sections * height * lax.axis_size("gy") * width)
     segment = lax.axis_index("segment")
 
-    mine = lax.all_to_all(acts, "segment", 1, 0, tiled=True)
-    plane_w = lax.all_gather(w_plane, "segment", axis=0, tiled=True)
-    depth_w = lax.all_gather(w_depth, "segment", axis=0, tiled=True)
+    block = acts[0].reshape(count, -1)
+    kernels = jnp.concatenate([w_plane.reshape(1, -1), w_depth.reshape(1, -1)], axis=1)
+    send = jnp.concatenate([block, jnp.broadcast_to(kernels, (count, kernels.shape[1]))], axis=1)
+    got = lax.all_to_all(send, "segment", 0, 0, tiled=True)
+    cut_a = block.shape[1]
+    cut_w = cut_a + w_plane[0].size
+    mine = got[:, :cut_a].reshape((count, zs) + acts.shape[2:])
+    plane_w = got[:, cut_a:cut_w].reshape((count,) + w_plane.shape[1:])
+    depth_w = got[:, cut_w:].reshape((count,) + w_depth.shape[1:])
 
     ids = (segment * zs + jnp.arange(zs, dtype=jnp.int32))[:, None] * (width // TILE) + jnp.arange(
         width // TILE, dtype=jnp.int32
@@ -156,8 +162,14 @@
     planes = jnp.stack(plane_list).reshape(layers, -1)
     depths = jnp.stack(depth_list).reshape(layers, -1)
     flat = jnp.concatenate([planes, depths], axis=1) * scale
-    flat = lax.psum_scatter(flat, "segment", scatter_dimension=0, tiled=True)
-    flat = lax.psum(flat, "gy")
+    flat = lax.all_to_all(flat, "segment", 0, 0, tiled=True).sum(axis=0)
+    spread_n = lax.axis_size("gy")
+    size = flat.shape[0]
+    piece = -(-size // spread_n)
+    flat = jnp.pad(flat, (0, piece * spread_n - size)).reshape(spread_n, piece)
+    part = lax.all_to_all(flat, "gy", 0, 0, tiled=True).sum(axis=0)
+    whole = lax.all_to_all(jnp.broadcast_to(part, (spread_n, piece)), "gy", 0, 0, tiled=True)
+    flat = whole.reshape(-1)[:size][None]
     cut = planes.shape[1]
     plane_sum = flat[:, :cut].reshape(-1, 3, 3, chans, chans)
     depth_sum = flat[:, cut:].reshape(-1, 3, chans, chans)

time: 604 us -> 286 us (0.47)
  blocking collectives: 286 us -> 0 us
  waiting for transfers between devices: 131 us -> 90.7 us
  starting transfers between devices: 120 us -> 135 us
  between operations: 15.3 us -> 2.14 us
  local copies, waits for them, and re-layouts: 7.11 us -> 15.5 us
    psum x1 -> x0, blocking collectives: 246 us -> none  [local(): flat = lax.psum(flat, 'gy')]
    unnamed x2 -> x0, waiting for transfers between devices: 77.7 us -> none
    all_to_all x1 -> x4, waiting for transfers between devices: 0.01 us -> 46 us  [the longest x1 15.5 us: local(): got = lax.all_to_all(send, 'segment', 0, 0, tiled=True)]
    all_gather x2 -> x0, blocking collectives: 40.5 us -> none  [the longest x1 21 us: local(): depth_w = lax.all_gather(w_depth, 'segment', axis=0, tiled=True)]
    all_to_all x1 -> x4, starting transfers between devices: 10.9 us -> 39.8 us  [the longest x1 21 us: local(): part = lax.all_to_all(flat, 'gy', 0, 0, tiled=True).sum(axis=0)]
    ppermute x18, starting transfers between devices: 80 us -> 65.8 us  [padded_2(): lax.ppermute(lax.slice_in_dim(block, block.shape[dim] - width, None, axis...]
    ppermute x18, waiting for transfers between devices: 51.8 us -> 43.2 us  [padded_2(): lax.ppermute(lax.slice_in_dim(block, 0, width, axis=dim), axis, backward)]
  transfers between devices with their start and end apart: 38 -> 40, of which waited for: 20 -> 22; matrix products, arithmetic and copies ran while one was open for 2% -> 6% of each run, Pallas kernels for 0% -> 0%
where the time goes in v2:
time: 286 us; the launch traced here: 285 us
  starting transfers between devices  135 us (47%)
  waiting for transfers between devices  90.7 us (32%)
  matrix products  37.5 us (13%)
  local copies, waits for them, and re-layouts  15.5 us (5%)
  other arithmetic  4.27 us (1%)
    ppermute x18, starting transfers between devices, padded_2(): lax.ppermute(lax.slice_in_dim(block, block.shape[dim] - width, None, axis...  65.8 us
    ppermute x18, waiting for transfers between devices, padded_2(): lax.ppermute(lax.slice_in_dim(block, 0, width, axis=dim), axis, backward)  43.2 us
    ppermute x18, starting transfers between devices, padded_2(): lax.ppermute(lax.slice_in_dim(block, 0, width, axis=dim), axis, backward)  29.1 us
    all_to_all x1, starting transfers between devices, local(): part = lax.all_to_all(flat, 'gy', 0, 0, tiled=True).sum(axis=0)  21 us
    all_to_all x1, waiting for transfers between devices, local(): got = lax.all_to_all(send, 'segment', 0, 0, tiled=True)  15.5 us
    dot_general x72, matrix products, plane_back(): jnp.einsum('oc,...yox->...ycx', kernel[i, j], padded[..., 2 - i:2 - i + h...  14 us
    dot_general x72, matrix products, plane_taps(): jnp.einsum('...yox,...ycx->oc', grad_mid, padded[..., i:i + height, :, j:...  12.9 us
    all_to_all x1, waiting for transfers between devices, local(): flat = lax.all_to_all(flat, 'segment', 0, 0, tiled=True).sum(axis=0)  11.8 us
  transfers between devices with their start and end apart: 40, of which 22 were waited for; matrix products, arithmetic and copies ran while one was open for 6% of the time, Pallas kernels for 0%

profile of v2, /device:TPU:1, one launch (start us, length us, event | category | flops | bytes accessed | tf_op | source)
XLA Modules:
  0.0 284.8 jit_solution(17372313737670031647)
XLA Ops:
  5.4 10.9 %all-to-all-start = ((bf16[8,2,14336]{2,1,0:T(2,128)(2,1)}), bf16[8,2,14336]{2,1,0:T(2,128)(2,1)S(1)}, u32[]{:S(2)}, u32[]{:S(2)}) async-start(bf16[8,2,14336]{2,1,0:T(2,128)(2,1)} %reshape.1683), calls=%async_computation | async-start | bytes 917504 | tf_op jit(solution)/shard_map/all_to_all | solution.py:129
  17.2 15.5 %all-to-all-done = bf16[8,2,14336]{2,1,0:T(2,128)(2,1)S(1)} async-done(((bf16[8,2,14336]{2,1,0:T(2,128)(2,1)}), bf16[8,2,14336]{2,1,0:T(2,128)(2,1)S(1)}, u32[]{:S(2)}, u32[]{:S(2)}) %all-to-all-start) | async-done | bytes 458784 | tf_op jit(solution)/shard_map/all_to_all | solution.py:129
  34.7 3.7 %collective-permute-start = (bf16[8,1,1,32,256]{4,3,2,0,1:T(8,128)(2,1)S(1)}, bf16[8,1,1,32,256]{4,3,2,0,1:T(8,128)(2,1)S(1)}, u32[]{:S(2)}, u32[]{:S(2)}) collective-permute-start(bf16[8,1,1,32,256]{4,3,2,0,1:T(8,128)(2,1)S(1)} %get-tuple-element.44), channel_id=1, source_target_pairs={{0,1},{1,2},{2,3},{3,4},{4,5},{5,6},{6,7},{7,8},{8,9},{9,10},{10,1... | collective-permute-start | bytes 393224 | tf_op jit(solution)/shard_map/ppermute | solution.py:16
  38.4 1.9 collective-permute-start.1
  48.4 4.0 %collective-permute-start.2 = (bf16[8,1,2,32,256]{4,3,2,0,1:T(8,128)(2,1)S(1)}, bf16[8,1,2,32,256]{4,3,2,0,1:T(8,128)(2,1)S(1)}, u32[]{:S(2)}, u32[]{:S(2)}) collective-permute-start(bf16[8,1,2,32,256]{4,3,2,0,1:T(8,128)(2,1)S(1)} %bitcast.2045), channel_id=1, source_target_pairs={{0,64},{64,128},{128,192},{192,256},{256,320},{320,384},{384,448},... | collective-permute-start | bytes 786440 | tf_op jit(solution)/shard_map/ppermute | solution.py:16
  52.6 2.2 collective-permute-done.3
  57.0 3.8 %collective-permute-start.5 = (bf16[1,2,32,256]{3,2,1,0:T(8,128)(2,1)S(1)}, bf16[1,2,32,256]{3,2,1,0:T(8,128)(2,1)S(1)}, u32[]{:S(2)}, u32[]{:S(2)}) collective-permute-start(bf16[1,2,32,256]{3,2,1,0:T(8,128)(2,1)S(1)} %fusion.85), channel_id=1, source_target_pairs={{0,64},{64,128},{128,192},{192,256},{256,320},{320,384},{384,448},... | collective-permute-start | bytes 98312 | tf_op jit(solution)/shard_map/ppermute | solution.py:16
  63.0 2.5 collective-permute-done.4
  67.3 7.1 %collective-permute-start.6 = (bf16[1,1,32,256]{3,2,1,0:T(8,128)(2,1)S(1)}, bf16[1,1,32,256]{3,2,1,0:T(8,128)(2,1)S(1)}, u32[]{:S(2)}, u32[]{:S(2)}) collective-permute-start(bf16[1,1,32,256]{3,2,1,0:T(8,128)(2,1)S(1)} %get-tuple-element.59), channel_id=1, source_target_pairs={{0,1},{1,2},{2,3},{3,4},{4,5},{5,6},{6,7},{7,8},{8,9},{9,10},{10,1... | collective-permute-start | bytes 49160 | tf_op jit(solution)/shard_map/ppermute | solution.py:16
  74.4 1.9 collective-permute-start.7
  76.5 2.9 %collective-permute-done.7 = bf16[1,1,32,256]{3,2,1,0:T(8,128)(2,1)S(1)} collective-permute-done((bf16[1,1,32,256]{3,2,1,0:T(8,128)(2,1)S(1)}, bf16[1,1,32,256]{3,2,1,0:T(8,128)(2,1)S(1)}, u32[]{:S(2)}, u32[]{:S(2)}) %collective-permute-start.7) | collective-permute-done | bytes 16416 | tf_op jit(solution)/shard_map/ppermute | solution.py:19
  81.2 2.2 collective-permute-start.9
  85.6 2.5 collective-permute-done.8
  89.9 3.4 %collective-permute-start.10 = (bf16[1,1,32,256]{3,2,1,0:T(8,128)(2,1)S(1)}, bf16[1,1,32,256]{3,2,1,0:T(8,128)(2,1)S(1)}, u32[]{:S(2)}, u32[]{:S(2)}) collective-permute-start(bf16[1,1,32,256]{3,2,1,0:T(8,128)(2,1)S(1)} %get-tuple-element.57), channel_id=1, source_target_pairs={{0,1},{1,2},{2,3},{3,4},{4,5},{5,6},{6,7},{7,8},{8,9},{9,10},{10,1... | collective-permute-start | bytes 49160 | tf_op jit(solution)/shard_map/ppermute | solution.py:16
  93.3 1.9 collective-permute-start.11
  95.4 2.9 %collective-permute-done.11 = bf16[1,1,32,256]{3,2,1,0:T(8,128)(2,1)S(1)} collective-permute-done((bf16[1,1,32,256]{3,2,1,0:T(8,128)(2,1)S(1)}, bf16[1,1,32,256]{3,2,1,0:T(8,128)(2,1)S(1)}, u32[]{:S(2)}, u32[]{:S(2)}) %collective-permute-start.11) | collective-permute-done | bytes 16416 | tf_op jit(solution)/shard_map/ppermute | solution.py:19
  100.2 3.8 %collective-permute-start.13 = (bf16[1,2,32,256]{3,2,1,0:T(8,128)(2,1)S(1)}, bf16[1,2,32,256]{3,2,1,0:T(8,128)(2,1)S(1)}, u32[]{:S(2)}, u32[]{:S(2)}) collective-permute-start(bf16[1,2,32,256]{3,2,1,0:T(8,128)(2,1)S(1)} %get-tuple-element.63), channel_id=1, source_target_pairs={{0,64},{64,128},{128,192},{192,256},{256,320},{320,384},{384,448},... | collective-permute-start | bytes 98312 | tf_op jit(solution)/shard_map/ppermute | solution.py:16
  106.1 2.8 collective-permute-done.12
  110.7 3.1 %collective-permute-start.14 = (bf16[1,1,32,256]{3,2,1,0:T(8,128)(2,1)S(1)}, bf16[1,1,32,256]{3,2,1,0:T(8,128)(2,1)S(1)}, u32[]{:S(2)}, u32[]{:S(2)}) collective-permute-start(bf16[1,1,32,256]{3,2,1,0:T(8,128)(2,1)S(1)} %get-tuple-element.55), channel_id=1, source_target_pairs={{0,1},{1,2},{2,3},{3,4},{4,5},{5,6},{6,7},{7,8},{8,9},{9,10},{10,1... | collective-permute-start | bytes 49160 | tf_op jit(solution)/shard_map/ppermute | solution.py:16
  113.8 1.9 collective-permute-start.15
  115.9 2.9 %collective-permute-done.15 = bf16[1,1,32,256]{3,2,1,0:T(8,128)(2,1)S(1)} collective-permute-done((bf16[1,1,32,256]{3,2,1,0:T(8,128)(2,1)S(1)}, bf16[1,1,32,256]{3,2,1,0:T(8,128)(2,1)S(1)}, u32[]{:S(2)}, u32[]{:S(2)}) %collective-permute-start.15) | collective-permute-done | bytes 16416 | tf_op jit(solution)/shard_map/ppermute | solution.py:19
  120.6 3.6 %collective-permute-start.17 = (bf16[1,2,32,256]{3,2,1,0:T(8,128)(2,1)S(1)}, bf16[1,2,32,256]{3,2,1,0:T(8,128)(2,1)S(1)}, u32[]{:S(2)}, u32[]{:S(2)}) collective-permute-start(bf16[1,2,32,256]{3,2,1,0:T(8,128)(2,1)S(1)} %get-tuple-element.65), channel_id=1, source_target_pairs={{0,64},{64,128},{128,192},{192,256},{256,320},{320,384},{384,448},... | collective-permute-start | bytes 98312 | tf_op jit(solution)/shard_map/ppermute | solution.py:16
  126.5 2.5 collective-permute-done.16
  130.8 3.4 %collective-permute-start.18 = (bf16[1,1,32,256]{3,2,1,0:T(8,128)(2,1)S(1)}, bf16[1,1,32,256]{3,2,1,0:T(8,128)(2,1)S(1)}, u32[]{:S(2)}, u32[]{:S(2)}) collective-permute-start(bf16[1,1,32,256]{3,2,1,0:T(8,128)(2,1)S(1)} %get-tuple-element.53), channel_id=1, source_target_pairs={{0,1},{1,2},{2,3},{3,4},{4,5},{5,6},{6,7},{7,8},{8,9},{9,10},{10,1... | collective-permute-start | bytes 49160 | tf_op jit(solution)/shard_map/ppermute | solution.py:16
  134.2 1.9 collective-permute-start.19
  136.3 2.9 %collective-permute-done.19 = bf16[1,1,32,256]{3,2,1,0:T(8,128)(2,1)S(1)} collective-permute-done((bf16[1,1,32,256]{3,2,1,0:T(8,128)(2,1)S(1)}, bf16[1,1,32,256]{3,2,1,0:T(8,128)(2,1)S(1)}, u32[]{:S(2)}, u32[]{:S(2)}) %collective-permute-start.19) | collective-permute-done | bytes 16416 | tf_op jit(solution)/shard_map/ppermute | solution.py:19
  141.0 2.9 %collective-permute-start.21 = (bf16[1,2,32,256]{3,2,1,0:T(8,128)(2,1)S(1)}, bf16[1,2,32,256]{3,2,1,0:T(8,128)(2,1)S(1)}, u32[]{:S(2)}, u32[]{:S(2)}) collective-permute-start(bf16[1,2,32,256]{3,2,1,0:T(8,128)(2,1)S(1)} %get-tuple-element.67), channel_id=1, source_target_pairs={{0,64},{64,128},{128,192},{192,256},{256,320},{320,384},{384,448},... | collective-permute-start | bytes 98312 | tf_op jit(solution)/shard_map/ppermute | solution.py:16
  146.0 2.5 collective-permute-done.20
  150.4 3.4 %collective-permute-start.22 = (bf16[1,1,32,256]{3,2,1,0:T(8,128)(2,1)S(1)}, bf16[1,1,32,256]{3,2,1,0:T(8,128)(2,1)S(1)}, u32[]{:S(2)}, u32[]{:S(2)}) collective-permute-start(bf16[1,1,32,256]{3,2,1,0:T(8,128)(2,1)S(1)} %get-tuple-element.51), channel_id=1, source_target_pairs={{0,1},{1,2},{2,3},{3,4},{4,5},{5,6},{6,7},{7,8},{8,9},{9,10},{10,1... | collective-permute-start | bytes 49160 | tf_op jit(solution)/shard_map/ppermute | solution.py:16
  153.7 2.1 collective-permute-start.23
  156.0 2.8 collective-permute-done.23
  160.6 2.9 %collective-permute-start.25 = (bf16[1,2,32,256]{3,2,1,0:T(8,128)(2,1)S(1)}, bf16[1,2,32,256]{3,2,1,0:T(8,128)(2,1)S(1)}, u32[]{:S(2)}, u32[]{:S(2)}) collective-permute-start(bf16[1,2,32,256]{3,2,1,0:T(8,128)(2,1)S(1)} %get-tuple-element.69), channel_id=1, source_target_pairs={{0,64},{64,128},{128,192},{192,256},{256,320},{320,384},{384,448},... | collective-permute-start | bytes 98312 | tf_op jit(solution)/shard_map/ppermute | solution.py:16
  165.6 2.5 collective-permute-done.24
  169.9 3.8 %collective-permute-start.26 = (bf16[1,1,32,256]{3,2,1,0:T(8,128)(2,1)S(1)}, bf16[1,1,32,256]{3,2,1,0:T(8,128)(2,1)S(1)}, u32[]{:S(2)}, u32[]{:S(2)}) collective-permute-start(bf16[1,1,32,256]{3,2,1,0:T(8,128)(2,1)S(1)} %get-tuple-element.49), channel_id=1, source_target_pairs={{0,1},{1,2},{2,3},{3,4},{4,5},{5,6},{6,7},{7,8},{8,9},{9,10},{10,1... | collective-permute-start | bytes 49160 | tf_op jit(solution)/shard_map/ppermute | solution.py:16
  175.9 2.9 %collective-permute-done.27 = bf16[1,1,32,256]{3,2,1,0:T(8,128)(2,1)S(1)} collective-permute-done((bf16[1,1,32,256]{3,2,1,0:T(8,128)(2,1)S(1)}, bf16[1,1,32,256]{3,2,1,0:T(8,128)(2,1)S(1)}, u32[]{:S(2)}, u32[]{:S(2)}) %collective-permute-start.27) | collective-permute-done | bytes 16416 | tf_op jit(solution)/shard_map/ppermute | solution.py:19
  180.6 2.9 %collective-permute-start.29 = (bf16[1,2,32,256]{3,2,1,0:T(8,128)(2,1)S(1)}, bf16[1,2,32,256]{3,2,1,0:T(8,128)(2,1)S(1)}, u32[]{:S(2)}, u32[]{:S(2)}) collective-permute-start(bf16[1,2,32,256]{3,2,1,0:T(8,128)(2,1)S(1)} %get-tuple-element.71), channel_id=1, source_target_pairs={{0,64},{64,128},{128,192},{192,256},{256,320},{320,384},{384,448},... | collective-permute-start | bytes 98312 | tf_op jit(solution)/shard_map/ppermute | solution.py:16
  185.6 2.5 collective-permute-done.28
  190.0 4.6 %collective-permute-start.30 = (bf16[1,1,32,256]{3,2,1,0:T(8,128)(2,1)S(1)}, bf16[1,1,32,256]{3,2,1,0:T(8,128)(2,1)S(1)}, u32[]{:S(2)}, u32[]{:S(2)}) collective-permute-start(bf16[1,1,32,256]{3,2,1,0:T(8,128)(2,1)S(1)} %get-tuple-element.47), channel_id=1, source_target_pairs={{0,1},{1,2},{2,3},{3,4},{4,5},{5,6},{6,7},{7,8},{8,9},{9,10},{10,1... | collective-permute-start | bytes 49160 | tf_op jit(solution)/shard_map/ppermute | solution.py:16
  196.7 2.9 %collective-permute-done.31 = bf16[1,1,32,256]{3,2,1,0:T(8,128)(2,1)S(1)} collective-permute-done((bf16[1,1,32,256]{3,2,1,0:T(8,128)(2,1)S(1)}, bf16[1,1,32,256]{3,2,1,0:T(8,128)(2,1)S(1)}, u32[]{:S(2)}, u32[]{:S(2)}) %collective-permute-start.31) | collective-permute-done | bytes 16416 | tf_op jit(solution)/shard_map/ppermute | solution.py:19
  201.4 2.9 %collective-permute-start.33 = (bf16[1,2,32,256]{3,2,1,0:T(8,128)(2,1)S(1)}, bf16[1,2,32,256]{3,2,1,0:T(8,128)(2,1)S(1)}, u32[]{:S(2)}, u32[]{:S(2)}) collective-permute-start(bf16[1,2,32,256]{3,2,1,0:T(8,128)(2,1)S(1)} %get-tuple-element.73), channel_id=1, source_target_pairs={{0,64},{64,128},{128,192},{192,256},{256,320},{320,384},{384,448},... | collective-permute-start | bytes 98312 | tf_op jit(solution)/shard_map/ppermute | solution.py:16
  206.7 2.2 collective-permute-done.32
  211.6 4.6 %collective-permute-start.34 = (bf16[1,1,32,256]{3,2,1,0:T(8,128)(2,1)S(1)}, bf16[1,1,32,256]{3,2,1,0:T(8,128)(2,1)S(1)}, u32[]{:S(2)}, u32[]{:S(2)}) collective-permute-start(bf16[1,1,32,256]{3,2,1,0:T(8,128)(2,1)S(1)} %get-tuple-element.45), channel_id=1, source_target_pairs={{0,1},{1,2},{2,3},{3,4},{4,5},{5,6},{6,7},{7,8},{8,9},{9,10},{10,1... | collective-permute-start | bytes 49160 | tf_op jit(solution)/shard_map/ppermute | solution.py:16
  219.3 3.5 %all-to-all-start.1 = ((f32[8,1,12288]{2,1,0:T(1,128)}), f32[8,1,12288]{2,1,0:T(1,128)S(1)}, u32[]{:S(2)}, u32[]{:S(2)}) async-start(f32[8,1,12288]{2,1,0:T(1,128)} %maximum_multiply_fusion), calls=%async_computation.1 | async-start | bytes 786432 | tf_op jit(solution)/shard_map/all_to_all | solution.py:165
  224.3 11.8 %all-to-all-done.1 = f32[8,1,12288]{2,1,0:T(1,128)S(1)} async-done(((f32[8,1,12288]{2,1,0:T(1,128)}), f32[8,1,12288]{2,1,0:T(1,128)S(1)}, u32[]{:S(2)}, u32[]{:S(2)}) %all-to-all-start.1) | async-done | bytes 393248 | tf_op jit(solution)/shard_map/all_to_all | solution.py:165
  237.1 21.0 %all-to-all-start.2 = ((f32[64,1,192]{2,1,0:T(1,128)}), f32[64,1,192]{2,1,0:T(1,128)S(1)}, u32[]{:S(2)}, u32[]{:S(2)}) async-start(f32[64,1,192]{2,1,0:T(1,128)} %all_to_all.26), calls=%async_computation.2 | async-start | bytes 131072 | tf_op jit(solution)/shard_map/all_to_all | solution.py:170
  258.2 9.6 %all-to-all-done.2 = f32[64,1,192]{2,1,0:T(1,128)S(1)} async-done(((f32[64,1,192]{2,1,0:T(1,128)}), f32[64,1,192]{2,1,0:T(1,128)S(1)}, u32[]{:S(2)}, u32[]{:S(2)}) %all-to-all-start.2) | async-done | bytes 49184 | tf_op jit(solution)/shard_map/all_to_all | solution.py:170
  268.6 4.4 %all-to-all-start.3 = ((f32[64,1,192]{2,1,0:T(1,128)}), f32[64,1,192]{2,1,0:T(1,128)S(1)}, u32[]{:S(2)}, u32[]{:S(2)}) async-start(f32[64,1,192]{2,1,0:T(1,128)} %broadcast_in_dim.21), calls=%async_computation.3 | async-start | bytes 131072 | tf_op jit(solution)/shard_map/all_to_all | solution.py:171
  273.8 9.1 %all-to-all-done.3 = f32[64,1,192]{2,1,0:T(1,128)S(1)} async-done(((f32[64,1,192]{2,1,0:T(1,128)}), f32[64,1,192]{2,1,0:T(1,128)S(1)}, u32[]{:S(2)}, u32[]{:S(2)}) %all-to-all-start.3) | async-done | bytes 49184 | tf_op jit(solution)/shard_map/all_to_all | solution.py:171
  (385 shorter events, 77.0 us)
Async XLA Ops:
  0.6 1.1 copy-start.1
  1.8 0.7 copy-start.2
  5.4 27.3 %all-to-all-start = ((bf16[8,2,14336]{2,1,0:T(2,128)(2,1)}), bf16[8,2,14336]{2,1,0:T(2,128)(2,1)S(1)}, u32[]{:S(2)}, u32[]{:S(2)}) async-start(bf16[8,2,14336]{2,1,0:T(2,128)(2,1)} %reshape.1683), calls=%async_computation | async-start | bytes 917504 | tf_op jit(solution)/shard_map/all_to_all | solution.py:129
  16.3 0.7 copy-start.3
  34.7 9.2 %collective-permute-start = (bf16[8,1,1,32,256]{4,3,2,0,1:T(8,128)(2,1)S(1)}, bf16[8,1,1,32,256]{4,3,2,0,1:T(8,128)(2,1)S(1)}, u32[]{:S(2)}, u32[]{:S(2)}) collective-permute-start(bf16[8,1,1,32,256]{4,3,2,0,1:T(8,128)(2,1)S(1)} %get-tuple-element.44), channel_id=1, source_target_pairs={{0,1},{1,2},{2,3},{3,4},{4,5},{5,6},{6,7},{7,8},{8,9},{9,10},{10,1... | collective-permute-start | bytes 393224 | tf_op jit(solution)/shard_map/ppermute | solution.py:16
  38.4 6.3 %collective-permute-start.1 = (bf16[8,1,1,32,256]{4,3,2,0,1:T(8,128)(2,1)S(1)}, bf16[8,1,1,32,256]{4,3,2,0,1:T(8,128)(2,1)S(1)}, u32[]{:S(2)}, u32[]{:S(2)}) collective-permute-start(bf16[8,1,1,32,256]{4,3,2,0,1:T(8,128)(2,1)S(1)} %get-tuple-element.43), channel_id=1, source_target_pairs={{1,0},{2,1},{3,2},{4,3},{5,4},{6,5},{7,6},{8,7},{9,8},{10,9},{11,1... | collective-permute-start | bytes 393224 | tf_op jit(solution)/shard_map/ppermute | solution.py:19
  47.1 7.8 %collective-permute-start.3 = (bf16[8,1,2,32,256]{4,3,2,0,1:T(8,128)(2,1)S(1)}, bf16[8,1,2,32,256]{4,3,2,0,1:T(8,128)(2,1)S(1)}, u32[]{:S(2)}, u32[]{:S(2)}) collective-permute-start(bf16[8,1,2,32,256]{4,3,2,0,1:T(8,128)(2,1)S(1)} %bitcast.2044), channel_id=1, source_target_pairs={{64,0},{128,64},{192,128},{256,192},{320,256},{384,320},{448,384},... | collective-permute-start | bytes 786440 | tf_op jit(solution)/shard_map/ppermute | solution.py:19
  48.4 8.2 %collective-permute-start.2 = (bf16[8,1,2,32,256]{4,3,2,0,1:T(8,128)(2,1)S(1)}, bf16[8,1,2,32,256]{4,3,2,0,1:T(8,128)(2,1)S(1)}, u32[]{:S(2)}, u32[]{:S(2)}) collective-permute-start(bf16[8,1,2,32,256]{4,3,2,0,1:T(8,128)(2,1)S(1)} %bitcast.2045), channel_id=1, source_target_pairs={{0,64},{64,128},{128,192},{192,256},{256,320},{320,384},{384,448},... | collective-permute-start | bytes 786440 | tf_op jit(solution)/shard_map/ppermute | solution.py:16
  55.0 1.9 copy-start
  57.0 5.8 %collective-permute-start.5 = (bf16[1,2,32,256]{3,2,1,0:T(8,128)(2,1)S(1)}, bf16[1,2,32,256]{3,2,1,0:T(8,128)(2,1)S(1)}, u32[]{:S(2)}, u32[]{:S(2)}) collective-permute-start(bf16[1,2,32,256]{3,2,1,0:T(8,128)(2,1)S(1)} %fusion.85), channel_id=1, source_target_pairs={{0,64},{64,128},{128,192},{192,256},{256,320},{320,384},{384,448},... | collective-permute-start | bytes 98312 | tf_op jit(solution)/shard_map/ppermute | solution.py:16
  60.8 4.7 %collective-permute-start.4 = (bf16[1,2,32,256]{3,2,1,0:T(8,128)(2,1)S(1)}, bf16[1,2,32,256]{3,2,1,0:T(8,128)(2,1)S(1)}, u32[]{:S(2)}, u32[]{:S(2)}) collective-permute-start(bf16[1,2,32,256]{3,2,1,0:T(8,128)(2,1)S(1)} %fusion.85), channel_id=1, source_target_pairs={{64,0},{128,64},{192,128},{256,192},{320,256},{384,320},{448,384},... | collective-permute-start | bytes 98312 | tf_op jit(solution)/shard_map/ppermute | solution.py:19
  67.3 9.2 %collective-permute-start.6 = (bf16[1,1,32,256]{3,2,1,0:T(8,128)(2,1)S(1)}, bf16[1,1,32,256]{3,2,1,0:T(8,128)(2,1)S(1)}, u32[]{:S(2)}, u32[]{:S(2)}) collective-permute-start(bf16[1,1,32,256]{3,2,1,0:T(8,128)(2,1)S(1)} %get-tuple-element.59), channel_id=1, source_target_pairs={{0,1},{1,2},{2,3},{3,4},{4,5},{5,6},{6,7},{7,8},{8,9},{9,10},{10,1... | collective-permute-start | bytes 49160 | tf_op jit(solution)/shard_map/ppermute | solution.py:16
  74.4 5.1 %collective-permute-start.7 = (bf16[1,1,32,256]{3,2,1,0:T(8,128)(2,1)S(1)}, bf16[1,1,32,256]{3,2,1,0:T(8,128)(2,1)S(1)}, u32[]{:S(2)}, u32[]{:S(2)}) collective-permute-start(bf16[1,1,32,256]{3,2,1,0:T(8,128)(2,1)S(1)} %get-tuple-element.60), channel_id=1, source_target_pairs={{1,0},{2,1},{3,2},{4,3},{5,4},{6,5},{7,6},{8,7},{9,8},{10,9},{11,1... | collective-permute-start | bytes 49160 | tf_op jit(solution)/shard_map/ppermute | solution.py:19
  81.2 4.2 %collective-permute-start.9 = (bf16[1,2,32,256]{3,2,1,0:T(8,128)(2,1)S(1)}, bf16[1,2,32,256]{3,2,1,0:T(8,128)(2,1)S(1)}, u32[]{:S(2)}, u32[]{:S(2)}) collective-permute-start(bf16[1,2,32,256]{3,2,1,0:T(8,128)(2,1)S(1)} %get-tuple-element.61), channel_id=1, source_target_pairs={{0,64},{64,128},{128,192},{192,256},{256,320},{320,384},{384,448},... | collective-permute-start | bytes 98312 | tf_op jit(solution)/shard_map/ppermute | solution.py:16
  83.4 4.7 %collective-permute-start.8 = (bf16[1,2,32,256]{3,2,1,0:T(8,128)(2,1)S(1)}, bf16[1,2,32,256]{3,2,1,0:T(8,128)(2,1)S(1)}, u32[]{:S(2)}, u32[]{:S(2)}) collective-permute-start(bf16[1,2,32,256]{3,2,1,0:T(8,128)(2,1)S(1)} %get-tuple-element.61), channel_id=1, source_target_pairs={{64,0},{128,64},{192,128},{256,192},{320,256},{384,320},{448,384},... | collective-permute-start | bytes 98312 | tf_op jit(solution)/shard_map/ppermute | solution.py:19
  89.9 5.5 %collective-permute-start.10 = (bf16[1,1,32,256]{3,2,1,0:T(8,128)(2,1)S(1)}, bf16[1,1,32,256]{3,2,1,0:T(8,128)(2,1)S(1)}, u32[]{:S(2)}, u32[]{:S(2)}) collective-permute-start(bf16[1,1,32,256]{3,2,1,0:T(8,128)(2,1)S(1)} %get-tuple-element.57), channel_id=1, source_target_pairs={{0,1},{1,2},{2,3},{3,4},{4,5},{5,6},{6,7},{7,8},{8,9},{9,10},{10,1... | collective-permute-start | bytes 49160 | tf_op jit(solution)/shard_map/ppermute | solution.py:16
  93.3 5.1 %collective-permute-start.11 = (bf16[1,1,32,256]{3,2,1,0:T(8,128)(2,1)S(1)}, bf16[1,1,32,256]{3,2,1,0:T(8,128)(2,1)S(1)}, u32[]{:S(2)}, u32[]{:S(2)}) collective-permute-start(bf16[1,1,32,256]{3,2,1,0:T(8,128)(2,1)S(1)} %get-tuple-element.58), channel_id=1, source_target_pairs={{1,0},{2,1},{3,2},{4,3},{5,4},{6,5},{7,6},{8,7},{9,8},{10,9},{11,1... | collective-permute-start | bytes 49160 | tf_op jit(solution)/shard_map/ppermute | solution.py:19
  100.2 5.8 %collective-permute-start.13 = (bf16[1,2,32,256]{3,2,1,0:T(8,128)(2,1)S(1)}, bf16[1,2,32,256]{3,2,1,0:T(8,128)(2,1)S(1)}, u32[]{:S(2)}, u32[]{:S(2)}) collective-permute-start(bf16[1,2,32,256]{3,2,1,0:T(8,128)(2,1)S(1)} %get-tuple-element.63), channel_id=1, source_target_pairs={{0,64},{64,128},{128,192},{192,256},{256,320},{320,384},{384,448},... | collective-permute-start | bytes 98312 | tf_op jit(solution)/shard_map/ppermute | solution.py:16
  103.9 4.9 %collective-permute-start.12 = (bf16[1,2,32,256]{3,2,1,0:T(8,128)(2,1)S(1)}, bf16[1,2,32,256]{3,2,1,0:T(8,128)(2,1)S(1)}, u32[]{:S(2)}, u32[]{:S(2)}) collective-permute-start(bf16[1,2,32,256]{3,2,1,0:T(8,128)(2,1)S(1)} %get-tuple-element.63), channel_id=1, source_target_pairs={{64,0},{128,64},{192,128},{256,192},{320,256},{384,320},{448,384},... | collective-permute-start | bytes 98312 | tf_op jit(solution)/shard_map/ppermute | solution.py:19
  110.7 5.2 %collective-permute-start.14 = (bf16[1,1,32,256]{3,2,1,0:T(8,128)(2,1)S(1)}, bf16[1,1,32,256]{3,2,1,0:T(8,128)(2,1)S(1)}, u32[]{:S(2)}, u32[]{:S(2)}) collective-permute-start(bf16[1,1,32,256]{3,2,1,0:T(8,128)(2,1)S(1)} %get-tuple-element.55), channel_id=1, source_target_pairs={{0,1},{1,2},{2,3},{3,4},{4,5},{5,6},{6,7},{7,8},{8,9},{9,10},{10,1... | collective-permute-start | bytes 49160 | tf_op jit(solution)/shard_map/ppermute | solution.py:16
  113.8 5.1 %collective-permute-start.15 = (bf16[1,1,32,256]{3,2,1,0:T(8,128)(2,1)S(1)}, bf16[1,1,32,256]{3,2,1,0:T(8,128)(2,1)S(1)}, u32[]{:S(2)}, u32[]{:S(2)}) collective-permute-start(bf16[1,1,32,256]{3,2,1,0:T(8,128)(2,1)S(1)} %get-tuple-element.56), channel_id=1, source_target_pairs={{1,0},{2,1},{3,2},{4,3},{5,4},{6,5},{7,6},{8,7},{9,8},{10,9},{11,1... | collective-permute-start | bytes 49160 | tf_op jit(solution)/shard_map/ppermute | solution.py:19
  120.6 5.6 %collective-permute-start.17 = (bf16[1,2,32,256]{3,2,1,0:T(8,128)(2,1)S(1)}, bf16[1,2,32,256]{3,2,1,0:T(8,128)(2,1)S(1)}, u32[]{:S(2)}, u32[]{:S(2)}) collective-permute-start(bf16[1,2,32,256]{3,2,1,0:T(8,128)(2,1)S(1)} %get-tuple-element.65), channel_id=1, source_target_pairs={{0,64},{64,128},{128,192},{192,256},{256,320},{320,384},{384,448},... | collective-permute-start | bytes 98312 | tf_op jit(solution)/shard_map/ppermute | solution.py:16
  124.3 4.7 %collective-permute-start.16 = (bf16[1,2,32,256]{3,2,1,0:T(8,128)(2,1)S(1)}, bf16[1,2,32,256]{3,2,1,0:T(8,128)(2,1)S(1)}, u32[]{:S(2)}, u32[]{:S(2)}) collective-permute-start(bf16[1,2,32,256]{3,2,1,0:T(8,128)(2,1)S(1)} %get-tuple-element.65), channel_id=1, source_target_pairs={{64,0},{128,64},{192,128},{256,192},{320,256},{384,320},{448,384},... | collective-permute-start | bytes 98312 | tf_op jit(solution)/shard_map/ppermute | solution.py:19
  130.8 5.5 %collective-permute-start.18 = (bf16[1,1,32,256]{3,2,1,0:T(8,128)(2,1)S(1)}, bf16[1,1,32,256]{3,2,1,0:T(8,128)(2,1)S(1)}, u32[]{:S(2)}, u32[]{:S(2)}) collective-permute-start(bf16[1,1,32,256]{3,2,1,0:T(8,128)(2,1)S(1)} %get-tuple-element.53), channel_id=1, source_target_pairs={{0,1},{1,2},{2,3},{3,4},{4,5},{5,6},{6,7},{7,8},{8,9},{9,10},{10,1... | collective-permute-start | bytes 49160 | tf_op jit(solution)/shard_map/ppermute | solution.py:16
  134.2 5.1 %collective-permute-start.19 = (bf16[1,1,32,256]{3,2,1,0:T(8,128)(2,1)S(1)}, bf16[1,1,32,256]{3,2,1,0:T(8,128)(2,1)S(1)}, u32[]{:S(2)}, u32[]{:S(2)}) collective-permute-start(bf16[1,1,32,256]{3,2,1,0:T(8,128)(2,1)S(1)} %get-tuple-element.54), channel_id=1, source_target_pairs={{1,0},{2,1},{3,2},{4,3},{5,4},{6,5},{7,6},{8,7},{9,8},{10,9},{11,1... | collective-permute-start | bytes 49160 | tf_op jit(solution)/shard_map/ppermute | solution.py:19
  141.0 4.8 %collective-permute-start.21 = (bf16[1,2,32,256]{3,2,1,0:T(8,128)(2,1)S(1)}, bf16[1,2,32,256]{3,2,1,0:T(8,128)(2,1)S(1)}, u32[]{:S(2)}, u32[]{:S(2)}) collective-permute-start(bf16[1,2,32,256]{3,2,1,0:T(8,128)(2,1)S(1)} %get-tuple-element.67), channel_id=1, source_target_pairs={{0,64},{64,128},{128,192},{192,256},{256,320},{320,384},{384,448},... | collective-permute-start | bytes 98312 | tf_op jit(solution)/shard_map/ppermute | solution.py:16
  143.9 4.7 %collective-permute-start.20 = (bf16[1,2,32,256]{3,2,1,0:T(8,128)(2,1)S(1)}, bf16[1,2,32,256]{3,2,1,0:T(8,128)(2,1)S(1)}, u32[]{:S(2)}, u32[]{:S(2)}) collective-permute-start(bf16[1,2,32,256]{3,2,1,0:T(8,128)(2,1)S(1)} %get-tuple-element.67), channel_id=1, source_target_pairs={{64,0},{128,64},{192,128},{256,192},{320,256},{384,320},{448,384},... | collective-permute-start | bytes 98312 | tf_op jit(solution)/shard_map/ppermute | solution.py:19
  150.4 5.7 %collective-permute-start.22 = (bf16[1,1,32,256]{3,2,1,0:T(8,128)(2,1)S(1)}, bf16[1,1,32,256]{3,2,1,0:T(8,128)(2,1)S(1)}, u32[]{:S(2)}, u32[]{:S(2)}) collective-permute-start(bf16[1,1,32,256]{3,2,1,0:T(8,128)(2,1)S(1)} %get-tuple-element.51), channel_id=1, source_target_pairs={{0,1},{1,2},{2,3},{3,4},{4,5},{5,6},{6,7},{7,8},{8,9},{9,10},{10,1... | collective-permute-start | bytes 49160 | tf_op jit(solution)/shard_map/ppermute | solution.py:16
  153.7 5.1 %collective-permute-start.23 = (bf16[1,1,32,256]{3,2,1,0:T(8,128)(2,1)S(1)}, bf16[1,1,32,256]{3,2,1,0:T(8,128)(2,1)S(1)}, u32[]{:S(2)}, u32[]{:S(2)}) collective-permute-start(bf16[1,1,32,256]{3,2,1,0:T(8,128)(2,1)S(1)} %get-tuple-element.52), channel_id=1, source_target_pairs={{1,0},{2,1},{3,2},{4,3},{5,4},{6,5},{7,6},{8,7},{9,8},{10,9},{11,1... | collective-permute-start | bytes 49160 | tf_op jit(solution)/shard_map/ppermute | solution.py:19
  160.6 4.8 %collective-permute-start.25 = (bf16[1,2,32,256]{3,2,1,0:T(8,128)(2,1)S(1)}, bf16[1,2,32,256]{3,2,1,0:T(8,128)(2,1)S(1)}, u32[]{:S(2)}, u32[]{:S(2)}) collective-permute-start(bf16[1,2,32,256]{3,2,1,0:T(8,128)(2,1)S(1)} %get-tuple-element.69), channel_id=1, source_target_pairs={{0,64},{64,128},{128,192},{192,256},{256,320},{320,384},{384,448},... | collective-permute-start | bytes 98312 | tf_op jit(solution)/shard_map/ppermute | solution.py:16
  163.4 4.7 %collective-permute-start.24 = (bf16[1,2,32,256]{3,2,1,0:T(8,128)(2,1)S(1)}, bf16[1,2,32,256]{3,2,1,0:T(8,128)(2,1)S(1)}, u32[]{:S(2)}, u32[]{:S(2)}) collective-permute-start(bf16[1,2,32,256]{3,2,1,0:T(8,128)(2,1)S(1)} %get-tuple-element.69), channel_id=1, source_target_pairs={{64,0},{128,64},{192,128},{256,192},{320,256},{384,320},{448,384},... | collective-permute-start | bytes 98312 | tf_op jit(solution)/shard_map/ppermute | solution.py:19
  169.9 6.0 %collective-permute-start.26 = (bf16[1,1,32,256]{3,2,1,0:T(8,128)(2,1)S(1)}, bf16[1,1,32,256]{3,2,1,0:T(8,128)(2,1)S(1)}, u32[]{:S(2)}, u32[]{:S(2)}) collective-permute-start(bf16[1,1,32,256]{3,2,1,0:T(8,128)(2,1)S(1)} %get-tuple-element.49), channel_id=1, source_target_pairs={{0,1},{1,2},{2,3},{3,4},{4,5},{5,6},{6,7},{7,8},{8,9},{9,10},{10,1... | collective-permute-start | bytes 49160 | tf_op jit(solution)/shard_map/ppermute | solution.py:16
  173.8 5.1 %collective-permute-start.27 = (bf16[1,1,32,256]{3,2,1,0:T(8,128)(2,1)S(1)}, bf16[1,1,32,256]{3,2,1,0:T(8,128)(2,1)S(1)}, u32[]{:S(2)}, u32[]{:S(2)}) collective-permute-start(bf16[1,1,32,256]{3,2,1,0:T(8,128)(2,1)S(1)} %get-tuple-element.50), channel_id=1, source_target_pairs={{1,0},{2,1},{3,2},{4,3},{5,4},{6,5},{7,6},{8,7},{9,8},{10,9},{11,1... | collective-permute-start | bytes 49160 | tf_op jit(solution)/shard_map/ppermute | solution.py:19
  180.6 4.8 %collective-permute-start.29 = (bf16[1,2,32,256]{3,2,1,0:T(8,128)(2,1)S(1)}, bf16[1,2,32,256]{3,2,1,0:T(8,128)(2,1)S(1)}, u32[]{:S(2)}, u32[]{:S(2)}) collective-permute-start(bf16[1,2,32,256]{3,2,1,0:T(8,128)(2,1)S(1)} %get-tuple-element.71), channel_id=1, source_target_pairs={{0,64},{64,128},{128,192},{192,256},{256,320},{320,384},{384,448},... | collective-permute-start | bytes 98312 | tf_op jit(solution)/shard_map/ppermute | solution.py:16
  183.5 4.7 %collective-permute-start.28 = (bf16[1,2,32,256]{3,2,1,0:T(8,128)(2,1)S(1)}, bf16[1,2,32,256]{3,2,1,0:T(8,128)(2,1)S(1)}, u32[]{:S(2)}, u32[]{:S(2)}) collective-permute-start(bf16[1,2,32,256]{3,2,1,0:T(8,128)(2,1)S(1)} %get-tuple-element.71), channel_id=1, source_target_pairs={{64,0},{128,64},{192,128},{256,192},{320,256},{384,320},{448,384},... | collective-permute-start | bytes 98312 | tf_op jit(solution)/shard_map/ppermute | solution.py:19
  190.0 6.7 %collective-permute-start.30 = (bf16[1,1,32,256]{3,2,1,0:T(8,128)(2,1)S(1)}, bf16[1,1,32,256]{3,2,1,0:T(8,128)(2,1)S(1)}, u32[]{:S(2)}, u32[]{:S(2)}) collective-permute-start(bf16[1,1,32,256]{3,2,1,0:T(8,128)(2,1)S(1)} %get-tuple-element.47), channel_id=1, source_target_pairs={{0,1},{1,2},{2,3},{3,4},{4,5},{5,6},{6,7},{7,8},{8,9},{9,10},{10,1... | collective-permute-start | bytes 49160 | tf_op jit(solution)/shard_map/ppermute | solution.py:16
  194.5 5.1 %collective-permute-start.31 = (bf16[1,1,32,256]{3,2,1,0:T(8,128)(2,1)S(1)}, bf16[1,1,32,256]{3,2,1,0:T(8,128)(2,1)S(1)}, u32[]{:S(2)}, u32[]{:S(2)}) collective-permute-start(bf16[1,1,32,256]{3,2,1,0:T(8,128)(2,1)S(1)} %get-tuple-element.48), channel_id=1, source_target_pairs={{1,0},{2,1},{3,2},{4,3},{5,4},{6,5},{7,6},{8,7},{9,8},{10,9},{11,1... | collective-permute-start | bytes 49160 | tf_op jit(solution)/shard_map/ppermute | solution.py:19
  201.4 5.1 %collective-permute-start.33 = (bf16[1,2,32,256]{3,2,1,0:T(8,128)(2,1)S(1)}, bf16[1,2,32,256]{3,2,1,0:T(8,128)(2,1)S(1)}, u32[]{:S(2)}, u32[]{:S(2)}) collective-permute-start(bf16[1,2,32,256]{3,2,1,0:T(8,128)(2,1)S(1)} %get-tuple-element.73), channel_id=1, source_target_pairs={{0,64},{64,128},{128,192},{192,256},{256,320},{320,384},{384,448},... | collective-permute-start | bytes 98312 | tf_op jit(solution)/shard_map/ppermute | solution.py:16
  204.2 4.7 %collective-permute-start.32 = (bf16[1,2,32,256]{3,2,1,0:T(8,128)(2,1)S(1)}, bf16[1,2,32,256]{3,2,1,0:T(8,128)(2,1)S(1)}, u32[]{:S(2)}, u32[]{:S(2)}) collective-permute-start(bf16[1,2,32,256]{3,2,1,0:T(8,128)(2,1)S(1)} %get-tuple-element.73), channel_id=1, source_target_pairs={{64,0},{128,64},{192,128},{256,192},{320,256},{384,320},{448,384},... | collective-permute-start | bytes 98312 | tf_op jit(solution)/shard_map/ppermute | solution.py:19
  211.6 11.2 %collective-permute-start.34 = (bf16[1,1,32,256]{3,2,1,0:T(8,128)(2,1)S(1)}, bf16[1,1,32,256]{3,2,1,0:T(8,128)(2,1)S(1)}, u32[]{:S(2)}, u32[]{:S(2)}) collective-permute-start(bf16[1,1,32,256]{3,2,1,0:T(8,128)(2,1)S(1)} %get-tuple-element.45), channel_id=1, source_target_pairs={{0,1},{1,2},{2,3},{3,4},{4,5},{5,6},{6,7},{7,8},{8,9},{9,10},{10,1... | collective-permute-start | bytes 49160 | tf_op jit(solution)/shard_map/ppermute | solution.py:16
  216.2 6.6 %collective-permute-start.35 = (bf16[1,1,32,256]{3,2,1,0:T(8,128)(2,1)S(1)}, bf16[1,1,32,256]{3,2,1,0:T(8,128)(2,1)S(1)}, u32[]{:S(2)}, u32[]{:S(2)}) collective-permute-start(bf16[1,1,32,256]{3,2,1,0:T(8,128)(2,1)S(1)} %get-tuple-element.46), channel_id=1, source_target_pairs={{1,0},{2,1},{3,2},{4,3},{5,4},{6,5},{7,6},{8,7},{9,8},{10,9},{11,1... | collective-permute-start | bytes 49160 | tf_op jit(solution)/shard_map/ppermute | solution.py:19
  219.3 16.7 %all-to-all-start.1 = ((f32[8,1,12288]{2,1,0:T(1,128)}), f32[8,1,12288]{2,1,0:T(1,128)S(1)}, u32[]{:S(2)}, u32[]{:S(2)}) async-start(f32[8,1,12288]{2,1,0:T(1,128)} %maximum_multiply_fusion), calls=%async_computation.1 | async-start | bytes 786432 | tf_op jit(solution)/shard_map/all_to_all | solution.py:165
  237.1 30.7 %all-to-all-start.2 = ((f32[64,1,192]{2,1,0:T(1,128)}), f32[64,1,192]{2,1,0:T(1,128)S(1)}, u32[]{:S(2)}, u32[]{:S(2)}) async-start(f32[64,1,192]{2,1,0:T(1,128)} %all_to_all.26), calls=%async_computation.2 | async-start | bytes 131072 | tf_op jit(solution)/shard_map/all_to_all | solution.py:170
  268.6 14.3 %all-to-all-start.3 = ((f32[64,1,192]{2,1,0:T(1,128)}), f32[64,1,192]{2,1,0:T(1,128)S(1)}, u32[]{:S(2)}, u32[]{:S(2)}) async-start(f32[64,1,192]{2,1,0:T(1,128)} %broadcast_in_dim.21), calls=%async_computation.3 | async-start | bytes 131072 | tf_op jit(solution)/shard_map/all_to_all | solution.py:171

commit v3 on v2

--- a/solution.py
+++ b/solution.py
@@ -6,6 +6,7 @@
 from jax.sharding import PartitionSpec as P
 
 TILE = 128
+HALO = 8
 
 
 def padded_2(block, sides, width):
@@ -19,6 +20,23 @@
         high = lax.ppermute(lax.slice_in_dim(block, 0, width, axis=dim), axis, backward)
         block = jnp.concatenate([low, block, high], axis=dim)
     return block
+
+
+def passed_along(block, axis, distance):
+    devices = range(lax.axis_size(axis))
+    route = [(i - distance, i) for i in devices if i - distance in devices]
+    return lax.ppermute(block, axis, route)
+
+
+def halo_plan(layers, depth):
+    need = [0] * layers
+    left = 0
+    for layer in reversed(range(layers)):
+        if left == 0:
+            left = min(depth, layer + 1)
+        need[layer] = left
+        left -= 1
+    return need
 
 
 def width_pad(field):
@@ -145,19 +163,48 @@
     value = depth_conv_all(deep, depth_w, zs)
     factor = silu_slope(value) * mask_full[None]
 
-    grad = grad_out
+    need = halo_plan(layers, HALO)
+    reach = -(-max(need) // height)
+    factor_b = factor.astype(jnp.bfloat16)
+    lows, highs, picks = {}, {}, {}
+    for dist in range(1, reach + 1):
+        chosen = [layer for layer in range(layers) if need[layer] > height * (dist - 1)]
+        picks[dist] = chosen
+        load = jnp.stack([factor_b[layer] for layer in chosen] + [grad_out])
+        lows[dist] = passed_along(load, "gy", dist)
+        highs[dist] = passed_along(load, "gy", -dist)
+
+    def halo_of(index_of, h, own):
+        span = -(-h // height)
+        low = jnp.concatenate([index_of(lows[d], d) for d in range(span, 0, -1)], axis=1)[:, -h:]
+        high = jnp.concatenate([index_of(highs[d], d) for d in range(1, span + 1)], axis=1)[:, :h]
+        return low, high
+
+    def refreshed(grad, h):
+        span = -(-h // height)
+        low = jnp.concatenate([passed_along(grad, "gy", d) for d in range(span, 0, -1)], axis=1)
+        high = jnp.concatenate([passed_along(grad, "gy", -d) for d in range(1, span + 1)], axis=1)
+        return jnp.concatenate([low[:, low.shape[1] - h :], grad, high[:, :h]], axis=1)
+
+    low, high = halo_of(lambda part, d: part[-1], need[layers - 1], grad_out)
+    grad = jnp.concatenate([low, grad_out, high], axis=1)
     plane_list = [None] * layers
     depth_list = [None] * layers
     for layer in reversed(range(layers)):
-        grad_mix = (grad.astype(jnp.float32) * factor[layer]).astype(jnp.bfloat16)
+        h = need[layer]
+        if grad.shape[1] != height + 2 * h:
+            grad = refreshed(grad, h)
+        low, high = halo_of(lambda part, d: part[picks[d].index(layer)], h, None)
+        wide = jnp.concatenate([low.astype(jnp.float32), factor[layer], high.astype(jnp.float32)], axis=1)
+        grad_mix = (grad.astype(jnp.float32) * wide).astype(jnp.bfloat16)
         mix_deep = padded_2(grad_mix, (("segment", 0),), 1)
         grad_mid = depth_back(mix_deep, depth_w[layer], zs).astype(jnp.bfloat16)
-        rows_grad = padded_2(grad_mid, (("gy", 1),), 1)
+        rows = grad.shape[1] - 2
         grad = (
-            grad.astype(jnp.float32) + plane_back(rows_grad, plane_w[layer], height, width)
+            grad[:, 1:-1].astype(jnp.float32) + plane_back(grad_mid, plane_w[layer], rows, width)
         ).astype(jnp.bfloat16)
-        depth_list[layer] = depth_taps(grad_mix, deep[layer], zs)
-        plane_list[layer] = plane_taps(grad_mid, rows_own[layer], height, width)
+        depth_list[layer] = depth_taps(grad_mix[:, h : h + height], deep[layer], zs)
+        plane_list[layer] = plane_taps(grad_mid[:, h : h + height], rows_own[layer], height, width)
 
     planes = jnp.stack(plane_list).reshape(layers, -1)
     depths = jnp.stack(depth_list).reshape(layers, -1)

time: 286 us -> 315 us (1.10)
  local copies, waits for them, and re-layouts: 15.5 us -> 53.6 us
  starting transfers between devices: 135 us -> 120 us
  waiting for transfers between devices: 90.7 us -> 78.7 us
  matrix products: 37.5 us -> 48.5 us
  other arithmetic: 4.27 us -> 8.52 us
    ppermute x18 -> x10, starting transfers between devices: 65.8 us -> 35.8 us  [padded_2(): lax.ppermute(lax.slice_in_dim(block, block.shape[dim] - width, None, axis...]
    ppermute x0 -> x8, starting transfers between devices: none -> 26.4 us  [passed_along(): return lax.ppermute(block, axis, route)]
    ppermute x18 -> x10, waiting for transfers between devices: 43.2 us -> 25.7 us  [padded_2(): lax.ppermute(lax.slice_in_dim(block, 0, width, axis=dim), axis, backward)]
    unnamed x14 -> x122, local copies, waits for them, and re-layouts: 3.44 us -> 19.9 us
    ppermute x18 -> x10, starting transfers between devices: 29.1 us -> 13.9 us  [padded_2(): lax.ppermute(lax.slice_in_dim(block, 0, width, axis=dim), axis, backward)]
    squeeze x24, local copies, waits for them, and re-layouts: 1.89 us -> 15.5 us  [depth_back(): kernel[k]]
    squeeze x8, local copies, waits for them, and re-layouts: 0.77 us -> 5.78 us  [local(): plane_w[layer]]
    dot_general x24, matrix products: 4.56 us -> 8.65 us  [depth_back(): jnp.einsum('oc,zyox->zycx', kernel[k], mix_deep[2 - k:2 - k + depth], pre...]
  transfers between devices with their start and end apart: 40 -> 32, of which waited for: 22 -> 20; matrix products, arithmetic and copies ran while one was open for 6% -> 8% of each run, Pallas kernels for 0% -> 0%
where the time goes in v3:
time: 315 us; the launch traced here: 312 us
  starting transfers between devices  120 us (38%)
  waiting for transfers between devices  78.7 us (25%)
  local copies, waits for them, and re-layouts  53.6 us (17%)
  matrix products  48.5 us (15%)
  other arithmetic  8.52 us (3%)
    ppermute x10, starting transfers between devices, padded_2(): lax.ppermute(lax.slice_in_dim(block, block.shape[dim] - width, None, axis...  35.8 us
    ppermute x8, starting transfers between devices, passed_along(): return lax.ppermute(block, axis, route)  26.4 us
    ppermute x10, waiting for transfers between devices, padded_2(): lax.ppermute(lax.slice_in_dim(block, 0, width, axis=dim), axis, backward)  25.7 us
    all_to_all x1, starting transfers between devices, local(): part = lax.all_to_all(flat, 'gy', 0, 0, tiled=True).sum(axis=0)  23.3 us
    unnamed x122, local copies, waits for them, and re-layouts  19.9 us
    dot_general x72, matrix products, plane_back(): jnp.einsum('oc,...yox->...ycx', kernel[i, j], padded[..., 2 - i:2 - i + h...  17.9 us
    all_to_all x1, waiting for transfers between devices, local(): got = lax.all_to_all(send, 'segment', 0, 0, tiled=True)  15.5 us
    squeeze x24, local copies, waits for them, and re-layouts, depth_back(): kernel[k]  15.5 us
  transfers between devices with their start and end apart: 32, of which 20 were waited for; matrix products, arithmetic and copies ran while one was open for 8% of the time, Pallas kernels for 0%

profile of v3, /device:TPU:1, one launch (start us, length us, event | category | flops | bytes accessed | tf_op | source)
XLA Modules:
  0.0 311.9 jit_solution(7301749039874748186)
XLA Ops:
  6.4 10.9 %all-to-all-start = ((bf16[8,2,14336]{2,1,0:T(2,128)(2,1)}), bf16[8,2,14336]{2,1,0:T(2,128)(2,1)S(1)}, u32[]{:S(2)}, u32[]{:S(2)}) async-start(bf16[8,2,14336]{2,1,0:T(2,128)(2,1)} %reshape.2284), calls=%async_computation | async-start | bytes 917504 | tf_op jit(solution)/shard_map/all_to_all | solution.py:147
  18.2 15.5 %all-to-all-done = bf16[8,2,14336]{2,1,0:T(2,128)(2,1)S(1)} async-done(((bf16[8,2,14336]{2,1,0:T(2,128)(2,1)}), bf16[8,2,14336]{2,1,0:T(2,128)(2,1)S(1)}, u32[]{:S(2)}, u32[]{:S(2)}) %all-to-all-start) | async-done | bytes 458784 | tf_op jit(solution)/shard_map/all_to_all | solution.py:147
  50.9 3.7 %collective-permute-start = (bf16[8,1,1,32,256]{4,3,2,0,1:T(8,128)(2,1)S(1)}, bf16[8,1,1,32,256]{4,3,2,0,1:T(8,128)(2,1)S(1)}, u32[]{:S(2)}, u32[]{:S(2)}) collective-permute-start(bf16[8,1,1,32,256]{4,3,2,0,1:T(8,128)(2,1)S(1)} %get-tuple-element.68), channel_id=1, source_target_pairs={{0,1},{1,2},{2,3},{3,4},{4,5},{5,6},{6,7},{7,8},{8,9},{9,10},{10,1... | collective-permute-start | bytes 393224 | tf_op jit(solution)/shard_map/ppermute | solution.py:17
  61.1 1.9 collective-permute-start.1
  63.5 3.9 %collective-permute-done.1 = bf16[8,1,1,32,256]{4,3,2,0,1:T(8,128)(2,1)S(1)} collective-permute-done((bf16[8,1,1,32,256]{4,3,2,0,1:T(8,128)(2,1)S(1)}, bf16[8,1,1,32,256]{4,3,2,0,1:T(8,128)(2,1)S(1)}, u32[]{:S(2)}, u32[]{:S(2)}) %collective-permute-start.1) | collective-permute-done | bytes 131104 | tf_op jit(solution)/shard_map/ppermute | solution.py:20
  69.7 1.3 collective-permute-start.3
  71.0 4.0 %collective-permute-start.2 = (bf16[8,1,2,32,256]{4,3,2,0,1:T(8,128)(2,1)S(1)}, bf16[8,1,2,32,256]{4,3,2,0,1:T(8,128)(2,1)S(1)}, u32[]{:S(2)}, u32[]{:S(2)}) collective-permute-start(bf16[8,1,2,32,256]{4,3,2,0,1:T(8,128)(2,1)S(1)} %bitcast.2035), channel_id=1, source_target_pairs={{0,64},{64,128},{128,192},{192,256},{256,320},{320,384},{384,448},... | collective-permute-start | bytes 786440 | tf_op jit(solution)/shard_map/ppermute | solution.py:17
  75.3 1.8 collective-permute-done.3
  77.3 1.6 collective-permute-done.2
  80.0 1.3 collective-permute-start.11
  81.3 6.6 %collective-permute-start.4 = (bf16[3,1,2,32,256]{4,3,2,1,0:T(8,128)(2,1)S(1)}, bf16[3,1,2,32,256]{4,3,2,1,0:T(8,128)(2,1)S(1)}, u32[]{:S(2)}, u32[]{:S(2)}) collective-permute-start(bf16[3,1,2,32,256]{4,3,2,1,0:T(8,128)(2,1)S(1)} %pad_maximum_fusion.19), channel_id=1, source_target_pairs={{0,4},{1,5},{2,6},{3,7},{4,8},{5,9},{6,10},{7,11},{8,12},{9,13},{1... | collective-permute-start | bytes 294920 | tf_op jit(solution)/shard_map/ppermute | solution.py:28
  87.9 1.3 collective-permute-start.10
  89.2 6.4 %collective-permute-start.5 = (bf16[5,1,2,32,256]{4,3,2,1,0:T(8,128)(2,1)S(1)}, bf16[5,1,2,32,256]{4,3,2,1,0:T(8,128)(2,1)S(1)}, u32[]{:S(2)}, u32[]{:S(2)}) collective-permute-start(bf16[5,1,2,32,256]{4,3,2,1,0:T(8,128)(2,1)S(1)} %pad_maximum_fusion.4), channel_id=1, source_target_pairs={{0,3},{1,4},{2,5},{3,6},{4,7},{5,8},{6,9},{7,10},{8,11},{9,12},{10... | collective-permute-start | bytes 491528 | tf_op jit(solution)/shard_map/ppermute | solution.py:28
  96.3 1.3 collective-permute-start.9
  98.4 4.0 %collective-permute-start.6 = (bf16[7,1,2,32,256]{4,3,2,1,0:T(8,128)(2,1)S(1)}, bf16[7,1,2,32,256]{4,3,2,1,0:T(8,128)(2,1)S(1)}, u32[]{:S(2)}, u32[]{:S(2)}) collective-permute-start(bf16[7,1,2,32,256]{4,3,2,1,0:T(8,128)(2,1)S(1)} %pad_maximum_fusion.3), channel_id=1, source_target_pairs={{0,2},{1,3},{2,4},{3,5},{4,6},{5,7},{6,8},{7,9},{8,10},{9,11},{10,... | collective-permute-start | bytes 688136 | tf_op jit(solution)/shard_map/ppermute | solution.py:28
  102.5 1.9 collective-permute-start.8
  104.4 3.6 %collective-permute-start.7 = (bf16[9,1,2,32,256]{4,3,2,1,0:T(8,128)(2,1)S(1)}, bf16[9,1,2,32,256]{4,3,2,1,0:T(8,128)(2,1)S(1)}, u32[]{:S(2)}, u32[]{:S(2)}) collective-permute-start(bf16[9,1,2,32,256]{4,3,2,1,0:T(8,128)(2,1)S(1)} %pad_maximum_fusion), channel_id=1, source_target_pairs={{0,1},{1,2},{2,3},{3,4},{4,5},{5,6},{6,7},{7,8},{8,9},{9,10},{10,1... | collective-permute-start | bytes 884744 | tf_op jit(solution)/shard_map/ppermute | solution.py:28
  108.9 3.1 collective-permute-done.7
  115.1 4.5 %collective-permute-start.13 = (bf16[1,18,32,256]{3,2,1,0:T(8,128)(2,1)}, bf16[1,18,32,256]{3,2,1,0:T(8,128)(2,1)}, u32[]{:S(2)}, u32[]{:S(2)}) collective-permute-start(bf16[1,18,32,256]{3,2,1,0:T(8,128)(2,1)} %fusion.50), channel_id=1, source_target_pairs={{0,64},{64,128},{128,192},{192,256},{256,320},{320,384},{384,448},... | collective-permute-start | bytes 884744 | tf_op jit(solution)/shard_map/ppermute | solution.py:17
  119.7 1.3 collective-permute-start.12
  134.9 3.7 %collective-permute-start.15 = (bf16[1,16,32,256]{3,2,1,0:T(8,128)(2,1)S(1)}, bf16[1,16,32,256]{3,2,1,0:T(8,128)(2,1)S(1)}, u32[]{:S(2)}, u32[]{:S(2)}) collective-permute-start(bf16[1,16,32,256]{3,2,1,0:T(8,128)(2,1)S(1)} %get-tuple-element.99), channel_id=1, source_target_pairs={{0,64},{64,128},{128,192},{192,256},{256,320},{320,384},{384,448},... | collective-permute-start | bytes 786440 | tf_op jit(solution)/shard_map/ppermute | solution.py:17
  138.7 1.5 collective-permute-start.14
  142.8 3.9 %collective-permute-done.14 = bf16[1,16,32,256]{3,2,1,0:T(8,128)(2,1)} collective-permute-done((bf16[1,16,32,256]{3,2,1,0:T(8,128)(2,1)S(1)}, bf16[1,16,32,256]{3,2,1,0:T(8,128)(2,1)}, u32[]{:S(2)}, u32[]{:S(2)}) %collective-permute-start.14) | collective-permute-done | bytes 262176 | tf_op jit(solution)/shard_map/ppermute | solution.py:20
  153.5 2.3 collective-permute-start.17
  155.8 1.3 collective-permute-start.16
  159.2 1.5 collective-permute-done.17
  161.0 3.9 %collective-permute-done.16 = bf16[1,14,32,256]{3,2,1,0:T(8,128)(2,1)S(1)} collective-permute-done((bf16[1,14,32,256]{3,2,1,0:T(8,128)(2,1)S(1)}, bf16[1,14,32,256]{3,2,1,0:T(8,128)(2,1)S(1)}, u32[]{:S(2)}, u32[]{:S(2)}) %collective-permute-start.16) | collective-permute-done | bytes 229408 | tf_op jit(solution)/shard_map/ppermute | solution.py:20
  170.6 3.8 %collective-permute-start.19 = (bf16[1,12,32,256]{3,2,1,0:T(8,128)(2,1)S(1)}, bf16[1,12,32,256]{3,2,1,0:T(8,128)(2,1)S(1)}, u32[]{:S(2)}, u32[]{:S(2)}) collective-permute-start(bf16[1,12,32,256]{3,2,1,0:T(8,128)(2,1)S(1)} %get-tuple-element.103), channel_id=1, source_target_pairs={{0,64},{64,128},{128,192},{192,256},{256,320},{320,384},{384,448},... | collective-permute-start | bytes 589832 | tf_op jit(solution)/shard_map/ppermute | solution.py:17
  174.4 1.3 collective-permute-start.18
  177.1 1.7 collective-permute-done.19
  179.1 3.9 %collective-permute-done.18 = bf16[1,12,32,256]{3,2,1,0:T(8,128)(2,1)S(1)} collective-permute-done((bf16[1,12,32,256]{3,2,1,0:T(8,128)(2,1)S(1)}, bf16[1,12,32,256]{3,2,1,0:T(8,128)(2,1)S(1)}, u32[]{:S(2)}, u32[]{:S(2)}) %collective-permute-start.18) | collective-permute-done | bytes 196640 | tf_op jit(solution)/shard_map/ppermute | solution.py:20
  188.6 3.0 collective-permute-start.21
  191.7 1.3 collective-permute-start.20
  195.1 2.7 collective-permute-done.20
  203.3 3.6 %collective-permute-start.23 = (bf16[1,8,32,256]{3,2,1,0:T(8,128)(2,1)S(1)}, bf16[1,8,32,256]{3,2,1,0:T(8,128)(2,1)S(1)}, u32[]{:S(2)}, u32[]{:S(2)}) collective-permute-start(bf16[1,8,32,256]{3,2,1,0:T(8,128)(2,1)S(1)} %get-tuple-element.107), channel_id=1, source_target_pairs={{0,64},{64,128},{128,192},{192,256},{256,320},{320,384},{384,448},... | collective-permute-start | bytes 393224 | tf_op jit(solution)/shard_map/ppermute | solution.py:17
  207.0 1.3 collective-permute-start.22
  210.4 2.5 collective-permute-done.22
  218.3 3.4 %collective-permute-start.25 = (bf16[1,6,32,256]{3,2,1,0:T(8,128)(2,1)S(1)}, bf16[1,6,32,256]{3,2,1,0:T(8,128)(2,1)S(1)}, u32[]{:S(2)}, u32[]{:S(2)}) collective-permute-start(bf16[1,6,32,256]{3,2,1,0:T(8,128)(2,1)S(1)} %get-tuple-element.109), channel_id=1, source_target_pairs={{0,64},{64,128},{128,192},{192,256},{256,320},{320,384},{384,448},... | collective-permute-start | bytes 294920 | tf_op jit(solution)/shard_map/ppermute | solution.py:17
  221.8 1.3 collective-permute-start.24
  225.2 1.9 collective-permute-done.24
  232.4 3.6 %collective-permute-start.27 = (bf16[1,4,32,256]{3,2,1,0:T(8,128)(2,1)S(1)}, bf16[1,4,32,256]{3,2,1,0:T(8,128)(2,1)S(1)}, u32[]{:S(2)}, u32[]{:S(2)}) collective-permute-start(bf16[1,4,32,256]{3,2,1,0:T(8,128)(2,1)S(1)} %get-tuple-element.111), channel_id=1, source_target_pairs={{0,64},{64,128},{128,192},{192,256},{256,320},{320,384},{384,448},... | collective-permute-start | bytes 196616 | tf_op jit(solution)/shard_map/ppermute | solution.py:17
  236.0 1.5 collective-permute-start.26
  244.9 5.1 %all-to-all-start.1 = ((f32[8,1,12288]{2,1,0:T(1,128)}), f32[8,1,12288]{2,1,0:T(1,128)S(1)}, u32[]{:S(2)}, u32[]{:S(2)}) async-start(f32[8,1,12288]{2,1,0:T(1,128)} %maximum_multiply_fusion.5), calls=%async_computation.1 | async-start | bytes 786432 | tf_op jit(solution)/shard_map/all_to_all | solution.py:212
  251.4 9.4 %all-to-all-done.1 = f32[8,1,12288]{2,1,0:T(1,128)S(1)} async-done(((f32[8,1,12288]{2,1,0:T(1,128)}), f32[8,1,12288]{2,1,0:T(1,128)S(1)}, u32[]{:S(2)}, u32[]{:S(2)}) %all-to-all-start.1) | async-done | bytes 393248 | tf_op jit(solution)/shard_map/all_to_all | solution.py:212
  261.9 23.3 %all-to-all-start.2 = ((f32[64,1,192]{2,1,0:T(1,128)}), f32[64,1,192]{2,1,0:T(1,128)S(1)}, u32[]{:S(2)}, u32[]{:S(2)}) async-start(f32[64,1,192]{2,1,0:T(1,128)} %all_to_all.26), calls=%async_computation.2 | async-start | bytes 131072 | tf_op jit(solution)/shard_map/all_to_all | solution.py:217
  285.3 9.6 %all-to-all-done.2 = f32[64,1,192]{2,1,0:T(1,128)S(1)} async-done(((f32[64,1,192]{2,1,0:T(1,128)}), f32[64,1,192]{2,1,0:T(1,128)S(1)}, u32[]{:S(2)}, u32[]{:S(2)}) %all-to-all-start.2) | async-done | bytes 49184 | tf_op jit(solution)/shard_map/all_to_all | solution.py:217
  295.7 4.4 %all-to-all-start.3 = ((f32[64,1,192]{2,1,0:T(1,128)}), f32[64,1,192]{2,1,0:T(1,128)S(1)}, u32[]{:S(2)}, u32[]{:S(2)}) async-start(f32[64,1,192]{2,1,0:T(1,128)} %broadcast_in_dim.21), calls=%async_computation.3 | async-start | bytes 131072 | tf_op jit(solution)/shard_map/all_to_all | solution.py:218
  301.0 9.1 %all-to-all-done.3 = f32[64,1,192]{2,1,0:T(1,128)S(1)} async-done(((f32[64,1,192]{2,1,0:T(1,128)}), f32[64,1,192]{2,1,0:T(1,128)S(1)}, u32[]{:S(2)}, u32[]{:S(2)}) %all-to-all-start.3) | async-done | bytes 49184 | tf_op jit(solution)/shard_map/all_to_all | solution.py:218
  (495 shorter events, 113.4 us)
Async XLA Ops:
  6.4 27.3 %all-to-all-start = ((bf16[8,2,14336]{2,1,0:T(2,128)(2,1)}), bf16[8,2,14336]{2,1,0:T(2,128)(2,1)S(1)}, u32[]{:S(2)}, u32[]{:S(2)}) async-start(bf16[8,2,14336]{2,1,0:T(2,128)(2,1)} %reshape.2284), calls=%async_computation | async-start | bytes 917504 | tf_op jit(solution)/shard_map/all_to_all | solution.py:147
  50.9 12.6 %collective-permute-start = (bf16[8,1,1,32,256]{4,3,2,0,1:T(8,128)(2,1)S(1)}, bf16[8,1,1,32,256]{4,3,2,0,1:T(8,128)(2,1)S(1)}, u32[]{:S(2)}, u32[]{:S(2)}) collective-permute-start(bf16[8,1,1,32,256]{4,3,2,0,1:T(8,128)(2,1)S(1)} %get-tuple-element.68), channel_id=1, source_target_pairs={{0,1},{1,2},{2,3},{3,4},{4,5},{5,6},{6,7},{7,8},{8,9},{9,10},{10,1... | collective-permute-start | bytes 393224 | tf_op jit(solution)/shard_map/ppermute | solution.py:17
  61.1 6.3 %collective-permute-start.1 = (bf16[8,1,1,32,256]{4,3,2,0,1:T(8,128)(2,1)S(1)}, bf16[8,1,1,32,256]{4,3,2,0,1:T(8,128)(2,1)S(1)}, u32[]{:S(2)}, u32[]{:S(2)}) collective-permute-start(bf16[8,1,1,32,256]{4,3,2,0,1:T(8,128)(2,1)S(1)} %get-tuple-element.67), channel_id=1, source_target_pairs={{1,0},{2,1},{3,2},{4,3},{5,4},{6,5},{7,6},{8,7},{9,8},{10,9},{11,1... | collective-permute-start | bytes 393224 | tf_op jit(solution)/shard_map/ppermute | solution.py:20
  69.7 7.4 %collective-permute-start.3 = (bf16[8,1,2,32,256]{4,3,2,0,1:T(8,128)(2,1)S(1)}, bf16[8,1,2,32,256]{4,3,2,0,1:T(8,128)(2,1)S(1)}, u32[]{:S(2)}, u32[]{:S(2)}) collective-permute-start(bf16[8,1,2,32,256]{4,3,2,0,1:T(8,128)(2,1)S(1)} %bitcast.2034), channel_id=1, source_target_pairs={{64,0},{128,64},{192,128},{256,192},{320,256},{384,320},{448,384},... | collective-permute-start | bytes 786440 | tf_op jit(solution)/shard_map/ppermute | solution.py:20
  71.0 7.8 %collective-permute-start.2 = (bf16[8,1,2,32,256]{4,3,2,0,1:T(8,128)(2,1)S(1)}, bf16[8,1,2,32,256]{4,3,2,0,1:T(8,128)(2,1)S(1)}, u32[]{:S(2)}, u32[]{:S(2)}) collective-permute-start(bf16[8,1,2,32,256]{4,3,2,0,1:T(8,128)(2,1)S(1)} %bitcast.2035), channel_id=1, source_target_pairs={{0,64},{64,128},{128,192},{192,256},{256,320},{320,384},{384,448},... | collective-permute-start | bytes 786440 | tf_op jit(solution)/shard_map/ppermute | solution.py:17
  78.9 46.1 %copy-start.15 = (bf16[8,1,2,32,256]{4,3,2,0,1:T(8,128)(2,1)}, bf16[8,1,2,32,256]{4,3,2,0,1:T(8,128)(2,1)S(1)}, u32[]{:S(2)}) copy-start(bf16[8,1,2,32,256]{4,3,2,0,1:T(8,128)(2,1)S(1)} %collective-permute-done.2) | copy-start | bytes 786436
  80.0 22.5 %collective-permute-start.11 = (bf16[3,1,2,32,256]{4,3,2,1,0:T(8,128)(2,1)S(1)}, bf16[3,1,2,32,256]{4,3,2,1,0:T(8,128)(2,1)S(1)}, u32[]{:S(2)}, u32[]{:S(2)}) collective-permute-start(bf16[3,1,2,32,256]{4,3,2,1,0:T(8,128)(2,1)S(1)} %pad_maximum_fusion.19), channel_id=1, source_target_pairs={{4,0},{5,1},{6,2},{7,3},{8,4},{9,5},{10,6},{11,7},{12,8},{13,9},{1... | collective-permute-start | bytes 294920 | tf_op jit(solution)/shard_map/ppermute | solution.py:28
  81.3 17.1 %collective-permute-start.4 = (bf16[3,1,2,32,256]{4,3,2,1,0:T(8,128)(2,1)S(1)}, bf16[3,1,2,32,256]{4,3,2,1,0:T(8,128)(2,1)S(1)}, u32[]{:S(2)}, u32[]{:S(2)}) collective-permute-start(bf16[3,1,2,32,256]{4,3,2,1,0:T(8,128)(2,1)S(1)} %pad_maximum_fusion.19), channel_id=1, source_target_pairs={{0,4},{1,5},{2,6},{3,7},{4,8},{5,9},{6,10},{7,11},{8,12},{9,13},{1... | collective-permute-start | bytes 294920 | tf_op jit(solution)/shard_map/ppermute | solution.py:28
  87.9 16.5 %collective-permute-start.10 = (bf16[5,1,2,32,256]{4,3,2,1,0:T(8,128)(2,1)S(1)}, bf16[5,1,2,32,256]{4,3,2,1,0:T(8,128)(2,1)S(1)}, u32[]{:S(2)}, u32[]{:S(2)}) collective-permute-start(bf16[5,1,2,32,256]{4,3,2,1,0:T(8,128)(2,1)S(1)} %pad_maximum_fusion.4), channel_id=1, source_target_pairs={{3,0},{4,1},{5,2},{6,3},{7,4},{8,5},{9,6},{10,7},{11,8},{12,9},{13... | collective-permute-start | bytes 491528 | tf_op jit(solution)/shard_map/ppermute | solution.py:28
  89.2 18.9 %collective-permute-start.5 = (bf16[5,1,2,32,256]{4,3,2,1,0:T(8,128)(2,1)S(1)}, bf16[5,1,2,32,256]{4,3,2,1,0:T(8,128)(2,1)S(1)}, u32[]{:S(2)}, u32[]{:S(2)}) collective-permute-start(bf16[5,1,2,32,256]{4,3,2,1,0:T(8,128)(2,1)S(1)} %pad_maximum_fusion.4), channel_id=1, source_target_pairs={{0,3},{1,4},{2,5},{3,6},{4,7},{5,8},{6,9},{7,10},{8,11},{9,12},{10... | collective-permute-start | bytes 491528 | tf_op jit(solution)/shard_map/ppermute | solution.py:28
  96.3 11.8 %collective-permute-start.9 = (bf16[7,1,2,32,256]{4,3,2,1,0:T(8,128)(2,1)S(1)}, bf16[7,1,2,32,256]{4,3,2,1,0:T(8,128)(2,1)S(1)}, u32[]{:S(2)}, u32[]{:S(2)}) collective-permute-start(bf16[7,1,2,32,256]{4,3,2,1,0:T(8,128)(2,1)S(1)} %pad_maximum_fusion.3), channel_id=1, source_target_pairs={{2,0},{3,1},{4,2},{5,3},{6,4},{7,5},{8,6},{9,7},{10,8},{11,9},{12,... | collective-permute-start | bytes 688136 | tf_op jit(solution)/shard_map/ppermute | solution.py:28
  98.4 10.4 %collective-permute-start.6 = (bf16[7,1,2,32,256]{4,3,2,1,0:T(8,128)(2,1)S(1)}, bf16[7,1,2,32,256]{4,3,2,1,0:T(8,128)(2,1)S(1)}, u32[]{:S(2)}, u32[]{:S(2)}) collective-permute-start(bf16[7,1,2,32,256]{4,3,2,1,0:T(8,128)(2,1)S(1)} %pad_maximum_fusion.3), channel_id=1, source_target_pairs={{0,2},{1,3},{2,4},{3,5},{4,6},{5,7},{6,8},{7,9},{8,10},{9,11},{10,... | collective-permute-start | bytes 688136 | tf_op jit(solution)/shard_map/ppermute | solution.py:28
  102.5 10.2 %collective-permute-start.8 = (bf16[9,1,2,32,256]{4,3,2,1,0:T(8,128)(2,1)S(1)}, bf16[9,1,2,32,256]{4,3,2,1,0:T(8,128)(2,1)S(1)}, u32[]{:S(2)}, u32[]{:S(2)}) collective-permute-start(bf16[9,1,2,32,256]{4,3,2,1,0:T(8,128)(2,1)S(1)} %pad_maximum_fusion), channel_id=1, source_target_pairs={{1,0},{2,1},{3,2},{4,3},{5,4},{6,5},{7,6},{8,7},{9,8},{10,9},{11,1... | collective-permute-start | bytes 884744 | tf_op jit(solution)/shard_map/ppermute | solution.py:28
  104.4 7.6 %collective-permute-start.7 = (bf16[9,1,2,32,256]{4,3,2,1,0:T(8,128)(2,1)S(1)}, bf16[9,1,2,32,256]{4,3,2,1,0:T(8,128)(2,1)S(1)}, u32[]{:S(2)}, u32[]{:S(2)}) collective-permute-start(bf16[9,1,2,32,256]{4,3,2,1,0:T(8,128)(2,1)S(1)} %pad_maximum_fusion), channel_id=1, source_target_pairs={{0,1},{1,2},{2,3},{3,4},{4,5},{5,6},{6,7},{7,8},{8,9},{9,10},{10,1... | collective-permute-start | bytes 884744 | tf_op jit(solution)/shard_map/ppermute | solution.py:28
  115.1 10.9 %collective-permute-start.13 = (bf16[1,18,32,256]{3,2,1,0:T(8,128)(2,1)}, bf16[1,18,32,256]{3,2,1,0:T(8,128)(2,1)}, u32[]{:S(2)}, u32[]{:S(2)}) collective-permute-start(bf16[1,18,32,256]{3,2,1,0:T(8,128)(2,1)} %fusion.50), channel_id=1, source_target_pairs={{0,64},{64,128},{128,192},{192,256},{256,320},{320,384},{384,448},... | collective-permute-start | bytes 884744 | tf_op jit(solution)/shard_map/ppermute | solution.py:17
  119.7 8.4 %collective-permute-start.12 = (bf16[1,18,32,256]{3,2,1,0:T(8,128)(2,1)}, bf16[1,18,32,256]{3,2,1,0:T(8,128)(2,1)}, u32[]{:S(2)}, u32[]{:S(2)}) collective-permute-start(bf16[1,18,32,256]{3,2,1,0:T(8,128)(2,1)} %fusion.50), channel_id=1, source_target_pairs={{64,0},{128,64},{192,128},{256,192},{320,256},{384,320},{448,384},... | collective-permute-start | bytes 884744 | tf_op jit(solution)/shard_map/ppermute | solution.py:20
  126.0 2.1 copy-start.40
  134.8 5.4 %copy-start.38 = (bf16[32,32]{1,0:T(8,128)(2,1)S(1)}, bf16[32,32]{1,0:T(8,128)(2,1)}, u32[]{:S(2)}) copy-start(bf16[32,32]{1,0:T(8,128)(2,1)} %squeeze.557) | copy-start | bytes 6148
  134.9 7.6 %collective-permute-start.15 = (bf16[1,16,32,256]{3,2,1,0:T(8,128)(2,1)S(1)}, bf16[1,16,32,256]{3,2,1,0:T(8,128)(2,1)S(1)}, u32[]{:S(2)}, u32[]{:S(2)}) collective-permute-start(bf16[1,16,32,256]{3,2,1,0:T(8,128)(2,1)S(1)} %get-tuple-element.99), channel_id=1, source_target_pairs={{0,64},{64,128},{128,192},{192,256},{256,320},{320,384},{384,448},... | collective-permute-start | bytes 786440 | tf_op jit(solution)/shard_map/ppermute | solution.py:17
  138.7 8.1 %collective-permute-start.14 = (bf16[1,16,32,256]{3,2,1,0:T(8,128)(2,1)S(1)}, bf16[1,16,32,256]{3,2,1,0:T(8,128)(2,1)}, u32[]{:S(2)}, u32[]{:S(2)}) collective-permute-start(bf16[1,16,32,256]{3,2,1,0:T(8,128)(2,1)S(1)} %get-tuple-element.99), channel_id=1, source_target_pairs={{64,0},{128,64},{192,128},{256,192},{320,256},{384,320},{448,384},... | collective-permute-start | bytes 786440 | tf_op jit(solution)/shard_map/ppermute | solution.py:20
  141.8 5.0 %copy-start.37 = (bf16[32,32]{1,0:T(8,128)(2,1)S(1)}, bf16[32,32]{1,0:T(8,128)(2,1)}, u32[]{:S(2)}) copy-start(bf16[32,32]{1,0:T(8,128)(2,1)} %squeeze.556) | copy-start | bytes 6148
  153.5 7.2 %collective-permute-start.17 = (bf16[1,14,32,256]{3,2,1,0:T(8,128)(2,1)S(1)}, bf16[1,14,32,256]{3,2,1,0:T(8,128)(2,1)S(1)}, u32[]{:S(2)}, u32[]{:S(2)}) collective-permute-start(bf16[1,14,32,256]{3,2,1,0:T(8,128)(2,1)S(1)} %get-tuple-element.101), channel_id=1, source_target_pairs={{0,64},{64,128},{128,192},{192,256},{256,320},{320,384},{384,448},... | collective-permute-start | bytes 688136 | tf_op jit(solution)/shard_map/ppermute | solution.py:17
  155.8 9.0 %collective-permute-start.16 = (bf16[1,14,32,256]{3,2,1,0:T(8,128)(2,1)S(1)}, bf16[1,14,32,256]{3,2,1,0:T(8,128)(2,1)S(1)}, u32[]{:S(2)}, u32[]{:S(2)}) collective-permute-start(bf16[1,14,32,256]{3,2,1,0:T(8,128)(2,1)S(1)} %get-tuple-element.101), channel_id=1, source_target_pairs={{64,0},{128,64},{192,128},{256,192},{320,256},{384,320},{448,384},... | collective-permute-start | bytes 688136 | tf_op jit(solution)/shard_map/ppermute | solution.py:20
  157.2 1.0 copy-start.16
  159.0 1.8 copy-start.35
  159.2 5.6 %copy-start.34 = (bf16[32,32]{1,0:T(8,128)(2,1)S(1)}, bf16[32,32]{1,0:T(8,128)(2,1)}, u32[]{:S(2)}) copy-start(bf16[32,32]{1,0:T(8,128)(2,1)} %squeeze.570) | copy-start | bytes 6148
  170.6 8.2 %collective-permute-start.19 = (bf16[1,12,32,256]{3,2,1,0:T(8,128)(2,1)S(1)}, bf16[1,12,32,256]{3,2,1,0:T(8,128)(2,1)S(1)}, u32[]{:S(2)}, u32[]{:S(2)}) collective-permute-start(bf16[1,12,32,256]{3,2,1,0:T(8,128)(2,1)S(1)} %get-tuple-element.103), channel_id=1, source_target_pairs={{0,64},{64,128},{128,192},{192,256},{256,320},{320,384},{384,448},... | collective-permute-start | bytes 589832 | tf_op jit(solution)/shard_map/ppermute | solution.py:17
  174.4 8.5 %collective-permute-start.18 = (bf16[1,12,32,256]{3,2,1,0:T(8,128)(2,1)S(1)}, bf16[1,12,32,256]{3,2,1,0:T(8,128)(2,1)S(1)}, u32[]{:S(2)}, u32[]{:S(2)}) collective-permute-start(bf16[1,12,32,256]{3,2,1,0:T(8,128)(2,1)S(1)} %get-tuple-element.103), channel_id=1, source_target_pairs={{64,0},{128,64},{192,128},{256,192},{320,256},{384,320},{448,384},... | collective-permute-start | bytes 589832 | tf_op jit(solution)/shard_map/ppermute | solution.py:20
  176.9 2.0 copy-start.32
  177.1 5.8 %copy-start.31 = (bf16[32,32]{1,0:T(8,128)(2,1)S(1)}, bf16[32,32]{1,0:T(8,128)(2,1)}, u32[]{:S(2)}) copy-start(bf16[32,32]{1,0:T(8,128)(2,1)} %squeeze.590) | copy-start | bytes 6148
  188.6 5.8 %collective-permute-start.21 = (bf16[1,10,32,256]{3,2,1,0:T(8,128)(2,1)S(1)}, bf16[1,10,32,256]{3,2,1,0:T(8,128)(2,1)S(1)}, u32[]{:S(2)}, u32[]{:S(2)}) collective-permute-start(bf16[1,10,32,256]{3,2,1,0:T(8,128)(2,1)S(1)} %get-tuple-element.105), channel_id=1, source_target_pairs={{0,64},{64,128},{128,192},{192,256},{256,320},{320,384},{384,448},... | collective-permute-start | bytes 491528 | tf_op jit(solution)/shard_map/ppermute | solution.py:17
  191.7 6.1 %collective-permute-start.20 = (bf16[1,10,32,256]{3,2,1,0:T(8,128)(2,1)S(1)}, bf16[1,10,32,256]{3,2,1,0:T(8,128)(2,1)S(1)}, u32[]{:S(2)}, u32[]{:S(2)}) collective-permute-start(bf16[1,10,32,256]{3,2,1,0:T(8,128)(2,1)S(1)} %get-tuple-element.105), channel_id=1, source_target_pairs={{64,0},{128,64},{192,128},{256,192},{320,256},{384,320},{448,384},... | collective-permute-start | bytes 491528 | tf_op jit(solution)/shard_map/ppermute | solution.py:20
  194.4 3.4 %copy-start.28 = (bf16[32,32]{1,0:T(8,128)(2,1)S(1)}, bf16[32,32]{1,0:T(8,128)(2,1)}, u32[]{:S(2)}) copy-start(bf16[32,32]{1,0:T(8,128)(2,1)} %squeeze.604) | copy-start | bytes 6148
  202.0 0.9 copy-start.4
  202.0 0.9 copy-start.19
  203.3 6.4 %collective-permute-start.23 = (bf16[1,8,32,256]{3,2,1,0:T(8,128)(2,1)S(1)}, bf16[1,8,32,256]{3,2,1,0:T(8,128)(2,1)S(1)}, u32[]{:S(2)}, u32[]{:S(2)}) collective-permute-start(bf16[1,8,32,256]{3,2,1,0:T(8,128)(2,1)S(1)} %get-tuple-element.107), channel_id=1, source_target_pairs={{0,64},{64,128},{128,192},{192,256},{256,320},{320,384},{384,448},... | collective-permute-start | bytes 393224 | tf_op jit(solution)/shard_map/ppermute | solution.py:17
  207.0 5.9 %collective-permute-start.22 = (bf16[1,8,32,256]{3,2,1,0:T(8,128)(2,1)S(1)}, bf16[1,8,32,256]{3,2,1,0:T(8,128)(2,1)S(1)}, u32[]{:S(2)}, u32[]{:S(2)}) collective-permute-start(bf16[1,8,32,256]{3,2,1,0:T(8,128)(2,1)S(1)} %get-tuple-element.107), channel_id=1, source_target_pairs={{64,0},{128,64},{192,128},{256,192},{320,256},{384,320},{448,384},... | collective-permute-start | bytes 393224 | tf_op jit(solution)/shard_map/ppermute | solution.py:20
  209.7 3.2 %copy-start.27 = (bf16[32,32]{1,0:T(8,128)(2,1)S(1)}, bf16[32,32]{1,0:T(8,128)(2,1)}, u32[]{:S(2)}) copy-start(bf16[32,32]{1,0:T(8,128)(2,1)} %squeeze.622) | copy-start | bytes 6148
  218.3 6.1 %collective-permute-start.25 = (bf16[1,6,32,256]{3,2,1,0:T(8,128)(2,1)S(1)}, bf16[1,6,32,256]{3,2,1,0:T(8,128)(2,1)S(1)}, u32[]{:S(2)}, u32[]{:S(2)}) collective-permute-start(bf16[1,6,32,256]{3,2,1,0:T(8,128)(2,1)S(1)} %get-tuple-element.109), channel_id=1, source_target_pairs={{0,64},{64,128},{128,192},{192,256},{256,320},{320,384},{384,448},... | collective-permute-start | bytes 294920 | tf_op jit(solution)/shard_map/ppermute | solution.py:17
  221.8 5.4 %collective-permute-start.24 = (bf16[1,6,32,256]{3,2,1,0:T(8,128)(2,1)S(1)}, bf16[1,6,32,256]{3,2,1,0:T(8,128)(2,1)S(1)}, u32[]{:S(2)}, u32[]{:S(2)}) collective-permute-start(bf16[1,6,32,256]{3,2,1,0:T(8,128)(2,1)S(1)} %get-tuple-element.109), channel_id=1, source_target_pairs={{64,0},{128,64},{192,128},{256,192},{320,256},{384,320},{448,384},... | collective-permute-start | bytes 294920 | tf_op jit(solution)/shard_map/ppermute | solution.py:20
  224.4 2.7 copy-start.26
  232.4 6.8 %collective-permute-start.27 = (bf16[1,4,32,256]{3,2,1,0:T(8,128)(2,1)S(1)}, bf16[1,4,32,256]{3,2,1,0:T(8,128)(2,1)S(1)}, u32[]{:S(2)}, u32[]{:S(2)}) collective-permute-start(bf16[1,4,32,256]{3,2,1,0:T(8,128)(2,1)S(1)} %get-tuple-element.111), channel_id=1, source_target_pairs={{0,64},{64,128},{128,192},{192,256},{256,320},{320,384},{384,448},... | collective-permute-start | bytes 196616 | tf_op jit(solution)/shard_map/ppermute | solution.py:17
  236.0 5.0 %collective-permute-start.26 = (bf16[1,4,32,256]{3,2,1,0:T(8,128)(2,1)S(1)}, bf16[1,4,32,256]{3,2,1,0:T(8,128)(2,1)S(1)}, u32[]{:S(2)}, u32[]{:S(2)}) collective-permute-start(bf16[1,4,32,256]{3,2,1,0:T(8,128)(2,1)S(1)} %get-tuple-element.111), channel_id=1, source_target_pairs={{64,0},{128,64},{192,128},{256,192},{320,256},{384,320},{448,384},... | collective-permute-start | bytes 196616 | tf_op jit(solution)/shard_map/ppermute | solution.py:20
  239.1 1.9 copy-start.42
  244.9 5.1 %copy-start.11 = (bf16[3,3,32,32]{3,2,1,0:T(8,128)(2,1)S(1)}, bf16[3,3,32,32]{3,2,1,0:T(8,128)(2,1)}, u32[]{:S(2)}) copy-start(bf16[3,3,32,32]{3,2,1,0:T(8,128)(2,1)} %squeeze.655) | copy-start | bytes 55300
  244.9 15.9 %all-to-all-start.1 = ((f32[8,1,12288]{2,1,0:T(1,128)}), f32[8,1,12288]{2,1,0:T(1,128)S(1)}, u32[]{:S(2)}, u32[]{:S(2)}) async-start(f32[8,1,12288]{2,1,0:T(1,128)} %maximum_multiply_fusion.5), calls=%async_computation.1 | async-start | bytes 786432 | tf_op jit(solution)/shard_map/all_to_all | solution.py:212
  261.9 33.1 %all-to-all-start.2 = ((f32[64,1,192]{2,1,0:T(1,128)}), f32[64,1,192]{2,1,0:T(1,128)S(1)}, u32[]{:S(2)}, u32[]{:S(2)}) async-start(f32[64,1,192]{2,1,0:T(1,128)} %all_to_all.26), calls=%async_computation.2 | async-start | bytes 131072 | tf_op jit(solution)/shard_map/all_to_all | solution.py:217
  295.7 14.4 %all-to-all-start.3 = ((f32[64,1,192]{2,1,0:T(1,128)}), f32[64,1,192]{2,1,0:T(1,128)S(1)}, u32[]{:S(2)}, u32[]{:S(2)}) async-start(f32[64,1,192]{2,1,0:T(1,128)} %broadcast_in_dim.21), calls=%async_computation.3 | async-start | bytes 131072 | tf_op jit(solution)/shard_map/all_to_all | solution.py:218
  (34 other events, 27.6 us)

commit v4 on v3

--- a/solution.py
+++ b/solution.py
@@ -203,18 +203,40 @@
         grad = (
             grad[:, 1:-1].astype(jnp.float32) + plane_back(grad_mid, plane_w[layer], rows, width)
         ).astype(jnp.bfloat16)
-        depth_list[layer] = depth_taps(grad_mix[:, h : h + height], deep[layer], zs)
-        plane_list[layer] = plane_taps(grad_mid[:, h : h + height], rows_own[layer], height, width)
-
-    planes = jnp.stack(plane_list).reshape(layers, -1)
-    depths = jnp.stack(depth_list).reshape(layers, -1)
+        depth_list[layer] = grad_mix[:, h : h + height]
+        plane_list[layer] = grad_mid[:, h : h + height]
+
+    mixes = jnp.stack(depth_list)
+    mids = jnp.stack(plane_list)
+    wide_rows = width_pad(rows_own)
+    planes = jnp.stack(
+        [
+            jnp.einsum(
+                "lzyox,lzycx->loc",
+                mids,
+                wide_rows[:, :, i : i + height, :, j : j + width],
+                preferred_element_type=jnp.float32,
+            )
+            for i in range(3)
+            for j in range(3)
+        ],
+        axis=1,
+    ).reshape(layers, -1)
+    depths = jnp.stack(
+        [
+            jnp.einsum(
+                "lzyox,lzycx->loc", mixes, deep[:, k : k + zs], preferred_element_type=jnp.float32
+            )
+            for k in range(3)
+        ],
+        axis=1,
+    ).reshape(layers, -1)
     flat = jnp.concatenate([planes, depths], axis=1) * scale
-    flat = lax.all_to_all(flat, "segment", 0, 0, tiled=True).sum(axis=0)
     spread_n = lax.axis_size("gy")
-    size = flat.shape[0]
+    size = flat.shape[1]
     piece = -(-size // spread_n)
-    flat = jnp.pad(flat, (0, piece * spread_n - size)).reshape(spread_n, piece)
-    part = lax.all_to_all(flat, "gy", 0, 0, tiled=True).sum(axis=0)
+    flat = jnp.pad(flat, ((0, 0), (0, piece * spread_n - size))).reshape(layers * spread_n, piece)
+    part = lax.all_to_all(flat, ("segment", "gy"), 0, 0, tiled=True).sum(axis=0)
     whole = lax.all_to_all(jnp.broadcast_to(part, (spread_n, piece)), "gy", 0, 0, tiled=True)
     flat = whole.reshape(-1)[:size][None]
     cut = planes.shape[1]

time: 315 us -> 278 us (0.88)
  local copies, waits for them, and re-layouts: 53.6 us -> 28.3 us
  matrix products: 48.5 us -> 30.8 us
  waiting for transfers between devices: 78.7 us -> 94.9 us
  other arithmetic: 8.52 us -> 3.02 us
    unnamed x122 -> x80, local copies, waits for them, and re-layouts: 19.9 us -> 2.78 us
    dot_general x96 -> x12, matrix products: 18.9 us -> 2.7 us  [the longest x9 2.06 us: local(): jnp.einsum('lzyox,lzycx->loc', mids, wide_rows[:, :, i:i + height, :, j:j...]
    ppermute x10, waiting for transfers between devices: 5.53 us -> 14 us  [padded_2(): lax.ppermute(lax.slice_in_dim(block, block.shape[dim] - width, None, axis...]
    ppermute x10, waiting for transfers between devices: 25.7 us -> 30.5 us  [padded_2(): lax.ppermute(lax.slice_in_dim(block, 0, width, axis=dim), axis, backward)]
    squeeze x24, local copies, waits for them, and re-layouts: 15.5 us -> 11.4 us  [depth_back(): kernel[k]]
    all_to_all x2 -> x1, waiting for transfers between devices: 19 us -> 22 us  [local(): part = lax.all_to_all(flat, ('segment', 'gy'), 0, 0, tiled=True).sum(axis=0)]
    all_to_all x2 -> x1, starting transfers between devices: 28.4 us -> 27 us  [local(): part = lax.all_to_all(flat, ('segment', 'gy'), 0, 0, tiled=True).sum(axis=0)]
  transfers between devices with their start and end apart: 32 -> 31, of which waited for: 20 -> 22; matrix products, arithmetic and copies ran while one was open for 8% -> 9% of each run, Pallas kernels for 0% -> 0%
where the time goes in v4:
time: 278 us; the launch traced here: 277 us
  starting transfers between devices  117 us (42%)
  waiting for transfers between devices  94.9 us (34%)
  matrix products  30.8 us (11%)
  local copies, waits for them, and re-layouts  28.3 us (10%)
  other arithmetic  3.02 us (1%)
    ppermute x10, starting transfers between devices, padded_2(): lax.ppermute(lax.slice_in_dim(block, block.shape[dim] - width, None, axis...  35 us
    ppermute x10, waiting for transfers between devices, padded_2(): lax.ppermute(lax.slice_in_dim(block, 0, width, axis=dim), axis, backward)  30.5 us
    all_to_all x1, starting transfers between devices, local(): part = lax.all_to_all(flat, ('segment', 'gy'), 0, 0, tiled=True).sum(axis=0)  27 us
    ppermute x8, starting transfers between devices, passed_along(): return lax.ppermute(block, axis, route)  26.5 us
    all_to_all x1, waiting for transfers between devices, local(): part = lax.all_to_all(flat, ('segment', 'gy'), 0, 0, tiled=True).sum(axis=0)  22 us
    dot_general x72, matrix products, plane_back(): jnp.einsum('oc,...yox->...ycx', kernel[i, j], padded[..., 2 - i:2 - i + h...  17.9 us
    all_to_all x1, waiting for transfers between devices, local(): got = lax.all_to_all(send, 'segment', 0, 0, tiled=True)  15.6 us
    ppermute x10, waiting for transfers between devices, padded_2(): lax.ppermute(lax.slice_in_dim(block, block.shape[dim] - width, None, axis...  14 us
  transfers between devices with their start and end apart: 31, of which 22 were waited for; matrix products, arithmetic and copies ran while one was open for 9% of the time, Pallas kernels for 0%

profile of v4, /device:TPU:1, one launch (start us, length us, event | category | flops | bytes accessed | tf_op | source)
XLA Modules:
  0.0 276.7 jit_solution(6990242407502253517)
XLA Ops:
  6.4 10.9 %all-to-all-start = ((bf16[8,2,14336]{2,1,0:T(2,128)(2,1)}), bf16[8,2,14336]{2,1,0:T(2,128)(2,1)S(1)}, u32[]{:S(2)}, u32[]{:S(2)}) async-start(bf16[8,2,14336]{2,1,0:T(2,128)(2,1)} %reshape.1613), calls=%async_computation | async-start | bytes 917504 | tf_op jit(solution)/shard_map/all_to_all | solution.py:147
  18.1 15.6 %all-to-all-done = bf16[8,2,14336]{2,1,0:T(2,128)(2,1)S(1)} async-done(((bf16[8,2,14336]{2,1,0:T(2,128)(2,1)}), bf16[8,2,14336]{2,1,0:T(2,128)(2,1)S(1)}, u32[]{:S(2)}, u32[]{:S(2)}) %all-to-all-start) | async-done | bytes 458784 | tf_op jit(solution)/shard_map/all_to_all | solution.py:147
  34.8 3.7 %collective-permute-start = (bf16[8,1,1,32,256]{4,3,2,0,1:T(8,128)(2,1)S(1)}, bf16[8,1,1,32,256]{4,3,2,0,1:T(8,128)(2,1)S(1)}, u32[]{:S(2)}, u32[]{:S(2)}) collective-permute-start(bf16[8,1,1,32,256]{4,3,2,0,1:T(8,128)(2,1)S(1)} %get-tuple-element.59), channel_id=1, source_target_pairs={{0,1},{1,2},{2,3},{3,4},{4,5},{5,6},{6,7},{7,8},{8,9},{9,10},{10,1... | collective-permute-start | bytes 393224 | tf_op jit(solution)/shard_map/ppermute | solution.py:17
  38.5 1.9 collective-permute-start.1
  41.9 2.9 %collective-permute-done.1 = bf16[8,1,1,32,256]{4,3,2,0,1:T(8,128)(2,1)S(1)} collective-permute-done((bf16[8,1,1,32,256]{4,3,2,0,1:T(8,128)(2,1)S(1)}, bf16[8,1,1,32,256]{4,3,2,0,1:T(8,128)(2,1)S(1)}, u32[]{:S(2)}, u32[]{:S(2)}) %collective-permute-start.1) | collective-permute-done | bytes 131104 | tf_op jit(solution)/shard_map/ppermute | solution.py:20
  47.3 1.3 collective-permute-start.3
  63.6 4.0 %collective-permute-start.2 = (bf16[8,1,2,32,256]{4,3,2,0,1:T(8,128)(2,1)S(1)}, bf16[8,1,2,32,256]{4,3,2,0,1:T(8,128)(2,1)S(1)}, u32[]{:S(2)}, u32[]{:S(2)}) collective-permute-start(bf16[8,1,2,32,256]{4,3,2,0,1:T(8,128)(2,1)S(1)} %bitcast.1429), channel_id=1, source_target_pairs={{0,64},{64,128},{128,192},{192,256},{256,320},{320,384},{384,448},... | collective-permute-start | bytes 786440 | tf_op jit(solution)/shard_map/ppermute | solution.py:17
  68.0 3.4 %collective-permute-done.2 = bf16[8,1,2,32,256]{4,3,2,0,1:T(8,128)(2,1)S(1)} collective-permute-done((bf16[8,1,2,32,256]{4,3,2,0,1:T(8,128)(2,1)S(1)}, bf16[8,1,2,32,256]{4,3,2,0,1:T(8,128)(2,1)S(1)}, u32[]{:S(2)}, u32[]{:S(2)}) %collective-permute-start.2) | collective-permute-done | bytes 262176 | tf_op jit(solution)/shard_map/ppermute | solution.py:17
  71.8 1.3 collective-permute-start.11
  73.1 6.6 %collective-permute-start.4 = (bf16[3,1,2,32,256]{4,3,2,1,0:T(8,128)(2,1)S(1)}, bf16[3,1,2,32,256]{4,3,2,1,0:T(8,128)(2,1)S(1)}, u32[]{:S(2)}, u32[]{:S(2)}) collective-permute-start(bf16[3,1,2,32,256]{4,3,2,1,0:T(8,128)(2,1)S(1)} %pad_maximum_fusion.12), channel_id=1, source_target_pairs={{0,4},{1,5},{2,6},{3,7},{4,8},{5,9},{6,10},{7,11},{8,12},{9,13},{1... | collective-permute-start | bytes 294920 | tf_op jit(solution)/shard_map/ppermute | solution.py:28
  79.7 1.3 collective-permute-start.10
  81.0 6.4 %collective-permute-start.5 = (bf16[5,1,2,32,256]{4,3,2,1,0:T(8,128)(2,1)S(1)}, bf16[5,1,2,32,256]{4,3,2,1,0:T(8,128)(2,1)S(1)}, u32[]{:S(2)}, u32[]{:S(2)}) collective-permute-start(bf16[5,1,2,32,256]{4,3,2,1,0:T(8,128)(2,1)S(1)} %pad_maximum_fusion.5), channel_id=1, source_target_pairs={{0,3},{1,4},{2,5},{3,6},{4,7},{5,8},{6,9},{7,10},{8,11},{9,12},{10... | collective-permute-start | bytes 491528 | tf_op jit(solution)/shard_map/ppermute | solution.py:28
  87.5 1.3 collective-permute-start.9
  88.9 4.0 %collective-permute-start.6 = (bf16[7,1,2,32,256]{4,3,2,1,0:T(8,128)(2,1)S(1)}, bf16[7,1,2,32,256]{4,3,2,1,0:T(8,128)(2,1)S(1)}, u32[]{:S(2)}, u32[]{:S(2)}) collective-permute-start(bf16[7,1,2,32,256]{4,3,2,1,0:T(8,128)(2,1)S(1)} %pad_maximum_fusion.4), channel_id=1, source_target_pairs={{0,2},{1,3},{2,4},{3,5},{4,6},{5,7},{6,8},{7,9},{8,10},{9,11},{10,... | collective-permute-start | bytes 688136 | tf_op jit(solution)/shard_map/ppermute | solution.py:28
  93.0 1.9 collective-permute-start.8
  94.9 3.6 %collective-permute-start.7 = (bf16[9,1,2,32,256]{4,3,2,1,0:T(8,128)(2,1)S(1)}, bf16[9,1,2,32,256]{4,3,2,1,0:T(8,128)(2,1)S(1)}, u32[]{:S(2)}, u32[]{:S(2)}) collective-permute-start(bf16[9,1,2,32,256]{4,3,2,1,0:T(8,128)(2,1)S(1)} %pad_maximum_fusion.1), channel_id=1, source_target_pairs={{0,1},{1,2},{2,3},{3,4},{4,5},{5,6},{6,7},{7,8},{8,9},{9,10},{10,1... | collective-permute-start | bytes 884744 | tf_op jit(solution)/shard_map/ppermute | solution.py:28
  99.5 3.1 %collective-permute-done.7 = bf16[9,1,2,32,256]{4,3,2,1,0:T(8,128)(2,1)S(1)} collective-permute-done((bf16[9,1,2,32,256]{4,3,2,1,0:T(8,128)(2,1)S(1)}, bf16[9,1,2,32,256]{4,3,2,1,0:T(8,128)(2,1)S(1)}, u32[]{:S(2)}, u32[]{:S(2)}) %collective-permute-start.7) | collective-permute-done | bytes 294944 | tf_op jit(solution)/shard_map/ppermute | solution.py:28
  102.9 3.8 %collective-permute-start.13 = (bf16[1,18,32,256]{3,2,1,0:T(8,128)(2,1)S(1)}, bf16[1,18,32,256]{3,2,1,0:T(8,128)(2,1)S(1)}, u32[]{:S(2)}, u32[]{:S(2)}) collective-permute-start(bf16[1,18,32,256]{3,2,1,0:T(8,128)(2,1)S(1)} %fusion.65), channel_id=1, source_target_pairs={{0,64},{64,128},{128,192},{192,256},{256,320},{320,384},{384,448},... | collective-permute-start | bytes 884744 | tf_op jit(solution)/shard_map/ppermute | solution.py:17
  106.7 1.3 collective-permute-start.12
  108.6 1.8 collective-permute-done.13
  110.6 3.7 %collective-permute-done.12 = bf16[1,18,32,256]{3,2,1,0:T(8,128)(2,1)S(1)} collective-permute-done((bf16[1,18,32,256]{3,2,1,0:T(8,128)(2,1)S(1)}, bf16[1,18,32,256]{3,2,1,0:T(8,128)(2,1)S(1)}, u32[]{:S(2)}, u32[]{:S(2)}) %collective-permute-start.12) | collective-permute-done | bytes 294944 | tf_op jit(solution)/shard_map/ppermute | solution.py:20
  117.3 2.2 collective-permute-start.15
  119.5 1.5 collective-permute-start.14
  121.3 2.4 collective-permute-done.15
  123.9 3.9 %collective-permute-done.14 = bf16[1,16,32,256]{3,2,1,0:T(8,128)(2,1)S(1)} collective-permute-done((bf16[1,16,32,256]{3,2,1,0:T(8,128)(2,1)S(1)}, bf16[1,16,32,256]{3,2,1,0:T(8,128)(2,1)S(1)}, u32[]{:S(2)}, u32[]{:S(2)}) %collective-permute-start.14) | collective-permute-done | bytes 262176 | tf_op jit(solution)/shard_map/ppermute | solution.py:20
  130.6 3.8 %collective-permute-start.17 = (bf16[1,14,32,256]{3,2,1,0:T(8,128)(2,1)S(1)}, bf16[1,14,32,256]{3,2,1,0:T(8,128)(2,1)S(1)}, u32[]{:S(2)}, u32[]{:S(2)}) collective-permute-start(bf16[1,14,32,256]{3,2,1,0:T(8,128)(2,1)S(1)} %get-tuple-element.93), channel_id=1, source_target_pairs={{0,64},{64,128},{128,192},{192,256},{256,320},{320,384},{384,448},... | collective-permute-start | bytes 688136 | tf_op jit(solution)/shard_map/ppermute | solution.py:17
  134.4 1.3 collective-permute-start.16
  135.9 3.0 %collective-permute-done.17 = bf16[1,14,32,256]{3,2,1,0:T(8,128)(2,1)S(1)} collective-permute-done((bf16[1,14,32,256]{3,2,1,0:T(8,128)(2,1)S(1)}, bf16[1,14,32,256]{3,2,1,0:T(8,128)(2,1)S(1)}, u32[]{:S(2)}, u32[]{:S(2)}) %collective-permute-start.17) | collective-permute-done | bytes 229408 | tf_op jit(solution)/shard_map/ppermute | solution.py:17
  139.2 4.1 %collective-permute-done.16 = bf16[1,14,32,256]{3,2,1,0:T(8,128)(2,1)S(1)} collective-permute-done((bf16[1,14,32,256]{3,2,1,0:T(8,128)(2,1)S(1)}, bf16[1,14,32,256]{3,2,1,0:T(8,128)(2,1)S(1)}, u32[]{:S(2)}, u32[]{:S(2)}) %collective-permute-start.16) | collective-permute-done | bytes 229408 | tf_op jit(solution)/shard_map/ppermute | solution.py:20
  146.0 3.7 %collective-permute-start.19 = (bf16[1,12,32,256]{3,2,1,0:T(8,128)(2,1)S(1)}, bf16[1,12,32,256]{3,2,1,0:T(8,128)(2,1)S(1)}, u32[]{:S(2)}, u32[]{:S(2)}) collective-permute-start(bf16[1,12,32,256]{3,2,1,0:T(8,128)(2,1)S(1)} %get-tuple-element.95), channel_id=1, source_target_pairs={{0,64},{64,128},{128,192},{192,256},{256,320},{320,384},{384,448},... | collective-permute-start | bytes 589832 | tf_op jit(solution)/shard_map/ppermute | solution.py:17
  149.6 1.3 collective-permute-start.18
  151.2 2.3 collective-permute-done.19
  153.8 3.5 %collective-permute-done.18 = bf16[1,12,32,256]{3,2,1,0:T(8,128)(2,1)S(1)} collective-permute-done((bf16[1,12,32,256]{3,2,1,0:T(8,128)(2,1)S(1)}, bf16[1,12,32,256]{3,2,1,0:T(8,128)(2,1)S(1)}, u32[]{:S(2)}, u32[]{:S(2)}) %collective-permute-start.18) | collective-permute-done | bytes 196640 | tf_op jit(solution)/shard_map/ppermute | solution.py:20
  159.9 2.9 %collective-permute-start.21 = (bf16[1,10,32,256]{3,2,1,0:T(8,128)(2,1)S(1)}, bf16[1,10,32,256]{3,2,1,0:T(8,128)(2,1)S(1)}, u32[]{:S(2)}, u32[]{:S(2)}) collective-permute-start(bf16[1,10,32,256]{3,2,1,0:T(8,128)(2,1)S(1)} %get-tuple-element.97), channel_id=1, source_target_pairs={{0,64},{64,128},{128,192},{192,256},{256,320},{320,384},{384,448},... | collective-permute-start | bytes 491528 | tf_op jit(solution)/shard_map/ppermute | solution.py:17
  162.8 1.3 collective-permute-start.20
  165.3 3.6 %collective-permute-done.20 = bf16[1,10,32,256]{3,2,1,0:T(8,128)(2,1)S(1)} collective-permute-done((bf16[1,10,32,256]{3,2,1,0:T(8,128)(2,1)S(1)}, bf16[1,10,32,256]{3,2,1,0:T(8,128)(2,1)S(1)}, u32[]{:S(2)}, u32[]{:S(2)}) %collective-permute-start.20) | collective-permute-done | bytes 163872 | tf_op jit(solution)/shard_map/ppermute | solution.py:20
  171.3 3.2 %collective-permute-start.23 = (bf16[1,8,32,256]{3,2,1,0:T(8,128)(2,1)S(1)}, bf16[1,8,32,256]{3,2,1,0:T(8,128)(2,1)S(1)}, u32[]{:S(2)}, u32[]{:S(2)}) collective-permute-start(bf16[1,8,32,256]{3,2,1,0:T(8,128)(2,1)S(1)} %get-tuple-element.99), channel_id=1, source_target_pairs={{0,64},{64,128},{128,192},{192,256},{256,320},{320,384},{384,448},... | collective-permute-start | bytes 393224 | tf_op jit(solution)/shard_map/ppermute | solution.py:17
  174.6 1.3 collective-permute-start.22
  176.7 4.1 %collective-permute-done.22 = bf16[1,8,32,256]{3,2,1,0:T(8,128)(2,1)S(1)} collective-permute-done((bf16[1,8,32,256]{3,2,1,0:T(8,128)(2,1)S(1)}, bf16[1,8,32,256]{3,2,1,0:T(8,128)(2,1)S(1)}, u32[]{:S(2)}, u32[]{:S(2)}) %collective-permute-start.22) | collective-permute-done | bytes 131104 | tf_op jit(solution)/shard_map/ppermute | solution.py:20
  183.1 3.5 %collective-permute-start.25 = (bf16[1,6,32,256]{3,2,1,0:T(8,128)(2,1)S(1)}, bf16[1,6,32,256]{3,2,1,0:T(8,128)(2,1)S(1)}, u32[]{:S(2)}, u32[]{:S(2)}) collective-permute-start(bf16[1,6,32,256]{3,2,1,0:T(8,128)(2,1)S(1)} %get-tuple-element.101), channel_id=1, source_target_pairs={{0,64},{64,128},{128,192},{192,256},{256,320},{320,384},{384,448},... | collective-permute-start | bytes 294920 | tf_op jit(solution)/shard_map/ppermute | solution.py:17
  186.6 1.3 collective-permute-start.24
  188.4 3.5 %collective-permute-done.24 = bf16[1,6,32,256]{3,2,1,0:T(8,128)(2,1)S(1)} collective-permute-done((bf16[1,6,32,256]{3,2,1,0:T(8,128)(2,1)S(1)}, bf16[1,6,32,256]{3,2,1,0:T(8,128)(2,1)S(1)}, u32[]{:S(2)}, u32[]{:S(2)}) %collective-permute-start.24) | collective-permute-done | bytes 98336 | tf_op jit(solution)/shard_map/ppermute | solution.py:20
  194.1 4.3 %collective-permute-start.27 = (bf16[1,4,32,256]{3,2,1,0:T(8,128)(2,1)S(1)}, bf16[1,4,32,256]{3,2,1,0:T(8,128)(2,1)}, u32[]{:S(2)}, u32[]{:S(2)}) collective-permute-start(bf16[1,4,32,256]{3,2,1,0:T(8,128)(2,1)S(1)} %get-tuple-element.103), channel_id=1, source_target_pairs={{0,64},{64,128},{128,192},{192,256},{256,320},{320,384},{384,448},... | collective-permute-start | bytes 196616 | tf_op jit(solution)/shard_map/ppermute | solution.py:17
  208.2 1.7 mul.87
  209.9 27.0 %all-to-all-start.1 = ((f32[512,1,192]{2,1,0:T(1,128)}), f32[512,1,192]{2,1,0:T(1,128)S(1)}, u32[]{:S(2)}, u32[]{:S(2)}) async-start(f32[512,1,192]{2,1,0:T(1,128)} %mul.87), calls=%async_computation.1 | async-start | bytes 1048576 | tf_op jit(solution)/shard_map/all_to_all | solution.py:239
  237.7 22.0 %all-to-all-done.1 = f32[512,1,192]{2,1,0:T(1,128)S(1)} async-done(((f32[512,1,192]{2,1,0:T(1,128)}), f32[512,1,192]{2,1,0:T(1,128)S(1)}, u32[]{:S(2)}, u32[]{:S(2)}) %all-to-all-start.1) | async-done | bytes 393248 | tf_op jit(solution)/shard_map/all_to_all | solution.py:239
  260.9 4.2 %all-to-all-start.2 = ((f32[64,1,192]{2,1,0:T(1,128)}), f32[64,1,192]{2,1,0:T(1,128)S(1)}, u32[]{:S(2)}, u32[]{:S(2)}) async-start(f32[64,1,192]{2,1,0:T(1,128)} %broadcast_in_dim.21), calls=%async_computation.2 | async-start | bytes 131072 | tf_op jit(solution)/shard_map/all_to_all | solution.py:240
  265.9 9.0 %all-to-all-done.2 = f32[64,1,192]{2,1,0:T(1,128)S(1)} async-done(((f32[64,1,192]{2,1,0:T(1,128)}), f32[64,1,192]{2,1,0:T(1,128)S(1)}, u32[]{:S(2)}, u32[]{:S(2)}) %all-to-all-start.2) | async-done | bytes 49184 | tf_op jit(solution)/shard_map/all_to_all | solution.py:240
  (314 shorter events, 64.8 us)
Async XLA Ops:
  4.3 13.0 %copy-start.21 = (s32[1,12]{1,0:T(1,128)S(1)}, s32[1,12]{1,0:T(1,128)}, u32[]{:S(2)}) copy-start(s32[1,12]{1,0:T(1,128)} %param.9) | copy-start | bytes 148
  6.4 27.3 %all-to-all-start = ((bf16[8,2,14336]{2,1,0:T(2,128)(2,1)}), bf16[8,2,14336]{2,1,0:T(2,128)(2,1)S(1)}, u32[]{:S(2)}, u32[]{:S(2)}) async-start(bf16[8,2,14336]{2,1,0:T(2,128)(2,1)} %reshape.1613), calls=%async_computation | async-start | bytes 917504 | tf_op jit(solution)/shard_map/all_to_all | solution.py:147
  34.8 7.0 %collective-permute-start = (bf16[8,1,1,32,256]{4,3,2,0,1:T(8,128)(2,1)S(1)}, bf16[8,1,1,32,256]{4,3,2,0,1:T(8,128)(2,1)S(1)}, u32[]{:S(2)}, u32[]{:S(2)}) collective-permute-start(bf16[8,1,1,32,256]{4,3,2,0,1:T(8,128)(2,1)S(1)} %get-tuple-element.59), channel_id=1, source_target_pairs={{0,1},{1,2},{2,3},{3,4},{4,5},{5,6},{6,7},{7,8},{8,9},{9,10},{10,1... | collective-permute-start | bytes 393224 | tf_op jit(solution)/shard_map/ppermute | solution.py:17
  38.5 6.3 %collective-permute-start.1 = (bf16[8,1,1,32,256]{4,3,2,0,1:T(8,128)(2,1)S(1)}, bf16[8,1,1,32,256]{4,3,2,0,1:T(8,128)(2,1)S(1)}, u32[]{:S(2)}, u32[]{:S(2)}) collective-permute-start(bf16[8,1,1,32,256]{4,3,2,0,1:T(8,128)(2,1)S(1)} %get-tuple-element.60), channel_id=1, source_target_pairs={{1,0},{2,1},{3,2},{4,3},{5,4},{6,5},{7,6},{8,7},{9,8},{10,9},{11,1... | collective-permute-start | bytes 393224 | tf_op jit(solution)/shard_map/ppermute | solution.py:20
  47.3 20.5 %collective-permute-start.3 = (bf16[8,1,2,32,256]{4,3,2,0,1:T(8,128)(2,1)S(1)}, bf16[8,1,2,32,256]{4,3,2,0,1:T(8,128)(2,1)S(1)}, u32[]{:S(2)}, u32[]{:S(2)}) collective-permute-start(bf16[8,1,2,32,256]{4,3,2,0,1:T(8,128)(2,1)S(1)} %bitcast.1428), channel_id=1, source_target_pairs={{64,0},{128,64},{192,128},{256,192},{320,256},{384,320},{448,384},... | collective-permute-start | bytes 786440 | tf_op jit(solution)/shard_map/ppermute | solution.py:20
  61.0 10.4 %copy-start.22 = (f32[256]{0:T(256)S(1)}, f32[256]{0:T(256)}, u32[]{:S(2)}) copy-start(f32[256]{0:T(256)} %broadcast_bitcast_fusion) | copy-start | bytes 3076
  63.6 7.8 %collective-permute-start.2 = (bf16[8,1,2,32,256]{4,3,2,0,1:T(8,128)(2,1)S(1)}, bf16[8,1,2,32,256]{4,3,2,0,1:T(8,128)(2,1)S(1)}, u32[]{:S(2)}, u32[]{:S(2)}) collective-permute-start(bf16[8,1,2,32,256]{4,3,2,0,1:T(8,128)(2,1)S(1)} %bitcast.1429), channel_id=1, source_target_pairs={{0,64},{64,128},{128,192},{192,256},{256,320},{320,384},{384,448},... | collective-permute-start | bytes 786440 | tf_op jit(solution)/shard_map/ppermute | solution.py:17
  71.8 21.2 %collective-permute-start.11 = (bf16[3,1,2,32,256]{4,3,2,1,0:T(8,128)(2,1)S(1)}, bf16[3,1,2,32,256]{4,3,2,1,0:T(8,128)(2,1)S(1)}, u32[]{:S(2)}, u32[]{:S(2)}) collective-permute-start(bf16[3,1,2,32,256]{4,3,2,1,0:T(8,128)(2,1)S(1)} %pad_maximum_fusion.12), channel_id=1, source_target_pairs={{4,0},{5,1},{6,2},{7,3},{8,4},{9,5},{10,6},{11,7},{12,8},{13,9},{1... | collective-permute-start | bytes 294920 | tf_op jit(solution)/shard_map/ppermute | solution.py:28
  73.1 15.8 %collective-permute-start.4 = (bf16[3,1,2,32,256]{4,3,2,1,0:T(8,128)(2,1)S(1)}, bf16[3,1,2,32,256]{4,3,2,1,0:T(8,128)(2,1)S(1)}, u32[]{:S(2)}, u32[]{:S(2)}) collective-permute-start(bf16[3,1,2,32,256]{4,3,2,1,0:T(8,128)(2,1)S(1)} %pad_maximum_fusion.12), channel_id=1, source_target_pairs={{0,4},{1,5},{2,6},{3,7},{4,8},{5,9},{6,10},{7,11},{8,12},{9,13},{1... | collective-permute-start | bytes 294920 | tf_op jit(solution)/shard_map/ppermute | solution.py:28
  79.7 15.2 %collective-permute-start.10 = (bf16[5,1,2,32,256]{4,3,2,1,0:T(8,128)(2,1)S(1)}, bf16[5,1,2,32,256]{4,3,2,1,0:T(8,128)(2,1)S(1)}, u32[]{:S(2)}, u32[]{:S(2)}) collective-permute-start(bf16[5,1,2,32,256]{4,3,2,1,0:T(8,128)(2,1)S(1)} %pad_maximum_fusion.5), channel_id=1, source_target_pairs={{3,0},{4,1},{5,2},{6,3},{7,4},{8,5},{9,6},{10,7},{11,8},{12,9},{13... | collective-permute-start | bytes 491528 | tf_op jit(solution)/shard_map/ppermute | solution.py:28
  81.0 17.6 %collective-permute-start.5 = (bf16[5,1,2,32,256]{4,3,2,1,0:T(8,128)(2,1)S(1)}, bf16[5,1,2,32,256]{4,3,2,1,0:T(8,128)(2,1)S(1)}, u32[]{:S(2)}, u32[]{:S(2)}) collective-permute-start(bf16[5,1,2,32,256]{4,3,2,1,0:T(8,128)(2,1)S(1)} %pad_maximum_fusion.5), channel_id=1, source_target_pairs={{0,3},{1,4},{2,5},{3,6},{4,7},{5,8},{6,9},{7,10},{8,11},{9,12},{10... | collective-permute-start | bytes 491528 | tf_op jit(solution)/shard_map/ppermute | solution.py:28
  87.5 11.1 %collective-permute-start.9 = (bf16[7,1,2,32,256]{4,3,2,1,0:T(8,128)(2,1)S(1)}, bf16[7,1,2,32,256]{4,3,2,1,0:T(8,128)(2,1)S(1)}, u32[]{:S(2)}, u32[]{:S(2)}) collective-permute-start(bf16[7,1,2,32,256]{4,3,2,1,0:T(8,128)(2,1)S(1)} %pad_maximum_fusion.4), channel_id=1, source_target_pairs={{2,0},{3,1},{4,2},{5,3},{6,4},{7,5},{8,6},{9,7},{10,8},{11,9},{12,... | collective-permute-start | bytes 688136 | tf_op jit(solution)/shard_map/ppermute | solution.py:28
  88.9 10.5 %collective-permute-start.6 = (bf16[7,1,2,32,256]{4,3,2,1,0:T(8,128)(2,1)S(1)}, bf16[7,1,2,32,256]{4,3,2,1,0:T(8,128)(2,1)S(1)}, u32[]{:S(2)}, u32[]{:S(2)}) collective-permute-start(bf16[7,1,2,32,256]{4,3,2,1,0:T(8,128)(2,1)S(1)} %pad_maximum_fusion.4), channel_id=1, source_target_pairs={{0,2},{1,3},{2,4},{3,5},{4,6},{5,7},{6,8},{7,9},{8,10},{9,11},{10,... | collective-permute-start | bytes 688136 | tf_op jit(solution)/shard_map/ppermute | solution.py:28
  93.0 9.7 %collective-permute-start.8 = (bf16[9,1,2,32,256]{4,3,2,1,0:T(8,128)(2,1)S(1)}, bf16[9,1,2,32,256]{4,3,2,1,0:T(8,128)(2,1)S(1)}, u32[]{:S(2)}, u32[]{:S(2)}) collective-permute-start(bf16[9,1,2,32,256]{4,3,2,1,0:T(8,128)(2,1)S(1)} %pad_maximum_fusion.1), channel_id=1, source_target_pairs={{1,0},{2,1},{3,2},{4,3},{5,4},{6,5},{7,6},{8,7},{9,8},{10,9},{11,1... | collective-permute-start | bytes 884744 | tf_op jit(solution)/shard_map/ppermute | solution.py:28
  94.9 7.7 %collective-permute-start.7 = (bf16[9,1,2,32,256]{4,3,2,1,0:T(8,128)(2,1)S(1)}, bf16[9,1,2,32,256]{4,3,2,1,0:T(8,128)(2,1)S(1)}, u32[]{:S(2)}, u32[]{:S(2)}) collective-permute-start(bf16[9,1,2,32,256]{4,3,2,1,0:T(8,128)(2,1)S(1)} %pad_maximum_fusion.1), channel_id=1, source_target_pairs={{0,1},{1,2},{2,3},{3,4},{4,5},{5,6},{6,7},{7,8},{8,9},{9,10},{10,1... | collective-permute-start | bytes 884744 | tf_op jit(solution)/shard_map/ppermute | solution.py:28
  102.9 7.5 %collective-permute-start.13 = (bf16[1,18,32,256]{3,2,1,0:T(8,128)(2,1)S(1)}, bf16[1,18,32,256]{3,2,1,0:T(8,128)(2,1)S(1)}, u32[]{:S(2)}, u32[]{:S(2)}) collective-permute-start(bf16[1,18,32,256]{3,2,1,0:T(8,128)(2,1)S(1)} %fusion.65), channel_id=1, source_target_pairs={{0,64},{64,128},{128,192},{192,256},{256,320},{320,384},{384,448},... | collective-permute-start | bytes 884744 | tf_op jit(solution)/shard_map/ppermute | solution.py:17
  106.7 7.6 %collective-permute-start.12 = (bf16[1,18,32,256]{3,2,1,0:T(8,128)(2,1)S(1)}, bf16[1,18,32,256]{3,2,1,0:T(8,128)(2,1)S(1)}, u32[]{:S(2)}, u32[]{:S(2)}) collective-permute-start(bf16[1,18,32,256]{3,2,1,0:T(8,128)(2,1)S(1)} %fusion.65), channel_id=1, source_target_pairs={{64,0},{128,64},{192,128},{256,192},{320,256},{384,320},{448,384},... | collective-permute-start | bytes 884744 | tf_op jit(solution)/shard_map/ppermute | solution.py:20
  108.5 5.9 %copy-start.13 = (bf16[32,32]{1,0:T(8,128)(2,1)S(1)}, bf16[32,32]{1,0:T(8,128)(2,1)}, u32[]{:S(2)}) copy-start(bf16[32,32]{1,0:T(8,128)(2,1)} %squeeze.502) | copy-start | bytes 6148
  116.9 6.7 %copy-start.12 = (bf16[32,32]{1,0:T(8,128)(2,1)S(1)}, bf16[32,32]{1,0:T(8,128)(2,1)}, u32[]{:S(2)}) copy-start(bf16[32,32]{1,0:T(8,128)(2,1)} %squeeze.526) | copy-start | bytes 6148
  117.3 10.5 %copy-start.9 = (bf16[32,32]{1,0:T(8,128)(2,1)S(1)}, bf16[32,32]{1,0:T(8,128)(2,1)}, u32[]{:S(2)}) copy-start(bf16[32,32]{1,0:T(8,128)(2,1)} %squeeze.524) | copy-start | bytes 6148
  117.3 6.4 %collective-permute-start.15 = (bf16[1,16,32,256]{3,2,1,0:T(8,128)(2,1)S(1)}, bf16[1,16,32,256]{3,2,1,0:T(8,128)(2,1)S(1)}, u32[]{:S(2)}, u32[]{:S(2)}) collective-permute-start(bf16[1,16,32,256]{3,2,1,0:T(8,128)(2,1)S(1)} %get-tuple-element.91), channel_id=1, source_target_pairs={{0,64},{64,128},{128,192},{192,256},{256,320},{320,384},{384,448},... | collective-permute-start | bytes 786440 | tf_op jit(solution)/shard_map/ppermute | solution.py:17
  119.5 8.3 %collective-permute-start.14 = (bf16[1,16,32,256]{3,2,1,0:T(8,128)(2,1)S(1)}, bf16[1,16,32,256]{3,2,1,0:T(8,128)(2,1)S(1)}, u32[]{:S(2)}, u32[]{:S(2)}) collective-permute-start(bf16[1,16,32,256]{3,2,1,0:T(8,128)(2,1)S(1)} %get-tuple-element.91), channel_id=1, source_target_pairs={{64,0},{128,64},{192,128},{256,192},{320,256},{384,320},{448,384},... | collective-permute-start | bytes 786440 | tf_op jit(solution)/shard_map/ppermute | solution.py:20
  130.2 5.4 %copy-start.10 = (bf16[32,32]{1,0:T(8,128)(2,1)S(1)}, bf16[32,32]{1,0:T(8,128)(2,1)}, u32[]{:S(2)}) copy-start(bf16[32,32]{1,0:T(8,128)(2,1)} %squeeze.539) | copy-start | bytes 6148
  130.3 8.7 %copy-start.8 = (bf16[32,32]{1,0:T(8,128)(2,1)S(1)}, bf16[32,32]{1,0:T(8,128)(2,1)}, u32[]{:S(2)}) copy-start(bf16[32,32]{1,0:T(8,128)(2,1)} %squeeze.540) | copy-start | bytes 6148
  130.3 13.0 %copy-start.7 = (bf16[32,32]{1,0:T(8,128)(2,1)S(1)}, bf16[32,32]{1,0:T(8,128)(2,1)}, u32[]{:S(2)}) copy-start(bf16[32,32]{1,0:T(8,128)(2,1)} %squeeze.538) | copy-start | bytes 6148
  130.6 8.3 %collective-permute-start.17 = (bf16[1,14,32,256]{3,2,1,0:T(8,128)(2,1)S(1)}, bf16[1,14,32,256]{3,2,1,0:T(8,128)(2,1)S(1)}, u32[]{:S(2)}, u32[]{:S(2)}) collective-permute-start(bf16[1,14,32,256]{3,2,1,0:T(8,128)(2,1)S(1)} %get-tuple-element.93), channel_id=1, source_target_pairs={{0,64},{64,128},{128,192},{192,256},{256,320},{320,384},{384,448},... | collective-permute-start | bytes 688136 | tf_op jit(solution)/shard_map/ppermute | solution.py:17
  134.4 8.9 %collective-permute-start.16 = (bf16[1,14,32,256]{3,2,1,0:T(8,128)(2,1)S(1)}, bf16[1,14,32,256]{3,2,1,0:T(8,128)(2,1)S(1)}, u32[]{:S(2)}, u32[]{:S(2)}) collective-permute-start(bf16[1,14,32,256]{3,2,1,0:T(8,128)(2,1)S(1)} %get-tuple-element.93), channel_id=1, source_target_pairs={{64,0},{128,64},{192,128},{256,192},{320,256},{384,320},{448,384},... | collective-permute-start | bytes 688136 | tf_op jit(solution)/shard_map/ppermute | solution.py:20
  145.4 5.5 %copy-start.6 = (bf16[32,32]{1,0:T(8,128)(2,1)S(1)}, bf16[32,32]{1,0:T(8,128)(2,1)}, u32[]{:S(2)}) copy-start(bf16[32,32]{1,0:T(8,128)(2,1)} %squeeze.559) | copy-start | bytes 6148
  145.7 7.8 %copy-start.5 = (bf16[32,32]{1,0:T(8,128)(2,1)S(1)}, bf16[32,32]{1,0:T(8,128)(2,1)}, u32[]{:S(2)}) copy-start(bf16[32,32]{1,0:T(8,128)(2,1)} %squeeze.560) | copy-start | bytes 6148
  146.0 7.5 %collective-permute-start.19 = (bf16[1,12,32,256]{3,2,1,0:T(8,128)(2,1)S(1)}, bf16[1,12,32,256]{3,2,1,0:T(8,128)(2,1)S(1)}, u32[]{:S(2)}, u32[]{:S(2)}) collective-permute-start(bf16[1,12,32,256]{3,2,1,0:T(8,128)(2,1)S(1)} %get-tuple-element.95), channel_id=1, source_target_pairs={{0,64},{64,128},{128,192},{192,256},{256,320},{320,384},{384,448},... | collective-permute-start | bytes 589832 | tf_op jit(solution)/shard_map/ppermute | solution.py:17
  149.6 7.7 %collective-permute-start.18 = (bf16[1,12,32,256]{3,2,1,0:T(8,128)(2,1)S(1)}, bf16[1,12,32,256]{3,2,1,0:T(8,128)(2,1)S(1)}, u32[]{:S(2)}, u32[]{:S(2)}) collective-permute-start(bf16[1,12,32,256]{3,2,1,0:T(8,128)(2,1)S(1)} %get-tuple-element.95), channel_id=1, source_target_pairs={{64,0},{128,64},{192,128},{256,192},{320,256},{384,320},{448,384},... | collective-permute-start | bytes 589832 | tf_op jit(solution)/shard_map/ppermute | solution.py:20
  159.9 9.2 %copy-start.2 = (bf16[3,3,32,32]{3,2,1,0:T(8,128)(2,1)S(1)}, bf16[3,3,32,32]{3,2,1,0:T(8,128)(2,1)}, u32[]{:S(2)}) copy-start(bf16[3,3,32,32]{3,2,1,0:T(8,128)(2,1)} %squeeze.575) | copy-start | bytes 55300
  159.9 5.2 %collective-permute-start.21 = (bf16[1,10,32,256]{3,2,1,0:T(8,128)(2,1)S(1)}, bf16[1,10,32,256]{3,2,1,0:T(8,128)(2,1)S(1)}, u32[]{:S(2)}, u32[]{:S(2)}) collective-permute-start(bf16[1,10,32,256]{3,2,1,0:T(8,128)(2,1)S(1)} %get-tuple-element.97), channel_id=1, source_target_pairs={{0,64},{64,128},{128,192},{192,256},{256,320},{320,384},{384,448},... | collective-permute-start | bytes 491528 | tf_op jit(solution)/shard_map/ppermute | solution.py:17
  162.8 6.1 %collective-permute-start.20 = (bf16[1,10,32,256]{3,2,1,0:T(8,128)(2,1)S(1)}, bf16[1,10,32,256]{3,2,1,0:T(8,128)(2,1)S(1)}, u32[]{:S(2)}, u32[]{:S(2)}) collective-permute-start(bf16[1,10,32,256]{3,2,1,0:T(8,128)(2,1)S(1)} %get-tuple-element.97), channel_id=1, source_target_pairs={{64,0},{128,64},{192,128},{256,192},{320,256},{384,320},{448,384},... | collective-permute-start | bytes 491528 | tf_op jit(solution)/shard_map/ppermute | solution.py:20
  170.8 5.7 %copy-start.19 = (bf16[32,32]{1,0:T(8,128)(2,1)S(1)}, bf16[32,32]{1,0:T(8,128)(2,1)}, u32[]{:S(2)}) copy-start(bf16[32,32]{1,0:T(8,128)(2,1)} %squeeze.592) | copy-start | bytes 6148
  171.0 10.0 %copy-start.1 = (bf16[3,3,32,32]{3,2,1,0:T(8,128)(2,1)S(1)}, bf16[3,3,32,32]{3,2,1,0:T(8,128)(2,1)}, u32[]{:S(2)}) copy-start(bf16[3,3,32,32]{3,2,1,0:T(8,128)(2,1)} %squeeze.593) | copy-start | bytes 55300
  171.3 5.2 %collective-permute-start.23 = (bf16[1,8,32,256]{3,2,1,0:T(8,128)(2,1)S(1)}, bf16[1,8,32,256]{3,2,1,0:T(8,128)(2,1)S(1)}, u32[]{:S(2)}, u32[]{:S(2)}) collective-permute-start(bf16[1,8,32,256]{3,2,1,0:T(8,128)(2,1)S(1)} %get-tuple-element.99), channel_id=1, source_target_pairs={{0,64},{64,128},{128,192},{192,256},{256,320},{320,384},{384,448},... | collective-permute-start | bytes 393224 | tf_op jit(solution)/shard_map/ppermute | solution.py:17
  174.6 6.2 %collective-permute-start.22 = (bf16[1,8,32,256]{3,2,1,0:T(8,128)(2,1)S(1)}, bf16[1,8,32,256]{3,2,1,0:T(8,128)(2,1)S(1)}, u32[]{:S(2)}, u32[]{:S(2)}) collective-permute-start(bf16[1,8,32,256]{3,2,1,0:T(8,128)(2,1)S(1)} %get-tuple-element.99), channel_id=1, source_target_pairs={{64,0},{128,64},{192,128},{256,192},{320,256},{384,320},{448,384},... | collective-permute-start | bytes 393224 | tf_op jit(solution)/shard_map/ppermute | solution.py:20
  182.2 5.7 %copy-start.18 = (bf16[32,32]{1,0:T(8,128)(2,1)S(1)}, bf16[32,32]{1,0:T(8,128)(2,1)}, u32[]{:S(2)}) copy-start(bf16[32,32]{1,0:T(8,128)(2,1)} %squeeze.605) | copy-start | bytes 6148
  182.4 5.8 %copy-start.17 = (bf16[32,32]{1,0:T(8,128)(2,1)S(1)}, bf16[32,32]{1,0:T(8,128)(2,1)}, u32[]{:S(2)}) copy-start(bf16[32,32]{1,0:T(8,128)(2,1)} %squeeze.606) | copy-start | bytes 6148
  182.7 9.5 %copy-start.4 = (bf16[3,3,32,32]{3,2,1,0:T(8,128)(2,1)S(1)}, bf16[3,3,32,32]{3,2,1,0:T(8,128)(2,1)}, u32[]{:S(2)}) copy-start(bf16[3,3,32,32]{3,2,1,0:T(8,128)(2,1)} %squeeze.607) | copy-start | bytes 55300
  183.1 5.1 %collective-permute-start.25 = (bf16[1,6,32,256]{3,2,1,0:T(8,128)(2,1)S(1)}, bf16[1,6,32,256]{3,2,1,0:T(8,128)(2,1)S(1)}, u32[]{:S(2)}, u32[]{:S(2)}) collective-permute-start(bf16[1,6,32,256]{3,2,1,0:T(8,128)(2,1)S(1)} %get-tuple-element.101), channel_id=1, source_target_pairs={{0,64},{64,128},{128,192},{192,256},{256,320},{320,384},{384,448},... | collective-permute-start | bytes 294920 | tf_op jit(solution)/shard_map/ppermute | solution.py:17
  186.6 5.4 %collective-permute-start.24 = (bf16[1,6,32,256]{3,2,1,0:T(8,128)(2,1)S(1)}, bf16[1,6,32,256]{3,2,1,0:T(8,128)(2,1)S(1)}, u32[]{:S(2)}, u32[]{:S(2)}) collective-permute-start(bf16[1,6,32,256]{3,2,1,0:T(8,128)(2,1)S(1)} %get-tuple-element.101), channel_id=1, source_target_pairs={{64,0},{128,64},{192,128},{256,192},{320,256},{384,320},{448,384},... | collective-permute-start | bytes 294920 | tf_op jit(solution)/shard_map/ppermute | solution.py:20
  192.8 6.9 %copy-start.16 = (bf16[32,32]{1,0:T(8,128)(2,1)S(1)}, bf16[32,32]{1,0:T(8,128)(2,1)}, u32[]{:S(2)}) copy-start(bf16[32,32]{1,0:T(8,128)(2,1)} %squeeze.621) | copy-start | bytes 6148
  194.1 6.8 %collective-permute-start.27 = (bf16[1,4,32,256]{3,2,1,0:T(8,128)(2,1)S(1)}, bf16[1,4,32,256]{3,2,1,0:T(8,128)(2,1)}, u32[]{:S(2)}, u32[]{:S(2)}) collective-permute-start(bf16[1,4,32,256]{3,2,1,0:T(8,128)(2,1)S(1)} %get-tuple-element.103), channel_id=1, source_target_pairs={{0,64},{64,128},{128,192},{192,256},{256,320},{320,384},{384,448},... | collective-permute-start | bytes 196616 | tf_op jit(solution)/shard_map/ppermute | solution.py:17
  198.4 5.1 %collective-permute-start.26 = (bf16[1,4,32,256]{3,2,1,0:T(8,128)(2,1)S(1)}, bf16[1,4,32,256]{3,2,1,0:T(8,128)(2,1)}, u32[]{:S(2)}, u32[]{:S(2)}) collective-permute-start(bf16[1,4,32,256]{3,2,1,0:T(8,128)(2,1)S(1)} %get-tuple-element.103), channel_id=1, source_target_pairs={{64,0},{128,64},{192,128},{256,192},{320,256},{384,320},{448,384},... | collective-permute-start | bytes 196616 | tf_op jit(solution)/shard_map/ppermute | solution.py:20
  209.9 49.7 %all-to-all-start.1 = ((f32[512,1,192]{2,1,0:T(1,128)}), f32[512,1,192]{2,1,0:T(1,128)S(1)}, u32[]{:S(2)}, u32[]{:S(2)}) async-start(f32[512,1,192]{2,1,0:T(1,128)} %mul.87), calls=%async_computation.1 | async-start | bytes 1048576 | tf_op jit(solution)/shard_map/all_to_all | solution.py:239
  260.9 14.0 %all-to-all-start.2 = ((f32[64,1,192]{2,1,0:T(1,128)}), f32[64,1,192]{2,1,0:T(1,128)S(1)}, u32[]{:S(2)}, u32[]{:S(2)}) async-start(f32[64,1,192]{2,1,0:T(1,128)} %broadcast_in_dim.21), calls=%async_computation.2 | async-start | bytes 131072 | tf_op jit(solution)/shard_map/all_to_all | solution.py:240
  (6 other events, 20.6 us)

commit v5 on v4

--- a/solution.py
+++ b/solution.py
@@ -141,15 +141,16 @@
     scale = 1.0 / math.sqrt(sections * height * lax.axis_size("gy") * width)
     segment = lax.axis_index("segment")
 
-    block = acts[0].reshape(count, -1)
-    kernels = jnp.concatenate([w_plane.reshape(1, -1), w_depth.reshape(1, -1)], axis=1)
-    send = jnp.concatenate([block, jnp.broadcast_to(kernels, (count, kernels.shape[1]))], axis=1)
+    block = acts[0].reshape(count, -1, width)
+    kernels = jnp.concatenate([w_plane.reshape(-1), w_depth.reshape(-1)]).reshape(-1, width)
+    send = jnp.concatenate([block, jnp.broadcast_to(kernels[None], (count,) + kernels.shape)], axis=1)
     got = lax.all_to_all(send, "segment", 0, 0, tiled=True)
     cut_a = block.shape[1]
-    cut_w = cut_a + w_plane[0].size
     mine = got[:, :cut_a].reshape((count, zs) + acts.shape[2:])
-    plane_w = got[:, cut_a:cut_w].reshape((count,) + w_plane.shape[1:])
-    depth_w = got[:, cut_w:].reshape((count,) + w_depth.shape[1:])
+    taps = w_plane.shape[1] * w_plane.shape[2]
+    weights = lax.optimization_barrier(got[:, cut_a:].reshape(count, -1, chans, chans))
+    plane_w = weights[:, :taps].reshape((count,) + w_plane.shape[1:])
+    depth_w = weights[:, taps:].reshape((count,) + w_depth.shape[1:])
 
     ids = (segment * zs + jnp.arange(zs, dtype=jnp.int32))[:, None] * (width // TILE) + jnp.arange(
         width // TILE, dtype=jnp.int32

time: 278 us -> 267 us (0.960)
  local copies, waits for them, and re-layouts: 28.3 us -> 12 us
  matrix products: 30.8 us -> 33.7 us
    squeeze x32 -> x0, local copies, waits for them, and re-layouts: 14.7 us -> none  [the longest x24 11.4 us: depth_back(): kernel[k]]
  transfers between devices with their start and end apart: 31 -> 31, of which waited for: 22 -> 22; matrix products, arithmetic and copies ran while one was open for 9% -> 5% of each run, Pallas kernels for 0% -> 0%
where the time goes in v5:
time: 267 us; the launch traced here: 265 us
  starting transfers between devices  118 us (44%)
  waiting for transfers between devices  95.4 us (36%)
  matrix products  33.7 us (13%)
  local copies, waits for them, and re-layouts  12 us (4%)
  other arithmetic  3.57 us (1%)
    ppermute x10, starting transfers between devices, padded_2(): lax.ppermute(lax.slice_in_dim(block, block.shape[dim] - width, None, axis...  35.2 us
    ppermute x10, waiting for transfers between devices, padded_2(): lax.ppermute(lax.slice_in_dim(block, 0, width, axis=dim), axis, backward)  30.3 us
    all_to_all x1, starting transfers between devices, local(): part = lax.all_to_all(flat, ('segment', 'gy'), 0, 0, tiled=True).sum(axis=0)  27.9 us
    ppermute x8, starting transfers between devices, passed_along(): return lax.ppermute(block, axis, route)  26.4 us
    all_to_all x1, waiting for transfers between devices, local(): part = lax.all_to_all(flat, ('segment', 'gy'), 0, 0, tiled=True).sum(axis=0)  22.1 us
    dot_general x72, matrix products, plane_back(): jnp.einsum('oc,...yox->...ycx', kernel[i, j], padded[..., 2 - i:2 - i + h...  20.5 us
    all_to_all x1, waiting for transfers between devices, local(): got = lax.all_to_all(send, 'segment', 0, 0, tiled=True)  16.2 us
    ppermute x10, waiting for transfers between devices, padded_2(): lax.ppermute(lax.slice_in_dim(block, block.shape[dim] - width, None, axis...  13.9 us
  transfers between devices with their start and end apart: 31, of which 22 were waited for; matrix products, arithmetic and copies ran while one was open for 5% of the time, Pallas kernels for 0%

profile of v5, /device:TPU:1, one launch (start us, length us, event | category | flops | bytes accessed | tf_op | source)
XLA Modules:
  0.0 265.2 jit_solution(1423068047912920159)
XLA Ops:
  2.5 1.7 pad_maximum_fusion
  4.3 10.9 %all-to-all-start = ((bf16[8,112,256]{2,1,0:T(8,128)(2,1)}), bf16[8,112,256]{2,1,0:T(8,128)(2,1)S(1)}, u32[]{:S(2)}, u32[]{:S(2)}) async-start(bf16[8,112,256]{2,1,0:T(8,128)(2,1)} %pad_maximum_fusion), calls=%async_computation | async-start | bytes 917504 | tf_op jit(solution)/shard_map/all_to_all | solution.py:147
  15.4 16.2 %all-to-all-done = bf16[8,112,256]{2,1,0:T(8,128)(2,1)S(1)} async-done(((bf16[8,112,256]{2,1,0:T(8,128)(2,1)}), bf16[8,112,256]{2,1,0:T(8,128)(2,1)S(1)}, u32[]{:S(2)}, u32[]{:S(2)}) %all-to-all-start) | async-done | bytes 458784 | tf_op jit(solution)/shard_map/all_to_all | solution.py:147
  31.7 3.7 %collective-permute-start = (bf16[8,1,1,32,256]{4,3,2,0,1:T(8,128)(2,1)S(1)}, bf16[8,1,1,32,256]{4,3,2,0,1:T(8,128)(2,1)S(1)}, u32[]{:S(2)}, u32[]{:S(2)}) collective-permute-start(bf16[8,1,1,32,256]{4,3,2,0,1:T(8,128)(2,1)S(1)} %get-tuple-element.35), channel_id=1, source_target_pairs={{0,1},{1,2},{2,3},{3,4},{4,5},{5,6},{6,7},{7,8},{8,9},{9,10},{10,1... | collective-permute-start | bytes 393224 | tf_op jit(solution)/shard_map/ppermute | solution.py:17
  35.3 1.9 collective-permute-start.1
  37.8 3.8 %collective-permute-done.1 = bf16[8,1,1,32,256]{4,3,2,0,1:T(8,128)(2,1)S(1)} collective-permute-done((bf16[8,1,1,32,256]{4,3,2,0,1:T(8,128)(2,1)S(1)}, bf16[8,1,1,32,256]{4,3,2,0,1:T(8,128)(2,1)S(1)}, u32[]{:S(2)}, u32[]{:S(2)}) %collective-permute-start.1) | collective-permute-done | bytes 131104 | tf_op jit(solution)/shard_map/ppermute | solution.py:20
  44.1 1.3 collective-permute-start.3
  47.0 4.0 %collective-permute-start.2 = (bf16[8,1,2,32,256]{4,3,2,0,1:T(8,128)(2,1)S(1)}, bf16[8,1,2,32,256]{4,3,2,0,1:T(8,128)(2,1)S(1)}, u32[]{:S(2)}, u32[]{:S(2)}) collective-permute-start(bf16[8,1,2,32,256]{4,3,2,0,1:T(8,128)(2,1)S(1)} %bitcast.1403), channel_id=1, source_target_pairs={{0,64},{64,128},{128,192},{192,256},{256,320},{320,384},{384,448},... | collective-permute-start | bytes 786440 | tf_op jit(solution)/shard_map/ppermute | solution.py:17
  51.7 3.1 %collective-permute-done.2 = bf16[8,1,2,32,256]{4,3,2,0,1:T(8,128)(2,1)S(1)} collective-permute-done((bf16[8,1,2,32,256]{4,3,2,0,1:T(8,128)(2,1)S(1)}, bf16[8,1,2,32,256]{4,3,2,0,1:T(8,128)(2,1)S(1)}, u32[]{:S(2)}, u32[]{:S(2)}) %collective-permute-start.2) | collective-permute-done | bytes 262176 | tf_op jit(solution)/shard_map/ppermute | solution.py:17
  55.3 1.3 collective-permute-start.11
  56.6 6.6 %collective-permute-start.4 = (bf16[3,1,2,32,256]{4,3,2,1,0:T(8,128)(2,1)S(1)}, bf16[3,1,2,32,256]{4,3,2,1,0:T(8,128)(2,1)S(1)}, u32[]{:S(2)}, u32[]{:S(2)}) collective-permute-start(bf16[3,1,2,32,256]{4,3,2,1,0:T(8,128)(2,1)S(1)} %pad_maximum_fusion.13), channel_id=1, source_target_pairs={{0,4},{1,5},{2,6},{3,7},{4,8},{5,9},{6,10},{7,11},{8,12},{9,13},{1... | collective-permute-start | bytes 294920 | tf_op jit(solution)/shard_map/ppermute | solution.py:28
  63.2 1.3 collective-permute-start.10
  64.5 6.4 %collective-permute-start.5 = (bf16[5,1,2,32,256]{4,3,2,1,0:T(8,128)(2,1)S(1)}, bf16[5,1,2,32,256]{4,3,2,1,0:T(8,128)(2,1)S(1)}, u32[]{:S(2)}, u32[]{:S(2)}) collective-permute-start(bf16[5,1,2,32,256]{4,3,2,1,0:T(8,128)(2,1)S(1)} %pad_maximum_fusion.6), channel_id=1, source_target_pairs={{0,3},{1,4},{2,5},{3,6},{4,7},{5,8},{6,9},{7,10},{8,11},{9,12},{10... | collective-permute-start | bytes 491528 | tf_op jit(solution)/shard_map/ppermute | solution.py:28
  71.0 1.3 collective-permute-start.9
  72.4 4.0 %collective-permute-start.6 = (bf16[7,1,2,32,256]{4,3,2,1,0:T(8,128)(2,1)S(1)}, bf16[7,1,2,32,256]{4,3,2,1,0:T(8,128)(2,1)S(1)}, u32[]{:S(2)}, u32[]{:S(2)}) collective-permute-start(bf16[7,1,2,32,256]{4,3,2,1,0:T(8,128)(2,1)S(1)} %pad_maximum_fusion.5), channel_id=1, source_target_pairs={{0,2},{1,3},{2,4},{3,5},{4,6},{5,7},{6,8},{7,9},{8,10},{9,11},{10,... | collective-permute-start | bytes 688136 | tf_op jit(solution)/shard_map/ppermute | solution.py:28
  76.4 1.9 collective-permute-start.8
  78.4 3.6 %collective-permute-start.7 = (bf16[9,1,2,32,256]{4,3,2,1,0:T(8,128)(2,1)S(1)}, bf16[9,1,2,32,256]{4,3,2,1,0:T(8,128)(2,1)S(1)}, u32[]{:S(2)}, u32[]{:S(2)}) collective-permute-start(bf16[9,1,2,32,256]{4,3,2,1,0:T(8,128)(2,1)S(1)} %pad_maximum_fusion.2), channel_id=1, source_target_pairs={{0,1},{1,2},{2,3},{3,4},{4,5},{5,6},{6,7},{7,8},{8,9},{9,10},{10,1... | collective-permute-start | bytes 884744 | tf_op jit(solution)/shard_map/ppermute | solution.py:28
  82.9 3.1 %collective-permute-done.7 = bf16[9,1,2,32,256]{4,3,2,1,0:T(8,128)(2,1)S(1)} collective-permute-done((bf16[9,1,2,32,256]{4,3,2,1,0:T(8,128)(2,1)S(1)}, bf16[9,1,2,32,256]{4,3,2,1,0:T(8,128)(2,1)S(1)}, u32[]{:S(2)}, u32[]{:S(2)}) %collective-permute-start.7) | collective-permute-done | bytes 294944 | tf_op jit(solution)/shard_map/ppermute | solution.py:28
  86.4 3.8 %collective-permute-start.13 = (bf16[1,18,32,256]{3,2,1,0:T(8,128)(2,1)S(1)}, bf16[1,18,32,256]{3,2,1,0:T(8,128)(2,1)S(1)}, u32[]{:S(2)}, u32[]{:S(2)}) collective-permute-start(bf16[1,18,32,256]{3,2,1,0:T(8,128)(2,1)S(1)} %fusion.65), channel_id=1, source_target_pairs={{0,64},{64,128},{128,192},{192,256},{256,320},{320,384},{384,448},... | collective-permute-start | bytes 884744 | tf_op jit(solution)/shard_map/ppermute | solution.py:17
  92.1 1.8 collective-permute-done.13
  94.1 3.7 %collective-permute-done.12 = bf16[1,18,32,256]{3,2,1,0:T(8,128)(2,1)S(1)} collective-permute-done((bf16[1,18,32,256]{3,2,1,0:T(8,128)(2,1)S(1)}, bf16[1,18,32,256]{3,2,1,0:T(8,128)(2,1)S(1)}, u32[]{:S(2)}, u32[]{:S(2)}) %collective-permute-start.12) | collective-permute-done | bytes 294944 | tf_op jit(solution)/shard_map/ppermute | solution.py:20
  100.5 2.2 collective-permute-start.15
  102.7 1.3 collective-permute-start.14
  104.2 2.6 collective-permute-done.15
  107.1 3.9 %collective-permute-done.14 = bf16[1,16,32,256]{3,2,1,0:T(8,128)(2,1)S(1)} collective-permute-done((bf16[1,16,32,256]{3,2,1,0:T(8,128)(2,1)S(1)}, bf16[1,16,32,256]{3,2,1,0:T(8,128)(2,1)S(1)}, u32[]{:S(2)}, u32[]{:S(2)}) %collective-permute-start.14) | collective-permute-done | bytes 262176 | tf_op jit(solution)/shard_map/ppermute | solution.py:20
  113.5 3.8 %collective-permute-start.17 = (bf16[1,14,32,256]{3,2,1,0:T(8,128)(2,1)S(1)}, bf16[1,14,32,256]{3,2,1,0:T(8,128)(2,1)S(1)}, u32[]{:S(2)}, u32[]{:S(2)}) collective-permute-start(bf16[1,14,32,256]{3,2,1,0:T(8,128)(2,1)S(1)} %get-tuple-element.69), channel_id=1, source_target_pairs={{0,64},{64,128},{128,192},{192,256},{256,320},{320,384},{384,448},... | collective-permute-start | bytes 688136 | tf_op jit(solution)/shard_map/ppermute | solution.py:17
  117.3 1.3 collective-permute-start.16
  118.8 3.0 %collective-permute-done.17 = bf16[1,14,32,256]{3,2,1,0:T(8,128)(2,1)S(1)} collective-permute-done((bf16[1,14,32,256]{3,2,1,0:T(8,128)(2,1)S(1)}, bf16[1,14,32,256]{3,2,1,0:T(8,128)(2,1)S(1)}, u32[]{:S(2)}, u32[]{:S(2)}) %collective-permute-start.17) | collective-permute-done | bytes 229408 | tf_op jit(solution)/shard_map/ppermute | solution.py:17
  122.0 4.1 %collective-permute-done.16 = bf16[1,14,32,256]{3,2,1,0:T(8,128)(2,1)S(1)} collective-permute-done((bf16[1,14,32,256]{3,2,1,0:T(8,128)(2,1)S(1)}, bf16[1,14,32,256]{3,2,1,0:T(8,128)(2,1)S(1)}, u32[]{:S(2)}, u32[]{:S(2)}) %collective-permute-start.16) | collective-permute-done | bytes 229408 | tf_op jit(solution)/shard_map/ppermute | solution.py:20
  128.6 3.6 %collective-permute-start.19 = (bf16[1,12,32,256]{3,2,1,0:T(8,128)(2,1)S(1)}, bf16[1,12,32,256]{3,2,1,0:T(8,128)(2,1)S(1)}, u32[]{:S(2)}, u32[]{:S(2)}) collective-permute-start(bf16[1,12,32,256]{3,2,1,0:T(8,128)(2,1)S(1)} %get-tuple-element.71), channel_id=1, source_target_pairs={{0,64},{64,128},{128,192},{192,256},{256,320},{320,384},{384,448},... | collective-permute-start | bytes 589832 | tf_op jit(solution)/shard_map/ppermute | solution.py:17
  132.3 1.5 collective-permute-start.18
  134.0 2.1 collective-permute-done.19
  136.4 3.6 %collective-permute-done.18 = bf16[1,12,32,256]{3,2,1,0:T(8,128)(2,1)S(1)} collective-permute-done((bf16[1,12,32,256]{3,2,1,0:T(8,128)(2,1)S(1)}, bf16[1,12,32,256]{3,2,1,0:T(8,128)(2,1)S(1)}, u32[]{:S(2)}, u32[]{:S(2)}) %collective-permute-start.18) | collective-permute-done | bytes 196640 | tf_op jit(solution)/shard_map/ppermute | solution.py:20
  142.3 2.8 %collective-permute-start.21 = (bf16[1,10,32,256]{3,2,1,0:T(8,128)(2,1)S(1)}, bf16[1,10,32,256]{3,2,1,0:T(8,128)(2,1)S(1)}, u32[]{:S(2)}, u32[]{:S(2)}) collective-permute-start(bf16[1,10,32,256]{3,2,1,0:T(8,128)(2,1)S(1)} %get-tuple-element.73), channel_id=1, source_target_pairs={{0,64},{64,128},{128,192},{192,256},{256,320},{320,384},{384,448},... | collective-permute-start | bytes 491528 | tf_op jit(solution)/shard_map/ppermute | solution.py:17
  147.6 3.6 %collective-permute-done.20 = bf16[1,10,32,256]{3,2,1,0:T(8,128)(2,1)S(1)} collective-permute-done((bf16[1,10,32,256]{3,2,1,0:T(8,128)(2,1)S(1)}, bf16[1,10,32,256]{3,2,1,0:T(8,128)(2,1)S(1)}, u32[]{:S(2)}, u32[]{:S(2)}) %collective-permute-start.20) | collective-permute-done | bytes 163872 | tf_op jit(solution)/shard_map/ppermute | solution.py:20
  153.4 3.5 %collective-permute-start.23 = (bf16[1,8,32,256]{3,2,1,0:T(8,128)(2,1)S(1)}, bf16[1,8,32,256]{3,2,1,0:T(8,128)(2,1)S(1)}, u32[]{:S(2)}, u32[]{:S(2)}) collective-permute-start(bf16[1,8,32,256]{3,2,1,0:T(8,128)(2,1)S(1)} %get-tuple-element.75), channel_id=1, source_target_pairs={{0,64},{64,128},{128,192},{192,256},{256,320},{320,384},{384,448},... | collective-permute-start | bytes 393224 | tf_op jit(solution)/shard_map/ppermute | solution.py:17
  156.9 1.3 collective-permute-start.22
  159.0 3.8 %collective-permute-done.22 = bf16[1,8,32,256]{3,2,1,0:T(8,128)(2,1)S(1)} collective-permute-done((bf16[1,8,32,256]{3,2,1,0:T(8,128)(2,1)S(1)}, bf16[1,8,32,256]{3,2,1,0:T(8,128)(2,1)S(1)}, u32[]{:S(2)}, u32[]{:S(2)}) %collective-permute-start.22) | collective-permute-done | bytes 131104 | tf_op jit(solution)/shard_map/ppermute | solution.py:20
  165.0 3.5 %collective-permute-start.25 = (bf16[1,6,32,256]{3,2,1,0:T(8,128)(2,1)S(1)}, bf16[1,6,32,256]{3,2,1,0:T(8,128)(2,1)S(1)}, u32[]{:S(2)}, u32[]{:S(2)}) collective-permute-start(bf16[1,6,32,256]{3,2,1,0:T(8,128)(2,1)S(1)} %get-tuple-element.77), channel_id=1, source_target_pairs={{0,64},{64,128},{128,192},{192,256},{256,320},{320,384},{384,448},... | collective-permute-start | bytes 294920 | tf_op jit(solution)/shard_map/ppermute | solution.py:17
  170.2 3.6 %collective-permute-done.24 = bf16[1,6,32,256]{3,2,1,0:T(8,128)(2,1)S(1)} collective-permute-done((bf16[1,6,32,256]{3,2,1,0:T(8,128)(2,1)S(1)}, bf16[1,6,32,256]{3,2,1,0:T(8,128)(2,1)S(1)}, u32[]{:S(2)}, u32[]{:S(2)}) %collective-permute-start.24) | collective-permute-done | bytes 98336 | tf_op jit(solution)/shard_map/ppermute | solution.py:20
  175.5 1.5 fusion.187
  177.1 4.3 %collective-permute-start.27 = (bf16[1,4,32,256]{3,2,1,0:T(8,128)(2,1)S(1)}, bf16[1,4,32,256]{3,2,1,0:T(8,128)(2,1)}, u32[]{:S(2)}, u32[]{:S(2)}) collective-permute-start(bf16[1,4,32,256]{3,2,1,0:T(8,128)(2,1)S(1)} %get-tuple-element.79), channel_id=1, source_target_pairs={{0,64},{64,128},{128,192},{192,256},{256,320},{320,384},{384,448},... | collective-permute-start | bytes 196616 | tf_op jit(solution)/shard_map/ppermute | solution.py:17
  185.0 1.8 reshape.1378
  195.8 1.7 mul.87
  197.5 27.9 %all-to-all-start.1 = ((f32[512,1,192]{2,1,0:T(1,128)}), f32[512,1,192]{2,1,0:T(1,128)S(1)}, u32[]{:S(2)}, u32[]{:S(2)}) async-start(f32[512,1,192]{2,1,0:T(1,128)} %mul.87), calls=%async_computation.1 | async-start | bytes 1048576 | tf_op jit(solution)/shard_map/all_to_all | solution.py:240
  226.0 22.1 %all-to-all-done.1 = f32[512,1,192]{2,1,0:T(1,128)S(1)} async-done(((f32[512,1,192]{2,1,0:T(1,128)}), f32[512,1,192]{2,1,0:T(1,128)S(1)}, u32[]{:S(2)}, u32[]{:S(2)}) %all-to-all-start.1) | async-done | bytes 393248 | tf_op jit(solution)/shard_map/all_to_all | solution.py:240
  249.4 4.2 %all-to-all-start.2 = ((f32[64,1,192]{2,1,0:T(1,128)}), f32[64,1,192]{2,1,0:T(1,128)S(1)}, u32[]{:S(2)}, u32[]{:S(2)}) async-start(f32[64,1,192]{2,1,0:T(1,128)} %broadcast_in_dim.21), calls=%async_computation.2 | async-start | bytes 131072 | tf_op jit(solution)/shard_map/all_to_all | solution.py:241
  254.4 9.0 %all-to-all-done.2 = f32[64,1,192]{2,1,0:T(1,128)S(1)} async-done(((f32[64,1,192]{2,1,0:T(1,128)}), f32[64,1,192]{2,1,0:T(1,128)S(1)}, u32[]{:S(2)}, u32[]{:S(2)}) %all-to-all-start.2) | async-done | bytes 49184 | tf_op jit(solution)/shard_map/all_to_all | solution.py:241
  (260 shorter events, 49.9 us)
Async XLA Ops:
  0.6 14.5 %copy-start.11 = (s32[1,12]{1,0:T(1,128)S(1)}, s32[1,12]{1,0:T(1,128)}, u32[]{:S(2)}) copy-start(s32[1,12]{1,0:T(1,128)} %param.9) | copy-start | bytes 148
  4.3 27.3 %all-to-all-start = ((bf16[8,112,256]{2,1,0:T(8,128)(2,1)}), bf16[8,112,256]{2,1,0:T(8,128)(2,1)S(1)}, u32[]{:S(2)}, u32[]{:S(2)}) async-start(bf16[8,112,256]{2,1,0:T(8,128)(2,1)} %pad_maximum_fusion), calls=%async_computation | async-start | bytes 917504 | tf_op jit(solution)/shard_map/all_to_all | solution.py:147
  31.7 6.1 %collective-permute-start = (bf16[8,1,1,32,256]{4,3,2,0,1:T(8,128)(2,1)S(1)}, bf16[8,1,1,32,256]{4,3,2,0,1:T(8,128)(2,1)S(1)}, u32[]{:S(2)}, u32[]{:S(2)}) collective-permute-start(bf16[8,1,1,32,256]{4,3,2,0,1:T(8,128)(2,1)S(1)} %get-tuple-element.35), channel_id=1, source_target_pairs={{0,1},{1,2},{2,3},{3,4},{4,5},{5,6},{6,7},{7,8},{8,9},{9,10},{10,1... | collective-permute-start | bytes 393224 | tf_op jit(solution)/shard_map/ppermute | solution.py:17
  35.3 6.3 %collective-permute-start.1 = (bf16[8,1,1,32,256]{4,3,2,0,1:T(8,128)(2,1)S(1)}, bf16[8,1,1,32,256]{4,3,2,0,1:T(8,128)(2,1)S(1)}, u32[]{:S(2)}, u32[]{:S(2)}) collective-permute-start(bf16[8,1,1,32,256]{4,3,2,0,1:T(8,128)(2,1)S(1)} %get-tuple-element.36), channel_id=1, source_target_pairs={{1,0},{2,1},{3,2},{4,3},{5,4},{6,5},{7,6},{8,7},{9,8},{10,9},{11,1... | collective-permute-start | bytes 393224 | tf_op jit(solution)/shard_map/ppermute | solution.py:20
  37.8 4.7 %copy-start.5 = (bf16[8,1,1,32,256]{4,3,2,0,1:T(8,128)(2,1)}, bf16[8,1,1,32,256]{4,3,2,0,1:T(8,128)(2,1)S(1)}, u32[]{:S(2)}) copy-start(bf16[8,1,1,32,256]{4,3,2,0,1:T(8,128)(2,1)S(1)} %collective-permute-done) | copy-start | bytes 393220
  41.6 2.3 copy-start.3
  44.1 7.4 %collective-permute-start.3 = (bf16[8,1,2,32,256]{4,3,2,0,1:T(8,128)(2,1)S(1)}, bf16[8,1,2,32,256]{4,3,2,0,1:T(8,128)(2,1)S(1)}, u32[]{:S(2)}, u32[]{:S(2)}) collective-permute-start(bf16[8,1,2,32,256]{4,3,2,0,1:T(8,128)(2,1)S(1)} %bitcast.1402), channel_id=1, source_target_pairs={{64,0},{128,64},{192,128},{256,192},{320,256},{384,320},{448,384},... | collective-permute-start | bytes 786440 | tf_op jit(solution)/shard_map/ppermute | solution.py:20
  46.6 128.8 %copy-start.9 = (bf16[1,9,32,32]{2,3,1,0:T(8,128)(2,1)}, bf16[1,9,32,32]{2,3,1,0:T(8,128)(2,1)S(1)}, u32[]{:S(2)}) copy-start(bf16[1,9,32,32]{2,3,1,0:T(8,128)(2,1)S(1)} %copy.244) | copy-start | bytes 55300
  47.0 7.8 %collective-permute-start.2 = (bf16[8,1,2,32,256]{4,3,2,0,1:T(8,128)(2,1)S(1)}, bf16[8,1,2,32,256]{4,3,2,0,1:T(8,128)(2,1)S(1)}, u32[]{:S(2)}, u32[]{:S(2)}) collective-permute-start(bf16[8,1,2,32,256]{4,3,2,0,1:T(8,128)(2,1)S(1)} %bitcast.1403), channel_id=1, source_target_pairs={{0,64},{64,128},{128,192},{192,256},{256,320},{320,384},{384,448},... | collective-permute-start | bytes 786440 | tf_op jit(solution)/shard_map/ppermute | solution.py:17
  51.5 3.7 %copy-start.1 = (bf16[8,1,2,32,256]{4,3,2,0,1:T(8,128)(2,1)}, bf16[8,1,2,32,256]{4,3,2,0,1:T(8,128)(2,1)S(1)}, u32[]{:S(2)}) copy-start(bf16[8,1,2,32,256]{4,3,2,0,1:T(8,128)(2,1)S(1)} %collective-permute-done.3) | copy-start | bytes 786436
  51.7 3.5 %copy-start = (bf16[1,2,32,256]{3,2,1,0:T(8,128)(2,1)S(1)}, bf16[1,2,32,256]{3,2,1,0:T(8,128)(2,1)}, u32[]{:S(2)}) copy-start(bf16[1,2,32,256]{3,2,1,0:T(8,128)(2,1)} %param.6) | copy-start | bytes 98308
  55.3 21.2 %collective-permute-start.11 = (bf16[3,1,2,32,256]{4,3,2,1,0:T(8,128)(2,1)S(1)}, bf16[3,1,2,32,256]{4,3,2,1,0:T(8,128)(2,1)S(1)}, u32[]{:S(2)}, u32[]{:S(2)}) collective-permute-start(bf16[3,1,2,32,256]{4,3,2,1,0:T(8,128)(2,1)S(1)} %pad_maximum_fusion.13), channel_id=1, source_target_pairs={{4,0},{5,1},{6,2},{7,3},{8,4},{9,5},{10,6},{11,7},{12,8},{13,9},{1... | collective-permute-start | bytes 294920 | tf_op jit(solution)/shard_map/ppermute | solution.py:28
  56.6 15.8 %collective-permute-start.4 = (bf16[3,1,2,32,256]{4,3,2,1,0:T(8,128)(2,1)S(1)}, bf16[3,1,2,32,256]{4,3,2,1,0:T(8,128)(2,1)S(1)}, u32[]{:S(2)}, u32[]{:S(2)}) collective-permute-start(bf16[3,1,2,32,256]{4,3,2,1,0:T(8,128)(2,1)S(1)} %pad_maximum_fusion.13), channel_id=1, source_target_pairs={{0,4},{1,5},{2,6},{3,7},{4,8},{5,9},{6,10},{7,11},{8,12},{9,13},{1... | collective-permute-start | bytes 294920 | tf_op jit(solution)/shard_map/ppermute | solution.py:28
  63.2 15.2 %collective-permute-start.10 = (bf16[5,1,2,32,256]{4,3,2,1,0:T(8,128)(2,1)S(1)}, bf16[5,1,2,32,256]{4,3,2,1,0:T(8,128)(2,1)S(1)}, u32[]{:S(2)}, u32[]{:S(2)}) collective-permute-start(bf16[5,1,2,32,256]{4,3,2,1,0:T(8,128)(2,1)S(1)} %pad_maximum_fusion.6), channel_id=1, source_target_pairs={{3,0},{4,1},{5,2},{6,3},{7,4},{8,5},{9,6},{10,7},{11,8},{12,9},{13... | collective-permute-start | bytes 491528 | tf_op jit(solution)/shard_map/ppermute | solution.py:28
  64.5 17.6 %collective-permute-start.5 = (bf16[5,1,2,32,256]{4,3,2,1,0:T(8,128)(2,1)S(1)}, bf16[5,1,2,32,256]{4,3,2,1,0:T(8,128)(2,1)S(1)}, u32[]{:S(2)}, u32[]{:S(2)}) collective-permute-start(bf16[5,1,2,32,256]{4,3,2,1,0:T(8,128)(2,1)S(1)} %pad_maximum_fusion.6), channel_id=1, source_target_pairs={{0,3},{1,4},{2,5},{3,6},{4,7},{5,8},{6,9},{7,10},{8,11},{9,12},{10... | collective-permute-start | bytes 491528 | tf_op jit(solution)/shard_map/ppermute | solution.py:28
  71.0 11.1 %collective-permute-start.9 = (bf16[7,1,2,32,256]{4,3,2,1,0:T(8,128)(2,1)S(1)}, bf16[7,1,2,32,256]{4,3,2,1,0:T(8,128)(2,1)S(1)}, u32[]{:S(2)}, u32[]{:S(2)}) collective-permute-start(bf16[7,1,2,32,256]{4,3,2,1,0:T(8,128)(2,1)S(1)} %pad_maximum_fusion.5), channel_id=1, source_target_pairs={{2,0},{3,1},{4,2},{5,3},{6,4},{7,5},{8,6},{9,7},{10,8},{11,9},{12,... | collective-permute-start | bytes 688136 | tf_op jit(solution)/shard_map/ppermute | solution.py:28
  72.4 10.5 %collective-permute-start.6 = (bf16[7,1,2,32,256]{4,3,2,1,0:T(8,128)(2,1)S(1)}, bf16[7,1,2,32,256]{4,3,2,1,0:T(8,128)(2,1)S(1)}, u32[]{:S(2)}, u32[]{:S(2)}) collective-permute-start(bf16[7,1,2,32,256]{4,3,2,1,0:T(8,128)(2,1)S(1)} %pad_maximum_fusion.5), channel_id=1, source_target_pairs={{0,2},{1,3},{2,4},{3,5},{4,6},{5,7},{6,8},{7,9},{8,10},{9,11},{10,... | collective-permute-start | bytes 688136 | tf_op jit(solution)/shard_map/ppermute | solution.py:28
  76.4 9.7 %collective-permute-start.8 = (bf16[9,1,2,32,256]{4,3,2,1,0:T(8,128)(2,1)S(1)}, bf16[9,1,2,32,256]{4,3,2,1,0:T(8,128)(2,1)S(1)}, u32[]{:S(2)}, u32[]{:S(2)}) collective-permute-start(bf16[9,1,2,32,256]{4,3,2,1,0:T(8,128)(2,1)S(1)} %pad_maximum_fusion.2), channel_id=1, source_target_pairs={{1,0},{2,1},{3,2},{4,3},{5,4},{6,5},{7,6},{8,7},{9,8},{10,9},{11,1... | collective-permute-start | bytes 884744 | tf_op jit(solution)/shard_map/ppermute | solution.py:28
  78.4 7.7 %collective-permute-start.7 = (bf16[9,1,2,32,256]{4,3,2,1,0:T(8,128)(2,1)S(1)}, bf16[9,1,2,32,256]{4,3,2,1,0:T(8,128)(2,1)S(1)}, u32[]{:S(2)}, u32[]{:S(2)}) collective-permute-start(bf16[9,1,2,32,256]{4,3,2,1,0:T(8,128)(2,1)S(1)} %pad_maximum_fusion.2), channel_id=1, source_target_pairs={{0,1},{1,2},{2,3},{3,4},{4,5},{5,6},{6,7},{7,8},{8,9},{9,10},{10,1... | collective-permute-start | bytes 884744 | tf_op jit(solution)/shard_map/ppermute | solution.py:28
  86.4 7.5 %collective-permute-start.13 = (bf16[1,18,32,256]{3,2,1,0:T(8,128)(2,1)S(1)}, bf16[1,18,32,256]{3,2,1,0:T(8,128)(2,1)S(1)}, u32[]{:S(2)}, u32[]{:S(2)}) collective-permute-start(bf16[1,18,32,256]{3,2,1,0:T(8,128)(2,1)S(1)} %fusion.65), channel_id=1, source_target_pairs={{0,64},{64,128},{128,192},{192,256},{256,320},{320,384},{384,448},... | collective-permute-start | bytes 884744 | tf_op jit(solution)/shard_map/ppermute | solution.py:17
  90.2 7.6 %collective-permute-start.12 = (bf16[1,18,32,256]{3,2,1,0:T(8,128)(2,1)S(1)}, bf16[1,18,32,256]{3,2,1,0:T(8,128)(2,1)S(1)}, u32[]{:S(2)}, u32[]{:S(2)}) collective-permute-start(bf16[1,18,32,256]{3,2,1,0:T(8,128)(2,1)S(1)} %fusion.65), channel_id=1, source_target_pairs={{64,0},{128,64},{192,128},{256,192},{320,256},{384,320},{448,384},... | collective-permute-start | bytes 884744 | tf_op jit(solution)/shard_map/ppermute | solution.py:20
  100.5 6.3 %collective-permute-start.15 = (bf16[1,16,32,256]{3,2,1,0:T(8,128)(2,1)S(1)}, bf16[1,16,32,256]{3,2,1,0:T(8,128)(2,1)S(1)}, u32[]{:S(2)}, u32[]{:S(2)}) collective-permute-start(bf16[1,16,32,256]{3,2,1,0:T(8,128)(2,1)S(1)} %get-tuple-element.67), channel_id=1, source_target_pairs={{0,64},{64,128},{128,192},{192,256},{256,320},{320,384},{384,448},... | collective-permute-start | bytes 786440 | tf_op jit(solution)/shard_map/ppermute | solution.py:17
  102.7 8.3 %collective-permute-start.14 = (bf16[1,16,32,256]{3,2,1,0:T(8,128)(2,1)S(1)}, bf16[1,16,32,256]{3,2,1,0:T(8,128)(2,1)S(1)}, u32[]{:S(2)}, u32[]{:S(2)}) collective-permute-start(bf16[1,16,32,256]{3,2,1,0:T(8,128)(2,1)S(1)} %get-tuple-element.67), channel_id=1, source_target_pairs={{64,0},{128,64},{192,128},{256,192},{320,256},{384,320},{448,384},... | collective-permute-start | bytes 786440 | tf_op jit(solution)/shard_map/ppermute | solution.py:20
  113.5 8.3 %collective-permute-start.17 = (bf16[1,14,32,256]{3,2,1,0:T(8,128)(2,1)S(1)}, bf16[1,14,32,256]{3,2,1,0:T(8,128)(2,1)S(1)}, u32[]{:S(2)}, u32[]{:S(2)}) collective-permute-start(bf16[1,14,32,256]{3,2,1,0:T(8,128)(2,1)S(1)} %get-tuple-element.69), channel_id=1, source_target_pairs={{0,64},{64,128},{128,192},{192,256},{256,320},{320,384},{384,448},... | collective-permute-start | bytes 688136 | tf_op jit(solution)/shard_map/ppermute | solution.py:17
  117.3 8.9 %collective-permute-start.16 = (bf16[1,14,32,256]{3,2,1,0:T(8,128)(2,1)S(1)}, bf16[1,14,32,256]{3,2,1,0:T(8,128)(2,1)S(1)}, u32[]{:S(2)}, u32[]{:S(2)}) collective-permute-start(bf16[1,14,32,256]{3,2,1,0:T(8,128)(2,1)S(1)} %get-tuple-element.69), channel_id=1, source_target_pairs={{64,0},{128,64},{192,128},{256,192},{320,256},{384,320},{448,384},... | collective-permute-start | bytes 688136 | tf_op jit(solution)/shard_map/ppermute | solution.py:20
  128.6 7.5 %collective-permute-start.19 = (bf16[1,12,32,256]{3,2,1,0:T(8,128)(2,1)S(1)}, bf16[1,12,32,256]{3,2,1,0:T(8,128)(2,1)S(1)}, u32[]{:S(2)}, u32[]{:S(2)}) collective-permute-start(bf16[1,12,32,256]{3,2,1,0:T(8,128)(2,1)S(1)} %get-tuple-element.71), channel_id=1, source_target_pairs={{0,64},{64,128},{128,192},{192,256},{256,320},{320,384},{384,448},... | collective-permute-start | bytes 589832 | tf_op jit(solution)/shard_map/ppermute | solution.py:17
  132.3 7.7 %collective-permute-start.18 = (bf16[1,12,32,256]{3,2,1,0:T(8,128)(2,1)S(1)}, bf16[1,12,32,256]{3,2,1,0:T(8,128)(2,1)S(1)}, u32[]{:S(2)}, u32[]{:S(2)}) collective-permute-start(bf16[1,12,32,256]{3,2,1,0:T(8,128)(2,1)S(1)} %get-tuple-element.71), channel_id=1, source_target_pairs={{64,0},{128,64},{192,128},{256,192},{320,256},{384,320},{448,384},... | collective-permute-start | bytes 589832 | tf_op jit(solution)/shard_map/ppermute | solution.py:20
  142.3 5.1 %collective-permute-start.21 = (bf16[1,10,32,256]{3,2,1,0:T(8,128)(2,1)S(1)}, bf16[1,10,32,256]{3,2,1,0:T(8,128)(2,1)S(1)}, u32[]{:S(2)}, u32[]{:S(2)}) collective-permute-start(bf16[1,10,32,256]{3,2,1,0:T(8,128)(2,1)S(1)} %get-tuple-element.73), channel_id=1, source_target_pairs={{0,64},{64,128},{128,192},{192,256},{256,320},{320,384},{384,448},... | collective-permute-start | bytes 491528 | tf_op jit(solution)/shard_map/ppermute | solution.py:17
  145.1 6.1 %collective-permute-start.20 = (bf16[1,10,32,256]{3,2,1,0:T(8,128)(2,1)S(1)}, bf16[1,10,32,256]{3,2,1,0:T(8,128)(2,1)S(1)}, u32[]{:S(2)}, u32[]{:S(2)}) collective-permute-start(bf16[1,10,32,256]{3,2,1,0:T(8,128)(2,1)S(1)} %get-tuple-element.73), channel_id=1, source_target_pairs={{64,0},{128,64},{192,128},{256,192},{320,256},{384,320},{448,384},... | collective-permute-start | bytes 491528 | tf_op jit(solution)/shard_map/ppermute | solution.py:20
  153.4 5.4 %collective-permute-start.23 = (bf16[1,8,32,256]{3,2,1,0:T(8,128)(2,1)S(1)}, bf16[1,8,32,256]{3,2,1,0:T(8,128)(2,1)S(1)}, u32[]{:S(2)}, u32[]{:S(2)}) collective-permute-start(bf16[1,8,32,256]{3,2,1,0:T(8,128)(2,1)S(1)} %get-tuple-element.75), channel_id=1, source_target_pairs={{0,64},{64,128},{128,192},{192,256},{256,320},{320,384},{384,448},... | collective-permute-start | bytes 393224 | tf_op jit(solution)/shard_map/ppermute | solution.py:17
  156.9 5.9 %collective-permute-start.22 = (bf16[1,8,32,256]{3,2,1,0:T(8,128)(2,1)S(1)}, bf16[1,8,32,256]{3,2,1,0:T(8,128)(2,1)S(1)}, u32[]{:S(2)}, u32[]{:S(2)}) collective-permute-start(bf16[1,8,32,256]{3,2,1,0:T(8,128)(2,1)S(1)} %get-tuple-element.75), channel_id=1, source_target_pairs={{64,0},{128,64},{192,128},{256,192},{320,256},{384,320},{448,384},... | collective-permute-start | bytes 393224 | tf_op jit(solution)/shard_map/ppermute | solution.py:20
  165.0 5.1 %collective-permute-start.25 = (bf16[1,6,32,256]{3,2,1,0:T(8,128)(2,1)S(1)}, bf16[1,6,32,256]{3,2,1,0:T(8,128)(2,1)S(1)}, u32[]{:S(2)}, u32[]{:S(2)}) collective-permute-start(bf16[1,6,32,256]{3,2,1,0:T(8,128)(2,1)S(1)} %get-tuple-element.77), channel_id=1, source_target_pairs={{0,64},{64,128},{128,192},{192,256},{256,320},{320,384},{384,448},... | collective-permute-start | bytes 294920 | tf_op jit(solution)/shard_map/ppermute | solution.py:17
  168.4 5.4 %collective-permute-start.24 = (bf16[1,6,32,256]{3,2,1,0:T(8,128)(2,1)S(1)}, bf16[1,6,32,256]{3,2,1,0:T(8,128)(2,1)S(1)}, u32[]{:S(2)}, u32[]{:S(2)}) collective-permute-start(bf16[1,6,32,256]{3,2,1,0:T(8,128)(2,1)S(1)} %get-tuple-element.77), channel_id=1, source_target_pairs={{64,0},{128,64},{192,128},{256,192},{320,256},{384,320},{448,384},... | collective-permute-start | bytes 294920 | tf_op jit(solution)/shard_map/ppermute | solution.py:20
  175.4 8.4 %copy-start.2 = (bf16[8,1,2,32,256]{4,3,2,0,1:T(8,128)(2,1)S(1)}, bf16[8,1,2,32,256]{4,3,2,0,1:T(8,128)(2,1)}, u32[]{:S(2)}) copy-start(bf16[8,1,2,32,256]{4,3,2,0,1:T(8,128)(2,1)} %copy-done.1) | copy-start | bytes 786436
  177.1 9.7 %collective-permute-start.27 = (bf16[1,4,32,256]{3,2,1,0:T(8,128)(2,1)S(1)}, bf16[1,4,32,256]{3,2,1,0:T(8,128)(2,1)}, u32[]{:S(2)}, u32[]{:S(2)}) collective-permute-start(bf16[1,4,32,256]{3,2,1,0:T(8,128)(2,1)S(1)} %get-tuple-element.79), channel_id=1, source_target_pairs={{0,64},{64,128},{128,192},{192,256},{256,320},{320,384},{384,448},... | collective-permute-start | bytes 196616 | tf_op jit(solution)/shard_map/ppermute | solution.py:17
  181.3 6.5 %collective-permute-start.26 = (bf16[1,4,32,256]{3,2,1,0:T(8,128)(2,1)S(1)}, bf16[1,4,32,256]{3,2,1,0:T(8,128)(2,1)}, u32[]{:S(2)}, u32[]{:S(2)}) collective-permute-start(bf16[1,4,32,256]{3,2,1,0:T(8,128)(2,1)S(1)} %get-tuple-element.79), channel_id=1, source_target_pairs={{64,0},{128,64},{192,128},{256,192},{320,256},{384,320},{448,384},... | collective-permute-start | bytes 196616 | tf_op jit(solution)/shard_map/ppermute | solution.py:20
  187.8 5.0 %copy-start.6 = (bf16[8,1,1,32,256]{4,3,2,0,1:T(8,128)(2,1)S(1)}, bf16[8,1,1,32,256]{4,3,2,0,1:T(8,128)(2,1)}, u32[]{:S(2)}) copy-start(bf16[8,1,1,32,256]{4,3,2,0,1:T(8,128)(2,1)} %copy-done.5) | copy-start | bytes 393220
  193.3 0.9 copy-start.4
  194.8 0.9 copy-start.7
  195.7 29.7 %copy-start.8 = (bf16[1,9,32,32]{2,3,1,0:T(8,128)(2,1)S(1)}, bf16[1,9,32,32]{2,3,1,0:T(8,128)(2,1)}, u32[]{:S(2)}) copy-start(bf16[1,9,32,32]{2,3,1,0:T(8,128)(2,1)} %copy.248) | copy-start | bytes 55300
  197.5 56.1 %copy-start.10 = (bf16[1,4,32,256]{3,2,1,0:T(8,128)(2,1)S(1)}, bf16[1,4,32,256]{3,2,1,0:T(8,128)(2,1)}, u32[]{:S(2)}) copy-start(bf16[1,4,32,256]{3,2,1,0:T(8,128)(2,1)} %get-tuple-element.80) | copy-start | bytes 196612
  197.5 50.6 %all-to-all-start.1 = ((f32[512,1,192]{2,1,0:T(1,128)}), f32[512,1,192]{2,1,0:T(1,128)S(1)}, u32[]{:S(2)}, u32[]{:S(2)}) async-start(f32[512,1,192]{2,1,0:T(1,128)} %mul.87), calls=%async_computation.1 | async-start | bytes 1048576 | tf_op jit(solution)/shard_map/all_to_all | solution.py:240
  249.4 14.0 %all-to-all-start.2 = ((f32[64,1,192]{2,1,0:T(1,128)}), f32[64,1,192]{2,1,0:T(1,128)S(1)}, u32[]{:S(2)}, u32[]{:S(2)}) async-start(f32[64,1,192]{2,1,0:T(1,128)} %broadcast_in_dim.21), calls=%async_computation.2 | async-start | bytes 131072 | tf_op jit(solution)/shard_map/all_to_all | solution.py:241

commit v6 on v5

--- a/solution.py
+++ b/solution.py
@@ -207,31 +207,28 @@
         depth_list[layer] = grad_mix[:, h : h + height]
         plane_list[layer] = grad_mid[:, h : h + height]
 
-    mixes = jnp.stack(depth_list)
-    mids = jnp.stack(plane_list)
     wide_rows = width_pad(rows_own)
-    planes = jnp.stack(
-        [
-            jnp.einsum(
-                "lzyox,lzycx->loc",
-                mids,
-                wide_rows[:, :, i : i + height, :, j : j + width],
-                preferred_element_type=jnp.float32,
-            )
-            for i in range(3)
-            for j in range(3)
-        ],
-        axis=1,
-    ).reshape(layers, -1)
-    depths = jnp.stack(
-        [
-            jnp.einsum(
-                "lzyox,lzycx->loc", mixes, deep[:, k : k + zs], preferred_element_type=jnp.float32
-            )
-            for k in range(3)
-        ],
-        axis=1,
-    ).reshape(layers, -1)
+
+    def kernel_grads(chosen):
+        mids = jnp.stack([plane_list[layer] for layer in chosen])
+        mixes = jnp.stack([depth_list[layer] for layer in chosen])
+        rows = wide_rows[chosen[0] : chosen[-1] + 1]
+        shifted = jnp.concatenate(
+            [rows[:, :, i : i + height, :, j : j + width] for i in range(3) for j in range(3)],
+            axis=3,
+        )
+        planes = jnp.einsum("lzyox,lzykx->lok", mids, shifted, preferred_element_type=jnp.float32)
+        planes = planes.reshape(len(chosen), chans, 9, chans).transpose(0, 2, 1, 3)
+        deeps = deep[chosen[0] : chosen[-1] + 1]
+        stacked = jnp.concatenate([deeps[:, k : k + zs] for k in range(3)], axis=3)
+        depths = jnp.einsum("lzyox,lzykx->lok", mixes, stacked, preferred_element_type=jnp.float32)
+        depths = depths.reshape(len(chosen), chans, 3, chans).transpose(0, 2, 1, 3)
+        return planes.reshape(len(chosen), -1), depths.reshape(len(chosen), -1)
+
+    first_p, first_d = kernel_grads([0])
+    rest_p, rest_d = kernel_grads(list(range(1, layers)))
+    planes = jnp.concatenate([first_p, rest_p])
+    depths = jnp.concatenate([first_d, rest_d])
     flat = jnp.concatenate([planes, depths], axis=1) * scale
     spread_n = lax.axis_size("gy")
     size = flat.shape[1]

time: 267 us -> 260 us (0.974)
  waiting for transfers between devices: 95.4 us -> 90.7 us
  transfers between devices with their start and end apart: 31 -> 31, of which waited for: 22 -> 22; matrix products, arithmetic and copies ran while one was open for 5% -> 6% of each run, Pallas kernels for 0% -> 0%
where the time goes in v6:
time: 260 us; the launch traced here: 258 us
  starting transfers between devices  118 us (45%)
  waiting for transfers between devices  90.7 us (35%)
  matrix products  31.6 us (12%)
  local copies, waits for them, and re-layouts  11.2 us (4%)
  other arithmetic  4.29 us (2%)
    ppermute x10, starting transfers between devices, padded_2(): lax.ppermute(lax.slice_in_dim(block, block.shape[dim] - width, None, axis...  35.3 us
    ppermute x10, waiting for transfers between devices, padded_2(): lax.ppermute(lax.slice_in_dim(block, 0, width, axis=dim), axis, backward)  28 us
    all_to_all x1, starting transfers between devices, local(): part = lax.all_to_all(flat, ('segment', 'gy'), 0, 0, tiled=True).sum(axis=0)  27.3 us
    ppermute x8, starting transfers between devices, passed_along(): return lax.ppermute(block, axis, route)  26.9 us
    all_to_all x1, waiting for transfers between devices, local(): part = lax.all_to_all(flat, ('segment', 'gy'), 0, 0, tiled=True).sum(axis=0)  22.1 us
    dot_general x72, matrix products, plane_back(): jnp.einsum('oc,...yox->...ycx', kernel[i, j], padded[..., 2 - i:2 - i + h...  18.4 us
    all_to_all x1, waiting for transfers between devices, local(): got = lax.all_to_all(send, 'segment', 0, 0, tiled=True)  16.2 us
    ppermute x10, starting transfers between devices, padded_2(): lax.ppermute(lax.slice_in_dim(block, 0, width, axis=dim), axis, backward)  13.7 us
  transfers between devices with their start and end apart: 31, of which 22 were waited for; matrix products, arithmetic and copies ran while one was open for 6% of the time, Pallas kernels for 0%

profile of v6, /device:TPU:1, one launch (start us, length us, event | category | flops | bytes accessed | tf_op | source)
XLA Modules:
  0.0 258.4 jit_solution(12772873218484790366)
XLA Ops:
  2.5 1.8 pad_maximum_fusion
  4.3 10.9 %all-to-all-start = ((bf16[8,112,256]{2,1,0:T(8,128)(2,1)}), bf16[8,112,256]{2,1,0:T(8,128)(2,1)S(1)}, u32[]{:S(2)}, u32[]{:S(2)}) async-start(bf16[8,112,256]{2,1,0:T(8,128)(2,1)} %pad_maximum_fusion), calls=%async_computation | async-start | bytes 917504 | tf_op jit(solution)/shard_map/all_to_all | solution.py:147
  15.5 16.2 %all-to-all-done = bf16[8,112,256]{2,1,0:T(8,128)(2,1)S(1)} async-done(((bf16[8,112,256]{2,1,0:T(8,128)(2,1)}), bf16[8,112,256]{2,1,0:T(8,128)(2,1)S(1)}, u32[]{:S(2)}, u32[]{:S(2)}) %all-to-all-start) | async-done | bytes 458784 | tf_op jit(solution)/shard_map/all_to_all | solution.py:147
  31.7 3.7 %collective-permute-start = (bf16[8,1,1,32,256]{4,3,2,0,1:T(8,128)(2,1)S(1)}, bf16[8,1,1,32,256]{4,3,2,0,1:T(8,128)(2,1)S(1)}, u32[]{:S(2)}, u32[]{:S(2)}) collective-permute-start(bf16[8,1,1,32,256]{4,3,2,0,1:T(8,128)(2,1)S(1)} %get-tuple-element.35), channel_id=1, source_target_pairs={{0,1},{1,2},{2,3},{3,4},{4,5},{5,6},{6,7},{7,8},{8,9},{9,10},{10,1... | collective-permute-start | bytes 393224 | tf_op jit(solution)/shard_map/ppermute | solution.py:17
  35.4 1.9 collective-permute-start.1
  40.0 1.6 collective-permute-done.1
  44.1 1.3 collective-permute-start.3
  45.4 4.0 %collective-permute-start.2 = (bf16[8,1,2,32,256]{4,3,2,0,1:T(8,128)(2,1)S(1)}, bf16[8,1,2,32,256]{4,3,2,0,1:T(8,128)(2,1)S(1)}, u32[]{:S(2)}, u32[]{:S(2)}) collective-permute-start(bf16[8,1,2,32,256]{4,3,2,0,1:T(8,128)(2,1)S(1)} %bitcast.1364), channel_id=1, source_target_pairs={{0,64},{64,128},{128,192},{192,256},{256,320},{320,384},{384,448},... | collective-permute-start | bytes 786440 | tf_op jit(solution)/shard_map/ppermute | solution.py:17
  51.7 1.5 collective-permute-done.2
  53.7 1.3 collective-permute-start.11
  55.0 6.8 %collective-permute-start.4 = (bf16[3,1,2,32,256]{4,3,2,1,0:T(8,128)(2,1)S(1)}, bf16[3,1,2,32,256]{4,3,2,1,0:T(8,128)(2,1)S(1)}, u32[]{:S(2)}, u32[]{:S(2)}) collective-permute-start(bf16[3,1,2,32,256]{4,3,2,1,0:T(8,128)(2,1)S(1)} %pad_maximum_fusion.12), channel_id=1, source_target_pairs={{0,4},{1,5},{2,6},{3,7},{4,8},{5,9},{6,10},{7,11},{8,12},{9,13},{1... | collective-permute-start | bytes 294920 | tf_op jit(solution)/shard_map/ppermute | solution.py:28
  61.8 1.3 collective-permute-start.10
  63.1 6.6 %collective-permute-start.5 = (bf16[5,1,2,32,256]{4,3,2,1,0:T(8,128)(2,1)S(1)}, bf16[5,1,2,32,256]{4,3,2,1,0:T(8,128)(2,1)S(1)}, u32[]{:S(2)}, u32[]{:S(2)}) collective-permute-start(bf16[5,1,2,32,256]{4,3,2,1,0:T(8,128)(2,1)S(1)} %pad_maximum_fusion.5), channel_id=1, source_target_pairs={{0,3},{1,4},{2,5},{3,6},{4,7},{5,8},{6,9},{7,10},{8,11},{9,12},{10... | collective-permute-start | bytes 491528 | tf_op jit(solution)/shard_map/ppermute | solution.py:28
  69.9 1.3 collective-permute-start.9
  71.3 4.0 %collective-permute-start.6 = (bf16[7,1,2,32,256]{4,3,2,1,0:T(8,128)(2,1)S(1)}, bf16[7,1,2,32,256]{4,3,2,1,0:T(8,128)(2,1)S(1)}, u32[]{:S(2)}, u32[]{:S(2)}) collective-permute-start(bf16[7,1,2,32,256]{4,3,2,1,0:T(8,128)(2,1)S(1)} %pad_maximum_fusion.4), channel_id=1, source_target_pairs={{0,2},{1,3},{2,4},{3,5},{4,6},{5,7},{6,8},{7,9},{8,10},{9,11},{10,... | collective-permute-start | bytes 688136 | tf_op jit(solution)/shard_map/ppermute | solution.py:28
  75.3 1.9 collective-permute-start.8
  77.3 3.6 %collective-permute-start.7 = (bf16[9,1,2,32,256]{4,3,2,1,0:T(8,128)(2,1)S(1)}, bf16[9,1,2,32,256]{4,3,2,1,0:T(8,128)(2,1)S(1)}, u32[]{:S(2)}, u32[]{:S(2)}) collective-permute-start(bf16[9,1,2,32,256]{4,3,2,1,0:T(8,128)(2,1)S(1)} %pad_maximum_fusion.1), channel_id=1, source_target_pairs={{0,1},{1,2},{2,3},{3,4},{4,5},{5,6},{6,7},{7,8},{8,9},{9,10},{10,1... | collective-permute-start | bytes 884744 | tf_op jit(solution)/shard_map/ppermute | solution.py:28
  81.7 3.1 %collective-permute-done.7 = bf16[9,1,2,32,256]{4,3,2,1,0:T(8,128)(2,1)S(1)} collective-permute-done((bf16[9,1,2,32,256]{4,3,2,1,0:T(8,128)(2,1)S(1)}, bf16[9,1,2,32,256]{4,3,2,1,0:T(8,128)(2,1)S(1)}, u32[]{:S(2)}, u32[]{:S(2)}) %collective-permute-start.7) | collective-permute-done | bytes 294944 | tf_op jit(solution)/shard_map/ppermute | solution.py:28
  85.1 3.9 %collective-permute-start.13 = (bf16[1,18,32,256]{3,2,1,0:T(8,128)(2,1)S(1)}, bf16[1,18,32,256]{3,2,1,0:T(8,128)(2,1)S(1)}, u32[]{:S(2)}, u32[]{:S(2)}) collective-permute-start(bf16[1,18,32,256]{3,2,1,0:T(8,128)(2,1)S(1)} %fusion.61), channel_id=1, source_target_pairs={{0,64},{64,128},{128,192},{192,256},{256,320},{320,384},{384,448},... | collective-permute-start | bytes 884744 | tf_op jit(solution)/shard_map/ppermute | solution.py:17
  89.0 1.3 collective-permute-start.12
  92.9 3.8 %collective-permute-done.12 = bf16[1,18,32,256]{3,2,1,0:T(8,128)(2,1)S(1)} collective-permute-done((bf16[1,18,32,256]{3,2,1,0:T(8,128)(2,1)S(1)}, bf16[1,18,32,256]{3,2,1,0:T(8,128)(2,1)S(1)}, u32[]{:S(2)}, u32[]{:S(2)}) %collective-permute-start.12) | collective-permute-done | bytes 294944 | tf_op jit(solution)/shard_map/ppermute | solution.py:20
  99.4 2.2 collective-permute-start.15
  101.6 1.3 collective-permute-start.14
  103.1 2.7 %collective-permute-done.15 = bf16[1,16,32,256]{3,2,1,0:T(8,128)(2,1)S(1)} collective-permute-done((bf16[1,16,32,256]{3,2,1,0:T(8,128)(2,1)S(1)}, bf16[1,16,32,256]{3,2,1,0:T(8,128)(2,1)S(1)}, u32[]{:S(2)}, u32[]{:S(2)}) %collective-permute-start.15) | collective-permute-done | bytes 262176 | tf_op jit(solution)/shard_map/ppermute | solution.py:17
  106.0 3.9 %collective-permute-done.14 = bf16[1,16,32,256]{3,2,1,0:T(8,128)(2,1)S(1)} collective-permute-done((bf16[1,16,32,256]{3,2,1,0:T(8,128)(2,1)S(1)}, bf16[1,16,32,256]{3,2,1,0:T(8,128)(2,1)S(1)}, u32[]{:S(2)}, u32[]{:S(2)}) %collective-permute-start.14) | collective-permute-done | bytes 262176 | tf_op jit(solution)/shard_map/ppermute | solution.py:20
  112.5 3.8 %collective-permute-start.17 = (bf16[1,14,32,256]{3,2,1,0:T(8,128)(2,1)S(1)}, bf16[1,14,32,256]{3,2,1,0:T(8,128)(2,1)S(1)}, u32[]{:S(2)}, u32[]{:S(2)}) collective-permute-start(bf16[1,14,32,256]{3,2,1,0:T(8,128)(2,1)S(1)} %get-tuple-element.69), channel_id=1, source_target_pairs={{0,64},{64,128},{128,192},{192,256},{256,320},{320,384},{384,448},... | collective-permute-start | bytes 688136 | tf_op jit(solution)/shard_map/ppermute | solution.py:17
  116.2 1.3 collective-permute-start.16
  117.8 3.1 %collective-permute-done.17 = bf16[1,14,32,256]{3,2,1,0:T(8,128)(2,1)S(1)} collective-permute-done((bf16[1,14,32,256]{3,2,1,0:T(8,128)(2,1)S(1)}, bf16[1,14,32,256]{3,2,1,0:T(8,128)(2,1)S(1)}, u32[]{:S(2)}, u32[]{:S(2)}) %collective-permute-start.17) | collective-permute-done | bytes 229408 | tf_op jit(solution)/shard_map/ppermute | solution.py:17
  121.1 4.1 %collective-permute-done.16 = bf16[1,14,32,256]{3,2,1,0:T(8,128)(2,1)S(1)} collective-permute-done((bf16[1,14,32,256]{3,2,1,0:T(8,128)(2,1)S(1)}, bf16[1,14,32,256]{3,2,1,0:T(8,128)(2,1)S(1)}, u32[]{:S(2)}, u32[]{:S(2)}) %collective-permute-start.16) | collective-permute-done | bytes 229408 | tf_op jit(solution)/shard_map/ppermute | solution.py:20
  127.7 3.7 %collective-permute-start.19 = (bf16[1,12,32,256]{3,2,1,0:T(8,128)(2,1)S(1)}, bf16[1,12,32,256]{3,2,1,0:T(8,128)(2,1)S(1)}, u32[]{:S(2)}, u32[]{:S(2)}) collective-permute-start(bf16[1,12,32,256]{3,2,1,0:T(8,128)(2,1)S(1)} %get-tuple-element.71), channel_id=1, source_target_pairs={{0,64},{64,128},{128,192},{192,256},{256,320},{320,384},{384,448},... | collective-permute-start | bytes 589832 | tf_op jit(solution)/shard_map/ppermute | solution.py:17
  131.4 1.5 collective-permute-start.18
  133.1 2.1 collective-permute-done.19
  135.5 3.6 %collective-permute-done.18 = bf16[1,12,32,256]{3,2,1,0:T(8,128)(2,1)S(1)} collective-permute-done((bf16[1,12,32,256]{3,2,1,0:T(8,128)(2,1)S(1)}, bf16[1,12,32,256]{3,2,1,0:T(8,128)(2,1)S(1)}, u32[]{:S(2)}, u32[]{:S(2)}) %collective-permute-start.18) | collective-permute-done | bytes 196640 | tf_op jit(solution)/shard_map/ppermute | solution.py:20
  141.4 2.7 %collective-permute-start.21 = (bf16[1,10,32,256]{3,2,1,0:T(8,128)(2,1)S(1)}, bf16[1,10,32,256]{3,2,1,0:T(8,128)(2,1)S(1)}, u32[]{:S(2)}, u32[]{:S(2)}) collective-permute-start(bf16[1,10,32,256]{3,2,1,0:T(8,128)(2,1)S(1)} %get-tuple-element.73), channel_id=1, source_target_pairs={{0,64},{64,128},{128,192},{192,256},{256,320},{320,384},{384,448},... | collective-permute-start | bytes 491528 | tf_op jit(solution)/shard_map/ppermute | solution.py:17
  144.1 1.3 collective-permute-start.20
  146.5 3.6 %collective-permute-done.20 = bf16[1,10,32,256]{3,2,1,0:T(8,128)(2,1)S(1)} collective-permute-done((bf16[1,10,32,256]{3,2,1,0:T(8,128)(2,1)S(1)}, bf16[1,10,32,256]{3,2,1,0:T(8,128)(2,1)S(1)}, u32[]{:S(2)}, u32[]{:S(2)}) %collective-permute-start.20) | collective-permute-done | bytes 163872 | tf_op jit(solution)/shard_map/ppermute | solution.py:20
  152.3 3.6 %collective-permute-start.23 = (bf16[1,8,32,256]{3,2,1,0:T(8,128)(2,1)S(1)}, bf16[1,8,32,256]{3,2,1,0:T(8,128)(2,1)S(1)}, u32[]{:S(2)}, u32[]{:S(2)}) collective-permute-start(bf16[1,8,32,256]{3,2,1,0:T(8,128)(2,1)S(1)} %get-tuple-element.75), channel_id=1, source_target_pairs={{0,64},{64,128},{128,192},{192,256},{256,320},{320,384},{384,448},... | collective-permute-start | bytes 393224 | tf_op jit(solution)/shard_map/ppermute | solution.py:17
  155.9 1.3 collective-permute-start.22
  158.1 3.8 %collective-permute-done.22 = bf16[1,8,32,256]{3,2,1,0:T(8,128)(2,1)S(1)} collective-permute-done((bf16[1,8,32,256]{3,2,1,0:T(8,128)(2,1)S(1)}, bf16[1,8,32,256]{3,2,1,0:T(8,128)(2,1)S(1)}, u32[]{:S(2)}, u32[]{:S(2)}) %collective-permute-start.22) | collective-permute-done | bytes 131104 | tf_op jit(solution)/shard_map/ppermute | solution.py:20
  164.7 4.1 %collective-permute-start.25 = (bf16[1,6,32,256]{3,2,1,0:T(8,128)(2,1)S(1)}, bf16[1,6,32,256]{3,2,1,0:T(8,128)(2,1)}, u32[]{:S(2)}, u32[]{:S(2)}) collective-permute-start(bf16[1,6,32,256]{3,2,1,0:T(8,128)(2,1)S(1)} %get-tuple-element.77), channel_id=1, source_target_pairs={{0,64},{64,128},{128,192},{192,256},{256,320},{320,384},{384,448},... | collective-permute-start | bytes 294920 | tf_op jit(solution)/shard_map/ppermute | solution.py:17
  172.2 1.9 collective-permute-done.24
  176.9 1.5 fusion.175
  178.4 3.6 %collective-permute-start.27 = (bf16[1,4,32,256]{3,2,1,0:T(8,128)(2,1)S(1)}, bf16[1,4,32,256]{3,2,1,0:T(8,128)(2,1)}, u32[]{:S(2)}, u32[]{:S(2)}) collective-permute-start(bf16[1,4,32,256]{3,2,1,0:T(8,128)(2,1)S(1)} %get-tuple-element.79), channel_id=1, source_target_pairs={{0,64},{64,128},{128,192},{192,256},{256,320},{320,384},{384,448},... | collective-permute-start | bytes 196616 | tf_op jit(solution)/shard_map/ppermute | solution.py:17
  189.5 1.7 mul.87
  191.2 27.3 %all-to-all-start.1 = ((f32[512,1,192]{2,1,0:T(1,128)}), f32[512,1,192]{2,1,0:T(1,128)S(1)}, u32[]{:S(2)}, u32[]{:S(2)}) async-start(f32[512,1,192]{2,1,0:T(1,128)} %mul.87), calls=%async_computation.1 | async-start | bytes 1048576 | tf_op jit(solution)/shard_map/all_to_all | solution.py:237
  219.2 22.1 %all-to-all-done.1 = f32[512,1,192]{2,1,0:T(1,128)S(1)} async-done(((f32[512,1,192]{2,1,0:T(1,128)}), f32[512,1,192]{2,1,0:T(1,128)S(1)}, u32[]{:S(2)}, u32[]{:S(2)}) %all-to-all-start.1) | async-done | bytes 393248 | tf_op jit(solution)/shard_map/all_to_all | solution.py:237
  242.5 4.2 %all-to-all-start.2 = ((f32[64,1,192]{2,1,0:T(1,128)}), f32[64,1,192]{2,1,0:T(1,128)S(1)}, u32[]{:S(2)}, u32[]{:S(2)}) async-start(f32[64,1,192]{2,1,0:T(1,128)} %broadcast_in_dim.21), calls=%async_computation.2 | async-start | bytes 131072 | tf_op jit(solution)/shard_map/all_to_all | solution.py:238
  247.5 9.0 %all-to-all-done.2 = f32[64,1,192]{2,1,0:T(1,128)S(1)} async-done(((f32[64,1,192]{2,1,0:T(1,128)}), f32[64,1,192]{2,1,0:T(1,128)S(1)}, u32[]{:S(2)}, u32[]{:S(2)}) %all-to-all-start.2) | async-done | bytes 49184 | tf_op jit(solution)/shard_map/all_to_all | solution.py:238
  (283 shorter events, 49.1 us)
Async XLA Ops:
  0.6 14.5 %copy-start.12 = (s32[1,12]{1,0:T(1,128)S(1)}, s32[1,12]{1,0:T(1,128)}, u32[]{:S(2)}) copy-start(s32[1,12]{1,0:T(1,128)} %param.9) | copy-start | bytes 148
  4.3 27.3 %all-to-all-start = ((bf16[8,112,256]{2,1,0:T(8,128)(2,1)}), bf16[8,112,256]{2,1,0:T(8,128)(2,1)S(1)}, u32[]{:S(2)}, u32[]{:S(2)}) async-start(bf16[8,112,256]{2,1,0:T(8,128)(2,1)} %pad_maximum_fusion), calls=%async_computation | async-start | bytes 917504 | tf_op jit(solution)/shard_map/all_to_all | solution.py:147
  31.7 8.3 %collective-permute-start = (bf16[8,1,1,32,256]{4,3,2,0,1:T(8,128)(2,1)S(1)}, bf16[8,1,1,32,256]{4,3,2,0,1:T(8,128)(2,1)S(1)}, u32[]{:S(2)}, u32[]{:S(2)}) collective-permute-start(bf16[8,1,1,32,256]{4,3,2,0,1:T(8,128)(2,1)S(1)} %get-tuple-element.35), channel_id=1, source_target_pairs={{0,1},{1,2},{2,3},{3,4},{4,5},{5,6},{6,7},{7,8},{8,9},{9,10},{10,1... | collective-permute-start | bytes 393224 | tf_op jit(solution)/shard_map/ppermute | solution.py:17
  35.4 6.3 %collective-permute-start.1 = (bf16[8,1,1,32,256]{4,3,2,0,1:T(8,128)(2,1)S(1)}, bf16[8,1,1,32,256]{4,3,2,0,1:T(8,128)(2,1)S(1)}, u32[]{:S(2)}, u32[]{:S(2)}) collective-permute-start(bf16[8,1,1,32,256]{4,3,2,0,1:T(8,128)(2,1)S(1)} %get-tuple-element.36), channel_id=1, source_target_pairs={{1,0},{2,1},{3,2},{4,3},{5,4},{6,5},{7,6},{8,7},{9,8},{10,9},{11,1... | collective-permute-start | bytes 393224 | tf_op jit(solution)/shard_map/ppermute | solution.py:20
  44.1 7.4 %collective-permute-start.3 = (bf16[8,1,2,32,256]{4,3,2,0,1:T(8,128)(2,1)S(1)}, bf16[8,1,2,32,256]{4,3,2,0,1:T(8,128)(2,1)S(1)}, u32[]{:S(2)}, u32[]{:S(2)}) collective-permute-start(bf16[8,1,2,32,256]{4,3,2,0,1:T(8,128)(2,1)S(1)} %bitcast.1363), channel_id=1, source_target_pairs={{64,0},{128,64},{192,128},{256,192},{320,256},{384,320},{448,384},... | collective-permute-start | bytes 786440 | tf_op jit(solution)/shard_map/ppermute | solution.py:20
  45.4 7.8 %collective-permute-start.2 = (bf16[8,1,2,32,256]{4,3,2,0,1:T(8,128)(2,1)S(1)}, bf16[8,1,2,32,256]{4,3,2,0,1:T(8,128)(2,1)S(1)}, u32[]{:S(2)}, u32[]{:S(2)}) collective-permute-start(bf16[8,1,2,32,256]{4,3,2,0,1:T(8,128)(2,1)S(1)} %bitcast.1364), channel_id=1, source_target_pairs={{0,64},{64,128},{128,192},{192,256},{256,320},{320,384},{384,448},... | collective-permute-start | bytes 786440 | tf_op jit(solution)/shard_map/ppermute | solution.py:17
  50.4 3.2 %copy-start = (bf16[7,1,2,288,256]{4,3,2,0,1:T(8,128)(2,1)}, bf16[7,1,2,288,256]{4,3,2,0,1:T(8,128)(2,1)S(1)}, u32[]{:S(2)}) copy-start(bf16[7,1,2,288,256]{4,3,2,0,1:T(8,128)(2,1)S(1)} %slice_dynamic-update-slice_fusion) | copy-start | bytes 6193156
  50.5 3.1 %copy-start.4 = (bf16[1,1,2,288,256]{4,3,2,0,1:T(8,128)(2,1)}, bf16[1,1,2,288,256]{4,3,2,0,1:T(8,128)(2,1)S(1)}, u32[]{:S(2)}) copy-start(bf16[1,1,2,288,256]{4,3,2,0,1:T(8,128)(2,1)S(1)} %constant_dynamic-update-slice_fusion.18) | copy-start | bytes 884740
  50.6 3.1 %copy-start.2 = (bf16[1,2,32,256]{3,2,1,0:T(8,128)(2,1)S(1)}, bf16[1,2,32,256]{3,2,1,0:T(8,128)(2,1)}, u32[]{:S(2)}) copy-start(bf16[1,2,32,256]{3,2,1,0:T(8,128)(2,1)} %param.6) | copy-start | bytes 98308
  51.5 19.7 %copy-start.3 = (bf16[8,1,2,32,256]{4,3,2,0,1:T(8,128)(2,1)}, bf16[8,1,2,32,256]{4,3,2,0,1:T(8,128)(2,1)S(1)}, u32[]{:S(2)}) copy-start(bf16[8,1,2,32,256]{4,3,2,0,1:T(8,128)(2,1)S(1)} %collective-permute-done.3) | copy-start | bytes 786436
  53.3 18.0 %copy-start.8 = (bf16[8,1,2,32,256]{4,3,2,0,1:T(8,128)(2,1)}, bf16[8,1,2,32,256]{4,3,2,0,1:T(8,128)(2,1)S(1)}, u32[]{:S(2)}) copy-start(bf16[8,1,2,32,256]{4,3,2,0,1:T(8,128)(2,1)S(1)} %collective-permute-done.2) | copy-start | bytes 786436
  53.7 21.7 %collective-permute-start.11 = (bf16[3,1,2,32,256]{4,3,2,1,0:T(8,128)(2,1)S(1)}, bf16[3,1,2,32,256]{4,3,2,1,0:T(8,128)(2,1)S(1)}, u32[]{:S(2)}, u32[]{:S(2)}) collective-permute-start(bf16[3,1,2,32,256]{4,3,2,1,0:T(8,128)(2,1)S(1)} %pad_maximum_fusion.12), channel_id=1, source_target_pairs={{4,0},{5,1},{6,2},{7,3},{8,4},{9,5},{10,6},{11,7},{12,8},{13,9},{1... | collective-permute-start | bytes 294920 | tf_op jit(solution)/shard_map/ppermute | solution.py:28
  55.0 16.3 %collective-permute-start.4 = (bf16[3,1,2,32,256]{4,3,2,1,0:T(8,128)(2,1)S(1)}, bf16[3,1,2,32,256]{4,3,2,1,0:T(8,128)(2,1)S(1)}, u32[]{:S(2)}, u32[]{:S(2)}) collective-permute-start(bf16[3,1,2,32,256]{4,3,2,1,0:T(8,128)(2,1)S(1)} %pad_maximum_fusion.12), channel_id=1, source_target_pairs={{0,4},{1,5},{2,6},{3,7},{4,8},{5,9},{6,10},{7,11},{8,12},{9,13},{1... | collective-permute-start | bytes 294920 | tf_op jit(solution)/shard_map/ppermute | solution.py:28
  61.8 15.5 %collective-permute-start.10 = (bf16[5,1,2,32,256]{4,3,2,1,0:T(8,128)(2,1)S(1)}, bf16[5,1,2,32,256]{4,3,2,1,0:T(8,128)(2,1)S(1)}, u32[]{:S(2)}, u32[]{:S(2)}) collective-permute-start(bf16[5,1,2,32,256]{4,3,2,1,0:T(8,128)(2,1)S(1)} %pad_maximum_fusion.5), channel_id=1, source_target_pairs={{3,0},{4,1},{5,2},{6,3},{7,4},{8,5},{9,6},{10,7},{11,8},{12,9},{13... | collective-permute-start | bytes 491528 | tf_op jit(solution)/shard_map/ppermute | solution.py:28
  63.1 17.8 %collective-permute-start.5 = (bf16[5,1,2,32,256]{4,3,2,1,0:T(8,128)(2,1)S(1)}, bf16[5,1,2,32,256]{4,3,2,1,0:T(8,128)(2,1)S(1)}, u32[]{:S(2)}, u32[]{:S(2)}) collective-permute-start(bf16[5,1,2,32,256]{4,3,2,1,0:T(8,128)(2,1)S(1)} %pad_maximum_fusion.5), channel_id=1, source_target_pairs={{0,3},{1,4},{2,5},{3,6},{4,7},{5,8},{6,9},{7,10},{8,11},{9,12},{10... | collective-permute-start | bytes 491528 | tf_op jit(solution)/shard_map/ppermute | solution.py:28
  69.9 11.2 %collective-permute-start.9 = (bf16[7,1,2,32,256]{4,3,2,1,0:T(8,128)(2,1)S(1)}, bf16[7,1,2,32,256]{4,3,2,1,0:T(8,128)(2,1)S(1)}, u32[]{:S(2)}, u32[]{:S(2)}) collective-permute-start(bf16[7,1,2,32,256]{4,3,2,1,0:T(8,128)(2,1)S(1)} %pad_maximum_fusion.4), channel_id=1, source_target_pairs={{2,0},{3,1},{4,2},{5,3},{6,4},{7,5},{8,6},{9,7},{10,8},{11,9},{12,... | collective-permute-start | bytes 688136 | tf_op jit(solution)/shard_map/ppermute | solution.py:28
  71.3 10.3 %collective-permute-start.6 = (bf16[7,1,2,32,256]{4,3,2,1,0:T(8,128)(2,1)S(1)}, bf16[7,1,2,32,256]{4,3,2,1,0:T(8,128)(2,1)S(1)}, u32[]{:S(2)}, u32[]{:S(2)}) collective-permute-start(bf16[7,1,2,32,256]{4,3,2,1,0:T(8,128)(2,1)S(1)} %pad_maximum_fusion.4), channel_id=1, source_target_pairs={{0,2},{1,3},{2,4},{3,5},{4,6},{5,7},{6,8},{7,9},{8,10},{9,11},{10,... | collective-permute-start | bytes 688136 | tf_op jit(solution)/shard_map/ppermute | solution.py:28
  75.3 9.5 %collective-permute-start.8 = (bf16[9,1,2,32,256]{4,3,2,1,0:T(8,128)(2,1)S(1)}, bf16[9,1,2,32,256]{4,3,2,1,0:T(8,128)(2,1)S(1)}, u32[]{:S(2)}, u32[]{:S(2)}) collective-permute-start(bf16[9,1,2,32,256]{4,3,2,1,0:T(8,128)(2,1)S(1)} %pad_maximum_fusion.1), channel_id=1, source_target_pairs={{1,0},{2,1},{3,2},{4,3},{5,4},{6,5},{7,6},{8,7},{9,8},{10,9},{11,1... | collective-permute-start | bytes 884744 | tf_op jit(solution)/shard_map/ppermute | solution.py:28
  77.3 7.5 %collective-permute-start.7 = (bf16[9,1,2,32,256]{4,3,2,1,0:T(8,128)(2,1)S(1)}, bf16[9,1,2,32,256]{4,3,2,1,0:T(8,128)(2,1)S(1)}, u32[]{:S(2)}, u32[]{:S(2)}) collective-permute-start(bf16[9,1,2,32,256]{4,3,2,1,0:T(8,128)(2,1)S(1)} %pad_maximum_fusion.1), channel_id=1, source_target_pairs={{0,1},{1,2},{2,3},{3,4},{4,5},{5,6},{6,7},{7,8},{8,9},{9,10},{10,1... | collective-permute-start | bytes 884744 | tf_op jit(solution)/shard_map/ppermute | solution.py:28
  85.1 7.6 %collective-permute-start.13 = (bf16[1,18,32,256]{3,2,1,0:T(8,128)(2,1)S(1)}, bf16[1,18,32,256]{3,2,1,0:T(8,128)(2,1)S(1)}, u32[]{:S(2)}, u32[]{:S(2)}) collective-permute-start(bf16[1,18,32,256]{3,2,1,0:T(8,128)(2,1)S(1)} %fusion.61), channel_id=1, source_target_pairs={{0,64},{64,128},{128,192},{192,256},{256,320},{320,384},{384,448},... | collective-permute-start | bytes 884744 | tf_op jit(solution)/shard_map/ppermute | solution.py:17
  89.0 7.7 %collective-permute-start.12 = (bf16[1,18,32,256]{3,2,1,0:T(8,128)(2,1)S(1)}, bf16[1,18,32,256]{3,2,1,0:T(8,128)(2,1)S(1)}, u32[]{:S(2)}, u32[]{:S(2)}) collective-permute-start(bf16[1,18,32,256]{3,2,1,0:T(8,128)(2,1)S(1)} %fusion.61), channel_id=1, source_target_pairs={{64,0},{128,64},{192,128},{256,192},{320,256},{384,320},{448,384},... | collective-permute-start | bytes 884744 | tf_op jit(solution)/shard_map/ppermute | solution.py:20
  99.4 6.4 %collective-permute-start.15 = (bf16[1,16,32,256]{3,2,1,0:T(8,128)(2,1)S(1)}, bf16[1,16,32,256]{3,2,1,0:T(8,128)(2,1)S(1)}, u32[]{:S(2)}, u32[]{:S(2)}) collective-permute-start(bf16[1,16,32,256]{3,2,1,0:T(8,128)(2,1)S(1)} %get-tuple-element.67), channel_id=1, source_target_pairs={{0,64},{64,128},{128,192},{192,256},{256,320},{320,384},{384,448},... | collective-permute-start | bytes 786440 | tf_op jit(solution)/shard_map/ppermute | solution.py:17
  101.6 8.3 %collective-permute-start.14 = (bf16[1,16,32,256]{3,2,1,0:T(8,128)(2,1)S(1)}, bf16[1,16,32,256]{3,2,1,0:T(8,128)(2,1)S(1)}, u32[]{:S(2)}, u32[]{:S(2)}) collective-permute-start(bf16[1,16,32,256]{3,2,1,0:T(8,128)(2,1)S(1)} %get-tuple-element.67), channel_id=1, source_target_pairs={{64,0},{128,64},{192,128},{256,192},{320,256},{384,320},{448,384},... | collective-permute-start | bytes 786440 | tf_op jit(solution)/shard_map/ppermute | solution.py:20
  112.5 8.4 %collective-permute-start.17 = (bf16[1,14,32,256]{3,2,1,0:T(8,128)(2,1)S(1)}, bf16[1,14,32,256]{3,2,1,0:T(8,128)(2,1)S(1)}, u32[]{:S(2)}, u32[]{:S(2)}) collective-permute-start(bf16[1,14,32,256]{3,2,1,0:T(8,128)(2,1)S(1)} %get-tuple-element.69), channel_id=1, source_target_pairs={{0,64},{64,128},{128,192},{192,256},{256,320},{320,384},{384,448},... | collective-permute-start | bytes 688136 | tf_op jit(solution)/shard_map/ppermute | solution.py:17
  116.2 9.0 %collective-permute-start.16 = (bf16[1,14,32,256]{3,2,1,0:T(8,128)(2,1)S(1)}, bf16[1,14,32,256]{3,2,1,0:T(8,128)(2,1)S(1)}, u32[]{:S(2)}, u32[]{:S(2)}) collective-permute-start(bf16[1,14,32,256]{3,2,1,0:T(8,128)(2,1)S(1)} %get-tuple-element.69), channel_id=1, source_target_pairs={{64,0},{128,64},{192,128},{256,192},{320,256},{384,320},{448,384},... | collective-permute-start | bytes 688136 | tf_op jit(solution)/shard_map/ppermute | solution.py:20
  127.7 7.6 %collective-permute-start.19 = (bf16[1,12,32,256]{3,2,1,0:T(8,128)(2,1)S(1)}, bf16[1,12,32,256]{3,2,1,0:T(8,128)(2,1)S(1)}, u32[]{:S(2)}, u32[]{:S(2)}) collective-permute-start(bf16[1,12,32,256]{3,2,1,0:T(8,128)(2,1)S(1)} %get-tuple-element.71), channel_id=1, source_target_pairs={{0,64},{64,128},{128,192},{192,256},{256,320},{320,384},{384,448},... | collective-permute-start | bytes 589832 | tf_op jit(solution)/shard_map/ppermute | solution.py:17
  131.4 7.7 %collective-permute-start.18 = (bf16[1,12,32,256]{3,2,1,0:T(8,128)(2,1)S(1)}, bf16[1,12,32,256]{3,2,1,0:T(8,128)(2,1)S(1)}, u32[]{:S(2)}, u32[]{:S(2)}) collective-permute-start(bf16[1,12,32,256]{3,2,1,0:T(8,128)(2,1)S(1)} %get-tuple-element.71), channel_id=1, source_target_pairs={{64,0},{128,64},{192,128},{256,192},{320,256},{384,320},{448,384},... | collective-permute-start | bytes 589832 | tf_op jit(solution)/shard_map/ppermute | solution.py:20
  141.4 4.9 %collective-permute-start.21 = (bf16[1,10,32,256]{3,2,1,0:T(8,128)(2,1)S(1)}, bf16[1,10,32,256]{3,2,1,0:T(8,128)(2,1)S(1)}, u32[]{:S(2)}, u32[]{:S(2)}) collective-permute-start(bf16[1,10,32,256]{3,2,1,0:T(8,128)(2,1)S(1)} %get-tuple-element.73), channel_id=1, source_target_pairs={{0,64},{64,128},{128,192},{192,256},{256,320},{320,384},{384,448},... | collective-permute-start | bytes 491528 | tf_op jit(solution)/shard_map/ppermute | solution.py:17
  144.1 6.1 %collective-permute-start.20 = (bf16[1,10,32,256]{3,2,1,0:T(8,128)(2,1)S(1)}, bf16[1,10,32,256]{3,2,1,0:T(8,128)(2,1)S(1)}, u32[]{:S(2)}, u32[]{:S(2)}) collective-permute-start(bf16[1,10,32,256]{3,2,1,0:T(8,128)(2,1)S(1)} %get-tuple-element.73), channel_id=1, source_target_pairs={{64,0},{128,64},{192,128},{256,192},{320,256},{384,320},{448,384},... | collective-permute-start | bytes 491528 | tf_op jit(solution)/shard_map/ppermute | solution.py:20
  152.3 5.5 %collective-permute-start.23 = (bf16[1,8,32,256]{3,2,1,0:T(8,128)(2,1)S(1)}, bf16[1,8,32,256]{3,2,1,0:T(8,128)(2,1)S(1)}, u32[]{:S(2)}, u32[]{:S(2)}) collective-permute-start(bf16[1,8,32,256]{3,2,1,0:T(8,128)(2,1)S(1)} %get-tuple-element.75), channel_id=1, source_target_pairs={{0,64},{64,128},{128,192},{192,256},{256,320},{320,384},{384,448},... | collective-permute-start | bytes 393224 | tf_op jit(solution)/shard_map/ppermute | solution.py:17
  155.9 5.9 %collective-permute-start.22 = (bf16[1,8,32,256]{3,2,1,0:T(8,128)(2,1)S(1)}, bf16[1,8,32,256]{3,2,1,0:T(8,128)(2,1)S(1)}, u32[]{:S(2)}, u32[]{:S(2)}) collective-permute-start(bf16[1,8,32,256]{3,2,1,0:T(8,128)(2,1)S(1)} %get-tuple-element.75), channel_id=1, source_target_pairs={{64,0},{128,64},{192,128},{256,192},{320,256},{384,320},{448,384},... | collective-permute-start | bytes 393224 | tf_op jit(solution)/shard_map/ppermute | solution.py:20
  162.7 7.6 %slice-start = ((bf16[8,1,2,32,256]{4,3,2,0,1:T(8,128)(2,1)}), bf16[7,1,2,32,256]{4,3,2,0,1:T(8,128)(2,1)S(1)}, s32[]{:S(2)}) async-start(bf16[8,1,2,32,256]{4,3,2,0,1:T(8,128)(2,1)} %copy-done.3), calls=%async_computation.3 | async-start | bytes 458752 | tf_op jit(solution)/shard_map/slice | solution.py:223
  162.7 7.6 %slice-start.1 = ((bf16[8,1,2,32,256]{4,3,2,0,1:T(8,128)(2,1)}), bf16[7,1,2,32,256]{4,3,2,0,1:T(8,128)(2,1)S(1)}, s32[]{:S(2)}) async-start(bf16[8,1,2,32,256]{4,3,2,0,1:T(8,128)(2,1)} %copy-done.8), calls=%async_computation.4 | async-start | bytes 458752 | tf_op jit(solution)/shard_map/slice | solution.py:223
  164.7 6.5 %collective-permute-start.25 = (bf16[1,6,32,256]{3,2,1,0:T(8,128)(2,1)S(1)}, bf16[1,6,32,256]{3,2,1,0:T(8,128)(2,1)}, u32[]{:S(2)}, u32[]{:S(2)}) collective-permute-start(bf16[1,6,32,256]{3,2,1,0:T(8,128)(2,1)S(1)} %get-tuple-element.77), channel_id=1, source_target_pairs={{0,64},{64,128},{128,192},{192,256},{256,320},{320,384},{384,448},... | collective-permute-start | bytes 294920 | tf_op jit(solution)/shard_map/ppermute | solution.py:17
  168.7 5.5 %collective-permute-start.24 = (bf16[1,6,32,256]{3,2,1,0:T(8,128)(2,1)S(1)}, bf16[1,6,32,256]{3,2,1,0:T(8,128)(2,1)}, u32[]{:S(2)}, u32[]{:S(2)}) collective-permute-start(bf16[1,6,32,256]{3,2,1,0:T(8,128)(2,1)S(1)} %get-tuple-element.77), channel_id=1, source_target_pairs={{64,0},{128,64},{192,128},{256,192},{320,256},{384,320},{448,384},... | collective-permute-start | bytes 294920 | tf_op jit(solution)/shard_map/ppermute | solution.py:20
  170.3 5.0 %copy-start.6 = (bf16[1,9,32,32]{2,3,1,0:T(8,128)(2,1)S(1)}, bf16[1,9,32,32]{2,3,1,0:T(8,128)(2,1)}, u32[]{:S(2)}) copy-start(bf16[1,9,32,32]{2,3,1,0:T(8,128)(2,1)} %copy.252) | copy-start | bytes 55300
  170.9 5.9 %copy-start.7 = (bf16[1,6,32,256]{3,2,1,0:T(8,128)(2,1)S(1)}, bf16[1,6,32,256]{3,2,1,0:T(8,128)(2,1)}, u32[]{:S(2)}) copy-start(bf16[1,6,32,256]{3,2,1,0:T(8,128)(2,1)} %get-tuple-element.78) | copy-start | bytes 294916
  171.0 5.9 %copy-start.10 = (f32[1,1,32,256]{3,2,1,0:T(8,128)S(1)}, f32[1,1,32,256]{3,2,1,0:T(8,128)}, u32[]{:S(2)}) copy-start(f32[1,1,32,256]{3,2,1,0:T(8,128)} %get-tuple-element.89) | copy-start | bytes 98308
  171.0 5.9 %copy-start.11 = (f32[1,1,32,256]{3,2,1,0:T(8,128)S(1)}, f32[1,1,32,256]{3,2,1,0:T(8,128)}, u32[]{:S(2)}) copy-start(f32[1,1,32,256]{3,2,1,0:T(8,128)} %get-tuple-element.90) | copy-start | bytes 98308
  175.3 8.3 %copy-start.1 = (bf16[7,1,2,288,256]{4,3,2,0,1:T(8,128)(2,1)S(1)}, bf16[7,1,2,288,256]{4,3,2,0,1:T(8,128)(2,1)}, u32[]{:S(2)}) copy-start(bf16[7,1,2,288,256]{4,3,2,0,1:T(8,128)(2,1)} %copy-done) | copy-start | bytes 6193156
  178.4 7.0 %collective-permute-start.27 = (bf16[1,4,32,256]{3,2,1,0:T(8,128)(2,1)S(1)}, bf16[1,4,32,256]{3,2,1,0:T(8,128)(2,1)}, u32[]{:S(2)}, u32[]{:S(2)}) collective-permute-start(bf16[1,4,32,256]{3,2,1,0:T(8,128)(2,1)S(1)} %get-tuple-element.79), channel_id=1, source_target_pairs={{0,64},{64,128},{128,192},{192,256},{256,320},{320,384},{384,448},... | collective-permute-start | bytes 196616 | tf_op jit(solution)/shard_map/ppermute | solution.py:17
  182.1 5.0 %collective-permute-start.26 = (bf16[1,4,32,256]{3,2,1,0:T(8,128)(2,1)S(1)}, bf16[1,4,32,256]{3,2,1,0:T(8,128)(2,1)S(1)}, u32[]{:S(2)}, u32[]{:S(2)}) collective-permute-start(bf16[1,4,32,256]{3,2,1,0:T(8,128)(2,1)S(1)} %get-tuple-element.79), channel_id=1, source_target_pairs={{64,0},{128,64},{192,128},{256,192},{320,256},{384,320},{448,384},... | collective-permute-start | bytes 196616 | tf_op jit(solution)/shard_map/ppermute | solution.py:20
  184.6 4.1 %copy-start.5 = (bf16[1,9,32,32]{2,3,1,0:T(8,128)(2,1)S(1)}, bf16[1,9,32,32]{2,3,1,0:T(8,128)(2,1)}, u32[]{:S(2)}) copy-start(bf16[1,9,32,32]{2,3,1,0:T(8,128)(2,1)} %copy.256) | copy-start | bytes 55300
  189.4 57.3 %copy-start.9 = (bf16[1,4,32,256]{3,2,1,0:T(8,128)(2,1)S(1)}, bf16[1,4,32,256]{3,2,1,0:T(8,128)(2,1)}, u32[]{:S(2)}) copy-start(bf16[1,4,32,256]{3,2,1,0:T(8,128)(2,1)} %get-tuple-element.80) | copy-start | bytes 196612
  191.2 50.0 %all-to-all-start.1 = ((f32[512,1,192]{2,1,0:T(1,128)}), f32[512,1,192]{2,1,0:T(1,128)S(1)}, u32[]{:S(2)}, u32[]{:S(2)}) async-start(f32[512,1,192]{2,1,0:T(1,128)} %mul.87), calls=%async_computation.1 | async-start | bytes 1048576 | tf_op jit(solution)/shard_map/all_to_all | solution.py:237
  242.5 14.0 %all-to-all-start.2 = ((f32[64,1,192]{2,1,0:T(1,128)}), f32[64,1,192]{2,1,0:T(1,128)S(1)}, u32[]{:S(2)}, u32[]{:S(2)}) async-start(f32[64,1,192]{2,1,0:T(1,128)} %broadcast_in_dim.21), calls=%async_computation.2 | async-start | bytes 131072 | tf_op jit(solution)/shard_map/all_to_all | solution.py:238

commit v7 on v6

--- a/solution.py
+++ b/solution.py
@@ -6,7 +6,7 @@
 from jax.sharding import PartitionSpec as P
 
 TILE = 128
-HALO = 8
+HALO = 4
 
 
 def padded_2(block, sides, width):

time: 260 us -> 246 us (0.946)
  starting transfers between devices: 118 us -> 109 us
    all_to_all x1, starting transfers between devices: 27.3 us -> 20 us  [local(): part = lax.all_to_all(flat, ('segment', 'gy'), 0, 0, tiled=True).sum(axis=0)]
    ppermute x10, waiting for transfers between devices: 11.7 us -> 5.11 us  [padded_2(): lax.ppermute(lax.slice_in_dim(block, block.shape[dim] - width, None, axis...]
    ppermute x8, waiting for transfers between devices: 3.7 us -> 9.99 us  [passed_along(): return lax.ppermute(block, axis, route)]
    dot_general x72, matrix products: 18.4 us -> 15.4 us  [plane_back(): jnp.einsum('oc,...yox->...ycx', kernel[i, j], padded[..., 2 - i:2 - i + h...]
where the time goes in v7:
time: 246 us; the launch traced here: 245 us
  starting transfers between devices  109 us (44%)
  waiting for transfers between devices  89.2 us (36%)
  matrix products  29.3 us (12%)
  local copies, waits for them, and re-layouts  11.2 us (5%)
  other arithmetic  3.53 us (1%)
    ppermute x10, starting transfers between devices, padded_2(): lax.ppermute(lax.slice_in_dim(block, block.shape[dim] - width, None, axis...  34.2 us
    ppermute x10, waiting for transfers between devices, padded_2(): lax.ppermute(lax.slice_in_dim(block, 0, width, axis=dim), axis, backward)  26.9 us
    ppermute x8, starting transfers between devices, passed_along(): return lax.ppermute(block, axis, route)  25.8 us
    all_to_all x1, waiting for transfers between devices, local(): part = lax.all_to_all(flat, ('segment', 'gy'), 0, 0, tiled=True).sum(axis=0)  22.1 us
    all_to_all x1, starting transfers between devices, local(): part = lax.all_to_all(flat, ('segment', 'gy'), 0, 0, tiled=True).sum(axis=0)  20 us
    all_to_all x1, waiting for transfers between devices, local(): got = lax.all_to_all(send, 'segment', 0, 0, tiled=True)  16.2 us
    dot_general x72, matrix products, plane_back(): jnp.einsum('oc,...yox->...ycx', kernel[i, j], padded[..., 2 - i:2 - i + h...  15.4 us
    ppermute x10, starting transfers between devices, padded_2(): lax.ppermute(lax.slice_in_dim(block, 0, width, axis=dim), axis, backward)  14.3 us
  transfers between devices with their start and end apart: 31, of which 22 were waited for; matrix products, arithmetic and copies ran while one was open for 6% of the time, Pallas kernels for 0%

profile of v7, /device:TPU:1, one launch (start us, length us, event | category | flops | bytes accessed | tf_op | source)
XLA Modules:
  0.0 244.9 jit_solution(7024455322660859271)
XLA Ops:
  2.5 1.8 pad_maximum_fusion
  4.3 10.9 %all-to-all-start = ((bf16[8,112,256]{2,1,0:T(8,128)(2,1)}), bf16[8,112,256]{2,1,0:T(8,128)(2,1)S(1)}, u32[]{:S(2)}, u32[]{:S(2)}) async-start(bf16[8,112,256]{2,1,0:T(8,128)(2,1)} %pad_maximum_fusion), calls=%async_computation | async-start | bytes 917504 | tf_op jit(solution)/shard_map/all_to_all | solution.py:147
  15.4 16.2 %all-to-all-done = bf16[8,112,256]{2,1,0:T(8,128)(2,1)S(1)} async-done(((bf16[8,112,256]{2,1,0:T(8,128)(2,1)}), bf16[8,112,256]{2,1,0:T(8,128)(2,1)S(1)}, u32[]{:S(2)}, u32[]{:S(2)}) %all-to-all-start) | async-done | bytes 458784 | tf_op jit(solution)/shard_map/all_to_all | solution.py:147
  31.7 2.5 %collective-permute-start.1 = (bf16[8,1,1,32,256]{4,3,2,0,1:T(8,128)(2,1)S(1)}, bf16[8,1,1,32,256]{4,3,2,0,1:T(8,128)(2,1)S(1)}, u32[]{:S(2)}, u32[]{:S(2)}) collective-permute-start(bf16[8,1,1,32,256]{4,3,2,0,1:T(8,128)(2,1)S(1)} %get-tuple-element.39), channel_id=1, source_target_pairs={{1,0},{2,1},{3,2},{4,3},{5,4},{6,5},{7,6},{8,7},{9,8},{10,9},{11,1... | collective-permute-start | bytes 393224 | tf_op jit(solution)/shard_map/ppermute | solution.py:20
  34.2 3.1 %collective-permute-start = (bf16[8,1,1,32,256]{4,3,2,0,1:T(8,128)(2,1)S(1)}, bf16[8,1,1,32,256]{4,3,2,0,1:T(8,128)(2,1)S(1)}, u32[]{:S(2)}, u32[]{:S(2)}) collective-permute-start(bf16[8,1,1,32,256]{4,3,2,0,1:T(8,128)(2,1)S(1)} %get-tuple-element.38), channel_id=1, source_target_pairs={{0,1},{1,2},{2,3},{3,4},{4,5},{5,6},{6,7},{7,8},{8,9},{9,10},{10,1... | collective-permute-start | bytes 393224 | tf_op jit(solution)/shard_map/ppermute | solution.py:17
  42.1 1.3 collective-permute-start.3
  43.4 4.0 %collective-permute-start.2 = (bf16[8,1,2,32,256]{4,3,2,0,1:T(8,128)(2,1)S(1)}, bf16[8,1,2,32,256]{4,3,2,0,1:T(8,128)(2,1)S(1)}, u32[]{:S(2)}, u32[]{:S(2)}) collective-permute-start(bf16[8,1,2,32,256]{4,3,2,0,1:T(8,128)(2,1)S(1)} %bitcast.1331), channel_id=1, source_target_pairs={{0,64},{64,128},{128,192},{192,256},{256,320},{320,384},{384,448},... | collective-permute-start | bytes 786440 | tf_op jit(solution)/shard_map/ppermute | solution.py:17
  48.3 3.5 %collective-permute-done.3 = bf16[8,1,2,32,256]{4,3,2,0,1:T(8,128)(2,1)S(1)} collective-permute-done((bf16[8,1,2,32,256]{4,3,2,0,1:T(8,128)(2,1)S(1)}, bf16[8,1,2,32,256]{4,3,2,0,1:T(8,128)(2,1)S(1)}, u32[]{:S(2)}, u32[]{:S(2)}) %collective-permute-start.3) | collective-permute-done | bytes 262176 | tf_op jit(solution)/shard_map/ppermute | solution.py:20
  52.1 1.4 collective-permute-done.2
  53.9 2.4 collective-permute-start.6
  56.3 3.2 %collective-permute-start.5 = (bf16[9,1,2,32,256]{4,3,2,1,0:T(8,128)(2,1)S(1)}, bf16[9,1,2,32,256]{4,3,2,1,0:T(8,128)(2,1)S(1)}, u32[]{:S(2)}, u32[]{:S(2)}) collective-permute-start(bf16[9,1,2,32,256]{4,3,2,1,0:T(8,128)(2,1)S(1)} %pad_maximum_fusion.1), channel_id=1, source_target_pairs={{0,1},{1,2},{2,3},{3,4},{4,5},{5,6},{6,7},{7,8},{8,9},{9,10},{10,1... | collective-permute-start | bytes 884744 | tf_op jit(solution)/shard_map/ppermute | solution.py:28
  59.5 3.1 %collective-permute-start.4 = (bf16[5,1,2,32,256]{4,3,2,1,0:T(8,128)(2,1)S(1)}, bf16[5,1,2,32,256]{4,3,2,1,0:T(8,128)(2,1)S(1)}, u32[]{:S(2)}, u32[]{:S(2)}) collective-permute-start(bf16[5,1,2,32,256]{4,3,2,1,0:T(8,128)(2,1)S(1)} %pad_maximum_fusion.4), channel_id=1, source_target_pairs={{0,2},{1,3},{2,4},{3,5},{4,6},{5,7},{6,8},{7,9},{8,10},{9,11},{10,... | collective-permute-start | bytes 491528 | tf_op jit(solution)/shard_map/ppermute | solution.py:28
  62.7 1.3 collective-permute-start.7
  64.0 2.6 %collective-permute-done.4 = bf16[5,1,2,32,256]{4,3,2,1,0:T(8,128)(2,1)S(1)} collective-permute-done((bf16[5,1,2,32,256]{4,3,2,1,0:T(8,128)(2,1)S(1)}, bf16[5,1,2,32,256]{4,3,2,1,0:T(8,128)(2,1)S(1)}, u32[]{:S(2)}, u32[]{:S(2)}) %collective-permute-start.4) | collective-permute-done | bytes 163872 | tf_op jit(solution)/shard_map/ppermute | solution.py:28
  66.7 3.8 %collective-permute-done.7 = bf16[5,1,2,32,256]{4,3,2,1,0:T(8,128)(2,1)S(1)} collective-permute-done((bf16[5,1,2,32,256]{4,3,2,1,0:T(8,128)(2,1)S(1)}, bf16[5,1,2,32,256]{4,3,2,1,0:T(8,128)(2,1)S(1)}, u32[]{:S(2)}, u32[]{:S(2)}) %collective-permute-start.7) | collective-permute-done | bytes 163872 | tf_op jit(solution)/shard_map/ppermute | solution.py:28
  70.8 4.1 %collective-permute-start.9 = (bf16[1,10,32,256]{3,2,1,0:T(8,128)(2,1)S(1)}, bf16[1,10,32,256]{3,2,1,0:T(8,128)(2,1)S(1)}, u32[]{:S(2)}, u32[]{:S(2)}) collective-permute-start(bf16[1,10,32,256]{3,2,1,0:T(8,128)(2,1)S(1)} %fusion.59), channel_id=1, source_target_pairs={{0,64},{64,128},{128,192},{192,256},{256,320},{320,384},{384,448},... | collective-permute-start | bytes 491528 | tf_op jit(solution)/shard_map/ppermute | solution.py:17
  74.9 1.3 collective-permute-start.8
  76.6 2.1 collective-permute-done.9
  79.0 3.7 %collective-permute-done.8 = bf16[1,10,32,256]{3,2,1,0:T(8,128)(2,1)S(1)} collective-permute-done((bf16[1,10,32,256]{3,2,1,0:T(8,128)(2,1)S(1)}, bf16[1,10,32,256]{3,2,1,0:T(8,128)(2,1)S(1)}, u32[]{:S(2)}, u32[]{:S(2)}) %collective-permute-start.8) | collective-permute-done | bytes 163872 | tf_op jit(solution)/shard_map/ppermute | solution.py:20
  84.9 2.2 collective-permute-start.11
  87.1 1.3 collective-permute-start.10
  89.2 3.6 %collective-permute-done.10 = bf16[1,8,32,256]{3,2,1,0:T(8,128)(2,1)S(1)} collective-permute-done((bf16[1,8,32,256]{3,2,1,0:T(8,128)(2,1)S(1)}, bf16[1,8,32,256]{3,2,1,0:T(8,128)(2,1)S(1)}, u32[]{:S(2)}, u32[]{:S(2)}) %collective-permute-start.10) | collective-permute-done | bytes 131104 | tf_op jit(solution)/shard_map/ppermute | solution.py:20
  94.9 4.5 %collective-permute-start.13 = (bf16[1,6,32,256]{3,2,1,0:T(8,128)(2,1)S(1)}, bf16[1,6,32,256]{3,2,1,0:T(8,128)(2,1)S(1)}, u32[]{:S(2)}, u32[]{:S(2)}) collective-permute-start(bf16[1,6,32,256]{3,2,1,0:T(8,128)(2,1)S(1)} %get-tuple-element.60), channel_id=1, source_target_pairs={{0,64},{64,128},{128,192},{192,256},{256,320},{320,384},{384,448},... | collective-permute-start | bytes 294920 | tf_op jit(solution)/shard_map/ppermute | solution.py:17
  99.6 1.3 collective-permute-start.12
  101.2 3.7 %collective-permute-done.12 = bf16[1,6,32,256]{3,2,1,0:T(8,128)(2,1)S(1)} collective-permute-done((bf16[1,6,32,256]{3,2,1,0:T(8,128)(2,1)S(1)}, bf16[1,6,32,256]{3,2,1,0:T(8,128)(2,1)S(1)}, u32[]{:S(2)}, u32[]{:S(2)}) %collective-permute-start.12) | collective-permute-done | bytes 98336 | tf_op jit(solution)/shard_map/ppermute | solution.py:20
  106.9 3.1 %collective-permute-start.15 = (bf16[1,4,32,256]{3,2,1,0:T(8,128)(2,1)S(1)}, bf16[1,4,32,256]{3,2,1,0:T(8,128)(2,1)S(1)}, u32[]{:S(2)}, u32[]{:S(2)}) collective-permute-start(bf16[1,4,32,256]{3,2,1,0:T(8,128)(2,1)S(1)} %get-tuple-element.62), channel_id=1, source_target_pairs={{0,64},{64,128},{128,192},{192,256},{256,320},{320,384},{384,448},... | collective-permute-start | bytes 196616 | tf_op jit(solution)/shard_map/ppermute | solution.py:17
  110.3 1.3 collective-permute-start.14
  111.8 3.5 %collective-permute-done.14 = bf16[1,4,32,256]{3,2,1,0:T(8,128)(2,1)S(1)} collective-permute-done((bf16[1,4,32,256]{3,2,1,0:T(8,128)(2,1)S(1)}, bf16[1,4,32,256]{3,2,1,0:T(8,128)(2,1)S(1)}, u32[]{:S(2)}, u32[]{:S(2)}) %collective-permute-start.14) | collective-permute-done | bytes 65568 | tf_op jit(solution)/shard_map/ppermute | solution.py:20
  117.1 4.1 %collective-permute-start.16 = (bf16[1,2,32,256]{3,2,1,0:T(8,128)(2,1)S(1)}, bf16[1,2,32,256]{3,2,1,0:T(8,128)(2,1)S(1)}, u32[]{:S(2)}, u32[]{:S(2)}) collective-permute-start(bf16[1,2,32,256]{3,2,1,0:T(8,128)(2,1)S(1)} %fusion.49), channel_id=1, source_target_pairs={{0,2},{1,3},{2,4},{3,5},{4,6},{5,7},{6,8},{7,9},{8,10},{9,11},{10,... | collective-permute-start | bytes 98312 | tf_op jit(solution)/shard_map/ppermute | solution.py:28
  121.2 8.5 %collective-permute-start.17 = (bf16[1,2,32,256]{3,2,1,0:T(8,128)(2,1)S(1)}, bf16[1,2,32,256]{3,2,1,0:T(8,128)(2,1)S(1)}, u32[]{:S(2)}, u32[]{:S(2)}) collective-permute-start(bf16[1,2,32,256]{3,2,1,0:T(8,128)(2,1)S(1)} %fusion.49), channel_id=1, source_target_pairs={{0,1},{1,2},{2,3},{3,4},{4,5},{5,6},{6,7},{7,8},{8,9},{9,10},{10,1... | collective-permute-start | bytes 98312 | tf_op jit(solution)/shard_map/ppermute | solution.py:28
  129.7 1.9 collective-permute-start.18
  131.6 1.3 collective-permute-start.19
  133.0 1.9 collective-permute-done.18
  134.9 1.5 collective-permute-done.19
  136.5 2.9 %collective-permute-start.21 = (bf16[1,10,32,256]{3,2,1,0:T(8,128)(2,1)S(1)}, bf16[1,10,32,256]{3,2,1,0:T(8,128)(2,1)S(1)}, u32[]{:S(2)}, u32[]{:S(2)}) collective-permute-start(bf16[1,10,32,256]{3,2,1,0:T(8,128)(2,1)S(1)} %fusion.61), channel_id=1, source_target_pairs={{0,64},{64,128},{128,192},{192,256},{256,320},{320,384},{384,448},... | collective-permute-start | bytes 491528 | tf_op jit(solution)/shard_map/ppermute | solution.py:17
  139.4 1.3 collective-permute-start.20
  141.8 3.6 %collective-permute-done.20 = bf16[1,10,32,256]{3,2,1,0:T(8,128)(2,1)S(1)} collective-permute-done((bf16[1,10,32,256]{3,2,1,0:T(8,128)(2,1)S(1)}, bf16[1,10,32,256]{3,2,1,0:T(8,128)(2,1)S(1)}, u32[]{:S(2)}, u32[]{:S(2)}) %collective-permute-start.20) | collective-permute-done | bytes 163872 | tf_op jit(solution)/shard_map/ppermute | solution.py:20
  147.7 2.9 %collective-permute-start.23 = (bf16[1,8,32,256]{3,2,1,0:T(8,128)(2,1)S(1)}, bf16[1,8,32,256]{3,2,1,0:T(8,128)(2,1)S(1)}, u32[]{:S(2)}, u32[]{:S(2)}) collective-permute-start(bf16[1,8,32,256]{3,2,1,0:T(8,128)(2,1)S(1)} %get-tuple-element.64), channel_id=1, source_target_pairs={{0,64},{64,128},{128,192},{192,256},{256,320},{320,384},{384,448},... | collective-permute-start | bytes 393224 | tf_op jit(solution)/shard_map/ppermute | solution.py:17
  152.7 3.6 %collective-permute-done.22 = bf16[1,8,32,256]{3,2,1,0:T(8,128)(2,1)S(1)} collective-permute-done((bf16[1,8,32,256]{3,2,1,0:T(8,128)(2,1)S(1)}, bf16[1,8,32,256]{3,2,1,0:T(8,128)(2,1)S(1)}, u32[]{:S(2)}, u32[]{:S(2)}) %collective-permute-start.22) | collective-permute-done | bytes 131104 | tf_op jit(solution)/shard_map/ppermute | solution.py:20
  158.4 3.9 %collective-permute-start.25 = (bf16[1,6,32,256]{3,2,1,0:T(8,128)(2,1)S(1)}, bf16[1,6,32,256]{3,2,1,0:T(8,128)(2,1)}, u32[]{:S(2)}, u32[]{:S(2)}) collective-permute-start(bf16[1,6,32,256]{3,2,1,0:T(8,128)(2,1)S(1)} %get-tuple-element.66), channel_id=1, source_target_pairs={{0,64},{64,128},{128,192},{192,256},{256,320},{320,384},{384,448},... | collective-permute-start | bytes 294920 | tf_op jit(solution)/shard_map/ppermute | solution.py:17
  162.4 1.5 collective-permute-start.24
  170.4 3.6 %collective-permute-start.27 = (bf16[1,4,32,256]{3,2,1,0:T(8,128)(2,1)}, bf16[1,4,32,256]{3,2,1,0:T(8,128)(2,1)}, u32[]{:S(2)}, u32[]{:S(2)}) collective-permute-start(bf16[1,4,32,256]{3,2,1,0:T(8,128)(2,1)} %get-tuple-element.68), channel_id=1, source_target_pairs={{0,64},{64,128},{128,192},{192,256},{256,320},{320,384},{384,448},... | collective-permute-start | bytes 196616 | tf_op jit(solution)/shard_map/ppermute | solution.py:17
  174.0 1.7 fusion.195
  183.3 1.7 mul.99
  185.1 20.0 %all-to-all-start.1 = ((f32[512,1,192]{2,1,0:T(1,128)}), f32[512,1,192]{2,1,0:T(1,128)S(1)}, u32[]{:S(2)}, u32[]{:S(2)}) async-start(f32[512,1,192]{2,1,0:T(1,128)} %mul.99), calls=%async_computation.1 | async-start | bytes 1048576 | tf_op jit(solution)/shard_map/all_to_all | solution.py:237
  205.7 22.1 %all-to-all-done.1 = f32[512,1,192]{2,1,0:T(1,128)S(1)} async-done(((f32[512,1,192]{2,1,0:T(1,128)}), f32[512,1,192]{2,1,0:T(1,128)S(1)}, u32[]{:S(2)}, u32[]{:S(2)}) %all-to-all-start.1) | async-done | bytes 393248 | tf_op jit(solution)/shard_map/all_to_all | solution.py:237
  229.0 4.2 %all-to-all-start.2 = ((f32[64,1,192]{2,1,0:T(1,128)}), f32[64,1,192]{2,1,0:T(1,128)S(1)}, u32[]{:S(2)}, u32[]{:S(2)}) async-start(f32[64,1,192]{2,1,0:T(1,128)} %broadcast_in_dim.21), calls=%async_computation.2 | async-start | bytes 131072 | tf_op jit(solution)/shard_map/all_to_all | solution.py:238
  234.1 9.0 %all-to-all-done.2 = f32[64,1,192]{2,1,0:T(1,128)S(1)} async-done(((f32[64,1,192]{2,1,0:T(1,128)}), f32[64,1,192]{2,1,0:T(1,128)S(1)}, u32[]{:S(2)}, u32[]{:S(2)}) %all-to-all-start.2) | async-done | bytes 49184 | tf_op jit(solution)/shard_map/all_to_all | solution.py:238
  (275 shorter events, 44.7 us)
Async XLA Ops:
  0.6 14.5 %copy-start.11 = (s32[1,12]{1,0:T(1,128)S(1)}, s32[1,12]{1,0:T(1,128)}, u32[]{:S(2)}) copy-start(s32[1,12]{1,0:T(1,128)} %param.9) | copy-start | bytes 148
  4.3 27.3 %all-to-all-start = ((bf16[8,112,256]{2,1,0:T(8,128)(2,1)}), bf16[8,112,256]{2,1,0:T(8,128)(2,1)S(1)}, u32[]{:S(2)}, u32[]{:S(2)}) async-start(bf16[8,112,256]{2,1,0:T(8,128)(2,1)} %pad_maximum_fusion), calls=%async_computation | async-start | bytes 917504 | tf_op jit(solution)/shard_map/all_to_all | solution.py:147
  31.7 7.7 %collective-permute-start.1 = (bf16[8,1,1,32,256]{4,3,2,0,1:T(8,128)(2,1)S(1)}, bf16[8,1,1,32,256]{4,3,2,0,1:T(8,128)(2,1)S(1)}, u32[]{:S(2)}, u32[]{:S(2)}) collective-permute-start(bf16[8,1,1,32,256]{4,3,2,0,1:T(8,128)(2,1)S(1)} %get-tuple-element.39), channel_id=1, source_target_pairs={{1,0},{2,1},{3,2},{4,3},{5,4},{6,5},{7,6},{8,7},{9,8},{10,9},{11,1... | collective-permute-start | bytes 393224 | tf_op jit(solution)/shard_map/ppermute | solution.py:20
  34.2 5.2 %collective-permute-start = (bf16[8,1,1,32,256]{4,3,2,0,1:T(8,128)(2,1)S(1)}, bf16[8,1,1,32,256]{4,3,2,0,1:T(8,128)(2,1)S(1)}, u32[]{:S(2)}, u32[]{:S(2)}) collective-permute-start(bf16[8,1,1,32,256]{4,3,2,0,1:T(8,128)(2,1)S(1)} %get-tuple-element.38), channel_id=1, source_target_pairs={{0,1},{1,2},{2,3},{3,4},{4,5},{5,6},{6,7},{7,8},{8,9},{9,10},{10,1... | collective-permute-start | bytes 393224 | tf_op jit(solution)/shard_map/ppermute | solution.py:17
  42.1 9.8 %collective-permute-start.3 = (bf16[8,1,2,32,256]{4,3,2,0,1:T(8,128)(2,1)S(1)}, bf16[8,1,2,32,256]{4,3,2,0,1:T(8,128)(2,1)S(1)}, u32[]{:S(2)}, u32[]{:S(2)}) collective-permute-start(bf16[8,1,2,32,256]{4,3,2,0,1:T(8,128)(2,1)S(1)} %bitcast.1330), channel_id=1, source_target_pairs={{64,0},{128,64},{192,128},{256,192},{320,256},{384,320},{448,384},... | collective-permute-start | bytes 786440 | tf_op jit(solution)/shard_map/ppermute | solution.py:20
  43.4 10.0 %collective-permute-start.2 = (bf16[8,1,2,32,256]{4,3,2,0,1:T(8,128)(2,1)S(1)}, bf16[8,1,2,32,256]{4,3,2,0,1:T(8,128)(2,1)S(1)}, u32[]{:S(2)}, u32[]{:S(2)}) collective-permute-start(bf16[8,1,2,32,256]{4,3,2,0,1:T(8,128)(2,1)S(1)} %bitcast.1331), channel_id=1, source_target_pairs={{0,64},{64,128},{128,192},{192,256},{256,320},{320,384},{384,448},... | collective-permute-start | bytes 786440 | tf_op jit(solution)/shard_map/ppermute | solution.py:17
  48.0 5.8 %copy-start = (bf16[7,1,2,288,256]{4,3,2,0,1:T(8,128)(2,1)}, bf16[7,1,2,288,256]{4,3,2,0,1:T(8,128)(2,1)S(1)}, u32[]{:S(2)}) copy-start(bf16[7,1,2,288,256]{4,3,2,0,1:T(8,128)(2,1)S(1)} %slice_dynamic-update-slice_fusion) | copy-start | bytes 6193156
  48.3 3.8 %copy-start.6 = (bf16[1,1,2,288,256]{4,3,2,0,1:T(8,128)(2,1)}, bf16[1,1,2,288,256]{4,3,2,0,1:T(8,128)(2,1)S(1)}, u32[]{:S(2)}) copy-start(bf16[1,1,2,288,256]{4,3,2,0,1:T(8,128)(2,1)S(1)} %constant_dynamic-update-slice_fusion.20) | copy-start | bytes 884740
  48.3 5.5 %copy-start.4 = (bf16[1,2,32,256]{3,2,1,0:T(8,128)(2,1)S(1)}, bf16[1,2,32,256]{3,2,1,0:T(8,128)(2,1)}, u32[]{:S(2)}) copy-start(bf16[1,2,32,256]{3,2,1,0:T(8,128)(2,1)} %param.6) | copy-start | bytes 98308
  51.9 12.1 %copy-start.2 = (bf16[8,1,2,32,256]{4,3,2,0,1:T(8,128)(2,1)}, bf16[8,1,2,32,256]{4,3,2,0,1:T(8,128)(2,1)S(1)}, u32[]{:S(2)}) copy-start(bf16[8,1,2,32,256]{4,3,2,0,1:T(8,128)(2,1)S(1)} %collective-permute-done.3) | copy-start | bytes 786436
  53.4 10.6 %copy-start.9 = (bf16[8,1,2,32,256]{4,3,2,0,1:T(8,128)(2,1)}, bf16[8,1,2,32,256]{4,3,2,0,1:T(8,128)(2,1)S(1)}, u32[]{:S(2)}) copy-start(bf16[8,1,2,32,256]{4,3,2,0,1:T(8,128)(2,1)S(1)} %collective-permute-done.2) | copy-start | bytes 786436
  53.9 16.7 %collective-permute-start.6 = (bf16[9,1,2,32,256]{4,3,2,1,0:T(8,128)(2,1)S(1)}, bf16[9,1,2,32,256]{4,3,2,1,0:T(8,128)(2,1)S(1)}, u32[]{:S(2)}, u32[]{:S(2)}) collective-permute-start(bf16[9,1,2,32,256]{4,3,2,1,0:T(8,128)(2,1)S(1)} %pad_maximum_fusion.1), channel_id=1, source_target_pairs={{1,0},{2,1},{3,2},{4,3},{5,4},{6,5},{7,6},{8,7},{9,8},{10,9},{11,1... | collective-permute-start | bytes 884744 | tf_op jit(solution)/shard_map/ppermute | solution.py:28
  56.3 14.3 %collective-permute-start.5 = (bf16[9,1,2,32,256]{4,3,2,1,0:T(8,128)(2,1)S(1)}, bf16[9,1,2,32,256]{4,3,2,1,0:T(8,128)(2,1)S(1)}, u32[]{:S(2)}, u32[]{:S(2)}) collective-permute-start(bf16[9,1,2,32,256]{4,3,2,1,0:T(8,128)(2,1)S(1)} %pad_maximum_fusion.1), channel_id=1, source_target_pairs={{0,1},{1,2},{2,3},{3,4},{4,5},{5,6},{6,7},{7,8},{8,9},{9,10},{10,1... | collective-permute-start | bytes 884744 | tf_op jit(solution)/shard_map/ppermute | solution.py:28
  59.5 7.1 %collective-permute-start.4 = (bf16[5,1,2,32,256]{4,3,2,1,0:T(8,128)(2,1)S(1)}, bf16[5,1,2,32,256]{4,3,2,1,0:T(8,128)(2,1)S(1)}, u32[]{:S(2)}, u32[]{:S(2)}) collective-permute-start(bf16[5,1,2,32,256]{4,3,2,1,0:T(8,128)(2,1)S(1)} %pad_maximum_fusion.4), channel_id=1, source_target_pairs={{0,2},{1,3},{2,4},{3,5},{4,6},{5,7},{6,8},{7,9},{8,10},{9,11},{10,... | collective-permute-start | bytes 491528 | tf_op jit(solution)/shard_map/ppermute | solution.py:28
  62.7 7.9 %collective-permute-start.7 = (bf16[5,1,2,32,256]{4,3,2,1,0:T(8,128)(2,1)S(1)}, bf16[5,1,2,32,256]{4,3,2,1,0:T(8,128)(2,1)S(1)}, u32[]{:S(2)}, u32[]{:S(2)}) collective-permute-start(bf16[5,1,2,32,256]{4,3,2,1,0:T(8,128)(2,1)S(1)} %pad_maximum_fusion.4), channel_id=1, source_target_pairs={{2,0},{3,1},{4,2},{5,3},{6,4},{7,5},{8,6},{9,7},{10,8},{11,9},{12,... | collective-permute-start | bytes 491528 | tf_op jit(solution)/shard_map/ppermute | solution.py:28
  70.8 7.9 %collective-permute-start.9 = (bf16[1,10,32,256]{3,2,1,0:T(8,128)(2,1)S(1)}, bf16[1,10,32,256]{3,2,1,0:T(8,128)(2,1)S(1)}, u32[]{:S(2)}, u32[]{:S(2)}) collective-permute-start(bf16[1,10,32,256]{3,2,1,0:T(8,128)(2,1)S(1)} %fusion.59), channel_id=1, source_target_pairs={{0,64},{64,128},{128,192},{192,256},{256,320},{320,384},{384,448},... | collective-permute-start | bytes 491528 | tf_op jit(solution)/shard_map/ppermute | solution.py:17
  74.9 7.7 %collective-permute-start.8 = (bf16[1,10,32,256]{3,2,1,0:T(8,128)(2,1)S(1)}, bf16[1,10,32,256]{3,2,1,0:T(8,128)(2,1)S(1)}, u32[]{:S(2)}, u32[]{:S(2)}) collective-permute-start(bf16[1,10,32,256]{3,2,1,0:T(8,128)(2,1)S(1)} %fusion.59), channel_id=1, source_target_pairs={{64,0},{128,64},{192,128},{256,192},{320,256},{384,320},{448,384},... | collective-permute-start | bytes 491528 | tf_op jit(solution)/shard_map/ppermute | solution.py:20
  84.9 4.1 %collective-permute-start.11 = (bf16[1,8,32,256]{3,2,1,0:T(8,128)(2,1)S(1)}, bf16[1,8,32,256]{3,2,1,0:T(8,128)(2,1)S(1)}, u32[]{:S(2)}, u32[]{:S(2)}) collective-permute-start(bf16[1,8,32,256]{3,2,1,0:T(8,128)(2,1)S(1)} %get-tuple-element.58), channel_id=1, source_target_pairs={{0,64},{64,128},{128,192},{192,256},{256,320},{320,384},{384,448},... | collective-permute-start | bytes 393224 | tf_op jit(solution)/shard_map/ppermute | solution.py:17
  87.1 5.7 %collective-permute-start.10 = (bf16[1,8,32,256]{3,2,1,0:T(8,128)(2,1)S(1)}, bf16[1,8,32,256]{3,2,1,0:T(8,128)(2,1)S(1)}, u32[]{:S(2)}, u32[]{:S(2)}) collective-permute-start(bf16[1,8,32,256]{3,2,1,0:T(8,128)(2,1)S(1)} %get-tuple-element.58), channel_id=1, source_target_pairs={{64,0},{128,64},{192,128},{256,192},{320,256},{384,320},{448,384},... | collective-permute-start | bytes 393224 | tf_op jit(solution)/shard_map/ppermute | solution.py:20
  94.9 6.1 %collective-permute-start.13 = (bf16[1,6,32,256]{3,2,1,0:T(8,128)(2,1)S(1)}, bf16[1,6,32,256]{3,2,1,0:T(8,128)(2,1)S(1)}, u32[]{:S(2)}, u32[]{:S(2)}) collective-permute-start(bf16[1,6,32,256]{3,2,1,0:T(8,128)(2,1)S(1)} %get-tuple-element.60), channel_id=1, source_target_pairs={{0,64},{64,128},{128,192},{192,256},{256,320},{320,384},{384,448},... | collective-permute-start | bytes 294920 | tf_op jit(solution)/shard_map/ppermute | solution.py:17
  99.6 5.4 %collective-permute-start.12 = (bf16[1,6,32,256]{3,2,1,0:T(8,128)(2,1)S(1)}, bf16[1,6,32,256]{3,2,1,0:T(8,128)(2,1)S(1)}, u32[]{:S(2)}, u32[]{:S(2)}) collective-permute-start(bf16[1,6,32,256]{3,2,1,0:T(8,128)(2,1)S(1)} %get-tuple-element.60), channel_id=1, source_target_pairs={{64,0},{128,64},{192,128},{256,192},{320,256},{384,320},{448,384},... | collective-permute-start | bytes 294920 | tf_op jit(solution)/shard_map/ppermute | solution.py:20
  106.9 4.6 %collective-permute-start.15 = (bf16[1,4,32,256]{3,2,1,0:T(8,128)(2,1)S(1)}, bf16[1,4,32,256]{3,2,1,0:T(8,128)(2,1)S(1)}, u32[]{:S(2)}, u32[]{:S(2)}) collective-permute-start(bf16[1,4,32,256]{3,2,1,0:T(8,128)(2,1)S(1)} %get-tuple-element.62), channel_id=1, source_target_pairs={{0,64},{64,128},{128,192},{192,256},{256,320},{320,384},{384,448},... | collective-permute-start | bytes 196616 | tf_op jit(solution)/shard_map/ppermute | solution.py:17
  110.3 5.0 %collective-permute-start.14 = (bf16[1,4,32,256]{3,2,1,0:T(8,128)(2,1)S(1)}, bf16[1,4,32,256]{3,2,1,0:T(8,128)(2,1)S(1)}, u32[]{:S(2)}, u32[]{:S(2)}) collective-permute-start(bf16[1,4,32,256]{3,2,1,0:T(8,128)(2,1)S(1)} %get-tuple-element.62), channel_id=1, source_target_pairs={{64,0},{128,64},{192,128},{256,192},{320,256},{384,320},{448,384},... | collective-permute-start | bytes 196616 | tf_op jit(solution)/shard_map/ppermute | solution.py:20
  117.1 15.9 %collective-permute-start.16 = (bf16[1,2,32,256]{3,2,1,0:T(8,128)(2,1)S(1)}, bf16[1,2,32,256]{3,2,1,0:T(8,128)(2,1)S(1)}, u32[]{:S(2)}, u32[]{:S(2)}) collective-permute-start(bf16[1,2,32,256]{3,2,1,0:T(8,128)(2,1)S(1)} %fusion.49), channel_id=1, source_target_pairs={{0,2},{1,3},{2,4},{3,5},{4,6},{5,7},{6,8},{7,9},{8,10},{9,11},{10,... | collective-permute-start | bytes 98312 | tf_op jit(solution)/shard_map/ppermute | solution.py:28
  121.2 11.8 %collective-permute-start.17 = (bf16[1,2,32,256]{3,2,1,0:T(8,128)(2,1)S(1)}, bf16[1,2,32,256]{3,2,1,0:T(8,128)(2,1)S(1)}, u32[]{:S(2)}, u32[]{:S(2)}) collective-permute-start(bf16[1,2,32,256]{3,2,1,0:T(8,128)(2,1)S(1)} %fusion.49), channel_id=1, source_target_pairs={{0,1},{1,2},{2,3},{3,4},{4,5},{5,6},{6,7},{7,8},{8,9},{9,10},{10,1... | collective-permute-start | bytes 98312 | tf_op jit(solution)/shard_map/ppermute | solution.py:28
  129.7 5.2 %collective-permute-start.18 = (bf16[1,2,32,256]{3,2,1,0:T(8,128)(2,1)S(1)}, bf16[1,2,32,256]{3,2,1,0:T(8,128)(2,1)S(1)}, u32[]{:S(2)}, u32[]{:S(2)}) collective-permute-start(bf16[1,2,32,256]{3,2,1,0:T(8,128)(2,1)S(1)} %fusion.49), channel_id=1, source_target_pairs={{1,0},{2,1},{3,2},{4,3},{5,4},{6,5},{7,6},{8,7},{9,8},{10,9},{11,1... | collective-permute-start | bytes 98312 | tf_op jit(solution)/shard_map/ppermute | solution.py:28
  131.6 4.9 %collective-permute-start.19 = (bf16[1,2,32,256]{3,2,1,0:T(8,128)(2,1)S(1)}, bf16[1,2,32,256]{3,2,1,0:T(8,128)(2,1)S(1)}, u32[]{:S(2)}, u32[]{:S(2)}) collective-permute-start(bf16[1,2,32,256]{3,2,1,0:T(8,128)(2,1)S(1)} %fusion.49), channel_id=1, source_target_pairs={{2,0},{3,1},{4,2},{5,3},{6,4},{7,5},{8,6},{9,7},{10,8},{11,9},{12,... | collective-permute-start | bytes 98312 | tf_op jit(solution)/shard_map/ppermute | solution.py:28
  136.5 5.1 %collective-permute-start.21 = (bf16[1,10,32,256]{3,2,1,0:T(8,128)(2,1)S(1)}, bf16[1,10,32,256]{3,2,1,0:T(8,128)(2,1)S(1)}, u32[]{:S(2)}, u32[]{:S(2)}) collective-permute-start(bf16[1,10,32,256]{3,2,1,0:T(8,128)(2,1)S(1)} %fusion.61), channel_id=1, source_target_pairs={{0,64},{64,128},{128,192},{192,256},{256,320},{320,384},{384,448},... | collective-permute-start | bytes 491528 | tf_op jit(solution)/shard_map/ppermute | solution.py:17
  139.4 6.1 %collective-permute-start.20 = (bf16[1,10,32,256]{3,2,1,0:T(8,128)(2,1)S(1)}, bf16[1,10,32,256]{3,2,1,0:T(8,128)(2,1)S(1)}, u32[]{:S(2)}, u32[]{:S(2)}) collective-permute-start(bf16[1,10,32,256]{3,2,1,0:T(8,128)(2,1)S(1)} %fusion.61), channel_id=1, source_target_pairs={{64,0},{128,64},{192,128},{256,192},{320,256},{384,320},{448,384},... | collective-permute-start | bytes 491528 | tf_op jit(solution)/shard_map/ppermute | solution.py:20
  147.7 4.8 %collective-permute-start.23 = (bf16[1,8,32,256]{3,2,1,0:T(8,128)(2,1)S(1)}, bf16[1,8,32,256]{3,2,1,0:T(8,128)(2,1)S(1)}, u32[]{:S(2)}, u32[]{:S(2)}) collective-permute-start(bf16[1,8,32,256]{3,2,1,0:T(8,128)(2,1)S(1)} %get-tuple-element.64), channel_id=1, source_target_pairs={{0,64},{64,128},{128,192},{192,256},{256,320},{320,384},{384,448},... | collective-permute-start | bytes 393224 | tf_op jit(solution)/shard_map/ppermute | solution.py:17
  150.5 5.7 %collective-permute-start.22 = (bf16[1,8,32,256]{3,2,1,0:T(8,128)(2,1)S(1)}, bf16[1,8,32,256]{3,2,1,0:T(8,128)(2,1)S(1)}, u32[]{:S(2)}, u32[]{:S(2)}) collective-permute-start(bf16[1,8,32,256]{3,2,1,0:T(8,128)(2,1)S(1)} %get-tuple-element.64), channel_id=1, source_target_pairs={{64,0},{128,64},{192,128},{256,192},{320,256},{384,320},{448,384},... | collective-permute-start | bytes 393224 | tf_op jit(solution)/shard_map/ppermute | solution.py:20
  157.1 6.9 %slice-start = ((bf16[8,1,2,32,256]{4,3,2,0,1:T(8,128)(2,1)}), bf16[7,1,2,32,256]{4,3,2,0,1:T(8,128)(2,1)S(1)}, s32[]{:S(2)}) async-start(bf16[8,1,2,32,256]{4,3,2,0,1:T(8,128)(2,1)} %copy-done.2), calls=%async_computation.3 | async-start | bytes 458752 | tf_op jit(solution)/shard_map/slice | solution.py:223
  157.1 6.9 %slice-start.1 = ((bf16[8,1,2,32,256]{4,3,2,0,1:T(8,128)(2,1)}), bf16[7,1,2,32,256]{4,3,2,0,1:T(8,128)(2,1)S(1)}, s32[]{:S(2)}) async-start(bf16[8,1,2,32,256]{4,3,2,0,1:T(8,128)(2,1)} %copy-done.9), calls=%async_computation.4 | async-start | bytes 458752 | tf_op jit(solution)/shard_map/slice | solution.py:223
  158.4 7.1 %collective-permute-start.25 = (bf16[1,6,32,256]{3,2,1,0:T(8,128)(2,1)S(1)}, bf16[1,6,32,256]{3,2,1,0:T(8,128)(2,1)}, u32[]{:S(2)}, u32[]{:S(2)}) collective-permute-start(bf16[1,6,32,256]{3,2,1,0:T(8,128)(2,1)S(1)} %get-tuple-element.66), channel_id=1, source_target_pairs={{0,64},{64,128},{128,192},{192,256},{256,320},{320,384},{384,448},... | collective-permute-start | bytes 294920 | tf_op jit(solution)/shard_map/ppermute | solution.py:17
  162.4 5.4 %collective-permute-start.24 = (bf16[1,6,32,256]{3,2,1,0:T(8,128)(2,1)S(1)}, bf16[1,6,32,256]{3,2,1,0:T(8,128)(2,1)S(1)}, u32[]{:S(2)}, u32[]{:S(2)}) collective-permute-start(bf16[1,6,32,256]{3,2,1,0:T(8,128)(2,1)S(1)} %get-tuple-element.66), channel_id=1, source_target_pairs={{64,0},{128,64},{192,128},{256,192},{320,256},{384,320},{448,384},... | collective-permute-start | bytes 294920 | tf_op jit(solution)/shard_map/ppermute | solution.py:20
  168.0 9.0 %copy-start.1 = (bf16[7,1,2,288,256]{4,3,2,0,1:T(8,128)(2,1)S(1)}, bf16[7,1,2,288,256]{4,3,2,0,1:T(8,128)(2,1)}, u32[]{:S(2)}) copy-start(bf16[7,1,2,288,256]{4,3,2,0,1:T(8,128)(2,1)} %copy-done) | copy-start | bytes 6193156
  170.4 9.2 %collective-permute-start.27 = (bf16[1,4,32,256]{3,2,1,0:T(8,128)(2,1)}, bf16[1,4,32,256]{3,2,1,0:T(8,128)(2,1)}, u32[]{:S(2)}, u32[]{:S(2)}) collective-permute-start(bf16[1,4,32,256]{3,2,1,0:T(8,128)(2,1)} %get-tuple-element.68), channel_id=1, source_target_pairs={{0,64},{64,128},{128,192},{192,256},{256,320},{320,384},{384,448},... | collective-permute-start | bytes 196616 | tf_op jit(solution)/shard_map/ppermute | solution.py:17
  175.7 5.3 %collective-permute-start.26 = (bf16[1,4,32,256]{3,2,1,0:T(8,128)(2,1)}, bf16[1,4,32,256]{3,2,1,0:T(8,128)(2,1)}, u32[]{:S(2)}, u32[]{:S(2)}) collective-permute-start(bf16[1,4,32,256]{3,2,1,0:T(8,128)(2,1)} %get-tuple-element.68), channel_id=1, source_target_pairs={{64,0},{128,64},{192,128},{256,192},{320,256},{384,320},{448,384},... | collective-permute-start | bytes 196616 | tf_op jit(solution)/shard_map/ppermute | solution.py:20
  177.7 3.3 %copy-start.3 = (f32[4,256,32]{1,2,0:T(8,128)S(1)}, f32[4,256,32]{1,2,0:T(8,128)}, u32[]{:S(2)}) copy-start(f32[4,256,32]{1,2,0:T(8,128)} %fusion.195) | copy-start | bytes 393220
  178.7 3.3 %copy-start.8 = (bf16[1,9,32,32]{2,3,1,0:T(8,128)(2,1)S(1)}, bf16[1,9,32,32]{2,3,1,0:T(8,128)(2,1)}, u32[]{:S(2)}) copy-start(bf16[1,9,32,32]{2,3,1,0:T(8,128)(2,1)} %copy.256) | copy-start | bytes 55300
  179.1 3.6 %copy-start.7 = (bf16[1,1,2,288,256]{4,3,2,0,1:T(8,128)(2,1)S(1)}, bf16[1,1,2,288,256]{4,3,2,0,1:T(8,128)(2,1)}, u32[]{:S(2)}) copy-start(bf16[1,1,2,288,256]{4,3,2,0,1:T(8,128)(2,1)} %copy-done.6) | copy-start | bytes 884740
  179.1 4.1 %copy-start.5 = (f32[7,3072]{1,0:T(8,128)S(1)}, f32[7,3072]{1,0:T(8,128)}, u32[]{:S(2)}) copy-start(f32[7,3072]{1,0:T(8,128)} %reshape.1306) | copy-start | bytes 258052
  183.2 50.0 %copy-start.10 = (bf16[1,4,32,256]{3,2,1,0:T(8,128)(2,1)S(1)}, bf16[1,4,32,256]{3,2,1,0:T(8,128)(2,1)}, u32[]{:S(2)}) copy-start(bf16[1,4,32,256]{3,2,1,0:T(8,128)(2,1)} %get-tuple-element.69) | copy-start | bytes 196612
  185.1 42.7 %all-to-all-start.1 = ((f32[512,1,192]{2,1,0:T(1,128)}), f32[512,1,192]{2,1,0:T(1,128)S(1)}, u32[]{:S(2)}, u32[]{:S(2)}) async-start(f32[512,1,192]{2,1,0:T(1,128)} %mul.99), calls=%async_computation.1 | async-start | bytes 1048576 | tf_op jit(solution)/shard_map/all_to_all | solution.py:237
  229.0 14.0 %all-to-all-start.2 = ((f32[64,1,192]{2,1,0:T(1,128)}), f32[64,1,192]{2,1,0:T(1,128)S(1)}, u32[]{:S(2)}, u32[]{:S(2)}) async-start(f32[64,1,192]{2,1,0:T(1,128)} %broadcast_in_dim.21), calls=%async_computation.2 | async-start | bytes 131072 | tf_op jit(solution)/shard_map/all_to_all | solution.py:238

commit v8 on v7

--- a/solution.py
+++ b/solution.py
@@ -141,12 +141,13 @@
     scale = 1.0 / math.sqrt(sections * height * lax.axis_size("gy") * width)
     segment = lax.axis_index("segment")
 
-    block = acts[0].reshape(count, -1, width)
+    framed = jnp.pad(acts[0], [(1, 1)] + [(0, 0)] * (acts.ndim - 2))
+    block = jnp.stack([framed[d * zs : d * zs + zs + 2] for d in range(count)]).reshape(count, -1, width)
     kernels = jnp.concatenate([w_plane.reshape(-1), w_depth.reshape(-1)]).reshape(-1, width)
     send = jnp.concatenate([block, jnp.broadcast_to(kernels[None], (count,) + kernels.shape)], axis=1)
     got = lax.all_to_all(send, "segment", 0, 0, tiled=True)
     cut_a = block.shape[1]
-    mine = got[:, :cut_a].reshape((count, zs) + acts.shape[2:])
+    mine = got[:, :cut_a].reshape((count, zs + 2) + acts.shape[2:])
     taps = w_plane.shape[1] * w_plane.shape[2]
     weights = lax.optimization_barrier(got[:, cut_a:].reshape(count, -1, chans, chans))
     plane_w = weights[:, :taps].reshape((count,) + w_plane.shape[1:])
@@ -158,9 +159,9 @@
     hit = jnp.any(tiles[0][None, None, :] == ids[:, :, None], axis=2)
     mask_full = jnp.repeat(hit.astype(jnp.float32), TILE, axis=1)[:, None, None, :]
 
-    rows_own = padded_2(mine, (("gy", 2),), 1)
-    mid = plane_conv_all(rows_own, plane_w, height, width).astype(jnp.bfloat16)
-    deep = padded_2(mid, (("segment", 1),), 1)
+    rows_all = padded_2(mine, (("gy", 2),), 1)
+    deep = plane_conv_all(rows_all, plane_w, height, width).astype(jnp.bfloat16)
+    rows_own = rows_all[:, 1 : 1 + zs]
     value = depth_conv_all(deep, depth_w, zs)
     factor = silu_slope(value) * mask_full[None]
 

time: 246 us -> 258 us (1.049)
  local copies, waits for them, and re-layouts: 11.2 us -> 22.7 us
  starting transfers between devices: 109 us -> 105 us
  waiting for transfers between devices: 89.2 us -> 92.5 us
    all_to_all x1, waiting for transfers between devices: 16.2 us -> 27.5 us  [local(): got = lax.all_to_all(send, 'segment', 0, 0, tiled=True)]
    slice x9, local copies, waits for them, and re-layouts: 1.57 us -> 10.6 us  [local(): plane_w[layer]]
    ppermute x10 -> x9, starting transfers between devices: 34.2 us -> 26.3 us  [padded_2(): lax.ppermute(lax.slice_in_dim(block, block.shape[dim] - width, None, axis...]
    ppermute x8, waiting for transfers between devices: 9.99 us -> 5.78 us  [passed_along(): return lax.ppermute(block, axis, route)]
    all_to_all x1, starting transfers between devices: 20 us -> 23.9 us  [local(): part = lax.all_to_all(flat, ('segment', 'gy'), 0, 0, tiled=True).sum(axis=0)]
    ppermute x10 -> x9, waiting for transfers between devices: 26.9 us -> 24.9 us  [padded_2(): lax.ppermute(lax.slice_in_dim(block, 0, width, axis=dim), axis, backward)]
    ppermute x10 -> x9, starting transfers between devices: 14.3 us -> 12.9 us  [padded_2(): lax.ppermute(lax.slice_in_dim(block, 0, width, axis=dim), axis, backward)]
  transfers between devices with their start and end apart: 31 -> 29, of which waited for: 22 -> 19; matrix products, arithmetic and copies ran while one was open for 6% -> 9% of each run, Pallas kernels for 0% -> 0%
where the time goes in v8:
time: 258 us; the launch traced here: 256 us
  starting transfers between devices  105 us (41%)
  waiting for transfers between devices  92.5 us (36%)
  matrix products  29.7 us (12%)
  local copies, waits for them, and re-layouts  22.7 us (9%)
  other arithmetic  3.22 us (1%)
    all_to_all x1, waiting for transfers between devices, local(): got = lax.all_to_all(send, 'segment', 0, 0, tiled=True)  27.5 us
    ppermute x8, starting transfers between devices, passed_along(): return lax.ppermute(block, axis, route)  27.4 us
    ppermute x9, starting transfers between devices, padded_2(): lax.ppermute(lax.slice_in_dim(block, block.shape[dim] - width, None, axis...  26.3 us
    ppermute x9, waiting for transfers between devices, padded_2(): lax.ppermute(lax.slice_in_dim(block, 0, width, axis=dim), axis, backward)  24.9 us
    all_to_all x1, starting transfers between devices, local(): part = lax.all_to_all(flat, ('segment', 'gy'), 0, 0, tiled=True).sum(axis=0)  23.9 us
    all_to_all x1, waiting for transfers between devices, local(): part = lax.all_to_all(flat, ('segment', 'gy'), 0, 0, tiled=True).sum(axis=0)  22.1 us
    dot_general x72, matrix products, plane_back(): jnp.einsum('oc,...yox->...ycx', kernel[i, j], padded[..., 2 - i:2 - i + h...  15.3 us
    ppermute x9, starting transfers between devices, padded_2(): lax.ppermute(lax.slice_in_dim(block, 0, width, axis=dim), axis, backward)  12.9 us
  transfers between devices with their start and end apart: 29, of which 19 were waited for; matrix products, arithmetic and copies ran while one was open for 9% of the time, Pallas kernels for 0%

profile of v8, /device:TPU:1, one launch (start us, length us, event | category | flops | bytes accessed | tf_op | source)
XLA Modules:
  0.0 256.0 jit_solution(16693101795655379516)
XLA Ops:
  5.0 10.9 %all-to-all-start = ((bf16[8,240,256]{2,1,0:T(8,128)(2,1)}), bf16[8,240,256]{2,1,0:T(8,128)(2,1)S(1)}, u32[]{:S(2)}, u32[]{:S(2)}) async-start(bf16[8,240,256]{2,1,0:T(8,128)(2,1)} %pad_maximum_fusion.1), calls=%async_computation | async-start | bytes 1966080 | tf_op jit(solution)/shard_map/all_to_all | solution.py:148
  16.1 27.5 %all-to-all-done = bf16[8,240,256]{2,1,0:T(8,128)(2,1)S(1)} async-done(((bf16[8,240,256]{2,1,0:T(8,128)(2,1)}), bf16[8,240,256]{2,1,0:T(8,128)(2,1)S(1)}, u32[]{:S(2)}, u32[]{:S(2)}) %all-to-all-start) | async-done | bytes 983072 | tf_op jit(solution)/shard_map/all_to_all | solution.py:148
  44.5 2.4 collective-permute-start.1
  47.2 3.2 %collective-permute-start = (bf16[8,3,1,32,256]{4,3,2,1,0:T(8,128)(2,1)S(1)}, bf16[8,3,1,32,256]{4,3,2,1,0:T(8,128)(2,1)S(1)}, u32[]{:S(2)}, u32[]{:S(2)}) collective-permute-start(bf16[8,3,1,32,256]{4,3,2,1,0:T(8,128)(2,1)S(1)} %get-tuple-element.17), channel_id=1, source_target_pairs={{0,1},{1,2},{2,3},{3,4},{4,5},{5,6},{6,7},{7,8},{8,9},{9,10},{10,1... | collective-permute-start | bytes 1179656 | tf_op jit(solution)/shard_map/ppermute | solution.py:17
  53.0 1.6 copy.232
  54.6 1.6 copy.237
  57.9 1.6 copy.252
  59.5 1.6 copy.256
  66.5 1.9 collective-permute-start.4
  68.5 3.6 %collective-permute-start.3 = (bf16[9,1,2,32,256]{4,3,2,1,0:T(8,128)(2,1)S(1)}, bf16[9,1,2,32,256]{4,3,2,1,0:T(8,128)(2,1)S(1)}, u32[]{:S(2)}, u32[]{:S(2)}) collective-permute-start(bf16[9,1,2,32,256]{4,3,2,1,0:T(8,128)(2,1)S(1)} %pad_maximum_fusion.2), channel_id=1, source_target_pairs={{0,1},{1,2},{2,3},{3,4},{4,5},{5,6},{6,7},{7,8},{8,9},{9,10},{10,1... | collective-permute-start | bytes 884744 | tf_op jit(solution)/shard_map/ppermute | solution.py:28
  72.2 1.3 collective-permute-start.5
  73.5 4.0 %collective-permute-start.2 = (bf16[5,1,2,32,256]{4,3,2,1,0:T(8,128)(2,1)S(1)}, bf16[5,1,2,32,256]{4,3,2,1,0:T(8,128)(2,1)S(1)}, u32[]{:S(2)}, u32[]{:S(2)}) collective-permute-start(bf16[5,1,2,32,256]{4,3,2,1,0:T(8,128)(2,1)S(1)} %pad_maximum_fusion.5), channel_id=1, source_target_pairs={{0,2},{1,3},{2,4},{3,5},{4,6},{5,7},{6,8},{7,9},{8,10},{9,11},{10,... | collective-permute-start | bytes 491528 | tf_op jit(solution)/shard_map/ppermute | solution.py:28
  79.1 1.9 collective-permute-done.2
  81.3 2.1 collective-permute-start.7
  83.5 1.3 collective-permute-start.6
  85.8 1.3 collective-permute-done.7
  87.3 3.6 %collective-permute-done.6 = bf16[1,10,32,256]{3,2,1,0:T(8,128)(2,1)S(1)} collective-permute-done((bf16[1,10,32,256]{3,2,1,0:T(8,128)(2,1)S(1)}, bf16[1,10,32,256]{3,2,1,0:T(8,128)(2,1)S(1)}, u32[]{:S(2)}, u32[]{:S(2)}) %collective-permute-start.6) | collective-permute-done | bytes 163872 | tf_op jit(solution)/shard_map/ppermute | solution.py:20
  93.1 2.1 collective-permute-start.9
  95.2 1.3 collective-permute-start.8
  97.3 3.6 %collective-permute-done.8 = bf16[1,8,32,256]{3,2,1,0:T(8,128)(2,1)S(1)} collective-permute-done((bf16[1,8,32,256]{3,2,1,0:T(8,128)(2,1)S(1)}, bf16[1,8,32,256]{3,2,1,0:T(8,128)(2,1)S(1)}, u32[]{:S(2)}, u32[]{:S(2)}) %collective-permute-start.8) | collective-permute-done | bytes 131104 | tf_op jit(solution)/shard_map/ppermute | solution.py:20
  103.0 2.3 collective-permute-start.11
  105.6 1.3 collective-permute-start.10
  107.2 3.7 %collective-permute-done.10 = bf16[1,6,32,256]{3,2,1,0:T(8,128)(2,1)S(1)} collective-permute-done((bf16[1,6,32,256]{3,2,1,0:T(8,128)(2,1)S(1)}, bf16[1,6,32,256]{3,2,1,0:T(8,128)(2,1)S(1)}, u32[]{:S(2)}, u32[]{:S(2)}) %collective-permute-start.10) | collective-permute-done | bytes 98336 | tf_op jit(solution)/shard_map/ppermute | solution.py:20
  112.9 3.4 %collective-permute-start.13 = (bf16[1,4,32,256]{3,2,1,0:T(8,128)(2,1)S(1)}, bf16[1,4,32,256]{3,2,1,0:T(8,128)(2,1)S(1)}, u32[]{:S(2)}, u32[]{:S(2)}) collective-permute-start(bf16[1,4,32,256]{3,2,1,0:T(8,128)(2,1)S(1)} %get-tuple-element.76), channel_id=1, source_target_pairs={{0,64},{64,128},{128,192},{192,256},{256,320},{320,384},{384,448},... | collective-permute-start | bytes 196616 | tf_op jit(solution)/shard_map/ppermute | solution.py:17
  116.4 1.3 collective-permute-start.12
  117.9 3.5 %collective-permute-done.12 = bf16[1,4,32,256]{3,2,1,0:T(8,128)(2,1)S(1)} collective-permute-done((bf16[1,4,32,256]{3,2,1,0:T(8,128)(2,1)S(1)}, bf16[1,4,32,256]{3,2,1,0:T(8,128)(2,1)S(1)}, u32[]{:S(2)}, u32[]{:S(2)}) %collective-permute-start.12) | collective-permute-done | bytes 65568 | tf_op jit(solution)/shard_map/ppermute | solution.py:20
  123.2 3.5 %collective-permute-start.14 = (bf16[1,2,32,256]{3,2,1,0:T(8,128)(2,1)S(1)}, bf16[1,2,32,256]{3,2,1,0:T(8,128)(2,1)S(1)}, u32[]{:S(2)}, u32[]{:S(2)}) collective-permute-start(bf16[1,2,32,256]{3,2,1,0:T(8,128)(2,1)S(1)} %fusion.46), channel_id=1, source_target_pairs={{0,2},{1,3},{2,4},{3,5},{4,6},{5,7},{6,8},{7,9},{8,10},{9,11},{10,... | collective-permute-start | bytes 98312 | tf_op jit(solution)/shard_map/ppermute | solution.py:28
  126.8 9.8 %collective-permute-start.15 = (bf16[1,2,32,256]{3,2,1,0:T(8,128)(2,1)S(1)}, bf16[1,2,32,256]{3,2,1,0:T(8,128)(2,1)S(1)}, u32[]{:S(2)}, u32[]{:S(2)}) collective-permute-start(bf16[1,2,32,256]{3,2,1,0:T(8,128)(2,1)S(1)} %fusion.46), channel_id=1, source_target_pairs={{0,1},{1,2},{2,3},{3,4},{4,5},{5,6},{6,7},{7,8},{8,9},{9,10},{10,1... | collective-permute-start | bytes 98312 | tf_op jit(solution)/shard_map/ppermute | solution.py:28
  136.6 1.9 collective-permute-start.16
  138.5 1.3 collective-permute-start.17
  139.9 1.9 collective-permute-done.16
  141.8 1.9 collective-permute-done.17
  143.8 3.2 %collective-permute-start.19 = (bf16[1,10,32,256]{3,2,1,0:T(8,128)(2,1)S(1)}, bf16[1,10,32,256]{3,2,1,0:T(8,128)(2,1)S(1)}, u32[]{:S(2)}, u32[]{:S(2)}) collective-permute-start(bf16[1,10,32,256]{3,2,1,0:T(8,128)(2,1)S(1)} %fusion.66), channel_id=1, source_target_pairs={{0,64},{64,128},{128,192},{192,256},{256,320},{320,384},{384,448},... | collective-permute-start | bytes 491528 | tf_op jit(solution)/shard_map/ppermute | solution.py:17
  147.0 1.5 collective-permute-start.18
  150.1 3.8 %collective-permute-done.18 = bf16[1,10,32,256]{3,2,1,0:T(8,128)(2,1)S(1)} collective-permute-done((bf16[1,10,32,256]{3,2,1,0:T(8,128)(2,1)S(1)}, bf16[1,10,32,256]{3,2,1,0:T(8,128)(2,1)S(1)}, u32[]{:S(2)}, u32[]{:S(2)}) %collective-permute-start.18) | collective-permute-done | bytes 163872 | tf_op jit(solution)/shard_map/ppermute | solution.py:20
  156.0 2.8 %collective-permute-start.21 = (bf16[1,8,32,256]{3,2,1,0:T(8,128)(2,1)S(1)}, bf16[1,8,32,256]{3,2,1,0:T(8,128)(2,1)S(1)}, u32[]{:S(2)}, u32[]{:S(2)}) collective-permute-start(bf16[1,8,32,256]{3,2,1,0:T(8,128)(2,1)S(1)} %get-tuple-element.78), channel_id=1, source_target_pairs={{0,64},{64,128},{128,192},{192,256},{256,320},{320,384},{384,448},... | collective-permute-start | bytes 393224 | tf_op jit(solution)/shard_map/ppermute | solution.py:17
  158.9 1.3 collective-permute-start.20
  161.0 3.6 %collective-permute-done.20 = bf16[1,8,32,256]{3,2,1,0:T(8,128)(2,1)S(1)} collective-permute-done((bf16[1,8,32,256]{3,2,1,0:T(8,128)(2,1)S(1)}, bf16[1,8,32,256]{3,2,1,0:T(8,128)(2,1)S(1)}, u32[]{:S(2)}, u32[]{:S(2)}) %collective-permute-start.20) | collective-permute-done | bytes 131104 | tf_op jit(solution)/shard_map/ppermute | solution.py:20
  166.7 3.6 %collective-permute-start.23 = (bf16[1,6,32,256]{3,2,1,0:T(8,128)(2,1)S(1)}, bf16[1,6,32,256]{3,2,1,0:T(8,128)(2,1)}, u32[]{:S(2)}, u32[]{:S(2)}) collective-permute-start(bf16[1,6,32,256]{3,2,1,0:T(8,128)(2,1)S(1)} %get-tuple-element.80), channel_id=1, source_target_pairs={{0,64},{64,128},{128,192},{192,256},{256,320},{320,384},{384,448},... | collective-permute-start | bytes 294920 | tf_op jit(solution)/shard_map/ppermute | solution.py:17
  170.4 1.3 collective-permute-start.22
  173.7 2.2 collective-permute-done.22
  179.4 3.6 %collective-permute-start.25 = (bf16[1,4,32,256]{3,2,1,0:T(8,128)(2,1)S(1)}, bf16[1,4,32,256]{3,2,1,0:T(8,128)(2,1)}, u32[]{:S(2)}, u32[]{:S(2)}) collective-permute-start(bf16[1,4,32,256]{3,2,1,0:T(8,128)(2,1)S(1)} %get-tuple-element.82), channel_id=1, source_target_pairs={{0,64},{64,128},{128,192},{192,256},{256,320},{320,384},{384,448},... | collective-permute-start | bytes 196616 | tf_op jit(solution)/shard_map/ppermute | solution.py:17
  183.2 1.3 collective-permute-start.24
  190.7 1.7 mul.99
  192.4 23.9 %all-to-all-start.1 = ((f32[512,1,192]{2,1,0:T(1,128)}), f32[512,1,192]{2,1,0:T(1,128)S(1)}, u32[]{:S(2)}, u32[]{:S(2)}) async-start(f32[512,1,192]{2,1,0:T(1,128)} %mul.99), calls=%async_computation.1 | async-start | bytes 1048576 | tf_op jit(solution)/shard_map/all_to_all | solution.py:238
  216.9 22.1 %all-to-all-done.1 = f32[512,1,192]{2,1,0:T(1,128)S(1)} async-done(((f32[512,1,192]{2,1,0:T(1,128)}), f32[512,1,192]{2,1,0:T(1,128)S(1)}, u32[]{:S(2)}, u32[]{:S(2)}) %all-to-all-start.1) | async-done | bytes 393248 | tf_op jit(solution)/shard_map/all_to_all | solution.py:238
  240.2 4.2 %all-to-all-start.2 = ((f32[64,1,192]{2,1,0:T(1,128)}), f32[64,1,192]{2,1,0:T(1,128)S(1)}, u32[]{:S(2)}, u32[]{:S(2)}) async-start(f32[64,1,192]{2,1,0:T(1,128)} %broadcast_in_dim.21), calls=%async_computation.2 | async-start | bytes 131072 | tf_op jit(solution)/shard_map/all_to_all | solution.py:239
  245.2 8.9 %all-to-all-done.2 = f32[64,1,192]{2,1,0:T(1,128)S(1)} async-done(((f32[64,1,192]{2,1,0:T(1,128)}), f32[64,1,192]{2,1,0:T(1,128)S(1)}, u32[]{:S(2)}, u32[]{:S(2)}) %all-to-all-start.2) | async-done | bytes 49184 | tf_op jit(solution)/shard_map/all_to_all | solution.py:239
  (276 shorter events, 50.5 us)
Async XLA Ops:
  0.6 3.1 %copy-start = (bf16[1,8,2,32,256]{4,3,2,1,0:T(8,128)(2,1)S(1)}, bf16[1,8,2,32,256]{4,3,2,1,0:T(8,128)(2,1)}, u32[]{:S(2)}) copy-start(bf16[1,8,2,32,256]{4,3,2,1,0:T(8,128)(2,1)} %param.5) | copy-start | bytes 786436
  3.9 11.9 %copy-start.12 = (s32[1,12]{1,0:T(1,128)S(1)}, s32[1,12]{1,0:T(1,128)}, u32[]{:S(2)}) copy-start(s32[1,12]{1,0:T(1,128)} %param.9) | copy-start | bytes 148
  5.0 38.7 %all-to-all-start = ((bf16[8,240,256]{2,1,0:T(8,128)(2,1)}), bf16[8,240,256]{2,1,0:T(8,128)(2,1)S(1)}, u32[]{:S(2)}, u32[]{:S(2)}) async-start(bf16[8,240,256]{2,1,0:T(8,128)(2,1)} %pad_maximum_fusion.1), calls=%async_computation | async-start | bytes 1966080 | tf_op jit(solution)/shard_map/all_to_all | solution.py:148
  44.5 17.0 %collective-permute-start.1 = (bf16[8,3,1,32,256]{4,3,2,1,0:T(8,128)(2,1)}, bf16[8,3,1,32,256]{4,3,2,1,0:T(8,128)(2,1)S(1)}, u32[]{:S(2)}, u32[]{:S(2)}) collective-permute-start(bf16[8,3,1,32,256]{4,3,2,1,0:T(8,128)(2,1)} %get-tuple-element.18), channel_id=1, source_target_pairs={{1,0},{2,1},{3,2},{4,3},{5,4},{6,5},{7,6},{8,7},{9,8},{10,9},{11,1... | collective-permute-start | bytes 1179656 | tf_op jit(solution)/shard_map/ppermute | solution.py:20
  47.2 14.3 %collective-permute-start = (bf16[8,3,1,32,256]{4,3,2,1,0:T(8,128)(2,1)S(1)}, bf16[8,3,1,32,256]{4,3,2,1,0:T(8,128)(2,1)S(1)}, u32[]{:S(2)}, u32[]{:S(2)}) collective-permute-start(bf16[8,3,1,32,256]{4,3,2,1,0:T(8,128)(2,1)S(1)} %get-tuple-element.17), channel_id=1, source_target_pairs={{0,1},{1,2},{2,3},{3,4},{4,5},{5,6},{6,7},{7,8},{8,9},{9,10},{10,1... | collective-permute-start | bytes 1179656 | tf_op jit(solution)/shard_map/ppermute | solution.py:17
  65.8 0.8 copy-start.3
  66.5 14.6 %collective-permute-start.4 = (bf16[9,1,2,32,256]{4,3,2,1,0:T(8,128)(2,1)S(1)}, bf16[9,1,2,32,256]{4,3,2,1,0:T(8,128)(2,1)S(1)}, u32[]{:S(2)}, u32[]{:S(2)}) collective-permute-start(bf16[9,1,2,32,256]{4,3,2,1,0:T(8,128)(2,1)S(1)} %pad_maximum_fusion.2), channel_id=1, source_target_pairs={{1,0},{2,1},{3,2},{4,3},{5,4},{6,5},{7,6},{8,7},{9,8},{10,9},{11,1... | collective-permute-start | bytes 884744 | tf_op jit(solution)/shard_map/ppermute | solution.py:28
  68.5 12.6 %collective-permute-start.3 = (bf16[9,1,2,32,256]{4,3,2,1,0:T(8,128)(2,1)S(1)}, bf16[9,1,2,32,256]{4,3,2,1,0:T(8,128)(2,1)S(1)}, u32[]{:S(2)}, u32[]{:S(2)}) collective-permute-start(bf16[9,1,2,32,256]{4,3,2,1,0:T(8,128)(2,1)S(1)} %pad_maximum_fusion.2), channel_id=1, source_target_pairs={{0,1},{1,2},{2,3},{3,4},{4,5},{5,6},{6,7},{7,8},{8,9},{9,10},{10,1... | collective-permute-start | bytes 884744 | tf_op jit(solution)/shard_map/ppermute | solution.py:28
  72.2 8.9 %collective-permute-start.5 = (bf16[5,1,2,32,256]{4,3,2,1,0:T(8,128)(2,1)S(1)}, bf16[5,1,2,32,256]{4,3,2,1,0:T(8,128)(2,1)S(1)}, u32[]{:S(2)}, u32[]{:S(2)}) collective-permute-start(bf16[5,1,2,32,256]{4,3,2,1,0:T(8,128)(2,1)S(1)} %pad_maximum_fusion.5), channel_id=1, source_target_pairs={{2,0},{3,1},{4,2},{5,3},{6,4},{7,5},{8,6},{9,7},{10,8},{11,9},{12,... | collective-permute-start | bytes 491528 | tf_op jit(solution)/shard_map/ppermute | solution.py:28
  73.5 7.5 %collective-permute-start.2 = (bf16[5,1,2,32,256]{4,3,2,1,0:T(8,128)(2,1)S(1)}, bf16[5,1,2,32,256]{4,3,2,1,0:T(8,128)(2,1)S(1)}, u32[]{:S(2)}, u32[]{:S(2)}) collective-permute-start(bf16[5,1,2,32,256]{4,3,2,1,0:T(8,128)(2,1)S(1)} %pad_maximum_fusion.5), channel_id=1, source_target_pairs={{0,2},{1,3},{2,4},{3,5},{4,6},{5,7},{6,8},{7,9},{8,10},{9,11},{10,... | collective-permute-start | bytes 491528 | tf_op jit(solution)/shard_map/ppermute | solution.py:28
  79.1 2.2 copy-start.1
  81.3 5.8 %collective-permute-start.7 = (bf16[1,10,32,256]{3,2,1,0:T(8,128)(2,1)S(1)}, bf16[1,10,32,256]{3,2,1,0:T(8,128)(2,1)S(1)}, u32[]{:S(2)}, u32[]{:S(2)}) collective-permute-start(bf16[1,10,32,256]{3,2,1,0:T(8,128)(2,1)S(1)} %fusion.64), channel_id=1, source_target_pairs={{0,64},{64,128},{128,192},{192,256},{256,320},{320,384},{384,448},... | collective-permute-start | bytes 491528 | tf_op jit(solution)/shard_map/ppermute | solution.py:17
  83.5 7.4 %collective-permute-start.6 = (bf16[1,10,32,256]{3,2,1,0:T(8,128)(2,1)S(1)}, bf16[1,10,32,256]{3,2,1,0:T(8,128)(2,1)S(1)}, u32[]{:S(2)}, u32[]{:S(2)}) collective-permute-start(bf16[1,10,32,256]{3,2,1,0:T(8,128)(2,1)S(1)} %fusion.64), channel_id=1, source_target_pairs={{64,0},{128,64},{192,128},{256,192},{320,256},{384,320},{448,384},... | collective-permute-start | bytes 491528 | tf_op jit(solution)/shard_map/ppermute | solution.py:20
  85.5 5.6 %copy-start.5 = (bf16[1,9,32,32]{2,3,1,0:T(8,128)(2,1)S(1)}, bf16[1,9,32,32]{2,3,1,0:T(8,128)(2,1)}, u32[]{:S(2)}) copy-start(bf16[1,9,32,32]{2,3,1,0:T(8,128)(2,1)} %copy.222) | copy-start | bytes 55300
  93.1 4.0 %collective-permute-start.9 = (bf16[1,8,32,256]{3,2,1,0:T(8,128)(2,1)S(1)}, bf16[1,8,32,256]{3,2,1,0:T(8,128)(2,1)S(1)}, u32[]{:S(2)}, u32[]{:S(2)}) collective-permute-start(bf16[1,8,32,256]{3,2,1,0:T(8,128)(2,1)S(1)} %get-tuple-element.72), channel_id=1, source_target_pairs={{0,64},{64,128},{128,192},{192,256},{256,320},{320,384},{384,448},... | collective-permute-start | bytes 393224 | tf_op jit(solution)/shard_map/ppermute | solution.py:17
  95.2 5.7 %collective-permute-start.8 = (bf16[1,8,32,256]{3,2,1,0:T(8,128)(2,1)S(1)}, bf16[1,8,32,256]{3,2,1,0:T(8,128)(2,1)S(1)}, u32[]{:S(2)}, u32[]{:S(2)}) collective-permute-start(bf16[1,8,32,256]{3,2,1,0:T(8,128)(2,1)S(1)} %get-tuple-element.72), channel_id=1, source_target_pairs={{64,0},{128,64},{192,128},{256,192},{320,256},{384,320},{448,384},... | collective-permute-start | bytes 393224 | tf_op jit(solution)/shard_map/ppermute | solution.py:20
  102.4 8.7 %copy-start.9 = (bf16[1,9,32,32]{2,3,1,0:T(8,128)(2,1)S(1)}, bf16[1,9,32,32]{2,3,1,0:T(8,128)(2,1)}, u32[]{:S(2)}) copy-start(bf16[1,9,32,32]{2,3,1,0:T(8,128)(2,1)} %copy.232) | copy-start | bytes 55300
  103.0 3.9 %collective-permute-start.11 = (bf16[1,6,32,256]{3,2,1,0:T(8,128)(2,1)S(1)}, bf16[1,6,32,256]{3,2,1,0:T(8,128)(2,1)S(1)}, u32[]{:S(2)}, u32[]{:S(2)}) collective-permute-start(bf16[1,6,32,256]{3,2,1,0:T(8,128)(2,1)S(1)} %get-tuple-element.74), channel_id=1, source_target_pairs={{0,64},{64,128},{128,192},{192,256},{256,320},{320,384},{384,448},... | collective-permute-start | bytes 294920 | tf_op jit(solution)/shard_map/ppermute | solution.py:17
  105.6 5.4 %collective-permute-start.10 = (bf16[1,6,32,256]{3,2,1,0:T(8,128)(2,1)S(1)}, bf16[1,6,32,256]{3,2,1,0:T(8,128)(2,1)S(1)}, u32[]{:S(2)}, u32[]{:S(2)}) collective-permute-start(bf16[1,6,32,256]{3,2,1,0:T(8,128)(2,1)S(1)} %get-tuple-element.74), channel_id=1, source_target_pairs={{64,0},{128,64},{192,128},{256,192},{320,256},{384,320},{448,384},... | collective-permute-start | bytes 294920 | tf_op jit(solution)/shard_map/ppermute | solution.py:20
  111.7 9.9 %copy-start.7 = (bf16[1,9,32,32]{2,3,1,0:T(8,128)(2,1)S(1)}, bf16[1,9,32,32]{2,3,1,0:T(8,128)(2,1)}, u32[]{:S(2)}) copy-start(bf16[1,9,32,32]{2,3,1,0:T(8,128)(2,1)} %copy.237) | copy-start | bytes 55300
  112.9 4.9 %collective-permute-start.13 = (bf16[1,4,32,256]{3,2,1,0:T(8,128)(2,1)S(1)}, bf16[1,4,32,256]{3,2,1,0:T(8,128)(2,1)S(1)}, u32[]{:S(2)}, u32[]{:S(2)}) collective-permute-start(bf16[1,4,32,256]{3,2,1,0:T(8,128)(2,1)S(1)} %get-tuple-element.76), channel_id=1, source_target_pairs={{0,64},{64,128},{128,192},{192,256},{256,320},{320,384},{384,448},... | collective-permute-start | bytes 196616 | tf_op jit(solution)/shard_map/ppermute | solution.py:17
  116.4 5.0 %collective-permute-start.12 = (bf16[1,4,32,256]{3,2,1,0:T(8,128)(2,1)S(1)}, bf16[1,4,32,256]{3,2,1,0:T(8,128)(2,1)S(1)}, u32[]{:S(2)}, u32[]{:S(2)}) collective-permute-start(bf16[1,4,32,256]{3,2,1,0:T(8,128)(2,1)S(1)} %get-tuple-element.76), channel_id=1, source_target_pairs={{64,0},{128,64},{192,128},{256,192},{320,256},{384,320},{448,384},... | collective-permute-start | bytes 196616 | tf_op jit(solution)/shard_map/ppermute | solution.py:20
  123.2 16.6 %collective-permute-start.14 = (bf16[1,2,32,256]{3,2,1,0:T(8,128)(2,1)S(1)}, bf16[1,2,32,256]{3,2,1,0:T(8,128)(2,1)S(1)}, u32[]{:S(2)}, u32[]{:S(2)}) collective-permute-start(bf16[1,2,32,256]{3,2,1,0:T(8,128)(2,1)S(1)} %fusion.46), channel_id=1, source_target_pairs={{0,2},{1,3},{2,4},{3,5},{4,6},{5,7},{6,8},{7,9},{8,10},{9,11},{10,... | collective-permute-start | bytes 98312 | tf_op jit(solution)/shard_map/ppermute | solution.py:28
  126.8 13.0 %collective-permute-start.15 = (bf16[1,2,32,256]{3,2,1,0:T(8,128)(2,1)S(1)}, bf16[1,2,32,256]{3,2,1,0:T(8,128)(2,1)S(1)}, u32[]{:S(2)}, u32[]{:S(2)}) collective-permute-start(bf16[1,2,32,256]{3,2,1,0:T(8,128)(2,1)S(1)} %fusion.46), channel_id=1, source_target_pairs={{0,1},{1,2},{2,3},{3,4},{4,5},{5,6},{6,7},{7,8},{8,9},{9,10},{10,1... | collective-permute-start | bytes 98312 | tf_op jit(solution)/shard_map/ppermute | solution.py:28
  136.6 5.2 %collective-permute-start.16 = (bf16[1,2,32,256]{3,2,1,0:T(8,128)(2,1)S(1)}, bf16[1,2,32,256]{3,2,1,0:T(8,128)(2,1)S(1)}, u32[]{:S(2)}, u32[]{:S(2)}) collective-permute-start(bf16[1,2,32,256]{3,2,1,0:T(8,128)(2,1)S(1)} %fusion.46), channel_id=1, source_target_pairs={{1,0},{2,1},{3,2},{4,3},{5,4},{6,5},{7,6},{8,7},{9,8},{10,9},{11,1... | collective-permute-start | bytes 98312 | tf_op jit(solution)/shard_map/ppermute | solution.py:28
  138.5 5.2 %collective-permute-start.17 = (bf16[1,2,32,256]{3,2,1,0:T(8,128)(2,1)S(1)}, bf16[1,2,32,256]{3,2,1,0:T(8,128)(2,1)S(1)}, u32[]{:S(2)}, u32[]{:S(2)}) collective-permute-start(bf16[1,2,32,256]{3,2,1,0:T(8,128)(2,1)S(1)} %fusion.46), channel_id=1, source_target_pairs={{2,0},{3,1},{4,2},{5,3},{6,4},{7,5},{8,6},{9,7},{10,8},{11,9},{12,... | collective-permute-start | bytes 98312 | tf_op jit(solution)/shard_map/ppermute | solution.py:28
  143.8 10.3 %copy-start.4 = (bf16[1,9,32,32]{2,3,1,0:T(8,128)(2,1)S(1)}, bf16[1,9,32,32]{2,3,1,0:T(8,128)(2,1)}, u32[]{:S(2)}) copy-start(bf16[1,9,32,32]{2,3,1,0:T(8,128)(2,1)} %copy.242) | copy-start | bytes 55300
  143.8 6.0 %collective-permute-start.19 = (bf16[1,10,32,256]{3,2,1,0:T(8,128)(2,1)S(1)}, bf16[1,10,32,256]{3,2,1,0:T(8,128)(2,1)S(1)}, u32[]{:S(2)}, u32[]{:S(2)}) collective-permute-start(bf16[1,10,32,256]{3,2,1,0:T(8,128)(2,1)S(1)} %fusion.66), channel_id=1, source_target_pairs={{0,64},{64,128},{128,192},{192,256},{256,320},{320,384},{384,448},... | collective-permute-start | bytes 491528 | tf_op jit(solution)/shard_map/ppermute | solution.py:17
  147.0 6.8 %collective-permute-start.18 = (bf16[1,10,32,256]{3,2,1,0:T(8,128)(2,1)S(1)}, bf16[1,10,32,256]{3,2,1,0:T(8,128)(2,1)S(1)}, u32[]{:S(2)}, u32[]{:S(2)}) collective-permute-start(bf16[1,10,32,256]{3,2,1,0:T(8,128)(2,1)S(1)} %fusion.66), channel_id=1, source_target_pairs={{64,0},{128,64},{192,128},{256,192},{320,256},{384,320},{448,384},... | collective-permute-start | bytes 491528 | tf_op jit(solution)/shard_map/ppermute | solution.py:20
  156.0 4.8 %collective-permute-start.21 = (bf16[1,8,32,256]{3,2,1,0:T(8,128)(2,1)S(1)}, bf16[1,8,32,256]{3,2,1,0:T(8,128)(2,1)S(1)}, u32[]{:S(2)}, u32[]{:S(2)}) collective-permute-start(bf16[1,8,32,256]{3,2,1,0:T(8,128)(2,1)S(1)} %get-tuple-element.78), channel_id=1, source_target_pairs={{0,64},{64,128},{128,192},{192,256},{256,320},{320,384},{384,448},... | collective-permute-start | bytes 393224 | tf_op jit(solution)/shard_map/ppermute | solution.py:17
  158.9 5.7 %collective-permute-start.20 = (bf16[1,8,32,256]{3,2,1,0:T(8,128)(2,1)S(1)}, bf16[1,8,32,256]{3,2,1,0:T(8,128)(2,1)S(1)}, u32[]{:S(2)}, u32[]{:S(2)}) collective-permute-start(bf16[1,8,32,256]{3,2,1,0:T(8,128)(2,1)S(1)} %get-tuple-element.78), channel_id=1, source_target_pairs={{64,0},{128,64},{192,128},{256,192},{320,256},{384,320},{448,384},... | collective-permute-start | bytes 393224 | tf_op jit(solution)/shard_map/ppermute | solution.py:20
  166.7 5.9 %collective-permute-start.23 = (bf16[1,6,32,256]{3,2,1,0:T(8,128)(2,1)S(1)}, bf16[1,6,32,256]{3,2,1,0:T(8,128)(2,1)}, u32[]{:S(2)}, u32[]{:S(2)}) collective-permute-start(bf16[1,6,32,256]{3,2,1,0:T(8,128)(2,1)S(1)} %get-tuple-element.80), channel_id=1, source_target_pairs={{0,64},{64,128},{128,192},{192,256},{256,320},{320,384},{384,448},... | collective-permute-start | bytes 294920 | tf_op jit(solution)/shard_map/ppermute | solution.py:17
  170.4 5.5 %collective-permute-start.22 = (bf16[1,6,32,256]{3,2,1,0:T(8,128)(2,1)S(1)}, bf16[1,6,32,256]{3,2,1,0:T(8,128)(2,1)}, u32[]{:S(2)}, u32[]{:S(2)}) collective-permute-start(bf16[1,6,32,256]{3,2,1,0:T(8,128)(2,1)S(1)} %get-tuple-element.80), channel_id=1, source_target_pairs={{64,0},{128,64},{192,128},{256,192},{320,256},{384,320},{448,384},... | collective-permute-start | bytes 294920 | tf_op jit(solution)/shard_map/ppermute | solution.py:20
  172.2 4.8 %copy-start.8 = (bf16[1,9,32,32]{2,3,1,0:T(8,128)(2,1)S(1)}, bf16[1,9,32,32]{2,3,1,0:T(8,128)(2,1)}, u32[]{:S(2)}) copy-start(bf16[1,9,32,32]{2,3,1,0:T(8,128)(2,1)} %copy.252) | copy-start | bytes 55300
  173.7 4.8 %copy-start.11 = (f32[1,1,32,256]{3,2,1,0:T(8,128)S(1)}, f32[1,1,32,256]{3,2,1,0:T(8,128)}, u32[]{:S(2)}) copy-start(f32[1,1,32,256]{3,2,1,0:T(8,128)} %get-tuple-element.91) | copy-start | bytes 98308
  177.6 7.0 %copy-start.2 = (bf16[7,1,2,288,256]{4,3,2,1,0:T(8,128)(2,1)S(1)}, bf16[7,1,2,288,256]{4,3,2,1,0:T(8,128)(2,1)}, u32[]{:S(2)}) copy-start(bf16[7,1,2,288,256]{4,3,2,1,0:T(8,128)(2,1)} %copy-done.1) | copy-start | bytes 6193156
  179.4 7.0 %collective-permute-start.25 = (bf16[1,4,32,256]{3,2,1,0:T(8,128)(2,1)S(1)}, bf16[1,4,32,256]{3,2,1,0:T(8,128)(2,1)}, u32[]{:S(2)}, u32[]{:S(2)}) collective-permute-start(bf16[1,4,32,256]{3,2,1,0:T(8,128)(2,1)S(1)} %get-tuple-element.82), channel_id=1, source_target_pairs={{0,64},{64,128},{128,192},{192,256},{256,320},{320,384},{384,448},... | collective-permute-start | bytes 196616 | tf_op jit(solution)/shard_map/ppermute | solution.py:17
  183.2 5.1 %collective-permute-start.24 = (bf16[1,4,32,256]{3,2,1,0:T(8,128)(2,1)S(1)}, bf16[1,4,32,256]{3,2,1,0:T(8,128)(2,1)}, u32[]{:S(2)}, u32[]{:S(2)}) collective-permute-start(bf16[1,4,32,256]{3,2,1,0:T(8,128)(2,1)S(1)} %get-tuple-element.82), channel_id=1, source_target_pairs={{64,0},{128,64},{192,128},{256,192},{320,256},{384,320},{448,384},... | collective-permute-start | bytes 196616 | tf_op jit(solution)/shard_map/ppermute | solution.py:20
  185.6 3.8 %copy-start.6 = (bf16[1,9,32,32]{2,3,1,0:T(8,128)(2,1)S(1)}, bf16[1,9,32,32]{2,3,1,0:T(8,128)(2,1)}, u32[]{:S(2)}) copy-start(bf16[1,9,32,32]{2,3,1,0:T(8,128)(2,1)} %copy.256) | copy-start | bytes 55300
  190.7 53.7 %copy-start.10 = (bf16[1,4,32,256]{3,2,1,0:T(8,128)(2,1)S(1)}, bf16[1,4,32,256]{3,2,1,0:T(8,128)(2,1)}, u32[]{:S(2)}) copy-start(bf16[1,4,32,256]{3,2,1,0:T(8,128)(2,1)} %get-tuple-element.83) | copy-start | bytes 196612
  192.4 46.6 %all-to-all-start.1 = ((f32[512,1,192]{2,1,0:T(1,128)}), f32[512,1,192]{2,1,0:T(1,128)S(1)}, u32[]{:S(2)}, u32[]{:S(2)}) async-start(f32[512,1,192]{2,1,0:T(1,128)} %mul.99), calls=%async_computation.1 | async-start | bytes 1048576 | tf_op jit(solution)/shard_map/all_to_all | solution.py:238
  240.2 13.9 %all-to-all-start.2 = ((f32[64,1,192]{2,1,0:T(1,128)}), f32[64,1,192]{2,1,0:T(1,128)S(1)}, u32[]{:S(2)}, u32[]{:S(2)}) async-start(f32[64,1,192]{2,1,0:T(1,128)} %broadcast_in_dim.21), calls=%async_computation.2 | async-start | bytes 131072 | tf_op jit(solution)/shard_map/all_to_all | solution.py:239

commit v9 on v7

--- a/solution.py
+++ b/solution.py
@@ -167,18 +167,30 @@
     need = halo_plan(layers, HALO)
     reach = -(-max(need) // height)
     factor_b = factor.astype(jnp.bfloat16)
-    lows, highs, picks = {}, {}, {}
+    sources = [(factor_b[layer], need[layer]) for layer in range(layers)]
+    sources.append((grad_out, need[layers - 1]))
+    lows, highs, spots = {}, {}, {}
     for dist in range(1, reach + 1):
-        chosen = [layer for layer in range(layers) if need[layer] > height * (dist - 1)]
-        picks[dist] = chosen
-        load = jnp.stack([factor_b[layer] for layer in chosen] + [grad_out])
-        lows[dist] = passed_along(load, "gy", dist)
-        highs[dist] = passed_along(load, "gy", -dist)
-
-    def halo_of(index_of, h, own):
+        low_parts, high_parts, at = [], [], 0
+        for index, (part, h) in enumerate(sources):
+            k = min(height, h - height * (dist - 1))
+            if k > 0:
+                low_parts.append(part[:, height - k :])
+                high_parts.append(part[:, :k])
+                spots[(dist, index)] = (at, k)
+                at += k
+        lows[dist] = passed_along(jnp.concatenate(low_parts, axis=1), "gy", dist)
+        highs[dist] = passed_along(jnp.concatenate(high_parts, axis=1), "gy", -dist)
+
+    def halo_of(index, h):
         span = -(-h // height)
-        low = jnp.concatenate([index_of(lows[d], d) for d in range(span, 0, -1)], axis=1)[:, -h:]
-        high = jnp.concatenate([index_of(highs[d], d) for d in range(1, span + 1)], axis=1)[:, :h]
+
+        def take(block, d):
+            at, k = spots[(d, index)]
+            return block[:, at : at + k]
+
+        low = jnp.concatenate([take(lows[d], d) for d in range(span, 0, -1)], axis=1)
+        high = jnp.concatenate([take(highs[d], d) for d in range(1, span + 1)], axis=1)
         return low, high
 
     def refreshed(grad, h):
@@ -187,7 +199,7 @@
         high = jnp.concatenate([passed_along(grad, "gy", -d) for d in range(1, span + 1)], axis=1)
         return jnp.concatenate([low[:, low.shape[1] - h :], grad, high[:, :h]], axis=1)
 
-    low, high = halo_of(lambda part, d: part[-1], need[layers - 1], grad_out)
+    low, high = halo_of(layers, need[layers - 1])
     grad = jnp.concatenate([low, grad_out, high], axis=1)
     plane_list = [None] * layers
     depth_list = [None] * layers
@@ -195,7 +207,7 @@
         h = need[layer]
         if grad.shape[1] != height + 2 * h:
             grad = refreshed(grad, h)
-        low, high = halo_of(lambda part, d: part[picks[d].index(layer)], h, None)
+        low, high = halo_of(layer, h)
         wide = jnp.concatenate([low.astype(jnp.float32), factor[layer], high.astype(jnp.float32)], axis=1)
         grad_mix = (grad.astype(jnp.float32) * wide).astype(jnp.bfloat16)
         mix_deep = padded_2(grad_mix, (("segment", 0),), 1)
@@ -234,7 +246,8 @@
     size = flat.shape[1]
     piece = -(-size // spread_n)
     flat = jnp.pad(flat, ((0, 0), (0, piece * spread_n - size))).reshape(layers * spread_n, piece)
-    part = lax.all_to_all(flat, ("segment", "gy"), 0, 0, tiled=True).sum(axis=0)
+    sent = lax.all_to_all(flat.astype(jnp.bfloat16), ("segment", "gy"), 0, 0, tiled=True)
+    part = sent.astype(jnp.float32).sum(axis=0)
     whole = lax.all_to_all(jnp.broadcast_to(part, (spread_n, piece)), "gy", 0, 0, tiled=True)
     flat = whole.reshape(-1)[:size][None]
     cut = planes.shape[1]

time: 246 us -> 254 us (1.033)
  waiting for transfers between devices: 89.2 us -> 94.2 us
  starting transfers between devices: 109 us -> 112 us
    ppermute x8, waiting for transfers between devices: 9.99 us -> 14.5 us  [passed_along(): return lax.ppermute(block, axis, route)]
where the time goes in v9:
time: 254 us; the launch traced here: 252 us
  starting transfers between devices  112 us (44%)
  waiting for transfers between devices  94.2 us (37%)
  matrix products  30 us (12%)
  local copies, waits for them, and re-layouts  10.7 us (4%)
  other arithmetic  3.54 us (1%)
    ppermute x10, starting transfers between devices, padded_2(): lax.ppermute(lax.slice_in_dim(block, block.shape[dim] - width, None, axis...  34.2 us
    ppermute x8, starting transfers between devices, passed_along(): return lax.ppermute(block, axis, route)  27.6 us
    ppermute x10, waiting for transfers between devices, padded_2(): lax.ppermute(lax.slice_in_dim(block, 0, width, axis=dim), axis, backward)  26.7 us
    all_to_all x1, waiting for transfers between devices, local(): lax.all_to_all(flat.astype(jnp.bfloat16), ('segment', 'gy'), 0, 0, tiled=...  22.4 us
    all_to_all x1, starting transfers between devices, local(): lax.all_to_all(flat.astype(jnp.bfloat16), ('segment', 'gy'), 0, 0, tiled=...  20.5 us
    all_to_all x1, waiting for transfers between devices, local(): got = lax.all_to_all(send, 'segment', 0, 0, tiled=True)  16.2 us
    dot_general x72, matrix products, plane_back(): jnp.einsum('oc,...yox->...ycx', kernel[i, j], padded[..., 2 - i:2 - i + h...  16.1 us
    ppermute x8, waiting for transfers between devices, passed_along(): return lax.ppermute(block, axis, route)  14.5 us
  transfers between devices with their start and end apart: 31, of which 22 were waited for; matrix products, arithmetic and copies ran while one was open for 6% of the time, Pallas kernels for 0%

profile of v9, /device:TPU:1, one launch (start us, length us, event | category | flops | bytes accessed | tf_op | source)
XLA Modules:
  0.0 252.4 jit_solution(1914664052114070120)
XLA Ops:
  2.5 1.8 pad_maximum_fusion
  4.3 10.9 %all-to-all-start = ((bf16[8,112,256]{2,1,0:T(8,128)(2,1)}), bf16[8,112,256]{2,1,0:T(8,128)(2,1)S(1)}, u32[]{:S(2)}, u32[]{:S(2)}) async-start(bf16[8,112,256]{2,1,0:T(8,128)(2,1)} %pad_maximum_fusion), calls=%async_computation | async-start | bytes 917504 | tf_op jit(solution)/shard_map/all_to_all | solution.py:147
  15.5 16.2 %all-to-all-done = bf16[8,112,256]{2,1,0:T(8,128)(2,1)S(1)} async-done(((bf16[8,112,256]{2,1,0:T(8,128)(2,1)}), bf16[8,112,256]{2,1,0:T(8,128)(2,1)S(1)}, u32[]{:S(2)}, u32[]{:S(2)}) %all-to-all-start) | async-done | bytes 458784 | tf_op jit(solution)/shard_map/all_to_all | solution.py:147
  31.7 2.5 collective-permute-start.1
  34.2 3.1 %collective-permute-start = (bf16[8,1,1,32,256]{4,3,2,0,1:T(8,128)(2,1)S(1)}, bf16[8,1,1,32,256]{4,3,2,0,1:T(8,128)(2,1)S(1)}, u32[]{:S(2)}, u32[]{:S(2)}) collective-permute-start(bf16[8,1,1,32,256]{4,3,2,0,1:T(8,128)(2,1)S(1)} %get-tuple-element.56), channel_id=1, source_target_pairs={{0,1},{1,2},{2,3},{3,4},{4,5},{5,6},{6,7},{7,8},{8,9},{9,10},{10,1... | collective-permute-start | bytes 393224 | tf_op jit(solution)/shard_map/ppermute | solution.py:17
  42.1 1.3 collective-permute-start.3
  43.4 4.0 %collective-permute-start.2 = (bf16[8,1,2,32,256]{4,3,2,0,1:T(8,128)(2,1)S(1)}, bf16[8,1,2,32,256]{4,3,2,0,1:T(8,128)(2,1)S(1)}, u32[]{:S(2)}, u32[]{:S(2)}) collective-permute-start(bf16[8,1,2,32,256]{4,3,2,0,1:T(8,128)(2,1)S(1)} %bitcast.1326), channel_id=1, source_target_pairs={{0,64},{64,128},{128,192},{192,256},{256,320},{320,384},{384,448},... | collective-permute-start | bytes 786440 | tf_op jit(solution)/shard_map/ppermute | solution.py:17
  48.3 3.5 %collective-permute-done.3 = bf16[8,1,2,32,256]{4,3,2,0,1:T(8,128)(2,1)S(1)} collective-permute-done((bf16[8,1,2,32,256]{4,3,2,0,1:T(8,128)(2,1)S(1)}, bf16[8,1,2,32,256]{4,3,2,0,1:T(8,128)(2,1)S(1)}, u32[]{:S(2)}, u32[]{:S(2)}) %collective-permute-start.3) | collective-permute-done | bytes 262176 | tf_op jit(solution)/shard_map/ppermute | solution.py:20
  52.1 1.3 collective-permute-done.2
  54.0 3.5 %collective-permute-start.5 = (bf16[1,16,32,256]{3,2,1,0:T(8,128)(2,1)S(1)}, bf16[1,16,32,256]{3,2,1,0:T(8,128)(2,1)S(1)}, u32[]{:S(2)}, u32[]{:S(2)}) collective-permute-start(bf16[1,16,32,256]{3,2,1,0:T(8,128)(2,1)S(1)} %get-tuple-element.80), channel_id=1, source_target_pairs={{0,1},{1,2},{2,3},{3,4},{4,5},{5,6},{6,7},{7,8},{8,9},{9,10},{10,1... | collective-permute-start | bytes 786440 | tf_op jit(solution)/shard_map/ppermute | solution.py:28
  57.6 3.2 %collective-permute-start.4 = (bf16[1,8,32,256]{3,2,1,0:T(8,128)(2,1)S(1)}, bf16[1,8,32,256]{3,2,1,0:T(8,128)(2,1)S(1)}, u32[]{:S(2)}, u32[]{:S(2)}) collective-permute-start(bf16[1,8,32,256]{3,2,1,0:T(8,128)(2,1)S(1)} %get-tuple-element.79), channel_id=1, source_target_pairs={{0,2},{1,3},{2,4},{3,5},{4,6},{5,7},{6,8},{7,9},{8,10},{9,11},{10,... | collective-permute-start | bytes 393224 | tf_op jit(solution)/shard_map/ppermute | solution.py:28
  60.9 2.7 %collective-permute-done.4 = bf16[1,8,32,256]{3,2,1,0:T(8,128)(2,1)S(1)} collective-permute-done((bf16[1,8,32,256]{3,2,1,0:T(8,128)(2,1)S(1)}, bf16[1,8,32,256]{3,2,1,0:T(8,128)(2,1)S(1)}, u32[]{:S(2)}, u32[]{:S(2)}) %collective-permute-start.4) | collective-permute-done | bytes 131104 | tf_op jit(solution)/shard_map/ppermute | solution.py:28
  63.8 1.9 collective-permute-start.6
  65.7 1.3 collective-permute-start.7
  67.1 6.8 %collective-permute-done.7 = bf16[1,8,32,256]{3,2,1,0:T(8,128)(2,1)S(1)} collective-permute-done((bf16[1,8,32,256]{3,2,1,0:T(8,128)(2,1)S(1)}, bf16[1,8,32,256]{3,2,1,0:T(8,128)(2,1)S(1)}, u32[]{:S(2)}, u32[]{:S(2)}) %collective-permute-start.7) | collective-permute-done | bytes 131104 | tf_op jit(solution)/shard_map/ppermute | solution.py:28
  74.1 4.1 %collective-permute-start.9 = (bf16[1,10,32,256]{3,2,1,0:T(8,128)(2,1)S(1)}, bf16[1,10,32,256]{3,2,1,0:T(8,128)(2,1)S(1)}, u32[]{:S(2)}, u32[]{:S(2)}) collective-permute-start(bf16[1,10,32,256]{3,2,1,0:T(8,128)(2,1)S(1)} %fusion.60), channel_id=1, source_target_pairs={{0,64},{64,128},{128,192},{192,256},{256,320},{320,384},{384,448},... | collective-permute-start | bytes 491528 | tf_op jit(solution)/shard_map/ppermute | solution.py:17
  78.2 1.3 collective-permute-start.8
  80.6 3.6 %collective-permute-done.8 = bf16[1,10,32,256]{3,2,1,0:T(8,128)(2,1)S(1)} collective-permute-done((bf16[1,10,32,256]{3,2,1,0:T(8,128)(2,1)S(1)}, bf16[1,10,32,256]{3,2,1,0:T(8,128)(2,1)S(1)}, u32[]{:S(2)}, u32[]{:S(2)}) %collective-permute-start.8) | collective-permute-done | bytes 163872 | tf_op jit(solution)/shard_map/ppermute | solution.py:20
  86.5 2.2 collective-permute-start.11
  88.7 1.3 collective-permute-start.10
  90.8 3.6 %collective-permute-done.10 = bf16[1,8,32,256]{3,2,1,0:T(8,128)(2,1)S(1)} collective-permute-done((bf16[1,8,32,256]{3,2,1,0:T(8,128)(2,1)S(1)}, bf16[1,8,32,256]{3,2,1,0:T(8,128)(2,1)S(1)}, u32[]{:S(2)}, u32[]{:S(2)}) %collective-permute-start.10) | collective-permute-done | bytes 131104 | tf_op jit(solution)/shard_map/ppermute | solution.py:20
  96.5 4.0 %collective-permute-start.13 = (bf16[1,6,32,256]{3,2,1,0:T(8,128)(2,1)S(1)}, bf16[1,6,32,256]{3,2,1,0:T(8,128)(2,1)S(1)}, u32[]{:S(2)}, u32[]{:S(2)}) collective-permute-start(bf16[1,6,32,256]{3,2,1,0:T(8,128)(2,1)S(1)} %get-tuple-element.91), channel_id=1, source_target_pairs={{0,64},{64,128},{128,192},{192,256},{256,320},{320,384},{384,448},... | collective-permute-start | bytes 294920 | tf_op jit(solution)/shard_map/ppermute | solution.py:17
  100.7 1.3 collective-permute-start.12
  102.4 3.7 %collective-permute-done.12 = bf16[1,6,32,256]{3,2,1,0:T(8,128)(2,1)S(1)} collective-permute-done((bf16[1,6,32,256]{3,2,1,0:T(8,128)(2,1)S(1)}, bf16[1,6,32,256]{3,2,1,0:T(8,128)(2,1)S(1)}, u32[]{:S(2)}, u32[]{:S(2)}) %collective-permute-start.12) | collective-permute-done | bytes 98336 | tf_op jit(solution)/shard_map/ppermute | solution.py:20
  108.1 3.7 %collective-permute-start.15 = (bf16[1,4,32,256]{3,2,1,0:T(8,128)(2,1)S(1)}, bf16[1,4,32,256]{3,2,1,0:T(8,128)(2,1)S(1)}, u32[]{:S(2)}, u32[]{:S(2)}) collective-permute-start(bf16[1,4,32,256]{3,2,1,0:T(8,128)(2,1)S(1)} %get-tuple-element.93), channel_id=1, source_target_pairs={{0,64},{64,128},{128,192},{192,256},{256,320},{320,384},{384,448},... | collective-permute-start | bytes 196616 | tf_op jit(solution)/shard_map/ppermute | solution.py:17
  111.9 1.3 collective-permute-start.14
  113.4 3.5 %collective-permute-done.14 = bf16[1,4,32,256]{3,2,1,0:T(8,128)(2,1)S(1)} collective-permute-done((bf16[1,4,32,256]{3,2,1,0:T(8,128)(2,1)S(1)}, bf16[1,4,32,256]{3,2,1,0:T(8,128)(2,1)S(1)}, u32[]{:S(2)}, u32[]{:S(2)}) %collective-permute-start.14) | collective-permute-done | bytes 65568 | tf_op jit(solution)/shard_map/ppermute | solution.py:20
  118.7 3.5 %collective-permute-start.16 = (bf16[1,2,32,256]{3,2,1,0:T(8,128)(2,1)S(1)}, bf16[1,2,32,256]{3,2,1,0:T(8,128)(2,1)S(1)}, u32[]{:S(2)}, u32[]{:S(2)}) collective-permute-start(bf16[1,2,32,256]{3,2,1,0:T(8,128)(2,1)S(1)} %fusion.49), channel_id=1, source_target_pairs={{0,2},{1,3},{2,4},{3,5},{4,6},{5,7},{6,8},{7,9},{8,10},{9,11},{10,... | collective-permute-start | bytes 98312 | tf_op jit(solution)/shard_map/ppermute | solution.py:28
  122.2 10.9 %collective-permute-start.17 = (bf16[1,2,32,256]{3,2,1,0:T(8,128)(2,1)S(1)}, bf16[1,2,32,256]{3,2,1,0:T(8,128)(2,1)S(1)}, u32[]{:S(2)}, u32[]{:S(2)}) collective-permute-start(bf16[1,2,32,256]{3,2,1,0:T(8,128)(2,1)S(1)} %fusion.49), channel_id=1, source_target_pairs={{0,1},{1,2},{2,3},{3,4},{4,5},{5,6},{6,7},{7,8},{8,9},{9,10},{10,1... | collective-permute-start | bytes 98312 | tf_op jit(solution)/shard_map/ppermute | solution.py:28
  133.1 1.9 collective-permute-start.18
  135.0 1.3 collective-permute-start.19
  136.4 1.9 collective-permute-done.18
  138.3 3.0 %collective-permute-done.19 = bf16[1,2,32,256]{3,2,1,0:T(8,128)(2,1)S(1)} collective-permute-done((bf16[1,2,32,256]{3,2,1,0:T(8,128)(2,1)S(1)}, bf16[1,2,32,256]{3,2,1,0:T(8,128)(2,1)S(1)}, u32[]{:S(2)}, u32[]{:S(2)}) %collective-permute-start.19) | collective-permute-done | bytes 32800 | tf_op jit(solution)/shard_map/ppermute | solution.py:28
  141.4 2.9 %collective-permute-start.21 = (bf16[1,10,32,256]{3,2,1,0:T(8,128)(2,1)S(1)}, bf16[1,10,32,256]{3,2,1,0:T(8,128)(2,1)S(1)}, u32[]{:S(2)}, u32[]{:S(2)}) collective-permute-start(bf16[1,10,32,256]{3,2,1,0:T(8,128)(2,1)S(1)} %fusion.62), channel_id=1, source_target_pairs={{0,64},{64,128},{128,192},{192,256},{256,320},{320,384},{384,448},... | collective-permute-start | bytes 491528 | tf_op jit(solution)/shard_map/ppermute | solution.py:17
  144.2 1.3 collective-permute-start.20
  145.8 2.3 collective-permute-done.21
  148.4 3.7 %collective-permute-done.20 = bf16[1,10,32,256]{3,2,1,0:T(8,128)(2,1)S(1)} collective-permute-done((bf16[1,10,32,256]{3,2,1,0:T(8,128)(2,1)S(1)}, bf16[1,10,32,256]{3,2,1,0:T(8,128)(2,1)S(1)}, u32[]{:S(2)}, u32[]{:S(2)}) %collective-permute-start.20) | collective-permute-done | bytes 163872 | tf_op jit(solution)/shard_map/ppermute | solution.py:20
  154.3 2.9 %collective-permute-start.23 = (bf16[1,8,32,256]{3,2,1,0:T(8,128)(2,1)S(1)}, bf16[1,8,32,256]{3,2,1,0:T(8,128)(2,1)S(1)}, u32[]{:S(2)}, u32[]{:S(2)}) collective-permute-start(bf16[1,8,32,256]{3,2,1,0:T(8,128)(2,1)S(1)} %get-tuple-element.95), channel_id=1, source_target_pairs={{0,64},{64,128},{128,192},{192,256},{256,320},{320,384},{384,448},... | collective-permute-start | bytes 393224 | tf_op jit(solution)/shard_map/ppermute | solution.py:17
  157.1 1.3 collective-permute-start.22
  159.5 3.4 %collective-permute-done.22 = bf16[1,8,32,256]{3,2,1,0:T(8,128)(2,1)S(1)} collective-permute-done((bf16[1,8,32,256]{3,2,1,0:T(8,128)(2,1)S(1)}, bf16[1,8,32,256]{3,2,1,0:T(8,128)(2,1)S(1)}, u32[]{:S(2)}, u32[]{:S(2)}) %collective-permute-start.22) | collective-permute-done | bytes 131104 | tf_op jit(solution)/shard_map/ppermute | solution.py:20
  165.0 3.5 %collective-permute-start.25 = (bf16[1,6,32,256]{3,2,1,0:T(8,128)(2,1)S(1)}, bf16[1,6,32,256]{3,2,1,0:T(8,128)(2,1)}, u32[]{:S(2)}, u32[]{:S(2)}) collective-permute-start(bf16[1,6,32,256]{3,2,1,0:T(8,128)(2,1)S(1)} %get-tuple-element.97), channel_id=1, source_target_pairs={{0,64},{64,128},{128,192},{192,256},{256,320},{320,384},{384,448},... | collective-permute-start | bytes 294920 | tf_op jit(solution)/shard_map/ppermute | solution.py:17
  168.7 1.5 collective-permute-start.24
  176.6 3.8 %collective-permute-start.27 = (bf16[1,4,32,256]{3,2,1,0:T(8,128)(2,1)}, bf16[1,4,32,256]{3,2,1,0:T(8,128)(2,1)}, u32[]{:S(2)}, u32[]{:S(2)}) collective-permute-start(bf16[1,4,32,256]{3,2,1,0:T(8,128)(2,1)} %get-tuple-element.99), channel_id=1, source_target_pairs={{0,64},{64,128},{128,192},{192,256},{256,320},{320,384},{384,448},... | collective-permute-start | bytes 196616 | tf_op jit(solution)/shard_map/ppermute | solution.py:17
  180.5 1.7 fusion.196
  192.1 20.5 %all-to-all-start.1 = ((bf16[512,1,192]{2,1,0:T(2,128)(2,1)}), bf16[512,1,192]{2,1,0:T(2,128)(2,1)S(1)}, u32[]{:S(2)}, u32[]{:S(2)}) async-start(bf16[512,1,192]{2,1,0:T(2,128)(2,1)} %convert_element_type.456), calls=%async_computation.1 | async-start | bytes 1048576 | tf_op jit(solution)/shard_map/all_to_all | solution.py:249
  212.9 22.4 %all-to-all-done.1 = bf16[512,1,192]{2,1,0:T(2,128)(2,1)S(1)} async-done(((bf16[512,1,192]{2,1,0:T(2,128)(2,1)}), bf16[512,1,192]{2,1,0:T(2,128)(2,1)S(1)}, u32[]{:S(2)}, u32[]{:S(2)}) %all-to-all-start.1) | async-done | bytes 196640 | tf_op jit(solution)/shard_map/all_to_all | solution.py:249
  236.6 4.2 %all-to-all-start.2 = ((f32[64,1,192]{2,1,0:T(1,128)}), f32[64,1,192]{2,1,0:T(1,128)S(1)}, u32[]{:S(2)}, u32[]{:S(2)}) async-start(f32[64,1,192]{2,1,0:T(1,128)} %broadcast_in_dim.21), calls=%async_computation.2 | async-start | bytes 131072 | tf_op jit(solution)/shard_map/all_to_all | solution.py:251
  241.6 9.0 %all-to-all-done.2 = f32[64,1,192]{2,1,0:T(1,128)S(1)} async-done(((f32[64,1,192]{2,1,0:T(1,128)}), f32[64,1,192]{2,1,0:T(1,128)S(1)}, u32[]{:S(2)}, u32[]{:S(2)}) %all-to-all-start.2) | async-done | bytes 49184 | tf_op jit(solution)/shard_map/all_to_all | solution.py:251
  (285 shorter events, 45.5 us)
Async XLA Ops:
  0.6 14.5 %copy-start.11 = (s32[1,12]{1,0:T(1,128)S(1)}, s32[1,12]{1,0:T(1,128)}, u32[]{:S(2)}) copy-start(s32[1,12]{1,0:T(1,128)} %param.9) | copy-start | bytes 148
  4.3 27.3 %all-to-all-start = ((bf16[8,112,256]{2,1,0:T(8,128)(2,1)}), bf16[8,112,256]{2,1,0:T(8,128)(2,1)S(1)}, u32[]{:S(2)}, u32[]{:S(2)}) async-start(bf16[8,112,256]{2,1,0:T(8,128)(2,1)} %pad_maximum_fusion), calls=%async_computation | async-start | bytes 917504 | tf_op jit(solution)/shard_map/all_to_all | solution.py:147
  31.7 7.7 %collective-permute-start.1 = (bf16[8,1,1,32,256]{4,3,2,0,1:T(8,128)(2,1)S(1)}, bf16[8,1,1,32,256]{4,3,2,0,1:T(8,128)(2,1)S(1)}, u32[]{:S(2)}, u32[]{:S(2)}) collective-permute-start(bf16[8,1,1,32,256]{4,3,2,0,1:T(8,128)(2,1)S(1)} %get-tuple-element.57), channel_id=1, source_target_pairs={{1,0},{2,1},{3,2},{4,3},{5,4},{6,5},{7,6},{8,7},{9,8},{10,9},{11,1... | collective-permute-start | bytes 393224 | tf_op jit(solution)/shard_map/ppermute | solution.py:20
  34.2 5.2 %collective-permute-start = (bf16[8,1,1,32,256]{4,3,2,0,1:T(8,128)(2,1)S(1)}, bf16[8,1,1,32,256]{4,3,2,0,1:T(8,128)(2,1)S(1)}, u32[]{:S(2)}, u32[]{:S(2)}) collective-permute-start(bf16[8,1,1,32,256]{4,3,2,0,1:T(8,128)(2,1)S(1)} %get-tuple-element.56), channel_id=1, source_target_pairs={{0,1},{1,2},{2,3},{3,4},{4,5},{5,6},{6,7},{7,8},{8,9},{9,10},{10,1... | collective-permute-start | bytes 393224 | tf_op jit(solution)/shard_map/ppermute | solution.py:17
  42.1 9.8 %collective-permute-start.3 = (bf16[8,1,2,32,256]{4,3,2,0,1:T(8,128)(2,1)S(1)}, bf16[8,1,2,32,256]{4,3,2,0,1:T(8,128)(2,1)S(1)}, u32[]{:S(2)}, u32[]{:S(2)}) collective-permute-start(bf16[8,1,2,32,256]{4,3,2,0,1:T(8,128)(2,1)S(1)} %bitcast.1325), channel_id=1, source_target_pairs={{64,0},{128,64},{192,128},{256,192},{320,256},{384,320},{448,384},... | collective-permute-start | bytes 786440 | tf_op jit(solution)/shard_map/ppermute | solution.py:20
  43.4 10.0 %collective-permute-start.2 = (bf16[8,1,2,32,256]{4,3,2,0,1:T(8,128)(2,1)S(1)}, bf16[8,1,2,32,256]{4,3,2,0,1:T(8,128)(2,1)S(1)}, u32[]{:S(2)}, u32[]{:S(2)}) collective-permute-start(bf16[8,1,2,32,256]{4,3,2,0,1:T(8,128)(2,1)S(1)} %bitcast.1326), channel_id=1, source_target_pairs={{0,64},{64,128},{128,192},{192,256},{256,320},{320,384},{384,448},... | collective-permute-start | bytes 786440 | tf_op jit(solution)/shard_map/ppermute | solution.py:17
  48.0 5.8 %copy-start = (bf16[7,1,2,288,256]{4,3,2,0,1:T(8,128)(2,1)}, bf16[7,1,2,288,256]{4,3,2,0,1:T(8,128)(2,1)S(1)}, u32[]{:S(2)}) copy-start(bf16[7,1,2,288,256]{4,3,2,0,1:T(8,128)(2,1)S(1)} %slice_dynamic-update-slice_fusion) | copy-start | bytes 6193156
  48.3 3.8 %copy-start.5 = (bf16[1,1,2,288,256]{4,3,2,0,1:T(8,128)(2,1)}, bf16[1,1,2,288,256]{4,3,2,0,1:T(8,128)(2,1)S(1)}, u32[]{:S(2)}) copy-start(bf16[1,1,2,288,256]{4,3,2,0,1:T(8,128)(2,1)S(1)} %constant_dynamic-update-slice_fusion.48) | copy-start | bytes 884740
  51.9 9.0 %copy-start.2 = (bf16[8,1,2,32,256]{4,3,2,0,1:T(8,128)(2,1)}, bf16[8,1,2,32,256]{4,3,2,0,1:T(8,128)(2,1)S(1)}, u32[]{:S(2)}) copy-start(bf16[8,1,2,32,256]{4,3,2,0,1:T(8,128)(2,1)S(1)} %collective-permute-done.3) | copy-start | bytes 786436
  52.1 1.9 copy-start.7
  53.4 7.5 %copy-start.9 = (bf16[8,1,2,32,256]{4,3,2,0,1:T(8,128)(2,1)}, bf16[8,1,2,32,256]{4,3,2,0,1:T(8,128)(2,1)S(1)}, u32[]{:S(2)}) copy-start(bf16[8,1,2,32,256]{4,3,2,0,1:T(8,128)(2,1)S(1)} %collective-permute-done.2) | copy-start | bytes 786436
  54.0 9.7 %collective-permute-start.5 = (bf16[1,16,32,256]{3,2,1,0:T(8,128)(2,1)S(1)}, bf16[1,16,32,256]{3,2,1,0:T(8,128)(2,1)S(1)}, u32[]{:S(2)}, u32[]{:S(2)}) collective-permute-start(bf16[1,16,32,256]{3,2,1,0:T(8,128)(2,1)S(1)} %get-tuple-element.80), channel_id=1, source_target_pairs={{0,1},{1,2},{2,3},{3,4},{4,5},{5,6},{6,7},{7,8},{8,9},{9,10},{10,1... | collective-permute-start | bytes 786440 | tf_op jit(solution)/shard_map/ppermute | solution.py:28
  57.6 6.1 %collective-permute-start.4 = (bf16[1,8,32,256]{3,2,1,0:T(8,128)(2,1)S(1)}, bf16[1,8,32,256]{3,2,1,0:T(8,128)(2,1)S(1)}, u32[]{:S(2)}, u32[]{:S(2)}) collective-permute-start(bf16[1,8,32,256]{3,2,1,0:T(8,128)(2,1)S(1)} %get-tuple-element.79), channel_id=1, source_target_pairs={{0,2},{1,3},{2,4},{3,5},{4,6},{5,7},{6,8},{7,9},{8,10},{9,11},{10,... | collective-permute-start | bytes 393224 | tf_op jit(solution)/shard_map/ppermute | solution.py:28
  63.8 10.2 %collective-permute-start.6 = (bf16[1,16,32,256]{3,2,1,0:T(8,128)(2,1)S(1)}, bf16[1,16,32,256]{3,2,1,0:T(8,128)(2,1)S(1)}, u32[]{:S(2)}, u32[]{:S(2)}) collective-permute-start(bf16[1,16,32,256]{3,2,1,0:T(8,128)(2,1)S(1)} %get-tuple-element.78), channel_id=1, source_target_pairs={{1,0},{2,1},{3,2},{4,3},{5,4},{6,5},{7,6},{8,7},{9,8},{10,9},{11,1... | collective-permute-start | bytes 786440 | tf_op jit(solution)/shard_map/ppermute | solution.py:28
  65.7 8.2 %collective-permute-start.7 = (bf16[1,8,32,256]{3,2,1,0:T(8,128)(2,1)S(1)}, bf16[1,8,32,256]{3,2,1,0:T(8,128)(2,1)S(1)}, u32[]{:S(2)}, u32[]{:S(2)}) collective-permute-start(bf16[1,8,32,256]{3,2,1,0:T(8,128)(2,1)S(1)} %get-tuple-element.77), channel_id=1, source_target_pairs={{2,0},{3,1},{4,2},{5,3},{6,4},{7,5},{8,6},{9,7},{10,8},{11,9},{12,... | collective-permute-start | bytes 393224 | tf_op jit(solution)/shard_map/ppermute | solution.py:28
  74.1 6.4 %collective-permute-start.9 = (bf16[1,10,32,256]{3,2,1,0:T(8,128)(2,1)S(1)}, bf16[1,10,32,256]{3,2,1,0:T(8,128)(2,1)S(1)}, u32[]{:S(2)}, u32[]{:S(2)}) collective-permute-start(bf16[1,10,32,256]{3,2,1,0:T(8,128)(2,1)S(1)} %fusion.60), channel_id=1, source_target_pairs={{0,64},{64,128},{128,192},{192,256},{256,320},{320,384},{384,448},... | collective-permute-start | bytes 491528 | tf_op jit(solution)/shard_map/ppermute | solution.py:17
  78.2 6.1 %collective-permute-start.8 = (bf16[1,10,32,256]{3,2,1,0:T(8,128)(2,1)S(1)}, bf16[1,10,32,256]{3,2,1,0:T(8,128)(2,1)S(1)}, u32[]{:S(2)}, u32[]{:S(2)}) collective-permute-start(bf16[1,10,32,256]{3,2,1,0:T(8,128)(2,1)S(1)} %fusion.60), channel_id=1, source_target_pairs={{64,0},{128,64},{192,128},{256,192},{320,256},{384,320},{448,384},... | collective-permute-start | bytes 491528 | tf_op jit(solution)/shard_map/ppermute | solution.py:20
  86.5 4.1 %collective-permute-start.11 = (bf16[1,8,32,256]{3,2,1,0:T(8,128)(2,1)S(1)}, bf16[1,8,32,256]{3,2,1,0:T(8,128)(2,1)S(1)}, u32[]{:S(2)}, u32[]{:S(2)}) collective-permute-start(bf16[1,8,32,256]{3,2,1,0:T(8,128)(2,1)S(1)} %get-tuple-element.89), channel_id=1, source_target_pairs={{0,64},{64,128},{128,192},{192,256},{256,320},{320,384},{384,448},... | collective-permute-start | bytes 393224 | tf_op jit(solution)/shard_map/ppermute | solution.py:17
  88.7 5.7 %collective-permute-start.10 = (bf16[1,8,32,256]{3,2,1,0:T(8,128)(2,1)S(1)}, bf16[1,8,32,256]{3,2,1,0:T(8,128)(2,1)S(1)}, u32[]{:S(2)}, u32[]{:S(2)}) collective-permute-start(bf16[1,8,32,256]{3,2,1,0:T(8,128)(2,1)S(1)} %get-tuple-element.89), channel_id=1, source_target_pairs={{64,0},{128,64},{192,128},{256,192},{320,256},{384,320},{448,384},... | collective-permute-start | bytes 393224 | tf_op jit(solution)/shard_map/ppermute | solution.py:20
  96.5 5.7 %collective-permute-start.13 = (bf16[1,6,32,256]{3,2,1,0:T(8,128)(2,1)S(1)}, bf16[1,6,32,256]{3,2,1,0:T(8,128)(2,1)S(1)}, u32[]{:S(2)}, u32[]{:S(2)}) collective-permute-start(bf16[1,6,32,256]{3,2,1,0:T(8,128)(2,1)S(1)} %get-tuple-element.91), channel_id=1, source_target_pairs={{0,64},{64,128},{128,192},{192,256},{256,320},{320,384},{384,448},... | collective-permute-start | bytes 294920 | tf_op jit(solution)/shard_map/ppermute | solution.py:17
  100.7 5.4 %collective-permute-start.12 = (bf16[1,6,32,256]{3,2,1,0:T(8,128)(2,1)S(1)}, bf16[1,6,32,256]{3,2,1,0:T(8,128)(2,1)S(1)}, u32[]{:S(2)}, u32[]{:S(2)}) collective-permute-start(bf16[1,6,32,256]{3,2,1,0:T(8,128)(2,1)S(1)} %get-tuple-element.91), channel_id=1, source_target_pairs={{64,0},{128,64},{192,128},{256,192},{320,256},{384,320},{448,384},... | collective-permute-start | bytes 294920 | tf_op jit(solution)/shard_map/ppermute | solution.py:20
  108.1 5.1 %collective-permute-start.15 = (bf16[1,4,32,256]{3,2,1,0:T(8,128)(2,1)S(1)}, bf16[1,4,32,256]{3,2,1,0:T(8,128)(2,1)S(1)}, u32[]{:S(2)}, u32[]{:S(2)}) collective-permute-start(bf16[1,4,32,256]{3,2,1,0:T(8,128)(2,1)S(1)} %get-tuple-element.93), channel_id=1, source_target_pairs={{0,64},{64,128},{128,192},{192,256},{256,320},{320,384},{384,448},... | collective-permute-start | bytes 196616 | tf_op jit(solution)/shard_map/ppermute | solution.py:17
  111.9 5.0 %collective-permute-start.14 = (bf16[1,4,32,256]{3,2,1,0:T(8,128)(2,1)S(1)}, bf16[1,4,32,256]{3,2,1,0:T(8,128)(2,1)S(1)}, u32[]{:S(2)}, u32[]{:S(2)}) collective-permute-start(bf16[1,4,32,256]{3,2,1,0:T(8,128)(2,1)S(1)} %get-tuple-element.93), channel_id=1, source_target_pairs={{64,0},{128,64},{192,128},{256,192},{320,256},{384,320},{448,384},... | collective-permute-start | bytes 196616 | tf_op jit(solution)/shard_map/ppermute | solution.py:20
  118.7 17.6 %collective-permute-start.16 = (bf16[1,2,32,256]{3,2,1,0:T(8,128)(2,1)S(1)}, bf16[1,2,32,256]{3,2,1,0:T(8,128)(2,1)S(1)}, u32[]{:S(2)}, u32[]{:S(2)}) collective-permute-start(bf16[1,2,32,256]{3,2,1,0:T(8,128)(2,1)S(1)} %fusion.49), channel_id=1, source_target_pairs={{0,2},{1,3},{2,4},{3,5},{4,6},{5,7},{6,8},{7,9},{8,10},{9,11},{10,... | collective-permute-start | bytes 98312 | tf_op jit(solution)/shard_map/ppermute | solution.py:28
  122.2 14.1 %collective-permute-start.17 = (bf16[1,2,32,256]{3,2,1,0:T(8,128)(2,1)S(1)}, bf16[1,2,32,256]{3,2,1,0:T(8,128)(2,1)S(1)}, u32[]{:S(2)}, u32[]{:S(2)}) collective-permute-start(bf16[1,2,32,256]{3,2,1,0:T(8,128)(2,1)S(1)} %fusion.49), channel_id=1, source_target_pairs={{0,1},{1,2},{2,3},{3,4},{4,5},{5,6},{6,7},{7,8},{8,9},{9,10},{10,1... | collective-permute-start | bytes 98312 | tf_op jit(solution)/shard_map/ppermute | solution.py:28
  133.1 5.2 %collective-permute-start.18 = (bf16[1,2,32,256]{3,2,1,0:T(8,128)(2,1)S(1)}, bf16[1,2,32,256]{3,2,1,0:T(8,128)(2,1)S(1)}, u32[]{:S(2)}, u32[]{:S(2)}) collective-permute-start(bf16[1,2,32,256]{3,2,1,0:T(8,128)(2,1)S(1)} %fusion.49), channel_id=1, source_target_pairs={{1,0},{2,1},{3,2},{4,3},{5,4},{6,5},{7,6},{8,7},{9,8},{10,9},{11,1... | collective-permute-start | bytes 98312 | tf_op jit(solution)/shard_map/ppermute | solution.py:28
  135.0 6.3 %collective-permute-start.19 = (bf16[1,2,32,256]{3,2,1,0:T(8,128)(2,1)S(1)}, bf16[1,2,32,256]{3,2,1,0:T(8,128)(2,1)S(1)}, u32[]{:S(2)}, u32[]{:S(2)}) collective-permute-start(bf16[1,2,32,256]{3,2,1,0:T(8,128)(2,1)S(1)} %fusion.49), channel_id=1, source_target_pairs={{2,0},{3,1},{4,2},{5,3},{6,4},{7,5},{8,6},{9,7},{10,8},{11,9},{12,... | collective-permute-start | bytes 98312 | tf_op jit(solution)/shard_map/ppermute | solution.py:28
  141.4 6.8 %collective-permute-start.21 = (bf16[1,10,32,256]{3,2,1,0:T(8,128)(2,1)S(1)}, bf16[1,10,32,256]{3,2,1,0:T(8,128)(2,1)S(1)}, u32[]{:S(2)}, u32[]{:S(2)}) collective-permute-start(bf16[1,10,32,256]{3,2,1,0:T(8,128)(2,1)S(1)} %fusion.62), channel_id=1, source_target_pairs={{0,64},{64,128},{128,192},{192,256},{256,320},{320,384},{384,448},... | collective-permute-start | bytes 491528 | tf_op jit(solution)/shard_map/ppermute | solution.py:17
  144.2 7.8 %collective-permute-start.20 = (bf16[1,10,32,256]{3,2,1,0:T(8,128)(2,1)S(1)}, bf16[1,10,32,256]{3,2,1,0:T(8,128)(2,1)S(1)}, u32[]{:S(2)}, u32[]{:S(2)}) collective-permute-start(bf16[1,10,32,256]{3,2,1,0:T(8,128)(2,1)S(1)} %fusion.62), channel_id=1, source_target_pairs={{64,0},{128,64},{192,128},{256,192},{320,256},{384,320},{448,384},... | collective-permute-start | bytes 491528 | tf_op jit(solution)/shard_map/ppermute | solution.py:20
  154.3 5.0 %collective-permute-start.23 = (bf16[1,8,32,256]{3,2,1,0:T(8,128)(2,1)S(1)}, bf16[1,8,32,256]{3,2,1,0:T(8,128)(2,1)S(1)}, u32[]{:S(2)}, u32[]{:S(2)}) collective-permute-start(bf16[1,8,32,256]{3,2,1,0:T(8,128)(2,1)S(1)} %get-tuple-element.95), channel_id=1, source_target_pairs={{0,64},{64,128},{128,192},{192,256},{256,320},{320,384},{384,448},... | collective-permute-start | bytes 393224 | tf_op jit(solution)/shard_map/ppermute | solution.py:17
  157.1 5.7 %collective-permute-start.22 = (bf16[1,8,32,256]{3,2,1,0:T(8,128)(2,1)S(1)}, bf16[1,8,32,256]{3,2,1,0:T(8,128)(2,1)S(1)}, u32[]{:S(2)}, u32[]{:S(2)}) collective-permute-start(bf16[1,8,32,256]{3,2,1,0:T(8,128)(2,1)S(1)} %get-tuple-element.95), channel_id=1, source_target_pairs={{64,0},{128,64},{192,128},{256,192},{320,256},{384,320},{448,384},... | collective-permute-start | bytes 393224 | tf_op jit(solution)/shard_map/ppermute | solution.py:20
  163.7 6.6 %slice-start = ((bf16[8,1,2,32,256]{4,3,2,0,1:T(8,128)(2,1)}), bf16[7,1,2,32,256]{4,3,2,0,1:T(8,128)(2,1)S(1)}, s32[]{:S(2)}) async-start(bf16[8,1,2,32,256]{4,3,2,0,1:T(8,128)(2,1)} %copy-done.2), calls=%async_computation.3 | async-start | bytes 458752 | tf_op jit(solution)/shard_map/slice | solution.py:235
  163.7 6.6 %slice-start.1 = ((bf16[8,1,2,32,256]{4,3,2,0,1:T(8,128)(2,1)}), bf16[7,1,2,32,256]{4,3,2,0,1:T(8,128)(2,1)S(1)}, s32[]{:S(2)}) async-start(bf16[8,1,2,32,256]{4,3,2,0,1:T(8,128)(2,1)} %copy-done.9), calls=%async_computation.4 | async-start | bytes 458752 | tf_op jit(solution)/shard_map/slice | solution.py:235
  165.0 6.7 %collective-permute-start.25 = (bf16[1,6,32,256]{3,2,1,0:T(8,128)(2,1)S(1)}, bf16[1,6,32,256]{3,2,1,0:T(8,128)(2,1)}, u32[]{:S(2)}, u32[]{:S(2)}) collective-permute-start(bf16[1,6,32,256]{3,2,1,0:T(8,128)(2,1)S(1)} %get-tuple-element.97), channel_id=1, source_target_pairs={{0,64},{64,128},{128,192},{192,256},{256,320},{320,384},{384,448},... | collective-permute-start | bytes 294920 | tf_op jit(solution)/shard_map/ppermute | solution.py:17
  168.7 5.4 %collective-permute-start.24 = (bf16[1,6,32,256]{3,2,1,0:T(8,128)(2,1)S(1)}, bf16[1,6,32,256]{3,2,1,0:T(8,128)(2,1)S(1)}, u32[]{:S(2)}, u32[]{:S(2)}) collective-permute-start(bf16[1,6,32,256]{3,2,1,0:T(8,128)(2,1)S(1)} %get-tuple-element.97), channel_id=1, source_target_pairs={{64,0},{128,64},{192,128},{256,192},{320,256},{384,320},{448,384},... | collective-permute-start | bytes 294920 | tf_op jit(solution)/shard_map/ppermute | solution.py:20
  174.2 9.3 %copy-start.1 = (bf16[7,1,2,288,256]{4,3,2,0,1:T(8,128)(2,1)S(1)}, bf16[7,1,2,288,256]{4,3,2,0,1:T(8,128)(2,1)}, u32[]{:S(2)}) copy-start(bf16[7,1,2,288,256]{4,3,2,0,1:T(8,128)(2,1)} %copy-done) | copy-start | bytes 6193156
  176.6 9.5 %collective-permute-start.27 = (bf16[1,4,32,256]{3,2,1,0:T(8,128)(2,1)}, bf16[1,4,32,256]{3,2,1,0:T(8,128)(2,1)}, u32[]{:S(2)}, u32[]{:S(2)}) collective-permute-start(bf16[1,4,32,256]{3,2,1,0:T(8,128)(2,1)} %get-tuple-element.99), channel_id=1, source_target_pairs={{0,64},{64,128},{128,192},{192,256},{256,320},{320,384},{384,448},... | collective-permute-start | bytes 196616 | tf_op jit(solution)/shard_map/ppermute | solution.py:17
  182.2 5.3 %collective-permute-start.26 = (bf16[1,4,32,256]{3,2,1,0:T(8,128)(2,1)}, bf16[1,4,32,256]{3,2,1,0:T(8,128)(2,1)}, u32[]{:S(2)}, u32[]{:S(2)}) collective-permute-start(bf16[1,4,32,256]{3,2,1,0:T(8,128)(2,1)} %get-tuple-element.99), channel_id=1, source_target_pairs={{64,0},{128,64},{192,128},{256,192},{320,256},{384,320},{448,384},... | collective-permute-start | bytes 196616 | tf_op jit(solution)/shard_map/ppermute | solution.py:20
  184.2 3.3 %copy-start.3 = (f32[4,256,32]{1,2,0:T(8,128)S(1)}, f32[4,256,32]{1,2,0:T(8,128)}, u32[]{:S(2)}) copy-start(f32[4,256,32]{1,2,0:T(8,128)} %fusion.196) | copy-start | bytes 393220
  185.6 3.8 %copy-start.8 = (bf16[1,9,32,32]{2,3,1,0:T(8,128)(2,1)S(1)}, bf16[1,9,32,32]{2,3,1,0:T(8,128)(2,1)}, u32[]{:S(2)}) copy-start(bf16[1,9,32,32]{2,3,1,0:T(8,128)(2,1)} %copy.256) | copy-start | bytes 55300
  185.6 4.6 %copy-start.6 = (bf16[1,1,2,288,256]{4,3,2,0,1:T(8,128)(2,1)S(1)}, bf16[1,1,2,288,256]{4,3,2,0,1:T(8,128)(2,1)}, u32[]{:S(2)}) copy-start(bf16[1,1,2,288,256]{4,3,2,0,1:T(8,128)(2,1)} %copy-done.5) | copy-start | bytes 884740
  185.6 5.1 %copy-start.4 = (f32[7,3072]{1,0:T(8,128)S(1)}, f32[7,3072]{1,0:T(8,128)}, u32[]{:S(2)}) copy-start(f32[7,3072]{1,0:T(8,128)} %reshape.1339) | copy-start | bytes 258052
  190.3 50.5 %copy-start.10 = (bf16[1,4,32,256]{3,2,1,0:T(8,128)(2,1)S(1)}, bf16[1,4,32,256]{3,2,1,0:T(8,128)(2,1)}, u32[]{:S(2)}) copy-start(bf16[1,4,32,256]{3,2,1,0:T(8,128)(2,1)} %get-tuple-element.100) | copy-start | bytes 196612
  192.1 43.2 %all-to-all-start.1 = ((bf16[512,1,192]{2,1,0:T(2,128)(2,1)}), bf16[512,1,192]{2,1,0:T(2,128)(2,1)S(1)}, u32[]{:S(2)}, u32[]{:S(2)}) async-start(bf16[512,1,192]{2,1,0:T(2,128)(2,1)} %convert_element_type.456), calls=%async_computation.1 | async-start | bytes 1048576 | tf_op jit(solution)/shard_map/all_to_all | solution.py:249
  236.6 14.0 %all-to-all-start.2 = ((f32[64,1,192]{2,1,0:T(1,128)}), f32[64,1,192]{2,1,0:T(1,128)S(1)}, u32[]{:S(2)}, u32[]{:S(2)}) async-start(f32[64,1,192]{2,1,0:T(1,128)} %broadcast_in_dim.21), calls=%async_computation.2 | async-start | bytes 131072 | tf_op jit(solution)/shard_map/all_to_all | solution.py:251

commit v10 on v7

--- a/solution.py
+++ b/solution.py
@@ -233,8 +233,10 @@
     spread_n = lax.axis_size("gy")
     size = flat.shape[1]
     piece = -(-size // spread_n)
-    flat = jnp.pad(flat, ((0, 0), (0, piece * spread_n - size))).reshape(layers * spread_n, piece)
-    part = lax.all_to_all(flat, ("segment", "gy"), 0, 0, tiled=True).sum(axis=0)
+    flat = jnp.pad(flat, ((0, 0), (0, piece * spread_n - size)))
+    flat = flat.reshape(layers, spread_n, piece).transpose(1, 0, 2)
+    part = lax.all_to_all(flat, "gy", 0, 0, tiled=True).sum(axis=0)
+    part = lax.all_to_all(part, "segment", 0, 0, tiled=True).sum(axis=0)
     whole = lax.all_to_all(jnp.broadcast_to(part, (spread_n, piece)), "gy", 0, 0, tiled=True)
     flat = whole.reshape(-1)[:size][None]
     cut = planes.shape[1]

time: 246 us -> 251 us (1.020)
  starting transfers between devices: 109 us -> 112 us
    all_to_all x1, starting transfers between devices: 4.18 us -> 7.71 us  [local(): lax.all_to_all(jnp.broadcast_to(part, (spread_n, piece)), 'gy', 0, 0, til...]
    all_to_all x1 -> x2, waiting for transfers between devices: 22.1 us -> 23 us  [the longest x1 16.6 us: local(): part = lax.all_to_all(flat, 'gy', 0, 0, tiled=True).sum(axis=0)]
    all_to_all x1 -> x2, starting transfers between devices: 20 us -> 19.5 us  [the longest x1 15.7 us: local(): part = lax.all_to_all(flat, 'gy', 0, 0, tiled=True).sum(axis=0)]
  transfers between devices with their start and end apart: 31 -> 32, of which waited for: 22 -> 23; matrix products, arithmetic and copies ran while one was open for 6% -> 6% of each run, Pallas kernels for 0% -> 0%
where the time goes in v10:
time: 251 us; the launch traced here: 249 us
  starting transfers between devices  112 us (45%)
  waiting for transfers between devices  90.1 us (36%)
  matrix products  30 us (12%)
  local copies, waits for them, and re-layouts  11.4 us (5%)
  other arithmetic  3.08 us (1%)
    ppermute x10, starting transfers between devices, padded_2(): lax.ppermute(lax.slice_in_dim(block, block.shape[dim] - width, None, axis...  34.2 us
    ppermute x10, waiting for transfers between devices, padded_2(): lax.ppermute(lax.slice_in_dim(block, 0, width, axis=dim), axis, backward)  26.9 us
    ppermute x8, starting transfers between devices, passed_along(): return lax.ppermute(block, axis, route)  25.8 us
    all_to_all x1, waiting for transfers between devices, local(): part = lax.all_to_all(flat, 'gy', 0, 0, tiled=True).sum(axis=0)  16.6 us
    all_to_all x1, waiting for transfers between devices, local(): got = lax.all_to_all(send, 'segment', 0, 0, tiled=True)  16.2 us
    dot_general x72, matrix products, plane_back(): jnp.einsum('oc,...yox->...ycx', kernel[i, j], padded[..., 2 - i:2 - i + h...  16.1 us
    all_to_all x1, starting transfers between devices, local(): part = lax.all_to_all(flat, 'gy', 0, 0, tiled=True).sum(axis=0)  15.7 us
    ppermute x10, starting transfers between devices, padded_2(): lax.ppermute(lax.slice_in_dim(block, 0, width, axis=dim), axis, backward)  14.3 us
  transfers between devices with their start and end apart: 32, of which 23 were waited for; matrix products, arithmetic and copies ran while one was open for 6% of the time, Pallas kernels for 0%

profile of v10, /device:TPU:1, one launch (start us, length us, event | category | flops | bytes accessed | tf_op | source)
XLA Modules:
  0.0 249.3 jit_solution(15812861116836803385)
XLA Ops:
  2.5 1.8 pad_maximum_fusion
  4.3 10.9 %all-to-all-start = ((bf16[8,112,256]{2,1,0:T(8,128)(2,1)}), bf16[8,112,256]{2,1,0:T(8,128)(2,1)S(1)}, u32[]{:S(2)}, u32[]{:S(2)}) async-start(bf16[8,112,256]{2,1,0:T(8,128)(2,1)} %pad_maximum_fusion), calls=%async_computation | async-start | bytes 917504 | tf_op jit(solution)/shard_map/all_to_all | solution.py:147
  15.4 16.2 %all-to-all-done = bf16[8,112,256]{2,1,0:T(8,128)(2,1)S(1)} async-done(((bf16[8,112,256]{2,1,0:T(8,128)(2,1)}), bf16[8,112,256]{2,1,0:T(8,128)(2,1)S(1)}, u32[]{:S(2)}, u32[]{:S(2)}) %all-to-all-start) | async-done | bytes 458784 | tf_op jit(solution)/shard_map/all_to_all | solution.py:147
  31.7 2.5 %collective-permute-start.1 = (bf16[8,1,1,32,256]{4,3,2,0,1:T(8,128)(2,1)S(1)}, bf16[8,1,1,32,256]{4,3,2,0,1:T(8,128)(2,1)S(1)}, u32[]{:S(2)}, u32[]{:S(2)}) collective-permute-start(bf16[8,1,1,32,256]{4,3,2,0,1:T(8,128)(2,1)S(1)} %get-tuple-element.39), channel_id=1, source_target_pairs={{1,0},{2,1},{3,2},{4,3},{5,4},{6,5},{7,6},{8,7},{9,8},{10,9},{11,1... | collective-permute-start | bytes 393224 | tf_op jit(solution)/shard_map/ppermute | solution.py:20
  34.2 3.1 %collective-permute-start = (bf16[8,1,1,32,256]{4,3,2,0,1:T(8,128)(2,1)S(1)}, bf16[8,1,1,32,256]{4,3,2,0,1:T(8,128)(2,1)S(1)}, u32[]{:S(2)}, u32[]{:S(2)}) collective-permute-start(bf16[8,1,1,32,256]{4,3,2,0,1:T(8,128)(2,1)S(1)} %get-tuple-element.38), channel_id=1, source_target_pairs={{0,1},{1,2},{2,3},{3,4},{4,5},{5,6},{6,7},{7,8},{8,9},{9,10},{10,1... | collective-permute-start | bytes 393224 | tf_op jit(solution)/shard_map/ppermute | solution.py:17
  42.1 1.3 collective-permute-start.3
  43.4 4.0 %collective-permute-start.2 = (bf16[8,1,2,32,256]{4,3,2,0,1:T(8,128)(2,1)S(1)}, bf16[8,1,2,32,256]{4,3,2,0,1:T(8,128)(2,1)S(1)}, u32[]{:S(2)}, u32[]{:S(2)}) collective-permute-start(bf16[8,1,2,32,256]{4,3,2,0,1:T(8,128)(2,1)S(1)} %bitcast.1334), channel_id=1, source_target_pairs={{0,64},{64,128},{128,192},{192,256},{256,320},{320,384},{384,448},... | collective-permute-start | bytes 786440 | tf_op jit(solution)/shard_map/ppermute | solution.py:17
  48.3 3.5 %collective-permute-done.3 = bf16[8,1,2,32,256]{4,3,2,0,1:T(8,128)(2,1)S(1)} collective-permute-done((bf16[8,1,2,32,256]{4,3,2,0,1:T(8,128)(2,1)S(1)}, bf16[8,1,2,32,256]{4,3,2,0,1:T(8,128)(2,1)S(1)}, u32[]{:S(2)}, u32[]{:S(2)}) %collective-permute-start.3) | collective-permute-done | bytes 262176 | tf_op jit(solution)/shard_map/ppermute | solution.py:20
  52.1 1.4 collective-permute-done.2
  53.9 2.4 collective-permute-start.6
  56.3 3.2 %collective-permute-start.5 = (bf16[9,1,2,32,256]{4,3,2,1,0:T(8,128)(2,1)S(1)}, bf16[9,1,2,32,256]{4,3,2,1,0:T(8,128)(2,1)S(1)}, u32[]{:S(2)}, u32[]{:S(2)}) collective-permute-start(bf16[9,1,2,32,256]{4,3,2,1,0:T(8,128)(2,1)S(1)} %pad_maximum_fusion.1), channel_id=1, source_target_pairs={{0,1},{1,2},{2,3},{3,4},{4,5},{5,6},{6,7},{7,8},{8,9},{9,10},{10,1... | collective-permute-start | bytes 884744 | tf_op jit(solution)/shard_map/ppermute | solution.py:28
  59.6 3.1 %collective-permute-start.4 = (bf16[5,1,2,32,256]{4,3,2,1,0:T(8,128)(2,1)S(1)}, bf16[5,1,2,32,256]{4,3,2,1,0:T(8,128)(2,1)S(1)}, u32[]{:S(2)}, u32[]{:S(2)}) collective-permute-start(bf16[5,1,2,32,256]{4,3,2,1,0:T(8,128)(2,1)S(1)} %pad_maximum_fusion.4), channel_id=1, source_target_pairs={{0,2},{1,3},{2,4},{3,5},{4,6},{5,7},{6,8},{7,9},{8,10},{9,11},{10,... | collective-permute-start | bytes 491528 | tf_op jit(solution)/shard_map/ppermute | solution.py:28
  62.7 1.3 collective-permute-start.7
  64.0 2.6 %collective-permute-done.4 = bf16[5,1,2,32,256]{4,3,2,1,0:T(8,128)(2,1)S(1)} collective-permute-done((bf16[5,1,2,32,256]{4,3,2,1,0:T(8,128)(2,1)S(1)}, bf16[5,1,2,32,256]{4,3,2,1,0:T(8,128)(2,1)S(1)}, u32[]{:S(2)}, u32[]{:S(2)}) %collective-permute-start.4) | collective-permute-done | bytes 163872 | tf_op jit(solution)/shard_map/ppermute | solution.py:28
  66.7 3.8 %collective-permute-done.7 = bf16[5,1,2,32,256]{4,3,2,1,0:T(8,128)(2,1)S(1)} collective-permute-done((bf16[5,1,2,32,256]{4,3,2,1,0:T(8,128)(2,1)S(1)}, bf16[5,1,2,32,256]{4,3,2,1,0:T(8,128)(2,1)S(1)}, u32[]{:S(2)}, u32[]{:S(2)}) %collective-permute-start.7) | collective-permute-done | bytes 163872 | tf_op jit(solution)/shard_map/ppermute | solution.py:28
  70.8 4.1 %collective-permute-start.9 = (bf16[1,10,32,256]{3,2,1,0:T(8,128)(2,1)S(1)}, bf16[1,10,32,256]{3,2,1,0:T(8,128)(2,1)S(1)}, u32[]{:S(2)}, u32[]{:S(2)}) collective-permute-start(bf16[1,10,32,256]{3,2,1,0:T(8,128)(2,1)S(1)} %fusion.59), channel_id=1, source_target_pairs={{0,64},{64,128},{128,192},{192,256},{256,320},{320,384},{384,448},... | collective-permute-start | bytes 491528 | tf_op jit(solution)/shard_map/ppermute | solution.py:17
  74.9 1.3 collective-permute-start.8
  76.6 2.1 collective-permute-done.9
  79.0 3.7 %collective-permute-done.8 = bf16[1,10,32,256]{3,2,1,0:T(8,128)(2,1)S(1)} collective-permute-done((bf16[1,10,32,256]{3,2,1,0:T(8,128)(2,1)S(1)}, bf16[1,10,32,256]{3,2,1,0:T(8,128)(2,1)S(1)}, u32[]{:S(2)}, u32[]{:S(2)}) %collective-permute-start.8) | collective-permute-done | bytes 163872 | tf_op jit(solution)/shard_map/ppermute | solution.py:20
  84.9 2.2 collective-permute-start.11
  87.1 1.3 collective-permute-start.10
  89.2 3.6 %collective-permute-done.10 = bf16[1,8,32,256]{3,2,1,0:T(8,128)(2,1)S(1)} collective-permute-done((bf16[1,8,32,256]{3,2,1,0:T(8,128)(2,1)S(1)}, bf16[1,8,32,256]{3,2,1,0:T(8,128)(2,1)S(1)}, u32[]{:S(2)}, u32[]{:S(2)}) %collective-permute-start.10) | collective-permute-done | bytes 131104 | tf_op jit(solution)/shard_map/ppermute | solution.py:20
  94.9 4.5 %collective-permute-start.13 = (bf16[1,6,32,256]{3,2,1,0:T(8,128)(2,1)S(1)}, bf16[1,6,32,256]{3,2,1,0:T(8,128)(2,1)S(1)}, u32[]{:S(2)}, u32[]{:S(2)}) collective-permute-start(bf16[1,6,32,256]{3,2,1,0:T(8,128)(2,1)S(1)} %get-tuple-element.60), channel_id=1, source_target_pairs={{0,64},{64,128},{128,192},{192,256},{256,320},{320,384},{384,448},... | collective-permute-start | bytes 294920 | tf_op jit(solution)/shard_map/ppermute | solution.py:17
  99.6 1.3 collective-permute-start.12
  101.2 3.7 %collective-permute-done.12 = bf16[1,6,32,256]{3,2,1,0:T(8,128)(2,1)S(1)} collective-permute-done((bf16[1,6,32,256]{3,2,1,0:T(8,128)(2,1)S(1)}, bf16[1,6,32,256]{3,2,1,0:T(8,128)(2,1)S(1)}, u32[]{:S(2)}, u32[]{:S(2)}) %collective-permute-start.12) | collective-permute-done | bytes 98336 | tf_op jit(solution)/shard_map/ppermute | solution.py:20
  106.9 3.1 %collective-permute-start.15 = (bf16[1,4,32,256]{3,2,1,0:T(8,128)(2,1)S(1)}, bf16[1,4,32,256]{3,2,1,0:T(8,128)(2,1)S(1)}, u32[]{:S(2)}, u32[]{:S(2)}) collective-permute-start(bf16[1,4,32,256]{3,2,1,0:T(8,128)(2,1)S(1)} %get-tuple-element.62), channel_id=1, source_target_pairs={{0,64},{64,128},{128,192},{192,256},{256,320},{320,384},{384,448},... | collective-permute-start | bytes 196616 | tf_op jit(solution)/shard_map/ppermute | solution.py:17
  110.3 1.3 collective-permute-start.14
  111.8 3.5 %collective-permute-done.14 = bf16[1,4,32,256]{3,2,1,0:T(8,128)(2,1)S(1)} collective-permute-done((bf16[1,4,32,256]{3,2,1,0:T(8,128)(2,1)S(1)}, bf16[1,4,32,256]{3,2,1,0:T(8,128)(2,1)S(1)}, u32[]{:S(2)}, u32[]{:S(2)}) %collective-permute-start.14) | collective-permute-done | bytes 65568 | tf_op jit(solution)/shard_map/ppermute | solution.py:20
  117.1 4.1 %collective-permute-start.16 = (bf16[1,2,32,256]{3,2,1,0:T(8,128)(2,1)S(1)}, bf16[1,2,32,256]{3,2,1,0:T(8,128)(2,1)S(1)}, u32[]{:S(2)}, u32[]{:S(2)}) collective-permute-start(bf16[1,2,32,256]{3,2,1,0:T(8,128)(2,1)S(1)} %fusion.49), channel_id=1, source_target_pairs={{0,2},{1,3},{2,4},{3,5},{4,6},{5,7},{6,8},{7,9},{8,10},{9,11},{10,... | collective-permute-start | bytes 98312 | tf_op jit(solution)/shard_map/ppermute | solution.py:28
  121.2 8.5 %collective-permute-start.17 = (bf16[1,2,32,256]{3,2,1,0:T(8,128)(2,1)S(1)}, bf16[1,2,32,256]{3,2,1,0:T(8,128)(2,1)S(1)}, u32[]{:S(2)}, u32[]{:S(2)}) collective-permute-start(bf16[1,2,32,256]{3,2,1,0:T(8,128)(2,1)S(1)} %fusion.49), channel_id=1, source_target_pairs={{0,1},{1,2},{2,3},{3,4},{4,5},{5,6},{6,7},{7,8},{8,9},{9,10},{10,1... | collective-permute-start | bytes 98312 | tf_op jit(solution)/shard_map/ppermute | solution.py:28
  129.7 1.9 collective-permute-start.18
  133.0 1.9 collective-permute-done.18
  134.9 1.5 collective-permute-done.19
  136.5 2.9 %collective-permute-start.21 = (bf16[1,10,32,256]{3,2,1,0:T(8,128)(2,1)S(1)}, bf16[1,10,32,256]{3,2,1,0:T(8,128)(2,1)S(1)}, u32[]{:S(2)}, u32[]{:S(2)}) collective-permute-start(bf16[1,10,32,256]{3,2,1,0:T(8,128)(2,1)S(1)} %fusion.61), channel_id=1, source_target_pairs={{0,64},{64,128},{128,192},{192,256},{256,320},{320,384},{384,448},... | collective-permute-start | bytes 491528 | tf_op jit(solution)/shard_map/ppermute | solution.py:17
  139.4 1.3 collective-permute-start.20
  141.9 3.6 %collective-permute-done.20 = bf16[1,10,32,256]{3,2,1,0:T(8,128)(2,1)S(1)} collective-permute-done((bf16[1,10,32,256]{3,2,1,0:T(8,128)(2,1)S(1)}, bf16[1,10,32,256]{3,2,1,0:T(8,128)(2,1)S(1)}, u32[]{:S(2)}, u32[]{:S(2)}) %collective-permute-start.20) | collective-permute-done | bytes 163872 | tf_op jit(solution)/shard_map/ppermute | solution.py:20
  147.7 2.9 %collective-permute-start.23 = (bf16[1,8,32,256]{3,2,1,0:T(8,128)(2,1)S(1)}, bf16[1,8,32,256]{3,2,1,0:T(8,128)(2,1)S(1)}, u32[]{:S(2)}, u32[]{:S(2)}) collective-permute-start(bf16[1,8,32,256]{3,2,1,0:T(8,128)(2,1)S(1)} %get-tuple-element.64), channel_id=1, source_target_pairs={{0,64},{64,128},{128,192},{192,256},{256,320},{320,384},{384,448},... | collective-permute-start | bytes 393224 | tf_op jit(solution)/shard_map/ppermute | solution.py:17
  152.7 3.6 %collective-permute-done.22 = bf16[1,8,32,256]{3,2,1,0:T(8,128)(2,1)S(1)} collective-permute-done((bf16[1,8,32,256]{3,2,1,0:T(8,128)(2,1)S(1)}, bf16[1,8,32,256]{3,2,1,0:T(8,128)(2,1)S(1)}, u32[]{:S(2)}, u32[]{:S(2)}) %collective-permute-start.22) | collective-permute-done | bytes 131104 | tf_op jit(solution)/shard_map/ppermute | solution.py:20
  158.4 3.9 %collective-permute-start.25 = (bf16[1,6,32,256]{3,2,1,0:T(8,128)(2,1)S(1)}, bf16[1,6,32,256]{3,2,1,0:T(8,128)(2,1)}, u32[]{:S(2)}, u32[]{:S(2)}) collective-permute-start(bf16[1,6,32,256]{3,2,1,0:T(8,128)(2,1)S(1)} %get-tuple-element.66), channel_id=1, source_target_pairs={{0,64},{64,128},{128,192},{192,256},{256,320},{320,384},{384,448},... | collective-permute-start | bytes 294920 | tf_op jit(solution)/shard_map/ppermute | solution.py:17
  162.4 1.5 collective-permute-start.24
  170.4 3.6 %collective-permute-start.27 = (bf16[1,4,32,256]{3,2,1,0:T(8,128)(2,1)}, bf16[1,4,32,256]{3,2,1,0:T(8,128)(2,1)}, u32[]{:S(2)}, u32[]{:S(2)}) collective-permute-start(bf16[1,4,32,256]{3,2,1,0:T(8,128)(2,1)} %get-tuple-element.68), channel_id=1, source_target_pairs={{0,64},{64,128},{128,192},{192,256},{256,320},{320,384},{384,448},... | collective-permute-start | bytes 196616 | tf_op jit(solution)/shard_map/ppermute | solution.py:17
  174.0 1.7 fusion.195
  185.2 15.7 %all-to-all-start.1 = ((f32[64,8,192]{2,1,0:T(8,128)}), f32[64,8,192]{2,1,0:T(8,128)S(1)}, u32[]{:S(2)}, u32[]{:S(2)}) async-start(f32[64,8,192]{2,1,0:T(8,128)} %bitcast.1322), calls=%async_computation.1 | async-start | bytes 1048576 | tf_op jit(solution)/shard_map/all_to_all | solution.py:238
  201.6 16.6 %all-to-all-done.1 = f32[64,8,192]{2,1,0:T(8,128)S(1)} async-done(((f32[64,8,192]{2,1,0:T(8,128)}), f32[64,8,192]{2,1,0:T(8,128)S(1)}, u32[]{:S(2)}, u32[]{:S(2)}) %all-to-all-start.1) | async-done | bytes 393248 | tf_op jit(solution)/shard_map/all_to_all | solution.py:238
  218.9 3.8 %all-to-all-start.2 = ((f32[8,1,192]{2,1,0:T(1,128)}), f32[8,1,192]{2,1,0:T(1,128)S(1)}, u32[]{:S(2)}, u32[]{:S(2)}) async-start(f32[8,1,192]{2,1,0:T(1,128)} %all_to_all.18), calls=%async_computation.2 | async-start | bytes 16384 | tf_op jit(solution)/shard_map/all_to_all | solution.py:239
  222.8 6.5 %all-to-all-done.2 = f32[8,1,192]{2,1,0:T(1,128)S(1)} async-done(((f32[8,1,192]{2,1,0:T(1,128)}), f32[8,1,192]{2,1,0:T(1,128)S(1)}, u32[]{:S(2)}, u32[]{:S(2)}) %all-to-all-start.2) | async-done | bytes 6176 | tf_op jit(solution)/shard_map/all_to_all | solution.py:239
  229.9 7.7 %all-to-all-start.3 = ((f32[64,1,192]{2,1,0:T(1,128)}), f32[64,1,192]{2,1,0:T(1,128)S(1)}, u32[]{:S(2)}, u32[]{:S(2)}) async-start(f32[64,1,192]{2,1,0:T(1,128)} %broadcast_in_dim.21), calls=%async_computation.3 | async-start | bytes 131072 | tf_op jit(solution)/shard_map/all_to_all | solution.py:240
  238.5 9.0 %all-to-all-done.3 = f32[64,1,192]{2,1,0:T(1,128)S(1)} async-done(((f32[64,1,192]{2,1,0:T(1,128)}), f32[64,1,192]{2,1,0:T(1,128)S(1)}, u32[]{:S(2)}, u32[]{:S(2)}) %all-to-all-start.3) | async-done | bytes 49184 | tf_op jit(solution)/shard_map/all_to_all | solution.py:240
  (280 shorter events, 48.1 us)
Async XLA Ops:
  0.6 14.5 %copy-start.11 = (s32[1,12]{1,0:T(1,128)S(1)}, s32[1,12]{1,0:T(1,128)}, u32[]{:S(2)}) copy-start(s32[1,12]{1,0:T(1,128)} %param.9) | copy-start | bytes 148
  4.3 27.3 %all-to-all-start = ((bf16[8,112,256]{2,1,0:T(8,128)(2,1)}), bf16[8,112,256]{2,1,0:T(8,128)(2,1)S(1)}, u32[]{:S(2)}, u32[]{:S(2)}) async-start(bf16[8,112,256]{2,1,0:T(8,128)(2,1)} %pad_maximum_fusion), calls=%async_computation | async-start | bytes 917504 | tf_op jit(solution)/shard_map/all_to_all | solution.py:147
  31.7 7.7 %collective-permute-start.1 = (bf16[8,1,1,32,256]{4,3,2,0,1:T(8,128)(2,1)S(1)}, bf16[8,1,1,32,256]{4,3,2,0,1:T(8,128)(2,1)S(1)}, u32[]{:S(2)}, u32[]{:S(2)}) collective-permute-start(bf16[8,1,1,32,256]{4,3,2,0,1:T(8,128)(2,1)S(1)} %get-tuple-element.39), channel_id=1, source_target_pairs={{1,0},{2,1},{3,2},{4,3},{5,4},{6,5},{7,6},{8,7},{9,8},{10,9},{11,1... | collective-permute-start | bytes 393224 | tf_op jit(solution)/shard_map/ppermute | solution.py:20
  34.2 5.2 %collective-permute-start = (bf16[8,1,1,32,256]{4,3,2,0,1:T(8,128)(2,1)S(1)}, bf16[8,1,1,32,256]{4,3,2,0,1:T(8,128)(2,1)S(1)}, u32[]{:S(2)}, u32[]{:S(2)}) collective-permute-start(bf16[8,1,1,32,256]{4,3,2,0,1:T(8,128)(2,1)S(1)} %get-tuple-element.38), channel_id=1, source_target_pairs={{0,1},{1,2},{2,3},{3,4},{4,5},{5,6},{6,7},{7,8},{8,9},{9,10},{10,1... | collective-permute-start | bytes 393224 | tf_op jit(solution)/shard_map/ppermute | solution.py:17
  42.1 9.8 %collective-permute-start.3 = (bf16[8,1,2,32,256]{4,3,2,0,1:T(8,128)(2,1)S(1)}, bf16[8,1,2,32,256]{4,3,2,0,1:T(8,128)(2,1)S(1)}, u32[]{:S(2)}, u32[]{:S(2)}) collective-permute-start(bf16[8,1,2,32,256]{4,3,2,0,1:T(8,128)(2,1)S(1)} %bitcast.1333), channel_id=1, source_target_pairs={{64,0},{128,64},{192,128},{256,192},{320,256},{384,320},{448,384},... | collective-permute-start | bytes 786440 | tf_op jit(solution)/shard_map/ppermute | solution.py:20
  43.4 10.0 %collective-permute-start.2 = (bf16[8,1,2,32,256]{4,3,2,0,1:T(8,128)(2,1)S(1)}, bf16[8,1,2,32,256]{4,3,2,0,1:T(8,128)(2,1)S(1)}, u32[]{:S(2)}, u32[]{:S(2)}) collective-permute-start(bf16[8,1,2,32,256]{4,3,2,0,1:T(8,128)(2,1)S(1)} %bitcast.1334), channel_id=1, source_target_pairs={{0,64},{64,128},{128,192},{192,256},{256,320},{320,384},{384,448},... | collective-permute-start | bytes 786440 | tf_op jit(solution)/shard_map/ppermute | solution.py:17
  48.0 5.8 %copy-start = (bf16[7,1,2,288,256]{4,3,2,0,1:T(8,128)(2,1)}, bf16[7,1,2,288,256]{4,3,2,0,1:T(8,128)(2,1)S(1)}, u32[]{:S(2)}) copy-start(bf16[7,1,2,288,256]{4,3,2,0,1:T(8,128)(2,1)S(1)} %slice_dynamic-update-slice_fusion) | copy-start | bytes 6193156
  48.3 3.8 %copy-start.6 = (bf16[1,1,2,288,256]{4,3,2,0,1:T(8,128)(2,1)}, bf16[1,1,2,288,256]{4,3,2,0,1:T(8,128)(2,1)S(1)}, u32[]{:S(2)}) copy-start(bf16[1,1,2,288,256]{4,3,2,0,1:T(8,128)(2,1)S(1)} %constant_dynamic-update-slice_fusion.20) | copy-start | bytes 884740
  48.3 5.5 %copy-start.4 = (bf16[1,2,32,256]{3,2,1,0:T(8,128)(2,1)S(1)}, bf16[1,2,32,256]{3,2,1,0:T(8,128)(2,1)}, u32[]{:S(2)}) copy-start(bf16[1,2,32,256]{3,2,1,0:T(8,128)(2,1)} %param.6) | copy-start | bytes 98308
  51.9 12.1 %copy-start.2 = (bf16[8,1,2,32,256]{4,3,2,0,1:T(8,128)(2,1)}, bf16[8,1,2,32,256]{4,3,2,0,1:T(8,128)(2,1)S(1)}, u32[]{:S(2)}) copy-start(bf16[8,1,2,32,256]{4,3,2,0,1:T(8,128)(2,1)S(1)} %collective-permute-done.3) | copy-start | bytes 786436
  53.4 10.6 %copy-start.9 = (bf16[8,1,2,32,256]{4,3,2,0,1:T(8,128)(2,1)}, bf16[8,1,2,32,256]{4,3,2,0,1:T(8,128)(2,1)S(1)}, u32[]{:S(2)}) copy-start(bf16[8,1,2,32,256]{4,3,2,0,1:T(8,128)(2,1)S(1)} %collective-permute-done.2) | copy-start | bytes 786436
  53.9 16.7 %collective-permute-start.6 = (bf16[9,1,2,32,256]{4,3,2,1,0:T(8,128)(2,1)S(1)}, bf16[9,1,2,32,256]{4,3,2,1,0:T(8,128)(2,1)S(1)}, u32[]{:S(2)}, u32[]{:S(2)}) collective-permute-start(bf16[9,1,2,32,256]{4,3,2,1,0:T(8,128)(2,1)S(1)} %pad_maximum_fusion.1), channel_id=1, source_target_pairs={{1,0},{2,1},{3,2},{4,3},{5,4},{6,5},{7,6},{8,7},{9,8},{10,9},{11,1... | collective-permute-start | bytes 884744 | tf_op jit(solution)/shard_map/ppermute | solution.py:28
  56.3 14.3 %collective-permute-start.5 = (bf16[9,1,2,32,256]{4,3,2,1,0:T(8,128)(2,1)S(1)}, bf16[9,1,2,32,256]{4,3,2,1,0:T(8,128)(2,1)S(1)}, u32[]{:S(2)}, u32[]{:S(2)}) collective-permute-start(bf16[9,1,2,32,256]{4,3,2,1,0:T(8,128)(2,1)S(1)} %pad_maximum_fusion.1), channel_id=1, source_target_pairs={{0,1},{1,2},{2,3},{3,4},{4,5},{5,6},{6,7},{7,8},{8,9},{9,10},{10,1... | collective-permute-start | bytes 884744 | tf_op jit(solution)/shard_map/ppermute | solution.py:28
  59.6 7.1 %collective-permute-start.4 = (bf16[5,1,2,32,256]{4,3,2,1,0:T(8,128)(2,1)S(1)}, bf16[5,1,2,32,256]{4,3,2,1,0:T(8,128)(2,1)S(1)}, u32[]{:S(2)}, u32[]{:S(2)}) collective-permute-start(bf16[5,1,2,32,256]{4,3,2,1,0:T(8,128)(2,1)S(1)} %pad_maximum_fusion.4), channel_id=1, source_target_pairs={{0,2},{1,3},{2,4},{3,5},{4,6},{5,7},{6,8},{7,9},{8,10},{9,11},{10,... | collective-permute-start | bytes 491528 | tf_op jit(solution)/shard_map/ppermute | solution.py:28
  62.7 7.9 %collective-permute-start.7 = (bf16[5,1,2,32,256]{4,3,2,1,0:T(8,128)(2,1)S(1)}, bf16[5,1,2,32,256]{4,3,2,1,0:T(8,128)(2,1)S(1)}, u32[]{:S(2)}, u32[]{:S(2)}) collective-permute-start(bf16[5,1,2,32,256]{4,3,2,1,0:T(8,128)(2,1)S(1)} %pad_maximum_fusion.4), channel_id=1, source_target_pairs={{2,0},{3,1},{4,2},{5,3},{6,4},{7,5},{8,6},{9,7},{10,8},{11,9},{12,... | collective-permute-start | bytes 491528 | tf_op jit(solution)/shard_map/ppermute | solution.py:28
  70.8 7.9 %collective-permute-start.9 = (bf16[1,10,32,256]{3,2,1,0:T(8,128)(2,1)S(1)}, bf16[1,10,32,256]{3,2,1,0:T(8,128)(2,1)S(1)}, u32[]{:S(2)}, u32[]{:S(2)}) collective-permute-start(bf16[1,10,32,256]{3,2,1,0:T(8,128)(2,1)S(1)} %fusion.59), channel_id=1, source_target_pairs={{0,64},{64,128},{128,192},{192,256},{256,320},{320,384},{384,448},... | collective-permute-start | bytes 491528 | tf_op jit(solution)/shard_map/ppermute | solution.py:17
  74.9 7.7 %collective-permute-start.8 = (bf16[1,10,32,256]{3,2,1,0:T(8,128)(2,1)S(1)}, bf16[1,10,32,256]{3,2,1,0:T(8,128)(2,1)S(1)}, u32[]{:S(2)}, u32[]{:S(2)}) collective-permute-start(bf16[1,10,32,256]{3,2,1,0:T(8,128)(2,1)S(1)} %fusion.59), channel_id=1, source_target_pairs={{64,0},{128,64},{192,128},{256,192},{320,256},{384,320},{448,384},... | collective-permute-start | bytes 491528 | tf_op jit(solution)/shard_map/ppermute | solution.py:20
  84.9 4.1 %collective-permute-start.11 = (bf16[1,8,32,256]{3,2,1,0:T(8,128)(2,1)S(1)}, bf16[1,8,32,256]{3,2,1,0:T(8,128)(2,1)S(1)}, u32[]{:S(2)}, u32[]{:S(2)}) collective-permute-start(bf16[1,8,32,256]{3,2,1,0:T(8,128)(2,1)S(1)} %get-tuple-element.58), channel_id=1, source_target_pairs={{0,64},{64,128},{128,192},{192,256},{256,320},{320,384},{384,448},... | collective-permute-start | bytes 393224 | tf_op jit(solution)/shard_map/ppermute | solution.py:17
  87.1 5.7 %collective-permute-start.10 = (bf16[1,8,32,256]{3,2,1,0:T(8,128)(2,1)S(1)}, bf16[1,8,32,256]{3,2,1,0:T(8,128)(2,1)S(1)}, u32[]{:S(2)}, u32[]{:S(2)}) collective-permute-start(bf16[1,8,32,256]{3,2,1,0:T(8,128)(2,1)S(1)} %get-tuple-element.58), channel_id=1, source_target_pairs={{64,0},{128,64},{192,128},{256,192},{320,256},{384,320},{448,384},... | collective-permute-start | bytes 393224 | tf_op jit(solution)/shard_map/ppermute | solution.py:20
  94.9 6.1 %collective-permute-start.13 = (bf16[1,6,32,256]{3,2,1,0:T(8,128)(2,1)S(1)}, bf16[1,6,32,256]{3,2,1,0:T(8,128)(2,1)S(1)}, u32[]{:S(2)}, u32[]{:S(2)}) collective-permute-start(bf16[1,6,32,256]{3,2,1,0:T(8,128)(2,1)S(1)} %get-tuple-element.60), channel_id=1, source_target_pairs={{0,64},{64,128},{128,192},{192,256},{256,320},{320,384},{384,448},... | collective-permute-start | bytes 294920 | tf_op jit(solution)/shard_map/ppermute | solution.py:17
  99.6 5.4 %collective-permute-start.12 = (bf16[1,6,32,256]{3,2,1,0:T(8,128)(2,1)S(1)}, bf16[1,6,32,256]{3,2,1,0:T(8,128)(2,1)S(1)}, u32[]{:S(2)}, u32[]{:S(2)}) collective-permute-start(bf16[1,6,32,256]{3,2,1,0:T(8,128)(2,1)S(1)} %get-tuple-element.60), channel_id=1, source_target_pairs={{64,0},{128,64},{192,128},{256,192},{320,256},{384,320},{448,384},... | collective-permute-start | bytes 294920 | tf_op jit(solution)/shard_map/ppermute | solution.py:20
  106.9 4.6 %collective-permute-start.15 = (bf16[1,4,32,256]{3,2,1,0:T(8,128)(2,1)S(1)}, bf16[1,4,32,256]{3,2,1,0:T(8,128)(2,1)S(1)}, u32[]{:S(2)}, u32[]{:S(2)}) collective-permute-start(bf16[1,4,32,256]{3,2,1,0:T(8,128)(2,1)S(1)} %get-tuple-element.62), channel_id=1, source_target_pairs={{0,64},{64,128},{128,192},{192,256},{256,320},{320,384},{384,448},... | collective-permute-start | bytes 196616 | tf_op jit(solution)/shard_map/ppermute | solution.py:17
  110.3 5.0 %collective-permute-start.14 = (bf16[1,4,32,256]{3,2,1,0:T(8,128)(2,1)S(1)}, bf16[1,4,32,256]{3,2,1,0:T(8,128)(2,1)S(1)}, u32[]{:S(2)}, u32[]{:S(2)}) collective-permute-start(bf16[1,4,32,256]{3,2,1,0:T(8,128)(2,1)S(1)} %get-tuple-element.62), channel_id=1, source_target_pairs={{64,0},{128,64},{192,128},{256,192},{320,256},{384,320},{448,384},... | collective-permute-start | bytes 196616 | tf_op jit(solution)/shard_map/ppermute | solution.py:20
  117.1 15.9 %collective-permute-start.16 = (bf16[1,2,32,256]{3,2,1,0:T(8,128)(2,1)S(1)}, bf16[1,2,32,256]{3,2,1,0:T(8,128)(2,1)S(1)}, u32[]{:S(2)}, u32[]{:S(2)}) collective-permute-start(bf16[1,2,32,256]{3,2,1,0:T(8,128)(2,1)S(1)} %fusion.49), channel_id=1, source_target_pairs={{0,2},{1,3},{2,4},{3,5},{4,6},{5,7},{6,8},{7,9},{8,10},{9,11},{10,... | collective-permute-start | bytes 98312 | tf_op jit(solution)/shard_map/ppermute | solution.py:28
  121.2 11.8 %collective-permute-start.17 = (bf16[1,2,32,256]{3,2,1,0:T(8,128)(2,1)S(1)}, bf16[1,2,32,256]{3,2,1,0:T(8,128)(2,1)S(1)}, u32[]{:S(2)}, u32[]{:S(2)}) collective-permute-start(bf16[1,2,32,256]{3,2,1,0:T(8,128)(2,1)S(1)} %fusion.49), channel_id=1, source_target_pairs={{0,1},{1,2},{2,3},{3,4},{4,5},{5,6},{6,7},{7,8},{8,9},{9,10},{10,1... | collective-permute-start | bytes 98312 | tf_op jit(solution)/shard_map/ppermute | solution.py:28
  129.7 5.2 %collective-permute-start.18 = (bf16[1,2,32,256]{3,2,1,0:T(8,128)(2,1)S(1)}, bf16[1,2,32,256]{3,2,1,0:T(8,128)(2,1)S(1)}, u32[]{:S(2)}, u32[]{:S(2)}) collective-permute-start(bf16[1,2,32,256]{3,2,1,0:T(8,128)(2,1)S(1)} %fusion.49), channel_id=1, source_target_pairs={{1,0},{2,1},{3,2},{4,3},{5,4},{6,5},{7,6},{8,7},{9,8},{10,9},{11,1... | collective-permute-start | bytes 98312 | tf_op jit(solution)/shard_map/ppermute | solution.py:28
  131.6 4.9 %collective-permute-start.19 = (bf16[1,2,32,256]{3,2,1,0:T(8,128)(2,1)S(1)}, bf16[1,2,32,256]{3,2,1,0:T(8,128)(2,1)S(1)}, u32[]{:S(2)}, u32[]{:S(2)}) collective-permute-start(bf16[1,2,32,256]{3,2,1,0:T(8,128)(2,1)S(1)} %fusion.49), channel_id=1, source_target_pairs={{2,0},{3,1},{4,2},{5,3},{6,4},{7,5},{8,6},{9,7},{10,8},{11,9},{12,... | collective-permute-start | bytes 98312 | tf_op jit(solution)/shard_map/ppermute | solution.py:28
  136.5 5.1 %collective-permute-start.21 = (bf16[1,10,32,256]{3,2,1,0:T(8,128)(2,1)S(1)}, bf16[1,10,32,256]{3,2,1,0:T(8,128)(2,1)S(1)}, u32[]{:S(2)}, u32[]{:S(2)}) collective-permute-start(bf16[1,10,32,256]{3,2,1,0:T(8,128)(2,1)S(1)} %fusion.61), channel_id=1, source_target_pairs={{0,64},{64,128},{128,192},{192,256},{256,320},{320,384},{384,448},... | collective-permute-start | bytes 491528 | tf_op jit(solution)/shard_map/ppermute | solution.py:17
  139.4 6.1 %collective-permute-start.20 = (bf16[1,10,32,256]{3,2,1,0:T(8,128)(2,1)S(1)}, bf16[1,10,32,256]{3,2,1,0:T(8,128)(2,1)S(1)}, u32[]{:S(2)}, u32[]{:S(2)}) collective-permute-start(bf16[1,10,32,256]{3,2,1,0:T(8,128)(2,1)S(1)} %fusion.61), channel_id=1, source_target_pairs={{64,0},{128,64},{192,128},{256,192},{320,256},{384,320},{448,384},... | collective-permute-start | bytes 491528 | tf_op jit(solution)/shard_map/ppermute | solution.py:20
  147.7 4.8 %collective-permute-start.23 = (bf16[1,8,32,256]{3,2,1,0:T(8,128)(2,1)S(1)}, bf16[1,8,32,256]{3,2,1,0:T(8,128)(2,1)S(1)}, u32[]{:S(2)}, u32[]{:S(2)}) collective-permute-start(bf16[1,8,32,256]{3,2,1,0:T(8,128)(2,1)S(1)} %get-tuple-element.64), channel_id=1, source_target_pairs={{0,64},{64,128},{128,192},{192,256},{256,320},{320,384},{384,448},... | collective-permute-start | bytes 393224 | tf_op jit(solution)/shard_map/ppermute | solution.py:17
  150.5 5.7 %collective-permute-start.22 = (bf16[1,8,32,256]{3,2,1,0:T(8,128)(2,1)S(1)}, bf16[1,8,32,256]{3,2,1,0:T(8,128)(2,1)S(1)}, u32[]{:S(2)}, u32[]{:S(2)}) collective-permute-start(bf16[1,8,32,256]{3,2,1,0:T(8,128)(2,1)S(1)} %get-tuple-element.64), channel_id=1, source_target_pairs={{64,0},{128,64},{192,128},{256,192},{320,256},{384,320},{448,384},... | collective-permute-start | bytes 393224 | tf_op jit(solution)/shard_map/ppermute | solution.py:20
  157.1 6.9 %slice-start = ((bf16[8,1,2,32,256]{4,3,2,0,1:T(8,128)(2,1)}), bf16[7,1,2,32,256]{4,3,2,0,1:T(8,128)(2,1)S(1)}, s32[]{:S(2)}) async-start(bf16[8,1,2,32,256]{4,3,2,0,1:T(8,128)(2,1)} %copy-done.2), calls=%async_computation.4 | async-start | bytes 458752 | tf_op jit(solution)/shard_map/slice | solution.py:223
  157.1 6.9 %slice-start.1 = ((bf16[8,1,2,32,256]{4,3,2,0,1:T(8,128)(2,1)}), bf16[7,1,2,32,256]{4,3,2,0,1:T(8,128)(2,1)S(1)}, s32[]{:S(2)}) async-start(bf16[8,1,2,32,256]{4,3,2,0,1:T(8,128)(2,1)} %copy-done.9), calls=%async_computation.5 | async-start | bytes 458752 | tf_op jit(solution)/shard_map/slice | solution.py:223
  158.4 7.1 %collective-permute-start.25 = (bf16[1,6,32,256]{3,2,1,0:T(8,128)(2,1)S(1)}, bf16[1,6,32,256]{3,2,1,0:T(8,128)(2,1)}, u32[]{:S(2)}, u32[]{:S(2)}) collective-permute-start(bf16[1,6,32,256]{3,2,1,0:T(8,128)(2,1)S(1)} %get-tuple-element.66), channel_id=1, source_target_pairs={{0,64},{64,128},{128,192},{192,256},{256,320},{320,384},{384,448},... | collective-permute-start | bytes 294920 | tf_op jit(solution)/shard_map/ppermute | solution.py:17
  162.4 5.4 %collective-permute-start.24 = (bf16[1,6,32,256]{3,2,1,0:T(8,128)(2,1)S(1)}, bf16[1,6,32,256]{3,2,1,0:T(8,128)(2,1)S(1)}, u32[]{:S(2)}, u32[]{:S(2)}) collective-permute-start(bf16[1,6,32,256]{3,2,1,0:T(8,128)(2,1)S(1)} %get-tuple-element.66), channel_id=1, source_target_pairs={{64,0},{128,64},{192,128},{256,192},{320,256},{384,320},{448,384},... | collective-permute-start | bytes 294920 | tf_op jit(solution)/shard_map/ppermute | solution.py:20
  168.0 9.0 %copy-start.1 = (bf16[7,1,2,288,256]{4,3,2,0,1:T(8,128)(2,1)S(1)}, bf16[7,1,2,288,256]{4,3,2,0,1:T(8,128)(2,1)}, u32[]{:S(2)}) copy-start(bf16[7,1,2,288,256]{4,3,2,0,1:T(8,128)(2,1)} %copy-done) | copy-start | bytes 6193156
  170.4 9.2 %collective-permute-start.27 = (bf16[1,4,32,256]{3,2,1,0:T(8,128)(2,1)}, bf16[1,4,32,256]{3,2,1,0:T(8,128)(2,1)}, u32[]{:S(2)}, u32[]{:S(2)}) collective-permute-start(bf16[1,4,32,256]{3,2,1,0:T(8,128)(2,1)} %get-tuple-element.68), channel_id=1, source_target_pairs={{0,64},{64,128},{128,192},{192,256},{256,320},{320,384},{384,448},... | collective-permute-start | bytes 196616 | tf_op jit(solution)/shard_map/ppermute | solution.py:17
  175.7 5.3 %collective-permute-start.26 = (bf16[1,4,32,256]{3,2,1,0:T(8,128)(2,1)}, bf16[1,4,32,256]{3,2,1,0:T(8,128)(2,1)}, u32[]{:S(2)}, u32[]{:S(2)}) collective-permute-start(bf16[1,4,32,256]{3,2,1,0:T(8,128)(2,1)} %get-tuple-element.68), channel_id=1, source_target_pairs={{64,0},{128,64},{192,128},{256,192},{320,256},{384,320},{448,384},... | collective-permute-start | bytes 196616 | tf_op jit(solution)/shard_map/ppermute | solution.py:20
  177.7 3.3 %copy-start.3 = (f32[4,256,32]{1,2,0:T(8,128)S(1)}, f32[4,256,32]{1,2,0:T(8,128)}, u32[]{:S(2)}) copy-start(f32[4,256,32]{1,2,0:T(8,128)} %fusion.195) | copy-start | bytes 393220
  179.1 3.8 %copy-start.8 = (bf16[1,9,32,32]{2,3,1,0:T(8,128)(2,1)S(1)}, bf16[1,9,32,32]{2,3,1,0:T(8,128)(2,1)}, u32[]{:S(2)}) copy-start(bf16[1,9,32,32]{2,3,1,0:T(8,128)(2,1)} %copy.256) | copy-start | bytes 55300
  179.1 4.1 %copy-start.7 = (bf16[1,1,2,288,256]{4,3,2,0,1:T(8,128)(2,1)S(1)}, bf16[1,1,2,288,256]{4,3,2,0,1:T(8,128)(2,1)}, u32[]{:S(2)}) copy-start(bf16[1,1,2,288,256]{4,3,2,0,1:T(8,128)(2,1)} %copy-done.6) | copy-start | bytes 884740
  179.2 4.6 %copy-start.5 = (f32[7,3072]{1,0:T(8,128)S(1)}, f32[7,3072]{1,0:T(8,128)}, u32[]{:S(2)}) copy-start(f32[7,3072]{1,0:T(8,128)} %reshape.1296) | copy-start | bytes 258052
  184.1 53.6 %copy-start.10 = (bf16[1,4,32,256]{3,2,1,0:T(8,128)(2,1)S(1)}, bf16[1,4,32,256]{3,2,1,0:T(8,128)(2,1)}, u32[]{:S(2)}) copy-start(bf16[1,4,32,256]{3,2,1,0:T(8,128)(2,1)} %get-tuple-element.69) | copy-start | bytes 196612
  185.2 33.0 %all-to-all-start.1 = ((f32[64,8,192]{2,1,0:T(8,128)}), f32[64,8,192]{2,1,0:T(8,128)S(1)}, u32[]{:S(2)}, u32[]{:S(2)}) async-start(f32[64,8,192]{2,1,0:T(8,128)} %bitcast.1322), calls=%async_computation.1 | async-start | bytes 1048576 | tf_op jit(solution)/shard_map/all_to_all | solution.py:238
  218.9 10.4 %all-to-all-start.2 = ((f32[8,1,192]{2,1,0:T(1,128)}), f32[8,1,192]{2,1,0:T(1,128)S(1)}, u32[]{:S(2)}, u32[]{:S(2)}) async-start(f32[8,1,192]{2,1,0:T(1,128)} %all_to_all.18), calls=%async_computation.2 | async-start | bytes 16384 | tf_op jit(solution)/shard_map/all_to_all | solution.py:239
  229.9 17.5 %all-to-all-start.3 = ((f32[64,1,192]{2,1,0:T(1,128)}), f32[64,1,192]{2,1,0:T(1,128)S(1)}, u32[]{:S(2)}, u32[]{:S(2)}) async-start(f32[64,1,192]{2,1,0:T(1,128)} %broadcast_in_dim.21), calls=%async_computation.3 | async-start | bytes 131072 | tf_op jit(solution)/shard_map/all_to_all | solution.py:240

commit v11 on v7

--- a/solution.py
+++ b/solution.py
@@ -70,17 +70,16 @@
 
 def plane_back(rows_grad, kernel, height, width):
     padded = width_pad(rows_grad)
-    total = None
-    for i in range(3):
-        for j in range(3):
-            term = jnp.einsum(
-                "oc,...yox->...ycx",
-                kernel[i, j],
-                padded[..., 2 - i : 2 - i + height, :, 2 - j : 2 - j + width],
-                preferred_element_type=jnp.float32,
-            )
-            total = term if total is None else total + term
-    return total
+    stacked = jnp.concatenate(
+        [
+            padded[..., 2 - i : 2 - i + height, :, 2 - j : 2 - j + width]
+            for i in range(3)
+            for j in range(3)
+        ],
+        axis=-2,
+    )
+    flat = kernel.reshape(-1, kernel.shape[-1])
+    return jnp.einsum("kc,...ykx->...ycx", flat, stacked, preferred_element_type=jnp.float32)
 
 
 def plane_taps(grad_mid, rows_in, height, width):
@@ -102,16 +101,9 @@
 
 
 def depth_back(mix_deep, kernel, depth):
-    total = None
-    for k in range(3):
-        term = jnp.einsum(
-            "oc,zyox->zycx",
-            kernel[k],
-            mix_deep[2 - k : 2 - k + depth],
-            preferred_element_type=jnp.float32,
-        )
-        total = term if total is None else total + term
-    return total
+    stacked = jnp.concatenate([mix_deep[2 - k : 2 - k + depth] for k in range(3)], axis=-2)
+    flat = kernel.reshape(-1, kernel.shape[-1])
+    return jnp.einsum("kc,zykx->zycx", flat, stacked, preferred_element_type=jnp.float32)
 
 
 def depth_taps(grad_mix, deep, depth):

time: 246 us -> 245 us (level)
  matrix products: 29.3 us -> 13.7 us
  local copies, waits for them, and re-layouts: 11.2 us -> 18.3 us
  starting transfers between devices: 109 us -> 115 us
    dot_general x96 -> x16, matrix products: 24.2 us -> 7.91 us  [the longest x8 4.36 us: plane_back(): jnp.einsum('kc,...ykx->...ycx', flat, stacked, preferred_element_type=jnp...]
    unnamed x64 -> x118, local copies, waits for them, and re-layouts: 0.69 us -> 5.3 us
    all_to_all x1, starting transfers between devices: 20 us -> 23.4 us  [local(): part = lax.all_to_all(flat, ('segment', 'gy'), 0, 0, tiled=True).sum(axis=0)]
    ppermute x10, waiting for transfers between devices: 5.11 us -> 8.02 us  [padded_2(): lax.ppermute(lax.slice_in_dim(block, block.shape[dim] - width, None, axis...]
  transfers between devices with their start and end apart: 31 -> 31, of which waited for: 22 -> 20; matrix products, arithmetic and copies ran while one was open for 6% -> 5% of each run, Pallas kernels for 0% -> 0%
where the time goes in v11:
time: 245 us; the launch traced here: 243 us
  starting transfers between devices  115 us (47%)
  waiting for transfers between devices  89.9 us (37%)
  local copies, waits for them, and re-layouts  18.3 us (7%)
  matrix products  13.7 us (6%)
  other arithmetic  4.11 us (2%)
    ppermute x10, starting transfers between devices, padded_2(): lax.ppermute(lax.slice_in_dim(block, block.shape[dim] - width, None, axis...  34.1 us
    ppermute x8, starting transfers between devices, passed_along(): return lax.ppermute(block, axis, route)  28 us
    ppermute x10, waiting for transfers between devices, padded_2(): lax.ppermute(lax.slice_in_dim(block, 0, width, axis=dim), axis, backward)  25.8 us
    all_to_all x1, starting transfers between devices, local(): part = lax.all_to_all(flat, ('segment', 'gy'), 0, 0, tiled=True).sum(axis=0)  23.4 us
    all_to_all x1, waiting for transfers between devices, local(): part = lax.all_to_all(flat, ('segment', 'gy'), 0, 0, tiled=True).sum(axis=0)  22.5 us
    all_to_all x1, waiting for transfers between devices, local(): got = lax.all_to_all(send, 'segment', 0, 0, tiled=True)  16.2 us
    ppermute x10, starting transfers between devices, padded_2(): lax.ppermute(lax.slice_in_dim(block, 0, width, axis=dim), axis, backward)  14.3 us
    all_to_all x1, starting transfers between devices, local(): got = lax.all_to_all(send, 'segment', 0, 0, tiled=True)  10.9 us
  transfers between devices with their start and end apart: 31, of which 20 were waited for; matrix products, arithmetic and copies ran while one was open for 5% of the time, Pallas kernels for 0%

profile of v11, /device:TPU:1, one launch (start us, length us, event | category | flops | bytes accessed | tf_op | source)
XLA Modules:
  0.0 243.0 jit_solution(16934396589329418873)
XLA Ops:
  2.5 1.8 pad_maximum_fusion
  4.3 10.9 %all-to-all-start = ((bf16[8,112,256]{2,1,0:T(8,128)(2,1)}), bf16[8,112,256]{2,1,0:T(8,128)(2,1)S(1)}, u32[]{:S(2)}, u32[]{:S(2)}) async-start(bf16[8,112,256]{2,1,0:T(8,128)(2,1)} %pad_maximum_fusion), calls=%async_computation | async-start | bytes 917504 | tf_op jit(solution)/shard_map/all_to_all | solution.py:139
  15.4 16.2 %all-to-all-done = bf16[8,112,256]{2,1,0:T(8,128)(2,1)S(1)} async-done(((bf16[8,112,256]{2,1,0:T(8,128)(2,1)}), bf16[8,112,256]{2,1,0:T(8,128)(2,1)S(1)}, u32[]{:S(2)}, u32[]{:S(2)}) %all-to-all-start) | async-done | bytes 458784 | tf_op jit(solution)/shard_map/all_to_all | solution.py:139
  32.1 2.5 %collective-permute-start.1 = (bf16[8,1,1,32,256]{4,3,2,0,1:T(8,128)(2,1)S(1)}, bf16[8,1,1,32,256]{4,3,2,0,1:T(8,128)(2,1)S(1)}, u32[]{:S(2)}, u32[]{:S(2)}) collective-permute-start(bf16[8,1,1,32,256]{4,3,2,0,1:T(8,128)(2,1)S(1)} %get-tuple-element.49), channel_id=1, source_target_pairs={{1,0},{2,1},{3,2},{4,3},{5,4},{6,5},{7,6},{8,7},{9,8},{10,9},{11,1... | collective-permute-start | bytes 393224 | tf_op jit(solution)/shard_map/ppermute | solution.py:20
  34.6 3.1 %collective-permute-start = (bf16[8,1,1,32,256]{4,3,2,0,1:T(8,128)(2,1)S(1)}, bf16[8,1,1,32,256]{4,3,2,0,1:T(8,128)(2,1)S(1)}, u32[]{:S(2)}, u32[]{:S(2)}) collective-permute-start(bf16[8,1,1,32,256]{4,3,2,0,1:T(8,128)(2,1)S(1)} %get-tuple-element.48), channel_id=1, source_target_pairs={{0,1},{1,2},{2,3},{3,4},{4,5},{5,6},{6,7},{7,8},{8,9},{9,10},{10,1... | collective-permute-start | bytes 393224 | tf_op jit(solution)/shard_map/ppermute | solution.py:17
  42.4 1.3 collective-permute-start.3
  43.7 4.0 %collective-permute-start.2 = (bf16[8,1,2,32,256]{4,3,2,0,1:T(8,128)(2,1)S(1)}, bf16[8,1,2,32,256]{4,3,2,0,1:T(8,128)(2,1)S(1)}, u32[]{:S(2)}, u32[]{:S(2)}) collective-permute-start(bf16[8,1,2,32,256]{4,3,2,0,1:T(8,128)(2,1)S(1)} %bitcast.634), channel_id=1, source_target_pairs={{0,64},{64,128},{128,192},{192,256},{256,320},{320,384},{384,448},... | collective-permute-start | bytes 786440 | tf_op jit(solution)/shard_map/ppermute | solution.py:17
  48.5 2.6 %collective-permute-done.3 = bf16[8,1,2,32,256]{4,3,2,0,1:T(8,128)(2,1)S(1)} collective-permute-done((bf16[8,1,2,32,256]{4,3,2,0,1:T(8,128)(2,1)S(1)}, bf16[8,1,2,32,256]{4,3,2,0,1:T(8,128)(2,1)S(1)}, u32[]{:S(2)}, u32[]{:S(2)}) %collective-permute-start.3) | collective-permute-done | bytes 262176 | tf_op jit(solution)/shard_map/ppermute | solution.py:20
  51.3 1.5 collective-permute-done.2
  53.3 1.9 collective-permute-start.6
  55.2 4.4 %collective-permute-start.5 = (bf16[9,1,2,32,256]{4,3,2,1,0:T(8,128)(2,1)S(1)}, bf16[9,1,2,32,256]{4,3,2,1,0:T(8,128)(2,1)S(1)}, u32[]{:S(2)}, u32[]{:S(2)}) collective-permute-start(bf16[9,1,2,32,256]{4,3,2,1,0:T(8,128)(2,1)S(1)} %pad_maximum_fusion.1), channel_id=1, source_target_pairs={{0,1},{1,2},{2,3},{3,4},{4,5},{5,6},{6,7},{7,8},{8,9},{9,10},{10,1... | collective-permute-start | bytes 884744 | tf_op jit(solution)/shard_map/ppermute | solution.py:28
  59.7 1.3 collective-permute-start.7
  61.0 4.0 %collective-permute-start.4 = (bf16[5,1,2,32,256]{4,3,2,1,0:T(8,128)(2,1)S(1)}, bf16[5,1,2,32,256]{4,3,2,1,0:T(8,128)(2,1)S(1)}, u32[]{:S(2)}, u32[]{:S(2)}) collective-permute-start(bf16[5,1,2,32,256]{4,3,2,1,0:T(8,128)(2,1)S(1)} %pad_maximum_fusion.4), channel_id=1, source_target_pairs={{0,2},{1,3},{2,4},{3,5},{4,6},{5,7},{6,8},{7,9},{8,10},{9,11},{10,... | collective-permute-start | bytes 491528 | tf_op jit(solution)/shard_map/ppermute | solution.py:28
  65.0 3.6 %collective-permute-done.4 = bf16[5,1,2,32,256]{4,3,2,1,0:T(8,128)(2,1)S(1)} collective-permute-done((bf16[5,1,2,32,256]{4,3,2,1,0:T(8,128)(2,1)S(1)}, bf16[5,1,2,32,256]{4,3,2,1,0:T(8,128)(2,1)S(1)}, u32[]{:S(2)}, u32[]{:S(2)}) %collective-permute-start.4) | collective-permute-done | bytes 163872 | tf_op jit(solution)/shard_map/ppermute | solution.py:28
  68.9 4.1 %collective-permute-start.9 = (bf16[1,10,32,256]{3,2,1,0:T(8,128)(2,1)S(1)}, bf16[1,10,32,256]{3,2,1,0:T(8,128)(2,1)S(1)}, u32[]{:S(2)}, u32[]{:S(2)}) collective-permute-start(bf16[1,10,32,256]{3,2,1,0:T(8,128)(2,1)S(1)} %fusion.65), channel_id=1, source_target_pairs={{0,64},{64,128},{128,192},{192,256},{256,320},{320,384},{384,448},... | collective-permute-start | bytes 491528 | tf_op jit(solution)/shard_map/ppermute | solution.py:17
  73.0 1.3 collective-permute-start.8
  74.3 2.2 collective-permute-done.9
  76.5 3.8 %collective-permute-done.8 = bf16[1,10,32,256]{3,2,1,0:T(8,128)(2,1)S(1)} collective-permute-done((bf16[1,10,32,256]{3,2,1,0:T(8,128)(2,1)S(1)}, bf16[1,10,32,256]{3,2,1,0:T(8,128)(2,1)S(1)}, u32[]{:S(2)}, u32[]{:S(2)}) %collective-permute-start.8) | collective-permute-done | bytes 163872 | tf_op jit(solution)/shard_map/ppermute | solution.py:20
  81.7 2.2 collective-permute-start.11
  83.9 1.3 collective-permute-start.10
  85.8 3.8 %collective-permute-done.10 = bf16[1,8,32,256]{3,2,1,0:T(8,128)(2,1)S(1)} collective-permute-done((bf16[1,8,32,256]{3,2,1,0:T(8,128)(2,1)S(1)}, bf16[1,8,32,256]{3,2,1,0:T(8,128)(2,1)S(1)}, u32[]{:S(2)}, u32[]{:S(2)}) %collective-permute-start.10) | collective-permute-done | bytes 131104 | tf_op jit(solution)/shard_map/ppermute | solution.py:20
  90.8 4.0 %collective-permute-start.13 = (bf16[1,6,32,256]{3,2,1,0:T(8,128)(2,1)S(1)}, bf16[1,6,32,256]{3,2,1,0:T(8,128)(2,1)S(1)}, u32[]{:S(2)}, u32[]{:S(2)}) collective-permute-start(bf16[1,6,32,256]{3,2,1,0:T(8,128)(2,1)S(1)} %get-tuple-element.60), channel_id=1, source_target_pairs={{0,64},{64,128},{128,192},{192,256},{256,320},{320,384},{384,448},... | collective-permute-start | bytes 294920 | tf_op jit(solution)/shard_map/ppermute | solution.py:17
  94.9 1.3 collective-permute-start.12
  96.5 3.7 %collective-permute-done.12 = bf16[1,6,32,256]{3,2,1,0:T(8,128)(2,1)S(1)} collective-permute-done((bf16[1,6,32,256]{3,2,1,0:T(8,128)(2,1)S(1)}, bf16[1,6,32,256]{3,2,1,0:T(8,128)(2,1)S(1)}, u32[]{:S(2)}, u32[]{:S(2)}) %collective-permute-start.12) | collective-permute-done | bytes 98336 | tf_op jit(solution)/shard_map/ppermute | solution.py:20
  101.3 3.4 %collective-permute-start.15 = (bf16[1,4,32,256]{3,2,1,0:T(8,128)(2,1)S(1)}, bf16[1,4,32,256]{3,2,1,0:T(8,128)(2,1)S(1)}, u32[]{:S(2)}, u32[]{:S(2)}) collective-permute-start(bf16[1,4,32,256]{3,2,1,0:T(8,128)(2,1)S(1)} %get-tuple-element.62), channel_id=1, source_target_pairs={{0,64},{64,128},{128,192},{192,256},{256,320},{320,384},{384,448},... | collective-permute-start | bytes 196616 | tf_op jit(solution)/shard_map/ppermute | solution.py:17
  104.7 1.3 collective-permute-start.14
  106.6 3.1 %collective-permute-done.14 = bf16[1,4,32,256]{3,2,1,0:T(8,128)(2,1)S(1)} collective-permute-done((bf16[1,4,32,256]{3,2,1,0:T(8,128)(2,1)S(1)}, bf16[1,4,32,256]{3,2,1,0:T(8,128)(2,1)S(1)}, u32[]{:S(2)}, u32[]{:S(2)}) %collective-permute-start.14) | collective-permute-done | bytes 65568 | tf_op jit(solution)/shard_map/ppermute | solution.py:20
  110.7 3.5 %collective-permute-start.16 = (bf16[1,2,32,256]{3,2,1,0:T(8,128)(2,1)S(1)}, bf16[1,2,32,256]{3,2,1,0:T(8,128)(2,1)S(1)}, u32[]{:S(2)}, u32[]{:S(2)}) collective-permute-start(bf16[1,2,32,256]{3,2,1,0:T(8,128)(2,1)S(1)} %fusion.34), channel_id=1, source_target_pairs={{0,2},{1,3},{2,4},{3,5},{4,6},{5,7},{6,8},{7,9},{8,10},{9,11},{10,... | collective-permute-start | bytes 98312 | tf_op jit(solution)/shard_map/ppermute | solution.py:28
  114.2 9.7 %collective-permute-start.17 = (bf16[1,2,32,256]{3,2,1,0:T(8,128)(2,1)S(1)}, bf16[1,2,32,256]{3,2,1,0:T(8,128)(2,1)S(1)}, u32[]{:S(2)}, u32[]{:S(2)}) collective-permute-start(bf16[1,2,32,256]{3,2,1,0:T(8,128)(2,1)S(1)} %fusion.34), channel_id=1, source_target_pairs={{0,1},{1,2},{2,3},{3,4},{4,5},{5,6},{6,7},{7,8},{8,9},{9,10},{10,1... | collective-permute-start | bytes 98312 | tf_op jit(solution)/shard_map/ppermute | solution.py:28
  123.9 1.9 collective-permute-start.18
  125.9 1.3 collective-permute-start.19
  127.2 1.9 collective-permute-done.18
  129.2 2.8 %collective-permute-done.19 = bf16[1,2,32,256]{3,2,1,0:T(8,128)(2,1)S(1)} collective-permute-done((bf16[1,2,32,256]{3,2,1,0:T(8,128)(2,1)S(1)}, bf16[1,2,32,256]{3,2,1,0:T(8,128)(2,1)S(1)}, u32[]{:S(2)}, u32[]{:S(2)}) %collective-permute-start.19) | collective-permute-done | bytes 32800 | tf_op jit(solution)/shard_map/ppermute | solution.py:28
  132.1 2.9 %collective-permute-start.21 = (bf16[1,10,32,256]{3,2,1,0:T(8,128)(2,1)S(1)}, bf16[1,10,32,256]{3,2,1,0:T(8,128)(2,1)S(1)}, u32[]{:S(2)}, u32[]{:S(2)}) collective-permute-start(bf16[1,10,32,256]{3,2,1,0:T(8,128)(2,1)S(1)} %fusion.66), channel_id=1, source_target_pairs={{0,64},{64,128},{128,192},{192,256},{256,320},{320,384},{384,448},... | collective-permute-start | bytes 491528 | tf_op jit(solution)/shard_map/ppermute | solution.py:17
  134.9 1.3 collective-permute-start.20
  136.3 2.3 collective-permute-done.21
  138.6 3.8 %collective-permute-done.20 = bf16[1,10,32,256]{3,2,1,0:T(8,128)(2,1)S(1)} collective-permute-done((bf16[1,10,32,256]{3,2,1,0:T(8,128)(2,1)S(1)}, bf16[1,10,32,256]{3,2,1,0:T(8,128)(2,1)S(1)}, u32[]{:S(2)}, u32[]{:S(2)}) %collective-permute-start.20) | collective-permute-done | bytes 163872 | tf_op jit(solution)/shard_map/ppermute | solution.py:20
  143.7 2.8 %collective-permute-start.23 = (bf16[1,8,32,256]{3,2,1,0:T(8,128)(2,1)S(1)}, bf16[1,8,32,256]{3,2,1,0:T(8,128)(2,1)S(1)}, u32[]{:S(2)}, u32[]{:S(2)}) collective-permute-start(bf16[1,8,32,256]{3,2,1,0:T(8,128)(2,1)S(1)} %get-tuple-element.3), channel_id=1, source_target_pairs={{0,64},{64,128},{128,192},{192,256},{256,320},{320,384},{384,448},... | collective-permute-start | bytes 393224 | tf_op jit(solution)/shard_map/ppermute | solution.py:17
  146.6 1.3 collective-permute-start.22
  148.5 3.8 %collective-permute-done.22 = bf16[1,8,32,256]{3,2,1,0:T(8,128)(2,1)S(1)} collective-permute-done((bf16[1,8,32,256]{3,2,1,0:T(8,128)(2,1)S(1)}, bf16[1,8,32,256]{3,2,1,0:T(8,128)(2,1)S(1)}, u32[]{:S(2)}, u32[]{:S(2)}) %collective-permute-start.22) | collective-permute-done | bytes 131104 | tf_op jit(solution)/shard_map/ppermute | solution.py:20
  154.2 3.6 %collective-permute-start.25 = (bf16[1,6,32,256]{3,2,1,0:T(8,128)(2,1)}, bf16[1,6,32,256]{3,2,1,0:T(8,128)(2,1)}, u32[]{:S(2)}, u32[]{:S(2)}) collective-permute-start(bf16[1,6,32,256]{3,2,1,0:T(8,128)(2,1)} %get-tuple-element.64), channel_id=1, source_target_pairs={{0,64},{64,128},{128,192},{192,256},{256,320},{320,384},{384,448},... | collective-permute-start | bytes 294920 | tf_op jit(solution)/shard_map/ppermute | solution.py:17
  166.8 4.0 %collective-permute-start.27 = (bf16[1,4,32,256]{3,2,1,0:T(8,128)(2,1)}, bf16[1,4,32,256]{3,2,1,0:T(8,128)(2,1)S(1)}, u32[]{:S(2)}, u32[]{:S(2)}) collective-permute-start(bf16[1,4,32,256]{3,2,1,0:T(8,128)(2,1)} %get-tuple-element.66), channel_id=1, source_target_pairs={{0,64},{64,128},{128,192},{192,256},{256,320},{320,384},{384,448},... | collective-permute-start | bytes 196616 | tf_op jit(solution)/shard_map/ppermute | solution.py:17
  170.8 1.5 collective-permute-start.26
  178.1 1.7 mul.91
  179.8 23.4 %all-to-all-start.1 = ((f32[512,1,192]{2,1,0:T(1,128)}), f32[512,1,192]{2,1,0:T(1,128)S(1)}, u32[]{:S(2)}, u32[]{:S(2)}) async-start(f32[512,1,192]{2,1,0:T(1,128)} %mul.91), calls=%async_computation.1 | async-start | bytes 1048576 | tf_op jit(solution)/shard_map/all_to_all | solution.py:229
  203.4 22.5 %all-to-all-done.1 = f32[512,1,192]{2,1,0:T(1,128)S(1)} async-done(((f32[512,1,192]{2,1,0:T(1,128)}), f32[512,1,192]{2,1,0:T(1,128)S(1)}, u32[]{:S(2)}, u32[]{:S(2)}) %all-to-all-start.1) | async-done | bytes 393248 | tf_op jit(solution)/shard_map/all_to_all | solution.py:229
  227.2 4.2 %all-to-all-start.2 = ((f32[64,1,192]{2,1,0:T(1,128)}), f32[64,1,192]{2,1,0:T(1,128)S(1)}, u32[]{:S(2)}, u32[]{:S(2)}) async-start(f32[64,1,192]{2,1,0:T(1,128)} %broadcast_in_dim.21), calls=%async_computation.2 | async-start | bytes 131072 | tf_op jit(solution)/shard_map/all_to_all | solution.py:230
  232.2 8.9 %all-to-all-done.2 = f32[64,1,192]{2,1,0:T(1,128)S(1)} async-done(((f32[64,1,192]{2,1,0:T(1,128)}), f32[64,1,192]{2,1,0:T(1,128)S(1)}, u32[]{:S(2)}, u32[]{:S(2)}) %all-to-all-start.2) | async-done | bytes 49184 | tf_op jit(solution)/shard_map/all_to_all | solution.py:230
  (250 shorter events, 37.1 us)
Async XLA Ops:
  0.6 14.5 %copy-start.10 = (s32[1,12]{1,0:T(1,128)S(1)}, s32[1,12]{1,0:T(1,128)}, u32[]{:S(2)}) copy-start(s32[1,12]{1,0:T(1,128)} %param.9) | copy-start | bytes 148
  4.3 27.3 %all-to-all-start = ((bf16[8,112,256]{2,1,0:T(8,128)(2,1)}), bf16[8,112,256]{2,1,0:T(8,128)(2,1)S(1)}, u32[]{:S(2)}, u32[]{:S(2)}) async-start(bf16[8,112,256]{2,1,0:T(8,128)(2,1)} %pad_maximum_fusion), calls=%async_computation | async-start | bytes 917504 | tf_op jit(solution)/shard_map/all_to_all | solution.py:139
  32.1 6.3 %collective-permute-start.1 = (bf16[8,1,1,32,256]{4,3,2,0,1:T(8,128)(2,1)S(1)}, bf16[8,1,1,32,256]{4,3,2,0,1:T(8,128)(2,1)S(1)}, u32[]{:S(2)}, u32[]{:S(2)}) collective-permute-start(bf16[8,1,1,32,256]{4,3,2,0,1:T(8,128)(2,1)S(1)} %get-tuple-element.49), channel_id=1, source_target_pairs={{1,0},{2,1},{3,2},{4,3},{5,4},{6,5},{7,6},{8,7},{9,8},{10,9},{11,1... | collective-permute-start | bytes 393224 | tf_op jit(solution)/shard_map/ppermute | solution.py:20
  34.6 5.0 %collective-permute-start = (bf16[8,1,1,32,256]{4,3,2,0,1:T(8,128)(2,1)S(1)}, bf16[8,1,1,32,256]{4,3,2,0,1:T(8,128)(2,1)S(1)}, u32[]{:S(2)}, u32[]{:S(2)}) collective-permute-start(bf16[8,1,1,32,256]{4,3,2,0,1:T(8,128)(2,1)S(1)} %get-tuple-element.48), channel_id=1, source_target_pairs={{0,1},{1,2},{2,3},{3,4},{4,5},{5,6},{6,7},{7,8},{8,9},{9,10},{10,1... | collective-permute-start | bytes 393224 | tf_op jit(solution)/shard_map/ppermute | solution.py:17
  42.4 8.7 %collective-permute-start.3 = (bf16[8,1,2,32,256]{4,3,2,0,1:T(8,128)(2,1)S(1)}, bf16[8,1,2,32,256]{4,3,2,0,1:T(8,128)(2,1)S(1)}, u32[]{:S(2)}, u32[]{:S(2)}) collective-permute-start(bf16[8,1,2,32,256]{4,3,2,0,1:T(8,128)(2,1)S(1)} %bitcast.633), channel_id=1, source_target_pairs={{64,0},{128,64},{192,128},{256,192},{320,256},{384,320},{448,384},... | collective-permute-start | bytes 786440 | tf_op jit(solution)/shard_map/ppermute | solution.py:20
  43.7 9.2 %collective-permute-start.2 = (bf16[8,1,2,32,256]{4,3,2,0,1:T(8,128)(2,1)S(1)}, bf16[8,1,2,32,256]{4,3,2,0,1:T(8,128)(2,1)S(1)}, u32[]{:S(2)}, u32[]{:S(2)}) collective-permute-start(bf16[8,1,2,32,256]{4,3,2,0,1:T(8,128)(2,1)S(1)} %bitcast.634), channel_id=1, source_target_pairs={{0,64},{64,128},{128,192},{192,256},{256,320},{320,384},{384,448},... | collective-permute-start | bytes 786440 | tf_op jit(solution)/shard_map/ppermute | solution.py:17
  51.1 55.5 %copy-start = (bf16[8,1,2,32,256]{4,3,2,0,1:T(8,128)(2,1)}, bf16[8,1,2,32,256]{4,3,2,0,1:T(8,128)(2,1)S(1)}, u32[]{:S(2)}) copy-start(bf16[8,1,2,32,256]{4,3,2,0,1:T(8,128)(2,1)S(1)} %collective-permute-done.3) | copy-start | bytes 786436
  51.3 1.9 copy-start.3
  52.9 53.8 %copy-start.5 = (bf16[8,1,2,32,256]{4,3,2,0,1:T(8,128)(2,1)}, bf16[8,1,2,32,256]{4,3,2,0,1:T(8,128)(2,1)S(1)}, u32[]{:S(2)}) copy-start(bf16[8,1,2,32,256]{4,3,2,0,1:T(8,128)(2,1)S(1)} %collective-permute-done.2) | copy-start | bytes 786436
  53.3 15.4 %collective-permute-start.6 = (bf16[9,1,2,32,256]{4,3,2,1,0:T(8,128)(2,1)S(1)}, bf16[9,1,2,32,256]{4,3,2,1,0:T(8,128)(2,1)S(1)}, u32[]{:S(2)}, u32[]{:S(2)}) collective-permute-start(bf16[9,1,2,32,256]{4,3,2,1,0:T(8,128)(2,1)S(1)} %pad_maximum_fusion.1), channel_id=1, source_target_pairs={{1,0},{2,1},{3,2},{4,3},{5,4},{6,5},{7,6},{8,7},{9,8},{10,9},{11,1... | collective-permute-start | bytes 884744 | tf_op jit(solution)/shard_map/ppermute | solution.py:28
  55.2 13.4 %collective-permute-start.5 = (bf16[9,1,2,32,256]{4,3,2,1,0:T(8,128)(2,1)S(1)}, bf16[9,1,2,32,256]{4,3,2,1,0:T(8,128)(2,1)S(1)}, u32[]{:S(2)}, u32[]{:S(2)}) collective-permute-start(bf16[9,1,2,32,256]{4,3,2,1,0:T(8,128)(2,1)S(1)} %pad_maximum_fusion.1), channel_id=1, source_target_pairs={{0,1},{1,2},{2,3},{3,4},{4,5},{5,6},{6,7},{7,8},{8,9},{9,10},{10,1... | collective-permute-start | bytes 884744 | tf_op jit(solution)/shard_map/ppermute | solution.py:28
  59.7 8.9 %collective-permute-start.7 = (bf16[5,1,2,32,256]{4,3,2,1,0:T(8,128)(2,1)S(1)}, bf16[5,1,2,32,256]{4,3,2,1,0:T(8,128)(2,1)S(1)}, u32[]{:S(2)}, u32[]{:S(2)}) collective-permute-start(bf16[5,1,2,32,256]{4,3,2,1,0:T(8,128)(2,1)S(1)} %pad_maximum_fusion.4), channel_id=1, source_target_pairs={{2,0},{3,1},{4,2},{5,3},{6,4},{7,5},{8,6},{9,7},{10,8},{11,9},{12,... | collective-permute-start | bytes 491528 | tf_op jit(solution)/shard_map/ppermute | solution.py:28
  61.0 7.6 %collective-permute-start.4 = (bf16[5,1,2,32,256]{4,3,2,1,0:T(8,128)(2,1)S(1)}, bf16[5,1,2,32,256]{4,3,2,1,0:T(8,128)(2,1)S(1)}, u32[]{:S(2)}, u32[]{:S(2)}) collective-permute-start(bf16[5,1,2,32,256]{4,3,2,1,0:T(8,128)(2,1)S(1)} %pad_maximum_fusion.4), channel_id=1, source_target_pairs={{0,2},{1,3},{2,4},{3,5},{4,6},{5,7},{6,8},{7,9},{8,10},{9,11},{10,... | collective-permute-start | bytes 491528 | tf_op jit(solution)/shard_map/ppermute | solution.py:28
  68.9 7.7 %collective-permute-start.9 = (bf16[1,10,32,256]{3,2,1,0:T(8,128)(2,1)S(1)}, bf16[1,10,32,256]{3,2,1,0:T(8,128)(2,1)S(1)}, u32[]{:S(2)}, u32[]{:S(2)}) collective-permute-start(bf16[1,10,32,256]{3,2,1,0:T(8,128)(2,1)S(1)} %fusion.65), channel_id=1, source_target_pairs={{0,64},{64,128},{128,192},{192,256},{256,320},{320,384},{384,448},... | collective-permute-start | bytes 491528 | tf_op jit(solution)/shard_map/ppermute | solution.py:17
  73.0 7.3 %collective-permute-start.8 = (bf16[1,10,32,256]{3,2,1,0:T(8,128)(2,1)S(1)}, bf16[1,10,32,256]{3,2,1,0:T(8,128)(2,1)S(1)}, u32[]{:S(2)}, u32[]{:S(2)}) collective-permute-start(bf16[1,10,32,256]{3,2,1,0:T(8,128)(2,1)S(1)} %fusion.65), channel_id=1, source_target_pairs={{64,0},{128,64},{192,128},{256,192},{320,256},{384,320},{448,384},... | collective-permute-start | bytes 491528 | tf_op jit(solution)/shard_map/ppermute | solution.py:20
  81.7 4.1 %collective-permute-start.11 = (bf16[1,8,32,256]{3,2,1,0:T(8,128)(2,1)S(1)}, bf16[1,8,32,256]{3,2,1,0:T(8,128)(2,1)S(1)}, u32[]{:S(2)}, u32[]{:S(2)}) collective-permute-start(bf16[1,8,32,256]{3,2,1,0:T(8,128)(2,1)S(1)} %get-tuple-element.5), channel_id=1, source_target_pairs={{0,64},{64,128},{128,192},{192,256},{256,320},{320,384},{384,448},... | collective-permute-start | bytes 393224 | tf_op jit(solution)/shard_map/ppermute | solution.py:17
  83.9 5.7 %collective-permute-start.10 = (bf16[1,8,32,256]{3,2,1,0:T(8,128)(2,1)S(1)}, bf16[1,8,32,256]{3,2,1,0:T(8,128)(2,1)S(1)}, u32[]{:S(2)}, u32[]{:S(2)}) collective-permute-start(bf16[1,8,32,256]{3,2,1,0:T(8,128)(2,1)S(1)} %get-tuple-element.5), channel_id=1, source_target_pairs={{64,0},{128,64},{192,128},{256,192},{320,256},{384,320},{448,384},... | collective-permute-start | bytes 393224 | tf_op jit(solution)/shard_map/ppermute | solution.py:20
  85.3 5.1 %copy-start.1 = (bf16[1,1,2,288,256]{4,3,2,0,1:T(8,128)(2,1)}, bf16[1,1,2,288,256]{4,3,2,0,1:T(8,128)(2,1)S(1)}, u32[]{:S(2)}) copy-start(bf16[1,1,2,288,256]{4,3,2,0,1:T(8,128)(2,1)S(1)} %constant_dynamic-update-slice_fusion.82) | copy-start | bytes 884740
  90.8 5.7 %collective-permute-start.13 = (bf16[1,6,32,256]{3,2,1,0:T(8,128)(2,1)S(1)}, bf16[1,6,32,256]{3,2,1,0:T(8,128)(2,1)S(1)}, u32[]{:S(2)}, u32[]{:S(2)}) collective-permute-start(bf16[1,6,32,256]{3,2,1,0:T(8,128)(2,1)S(1)} %get-tuple-element.60), channel_id=1, source_target_pairs={{0,64},{64,128},{128,192},{192,256},{256,320},{320,384},{384,448},... | collective-permute-start | bytes 294920 | tf_op jit(solution)/shard_map/ppermute | solution.py:17
  94.9 5.4 %collective-permute-start.12 = (bf16[1,6,32,256]{3,2,1,0:T(8,128)(2,1)S(1)}, bf16[1,6,32,256]{3,2,1,0:T(8,128)(2,1)S(1)}, u32[]{:S(2)}, u32[]{:S(2)}) collective-permute-start(bf16[1,6,32,256]{3,2,1,0:T(8,128)(2,1)S(1)} %get-tuple-element.60), channel_id=1, source_target_pairs={{64,0},{128,64},{192,128},{256,192},{320,256},{384,320},{448,384},... | collective-permute-start | bytes 294920 | tf_op jit(solution)/shard_map/ppermute | solution.py:20
  101.3 5.3 %collective-permute-start.15 = (bf16[1,4,32,256]{3,2,1,0:T(8,128)(2,1)S(1)}, bf16[1,4,32,256]{3,2,1,0:T(8,128)(2,1)S(1)}, u32[]{:S(2)}, u32[]{:S(2)}) collective-permute-start(bf16[1,4,32,256]{3,2,1,0:T(8,128)(2,1)S(1)} %get-tuple-element.62), channel_id=1, source_target_pairs={{0,64},{64,128},{128,192},{192,256},{256,320},{320,384},{384,448},... | collective-permute-start | bytes 196616 | tf_op jit(solution)/shard_map/ppermute | solution.py:17
  104.7 5.0 %collective-permute-start.14 = (bf16[1,4,32,256]{3,2,1,0:T(8,128)(2,1)S(1)}, bf16[1,4,32,256]{3,2,1,0:T(8,128)(2,1)S(1)}, u32[]{:S(2)}, u32[]{:S(2)}) collective-permute-start(bf16[1,4,32,256]{3,2,1,0:T(8,128)(2,1)S(1)} %get-tuple-element.62), channel_id=1, source_target_pairs={{64,0},{128,64},{192,128},{256,192},{320,256},{384,320},{448,384},... | collective-permute-start | bytes 196616 | tf_op jit(solution)/shard_map/ppermute | solution.py:20
  110.1 26.1 %slice-start = ((bf16[8,1,2,32,256]{4,3,2,0,1:T(8,128)(2,1)}), bf16[1,1,2,32,256]{4,3,2,0,1:T(8,128)(2,1)S(1)}, s32[]{:S(2)}) async-start(bf16[8,1,2,32,256]{4,3,2,0,1:T(8,128)(2,1)} %copy-done), calls=%async_computation.3 | async-start | bytes 65536 | tf_op jit(solution)/shard_map/slice | solution.py:215
  110.1 26.2 %slice-start.2 = ((bf16[8,1,2,32,256]{4,3,2,0,1:T(8,128)(2,1)}), bf16[1,1,2,32,256]{4,3,2,0,1:T(8,128)(2,1)S(1)}, s32[]{:S(2)}) async-start(bf16[8,1,2,32,256]{4,3,2,0,1:T(8,128)(2,1)} %copy-done.5), calls=%async_computation.5 | async-start | bytes 65536 | tf_op jit(solution)/shard_map/slice | solution.py:215
  110.7 16.5 %collective-permute-start.16 = (bf16[1,2,32,256]{3,2,1,0:T(8,128)(2,1)S(1)}, bf16[1,2,32,256]{3,2,1,0:T(8,128)(2,1)S(1)}, u32[]{:S(2)}, u32[]{:S(2)}) collective-permute-start(bf16[1,2,32,256]{3,2,1,0:T(8,128)(2,1)S(1)} %fusion.34), channel_id=1, source_target_pairs={{0,2},{1,3},{2,4},{3,5},{4,6},{5,7},{6,8},{7,9},{8,10},{9,11},{10,... | collective-permute-start | bytes 98312 | tf_op jit(solution)/shard_map/ppermute | solution.py:28
  114.2 13.0 %collective-permute-start.17 = (bf16[1,2,32,256]{3,2,1,0:T(8,128)(2,1)S(1)}, bf16[1,2,32,256]{3,2,1,0:T(8,128)(2,1)S(1)}, u32[]{:S(2)}, u32[]{:S(2)}) collective-permute-start(bf16[1,2,32,256]{3,2,1,0:T(8,128)(2,1)S(1)} %fusion.34), channel_id=1, source_target_pairs={{0,1},{1,2},{2,3},{3,4},{4,5},{5,6},{6,7},{7,8},{8,9},{9,10},{10,1... | collective-permute-start | bytes 98312 | tf_op jit(solution)/shard_map/ppermute | solution.py:28
  123.9 5.2 %collective-permute-start.18 = (bf16[1,2,32,256]{3,2,1,0:T(8,128)(2,1)S(1)}, bf16[1,2,32,256]{3,2,1,0:T(8,128)(2,1)S(1)}, u32[]{:S(2)}, u32[]{:S(2)}) collective-permute-start(bf16[1,2,32,256]{3,2,1,0:T(8,128)(2,1)S(1)} %fusion.34), channel_id=1, source_target_pairs={{1,0},{2,1},{3,2},{4,3},{5,4},{6,5},{7,6},{8,7},{9,8},{10,9},{11,1... | collective-permute-start | bytes 98312 | tf_op jit(solution)/shard_map/ppermute | solution.py:28
  125.9 6.2 %collective-permute-start.19 = (bf16[1,2,32,256]{3,2,1,0:T(8,128)(2,1)S(1)}, bf16[1,2,32,256]{3,2,1,0:T(8,128)(2,1)S(1)}, u32[]{:S(2)}, u32[]{:S(2)}) collective-permute-start(bf16[1,2,32,256]{3,2,1,0:T(8,128)(2,1)S(1)} %fusion.34), channel_id=1, source_target_pairs={{2,0},{3,1},{4,2},{5,3},{6,4},{7,5},{8,6},{9,7},{10,8},{11,9},{12,... | collective-permute-start | bytes 98312 | tf_op jit(solution)/shard_map/ppermute | solution.py:28
  132.1 6.5 %collective-permute-start.21 = (bf16[1,10,32,256]{3,2,1,0:T(8,128)(2,1)S(1)}, bf16[1,10,32,256]{3,2,1,0:T(8,128)(2,1)S(1)}, u32[]{:S(2)}, u32[]{:S(2)}) collective-permute-start(bf16[1,10,32,256]{3,2,1,0:T(8,128)(2,1)S(1)} %fusion.66), channel_id=1, source_target_pairs={{0,64},{64,128},{128,192},{192,256},{256,320},{320,384},{384,448},... | collective-permute-start | bytes 491528 | tf_op jit(solution)/shard_map/ppermute | solution.py:17
  134.9 7.4 %collective-permute-start.20 = (bf16[1,10,32,256]{3,2,1,0:T(8,128)(2,1)S(1)}, bf16[1,10,32,256]{3,2,1,0:T(8,128)(2,1)S(1)}, u32[]{:S(2)}, u32[]{:S(2)}) collective-permute-start(bf16[1,10,32,256]{3,2,1,0:T(8,128)(2,1)S(1)} %fusion.66), channel_id=1, source_target_pairs={{64,0},{128,64},{192,128},{256,192},{320,256},{384,320},{448,384},... | collective-permute-start | bytes 491528 | tf_op jit(solution)/shard_map/ppermute | solution.py:20
  143.7 4.8 %collective-permute-start.23 = (bf16[1,8,32,256]{3,2,1,0:T(8,128)(2,1)S(1)}, bf16[1,8,32,256]{3,2,1,0:T(8,128)(2,1)S(1)}, u32[]{:S(2)}, u32[]{:S(2)}) collective-permute-start(bf16[1,8,32,256]{3,2,1,0:T(8,128)(2,1)S(1)} %get-tuple-element.3), channel_id=1, source_target_pairs={{0,64},{64,128},{128,192},{192,256},{256,320},{320,384},{384,448},... | collective-permute-start | bytes 393224 | tf_op jit(solution)/shard_map/ppermute | solution.py:17
  146.6 5.7 %collective-permute-start.22 = (bf16[1,8,32,256]{3,2,1,0:T(8,128)(2,1)S(1)}, bf16[1,8,32,256]{3,2,1,0:T(8,128)(2,1)S(1)}, u32[]{:S(2)}, u32[]{:S(2)}) collective-permute-start(bf16[1,8,32,256]{3,2,1,0:T(8,128)(2,1)S(1)} %get-tuple-element.3), channel_id=1, source_target_pairs={{64,0},{128,64},{192,128},{256,192},{320,256},{384,320},{448,384},... | collective-permute-start | bytes 393224 | tf_op jit(solution)/shard_map/ppermute | solution.py:20
  153.1 6.9 %slice-start.1 = ((bf16[8,1,2,32,256]{4,3,2,0,1:T(8,128)(2,1)}), bf16[7,1,2,32,256]{4,3,2,0,1:T(8,128)(2,1)S(1)}, s32[]{:S(2)}) async-start(bf16[8,1,2,32,256]{4,3,2,0,1:T(8,128)(2,1)} %copy-done), calls=%async_computation.4 | async-start | bytes 458752 | tf_op jit(solution)/shard_map/slice | solution.py:215
  153.1 6.9 %slice-start.3 = ((bf16[8,1,2,32,256]{4,3,2,0,1:T(8,128)(2,1)}), bf16[7,1,2,32,256]{4,3,2,0,1:T(8,128)(2,1)S(1)}, s32[]{:S(2)}) async-start(bf16[8,1,2,32,256]{4,3,2,0,1:T(8,128)(2,1)} %copy-done.5), calls=%async_computation.6 | async-start | bytes 458752 | tf_op jit(solution)/shard_map/slice | solution.py:215
  154.2 9.8 %collective-permute-start.25 = (bf16[1,6,32,256]{3,2,1,0:T(8,128)(2,1)}, bf16[1,6,32,256]{3,2,1,0:T(8,128)(2,1)}, u32[]{:S(2)}, u32[]{:S(2)}) collective-permute-start(bf16[1,6,32,256]{3,2,1,0:T(8,128)(2,1)} %get-tuple-element.64), channel_id=1, source_target_pairs={{0,64},{64,128},{128,192},{192,256},{256,320},{320,384},{384,448},... | collective-permute-start | bytes 294920 | tf_op jit(solution)/shard_map/ppermute | solution.py:17
  157.8 6.2 %collective-permute-start.24 = (bf16[1,6,32,256]{3,2,1,0:T(8,128)(2,1)}, bf16[1,6,32,256]{3,2,1,0:T(8,128)(2,1)}, u32[]{:S(2)}, u32[]{:S(2)}) collective-permute-start(bf16[1,6,32,256]{3,2,1,0:T(8,128)(2,1)} %get-tuple-element.64), channel_id=1, source_target_pairs={{64,0},{128,64},{192,128},{256,192},{320,256},{384,320},{448,384},... | collective-permute-start | bytes 294920 | tf_op jit(solution)/shard_map/ppermute | solution.py:20
  162.9 3.0 %copy-start.4 = (bf16[1,6,32,256]{3,2,1,0:T(8,128)(2,1)S(1)}, bf16[1,6,32,256]{3,2,1,0:T(8,128)(2,1)}, u32[]{:S(2)}) copy-start(bf16[1,6,32,256]{3,2,1,0:T(8,128)(2,1)} %get-tuple-element.65) | copy-start | bytes 294916
  162.9 3.0 %copy-start.6 = (f32[1,2,32,256]{3,2,1,0:T(8,128)S(1)}, f32[1,2,32,256]{3,2,1,0:T(8,128)}, u32[]{:S(2)}) copy-start(f32[1,2,32,256]{3,2,1,0:T(8,128)} %slice_bitcast_fusion.12) | copy-start | bytes 196612
  162.9 3.1 %copy-start.8 = (f32[1,1,32,256]{3,2,1,0:T(8,128)S(1)}, f32[1,1,32,256]{3,2,1,0:T(8,128)}, u32[]{:S(2)}) copy-start(f32[1,1,32,256]{3,2,1,0:T(8,128)} %get-tuple-element.75) | copy-start | bytes 98308
  166.8 8.1 %collective-permute-start.27 = (bf16[1,4,32,256]{3,2,1,0:T(8,128)(2,1)}, bf16[1,4,32,256]{3,2,1,0:T(8,128)(2,1)S(1)}, u32[]{:S(2)}, u32[]{:S(2)}) collective-permute-start(bf16[1,4,32,256]{3,2,1,0:T(8,128)(2,1)} %get-tuple-element.66), channel_id=1, source_target_pairs={{0,64},{64,128},{128,192},{192,256},{256,320},{320,384},{384,448},... | collective-permute-start | bytes 196616 | tf_op jit(solution)/shard_map/ppermute | solution.py:17
  170.8 5.3 %collective-permute-start.26 = (bf16[1,4,32,256]{3,2,1,0:T(8,128)(2,1)}, bf16[1,4,32,256]{3,2,1,0:T(8,128)(2,1)}, u32[]{:S(2)}, u32[]{:S(2)}) collective-permute-start(bf16[1,4,32,256]{3,2,1,0:T(8,128)(2,1)} %get-tuple-element.66), channel_id=1, source_target_pairs={{64,0},{128,64},{192,128},{256,192},{320,256},{384,320},{448,384},... | collective-permute-start | bytes 196616 | tf_op jit(solution)/shard_map/ppermute | solution.py:20
  174.4 1.7 copy-start.9
  174.5 3.0 %copy-start.2 = (bf16[1,1,2,288,256]{4,3,2,0,1:T(8,128)(2,1)S(1)}, bf16[1,1,2,288,256]{4,3,2,0,1:T(8,128)(2,1)}, u32[]{:S(2)}) copy-start(bf16[1,1,2,288,256]{4,3,2,0,1:T(8,128)(2,1)} %copy-done.1) | copy-start | bytes 884740
  179.8 51.6 %copy-start.7 = (bf16[1,4,32,256]{3,2,1,0:T(8,128)(2,1)S(1)}, bf16[1,4,32,256]{3,2,1,0:T(8,128)(2,1)}, u32[]{:S(2)}) copy-start(bf16[1,4,32,256]{3,2,1,0:T(8,128)(2,1)} %get-tuple-element.67) | copy-start | bytes 196612
  179.8 46.1 %all-to-all-start.1 = ((f32[512,1,192]{2,1,0:T(1,128)}), f32[512,1,192]{2,1,0:T(1,128)S(1)}, u32[]{:S(2)}, u32[]{:S(2)}) async-start(f32[512,1,192]{2,1,0:T(1,128)} %mul.91), calls=%async_computation.1 | async-start | bytes 1048576 | tf_op jit(solution)/shard_map/all_to_all | solution.py:229
  227.2 14.0 %all-to-all-start.2 = ((f32[64,1,192]{2,1,0:T(1,128)}), f32[64,1,192]{2,1,0:T(1,128)S(1)}, u32[]{:S(2)}, u32[]{:S(2)}) async-start(f32[64,1,192]{2,1,0:T(1,128)} %broadcast_in_dim.21), calls=%async_computation.2 | async-start | bytes 131072 | tf_op jit(solution)/shard_map/all_to_all | solution.py:230

commit v12 on v11

--- a/solution.py
+++ b/solution.py
@@ -45,27 +45,19 @@
 
 def plane_conv_all(rows_in, kernel, height, width):
     padded = width_pad(rows_in)
-    total = None
-    for i in range(3):
-        for j in range(3):
-            term = jnp.einsum(
-                "loc,lzycx->lzyox",
-                kernel[:, i, j],
-                padded[:, :, i : i + height, :, j : j + width],
-                preferred_element_type=jnp.float32,
-            )
-            total = term if total is None else total + term
-    return total
+    stacked = jnp.concatenate(
+        [padded[:, :, i : i + height, :, j : j + width] for i in range(3) for j in range(3)],
+        axis=-2,
+    )
+    flat = kernel.reshape((kernel.shape[0], 9) + kernel.shape[3:]).transpose(0, 2, 1, 3)
+    flat = flat.reshape(kernel.shape[0], kernel.shape[3], -1)
+    return jnp.einsum("lok,lzykx->lzyox", flat, stacked, preferred_element_type=jnp.float32)
 
 
 def depth_conv_all(deep, kernel, depth):
-    total = None
-    for k in range(3):
-        term = jnp.einsum(
-            "loc,lzycx->lzyox", kernel[:, k], deep[:, k : k + depth], preferred_element_type=jnp.float32
-        )
-        total = term if total is None else total + term
-    return total
+    stacked = jnp.concatenate([deep[:, k : k + depth] for k in range(3)], axis=-2)
+    flat = kernel.transpose(0, 2, 1, 3).reshape(kernel.shape[0], kernel.shape[2], -1)
+    return jnp.einsum("lok,lzykx->lzyox", flat, stacked, preferred_element_type=jnp.float32)
 
 
 def plane_back(rows_grad, kernel, height, width):
@@ -221,14 +213,14 @@
     rest_p, rest_d = kernel_grads(list(range(1, layers)))
     planes = jnp.concatenate([first_p, rest_p])
     depths = jnp.concatenate([first_d, rest_d])
-    flat = jnp.concatenate([planes, depths], axis=1) * scale
+    flat = jnp.concatenate([planes, depths], axis=1)
     spread_n = lax.axis_size("gy")
     size = flat.shape[1]
-    piece = -(-size // spread_n)
+    piece = 128 * -(-size // (128 * spread_n))
     flat = jnp.pad(flat, ((0, 0), (0, piece * spread_n - size))).reshape(layers * spread_n, piece)
     part = lax.all_to_all(flat, ("segment", "gy"), 0, 0, tiled=True).sum(axis=0)
     whole = lax.all_to_all(jnp.broadcast_to(part, (spread_n, piece)), "gy", 0, 0, tiled=True)
-    flat = whole.reshape(-1)[:size][None]
+    flat = whole.reshape(-1)[:size][None] * scale
     cut = planes.shape[1]
     plane_sum = flat[:, :cut].reshape(-1, 3, 3, chans, chans)
     depth_sum = flat[:, cut:].reshape(-1, 3, chans, chans)

time: 245 us -> 244 us (level)
  waiting for transfers between devices: 89.9 us -> 75.5 us
  starting transfers between devices: 115 us -> 129 us
    ppermute x10, waiting for transfers between devices: 25.8 us -> 9.76 us  [padded_2(): lax.ppermute(lax.slice_in_dim(block, 0, width, axis=dim), axis, backward)]
    ppermute x10, starting transfers between devices: 34.1 us -> 44.1 us  [padded_2(): lax.ppermute(lax.slice_in_dim(block, block.shape[dim] - width, None, axis...]
    all_to_all x1, starting transfers between devices: 23.4 us -> 28.9 us  [local(): part = lax.all_to_all(flat, ('segment', 'gy'), 0, 0, tiled=True).sum(axis=0)]
    unnamed x118 -> x132, local copies, waits for them, and re-layouts: 5.3 us -> 5.68 us
  transfers between devices with their start and end apart: 31 -> 31, of which waited for: 20 -> 19; matrix products, arithmetic and copies ran while one was open for 5% -> 5% of each run, Pallas kernels for 0% -> 0%
where the time goes in v12:
time: 244 us; the launch traced here: 243 us
  starting transfers between devices  129 us (53%)
  waiting for transfers between devices  75.5 us (31%)
  local copies, waits for them, and re-layouts  20.3 us (8%)
  matrix products  11.8 us (5%)
  other arithmetic  4.04 us (2%)
    ppermute x10, starting transfers between devices, padded_2(): lax.ppermute(lax.slice_in_dim(block, block.shape[dim] - width, None, axis...  44.1 us
    all_to_all x1, starting transfers between devices, local(): part = lax.all_to_all(flat, ('segment', 'gy'), 0, 0, tiled=True).sum(axis=0)  28.9 us
    ppermute x8, starting transfers between devices, passed_along(): return lax.ppermute(block, axis, route)  27.5 us
    all_to_all x1, waiting for transfers between devices, local(): part = lax.all_to_all(flat, ('segment', 'gy'), 0, 0, tiled=True).sum(axis=0)  22.3 us
    all_to_all x1, waiting for transfers between devices, local(): got = lax.all_to_all(send, 'segment', 0, 0, tiled=True)  16.2 us
    ppermute x10, starting transfers between devices, padded_2(): lax.ppermute(lax.slice_in_dim(block, 0, width, axis=dim), axis, backward)  13.5 us
    all_to_all x1, starting transfers between devices, local(): got = lax.all_to_all(send, 'segment', 0, 0, tiled=True)  10.9 us
    ppermute x10, waiting for transfers between devices, padded_2(): lax.ppermute(lax.slice_in_dim(block, 0, width, axis=dim), axis, backward)  9.76 us
  transfers between devices with their start and end apart: 31, of which 19 were waited for; matrix products, arithmetic and copies ran while one was open for 5% of the time, Pallas kernels for 0%

profile of v12, /device:TPU:1, one launch (start us, length us, event | category | flops | bytes accessed | tf_op | source)
XLA Modules:
  0.0 243.0 jit_solution(16709158263481343429)
XLA Ops:
  2.5 1.8 pad_maximum_fusion
  4.3 10.9 %all-to-all-start = ((bf16[8,112,256]{2,1,0:T(8,128)(2,1)}), bf16[8,112,256]{2,1,0:T(8,128)(2,1)S(1)}, u32[]{:S(2)}, u32[]{:S(2)}) async-start(bf16[8,112,256]{2,1,0:T(8,128)(2,1)} %pad_maximum_fusion), calls=%async_computation | async-start | bytes 917504 | tf_op jit(solution)/shard_map/all_to_all | solution.py:131
  15.5 16.2 %all-to-all-done = bf16[8,112,256]{2,1,0:T(8,128)(2,1)S(1)} async-done(((bf16[8,112,256]{2,1,0:T(8,128)(2,1)}), bf16[8,112,256]{2,1,0:T(8,128)(2,1)S(1)}, u32[]{:S(2)}, u32[]{:S(2)}) %all-to-all-start) | async-done | bytes 458784 | tf_op jit(solution)/shard_map/all_to_all | solution.py:131
  33.5 3.7 %collective-permute-start = (bf16[8,1,1,32,256]{4,3,2,0,1:T(8,128)(2,1)}, bf16[8,1,1,32,256]{4,3,2,0,1:T(8,128)(2,1)S(1)}, u32[]{:S(2)}, u32[]{:S(2)}) collective-permute-start(bf16[8,1,1,32,256]{4,3,2,0,1:T(8,128)(2,1)} %get-tuple-element.48), channel_id=1, source_target_pairs={{0,1},{1,2},{2,3},{3,4},{4,5},{5,6},{6,7},{7,8},{8,9},{9,10},{10,1... | collective-permute-start | bytes 393224 | tf_op jit(solution)/shard_map/ppermute | solution.py:17
  37.2 1.9 collective-permute-start.1
  40.4 3.3 %collective-permute-done.1 = bf16[8,1,1,32,256]{4,3,2,0,1:T(8,128)(2,1)S(1)} collective-permute-done((bf16[8,1,1,32,256]{4,3,2,0,1:T(8,128)(2,1)}, bf16[8,1,1,32,256]{4,3,2,0,1:T(8,128)(2,1)S(1)}, u32[]{:S(2)}, u32[]{:S(2)}) %collective-permute-start.1) | collective-permute-done | bytes 131104 | tf_op jit(solution)/shard_map/ppermute | solution.py:20
  45.3 2.2 collective-permute-start.2
  47.5 1.3 collective-permute-start.3
  49.6 1.4 collective-permute-done.2
  51.0 4.1 %collective-permute-done.3 = bf16[8,1,2,32,256]{4,3,2,0,1:T(8,128)(2,1)S(1)} collective-permute-done((bf16[8,1,2,32,256]{4,3,2,0,1:T(8,128)(2,1)S(1)}, bf16[8,1,2,32,256]{4,3,2,0,1:T(8,128)(2,1)S(1)}, u32[]{:S(2)}, u32[]{:S(2)}) %collective-permute-start.3) | collective-permute-done | bytes 262176 | tf_op jit(solution)/shard_map/ppermute | solution.py:20
  55.6 5.0 %collective-permute-start.4 = (bf16[5,1,2,32,256]{4,3,2,1,0:T(8,128)(2,1)S(1)}, bf16[5,1,2,32,256]{4,3,2,1,0:T(8,128)(2,1)S(1)}, u32[]{:S(2)}, u32[]{:S(2)}) collective-permute-start(bf16[5,1,2,32,256]{4,3,2,1,0:T(8,128)(2,1)S(1)} %pad_maximum_fusion.4), channel_id=1, source_target_pairs={{0,2},{1,3},{2,4},{3,5},{4,6},{5,7},{6,8},{7,9},{8,10},{9,11},{10,... | collective-permute-start | bytes 491528 | tf_op jit(solution)/shard_map/ppermute | solution.py:28
  60.6 1.3 collective-permute-start.7
  61.9 4.7 %collective-permute-start.5 = (bf16[9,1,2,32,256]{4,3,2,1,0:T(8,128)(2,1)S(1)}, bf16[9,1,2,32,256]{4,3,2,1,0:T(8,128)(2,1)S(1)}, u32[]{:S(2)}, u32[]{:S(2)}) collective-permute-start(bf16[9,1,2,32,256]{4,3,2,1,0:T(8,128)(2,1)S(1)} %pad_maximum_fusion.1), channel_id=1, source_target_pairs={{0,1},{1,2},{2,3},{3,4},{4,5},{5,6},{6,7},{7,8},{8,9},{9,10},{10,1... | collective-permute-start | bytes 884744 | tf_op jit(solution)/shard_map/ppermute | solution.py:28
  66.7 1.9 collective-permute-start.6
  68.7 1.6 collective-permute-done.5
  70.4 4.3 %collective-permute-done.6 = bf16[9,1,2,32,256]{4,3,2,1,0:T(8,128)(2,1)S(1)} collective-permute-done((bf16[9,1,2,32,256]{4,3,2,1,0:T(8,128)(2,1)S(1)}, bf16[9,1,2,32,256]{4,3,2,1,0:T(8,128)(2,1)S(1)}, u32[]{:S(2)}, u32[]{:S(2)}) %collective-permute-start.6) | collective-permute-done | bytes 294944 | tf_op jit(solution)/shard_map/ppermute | solution.py:28
  74.9 1.3 collective-permute-start.8
  76.2 4.0 %collective-permute-start.9 = (bf16[1,10,32,256]{3,2,1,0:T(8,128)(2,1)S(1)}, bf16[1,10,32,256]{3,2,1,0:T(8,128)(2,1)S(1)}, u32[]{:S(2)}, u32[]{:S(2)}) collective-permute-start(bf16[1,10,32,256]{3,2,1,0:T(8,128)(2,1)S(1)} %fusion.75), channel_id=1, source_target_pairs={{0,64},{64,128},{128,192},{192,256},{256,320},{320,384},{384,448},... | collective-permute-start | bytes 491528 | tf_op jit(solution)/shard_map/ppermute | solution.py:17
  80.9 1.5 collective-permute-done.9
  83.8 1.3 collective-permute-start.10
  85.1 4.4 %collective-permute-start.11 = (bf16[1,8,32,256]{3,2,1,0:T(8,128)(2,1)S(1)}, bf16[1,8,32,256]{3,2,1,0:T(8,128)(2,1)S(1)}, u32[]{:S(2)}, u32[]{:S(2)}) collective-permute-start(bf16[1,8,32,256]{3,2,1,0:T(8,128)(2,1)S(1)} %get-tuple-element.5), channel_id=1, source_target_pairs={{0,64},{64,128},{128,192},{192,256},{256,320},{320,384},{384,448},... | collective-permute-start | bytes 393224 | tf_op jit(solution)/shard_map/ppermute | solution.py:17
  89.9 1.5 collective-permute-done.11
  92.7 1.3 collective-permute-start.12
  94.0 4.4 %collective-permute-start.13 = (bf16[1,6,32,256]{3,2,1,0:T(8,128)(2,1)S(1)}, bf16[1,6,32,256]{3,2,1,0:T(8,128)(2,1)S(1)}, u32[]{:S(2)}, u32[]{:S(2)}) collective-permute-start(bf16[1,6,32,256]{3,2,1,0:T(8,128)(2,1)S(1)} %get-tuple-element.60), channel_id=1, source_target_pairs={{0,64},{64,128},{128,192},{192,256},{256,320},{320,384},{384,448},... | collective-permute-start | bytes 294920 | tf_op jit(solution)/shard_map/ppermute | solution.py:17
  98.5 1.6 collective-permute-done.13
  101.2 1.3 collective-permute-start.14
  102.5 4.4 %collective-permute-start.15 = (bf16[1,4,32,256]{3,2,1,0:T(8,128)(2,1)S(1)}, bf16[1,4,32,256]{3,2,1,0:T(8,128)(2,1)S(1)}, u32[]{:S(2)}, u32[]{:S(2)}) collective-permute-start(bf16[1,4,32,256]{3,2,1,0:T(8,128)(2,1)S(1)} %get-tuple-element.62), channel_id=1, source_target_pairs={{0,64},{64,128},{128,192},{192,256},{256,320},{320,384},{384,448},... | collective-permute-start | bytes 196616 | tf_op jit(solution)/shard_map/ppermute | solution.py:17
  109.3 5.3 %collective-permute-start.16 = (bf16[1,2,32,256]{3,2,1,0:T(8,128)(2,1)S(1)}, bf16[1,2,32,256]{3,2,1,0:T(8,128)(2,1)S(1)}, u32[]{:S(2)}, u32[]{:S(2)}) collective-permute-start(bf16[1,2,32,256]{3,2,1,0:T(8,128)(2,1)S(1)} %fusion.39), channel_id=1, source_target_pairs={{0,2},{1,3},{2,4},{3,5},{4,6},{5,7},{6,8},{7,9},{8,10},{9,11},{10,... | collective-permute-start | bytes 98312 | tf_op jit(solution)/shard_map/ppermute | solution.py:28
  114.6 6.0 %collective-permute-start.17 = (bf16[1,2,32,256]{3,2,1,0:T(8,128)(2,1)S(1)}, bf16[1,2,32,256]{3,2,1,0:T(8,128)(2,1)S(1)}, u32[]{:S(2)}, u32[]{:S(2)}) collective-permute-start(bf16[1,2,32,256]{3,2,1,0:T(8,128)(2,1)S(1)} %fusion.39), channel_id=1, source_target_pairs={{0,1},{1,2},{2,3},{3,4},{4,5},{5,6},{6,7},{7,8},{8,9},{9,10},{10,1... | collective-permute-start | bytes 98312 | tf_op jit(solution)/shard_map/ppermute | solution.py:28
  120.6 1.9 collective-permute-start.18
  122.6 1.3 collective-permute-start.19
  123.9 1.9 collective-permute-done.18
  125.9 1.3 collective-permute-done.19
  127.3 1.3 collective-permute-start.20
  128.6 4.6 %collective-permute-start.21 = (bf16[1,10,32,256]{3,2,1,0:T(8,128)(2,1)S(1)}, bf16[1,10,32,256]{3,2,1,0:T(8,128)(2,1)S(1)}, u32[]{:S(2)}, u32[]{:S(2)}) collective-permute-start(bf16[1,10,32,256]{3,2,1,0:T(8,128)(2,1)S(1)} %fusion.76), channel_id=1, source_target_pairs={{0,64},{64,128},{128,192},{192,256},{256,320},{320,384},{384,448},... | collective-permute-start | bytes 491528 | tf_op jit(solution)/shard_map/ppermute | solution.py:17
  133.3 1.2 collective-permute-done.20
  136.8 1.3 collective-permute-start.22
  138.1 4.7 %collective-permute-start.23 = (bf16[1,8,32,256]{3,2,1,0:T(8,128)(2,1)S(1)}, bf16[1,8,32,256]{3,2,1,0:T(8,128)(2,1)S(1)}, u32[]{:S(2)}, u32[]{:S(2)}) collective-permute-start(bf16[1,8,32,256]{3,2,1,0:T(8,128)(2,1)S(1)} %get-tuple-element.3), channel_id=1, source_target_pairs={{0,64},{64,128},{128,192},{192,256},{256,320},{320,384},{384,448},... | collective-permute-start | bytes 393224 | tf_op jit(solution)/shard_map/ppermute | solution.py:17
  143.5 1.3 collective-permute-done.23
  146.7 1.3 collective-permute-start.24
  148.0 5.8 %collective-permute-start.25 = (bf16[1,6,32,256]{3,2,1,0:T(8,128)(2,1)}, bf16[1,6,32,256]{3,2,1,0:T(8,128)(2,1)}, u32[]{:S(2)}, u32[]{:S(2)}) collective-permute-start(bf16[1,6,32,256]{3,2,1,0:T(8,128)(2,1)} %get-tuple-element.64), channel_id=1, source_target_pairs={{0,64},{64,128},{128,192},{192,256},{256,320},{320,384},{384,448},... | collective-permute-start | bytes 294920 | tf_op jit(solution)/shard_map/ppermute | solution.py:17
  161.5 1.3 collective-permute-start.26
  162.8 5.8 %collective-permute-start.27 = (bf16[1,4,32,256]{3,2,1,0:T(8,128)(2,1)}, bf16[1,4,32,256]{3,2,1,0:T(8,128)(2,1)}, u32[]{:S(2)}, u32[]{:S(2)}) collective-permute-start(bf16[1,4,32,256]{3,2,1,0:T(8,128)(2,1)} %get-tuple-element.66), channel_id=1, source_target_pairs={{0,64},{64,128},{128,192},{192,256},{256,320},{320,384},{384,448},... | collective-permute-start | bytes 196616 | tf_op jit(solution)/shard_map/ppermute | solution.py:17
  173.0 1.4 all_to_all.17
  174.4 28.9 %all-to-all-start.1 = ((f32[512,1,256]{2,1,0:T(1,128)}), f32[512,1,256]{2,1,0:T(1,128)S(1)}, u32[]{:S(2)}, u32[]{:S(2)}) async-start(f32[512,1,256]{2,1,0:T(1,128)} %all_to_all.17), calls=%async_computation.1 | async-start | bytes 1048576 | tf_op jit(solution)/shard_map/all_to_all | solution.py:221
  203.8 22.3 %all-to-all-done.1 = f32[512,1,256]{2,1,0:T(1,128)S(1)} async-done(((f32[512,1,256]{2,1,0:T(1,128)}), f32[512,1,256]{2,1,0:T(1,128)S(1)}, u32[]{:S(2)}, u32[]{:S(2)}) %all-to-all-start.1) | async-done | bytes 524320 | tf_op jit(solution)/shard_map/all_to_all | solution.py:221
  227.3 4.2 %all-to-all-start.2 = ((f32[64,1,256]{2,1,0:T(1,128)}), f32[64,1,256]{2,1,0:T(1,128)S(1)}, u32[]{:S(2)}, u32[]{:S(2)}) async-start(f32[64,1,256]{2,1,0:T(1,128)} %broadcast_in_dim.22), calls=%async_computation.2 | async-start | bytes 131072 | tf_op jit(solution)/shard_map/all_to_all | solution.py:222
  232.3 9.0 %all-to-all-done.2 = f32[64,1,256]{2,1,0:T(1,128)S(1)} async-done(((f32[64,1,256]{2,1,0:T(1,128)}), f32[64,1,256]{2,1,0:T(1,128)S(1)}, u32[]{:S(2)}, u32[]{:S(2)}) %all-to-all-start.2) | async-done | bytes 65568 | tf_op jit(solution)/shard_map/all_to_all | solution.py:222
  (259 shorter events, 35.8 us)
Async XLA Ops:
  0.6 14.6 %copy-start.14 = (s32[1,12]{1,0:T(1,128)S(1)}, s32[1,12]{1,0:T(1,128)}, u32[]{:S(2)}) copy-start(s32[1,12]{1,0:T(1,128)} %param.9) | copy-start | bytes 148
  4.3 27.3 %all-to-all-start = ((bf16[8,112,256]{2,1,0:T(8,128)(2,1)}), bf16[8,112,256]{2,1,0:T(8,128)(2,1)S(1)}, u32[]{:S(2)}, u32[]{:S(2)}) async-start(bf16[8,112,256]{2,1,0:T(8,128)(2,1)} %pad_maximum_fusion), calls=%async_computation | async-start | bytes 917504 | tf_op jit(solution)/shard_map/all_to_all | solution.py:131
  33.5 6.9 %collective-permute-start = (bf16[8,1,1,32,256]{4,3,2,0,1:T(8,128)(2,1)}, bf16[8,1,1,32,256]{4,3,2,0,1:T(8,128)(2,1)S(1)}, u32[]{:S(2)}, u32[]{:S(2)}) collective-permute-start(bf16[8,1,1,32,256]{4,3,2,0,1:T(8,128)(2,1)} %get-tuple-element.48), channel_id=1, source_target_pairs={{0,1},{1,2},{2,3},{3,4},{4,5},{5,6},{6,7},{7,8},{8,9},{9,10},{10,1... | collective-permute-start | bytes 393224 | tf_op jit(solution)/shard_map/ppermute | solution.py:17
  37.2 6.5 %collective-permute-start.1 = (bf16[8,1,1,32,256]{4,3,2,0,1:T(8,128)(2,1)}, bf16[8,1,1,32,256]{4,3,2,0,1:T(8,128)(2,1)S(1)}, u32[]{:S(2)}, u32[]{:S(2)}) collective-permute-start(bf16[8,1,1,32,256]{4,3,2,0,1:T(8,128)(2,1)} %get-tuple-element.49), channel_id=1, source_target_pairs={{1,0},{2,1},{3,2},{4,3},{5,4},{6,5},{7,6},{8,7},{9,8},{10,9},{11,1... | collective-permute-start | bytes 393224 | tf_op jit(solution)/shard_map/ppermute | solution.py:20
  45.3 5.7 %collective-permute-start.2 = (bf16[8,1,2,32,256]{4,3,2,0,1:T(8,128)(2,1)S(1)}, bf16[8,1,2,32,256]{4,3,2,0,1:T(8,128)(2,1)S(1)}, u32[]{:S(2)}, u32[]{:S(2)}) collective-permute-start(bf16[8,1,2,32,256]{4,3,2,0,1:T(8,128)(2,1)S(1)} %fusion.12), channel_id=1, source_target_pairs={{0,64},{64,128},{128,192},{192,256},{256,320},{320,384},{384,448},... | collective-permute-start | bytes 786440 | tf_op jit(solution)/shard_map/ppermute | solution.py:17
  47.5 7.6 %collective-permute-start.3 = (bf16[8,1,2,32,256]{4,3,2,0,1:T(8,128)(2,1)S(1)}, bf16[8,1,2,32,256]{4,3,2,0,1:T(8,128)(2,1)S(1)}, u32[]{:S(2)}, u32[]{:S(2)}) collective-permute-start(bf16[8,1,2,32,256]{4,3,2,0,1:T(8,128)(2,1)S(1)} %fusion.12), channel_id=1, source_target_pairs={{64,0},{128,64},{192,128},{256,192},{320,256},{384,320},{448,384},... | collective-permute-start | bytes 786440 | tf_op jit(solution)/shard_map/ppermute | solution.py:20
  49.6 5.9 %copy-start.2 = (bf16[1,2,32,256]{3,2,1,0:T(8,128)(2,1)S(1)}, bf16[1,2,32,256]{3,2,1,0:T(8,128)(2,1)}, u32[]{:S(2)}) copy-start(bf16[1,2,32,256]{3,2,1,0:T(8,128)(2,1)} %param.6) | copy-start | bytes 98308
  51.0 56.4 %copy-start.8 = (bf16[8,1,2,32,256]{4,3,2,0,1:T(8,128)(2,1)}, bf16[8,1,2,32,256]{4,3,2,0,1:T(8,128)(2,1)S(1)}, u32[]{:S(2)}) copy-start(bf16[8,1,2,32,256]{4,3,2,0,1:T(8,128)(2,1)S(1)} %collective-permute-done.2) | copy-start | bytes 786436
  55.1 52.3 %copy-start.9 = (bf16[8,1,2,32,256]{4,3,2,0,1:T(8,128)(2,1)}, bf16[8,1,2,32,256]{4,3,2,0,1:T(8,128)(2,1)S(1)}, u32[]{:S(2)}) copy-start(bf16[8,1,2,32,256]{4,3,2,0,1:T(8,128)(2,1)S(1)} %collective-permute-done.3) | copy-start | bytes 786436
  55.6 13.1 %collective-permute-start.4 = (bf16[5,1,2,32,256]{4,3,2,1,0:T(8,128)(2,1)S(1)}, bf16[5,1,2,32,256]{4,3,2,1,0:T(8,128)(2,1)S(1)}, u32[]{:S(2)}, u32[]{:S(2)}) collective-permute-start(bf16[5,1,2,32,256]{4,3,2,1,0:T(8,128)(2,1)S(1)} %pad_maximum_fusion.4), channel_id=1, source_target_pairs={{0,2},{1,3},{2,4},{3,5},{4,6},{5,7},{6,8},{7,9},{8,10},{9,11},{10,... | collective-permute-start | bytes 491528 | tf_op jit(solution)/shard_map/ppermute | solution.py:28
  60.6 8.1 %collective-permute-start.7 = (bf16[5,1,2,32,256]{4,3,2,1,0:T(8,128)(2,1)S(1)}, bf16[5,1,2,32,256]{4,3,2,1,0:T(8,128)(2,1)S(1)}, u32[]{:S(2)}, u32[]{:S(2)}) collective-permute-start(bf16[5,1,2,32,256]{4,3,2,1,0:T(8,128)(2,1)S(1)} %pad_maximum_fusion.4), channel_id=1, source_target_pairs={{2,0},{3,1},{4,2},{5,3},{6,4},{7,5},{8,6},{9,7},{10,8},{11,9},{12,... | collective-permute-start | bytes 491528 | tf_op jit(solution)/shard_map/ppermute | solution.py:28
  61.9 8.4 %collective-permute-start.5 = (bf16[9,1,2,32,256]{4,3,2,1,0:T(8,128)(2,1)S(1)}, bf16[9,1,2,32,256]{4,3,2,1,0:T(8,128)(2,1)S(1)}, u32[]{:S(2)}, u32[]{:S(2)}) collective-permute-start(bf16[9,1,2,32,256]{4,3,2,1,0:T(8,128)(2,1)S(1)} %pad_maximum_fusion.1), channel_id=1, source_target_pairs={{0,1},{1,2},{2,3},{3,4},{4,5},{5,6},{6,7},{7,8},{8,9},{9,10},{10,1... | collective-permute-start | bytes 884744 | tf_op jit(solution)/shard_map/ppermute | solution.py:28
  66.7 8.0 %collective-permute-start.6 = (bf16[9,1,2,32,256]{4,3,2,1,0:T(8,128)(2,1)S(1)}, bf16[9,1,2,32,256]{4,3,2,1,0:T(8,128)(2,1)S(1)}, u32[]{:S(2)}, u32[]{:S(2)}) collective-permute-start(bf16[9,1,2,32,256]{4,3,2,1,0:T(8,128)(2,1)S(1)} %pad_maximum_fusion.1), channel_id=1, source_target_pairs={{1,0},{2,1},{3,2},{4,3},{5,4},{6,5},{7,6},{8,7},{9,8},{10,9},{11,1... | collective-permute-start | bytes 884744 | tf_op jit(solution)/shard_map/ppermute | solution.py:28
  74.9 6.1 %collective-permute-start.8 = (bf16[1,10,32,256]{3,2,1,0:T(8,128)(2,1)S(1)}, bf16[1,10,32,256]{3,2,1,0:T(8,128)(2,1)S(1)}, u32[]{:S(2)}, u32[]{:S(2)}) collective-permute-start(bf16[1,10,32,256]{3,2,1,0:T(8,128)(2,1)S(1)} %fusion.75), channel_id=1, source_target_pairs={{64,0},{128,64},{192,128},{256,192},{320,256},{384,320},{448,384},... | collective-permute-start | bytes 491528 | tf_op jit(solution)/shard_map/ppermute | solution.py:20
  76.2 6.2 %collective-permute-start.9 = (bf16[1,10,32,256]{3,2,1,0:T(8,128)(2,1)S(1)}, bf16[1,10,32,256]{3,2,1,0:T(8,128)(2,1)S(1)}, u32[]{:S(2)}, u32[]{:S(2)}) collective-permute-start(bf16[1,10,32,256]{3,2,1,0:T(8,128)(2,1)S(1)} %fusion.75), channel_id=1, source_target_pairs={{0,64},{64,128},{128,192},{192,256},{256,320},{320,384},{384,448},... | collective-permute-start | bytes 491528 | tf_op jit(solution)/shard_map/ppermute | solution.py:17
  83.8 6.2 %collective-permute-start.10 = (bf16[1,8,32,256]{3,2,1,0:T(8,128)(2,1)S(1)}, bf16[1,8,32,256]{3,2,1,0:T(8,128)(2,1)S(1)}, u32[]{:S(2)}, u32[]{:S(2)}) collective-permute-start(bf16[1,8,32,256]{3,2,1,0:T(8,128)(2,1)S(1)} %get-tuple-element.5), channel_id=1, source_target_pairs={{64,0},{128,64},{192,128},{256,192},{320,256},{384,320},{448,384},... | collective-permute-start | bytes 393224 | tf_op jit(solution)/shard_map/ppermute | solution.py:20
  85.1 6.4 %collective-permute-start.11 = (bf16[1,8,32,256]{3,2,1,0:T(8,128)(2,1)S(1)}, bf16[1,8,32,256]{3,2,1,0:T(8,128)(2,1)S(1)}, u32[]{:S(2)}, u32[]{:S(2)}) collective-permute-start(bf16[1,8,32,256]{3,2,1,0:T(8,128)(2,1)S(1)} %get-tuple-element.5), channel_id=1, source_target_pairs={{0,64},{64,128},{128,192},{192,256},{256,320},{320,384},{384,448},... | collective-permute-start | bytes 393224 | tf_op jit(solution)/shard_map/ppermute | solution.py:17
  89.6 3.1 %copy-start = (bf16[1,1,2,288,256]{4,3,2,0,1:T(8,128)(2,1)}, bf16[1,1,2,288,256]{4,3,2,0,1:T(8,128)(2,1)S(1)}, u32[]{:S(2)}) copy-start(bf16[1,1,2,288,256]{4,3,2,0,1:T(8,128)(2,1)S(1)} %constant_dynamic-update-slice_fusion.83) | copy-start | bytes 884740
  92.4 8.5 %copy-start.4 = (bf16[1,9,32,32]{3,2,1,0:T(8,128)(2,1)S(1)}, bf16[1,9,32,32]{3,2,1,0:T(8,128)(2,1)}, u32[]{:S(2)}) copy-start(bf16[1,9,32,32]{3,2,1,0:T(8,128)(2,1)} %get-tuple-element.21) | copy-start | bytes 55300
  92.7 5.8 %collective-permute-start.12 = (bf16[1,6,32,256]{3,2,1,0:T(8,128)(2,1)S(1)}, bf16[1,6,32,256]{3,2,1,0:T(8,128)(2,1)S(1)}, u32[]{:S(2)}, u32[]{:S(2)}) collective-permute-start(bf16[1,6,32,256]{3,2,1,0:T(8,128)(2,1)S(1)} %get-tuple-element.60), channel_id=1, source_target_pairs={{64,0},{128,64},{192,128},{256,192},{320,256},{384,320},{448,384},... | collective-permute-start | bytes 294920 | tf_op jit(solution)/shard_map/ppermute | solution.py:20
  94.0 6.0 %collective-permute-start.13 = (bf16[1,6,32,256]{3,2,1,0:T(8,128)(2,1)S(1)}, bf16[1,6,32,256]{3,2,1,0:T(8,128)(2,1)S(1)}, u32[]{:S(2)}, u32[]{:S(2)}) collective-permute-start(bf16[1,6,32,256]{3,2,1,0:T(8,128)(2,1)S(1)} %get-tuple-element.60), channel_id=1, source_target_pairs={{0,64},{64,128},{128,192},{192,256},{256,320},{320,384},{384,448},... | collective-permute-start | bytes 294920 | tf_op jit(solution)/shard_map/ppermute | solution.py:17
  101.2 6.3 %collective-permute-start.14 = (bf16[1,4,32,256]{3,2,1,0:T(8,128)(2,1)S(1)}, bf16[1,4,32,256]{3,2,1,0:T(8,128)(2,1)S(1)}, u32[]{:S(2)}, u32[]{:S(2)}) collective-permute-start(bf16[1,4,32,256]{3,2,1,0:T(8,128)(2,1)S(1)} %get-tuple-element.62), channel_id=1, source_target_pairs={{64,0},{128,64},{192,128},{256,192},{320,256},{384,320},{448,384},... | collective-permute-start | bytes 196616 | tf_op jit(solution)/shard_map/ppermute | solution.py:20
  102.5 5.9 %collective-permute-start.15 = (bf16[1,4,32,256]{3,2,1,0:T(8,128)(2,1)S(1)}, bf16[1,4,32,256]{3,2,1,0:T(8,128)(2,1)S(1)}, u32[]{:S(2)}, u32[]{:S(2)}) collective-permute-start(bf16[1,4,32,256]{3,2,1,0:T(8,128)(2,1)S(1)} %get-tuple-element.62), channel_id=1, source_target_pairs={{0,64},{64,128},{128,192},{192,256},{256,320},{320,384},{384,448},... | collective-permute-start | bytes 196616 | tf_op jit(solution)/shard_map/ppermute | solution.py:17
  107.5 25.7 %slice-start = ((bf16[8,1,2,32,256]{4,3,2,0,1:T(8,128)(2,1)}), bf16[1,1,2,32,256]{4,3,2,0,1:T(8,128)(2,1)S(1)}, s32[]{:S(2)}) async-start(bf16[8,1,2,32,256]{4,3,2,0,1:T(8,128)(2,1)} %copy-done.8), calls=%async_computation.3 | async-start | bytes 65536 | tf_op jit(solution)/shard_map/slice | solution.py:207
  107.5 25.7 %slice-start.2 = ((bf16[8,1,2,32,256]{4,3,2,0,1:T(8,128)(2,1)}), bf16[1,1,2,32,256]{4,3,2,0,1:T(8,128)(2,1)S(1)}, s32[]{:S(2)}) async-start(bf16[8,1,2,32,256]{4,3,2,0,1:T(8,128)(2,1)} %copy-done.9), calls=%async_computation.5 | async-start | bytes 65536 | tf_op jit(solution)/shard_map/slice | solution.py:207
  109.3 14.6 %collective-permute-start.16 = (bf16[1,2,32,256]{3,2,1,0:T(8,128)(2,1)S(1)}, bf16[1,2,32,256]{3,2,1,0:T(8,128)(2,1)S(1)}, u32[]{:S(2)}, u32[]{:S(2)}) collective-permute-start(bf16[1,2,32,256]{3,2,1,0:T(8,128)(2,1)S(1)} %fusion.39), channel_id=1, source_target_pairs={{0,2},{1,3},{2,4},{3,5},{4,6},{5,7},{6,8},{7,9},{8,10},{9,11},{10,... | collective-permute-start | bytes 98312 | tf_op jit(solution)/shard_map/ppermute | solution.py:28
  114.6 9.3 %collective-permute-start.17 = (bf16[1,2,32,256]{3,2,1,0:T(8,128)(2,1)S(1)}, bf16[1,2,32,256]{3,2,1,0:T(8,128)(2,1)S(1)}, u32[]{:S(2)}, u32[]{:S(2)}) collective-permute-start(bf16[1,2,32,256]{3,2,1,0:T(8,128)(2,1)S(1)} %fusion.39), channel_id=1, source_target_pairs={{0,1},{1,2},{2,3},{3,4},{4,5},{5,6},{6,7},{7,8},{8,9},{9,10},{10,1... | collective-permute-start | bytes 98312 | tf_op jit(solution)/shard_map/ppermute | solution.py:28
  120.6 5.2 %collective-permute-start.18 = (bf16[1,2,32,256]{3,2,1,0:T(8,128)(2,1)S(1)}, bf16[1,2,32,256]{3,2,1,0:T(8,128)(2,1)S(1)}, u32[]{:S(2)}, u32[]{:S(2)}) collective-permute-start(bf16[1,2,32,256]{3,2,1,0:T(8,128)(2,1)S(1)} %fusion.39), channel_id=1, source_target_pairs={{1,0},{2,1},{3,2},{4,3},{5,4},{6,5},{7,6},{8,7},{9,8},{10,9},{11,1... | collective-permute-start | bytes 98312 | tf_op jit(solution)/shard_map/ppermute | solution.py:28
  122.6 4.7 %collective-permute-start.19 = (bf16[1,2,32,256]{3,2,1,0:T(8,128)(2,1)S(1)}, bf16[1,2,32,256]{3,2,1,0:T(8,128)(2,1)S(1)}, u32[]{:S(2)}, u32[]{:S(2)}) collective-permute-start(bf16[1,2,32,256]{3,2,1,0:T(8,128)(2,1)S(1)} %fusion.39), channel_id=1, source_target_pairs={{2,0},{3,1},{4,2},{5,3},{6,4},{7,5},{8,6},{9,7},{10,8},{11,9},{12,... | collective-permute-start | bytes 98312 | tf_op jit(solution)/shard_map/ppermute | solution.py:28
  127.3 7.2 %collective-permute-start.20 = (bf16[1,10,32,256]{3,2,1,0:T(8,128)(2,1)S(1)}, bf16[1,10,32,256]{3,2,1,0:T(8,128)(2,1)S(1)}, u32[]{:S(2)}, u32[]{:S(2)}) collective-permute-start(bf16[1,10,32,256]{3,2,1,0:T(8,128)(2,1)S(1)} %fusion.76), channel_id=1, source_target_pairs={{64,0},{128,64},{192,128},{256,192},{320,256},{384,320},{448,384},... | collective-permute-start | bytes 491528 | tf_op jit(solution)/shard_map/ppermute | solution.py:20
  128.6 6.9 %collective-permute-start.21 = (bf16[1,10,32,256]{3,2,1,0:T(8,128)(2,1)S(1)}, bf16[1,10,32,256]{3,2,1,0:T(8,128)(2,1)S(1)}, u32[]{:S(2)}, u32[]{:S(2)}) collective-permute-start(bf16[1,10,32,256]{3,2,1,0:T(8,128)(2,1)S(1)} %fusion.76), channel_id=1, source_target_pairs={{0,64},{64,128},{128,192},{192,256},{256,320},{320,384},{384,448},... | collective-permute-start | bytes 491528 | tf_op jit(solution)/shard_map/ppermute | solution.py:17
  135.4 1.0 copy-start.5
  136.8 6.7 %collective-permute-start.22 = (bf16[1,8,32,256]{3,2,1,0:T(8,128)(2,1)S(1)}, bf16[1,8,32,256]{3,2,1,0:T(8,128)(2,1)S(1)}, u32[]{:S(2)}, u32[]{:S(2)}) collective-permute-start(bf16[1,8,32,256]{3,2,1,0:T(8,128)(2,1)S(1)} %get-tuple-element.3), channel_id=1, source_target_pairs={{64,0},{128,64},{192,128},{256,192},{320,256},{384,320},{448,384},... | collective-permute-start | bytes 393224 | tf_op jit(solution)/shard_map/ppermute | solution.py:20
  138.1 6.7 %collective-permute-start.23 = (bf16[1,8,32,256]{3,2,1,0:T(8,128)(2,1)S(1)}, bf16[1,8,32,256]{3,2,1,0:T(8,128)(2,1)S(1)}, u32[]{:S(2)}, u32[]{:S(2)}) collective-permute-start(bf16[1,8,32,256]{3,2,1,0:T(8,128)(2,1)S(1)} %get-tuple-element.3), channel_id=1, source_target_pairs={{0,64},{64,128},{128,192},{192,256},{256,320},{320,384},{384,448},... | collective-permute-start | bytes 393224 | tf_op jit(solution)/shard_map/ppermute | solution.py:17
  145.2 9.4 %slice-start.1 = ((bf16[8,1,2,32,256]{4,3,2,0,1:T(8,128)(2,1)}), bf16[7,1,2,32,256]{4,3,2,0,1:T(8,128)(2,1)S(1)}, s32[]{:S(2)}) async-start(bf16[8,1,2,32,256]{4,3,2,0,1:T(8,128)(2,1)} %copy-done.8), calls=%async_computation.4 | async-start | bytes 458752 | tf_op jit(solution)/shard_map/slice | solution.py:207
  145.2 9.4 %slice-start.3 = ((bf16[8,1,2,32,256]{4,3,2,0,1:T(8,128)(2,1)}), bf16[7,1,2,32,256]{4,3,2,0,1:T(8,128)(2,1)S(1)}, s32[]{:S(2)}) async-start(bf16[8,1,2,32,256]{4,3,2,0,1:T(8,128)(2,1)} %copy-done.9), calls=%async_computation.6 | async-start | bytes 458752 | tf_op jit(solution)/shard_map/slice | solution.py:207
  146.7 12.0 %collective-permute-start.24 = (bf16[1,6,32,256]{3,2,1,0:T(8,128)(2,1)}, bf16[1,6,32,256]{3,2,1,0:T(8,128)(2,1)}, u32[]{:S(2)}, u32[]{:S(2)}) collective-permute-start(bf16[1,6,32,256]{3,2,1,0:T(8,128)(2,1)} %get-tuple-element.64), channel_id=1, source_target_pairs={{64,0},{128,64},{192,128},{256,192},{320,256},{384,320},{448,384},... | collective-permute-start | bytes 294920 | tf_op jit(solution)/shard_map/ppermute | solution.py:20
  148.0 10.7 %collective-permute-start.25 = (bf16[1,6,32,256]{3,2,1,0:T(8,128)(2,1)}, bf16[1,6,32,256]{3,2,1,0:T(8,128)(2,1)}, u32[]{:S(2)}, u32[]{:S(2)}) collective-permute-start(bf16[1,6,32,256]{3,2,1,0:T(8,128)(2,1)} %get-tuple-element.64), channel_id=1, source_target_pairs={{0,64},{64,128},{128,192},{192,256},{256,320},{320,384},{384,448},... | collective-permute-start | bytes 294920 | tf_op jit(solution)/shard_map/ppermute | solution.py:17
  156.8 3.8 %copy-start.3 = (bf16[1,9,32,32]{3,2,1,0:T(8,128)(2,1)S(1)}, bf16[1,9,32,32]{3,2,1,0:T(8,128)(2,1)}, u32[]{:S(2)}) copy-start(bf16[1,9,32,32]{3,2,1,0:T(8,128)(2,1)} %get-tuple-element.17) | copy-start | bytes 55300
  157.5 3.0 %copy-start.7 = (bf16[1,6,32,256]{3,2,1,0:T(8,128)(2,1)S(1)}, bf16[1,6,32,256]{3,2,1,0:T(8,128)(2,1)}, u32[]{:S(2)}) copy-start(bf16[1,6,32,256]{3,2,1,0:T(8,128)(2,1)} %get-tuple-element.65) | copy-start | bytes 294916
  157.5 3.1 %copy-start.10 = (f32[1,2,32,256]{3,2,1,0:T(8,128)S(1)}, f32[1,2,32,256]{3,2,1,0:T(8,128)}, u32[]{:S(2)}) copy-start(f32[1,2,32,256]{3,2,1,0:T(8,128)} %slice_bitcast_fusion.2) | copy-start | bytes 196612
  157.6 3.1 %copy-start.12 = (f32[1,1,32,256]{3,2,1,0:T(8,128)S(1)}, f32[1,1,32,256]{3,2,1,0:T(8,128)}, u32[]{:S(2)}) copy-start(f32[1,1,32,256]{3,2,1,0:T(8,128)} %get-tuple-element.75) | copy-start | bytes 98308
  161.5 9.7 %collective-permute-start.26 = (bf16[1,4,32,256]{3,2,1,0:T(8,128)(2,1)}, bf16[1,4,32,256]{3,2,1,0:T(8,128)(2,1)S(1)}, u32[]{:S(2)}, u32[]{:S(2)}) collective-permute-start(bf16[1,4,32,256]{3,2,1,0:T(8,128)(2,1)} %get-tuple-element.66), channel_id=1, source_target_pairs={{64,0},{128,64},{192,128},{256,192},{320,256},{384,320},{448,384},... | collective-permute-start | bytes 196616 | tf_op jit(solution)/shard_map/ppermute | solution.py:20
  162.8 8.4 %collective-permute-start.27 = (bf16[1,4,32,256]{3,2,1,0:T(8,128)(2,1)}, bf16[1,4,32,256]{3,2,1,0:T(8,128)(2,1)}, u32[]{:S(2)}, u32[]{:S(2)}) collective-permute-start(bf16[1,4,32,256]{3,2,1,0:T(8,128)(2,1)} %get-tuple-element.66), channel_id=1, source_target_pairs={{0,64},{64,128},{128,192},{192,256},{256,320},{320,384},{384,448},... | collective-permute-start | bytes 196616 | tf_op jit(solution)/shard_map/ppermute | solution.py:17
  170.4 2.1 copy-start.1
  173.0 58.5 %copy-start.11 = (bf16[1,4,32,256]{3,2,1,0:T(8,128)(2,1)S(1)}, bf16[1,4,32,256]{3,2,1,0:T(8,128)(2,1)}, u32[]{:S(2)}) copy-start(bf16[1,4,32,256]{3,2,1,0:T(8,128)(2,1)} %get-tuple-element.67) | copy-start | bytes 196612
  174.4 51.6 %all-to-all-start.1 = ((f32[512,1,256]{2,1,0:T(1,128)}), f32[512,1,256]{2,1,0:T(1,128)S(1)}, u32[]{:S(2)}, u32[]{:S(2)}) async-start(f32[512,1,256]{2,1,0:T(1,128)} %all_to_all.17), calls=%async_computation.1 | async-start | bytes 1048576 | tf_op jit(solution)/shard_map/all_to_all | solution.py:221
  227.3 14.0 %all-to-all-start.2 = ((f32[64,1,256]{2,1,0:T(1,128)}), f32[64,1,256]{2,1,0:T(1,128)S(1)}, u32[]{:S(2)}, u32[]{:S(2)}) async-start(f32[64,1,256]{2,1,0:T(1,128)} %broadcast_in_dim.22), calls=%async_computation.2 | async-start | bytes 131072 | tf_op jit(solution)/shard_map/all_to_all | solution.py:222
  (2 other events, 1.9 us)

commit v13 on v12

--- a/solution.py
+++ b/solution.py
@@ -6,7 +6,7 @@
 from jax.sharding import PartitionSpec as P
 
 TILE = 128
-HALO = 4
+HALO = 6
 
 
 def padded_2(block, sides, width):

time: 244 us -> 249 us (1.020)
  waiting for transfers between devices: 75.5 us -> 95.9 us
  starting transfers between devices: 129 us -> 112 us
    ppermute x10, waiting for transfers between devices: 9.76 us -> 27.6 us  [padded_2(): lax.ppermute(lax.slice_in_dim(block, 0, width, axis=dim), axis, backward)]
    all_to_all x1, starting transfers between devices: 28.9 us -> 20.3 us  [local(): part = lax.all_to_all(flat, ('segment', 'gy'), 0, 0, tiled=True).sum(axis=0)]
    ppermute x10, starting transfers between devices: 44.1 us -> 35.9 us  [padded_2(): lax.ppermute(lax.slice_in_dim(block, block.shape[dim] - width, None, axis...]
  transfers between devices with their start and end apart: 31 -> 31, of which waited for: 19 -> 20; matrix products, arithmetic and copies ran while one was open for 5% -> 5% of each run, Pallas kernels for 0% -> 0%
where the time goes in v13:
time: 249 us; the launch traced here: 247 us
  starting transfers between devices  112 us (45%)
  waiting for transfers between devices  95.9 us (39%)
  local copies, waits for them, and re-layouts  20.5 us (8%)
  matrix products  10.6 us (4%)
  other arithmetic  5.54 us (2%)
    ppermute x10, starting transfers between devices, padded_2(): lax.ppermute(lax.slice_in_dim(block, block.shape[dim] - width, None, axis...  35.9 us
    ppermute x10, waiting for transfers between devices, padded_2(): lax.ppermute(lax.slice_in_dim(block, 0, width, axis=dim), axis, backward)  27.6 us
    ppermute x8, starting transfers between devices, passed_along(): return lax.ppermute(block, axis, route)  27 us
    all_to_all x1, waiting for transfers between devices, local(): part = lax.all_to_all(flat, ('segment', 'gy'), 0, 0, tiled=True).sum(axis=0)  22.3 us
    all_to_all x1, starting transfers between devices, local(): part = lax.all_to_all(flat, ('segment', 'gy'), 0, 0, tiled=True).sum(axis=0)  20.3 us
    all_to_all x1, waiting for transfers between devices, local(): got = lax.all_to_all(send, 'segment', 0, 0, tiled=True)  16.2 us
    ppermute x10, starting transfers between devices, padded_2(): lax.ppermute(lax.slice_in_dim(block, 0, width, axis=dim), axis, backward)  14.3 us
    all_to_all x1, starting transfers between devices, local(): got = lax.all_to_all(send, 'segment', 0, 0, tiled=True)  10.9 us
  transfers between devices with their start and end apart: 31, of which 20 were waited for; matrix products, arithmetic and copies ran while one was open for 5% of the time, Pallas kernels for 0%

profile of v13, /device:TPU:1, one launch (start us, length us, event | category | flops | bytes accessed | tf_op | source)
XLA Modules:
  0.0 247.4 jit_solution(1197005659353913309)
XLA Ops:
  2.5 1.8 pad_maximum_fusion
  4.3 10.9 %all-to-all-start = ((bf16[8,112,256]{2,1,0:T(8,128)(2,1)}), bf16[8,112,256]{2,1,0:T(8,128)(2,1)S(1)}, u32[]{:S(2)}, u32[]{:S(2)}) async-start(bf16[8,112,256]{2,1,0:T(8,128)(2,1)} %pad_maximum_fusion), calls=%async_computation | async-start | bytes 917504 | tf_op jit(solution)/shard_map/all_to_all | solution.py:131
  15.5 16.2 %all-to-all-done = bf16[8,112,256]{2,1,0:T(8,128)(2,1)S(1)} async-done(((bf16[8,112,256]{2,1,0:T(8,128)(2,1)}), bf16[8,112,256]{2,1,0:T(8,128)(2,1)S(1)}, u32[]{:S(2)}, u32[]{:S(2)}) %all-to-all-start) | async-done | bytes 458784 | tf_op jit(solution)/shard_map/all_to_all | solution.py:131
  33.8 2.5 %collective-permute-start.1 = (bf16[8,1,1,32,256]{4,3,2,0,1:T(8,128)(2,1)}, bf16[8,1,1,32,256]{4,3,2,0,1:T(8,128)(2,1)S(1)}, u32[]{:S(2)}, u32[]{:S(2)}) collective-permute-start(bf16[8,1,1,32,256]{4,3,2,0,1:T(8,128)(2,1)} %get-tuple-element.47), channel_id=1, source_target_pairs={{1,0},{2,1},{3,2},{4,3},{5,4},{6,5},{7,6},{8,7},{9,8},{10,9},{11,1... | collective-permute-start | bytes 393224 | tf_op jit(solution)/shard_map/ppermute | solution.py:20
  36.2 3.1 %collective-permute-start = (bf16[8,1,1,32,256]{4,3,2,0,1:T(8,128)(2,1)S(1)}, bf16[8,1,1,32,256]{4,3,2,0,1:T(8,128)(2,1)S(1)}, u32[]{:S(2)}, u32[]{:S(2)}) collective-permute-start(bf16[8,1,1,32,256]{4,3,2,0,1:T(8,128)(2,1)S(1)} %get-tuple-element.46), channel_id=1, source_target_pairs={{0,1},{1,2},{2,3},{3,4},{4,5},{5,6},{6,7},{7,8},{8,9},{9,10},{10,1... | collective-permute-start | bytes 393224 | tf_op jit(solution)/shard_map/ppermute | solution.py:17
  42.9 1.3 collective-permute-start.3
  44.2 4.0 %collective-permute-start.2 = (bf16[8,1,2,32,256]{4,3,2,0,1:T(8,128)(2,1)S(1)}, bf16[8,1,2,32,256]{4,3,2,0,1:T(8,128)(2,1)S(1)}, u32[]{:S(2)}, u32[]{:S(2)}) collective-permute-start(bf16[8,1,2,32,256]{4,3,2,0,1:T(8,128)(2,1)S(1)} %fusion.20), channel_id=1, source_target_pairs={{0,64},{64,128},{128,192},{192,256},{256,320},{320,384},{384,448},... | collective-permute-start | bytes 786440 | tf_op jit(solution)/shard_map/ppermute | solution.py:17
  49.0 2.7 %collective-permute-done.3 = bf16[8,1,2,32,256]{4,3,2,0,1:T(8,128)(2,1)S(1)} collective-permute-done((bf16[8,1,2,32,256]{4,3,2,0,1:T(8,128)(2,1)S(1)}, bf16[8,1,2,32,256]{4,3,2,0,1:T(8,128)(2,1)S(1)}, u32[]{:S(2)}, u32[]{:S(2)}) %collective-permute-start.3) | collective-permute-done | bytes 262176 | tf_op jit(solution)/shard_map/ppermute | solution.py:20
  51.7 1.8 collective-permute-done.2
  53.8 1.9 collective-permute-start.7
  55.7 4.4 %collective-permute-start.6 = (bf16[9,1,2,32,256]{4,3,2,1,0:T(8,128)(2,1)S(1)}, bf16[9,1,2,32,256]{4,3,2,1,0:T(8,128)(2,1)S(1)}, u32[]{:S(2)}, u32[]{:S(2)}) collective-permute-start(bf16[9,1,2,32,256]{4,3,2,1,0:T(8,128)(2,1)S(1)} %pad_maximum_fusion.1), channel_id=1, source_target_pairs={{0,1},{1,2},{2,3},{3,4},{4,5},{5,6},{6,7},{7,8},{8,9},{9,10},{10,1... | collective-permute-start | bytes 884744 | tf_op jit(solution)/shard_map/ppermute | solution.py:28
  60.2 1.3 collective-permute-start.8
  61.5 4.0 %collective-permute-start.5 = (bf16[5,1,2,32,256]{4,3,2,1,0:T(8,128)(2,1)S(1)}, bf16[5,1,2,32,256]{4,3,2,1,0:T(8,128)(2,1)S(1)}, u32[]{:S(2)}, u32[]{:S(2)}) collective-permute-start(bf16[5,1,2,32,256]{4,3,2,1,0:T(8,128)(2,1)S(1)} %pad_maximum_fusion.4), channel_id=1, source_target_pairs={{0,2},{1,3},{2,4},{3,5},{4,6},{5,7},{6,8},{7,9},{8,10},{9,11},{10,... | collective-permute-start | bytes 491528 | tf_op jit(solution)/shard_map/ppermute | solution.py:28
  65.5 4.7 %collective-permute-start.4 = (bf16[3,1,2,32,256]{4,3,2,1,0:T(8,128)(2,1)S(1)}, bf16[3,1,2,32,256]{4,3,2,1,0:T(8,128)(2,1)S(1)}, u32[]{:S(2)}, u32[]{:S(2)}) collective-permute-start(bf16[3,1,2,32,256]{4,3,2,1,0:T(8,128)(2,1)S(1)} %pad_maximum_fusion.5), channel_id=1, source_target_pairs={{0,3},{1,4},{2,5},{3,6},{4,7},{5,8},{6,9},{7,10},{8,11},{9,12},{10... | collective-permute-start | bytes 294920 | tf_op jit(solution)/shard_map/ppermute | solution.py:28
  70.3 2.5 collective-permute-done.4
  74.1 7.5 %collective-permute-done.9 = bf16[3,1,2,32,256]{4,3,2,1,0:T(8,128)(2,1)S(1)} collective-permute-done((bf16[3,1,2,32,256]{4,3,2,1,0:T(8,128)(2,1)S(1)}, bf16[3,1,2,32,256]{4,3,2,1,0:T(8,128)(2,1)S(1)}, u32[]{:S(2)}, u32[]{:S(2)}) %collective-permute-start.9) | collective-permute-done | bytes 98336 | tf_op jit(solution)/shard_map/ppermute | solution.py:28
  81.9 4.1 %collective-permute-start.11 = (bf16[1,14,32,256]{3,2,1,0:T(8,128)(2,1)S(1)}, bf16[1,14,32,256]{3,2,1,0:T(8,128)(2,1)S(1)}, u32[]{:S(2)}, u32[]{:S(2)}) collective-permute-start(bf16[1,14,32,256]{3,2,1,0:T(8,128)(2,1)S(1)} %fusion.83), channel_id=1, source_target_pairs={{0,64},{64,128},{128,192},{192,256},{256,320},{320,384},{384,448},... | collective-permute-start | bytes 688136 | tf_op jit(solution)/shard_map/ppermute | solution.py:17
  86.1 1.3 collective-permute-start.10
  87.4 3.0 %collective-permute-done.11 = bf16[1,14,32,256]{3,2,1,0:T(8,128)(2,1)S(1)} collective-permute-done((bf16[1,14,32,256]{3,2,1,0:T(8,128)(2,1)S(1)}, bf16[1,14,32,256]{3,2,1,0:T(8,128)(2,1)S(1)}, u32[]{:S(2)}, u32[]{:S(2)}) %collective-permute-start.11) | collective-permute-done | bytes 229408 | tf_op jit(solution)/shard_map/ppermute | solution.py:17
  90.4 4.1 %collective-permute-done.10 = bf16[1,14,32,256]{3,2,1,0:T(8,128)(2,1)S(1)} collective-permute-done((bf16[1,14,32,256]{3,2,1,0:T(8,128)(2,1)S(1)}, bf16[1,14,32,256]{3,2,1,0:T(8,128)(2,1)S(1)}, u32[]{:S(2)}, u32[]{:S(2)}) %collective-permute-start.10) | collective-permute-done | bytes 229408 | tf_op jit(solution)/shard_map/ppermute | solution.py:20
  96.1 2.2 collective-permute-start.13
  98.3 1.3 collective-permute-start.12
  99.6 3.0 %collective-permute-done.13 = bf16[1,12,32,256]{3,2,1,0:T(8,128)(2,1)S(1)} collective-permute-done((bf16[1,12,32,256]{3,2,1,0:T(8,128)(2,1)S(1)}, bf16[1,12,32,256]{3,2,1,0:T(8,128)(2,1)S(1)}, u32[]{:S(2)}, u32[]{:S(2)}) %collective-permute-start.13) | collective-permute-done | bytes 196640 | tf_op jit(solution)/shard_map/ppermute | solution.py:17
  102.7 3.8 %collective-permute-done.12 = bf16[1,12,32,256]{3,2,1,0:T(8,128)(2,1)S(1)} collective-permute-done((bf16[1,12,32,256]{3,2,1,0:T(8,128)(2,1)S(1)}, bf16[1,12,32,256]{3,2,1,0:T(8,128)(2,1)S(1)}, u32[]{:S(2)}, u32[]{:S(2)}) %collective-permute-start.12) | collective-permute-done | bytes 196640 | tf_op jit(solution)/shard_map/ppermute | solution.py:20
  108.0 4.4 %collective-permute-start.15 = (bf16[1,10,32,256]{3,2,1,0:T(8,128)(2,1)S(1)}, bf16[1,10,32,256]{3,2,1,0:T(8,128)(2,1)S(1)}, u32[]{:S(2)}, u32[]{:S(2)}) collective-permute-start(bf16[1,10,32,256]{3,2,1,0:T(8,128)(2,1)S(1)} %get-tuple-element.62), channel_id=1, source_target_pairs={{0,64},{64,128},{128,192},{192,256},{256,320},{320,384},{384,448},... | collective-permute-start | bytes 491528 | tf_op jit(solution)/shard_map/ppermute | solution.py:17
  112.4 1.3 collective-permute-start.14
  113.8 1.3 collective-permute-done.15
  115.2 3.8 %collective-permute-done.14 = bf16[1,10,32,256]{3,2,1,0:T(8,128)(2,1)S(1)} collective-permute-done((bf16[1,10,32,256]{3,2,1,0:T(8,128)(2,1)S(1)}, bf16[1,10,32,256]{3,2,1,0:T(8,128)(2,1)S(1)}, u32[]{:S(2)}, u32[]{:S(2)}) %collective-permute-start.14) | collective-permute-done | bytes 163872 | tf_op jit(solution)/shard_map/ppermute | solution.py:20
  120.3 2.9 %collective-permute-start.17 = (bf16[1,8,32,256]{3,2,1,0:T(8,128)(2,1)S(1)}, bf16[1,8,32,256]{3,2,1,0:T(8,128)(2,1)S(1)}, u32[]{:S(2)}, u32[]{:S(2)}) collective-permute-start(bf16[1,8,32,256]{3,2,1,0:T(8,128)(2,1)S(1)} %get-tuple-element.64), channel_id=1, source_target_pairs={{0,64},{64,128},{128,192},{192,256},{256,320},{320,384},{384,448},... | collective-permute-start | bytes 393224 | tf_op jit(solution)/shard_map/ppermute | solution.py:17
  123.2 1.3 collective-permute-start.16
  125.2 4.0 %collective-permute-done.16 = bf16[1,8,32,256]{3,2,1,0:T(8,128)(2,1)S(1)} collective-permute-done((bf16[1,8,32,256]{3,2,1,0:T(8,128)(2,1)S(1)}, bf16[1,8,32,256]{3,2,1,0:T(8,128)(2,1)S(1)}, u32[]{:S(2)}, u32[]{:S(2)}) %collective-permute-start.16) | collective-permute-done | bytes 131104 | tf_op jit(solution)/shard_map/ppermute | solution.py:20
  130.4 3.5 %collective-permute-start.19 = (bf16[1,6,32,256]{3,2,1,0:T(8,128)(2,1)S(1)}, bf16[1,6,32,256]{3,2,1,0:T(8,128)(2,1)S(1)}, u32[]{:S(2)}, u32[]{:S(2)}) collective-permute-start(bf16[1,6,32,256]{3,2,1,0:T(8,128)(2,1)S(1)} %get-tuple-element.66), channel_id=1, source_target_pairs={{0,64},{64,128},{128,192},{192,256},{256,320},{320,384},{384,448},... | collective-permute-start | bytes 294920 | tf_op jit(solution)/shard_map/ppermute | solution.py:17
  133.9 1.3 collective-permute-start.18
  135.5 3.7 %collective-permute-done.18 = bf16[1,6,32,256]{3,2,1,0:T(8,128)(2,1)S(1)} collective-permute-done((bf16[1,6,32,256]{3,2,1,0:T(8,128)(2,1)S(1)}, bf16[1,6,32,256]{3,2,1,0:T(8,128)(2,1)S(1)}, u32[]{:S(2)}, u32[]{:S(2)}) %collective-permute-start.18) | collective-permute-done | bytes 98336 | tf_op jit(solution)/shard_map/ppermute | solution.py:20
  140.4 3.7 %collective-permute-start.21 = (bf16[1,4,32,256]{3,2,1,0:T(8,128)(2,1)S(1)}, bf16[1,4,32,256]{3,2,1,0:T(8,128)(2,1)S(1)}, u32[]{:S(2)}, u32[]{:S(2)}) collective-permute-start(bf16[1,4,32,256]{3,2,1,0:T(8,128)(2,1)S(1)} %get-tuple-element.68), channel_id=1, source_target_pairs={{0,64},{64,128},{128,192},{192,256},{256,320},{320,384},{384,448},... | collective-permute-start | bytes 196616 | tf_op jit(solution)/shard_map/ppermute | solution.py:17
  144.0 1.3 collective-permute-start.20
  145.4 3.7 %collective-permute-done.20 = bf16[1,4,32,256]{3,2,1,0:T(8,128)(2,1)S(1)} collective-permute-done((bf16[1,4,32,256]{3,2,1,0:T(8,128)(2,1)S(1)}, bf16[1,4,32,256]{3,2,1,0:T(8,128)(2,1)S(1)}, u32[]{:S(2)}, u32[]{:S(2)}) %collective-permute-start.20) | collective-permute-done | bytes 65568 | tf_op jit(solution)/shard_map/ppermute | solution.py:20
  150.0 7.5 %collective-permute-start.23 = (bf16[1,2,32,256]{3,2,1,0:T(8,128)(2,1)S(1)}, bf16[1,2,32,256]{3,2,1,0:T(8,128)(2,1)S(1)}, u32[]{:S(2)}, u32[]{:S(2)}) collective-permute-start(bf16[1,2,32,256]{3,2,1,0:T(8,128)(2,1)S(1)} %fusion.52), channel_id=1, source_target_pairs={{1,0},{2,1},{3,2},{4,3},{5,4},{6,5},{7,6},{8,7},{9,8},{10,9},{11,1... | collective-permute-start | bytes 98312 | tf_op jit(solution)/shard_map/ppermute | solution.py:28
  157.5 1.9 collective-permute-start.22
  161.2 3.5 %collective-permute-start.25 = (bf16[1,6,32,256]{3,2,1,0:T(8,128)(2,1)}, bf16[1,6,32,256]{3,2,1,0:T(8,128)(2,1)}, u32[]{:S(2)}, u32[]{:S(2)}) collective-permute-start(bf16[1,6,32,256]{3,2,1,0:T(8,128)(2,1)} %fusion.112), channel_id=1, source_target_pairs={{0,64},{64,128},{128,192},{192,256},{256,320},{320,384},{384,448},... | collective-permute-start | bytes 294920 | tf_op jit(solution)/shard_map/ppermute | solution.py:17
  174.5 4.6 %collective-permute-start.27 = (bf16[1,4,32,256]{3,2,1,0:T(8,128)(2,1)S(1)}, bf16[1,4,32,256]{3,2,1,0:T(8,128)(2,1)}, u32[]{:S(2)}, u32[]{:S(2)}) collective-permute-start(bf16[1,4,32,256]{3,2,1,0:T(8,128)(2,1)S(1)} %get-tuple-element.3), channel_id=1, source_target_pairs={{0,64},{64,128},{128,192},{192,256},{256,320},{320,384},{384,448},... | collective-permute-start | bytes 196616 | tf_op jit(solution)/shard_map/ppermute | solution.py:17
  179.2 1.5 collective-permute-start.26
  182.5 1.8 collective-permute-done.26
  186.0 1.4 all_to_all.17
  187.4 20.3 %all-to-all-start.1 = ((f32[512,1,256]{2,1,0:T(1,128)}), f32[512,1,256]{2,1,0:T(1,128)S(1)}, u32[]{:S(2)}, u32[]{:S(2)}) async-start(f32[512,1,256]{2,1,0:T(1,128)} %all_to_all.17), calls=%async_computation.1 | async-start | bytes 1048576 | tf_op jit(solution)/shard_map/all_to_all | solution.py:221
  208.2 22.3 %all-to-all-done.1 = f32[512,1,256]{2,1,0:T(1,128)S(1)} async-done(((f32[512,1,256]{2,1,0:T(1,128)}), f32[512,1,256]{2,1,0:T(1,128)S(1)}, u32[]{:S(2)}, u32[]{:S(2)}) %all-to-all-start.1) | async-done | bytes 524320 | tf_op jit(solution)/shard_map/all_to_all | solution.py:221
  231.7 4.1 %all-to-all-start.2 = ((f32[64,1,256]{2,1,0:T(1,128)}), f32[64,1,256]{2,1,0:T(1,128)S(1)}, u32[]{:S(2)}, u32[]{:S(2)}) async-start(f32[64,1,256]{2,1,0:T(1,128)} %broadcast_in_dim.22), calls=%async_computation.2 | async-start | bytes 131072 | tf_op jit(solution)/shard_map/all_to_all | solution.py:222
  236.7 9.0 %all-to-all-done.2 = f32[64,1,256]{2,1,0:T(1,128)S(1)} async-done(((f32[64,1,256]{2,1,0:T(1,128)}), f32[64,1,256]{2,1,0:T(1,128)S(1)}, u32[]{:S(2)}, u32[]{:S(2)}) %all-to-all-start.2) | async-done | bytes 65568 | tf_op jit(solution)/shard_map/all_to_all | solution.py:222
  (263 shorter events, 37.7 us)
Async XLA Ops:
  0.6 14.6 %copy-start.15 = (s32[1,12]{1,0:T(1,128)S(1)}, s32[1,12]{1,0:T(1,128)}, u32[]{:S(2)}) copy-start(s32[1,12]{1,0:T(1,128)} %param.9) | copy-start | bytes 148
  4.3 27.3 %all-to-all-start = ((bf16[8,112,256]{2,1,0:T(8,128)(2,1)}), bf16[8,112,256]{2,1,0:T(8,128)(2,1)S(1)}, u32[]{:S(2)}, u32[]{:S(2)}) async-start(bf16[8,112,256]{2,1,0:T(8,128)(2,1)} %pad_maximum_fusion), calls=%async_computation | async-start | bytes 917504 | tf_op jit(solution)/shard_map/all_to_all | solution.py:131
  33.8 6.6 %collective-permute-start.1 = (bf16[8,1,1,32,256]{4,3,2,0,1:T(8,128)(2,1)}, bf16[8,1,1,32,256]{4,3,2,0,1:T(8,128)(2,1)S(1)}, u32[]{:S(2)}, u32[]{:S(2)}) collective-permute-start(bf16[8,1,1,32,256]{4,3,2,0,1:T(8,128)(2,1)} %get-tuple-element.47), channel_id=1, source_target_pairs={{1,0},{2,1},{3,2},{4,3},{5,4},{6,5},{7,6},{8,7},{9,8},{10,9},{11,1... | collective-permute-start | bytes 393224 | tf_op jit(solution)/shard_map/ppermute | solution.py:20
  36.2 5.0 %collective-permute-start = (bf16[8,1,1,32,256]{4,3,2,0,1:T(8,128)(2,1)S(1)}, bf16[8,1,1,32,256]{4,3,2,0,1:T(8,128)(2,1)S(1)}, u32[]{:S(2)}, u32[]{:S(2)}) collective-permute-start(bf16[8,1,1,32,256]{4,3,2,0,1:T(8,128)(2,1)S(1)} %get-tuple-element.46), channel_id=1, source_target_pairs={{0,1},{1,2},{2,3},{3,4},{4,5},{5,6},{6,7},{7,8},{8,9},{9,10},{10,1... | collective-permute-start | bytes 393224 | tf_op jit(solution)/shard_map/ppermute | solution.py:17
  42.9 8.8 %collective-permute-start.3 = (bf16[8,1,2,32,256]{4,3,2,0,1:T(8,128)(2,1)S(1)}, bf16[8,1,2,32,256]{4,3,2,0,1:T(8,128)(2,1)S(1)}, u32[]{:S(2)}, u32[]{:S(2)}) collective-permute-start(bf16[8,1,2,32,256]{4,3,2,0,1:T(8,128)(2,1)S(1)} %fusion.20), channel_id=1, source_target_pairs={{64,0},{128,64},{192,128},{256,192},{320,256},{384,320},{448,384},... | collective-permute-start | bytes 786440 | tf_op jit(solution)/shard_map/ppermute | solution.py:20
  44.2 9.2 %collective-permute-start.2 = (bf16[8,1,2,32,256]{4,3,2,0,1:T(8,128)(2,1)S(1)}, bf16[8,1,2,32,256]{4,3,2,0,1:T(8,128)(2,1)S(1)}, u32[]{:S(2)}, u32[]{:S(2)}) collective-permute-start(bf16[8,1,2,32,256]{4,3,2,0,1:T(8,128)(2,1)S(1)} %fusion.20), channel_id=1, source_target_pairs={{0,64},{64,128},{128,192},{192,256},{256,320},{320,384},{384,448},... | collective-permute-start | bytes 786440 | tf_op jit(solution)/shard_map/ppermute | solution.py:17
  49.0 4.8 %copy-start = (bf16[1,2,32,256]{3,2,1,0:T(8,128)(2,1)S(1)}, bf16[1,2,32,256]{3,2,1,0:T(8,128)(2,1)}, u32[]{:S(2)}) copy-start(bf16[1,2,32,256]{3,2,1,0:T(8,128)(2,1)} %param.6) | copy-start | bytes 98308
  51.7 62.1 %copy-start.6 = (bf16[8,1,2,32,256]{4,3,2,0,1:T(8,128)(2,1)}, bf16[8,1,2,32,256]{4,3,2,0,1:T(8,128)(2,1)S(1)}, u32[]{:S(2)}) copy-start(bf16[8,1,2,32,256]{4,3,2,0,1:T(8,128)(2,1)S(1)} %collective-permute-done.3) | copy-start | bytes 786436
  53.4 60.4 %copy-start.7 = (bf16[8,1,2,32,256]{4,3,2,0,1:T(8,128)(2,1)}, bf16[8,1,2,32,256]{4,3,2,0,1:T(8,128)(2,1)S(1)}, u32[]{:S(2)}) copy-start(bf16[8,1,2,32,256]{4,3,2,0,1:T(8,128)(2,1)S(1)} %collective-permute-done.2) | copy-start | bytes 786436
  53.8 27.9 %collective-permute-start.7 = (bf16[9,1,2,32,256]{4,3,2,1,0:T(8,128)(2,1)S(1)}, bf16[9,1,2,32,256]{4,3,2,1,0:T(8,128)(2,1)S(1)}, u32[]{:S(2)}, u32[]{:S(2)}) collective-permute-start(bf16[9,1,2,32,256]{4,3,2,1,0:T(8,128)(2,1)S(1)} %pad_maximum_fusion.1), channel_id=1, source_target_pairs={{1,0},{2,1},{3,2},{4,3},{5,4},{6,5},{7,6},{8,7},{9,8},{10,9},{11,1... | collective-permute-start | bytes 884744 | tf_op jit(solution)/shard_map/ppermute | solution.py:28
  55.7 25.9 %collective-permute-start.6 = (bf16[9,1,2,32,256]{4,3,2,1,0:T(8,128)(2,1)S(1)}, bf16[9,1,2,32,256]{4,3,2,1,0:T(8,128)(2,1)S(1)}, u32[]{:S(2)}, u32[]{:S(2)}) collective-permute-start(bf16[9,1,2,32,256]{4,3,2,1,0:T(8,128)(2,1)S(1)} %pad_maximum_fusion.1), channel_id=1, source_target_pairs={{0,1},{1,2},{2,3},{3,4},{4,5},{5,6},{6,7},{7,8},{8,9},{9,10},{10,1... | collective-permute-start | bytes 884744 | tf_op jit(solution)/shard_map/ppermute | solution.py:28
  60.2 21.4 %collective-permute-start.8 = (bf16[5,1,2,32,256]{4,3,2,1,0:T(8,128)(2,1)S(1)}, bf16[5,1,2,32,256]{4,3,2,1,0:T(8,128)(2,1)S(1)}, u32[]{:S(2)}, u32[]{:S(2)}) collective-permute-start(bf16[5,1,2,32,256]{4,3,2,1,0:T(8,128)(2,1)S(1)} %pad_maximum_fusion.4), channel_id=1, source_target_pairs={{2,0},{3,1},{4,2},{5,3},{6,4},{7,5},{8,6},{9,7},{10,8},{11,9},{12,... | collective-permute-start | bytes 491528 | tf_op jit(solution)/shard_map/ppermute | solution.py:28
  61.5 20.1 %collective-permute-start.5 = (bf16[5,1,2,32,256]{4,3,2,1,0:T(8,128)(2,1)S(1)}, bf16[5,1,2,32,256]{4,3,2,1,0:T(8,128)(2,1)S(1)}, u32[]{:S(2)}, u32[]{:S(2)}) collective-permute-start(bf16[5,1,2,32,256]{4,3,2,1,0:T(8,128)(2,1)S(1)} %pad_maximum_fusion.4), channel_id=1, source_target_pairs={{0,2},{1,3},{2,4},{3,5},{4,6},{5,7},{6,8},{7,9},{8,10},{9,11},{10,... | collective-permute-start | bytes 491528 | tf_op jit(solution)/shard_map/ppermute | solution.py:28
  65.5 7.3 %collective-permute-start.4 = (bf16[3,1,2,32,256]{4,3,2,1,0:T(8,128)(2,1)S(1)}, bf16[3,1,2,32,256]{4,3,2,1,0:T(8,128)(2,1)S(1)}, u32[]{:S(2)}, u32[]{:S(2)}) collective-permute-start(bf16[3,1,2,32,256]{4,3,2,1,0:T(8,128)(2,1)S(1)} %pad_maximum_fusion.5), channel_id=1, source_target_pairs={{0,3},{1,4},{2,5},{3,6},{4,7},{5,8},{6,9},{7,10},{8,11},{9,12},{10... | collective-permute-start | bytes 294920 | tf_op jit(solution)/shard_map/ppermute | solution.py:28
  72.8 8.8 %collective-permute-start.9 = (bf16[3,1,2,32,256]{4,3,2,1,0:T(8,128)(2,1)S(1)}, bf16[3,1,2,32,256]{4,3,2,1,0:T(8,128)(2,1)S(1)}, u32[]{:S(2)}, u32[]{:S(2)}) collective-permute-start(bf16[3,1,2,32,256]{4,3,2,1,0:T(8,128)(2,1)S(1)} %pad_maximum_fusion.5), channel_id=1, source_target_pairs={{3,0},{4,1},{5,2},{6,3},{7,4},{8,5},{9,6},{10,7},{11,8},{12,9},{13... | collective-permute-start | bytes 294920 | tf_op jit(solution)/shard_map/ppermute | solution.py:28
  81.9 8.5 %collective-permute-start.11 = (bf16[1,14,32,256]{3,2,1,0:T(8,128)(2,1)S(1)}, bf16[1,14,32,256]{3,2,1,0:T(8,128)(2,1)S(1)}, u32[]{:S(2)}, u32[]{:S(2)}) collective-permute-start(bf16[1,14,32,256]{3,2,1,0:T(8,128)(2,1)S(1)} %fusion.83), channel_id=1, source_target_pairs={{0,64},{64,128},{128,192},{192,256},{256,320},{320,384},{384,448},... | collective-permute-start | bytes 688136 | tf_op jit(solution)/shard_map/ppermute | solution.py:17
  86.1 8.4 %collective-permute-start.10 = (bf16[1,14,32,256]{3,2,1,0:T(8,128)(2,1)S(1)}, bf16[1,14,32,256]{3,2,1,0:T(8,128)(2,1)S(1)}, u32[]{:S(2)}, u32[]{:S(2)}) collective-permute-start(bf16[1,14,32,256]{3,2,1,0:T(8,128)(2,1)S(1)} %fusion.83), channel_id=1, source_target_pairs={{64,0},{128,64},{192,128},{256,192},{320,256},{384,320},{448,384},... | collective-permute-start | bytes 688136 | tf_op jit(solution)/shard_map/ppermute | solution.py:20
  96.1 6.6 %collective-permute-start.13 = (bf16[1,12,32,256]{3,2,1,0:T(8,128)(2,1)S(1)}, bf16[1,12,32,256]{3,2,1,0:T(8,128)(2,1)S(1)}, u32[]{:S(2)}, u32[]{:S(2)}) collective-permute-start(bf16[1,12,32,256]{3,2,1,0:T(8,128)(2,1)S(1)} %get-tuple-element.5), channel_id=1, source_target_pairs={{0,64},{64,128},{128,192},{192,256},{256,320},{320,384},{384,448},... | collective-permute-start | bytes 589832 | tf_op jit(solution)/shard_map/ppermute | solution.py:17
  98.3 8.2 %collective-permute-start.12 = (bf16[1,12,32,256]{3,2,1,0:T(8,128)(2,1)S(1)}, bf16[1,12,32,256]{3,2,1,0:T(8,128)(2,1)S(1)}, u32[]{:S(2)}, u32[]{:S(2)}) collective-permute-start(bf16[1,12,32,256]{3,2,1,0:T(8,128)(2,1)S(1)} %get-tuple-element.5), channel_id=1, source_target_pairs={{64,0},{128,64},{192,128},{256,192},{320,256},{384,320},{448,384},... | collective-permute-start | bytes 589832 | tf_op jit(solution)/shard_map/ppermute | solution.py:20
  108.0 7.2 %collective-permute-start.15 = (bf16[1,10,32,256]{3,2,1,0:T(8,128)(2,1)S(1)}, bf16[1,10,32,256]{3,2,1,0:T(8,128)(2,1)S(1)}, u32[]{:S(2)}, u32[]{:S(2)}) collective-permute-start(bf16[1,10,32,256]{3,2,1,0:T(8,128)(2,1)S(1)} %get-tuple-element.62), channel_id=1, source_target_pairs={{0,64},{64,128},{128,192},{192,256},{256,320},{320,384},{384,448},... | collective-permute-start | bytes 491528 | tf_op jit(solution)/shard_map/ppermute | solution.py:17
  112.4 6.6 %collective-permute-start.14 = (bf16[1,10,32,256]{3,2,1,0:T(8,128)(2,1)S(1)}, bf16[1,10,32,256]{3,2,1,0:T(8,128)(2,1)S(1)}, u32[]{:S(2)}, u32[]{:S(2)}) collective-permute-start(bf16[1,10,32,256]{3,2,1,0:T(8,128)(2,1)S(1)} %get-tuple-element.62), channel_id=1, source_target_pairs={{64,0},{128,64},{192,128},{256,192},{320,256},{384,320},{448,384},... | collective-permute-start | bytes 491528 | tf_op jit(solution)/shard_map/ppermute | solution.py:20
  113.7 5.6 %copy-start.1 = (bf16[1,1,2,288,256]{4,3,2,0,1:T(8,128)(2,1)}, bf16[1,1,2,288,256]{4,3,2,0,1:T(8,128)(2,1)S(1)}, u32[]{:S(2)}) copy-start(bf16[1,1,2,288,256]{4,3,2,0,1:T(8,128)(2,1)S(1)} %constant_dynamic-update-slice_fusion.80) | copy-start | bytes 884740
  120.3 4.8 %collective-permute-start.17 = (bf16[1,8,32,256]{3,2,1,0:T(8,128)(2,1)S(1)}, bf16[1,8,32,256]{3,2,1,0:T(8,128)(2,1)S(1)}, u32[]{:S(2)}, u32[]{:S(2)}) collective-permute-start(bf16[1,8,32,256]{3,2,1,0:T(8,128)(2,1)S(1)} %get-tuple-element.64), channel_id=1, source_target_pairs={{0,64},{64,128},{128,192},{192,256},{256,320},{320,384},{384,448},... | collective-permute-start | bytes 393224 | tf_op jit(solution)/shard_map/ppermute | solution.py:17
  123.2 5.9 %collective-permute-start.16 = (bf16[1,8,32,256]{3,2,1,0:T(8,128)(2,1)S(1)}, bf16[1,8,32,256]{3,2,1,0:T(8,128)(2,1)S(1)}, u32[]{:S(2)}, u32[]{:S(2)}) collective-permute-start(bf16[1,8,32,256]{3,2,1,0:T(8,128)(2,1)S(1)} %get-tuple-element.64), channel_id=1, source_target_pairs={{64,0},{128,64},{192,128},{256,192},{320,256},{384,320},{448,384},... | collective-permute-start | bytes 393224 | tf_op jit(solution)/shard_map/ppermute | solution.py:20
  130.4 14.9 %slice-start.1 = ((bf16[8,1,2,32,256]{4,3,2,0,1:T(8,128)(2,1)}), bf16[1,1,2,32,256]{4,3,2,0,1:T(8,128)(2,1)S(1)}, s32[]{:S(2)}) async-start(bf16[8,1,2,32,256]{4,3,2,0,1:T(8,128)(2,1)} %copy-done.6), calls=%async_computation.4 | async-start | bytes 65536 | tf_op jit(solution)/shard_map/slice | solution.py:207
  130.4 14.9 %slice-start.3 = ((bf16[8,1,2,32,256]{4,3,2,0,1:T(8,128)(2,1)}), bf16[1,1,2,32,256]{4,3,2,0,1:T(8,128)(2,1)S(1)}, s32[]{:S(2)}) async-start(bf16[8,1,2,32,256]{4,3,2,0,1:T(8,128)(2,1)} %copy-done.7), calls=%async_computation.6 | async-start | bytes 65536 | tf_op jit(solution)/shard_map/slice | solution.py:207
  130.4 5.1 %collective-permute-start.19 = (bf16[1,6,32,256]{3,2,1,0:T(8,128)(2,1)S(1)}, bf16[1,6,32,256]{3,2,1,0:T(8,128)(2,1)S(1)}, u32[]{:S(2)}, u32[]{:S(2)}) collective-permute-start(bf16[1,6,32,256]{3,2,1,0:T(8,128)(2,1)S(1)} %get-tuple-element.66), channel_id=1, source_target_pairs={{0,64},{64,128},{128,192},{192,256},{256,320},{320,384},{384,448},... | collective-permute-start | bytes 294920 | tf_op jit(solution)/shard_map/ppermute | solution.py:17
  133.9 5.4 %collective-permute-start.18 = (bf16[1,6,32,256]{3,2,1,0:T(8,128)(2,1)S(1)}, bf16[1,6,32,256]{3,2,1,0:T(8,128)(2,1)S(1)}, u32[]{:S(2)}, u32[]{:S(2)}) collective-permute-start(bf16[1,6,32,256]{3,2,1,0:T(8,128)(2,1)S(1)} %get-tuple-element.66), channel_id=1, source_target_pairs={{64,0},{128,64},{192,128},{256,192},{320,256},{384,320},{448,384},... | collective-permute-start | bytes 294920 | tf_op jit(solution)/shard_map/ppermute | solution.py:20
  139.6 10.2 %copy-start.4 = (bf16[1,9,32,32]{3,2,1,0:T(8,128)(2,1)S(1)}, bf16[1,9,32,32]{3,2,1,0:T(8,128)(2,1)}, u32[]{:S(2)}) copy-start(bf16[1,9,32,32]{3,2,1,0:T(8,128)(2,1)} %get-tuple-element.18) | copy-start | bytes 55300
  140.1 26.8 %slice-start = ((bf16[8,1,2,32,256]{4,3,2,0,1:T(8,128)(2,1)}), bf16[7,1,2,32,256]{4,3,2,0,1:T(8,128)(2,1)S(1)}, s32[]{:S(2)}) async-start(bf16[8,1,2,32,256]{4,3,2,0,1:T(8,128)(2,1)} %copy-done.6), calls=%async_computation.3 | async-start | bytes 458752 | tf_op jit(solution)/shard_map/slice | solution.py:207
  140.1 26.8 %slice-start.2 = ((bf16[8,1,2,32,256]{4,3,2,0,1:T(8,128)(2,1)}), bf16[7,1,2,32,256]{4,3,2,0,1:T(8,128)(2,1)S(1)}, s32[]{:S(2)}) async-start(bf16[8,1,2,32,256]{4,3,2,0,1:T(8,128)(2,1)} %copy-done.7), calls=%async_computation.5 | async-start | bytes 458752 | tf_op jit(solution)/shard_map/slice | solution.py:207
  140.4 5.0 %collective-permute-start.21 = (bf16[1,4,32,256]{3,2,1,0:T(8,128)(2,1)S(1)}, bf16[1,4,32,256]{3,2,1,0:T(8,128)(2,1)S(1)}, u32[]{:S(2)}, u32[]{:S(2)}) collective-permute-start(bf16[1,4,32,256]{3,2,1,0:T(8,128)(2,1)S(1)} %get-tuple-element.68), channel_id=1, source_target_pairs={{0,64},{64,128},{128,192},{192,256},{256,320},{320,384},{384,448},... | collective-permute-start | bytes 196616 | tf_op jit(solution)/shard_map/ppermute | solution.py:17
  144.0 5.0 %collective-permute-start.20 = (bf16[1,4,32,256]{3,2,1,0:T(8,128)(2,1)S(1)}, bf16[1,4,32,256]{3,2,1,0:T(8,128)(2,1)S(1)}, u32[]{:S(2)}, u32[]{:S(2)}) collective-permute-start(bf16[1,4,32,256]{3,2,1,0:T(8,128)(2,1)S(1)} %get-tuple-element.68), channel_id=1, source_target_pairs={{64,0},{128,64},{192,128},{256,192},{320,256},{384,320},{448,384},... | collective-permute-start | bytes 196616 | tf_op jit(solution)/shard_map/ppermute | solution.py:20
  150.0 10.0 %collective-permute-start.23 = (bf16[1,2,32,256]{3,2,1,0:T(8,128)(2,1)S(1)}, bf16[1,2,32,256]{3,2,1,0:T(8,128)(2,1)S(1)}, u32[]{:S(2)}, u32[]{:S(2)}) collective-permute-start(bf16[1,2,32,256]{3,2,1,0:T(8,128)(2,1)S(1)} %fusion.52), channel_id=1, source_target_pairs={{1,0},{2,1},{3,2},{4,3},{5,4},{6,5},{7,6},{8,7},{9,8},{10,9},{11,1... | collective-permute-start | bytes 98312 | tf_op jit(solution)/shard_map/ppermute | solution.py:28
  157.5 3.1 %collective-permute-start.22 = (bf16[1,2,32,256]{3,2,1,0:T(8,128)(2,1)S(1)}, bf16[1,2,32,256]{3,2,1,0:T(8,128)(2,1)S(1)}, u32[]{:S(2)}, u32[]{:S(2)}) collective-permute-start(bf16[1,2,32,256]{3,2,1,0:T(8,128)(2,1)S(1)} %fusion.52), channel_id=1, source_target_pairs={{0,1},{1,2},{2,3},{3,4},{4,5},{5,6},{6,7},{7,8},{8,9},{9,10},{10,1... | collective-permute-start | bytes 98312 | tf_op jit(solution)/shard_map/ppermute | solution.py:28
  160.0 6.8 %copy-start.12 = (bf16[1,2,32,256]{3,2,1,0:T(8,128)(2,1)}, bf16[1,2,32,256]{3,2,1,0:T(8,128)(2,1)S(1)}, u32[]{:S(2)}) copy-start(bf16[1,2,32,256]{3,2,1,0:T(8,128)(2,1)S(1)} %collective-permute-done.23) | copy-start | bytes 98308
  160.6 6.3 %copy-start.13 = (bf16[1,2,32,256]{3,2,1,0:T(8,128)(2,1)}, bf16[1,2,32,256]{3,2,1,0:T(8,128)(2,1)S(1)}, u32[]{:S(2)}) copy-start(bf16[1,2,32,256]{3,2,1,0:T(8,128)(2,1)S(1)} %collective-permute-done.22) | copy-start | bytes 98308
  161.2 10.5 %collective-permute-start.25 = (bf16[1,6,32,256]{3,2,1,0:T(8,128)(2,1)}, bf16[1,6,32,256]{3,2,1,0:T(8,128)(2,1)}, u32[]{:S(2)}, u32[]{:S(2)}) collective-permute-start(bf16[1,6,32,256]{3,2,1,0:T(8,128)(2,1)} %fusion.112), channel_id=1, source_target_pairs={{0,64},{64,128},{128,192},{192,256},{256,320},{320,384},{384,448},... | collective-permute-start | bytes 294920 | tf_op jit(solution)/shard_map/ppermute | solution.py:17
  164.7 7.1 %collective-permute-start.24 = (bf16[1,6,32,256]{3,2,1,0:T(8,128)(2,1)}, bf16[1,6,32,256]{3,2,1,0:T(8,128)(2,1)}, u32[]{:S(2)}, u32[]{:S(2)}) collective-permute-start(bf16[1,6,32,256]{3,2,1,0:T(8,128)(2,1)} %fusion.112), channel_id=1, source_target_pairs={{64,0},{128,64},{192,128},{256,192},{320,256},{384,320},{448,384},... | collective-permute-start | bytes 294920 | tf_op jit(solution)/shard_map/ppermute | solution.py:20
  169.8 3.8 %copy-start.5 = (bf16[1,9,32,32]{3,2,1,0:T(8,128)(2,1)S(1)}, bf16[1,9,32,32]{3,2,1,0:T(8,128)(2,1)}, u32[]{:S(2)}) copy-start(bf16[1,9,32,32]{3,2,1,0:T(8,128)(2,1)} %get-tuple-element.17) | copy-start | bytes 55300
  169.8 3.9 %copy-start.8 = (f32[1,2,32,256]{3,2,1,0:T(8,128)S(1)}, f32[1,2,32,256]{3,2,1,0:T(8,128)}, u32[]{:S(2)}) copy-start(f32[1,2,32,256]{3,2,1,0:T(8,128)} %slice_bitcast_fusion.2) | copy-start | bytes 196612
  169.8 3.9 %copy-start.10 = (f32[1,1,32,256]{3,2,1,0:T(8,128)S(1)}, f32[1,1,32,256]{3,2,1,0:T(8,128)}, u32[]{:S(2)}) copy-start(f32[1,1,32,256]{3,2,1,0:T(8,128)} %get-tuple-element.76) | copy-start | bytes 98308
  174.5 7.9 %collective-permute-start.27 = (bf16[1,4,32,256]{3,2,1,0:T(8,128)(2,1)S(1)}, bf16[1,4,32,256]{3,2,1,0:T(8,128)(2,1)}, u32[]{:S(2)}, u32[]{:S(2)}) collective-permute-start(bf16[1,4,32,256]{3,2,1,0:T(8,128)(2,1)S(1)} %get-tuple-element.3), channel_id=1, source_target_pairs={{0,64},{64,128},{128,192},{192,256},{256,320},{320,384},{384,448},... | collective-permute-start | bytes 196616 | tf_op jit(solution)/shard_map/ppermute | solution.py:17
  179.2 5.1 %collective-permute-start.26 = (bf16[1,4,32,256]{3,2,1,0:T(8,128)(2,1)S(1)}, bf16[1,4,32,256]{3,2,1,0:T(8,128)(2,1)}, u32[]{:S(2)}, u32[]{:S(2)}) collective-permute-start(bf16[1,4,32,256]{3,2,1,0:T(8,128)(2,1)S(1)} %get-tuple-element.3), channel_id=1, source_target_pairs={{64,0},{128,64},{192,128},{256,192},{320,256},{384,320},{448,384},... | collective-permute-start | bytes 196616 | tf_op jit(solution)/shard_map/ppermute | solution.py:20
  186.0 49.9 %copy-start.3 = (bf16[1,9,32,32]{3,2,1,0:T(8,128)(2,1)S(1)}, bf16[1,9,32,32]{3,2,1,0:T(8,128)(2,1)}, u32[]{:S(2)}) copy-start(bf16[1,9,32,32]{3,2,1,0:T(8,128)(2,1)} %get-tuple-element.16) | copy-start | bytes 55300
  186.0 49.9 %copy-start.9 = (bf16[1,4,32,256]{3,2,1,0:T(8,128)(2,1)S(1)}, bf16[1,4,32,256]{3,2,1,0:T(8,128)(2,1)}, u32[]{:S(2)}) copy-start(bf16[1,4,32,256]{3,2,1,0:T(8,128)(2,1)} %get-tuple-element.4) | copy-start | bytes 196612
  187.4 43.1 %all-to-all-start.1 = ((f32[512,1,256]{2,1,0:T(1,128)}), f32[512,1,256]{2,1,0:T(1,128)S(1)}, u32[]{:S(2)}, u32[]{:S(2)}) async-start(f32[512,1,256]{2,1,0:T(1,128)} %all_to_all.17), calls=%async_computation.1 | async-start | bytes 1048576 | tf_op jit(solution)/shard_map/all_to_all | solution.py:221
  231.7 14.0 %all-to-all-start.2 = ((f32[64,1,256]{2,1,0:T(1,128)}), f32[64,1,256]{2,1,0:T(1,128)S(1)}, u32[]{:S(2)}, u32[]{:S(2)}) async-start(f32[64,1,256]{2,1,0:T(1,128)} %broadcast_in_dim.22), calls=%async_computation.2 | async-start | bytes 131072 | tf_op jit(solution)/shard_map/all_to_all | solution.py:222
  (3 other events, 9.2 us)

commit v14 on v12

--- a/solution.py
+++ b/solution.py
@@ -151,18 +151,31 @@
     need = halo_plan(layers, HALO)
     reach = -(-max(need) // height)
     factor_b = factor.astype(jnp.bfloat16)
-    lows, highs, picks = {}, {}, {}
-    for dist in range(1, reach + 1):
-        chosen = [layer for layer in range(layers) if need[layer] > height * (dist - 1)]
-        picks[dist] = chosen
-        load = jnp.stack([factor_b[layer] for layer in chosen] + [grad_out])
-        lows[dist] = passed_along(load, "gy", dist)
-        highs[dist] = passed_along(load, "gy", -dist)
-
-    def halo_of(index_of, h, own):
+    blocks = []
+    for layer in reversed(range(layers)):
+        if layer == layers - 1 or need[layer] != need[layer + 1] - 1:
+            blocks.append([])
+        blocks[-1].append(layer)
+    lows, highs, picks, block_of = {}, {}, {}, {}
+    for block, members in enumerate(blocks):
+        for layer in members:
+            block_of[layer] = block
+        for dist in range(1, reach + 1):
+            chosen = [layer for layer in members if need[layer] > height * (dist - 1)]
+            extra = [grad_out] if block == 0 else []
+            if not chosen and not extra:
+                continue
+            picks[(block, dist)] = chosen
+            load = jnp.stack([factor_b[layer] for layer in chosen] + extra)
+            lows[(block, dist)] = passed_along(load, "gy", dist)
+            highs[(block, dist)] = passed_along(load, "gy", -dist)
+
+    def halo_of(index_of, h, block):
         span = -(-h // height)
-        low = jnp.concatenate([index_of(lows[d], d) for d in range(span, 0, -1)], axis=1)[:, -h:]
-        high = jnp.concatenate([index_of(highs[d], d) for d in range(1, span + 1)], axis=1)[:, :h]
+        low = [index_of(lows[(block, d)], d) for d in range(span, 0, -1)]
+        high = [index_of(highs[(block, d)], d) for d in range(1, span + 1)]
+        low = jnp.concatenate(low, axis=1)[:, -h:]
+        high = jnp.concatenate(high, axis=1)[:, :h]
         return low, high
 
     def refreshed(grad, h):
@@ -171,7 +184,7 @@
         high = jnp.concatenate([passed_along(grad, "gy", -d) for d in range(1, span + 1)], axis=1)
         return jnp.concatenate([low[:, low.shape[1] - h :], grad, high[:, :h]], axis=1)
 
-    low, high = halo_of(lambda part, d: part[-1], need[layers - 1], grad_out)
+    low, high = halo_of(lambda part, d: part[-1], need[layers - 1], 0)
     grad = jnp.concatenate([low, grad_out, high], axis=1)
     plane_list = [None] * layers
     depth_list = [None] * layers
@@ -179,7 +192,9 @@
         h = need[layer]
         if grad.shape[1] != height + 2 * h:
             grad = refreshed(grad, h)
-        low, high = halo_of(lambda part, d: part[picks[d].index(layer)], h, None)
+        low, high = halo_of(
+            lambda part, d: part[picks[(block_of[layer], d)].index(layer)], h, block_of[layer]
+        )
         wide = jnp.concatenate([low.astype(jnp.float32), factor[layer], high.astype(jnp.float32)], axis=1)
         grad_mix = (grad.astype(jnp.float32) * wide).astype(jnp.bfloat16)
         mix_deep = padded_2(grad_mix, (("segment", 0),), 1)

time: 244 us -> 260 us (1.066)
  starting transfers between devices: 129 us -> 140 us
    ppermute x8 -> x12, starting transfers between devices: 27.5 us -> 38.5 us  [passed_along(): return lax.ppermute(block, axis, route)]
    ppermute x10, waiting for transfers between devices: 9.76 us -> 12.5 us  [padded_2(): lax.ppermute(lax.slice_in_dim(block, 0, width, axis=dim), axis, backward)]
    unnamed x132 -> x137, local copies, waits for them, and re-layouts: 5.68 us -> 6.03 us
    ppermute x8 -> x12, waiting for transfers between devices: 9.25 us -> 9.56 us  [passed_along(): return lax.ppermute(block, axis, route)]
  transfers between devices with their start and end apart: 31 -> 35, of which waited for: 19 -> 22; matrix products, arithmetic and copies ran while one was open for 5% -> 6% of each run, Pallas kernels for 0% -> 0%
where the time goes in v14:
time: 260 us; the launch traced here: 258 us
  starting transfers between devices  140 us (54%)
  waiting for transfers between devices  78.1 us (30%)
  local copies, waits for them, and re-layouts  21.2 us (8%)
  matrix products  11.8 us (5%)
  other arithmetic  4.03 us (2%)
    ppermute x10, starting transfers between devices, padded_2(): lax.ppermute(lax.slice_in_dim(block, block.shape[dim] - width, None, axis...  44.7 us
    ppermute x12, starting transfers between devices, passed_along(): return lax.ppermute(block, axis, route)  38.5 us
    all_to_all x1, starting transfers between devices, local(): part = lax.all_to_all(flat, ('segment', 'gy'), 0, 0, tiled=True).sum(axis=0)  28.7 us
    all_to_all x1, waiting for transfers between devices, local(): part = lax.all_to_all(flat, ('segment', 'gy'), 0, 0, tiled=True).sum(axis=0)  22.3 us
    all_to_all x1, waiting for transfers between devices, local(): got = lax.all_to_all(send, 'segment', 0, 0, tiled=True)  15.6 us
    ppermute x10, starting transfers between devices, padded_2(): lax.ppermute(lax.slice_in_dim(block, 0, width, axis=dim), axis, backward)  13.5 us
    ppermute x10, waiting for transfers between devices, padded_2(): lax.ppermute(lax.slice_in_dim(block, 0, width, axis=dim), axis, backward)  12.5 us
    all_to_all x1, starting transfers between devices, local(): got = lax.all_to_all(send, 'segment', 0, 0, tiled=True)  10.9 us
  transfers between devices with their start and end apart: 35, of which 22 were waited for; matrix products, arithmetic and copies ran while one was open for 6% of the time, Pallas kernels for 0%

profile of v14, /device:TPU:1, one launch (start us, length us, event | category | flops | bytes accessed | tf_op | source)
XLA Modules:
  0.0 258.1 jit_solution(6313237717281779417)
XLA Ops:
  2.5 1.8 pad_maximum_fusion
  4.3 10.9 %all-to-all-start = ((bf16[8,112,256]{2,1,0:T(8,128)(2,1)}), bf16[8,112,256]{2,1,0:T(8,128)(2,1)S(1)}, u32[]{:S(2)}, u32[]{:S(2)}) async-start(bf16[8,112,256]{2,1,0:T(8,128)(2,1)} %pad_maximum_fusion), calls=%async_computation | async-start | bytes 917504 | tf_op jit(solution)/shard_map/all_to_all | solution.py:131
  16.0 15.6 %all-to-all-done = bf16[8,112,256]{2,1,0:T(8,128)(2,1)S(1)} async-done(((bf16[8,112,256]{2,1,0:T(8,128)(2,1)}), bf16[8,112,256]{2,1,0:T(8,128)(2,1)S(1)}, u32[]{:S(2)}, u32[]{:S(2)}) %all-to-all-start) | async-done | bytes 458784 | tf_op jit(solution)/shard_map/all_to_all | solution.py:131
  33.5 3.7 %collective-permute-start = (bf16[8,1,1,32,256]{4,3,2,0,1:T(8,128)(2,1)}, bf16[8,1,1,32,256]{4,3,2,0,1:T(8,128)(2,1)S(1)}, u32[]{:S(2)}, u32[]{:S(2)}) collective-permute-start(bf16[8,1,1,32,256]{4,3,2,0,1:T(8,128)(2,1)} %get-tuple-element.37), channel_id=1, source_target_pairs={{0,1},{1,2},{2,3},{3,4},{4,5},{5,6},{6,7},{7,8},{8,9},{9,10},{10,1... | collective-permute-start | bytes 393224 | tf_op jit(solution)/shard_map/ppermute | solution.py:17
  37.2 1.9 collective-permute-start.1
  40.4 3.3 %collective-permute-done.1 = bf16[8,1,1,32,256]{4,3,2,0,1:T(8,128)(2,1)S(1)} collective-permute-done((bf16[8,1,1,32,256]{4,3,2,0,1:T(8,128)(2,1)}, bf16[8,1,1,32,256]{4,3,2,0,1:T(8,128)(2,1)S(1)}, u32[]{:S(2)}, u32[]{:S(2)}) %collective-permute-start.1) | collective-permute-done | bytes 131104 | tf_op jit(solution)/shard_map/ppermute | solution.py:20
  45.3 2.2 collective-permute-start.2
  47.5 1.3 collective-permute-start.3
  51.0 4.1 %collective-permute-done.3 = bf16[8,1,2,32,256]{4,3,2,0,1:T(8,128)(2,1)S(1)} collective-permute-done((bf16[8,1,2,32,256]{4,3,2,0,1:T(8,128)(2,1)S(1)}, bf16[8,1,2,32,256]{4,3,2,0,1:T(8,128)(2,1)S(1)}, u32[]{:S(2)}, u32[]{:S(2)}) %collective-permute-start.3) | collective-permute-done | bytes 262176 | tf_op jit(solution)/shard_map/ppermute | solution.py:20
  55.6 5.0 %collective-permute-start.20 = (bf16[2,1,2,32,256]{4,3,2,1,0:T(8,128)(2,1)S(1)}, bf16[2,1,2,32,256]{4,3,2,1,0:T(8,128)(2,1)S(1)}, u32[]{:S(2)}, u32[]{:S(2)}) collective-permute-start(bf16[2,1,2,32,256]{4,3,2,1,0:T(8,128)(2,1)S(1)} %pad_maximum_fusion.6), channel_id=1, source_target_pairs={{0,2},{1,3},{2,4},{3,5},{4,6},{5,7},{6,8},{7,9},{8,10},{9,11},{10,... | collective-permute-start | bytes 196616 | tf_op jit(solution)/shard_map/ppermute | solution.py:28
  60.6 1.3 collective-permute-start.23
  61.9 4.7 %collective-permute-start.21 = (bf16[4,1,2,32,256]{4,3,2,1,0:T(8,128)(2,1)S(1)}, bf16[4,1,2,32,256]{4,3,2,1,0:T(8,128)(2,1)S(1)}, u32[]{:S(2)}, u32[]{:S(2)}) collective-permute-start(bf16[4,1,2,32,256]{4,3,2,1,0:T(8,128)(2,1)S(1)} %pad_maximum_fusion.3), channel_id=1, source_target_pairs={{0,1},{1,2},{2,3},{3,4},{4,5},{5,6},{6,7},{7,8},{8,9},{9,10},{10,1... | collective-permute-start | bytes 393224 | tf_op jit(solution)/shard_map/ppermute | solution.py:28
  66.7 1.9 collective-permute-start.22
  68.6 3.2 %collective-permute-start.4 = (bf16[3,1,2,32,256]{4,3,2,1,0:T(8,128)(2,1)S(1)}, bf16[3,1,2,32,256]{4,3,2,1,0:T(8,128)(2,1)S(1)}, u32[]{:S(2)}, u32[]{:S(2)}) collective-permute-start(bf16[3,1,2,32,256]{4,3,2,1,0:T(8,128)(2,1)S(1)} %pad_maximum_fusion.4), channel_id=1, source_target_pairs={{0,2},{1,3},{2,4},{3,5},{4,6},{5,7},{6,8},{7,9},{8,10},{9,11},{10,... | collective-permute-start | bytes 294920 | tf_op jit(solution)/shard_map/ppermute | solution.py:28
  72.6 1.3 collective-permute-start.7
  73.9 5.0 %collective-permute-start.5 = (bf16[5,1,2,32,256]{4,3,2,1,0:T(8,128)(2,1)S(1)}, bf16[5,1,2,32,256]{4,3,2,1,0:T(8,128)(2,1)S(1)}, u32[]{:S(2)}, u32[]{:S(2)}) collective-permute-start(bf16[5,1,2,32,256]{4,3,2,1,0:T(8,128)(2,1)S(1)} %constant_dynamic-update-slice_fusion.9), channel_id=1, source_target_pairs={{0,1},{1,2},{2,3},{3,4},{4,5},{5,6},{6,7},{7,8},{8,9},{9,10},{10,1... | collective-permute-start | bytes 491528 | tf_op jit(solution)/shard_map/ppermute | solution.py:28
  78.9 1.9 collective-permute-start.6
  81.2 4.4 %collective-permute-done.6 = bf16[5,1,2,32,256]{4,3,2,1,0:T(8,128)(2,1)S(1)} collective-permute-done((bf16[5,1,2,32,256]{4,3,2,1,0:T(8,128)(2,1)S(1)}, bf16[5,1,2,32,256]{4,3,2,1,0:T(8,128)(2,1)S(1)}, u32[]{:S(2)}, u32[]{:S(2)}) %collective-permute-start.6) | collective-permute-done | bytes 163872 | tf_op jit(solution)/shard_map/ppermute | solution.py:28
  85.7 1.3 collective-permute-start.8
  87.0 4.0 %collective-permute-start.9 = (bf16[1,10,32,256]{3,2,1,0:T(8,128)(2,1)S(1)}, bf16[1,10,32,256]{3,2,1,0:T(8,128)(2,1)S(1)}, u32[]{:S(2)}, u32[]{:S(2)}) collective-permute-start(bf16[1,10,32,256]{3,2,1,0:T(8,128)(2,1)S(1)} %fusion.75), channel_id=1, source_target_pairs={{0,64},{64,128},{128,192},{192,256},{256,320},{320,384},{384,448},... | collective-permute-start | bytes 491528 | tf_op jit(solution)/shard_map/ppermute | solution.py:17
  91.7 1.5 collective-permute-done.9
  94.6 1.3 collective-permute-start.10
  95.9 4.4 %collective-permute-start.11 = (bf16[1,8,32,256]{3,2,1,0:T(8,128)(2,1)S(1)}, bf16[1,8,32,256]{3,2,1,0:T(8,128)(2,1)S(1)}, u32[]{:S(2)}, u32[]{:S(2)}) collective-permute-start(bf16[1,8,32,256]{3,2,1,0:T(8,128)(2,1)S(1)} %get-tuple-element.5), channel_id=1, source_target_pairs={{0,64},{64,128},{128,192},{192,256},{256,320},{320,384},{384,448},... | collective-permute-start | bytes 393224 | tf_op jit(solution)/shard_map/ppermute | solution.py:17
  100.8 1.5 collective-permute-done.11
  103.5 1.3 collective-permute-start.12
  104.8 4.4 %collective-permute-start.13 = (bf16[1,6,32,256]{3,2,1,0:T(8,128)(2,1)S(1)}, bf16[1,6,32,256]{3,2,1,0:T(8,128)(2,1)S(1)}, u32[]{:S(2)}, u32[]{:S(2)}) collective-permute-start(bf16[1,6,32,256]{3,2,1,0:T(8,128)(2,1)S(1)} %get-tuple-element.65), channel_id=1, source_target_pairs={{0,64},{64,128},{128,192},{192,256},{256,320},{320,384},{384,448},... | collective-permute-start | bytes 294920 | tf_op jit(solution)/shard_map/ppermute | solution.py:17
  109.8 1.8 collective-permute-done.13
  112.6 1.3 collective-permute-start.14
  113.9 4.5 %collective-permute-start.15 = (bf16[1,4,32,256]{3,2,1,0:T(8,128)(2,1)S(1)}, bf16[1,4,32,256]{3,2,1,0:T(8,128)(2,1)S(1)}, u32[]{:S(2)}, u32[]{:S(2)}) collective-permute-start(bf16[1,4,32,256]{3,2,1,0:T(8,128)(2,1)S(1)} %get-tuple-element.67), channel_id=1, source_target_pairs={{0,64},{64,128},{128,192},{192,256},{256,320},{320,384},{384,448},... | collective-permute-start | bytes 196616 | tf_op jit(solution)/shard_map/ppermute | solution.py:17
  120.7 5.0 %collective-permute-start.16 = (bf16[1,2,32,256]{3,2,1,0:T(8,128)(2,1)S(1)}, bf16[1,2,32,256]{3,2,1,0:T(8,128)(2,1)S(1)}, u32[]{:S(2)}, u32[]{:S(2)}) collective-permute-start(bf16[1,2,32,256]{3,2,1,0:T(8,128)(2,1)S(1)} %fusion.39), channel_id=1, source_target_pairs={{0,2},{1,3},{2,4},{3,5},{4,6},{5,7},{6,8},{7,9},{8,10},{9,11},{10,... | collective-permute-start | bytes 98312 | tf_op jit(solution)/shard_map/ppermute | solution.py:28
  125.7 5.9 %collective-permute-start.17 = (bf16[1,2,32,256]{3,2,1,0:T(8,128)(2,1)S(1)}, bf16[1,2,32,256]{3,2,1,0:T(8,128)(2,1)S(1)}, u32[]{:S(2)}, u32[]{:S(2)}) collective-permute-start(bf16[1,2,32,256]{3,2,1,0:T(8,128)(2,1)S(1)} %fusion.39), channel_id=1, source_target_pairs={{0,1},{1,2},{2,3},{3,4},{4,5},{5,6},{6,7},{7,8},{8,9},{9,10},{10,1... | collective-permute-start | bytes 98312 | tf_op jit(solution)/shard_map/ppermute | solution.py:28
  131.6 1.9 collective-permute-start.18
  133.6 1.3 collective-permute-start.19
  134.9 1.9 collective-permute-done.18
  136.9 3.0 %collective-permute-done.19 = bf16[1,2,32,256]{3,2,1,0:T(8,128)(2,1)S(1)} collective-permute-done((bf16[1,2,32,256]{3,2,1,0:T(8,128)(2,1)S(1)}, bf16[1,2,32,256]{3,2,1,0:T(8,128)(2,1)S(1)}, u32[]{:S(2)}, u32[]{:S(2)}) %collective-permute-start.19) | collective-permute-done | bytes 32800 | tf_op jit(solution)/shard_map/ppermute | solution.py:28
  139.9 1.3 collective-permute-start.24
  141.2 4.7 %collective-permute-start.25 = (bf16[1,10,32,256]{3,2,1,0:T(8,128)(2,1)S(1)}, bf16[1,10,32,256]{3,2,1,0:T(8,128)(2,1)S(1)}, u32[]{:S(2)}, u32[]{:S(2)}) collective-permute-start(bf16[1,10,32,256]{3,2,1,0:T(8,128)(2,1)S(1)} %fusion.76), channel_id=1, source_target_pairs={{0,64},{64,128},{128,192},{192,256},{256,320},{320,384},{384,448},... | collective-permute-start | bytes 491528 | tf_op jit(solution)/shard_map/ppermute | solution.py:17
  146.0 2.3 collective-permute-done.24
  148.4 1.5 collective-permute-done.25
  151.3 1.3 collective-permute-start.26
  152.6 4.7 %collective-permute-start.27 = (bf16[1,8,32,256]{3,2,1,0:T(8,128)(2,1)S(1)}, bf16[1,8,32,256]{3,2,1,0:T(8,128)(2,1)S(1)}, u32[]{:S(2)}, u32[]{:S(2)}) collective-permute-start(bf16[1,8,32,256]{3,2,1,0:T(8,128)(2,1)S(1)} %get-tuple-element.3), channel_id=1, source_target_pairs={{0,64},{64,128},{128,192},{192,256},{256,320},{320,384},{384,448},... | collective-permute-start | bytes 393224 | tf_op jit(solution)/shard_map/ppermute | solution.py:17
  162.9 5.7 %collective-permute-start.29 = (bf16[1,6,32,256]{3,2,1,0:T(8,128)(2,1)}, bf16[1,6,32,256]{3,2,1,0:T(8,128)(2,1)}, u32[]{:S(2)}, u32[]{:S(2)}) collective-permute-start(bf16[1,6,32,256]{3,2,1,0:T(8,128)(2,1)} %get-tuple-element.69), channel_id=1, source_target_pairs={{0,64},{64,128},{128,192},{192,256},{256,320},{320,384},{384,448},... | collective-permute-start | bytes 294920 | tf_op jit(solution)/shard_map/ppermute | solution.py:17
  177.7 6.2 %collective-permute-start.31 = (bf16[1,4,32,256]{3,2,1,0:T(8,128)(2,1)}, bf16[1,4,32,256]{3,2,1,0:T(8,128)(2,1)}, u32[]{:S(2)}, u32[]{:S(2)}) collective-permute-start(bf16[1,4,32,256]{3,2,1,0:T(8,128)(2,1)} %get-tuple-element.71), channel_id=1, source_target_pairs={{0,64},{64,128},{128,192},{192,256},{256,320},{320,384},{384,448},... | collective-permute-start | bytes 196616 | tf_op jit(solution)/shard_map/ppermute | solution.py:17
  188.3 1.4 all_to_all.17
  189.7 28.7 %all-to-all-start.1 = ((f32[512,1,256]{2,1,0:T(1,128)}), f32[512,1,256]{2,1,0:T(1,128)S(1)}, u32[]{:S(2)}, u32[]{:S(2)}) async-start(f32[512,1,256]{2,1,0:T(1,128)} %all_to_all.17), calls=%async_computation.1 | async-start | bytes 1048576 | tf_op jit(solution)/shard_map/all_to_all | solution.py:236
  218.9 22.3 %all-to-all-done.1 = f32[512,1,256]{2,1,0:T(1,128)S(1)} async-done(((f32[512,1,256]{2,1,0:T(1,128)}), f32[512,1,256]{2,1,0:T(1,128)S(1)}, u32[]{:S(2)}, u32[]{:S(2)}) %all-to-all-start.1) | async-done | bytes 524320 | tf_op jit(solution)/shard_map/all_to_all | solution.py:236
  242.4 4.2 %all-to-all-start.2 = ((f32[64,1,256]{2,1,0:T(1,128)}), f32[64,1,256]{2,1,0:T(1,128)S(1)}, u32[]{:S(2)}, u32[]{:S(2)}) async-start(f32[64,1,256]{2,1,0:T(1,128)} %broadcast_in_dim.22), calls=%async_computation.2 | async-start | bytes 131072 | tf_op jit(solution)/shard_map/all_to_all | solution.py:237
  247.5 8.9 %all-to-all-done.2 = f32[64,1,256]{2,1,0:T(1,128)S(1)} async-done(((f32[64,1,256]{2,1,0:T(1,128)}), f32[64,1,256]{2,1,0:T(1,128)S(1)}, u32[]{:S(2)}, u32[]{:S(2)}) %all-to-all-start.2) | async-done | bytes 65568 | tf_op jit(solution)/shard_map/all_to_all | solution.py:237
  (278 shorter events, 42.3 us)
Async XLA Ops:
  0.6 14.5 %copy-start.14 = (s32[1,12]{1,0:T(1,128)S(1)}, s32[1,12]{1,0:T(1,128)}, u32[]{:S(2)}) copy-start(s32[1,12]{1,0:T(1,128)} %param.9) | copy-start | bytes 148
  4.3 27.3 %all-to-all-start = ((bf16[8,112,256]{2,1,0:T(8,128)(2,1)}), bf16[8,112,256]{2,1,0:T(8,128)(2,1)S(1)}, u32[]{:S(2)}, u32[]{:S(2)}) async-start(bf16[8,112,256]{2,1,0:T(8,128)(2,1)} %pad_maximum_fusion), calls=%async_computation | async-start | bytes 917504 | tf_op jit(solution)/shard_map/all_to_all | solution.py:131
  33.5 6.9 %collective-permute-start = (bf16[8,1,1,32,256]{4,3,2,0,1:T(8,128)(2,1)}, bf16[8,1,1,32,256]{4,3,2,0,1:T(8,128)(2,1)S(1)}, u32[]{:S(2)}, u32[]{:S(2)}) collective-permute-start(bf16[8,1,1,32,256]{4,3,2,0,1:T(8,128)(2,1)} %get-tuple-element.37), channel_id=1, source_target_pairs={{0,1},{1,2},{2,3},{3,4},{4,5},{5,6},{6,7},{7,8},{8,9},{9,10},{10,1... | collective-permute-start | bytes 393224 | tf_op jit(solution)/shard_map/ppermute | solution.py:17
  37.2 6.5 %collective-permute-start.1 = (bf16[8,1,1,32,256]{4,3,2,0,1:T(8,128)(2,1)}, bf16[8,1,1,32,256]{4,3,2,0,1:T(8,128)(2,1)S(1)}, u32[]{:S(2)}, u32[]{:S(2)}) collective-permute-start(bf16[8,1,1,32,256]{4,3,2,0,1:T(8,128)(2,1)} %get-tuple-element.38), channel_id=1, source_target_pairs={{1,0},{2,1},{3,2},{4,3},{5,4},{6,5},{7,6},{8,7},{9,8},{10,9},{11,1... | collective-permute-start | bytes 393224 | tf_op jit(solution)/shard_map/ppermute | solution.py:20
  45.3 5.7 %collective-permute-start.2 = (bf16[8,1,2,32,256]{4,3,2,0,1:T(8,128)(2,1)S(1)}, bf16[8,1,2,32,256]{4,3,2,0,1:T(8,128)(2,1)S(1)}, u32[]{:S(2)}, u32[]{:S(2)}) collective-permute-start(bf16[8,1,2,32,256]{4,3,2,0,1:T(8,128)(2,1)S(1)} %fusion.12), channel_id=1, source_target_pairs={{0,64},{64,128},{128,192},{192,256},{256,320},{320,384},{384,448},... | collective-permute-start | bytes 786440 | tf_op jit(solution)/shard_map/ppermute | solution.py:17
  47.5 7.6 %collective-permute-start.3 = (bf16[8,1,2,32,256]{4,3,2,0,1:T(8,128)(2,1)S(1)}, bf16[8,1,2,32,256]{4,3,2,0,1:T(8,128)(2,1)S(1)}, u32[]{:S(2)}, u32[]{:S(2)}) collective-permute-start(bf16[8,1,2,32,256]{4,3,2,0,1:T(8,128)(2,1)S(1)} %fusion.12), channel_id=1, source_target_pairs={{64,0},{128,64},{192,128},{256,192},{320,256},{384,320},{448,384},... | collective-permute-start | bytes 786440 | tf_op jit(solution)/shard_map/ppermute | solution.py:20
  49.3 5.8 %copy-start.15 = (f32[256]{0:T(256)S(1)}, f32[256]{0:T(256)}, u32[]{:S(2)}) copy-start(f32[256]{0:T(256)} %broadcast_bitcast_fusion) | copy-start | bytes 3076
  50.1 18.5 %copy-start.2 = (bf16[1,2,32,256]{3,2,1,0:T(8,128)(2,1)S(1)}, bf16[1,2,32,256]{3,2,1,0:T(8,128)(2,1)}, u32[]{:S(2)}) copy-start(bf16[1,2,32,256]{3,2,1,0:T(8,128)(2,1)} %param.6) | copy-start | bytes 98308
  51.0 21.5 %copy-start.8 = (bf16[8,1,2,32,256]{4,3,2,0,1:T(8,128)(2,1)}, bf16[8,1,2,32,256]{4,3,2,0,1:T(8,128)(2,1)S(1)}, u32[]{:S(2)}) copy-start(bf16[8,1,2,32,256]{4,3,2,0,1:T(8,128)(2,1)S(1)} %collective-permute-done.2) | copy-start | bytes 786436
  55.2 17.4 %copy-start.9 = (bf16[8,1,2,32,256]{4,3,2,0,1:T(8,128)(2,1)}, bf16[8,1,2,32,256]{4,3,2,0,1:T(8,128)(2,1)S(1)}, u32[]{:S(2)}) copy-start(bf16[8,1,2,32,256]{4,3,2,0,1:T(8,128)(2,1)S(1)} %collective-permute-done.3) | copy-start | bytes 786436
  55.6 17.0 %collective-permute-start.20 = (bf16[2,1,2,32,256]{4,3,2,1,0:T(8,128)(2,1)S(1)}, bf16[2,1,2,32,256]{4,3,2,1,0:T(8,128)(2,1)S(1)}, u32[]{:S(2)}, u32[]{:S(2)}) collective-permute-start(bf16[2,1,2,32,256]{4,3,2,1,0:T(8,128)(2,1)S(1)} %pad_maximum_fusion.6), channel_id=1, source_target_pairs={{0,2},{1,3},{2,4},{3,5},{4,6},{5,7},{6,8},{7,9},{8,10},{9,11},{10,... | collective-permute-start | bytes 196616 | tf_op jit(solution)/shard_map/ppermute | solution.py:28
  60.6 13.3 %collective-permute-start.23 = (bf16[2,1,2,32,256]{4,3,2,1,0:T(8,128)(2,1)S(1)}, bf16[2,1,2,32,256]{4,3,2,1,0:T(8,128)(2,1)S(1)}, u32[]{:S(2)}, u32[]{:S(2)}) collective-permute-start(bf16[2,1,2,32,256]{4,3,2,1,0:T(8,128)(2,1)S(1)} %pad_maximum_fusion.6), channel_id=1, source_target_pairs={{2,0},{3,1},{4,2},{5,3},{6,4},{7,5},{8,6},{9,7},{10,8},{11,9},{12,... | collective-permute-start | bytes 196616 | tf_op jit(solution)/shard_map/ppermute | solution.py:28
  61.9 38.4 %collective-permute-start.21 = (bf16[4,1,2,32,256]{4,3,2,1,0:T(8,128)(2,1)S(1)}, bf16[4,1,2,32,256]{4,3,2,1,0:T(8,128)(2,1)S(1)}, u32[]{:S(2)}, u32[]{:S(2)}) collective-permute-start(bf16[4,1,2,32,256]{4,3,2,1,0:T(8,128)(2,1)S(1)} %pad_maximum_fusion.3), channel_id=1, source_target_pairs={{0,1},{1,2},{2,3},{3,4},{4,5},{5,6},{6,7},{7,8},{8,9},{9,10},{10,1... | collective-permute-start | bytes 393224 | tf_op jit(solution)/shard_map/ppermute | solution.py:28
  66.7 51.8 %collective-permute-start.22 = (bf16[4,1,2,32,256]{4,3,2,1,0:T(8,128)(2,1)S(1)}, bf16[4,1,2,32,256]{4,3,2,1,0:T(8,128)(2,1)S(1)}, u32[]{:S(2)}, u32[]{:S(2)}) collective-permute-start(bf16[4,1,2,32,256]{4,3,2,1,0:T(8,128)(2,1)S(1)} %pad_maximum_fusion.3), channel_id=1, source_target_pairs={{1,0},{2,1},{3,2},{4,3},{5,4},{6,5},{7,6},{8,7},{9,8},{10,9},{11,1... | collective-permute-start | bytes 393224 | tf_op jit(solution)/shard_map/ppermute | solution.py:28
  68.6 10.3 %collective-permute-start.4 = (bf16[3,1,2,32,256]{4,3,2,1,0:T(8,128)(2,1)S(1)}, bf16[3,1,2,32,256]{4,3,2,1,0:T(8,128)(2,1)S(1)}, u32[]{:S(2)}, u32[]{:S(2)}) collective-permute-start(bf16[3,1,2,32,256]{4,3,2,1,0:T(8,128)(2,1)S(1)} %pad_maximum_fusion.4), channel_id=1, source_target_pairs={{0,2},{1,3},{2,4},{3,5},{4,6},{5,7},{6,8},{7,9},{8,10},{9,11},{10,... | collective-permute-start | bytes 294920 | tf_op jit(solution)/shard_map/ppermute | solution.py:28
  72.6 8.3 %collective-permute-start.7 = (bf16[3,1,2,32,256]{4,3,2,1,0:T(8,128)(2,1)S(1)}, bf16[3,1,2,32,256]{4,3,2,1,0:T(8,128)(2,1)S(1)}, u32[]{:S(2)}, u32[]{:S(2)}) collective-permute-start(bf16[3,1,2,32,256]{4,3,2,1,0:T(8,128)(2,1)S(1)} %pad_maximum_fusion.4), channel_id=1, source_target_pairs={{2,0},{3,1},{4,2},{5,3},{6,4},{7,5},{8,6},{9,7},{10,8},{11,9},{12,... | collective-permute-start | bytes 294920 | tf_op jit(solution)/shard_map/ppermute | solution.py:28
  73.9 7.2 %collective-permute-start.5 = (bf16[5,1,2,32,256]{4,3,2,1,0:T(8,128)(2,1)S(1)}, bf16[5,1,2,32,256]{4,3,2,1,0:T(8,128)(2,1)S(1)}, u32[]{:S(2)}, u32[]{:S(2)}) collective-permute-start(bf16[5,1,2,32,256]{4,3,2,1,0:T(8,128)(2,1)S(1)} %constant_dynamic-update-slice_fusion.9), channel_id=1, source_target_pairs={{0,1},{1,2},{2,3},{3,4},{4,5},{5,6},{6,7},{7,8},{8,9},{9,10},{10,1... | collective-permute-start | bytes 491528 | tf_op jit(solution)/shard_map/ppermute | solution.py:28
  78.9 6.6 %collective-permute-start.6 = (bf16[5,1,2,32,256]{4,3,2,1,0:T(8,128)(2,1)S(1)}, bf16[5,1,2,32,256]{4,3,2,1,0:T(8,128)(2,1)S(1)}, u32[]{:S(2)}, u32[]{:S(2)}) collective-permute-start(bf16[5,1,2,32,256]{4,3,2,1,0:T(8,128)(2,1)S(1)} %constant_dynamic-update-slice_fusion.9), channel_id=1, source_target_pairs={{1,0},{2,1},{3,2},{4,3},{5,4},{6,5},{7,6},{8,7},{9,8},{10,9},{11,1... | collective-permute-start | bytes 491528 | tf_op jit(solution)/shard_map/ppermute | solution.py:28
  85.7 6.1 %collective-permute-start.8 = (bf16[1,10,32,256]{3,2,1,0:T(8,128)(2,1)S(1)}, bf16[1,10,32,256]{3,2,1,0:T(8,128)(2,1)S(1)}, u32[]{:S(2)}, u32[]{:S(2)}) collective-permute-start(bf16[1,10,32,256]{3,2,1,0:T(8,128)(2,1)S(1)} %fusion.75), channel_id=1, source_target_pairs={{64,0},{128,64},{192,128},{256,192},{320,256},{384,320},{448,384},... | collective-permute-start | bytes 491528 | tf_op jit(solution)/shard_map/ppermute | solution.py:20
  87.0 6.2 %collective-permute-start.9 = (bf16[1,10,32,256]{3,2,1,0:T(8,128)(2,1)S(1)}, bf16[1,10,32,256]{3,2,1,0:T(8,128)(2,1)S(1)}, u32[]{:S(2)}, u32[]{:S(2)}) collective-permute-start(bf16[1,10,32,256]{3,2,1,0:T(8,128)(2,1)S(1)} %fusion.75), channel_id=1, source_target_pairs={{0,64},{64,128},{128,192},{192,256},{256,320},{320,384},{384,448},... | collective-permute-start | bytes 491528 | tf_op jit(solution)/shard_map/ppermute | solution.py:17
  94.6 6.2 %collective-permute-start.10 = (bf16[1,8,32,256]{3,2,1,0:T(8,128)(2,1)S(1)}, bf16[1,8,32,256]{3,2,1,0:T(8,128)(2,1)S(1)}, u32[]{:S(2)}, u32[]{:S(2)}) collective-permute-start(bf16[1,8,32,256]{3,2,1,0:T(8,128)(2,1)S(1)} %get-tuple-element.5), channel_id=1, source_target_pairs={{64,0},{128,64},{192,128},{256,192},{320,256},{384,320},{448,384},... | collective-permute-start | bytes 393224 | tf_op jit(solution)/shard_map/ppermute | solution.py:20
  95.9 6.4 %collective-permute-start.11 = (bf16[1,8,32,256]{3,2,1,0:T(8,128)(2,1)S(1)}, bf16[1,8,32,256]{3,2,1,0:T(8,128)(2,1)S(1)}, u32[]{:S(2)}, u32[]{:S(2)}) collective-permute-start(bf16[1,8,32,256]{3,2,1,0:T(8,128)(2,1)S(1)} %get-tuple-element.5), channel_id=1, source_target_pairs={{0,64},{64,128},{128,192},{192,256},{256,320},{320,384},{384,448},... | collective-permute-start | bytes 393224 | tf_op jit(solution)/shard_map/ppermute | solution.py:17
  103.2 9.2 %copy-start.4 = (bf16[1,9,32,32]{3,2,1,0:T(8,128)(2,1)S(1)}, bf16[1,9,32,32]{3,2,1,0:T(8,128)(2,1)}, u32[]{:S(2)}) copy-start(bf16[1,9,32,32]{3,2,1,0:T(8,128)(2,1)} %get-tuple-element.21) | copy-start | bytes 55300
  103.5 6.2 %collective-permute-start.12 = (bf16[1,6,32,256]{3,2,1,0:T(8,128)(2,1)S(1)}, bf16[1,6,32,256]{3,2,1,0:T(8,128)(2,1)S(1)}, u32[]{:S(2)}, u32[]{:S(2)}) collective-permute-start(bf16[1,6,32,256]{3,2,1,0:T(8,128)(2,1)S(1)} %get-tuple-element.65), channel_id=1, source_target_pairs={{64,0},{128,64},{192,128},{256,192},{320,256},{384,320},{448,384},... | collective-permute-start | bytes 294920 | tf_op jit(solution)/shard_map/ppermute | solution.py:20
  104.8 6.7 %collective-permute-start.13 = (bf16[1,6,32,256]{3,2,1,0:T(8,128)(2,1)S(1)}, bf16[1,6,32,256]{3,2,1,0:T(8,128)(2,1)S(1)}, u32[]{:S(2)}, u32[]{:S(2)}) collective-permute-start(bf16[1,6,32,256]{3,2,1,0:T(8,128)(2,1)S(1)} %get-tuple-element.65), channel_id=1, source_target_pairs={{0,64},{64,128},{128,192},{192,256},{256,320},{320,384},{384,448},... | collective-permute-start | bytes 294920 | tf_op jit(solution)/shard_map/ppermute | solution.py:17
  112.6 6.1 %collective-permute-start.14 = (bf16[1,4,32,256]{3,2,1,0:T(8,128)(2,1)S(1)}, bf16[1,4,32,256]{3,2,1,0:T(8,128)(2,1)S(1)}, u32[]{:S(2)}, u32[]{:S(2)}) collective-permute-start(bf16[1,4,32,256]{3,2,1,0:T(8,128)(2,1)S(1)} %get-tuple-element.67), channel_id=1, source_target_pairs={{64,0},{128,64},{192,128},{256,192},{320,256},{384,320},{448,384},... | collective-permute-start | bytes 196616 | tf_op jit(solution)/shard_map/ppermute | solution.py:20
  113.9 5.8 %collective-permute-start.15 = (bf16[1,4,32,256]{3,2,1,0:T(8,128)(2,1)S(1)}, bf16[1,4,32,256]{3,2,1,0:T(8,128)(2,1)S(1)}, u32[]{:S(2)}, u32[]{:S(2)}) collective-permute-start(bf16[1,4,32,256]{3,2,1,0:T(8,128)(2,1)S(1)} %get-tuple-element.67), channel_id=1, source_target_pairs={{0,64},{64,128},{128,192},{192,256},{256,320},{320,384},{384,448},... | collective-permute-start | bytes 196616 | tf_op jit(solution)/shard_map/ppermute | solution.py:17
  118.5 27.5 %slice-start = ((bf16[8,1,2,32,256]{4,3,2,0,1:T(8,128)(2,1)}), bf16[1,1,2,32,256]{4,3,2,0,1:T(8,128)(2,1)S(1)}, s32[]{:S(2)}) async-start(bf16[8,1,2,32,256]{4,3,2,0,1:T(8,128)(2,1)} %copy-done.8), calls=%async_computation.3 | async-start | bytes 65536 | tf_op jit(solution)/shard_map/slice | solution.py:222
  118.5 27.5 %slice-start.2 = ((bf16[8,1,2,32,256]{4,3,2,0,1:T(8,128)(2,1)}), bf16[1,1,2,32,256]{4,3,2,0,1:T(8,128)(2,1)S(1)}, s32[]{:S(2)}) async-start(bf16[8,1,2,32,256]{4,3,2,0,1:T(8,128)(2,1)} %copy-done.9), calls=%async_computation.5 | async-start | bytes 65536 | tf_op jit(solution)/shard_map/slice | solution.py:222
  120.7 14.2 %collective-permute-start.16 = (bf16[1,2,32,256]{3,2,1,0:T(8,128)(2,1)S(1)}, bf16[1,2,32,256]{3,2,1,0:T(8,128)(2,1)S(1)}, u32[]{:S(2)}, u32[]{:S(2)}) collective-permute-start(bf16[1,2,32,256]{3,2,1,0:T(8,128)(2,1)S(1)} %fusion.39), channel_id=1, source_target_pairs={{0,2},{1,3},{2,4},{3,5},{4,6},{5,7},{6,8},{7,9},{8,10},{9,11},{10,... | collective-permute-start | bytes 98312 | tf_op jit(solution)/shard_map/ppermute | solution.py:28
  125.7 9.2 %collective-permute-start.17 = (bf16[1,2,32,256]{3,2,1,0:T(8,128)(2,1)S(1)}, bf16[1,2,32,256]{3,2,1,0:T(8,128)(2,1)S(1)}, u32[]{:S(2)}, u32[]{:S(2)}) collective-permute-start(bf16[1,2,32,256]{3,2,1,0:T(8,128)(2,1)S(1)} %fusion.39), channel_id=1, source_target_pairs={{0,1},{1,2},{2,3},{3,4},{4,5},{5,6},{6,7},{7,8},{8,9},{9,10},{10,1... | collective-permute-start | bytes 98312 | tf_op jit(solution)/shard_map/ppermute | solution.py:28
  131.6 5.2 %collective-permute-start.18 = (bf16[1,2,32,256]{3,2,1,0:T(8,128)(2,1)S(1)}, bf16[1,2,32,256]{3,2,1,0:T(8,128)(2,1)S(1)}, u32[]{:S(2)}, u32[]{:S(2)}) collective-permute-start(bf16[1,2,32,256]{3,2,1,0:T(8,128)(2,1)S(1)} %fusion.39), channel_id=1, source_target_pairs={{1,0},{2,1},{3,2},{4,3},{5,4},{6,5},{7,6},{8,7},{9,8},{10,9},{11,1... | collective-permute-start | bytes 98312 | tf_op jit(solution)/shard_map/ppermute | solution.py:28
  133.6 6.3 %collective-permute-start.19 = (bf16[1,2,32,256]{3,2,1,0:T(8,128)(2,1)S(1)}, bf16[1,2,32,256]{3,2,1,0:T(8,128)(2,1)S(1)}, u32[]{:S(2)}, u32[]{:S(2)}) collective-permute-start(bf16[1,2,32,256]{3,2,1,0:T(8,128)(2,1)S(1)} %fusion.39), channel_id=1, source_target_pairs={{2,0},{3,1},{4,2},{5,3},{6,4},{7,5},{8,6},{9,7},{10,8},{11,9},{12,... | collective-permute-start | bytes 98312 | tf_op jit(solution)/shard_map/ppermute | solution.py:28
  139.9 8.4 %collective-permute-start.24 = (bf16[1,10,32,256]{3,2,1,0:T(8,128)(2,1)S(1)}, bf16[1,10,32,256]{3,2,1,0:T(8,128)(2,1)S(1)}, u32[]{:S(2)}, u32[]{:S(2)}) collective-permute-start(bf16[1,10,32,256]{3,2,1,0:T(8,128)(2,1)S(1)} %fusion.76), channel_id=1, source_target_pairs={{64,0},{128,64},{192,128},{256,192},{320,256},{384,320},{448,384},... | collective-permute-start | bytes 491528 | tf_op jit(solution)/shard_map/ppermute | solution.py:20
  141.2 8.7 %collective-permute-start.25 = (bf16[1,10,32,256]{3,2,1,0:T(8,128)(2,1)S(1)}, bf16[1,10,32,256]{3,2,1,0:T(8,128)(2,1)S(1)}, u32[]{:S(2)}, u32[]{:S(2)}) collective-permute-start(bf16[1,10,32,256]{3,2,1,0:T(8,128)(2,1)S(1)} %fusion.76), channel_id=1, source_target_pairs={{0,64},{64,128},{128,192},{192,256},{256,320},{320,384},{384,448},... | collective-permute-start | bytes 491528 | tf_op jit(solution)/shard_map/ppermute | solution.py:17
  151.3 7.6 %collective-permute-start.26 = (bf16[1,8,32,256]{3,2,1,0:T(8,128)(2,1)S(1)}, bf16[1,8,32,256]{3,2,1,0:T(8,128)(2,1)S(1)}, u32[]{:S(2)}, u32[]{:S(2)}) collective-permute-start(bf16[1,8,32,256]{3,2,1,0:T(8,128)(2,1)S(1)} %get-tuple-element.3), channel_id=1, source_target_pairs={{64,0},{128,64},{192,128},{256,192},{320,256},{384,320},{448,384},... | collective-permute-start | bytes 393224 | tf_op jit(solution)/shard_map/ppermute | solution.py:20
  152.6 7.1 %collective-permute-start.27 = (bf16[1,8,32,256]{3,2,1,0:T(8,128)(2,1)S(1)}, bf16[1,8,32,256]{3,2,1,0:T(8,128)(2,1)S(1)}, u32[]{:S(2)}, u32[]{:S(2)}) collective-permute-start(bf16[1,8,32,256]{3,2,1,0:T(8,128)(2,1)S(1)} %get-tuple-element.3), channel_id=1, source_target_pairs={{0,64},{64,128},{128,192},{192,256},{256,320},{320,384},{384,448},... | collective-permute-start | bytes 393224 | tf_op jit(solution)/shard_map/ppermute | solution.py:17
  160.1 9.3 %slice-start.1 = ((bf16[8,1,2,32,256]{4,3,2,0,1:T(8,128)(2,1)}), bf16[7,1,2,32,256]{4,3,2,0,1:T(8,128)(2,1)S(1)}, s32[]{:S(2)}) async-start(bf16[8,1,2,32,256]{4,3,2,0,1:T(8,128)(2,1)} %copy-done.8), calls=%async_computation.4 | async-start | bytes 458752 | tf_op jit(solution)/shard_map/slice | solution.py:222
  160.1 9.3 %slice-start.3 = ((bf16[8,1,2,32,256]{4,3,2,0,1:T(8,128)(2,1)}), bf16[7,1,2,32,256]{4,3,2,0,1:T(8,128)(2,1)S(1)}, s32[]{:S(2)}) async-start(bf16[8,1,2,32,256]{4,3,2,0,1:T(8,128)(2,1)} %copy-done.9), calls=%async_computation.6 | async-start | bytes 458752 | tf_op jit(solution)/shard_map/slice | solution.py:222
  161.6 12.0 %collective-permute-start.28 = (bf16[1,6,32,256]{3,2,1,0:T(8,128)(2,1)}, bf16[1,6,32,256]{3,2,1,0:T(8,128)(2,1)}, u32[]{:S(2)}, u32[]{:S(2)}) collective-permute-start(bf16[1,6,32,256]{3,2,1,0:T(8,128)(2,1)} %get-tuple-element.69), channel_id=1, source_target_pairs={{64,0},{128,64},{192,128},{256,192},{320,256},{384,320},{448,384},... | collective-permute-start | bytes 294920 | tf_op jit(solution)/shard_map/ppermute | solution.py:20
  162.9 10.7 %collective-permute-start.29 = (bf16[1,6,32,256]{3,2,1,0:T(8,128)(2,1)}, bf16[1,6,32,256]{3,2,1,0:T(8,128)(2,1)}, u32[]{:S(2)}, u32[]{:S(2)}) collective-permute-start(bf16[1,6,32,256]{3,2,1,0:T(8,128)(2,1)} %get-tuple-element.69), channel_id=1, source_target_pairs={{0,64},{64,128},{128,192},{192,256},{256,320},{320,384},{384,448},... | collective-permute-start | bytes 294920 | tf_op jit(solution)/shard_map/ppermute | solution.py:17
  172.4 3.1 %copy-start.12 = (f32[1,1,32,256]{3,2,1,0:T(8,128)S(1)}, f32[1,1,32,256]{3,2,1,0:T(8,128)}, u32[]{:S(2)}) copy-start(f32[1,1,32,256]{3,2,1,0:T(8,128)} %get-tuple-element.79) | copy-start | bytes 98308
  172.4 3.1 %copy-start.13 = (f32[1,1,32,256]{3,2,1,0:T(8,128)S(1)}, f32[1,1,32,256]{3,2,1,0:T(8,128)}, u32[]{:S(2)}) copy-start(f32[1,1,32,256]{3,2,1,0:T(8,128)} %get-tuple-element.80) | copy-start | bytes 98308
  176.4 10.1 %collective-permute-start.30 = (bf16[1,4,32,256]{3,2,1,0:T(8,128)(2,1)}, bf16[1,4,32,256]{3,2,1,0:T(8,128)(2,1)}, u32[]{:S(2)}, u32[]{:S(2)}) collective-permute-start(bf16[1,4,32,256]{3,2,1,0:T(8,128)(2,1)} %get-tuple-element.71), channel_id=1, source_target_pairs={{64,0},{128,64},{192,128},{256,192},{320,256},{384,320},{448,384},... | collective-permute-start | bytes 196616 | tf_op jit(solution)/shard_map/ppermute | solution.py:20
  177.7 8.8 %collective-permute-start.31 = (bf16[1,4,32,256]{3,2,1,0:T(8,128)(2,1)}, bf16[1,4,32,256]{3,2,1,0:T(8,128)(2,1)}, u32[]{:S(2)}, u32[]{:S(2)}) collective-permute-start(bf16[1,4,32,256]{3,2,1,0:T(8,128)(2,1)} %get-tuple-element.71), channel_id=1, source_target_pairs={{0,64},{64,128},{128,192},{192,256},{256,320},{320,384},{384,448},... | collective-permute-start | bytes 196616 | tf_op jit(solution)/shard_map/ppermute | solution.py:17
  188.3 58.3 %copy-start.11 = (bf16[1,4,32,256]{3,2,1,0:T(8,128)(2,1)S(1)}, bf16[1,4,32,256]{3,2,1,0:T(8,128)(2,1)}, u32[]{:S(2)}) copy-start(bf16[1,4,32,256]{3,2,1,0:T(8,128)(2,1)} %get-tuple-element.72) | copy-start | bytes 196612
  189.7 51.5 %all-to-all-start.1 = ((f32[512,1,256]{2,1,0:T(1,128)}), f32[512,1,256]{2,1,0:T(1,128)S(1)}, u32[]{:S(2)}, u32[]{:S(2)}) async-start(f32[512,1,256]{2,1,0:T(1,128)} %all_to_all.17), calls=%async_computation.1 | async-start | bytes 1048576 | tf_op jit(solution)/shard_map/all_to_all | solution.py:236
  242.4 14.0 %all-to-all-start.2 = ((f32[64,1,256]{2,1,0:T(1,128)}), f32[64,1,256]{2,1,0:T(1,128)S(1)}, u32[]{:S(2)}, u32[]{:S(2)}) async-start(f32[64,1,256]{2,1,0:T(1,128)} %broadcast_in_dim.22), calls=%async_computation.2 | async-start | bytes 131072 | tf_op jit(solution)/shard_map/all_to_all | solution.py:237
  (7 other events, 14.0 us)

commit v15 on v12

--- a/solution.py
+++ b/solution.py
@@ -126,7 +126,9 @@
     segment = lax.axis_index("segment")
 
     block = acts[0].reshape(count, -1, width)
-    kernels = jnp.concatenate([w_plane.reshape(-1), w_depth.reshape(-1)]).reshape(-1, width)
+    kernels = jnp.concatenate(
+        [w_plane.reshape(-1, chans, chans), w_depth.reshape(-1, chans, chans)]
+    ).reshape(-1, width)
     send = jnp.concatenate([block, jnp.broadcast_to(kernels[None], (count,) + kernels.shape)], axis=1)
     got = lax.all_to_all(send, "segment", 0, 0, tiled=True)
     cut_a = block.shape[1]

time: 244 us -> 244 us (level)
  no operation moved by 1% of the time
where the time goes in v15:
time: 244 us; the launch traced here: 242 us
  starting transfers between devices  129 us (53%)
  waiting for transfers between devices  75.5 us (31%)
  local copies, waits for them, and re-layouts  18.6 us (8%)
  matrix products  11.8 us (5%)
  other arithmetic  4.97 us (2%)
    ppermute x10, starting transfers between devices, padded_2(): lax.ppermute(lax.slice_in_dim(block, block.shape[dim] - width, None, axis...  44.1 us
    all_to_all x1, starting transfers between devices, local(): part = lax.all_to_all(flat, ('segment', 'gy'), 0, 0, tiled=True).sum(axis=0)  28.9 us
    ppermute x8, starting transfers between devices, passed_along(): return lax.ppermute(block, axis, route)  27.5 us
    all_to_all x1, waiting for transfers between devices, local(): part = lax.all_to_all(flat, ('segment', 'gy'), 0, 0, tiled=True).sum(axis=0)  22.3 us
    all_to_all x1, waiting for transfers between devices, local(): got = lax.all_to_all(send, 'segment', 0, 0, tiled=True)  16.2 us
    ppermute x10, starting transfers between devices, padded_2(): lax.ppermute(lax.slice_in_dim(block, 0, width, axis=dim), axis, backward)  13.5 us
    all_to_all x1, starting transfers between devices, local(): got = lax.all_to_all(send, 'segment', 0, 0, tiled=True)  10.9 us
    ppermute x10, waiting for transfers between devices, padded_2(): lax.ppermute(lax.slice_in_dim(block, 0, width, axis=dim), axis, backward)  9.76 us
  transfers between devices with their start and end apart: 31, of which 19 were waited for; matrix products, arithmetic and copies ran while one was open for 5% of the time, Pallas kernels for 0%

profile of v15, /device:TPU:1, one launch (start us, length us, event | category | flops | bytes accessed | tf_op | source)
XLA Modules:
  0.0 242.1 jit_solution(14448458836842805119)
XLA Ops:
  1.7 1.8 pad_maximum_fusion
  3.5 10.9 %all-to-all-start = ((bf16[8,112,256]{2,1,0:T(8,128)(2,1)}), bf16[8,112,256]{2,1,0:T(8,128)(2,1)S(1)}, u32[]{:S(2)}, u32[]{:S(2)}) async-start(bf16[8,112,256]{2,1,0:T(8,128)(2,1)} %pad_maximum_fusion), calls=%async_computation | async-start | bytes 917504 | tf_op jit(solution)/shard_map/all_to_all | solution.py:133
  14.6 16.2 %all-to-all-done = bf16[8,112,256]{2,1,0:T(8,128)(2,1)S(1)} async-done(((bf16[8,112,256]{2,1,0:T(8,128)(2,1)}), bf16[8,112,256]{2,1,0:T(8,128)(2,1)S(1)}, u32[]{:S(2)}, u32[]{:S(2)}) %all-to-all-start) | async-done | bytes 458784 | tf_op jit(solution)/shard_map/all_to_all | solution.py:133
  32.7 3.7 %collective-permute-start = (bf16[8,1,1,32,256]{4,3,2,0,1:T(8,128)(2,1)}, bf16[8,1,1,32,256]{4,3,2,0,1:T(8,128)(2,1)S(1)}, u32[]{:S(2)}, u32[]{:S(2)}) collective-permute-start(bf16[8,1,1,32,256]{4,3,2,0,1:T(8,128)(2,1)} %get-tuple-element.48), channel_id=1, source_target_pairs={{0,1},{1,2},{2,3},{3,4},{4,5},{5,6},{6,7},{7,8},{8,9},{9,10},{10,1... | collective-permute-start | bytes 393224 | tf_op jit(solution)/shard_map/ppermute | solution.py:17
  36.4 1.9 collective-permute-start.1
  39.6 3.3 %collective-permute-done.1 = bf16[8,1,1,32,256]{4,3,2,0,1:T(8,128)(2,1)S(1)} collective-permute-done((bf16[8,1,1,32,256]{4,3,2,0,1:T(8,128)(2,1)}, bf16[8,1,1,32,256]{4,3,2,0,1:T(8,128)(2,1)S(1)}, u32[]{:S(2)}, u32[]{:S(2)}) %collective-permute-start.1) | collective-permute-done | bytes 131104 | tf_op jit(solution)/shard_map/ppermute | solution.py:20
  44.5 2.2 collective-permute-start.2
  46.7 1.3 collective-permute-start.3
  48.8 1.4 collective-permute-done.2
  50.2 4.1 %collective-permute-done.3 = bf16[8,1,2,32,256]{4,3,2,0,1:T(8,128)(2,1)S(1)} collective-permute-done((bf16[8,1,2,32,256]{4,3,2,0,1:T(8,128)(2,1)S(1)}, bf16[8,1,2,32,256]{4,3,2,0,1:T(8,128)(2,1)S(1)}, u32[]{:S(2)}, u32[]{:S(2)}) %collective-permute-start.3) | collective-permute-done | bytes 262176 | tf_op jit(solution)/shard_map/ppermute | solution.py:20
  54.7 5.0 %collective-permute-start.4 = (bf16[5,1,2,32,256]{4,3,2,1,0:T(8,128)(2,1)S(1)}, bf16[5,1,2,32,256]{4,3,2,1,0:T(8,128)(2,1)S(1)}, u32[]{:S(2)}, u32[]{:S(2)}) collective-permute-start(bf16[5,1,2,32,256]{4,3,2,1,0:T(8,128)(2,1)S(1)} %pad_maximum_fusion.4), channel_id=1, source_target_pairs={{0,2},{1,3},{2,4},{3,5},{4,6},{5,7},{6,8},{7,9},{8,10},{9,11},{10,... | collective-permute-start | bytes 491528 | tf_op jit(solution)/shard_map/ppermute | solution.py:28
  59.8 1.3 collective-permute-start.7
  61.1 4.7 %collective-permute-start.5 = (bf16[9,1,2,32,256]{4,3,2,1,0:T(8,128)(2,1)S(1)}, bf16[9,1,2,32,256]{4,3,2,1,0:T(8,128)(2,1)S(1)}, u32[]{:S(2)}, u32[]{:S(2)}) collective-permute-start(bf16[9,1,2,32,256]{4,3,2,1,0:T(8,128)(2,1)S(1)} %pad_maximum_fusion.1), channel_id=1, source_target_pairs={{0,1},{1,2},{2,3},{3,4},{4,5},{5,6},{6,7},{7,8},{8,9},{9,10},{10,1... | collective-permute-start | bytes 884744 | tf_op jit(solution)/shard_map/ppermute | solution.py:28
  65.9 1.9 collective-permute-start.6
  67.9 1.6 collective-permute-done.5
  69.6 4.3 %collective-permute-done.6 = bf16[9,1,2,32,256]{4,3,2,1,0:T(8,128)(2,1)S(1)} collective-permute-done((bf16[9,1,2,32,256]{4,3,2,1,0:T(8,128)(2,1)S(1)}, bf16[9,1,2,32,256]{4,3,2,1,0:T(8,128)(2,1)S(1)}, u32[]{:S(2)}, u32[]{:S(2)}) %collective-permute-start.6) | collective-permute-done | bytes 294944 | tf_op jit(solution)/shard_map/ppermute | solution.py:28
  74.0 1.3 collective-permute-start.8
  75.3 4.0 %collective-permute-start.9 = (bf16[1,10,32,256]{3,2,1,0:T(8,128)(2,1)S(1)}, bf16[1,10,32,256]{3,2,1,0:T(8,128)(2,1)S(1)}, u32[]{:S(2)}, u32[]{:S(2)}) collective-permute-start(bf16[1,10,32,256]{3,2,1,0:T(8,128)(2,1)S(1)} %fusion.75), channel_id=1, source_target_pairs={{0,64},{64,128},{128,192},{192,256},{256,320},{320,384},{384,448},... | collective-permute-start | bytes 491528 | tf_op jit(solution)/shard_map/ppermute | solution.py:17
  80.1 1.5 collective-permute-done.9
  82.9 1.3 collective-permute-start.10
  84.2 4.4 %collective-permute-start.11 = (bf16[1,8,32,256]{3,2,1,0:T(8,128)(2,1)S(1)}, bf16[1,8,32,256]{3,2,1,0:T(8,128)(2,1)S(1)}, u32[]{:S(2)}, u32[]{:S(2)}) collective-permute-start(bf16[1,8,32,256]{3,2,1,0:T(8,128)(2,1)S(1)} %get-tuple-element.5), channel_id=1, source_target_pairs={{0,64},{64,128},{128,192},{192,256},{256,320},{320,384},{384,448},... | collective-permute-start | bytes 393224 | tf_op jit(solution)/shard_map/ppermute | solution.py:17
  89.1 1.5 collective-permute-done.11
  91.9 1.3 collective-permute-start.12
  93.2 4.4 %collective-permute-start.13 = (bf16[1,6,32,256]{3,2,1,0:T(8,128)(2,1)S(1)}, bf16[1,6,32,256]{3,2,1,0:T(8,128)(2,1)S(1)}, u32[]{:S(2)}, u32[]{:S(2)}) collective-permute-start(bf16[1,6,32,256]{3,2,1,0:T(8,128)(2,1)S(1)} %get-tuple-element.60), channel_id=1, source_target_pairs={{0,64},{64,128},{128,192},{192,256},{256,320},{320,384},{384,448},... | collective-permute-start | bytes 294920 | tf_op jit(solution)/shard_map/ppermute | solution.py:17
  97.7 1.6 collective-permute-done.13
  100.3 1.3 collective-permute-start.14
  101.6 4.4 %collective-permute-start.15 = (bf16[1,4,32,256]{3,2,1,0:T(8,128)(2,1)S(1)}, bf16[1,4,32,256]{3,2,1,0:T(8,128)(2,1)S(1)}, u32[]{:S(2)}, u32[]{:S(2)}) collective-permute-start(bf16[1,4,32,256]{3,2,1,0:T(8,128)(2,1)S(1)} %get-tuple-element.62), channel_id=1, source_target_pairs={{0,64},{64,128},{128,192},{192,256},{256,320},{320,384},{384,448},... | collective-permute-start | bytes 196616 | tf_op jit(solution)/shard_map/ppermute | solution.py:17
  108.4 5.3 %collective-permute-start.16 = (bf16[1,2,32,256]{3,2,1,0:T(8,128)(2,1)S(1)}, bf16[1,2,32,256]{3,2,1,0:T(8,128)(2,1)S(1)}, u32[]{:S(2)}, u32[]{:S(2)}) collective-permute-start(bf16[1,2,32,256]{3,2,1,0:T(8,128)(2,1)S(1)} %fusion.39), channel_id=1, source_target_pairs={{0,2},{1,3},{2,4},{3,5},{4,6},{5,7},{6,8},{7,9},{8,10},{9,11},{10,... | collective-permute-start | bytes 98312 | tf_op jit(solution)/shard_map/ppermute | solution.py:28
  113.7 6.1 %collective-permute-start.17 = (bf16[1,2,32,256]{3,2,1,0:T(8,128)(2,1)S(1)}, bf16[1,2,32,256]{3,2,1,0:T(8,128)(2,1)S(1)}, u32[]{:S(2)}, u32[]{:S(2)}) collective-permute-start(bf16[1,2,32,256]{3,2,1,0:T(8,128)(2,1)S(1)} %fusion.39), channel_id=1, source_target_pairs={{0,1},{1,2},{2,3},{3,4},{4,5},{5,6},{6,7},{7,8},{8,9},{9,10},{10,1... | collective-permute-start | bytes 98312 | tf_op jit(solution)/shard_map/ppermute | solution.py:28
  119.8 1.9 collective-permute-start.18
  121.8 1.3 collective-permute-start.19
  123.1 1.9 collective-permute-done.18
  125.1 1.3 collective-permute-done.19
  126.5 1.3 collective-permute-start.20
  127.8 4.6 %collective-permute-start.21 = (bf16[1,10,32,256]{3,2,1,0:T(8,128)(2,1)S(1)}, bf16[1,10,32,256]{3,2,1,0:T(8,128)(2,1)S(1)}, u32[]{:S(2)}, u32[]{:S(2)}) collective-permute-start(bf16[1,10,32,256]{3,2,1,0:T(8,128)(2,1)S(1)} %fusion.76), channel_id=1, source_target_pairs={{0,64},{64,128},{128,192},{192,256},{256,320},{320,384},{384,448},... | collective-permute-start | bytes 491528 | tf_op jit(solution)/shard_map/ppermute | solution.py:17
  132.5 1.2 collective-permute-done.20
  136.0 1.3 collective-permute-start.22
  137.3 4.7 %collective-permute-start.23 = (bf16[1,8,32,256]{3,2,1,0:T(8,128)(2,1)S(1)}, bf16[1,8,32,256]{3,2,1,0:T(8,128)(2,1)S(1)}, u32[]{:S(2)}, u32[]{:S(2)}) collective-permute-start(bf16[1,8,32,256]{3,2,1,0:T(8,128)(2,1)S(1)} %get-tuple-element.3), channel_id=1, source_target_pairs={{0,64},{64,128},{128,192},{192,256},{256,320},{320,384},{384,448},... | collective-permute-start | bytes 393224 | tf_op jit(solution)/shard_map/ppermute | solution.py:17
  142.7 1.3 collective-permute-done.23
  145.9 1.3 collective-permute-start.24
  147.2 5.8 %collective-permute-start.25 = (bf16[1,6,32,256]{3,2,1,0:T(8,128)(2,1)}, bf16[1,6,32,256]{3,2,1,0:T(8,128)(2,1)}, u32[]{:S(2)}, u32[]{:S(2)}) collective-permute-start(bf16[1,6,32,256]{3,2,1,0:T(8,128)(2,1)} %get-tuple-element.64), channel_id=1, source_target_pairs={{0,64},{64,128},{128,192},{192,256},{256,320},{320,384},{384,448},... | collective-permute-start | bytes 294920 | tf_op jit(solution)/shard_map/ppermute | solution.py:17
  160.7 1.3 collective-permute-start.26
  162.0 5.8 %collective-permute-start.27 = (bf16[1,4,32,256]{3,2,1,0:T(8,128)(2,1)}, bf16[1,4,32,256]{3,2,1,0:T(8,128)(2,1)}, u32[]{:S(2)}, u32[]{:S(2)}) collective-permute-start(bf16[1,4,32,256]{3,2,1,0:T(8,128)(2,1)} %get-tuple-element.66), channel_id=1, source_target_pairs={{0,64},{64,128},{128,192},{192,256},{256,320},{320,384},{384,448},... | collective-permute-start | bytes 196616 | tf_op jit(solution)/shard_map/ppermute | solution.py:17
  172.2 1.4 all_to_all.17
  173.6 28.9 %all-to-all-start.1 = ((f32[512,1,256]{2,1,0:T(1,128)}), f32[512,1,256]{2,1,0:T(1,128)S(1)}, u32[]{:S(2)}, u32[]{:S(2)}) async-start(f32[512,1,256]{2,1,0:T(1,128)} %all_to_all.17), calls=%async_computation.1 | async-start | bytes 1048576 | tf_op jit(solution)/shard_map/all_to_all | solution.py:223
  203.0 22.3 %all-to-all-done.1 = f32[512,1,256]{2,1,0:T(1,128)S(1)} async-done(((f32[512,1,256]{2,1,0:T(1,128)}), f32[512,1,256]{2,1,0:T(1,128)S(1)}, u32[]{:S(2)}, u32[]{:S(2)}) %all-to-all-start.1) | async-done | bytes 524320 | tf_op jit(solution)/shard_map/all_to_all | solution.py:223
  226.5 4.2 %all-to-all-start.2 = ((f32[64,1,256]{2,1,0:T(1,128)}), f32[64,1,256]{2,1,0:T(1,128)S(1)}, u32[]{:S(2)}, u32[]{:S(2)}) async-start(f32[64,1,256]{2,1,0:T(1,128)} %broadcast_in_dim.22), calls=%async_computation.2 | async-start | bytes 131072 | tf_op jit(solution)/shard_map/all_to_all | solution.py:224
  231.5 9.0 %all-to-all-done.2 = f32[64,1,256]{2,1,0:T(1,128)S(1)} async-done(((f32[64,1,256]{2,1,0:T(1,128)}), f32[64,1,256]{2,1,0:T(1,128)S(1)}, u32[]{:S(2)}, u32[]{:S(2)}) %all-to-all-start.2) | async-done | bytes 65568 | tf_op jit(solution)/shard_map/all_to_all | solution.py:224
  (257 shorter events, 35.0 us)
Async XLA Ops:
  0.6 13.7 %copy-start.14 = (s32[1,12]{1,0:T(1,128)S(1)}, s32[1,12]{1,0:T(1,128)}, u32[]{:S(2)}) copy-start(s32[1,12]{1,0:T(1,128)} %param.9) | copy-start | bytes 148
  3.5 27.3 %all-to-all-start = ((bf16[8,112,256]{2,1,0:T(8,128)(2,1)}), bf16[8,112,256]{2,1,0:T(8,128)(2,1)S(1)}, u32[]{:S(2)}, u32[]{:S(2)}) async-start(bf16[8,112,256]{2,1,0:T(8,128)(2,1)} %pad_maximum_fusion), calls=%async_computation | async-start | bytes 917504 | tf_op jit(solution)/shard_map/all_to_all | solution.py:133
  32.7 6.9 %collective-permute-start = (bf16[8,1,1,32,256]{4,3,2,0,1:T(8,128)(2,1)}, bf16[8,1,1,32,256]{4,3,2,0,1:T(8,128)(2,1)S(1)}, u32[]{:S(2)}, u32[]{:S(2)}) collective-permute-start(bf16[8,1,1,32,256]{4,3,2,0,1:T(8,128)(2,1)} %get-tuple-element.48), channel_id=1, source_target_pairs={{0,1},{1,2},{2,3},{3,4},{4,5},{5,6},{6,7},{7,8},{8,9},{9,10},{10,1... | collective-permute-start | bytes 393224 | tf_op jit(solution)/shard_map/ppermute | solution.py:17
  36.4 6.5 %collective-permute-start.1 = (bf16[8,1,1,32,256]{4,3,2,0,1:T(8,128)(2,1)}, bf16[8,1,1,32,256]{4,3,2,0,1:T(8,128)(2,1)S(1)}, u32[]{:S(2)}, u32[]{:S(2)}) collective-permute-start(bf16[8,1,1,32,256]{4,3,2,0,1:T(8,128)(2,1)} %get-tuple-element.49), channel_id=1, source_target_pairs={{1,0},{2,1},{3,2},{4,3},{5,4},{6,5},{7,6},{8,7},{9,8},{10,9},{11,1... | collective-permute-start | bytes 393224 | tf_op jit(solution)/shard_map/ppermute | solution.py:20
  44.5 5.7 %collective-permute-start.2 = (bf16[8,1,2,32,256]{4,3,2,0,1:T(8,128)(2,1)S(1)}, bf16[8,1,2,32,256]{4,3,2,0,1:T(8,128)(2,1)S(1)}, u32[]{:S(2)}, u32[]{:S(2)}) collective-permute-start(bf16[8,1,2,32,256]{4,3,2,0,1:T(8,128)(2,1)S(1)} %fusion.12), channel_id=1, source_target_pairs={{0,64},{64,128},{128,192},{192,256},{256,320},{320,384},{384,448},... | collective-permute-start | bytes 786440 | tf_op jit(solution)/shard_map/ppermute | solution.py:17
  46.7 7.6 %collective-permute-start.3 = (bf16[8,1,2,32,256]{4,3,2,0,1:T(8,128)(2,1)S(1)}, bf16[8,1,2,32,256]{4,3,2,0,1:T(8,128)(2,1)S(1)}, u32[]{:S(2)}, u32[]{:S(2)}) collective-permute-start(bf16[8,1,2,32,256]{4,3,2,0,1:T(8,128)(2,1)S(1)} %fusion.12), channel_id=1, source_target_pairs={{64,0},{128,64},{192,128},{256,192},{320,256},{384,320},{448,384},... | collective-permute-start | bytes 786440 | tf_op jit(solution)/shard_map/ppermute | solution.py:20
  48.8 5.9 %copy-start.2 = (bf16[1,2,32,256]{3,2,1,0:T(8,128)(2,1)S(1)}, bf16[1,2,32,256]{3,2,1,0:T(8,128)(2,1)}, u32[]{:S(2)}) copy-start(bf16[1,2,32,256]{3,2,1,0:T(8,128)(2,1)} %param.6) | copy-start | bytes 98308
  50.2 56.4 %copy-start.8 = (bf16[8,1,2,32,256]{4,3,2,0,1:T(8,128)(2,1)}, bf16[8,1,2,32,256]{4,3,2,0,1:T(8,128)(2,1)S(1)}, u32[]{:S(2)}) copy-start(bf16[8,1,2,32,256]{4,3,2,0,1:T(8,128)(2,1)S(1)} %collective-permute-done.2) | copy-start | bytes 786436
  54.3 52.3 %copy-start.9 = (bf16[8,1,2,32,256]{4,3,2,0,1:T(8,128)(2,1)}, bf16[8,1,2,32,256]{4,3,2,0,1:T(8,128)(2,1)S(1)}, u32[]{:S(2)}) copy-start(bf16[8,1,2,32,256]{4,3,2,0,1:T(8,128)(2,1)S(1)} %collective-permute-done.3) | copy-start | bytes 786436
  54.7 13.1 %collective-permute-start.4 = (bf16[5,1,2,32,256]{4,3,2,1,0:T(8,128)(2,1)S(1)}, bf16[5,1,2,32,256]{4,3,2,1,0:T(8,128)(2,1)S(1)}, u32[]{:S(2)}, u32[]{:S(2)}) collective-permute-start(bf16[5,1,2,32,256]{4,3,2,1,0:T(8,128)(2,1)S(1)} %pad_maximum_fusion.4), channel_id=1, source_target_pairs={{0,2},{1,3},{2,4},{3,5},{4,6},{5,7},{6,8},{7,9},{8,10},{9,11},{10,... | collective-permute-start | bytes 491528 | tf_op jit(solution)/shard_map/ppermute | solution.py:28
  59.8 8.1 %collective-permute-start.7 = (bf16[5,1,2,32,256]{4,3,2,1,0:T(8,128)(2,1)S(1)}, bf16[5,1,2,32,256]{4,3,2,1,0:T(8,128)(2,1)S(1)}, u32[]{:S(2)}, u32[]{:S(2)}) collective-permute-start(bf16[5,1,2,32,256]{4,3,2,1,0:T(8,128)(2,1)S(1)} %pad_maximum_fusion.4), channel_id=1, source_target_pairs={{2,0},{3,1},{4,2},{5,3},{6,4},{7,5},{8,6},{9,7},{10,8},{11,9},{12,... | collective-permute-start | bytes 491528 | tf_op jit(solution)/shard_map/ppermute | solution.py:28
  61.1 8.4 %collective-permute-start.5 = (bf16[9,1,2,32,256]{4,3,2,1,0:T(8,128)(2,1)S(1)}, bf16[9,1,2,32,256]{4,3,2,1,0:T(8,128)(2,1)S(1)}, u32[]{:S(2)}, u32[]{:S(2)}) collective-permute-start(bf16[9,1,2,32,256]{4,3,2,1,0:T(8,128)(2,1)S(1)} %pad_maximum_fusion.1), channel_id=1, source_target_pairs={{0,1},{1,2},{2,3},{3,4},{4,5},{5,6},{6,7},{7,8},{8,9},{9,10},{10,1... | collective-permute-start | bytes 884744 | tf_op jit(solution)/shard_map/ppermute | solution.py:28
  65.9 8.0 %collective-permute-start.6 = (bf16[9,1,2,32,256]{4,3,2,1,0:T(8,128)(2,1)S(1)}, bf16[9,1,2,32,256]{4,3,2,1,0:T(8,128)(2,1)S(1)}, u32[]{:S(2)}, u32[]{:S(2)}) collective-permute-start(bf16[9,1,2,32,256]{4,3,2,1,0:T(8,128)(2,1)S(1)} %pad_maximum_fusion.1), channel_id=1, source_target_pairs={{1,0},{2,1},{3,2},{4,3},{5,4},{6,5},{7,6},{8,7},{9,8},{10,9},{11,1... | collective-permute-start | bytes 884744 | tf_op jit(solution)/shard_map/ppermute | solution.py:28
  74.0 6.1 %collective-permute-start.8 = (bf16[1,10,32,256]{3,2,1,0:T(8,128)(2,1)S(1)}, bf16[1,10,32,256]{3,2,1,0:T(8,128)(2,1)S(1)}, u32[]{:S(2)}, u32[]{:S(2)}) collective-permute-start(bf16[1,10,32,256]{3,2,1,0:T(8,128)(2,1)S(1)} %fusion.75), channel_id=1, source_target_pairs={{64,0},{128,64},{192,128},{256,192},{320,256},{384,320},{448,384},... | collective-permute-start | bytes 491528 | tf_op jit(solution)/shard_map/ppermute | solution.py:20
  75.3 6.2 %collective-permute-start.9 = (bf16[1,10,32,256]{3,2,1,0:T(8,128)(2,1)S(1)}, bf16[1,10,32,256]{3,2,1,0:T(8,128)(2,1)S(1)}, u32[]{:S(2)}, u32[]{:S(2)}) collective-permute-start(bf16[1,10,32,256]{3,2,1,0:T(8,128)(2,1)S(1)} %fusion.75), channel_id=1, source_target_pairs={{0,64},{64,128},{128,192},{192,256},{256,320},{320,384},{384,448},... | collective-permute-start | bytes 491528 | tf_op jit(solution)/shard_map/ppermute | solution.py:17
  82.9 6.2 %collective-permute-start.10 = (bf16[1,8,32,256]{3,2,1,0:T(8,128)(2,1)S(1)}, bf16[1,8,32,256]{3,2,1,0:T(8,128)(2,1)S(1)}, u32[]{:S(2)}, u32[]{:S(2)}) collective-permute-start(bf16[1,8,32,256]{3,2,1,0:T(8,128)(2,1)S(1)} %get-tuple-element.5), channel_id=1, source_target_pairs={{64,0},{128,64},{192,128},{256,192},{320,256},{384,320},{448,384},... | collective-permute-start | bytes 393224 | tf_op jit(solution)/shard_map/ppermute | solution.py:20
  84.2 6.4 %collective-permute-start.11 = (bf16[1,8,32,256]{3,2,1,0:T(8,128)(2,1)S(1)}, bf16[1,8,32,256]{3,2,1,0:T(8,128)(2,1)S(1)}, u32[]{:S(2)}, u32[]{:S(2)}) collective-permute-start(bf16[1,8,32,256]{3,2,1,0:T(8,128)(2,1)S(1)} %get-tuple-element.5), channel_id=1, source_target_pairs={{0,64},{64,128},{128,192},{192,256},{256,320},{320,384},{384,448},... | collective-permute-start | bytes 393224 | tf_op jit(solution)/shard_map/ppermute | solution.py:17
  88.8 3.1 %copy-start = (bf16[1,1,2,288,256]{4,3,2,0,1:T(8,128)(2,1)}, bf16[1,1,2,288,256]{4,3,2,0,1:T(8,128)(2,1)S(1)}, u32[]{:S(2)}) copy-start(bf16[1,1,2,288,256]{4,3,2,0,1:T(8,128)(2,1)S(1)} %constant_dynamic-update-slice_fusion.83) | copy-start | bytes 884740
  91.5 8.5 %copy-start.4 = (bf16[1,9,32,32]{3,2,1,0:T(8,128)(2,1)S(1)}, bf16[1,9,32,32]{3,2,1,0:T(8,128)(2,1)}, u32[]{:S(2)}) copy-start(bf16[1,9,32,32]{3,2,1,0:T(8,128)(2,1)} %get-tuple-element.21) | copy-start | bytes 55300
  91.9 5.8 %collective-permute-start.12 = (bf16[1,6,32,256]{3,2,1,0:T(8,128)(2,1)S(1)}, bf16[1,6,32,256]{3,2,1,0:T(8,128)(2,1)S(1)}, u32[]{:S(2)}, u32[]{:S(2)}) collective-permute-start(bf16[1,6,32,256]{3,2,1,0:T(8,128)(2,1)S(1)} %get-tuple-element.60), channel_id=1, source_target_pairs={{64,0},{128,64},{192,128},{256,192},{320,256},{384,320},{448,384},... | collective-permute-start | bytes 294920 | tf_op jit(solution)/shard_map/ppermute | solution.py:20
  93.2 6.0 %collective-permute-start.13 = (bf16[1,6,32,256]{3,2,1,0:T(8,128)(2,1)S(1)}, bf16[1,6,32,256]{3,2,1,0:T(8,128)(2,1)S(1)}, u32[]{:S(2)}, u32[]{:S(2)}) collective-permute-start(bf16[1,6,32,256]{3,2,1,0:T(8,128)(2,1)S(1)} %get-tuple-element.60), channel_id=1, source_target_pairs={{0,64},{64,128},{128,192},{192,256},{256,320},{320,384},{384,448},... | collective-permute-start | bytes 294920 | tf_op jit(solution)/shard_map/ppermute | solution.py:17
  100.3 6.3 %collective-permute-start.14 = (bf16[1,4,32,256]{3,2,1,0:T(8,128)(2,1)S(1)}, bf16[1,4,32,256]{3,2,1,0:T(8,128)(2,1)S(1)}, u32[]{:S(2)}, u32[]{:S(2)}) collective-permute-start(bf16[1,4,32,256]{3,2,1,0:T(8,128)(2,1)S(1)} %get-tuple-element.62), channel_id=1, source_target_pairs={{64,0},{128,64},{192,128},{256,192},{320,256},{384,320},{448,384},... | collective-permute-start | bytes 196616 | tf_op jit(solution)/shard_map/ppermute | solution.py:20
  101.6 5.9 %collective-permute-start.15 = (bf16[1,4,32,256]{3,2,1,0:T(8,128)(2,1)S(1)}, bf16[1,4,32,256]{3,2,1,0:T(8,128)(2,1)S(1)}, u32[]{:S(2)}, u32[]{:S(2)}) collective-permute-start(bf16[1,4,32,256]{3,2,1,0:T(8,128)(2,1)S(1)} %get-tuple-element.62), channel_id=1, source_target_pairs={{0,64},{64,128},{128,192},{192,256},{256,320},{320,384},{384,448},... | collective-permute-start | bytes 196616 | tf_op jit(solution)/shard_map/ppermute | solution.py:17
  106.6 25.8 %slice-start = ((bf16[8,1,2,32,256]{4,3,2,0,1:T(8,128)(2,1)}), bf16[1,1,2,32,256]{4,3,2,0,1:T(8,128)(2,1)S(1)}, s32[]{:S(2)}) async-start(bf16[8,1,2,32,256]{4,3,2,0,1:T(8,128)(2,1)} %copy-done.8), calls=%async_computation.3 | async-start | bytes 65536 | tf_op jit(solution)/shard_map/slice | solution.py:209
  106.6 25.8 %slice-start.2 = ((bf16[8,1,2,32,256]{4,3,2,0,1:T(8,128)(2,1)}), bf16[1,1,2,32,256]{4,3,2,0,1:T(8,128)(2,1)S(1)}, s32[]{:S(2)}) async-start(bf16[8,1,2,32,256]{4,3,2,0,1:T(8,128)(2,1)} %copy-done.9), calls=%async_computation.5 | async-start | bytes 65536 | tf_op jit(solution)/shard_map/slice | solution.py:209
  108.4 14.6 %collective-permute-start.16 = (bf16[1,2,32,256]{3,2,1,0:T(8,128)(2,1)S(1)}, bf16[1,2,32,256]{3,2,1,0:T(8,128)(2,1)S(1)}, u32[]{:S(2)}, u32[]{:S(2)}) collective-permute-start(bf16[1,2,32,256]{3,2,1,0:T(8,128)(2,1)S(1)} %fusion.39), channel_id=1, source_target_pairs={{0,2},{1,3},{2,4},{3,5},{4,6},{5,7},{6,8},{7,9},{8,10},{9,11},{10,... | collective-permute-start | bytes 98312 | tf_op jit(solution)/shard_map/ppermute | solution.py:28
  113.7 9.3 %collective-permute-start.17 = (bf16[1,2,32,256]{3,2,1,0:T(8,128)(2,1)S(1)}, bf16[1,2,32,256]{3,2,1,0:T(8,128)(2,1)S(1)}, u32[]{:S(2)}, u32[]{:S(2)}) collective-permute-start(bf16[1,2,32,256]{3,2,1,0:T(8,128)(2,1)S(1)} %fusion.39), channel_id=1, source_target_pairs={{0,1},{1,2},{2,3},{3,4},{4,5},{5,6},{6,7},{7,8},{8,9},{9,10},{10,1... | collective-permute-start | bytes 98312 | tf_op jit(solution)/shard_map/ppermute | solution.py:28
  119.8 5.2 %collective-permute-start.18 = (bf16[1,2,32,256]{3,2,1,0:T(8,128)(2,1)S(1)}, bf16[1,2,32,256]{3,2,1,0:T(8,128)(2,1)S(1)}, u32[]{:S(2)}, u32[]{:S(2)}) collective-permute-start(bf16[1,2,32,256]{3,2,1,0:T(8,128)(2,1)S(1)} %fusion.39), channel_id=1, source_target_pairs={{1,0},{2,1},{3,2},{4,3},{5,4},{6,5},{7,6},{8,7},{9,8},{10,9},{11,1... | collective-permute-start | bytes 98312 | tf_op jit(solution)/shard_map/ppermute | solution.py:28
  121.8 4.7 %collective-permute-start.19 = (bf16[1,2,32,256]{3,2,1,0:T(8,128)(2,1)S(1)}, bf16[1,2,32,256]{3,2,1,0:T(8,128)(2,1)S(1)}, u32[]{:S(2)}, u32[]{:S(2)}) collective-permute-start(bf16[1,2,32,256]{3,2,1,0:T(8,128)(2,1)S(1)} %fusion.39), channel_id=1, source_target_pairs={{2,0},{3,1},{4,2},{5,3},{6,4},{7,5},{8,6},{9,7},{10,8},{11,9},{12,... | collective-permute-start | bytes 98312 | tf_op jit(solution)/shard_map/ppermute | solution.py:28
  126.5 7.2 %collective-permute-start.20 = (bf16[1,10,32,256]{3,2,1,0:T(8,128)(2,1)S(1)}, bf16[1,10,32,256]{3,2,1,0:T(8,128)(2,1)S(1)}, u32[]{:S(2)}, u32[]{:S(2)}) collective-permute-start(bf16[1,10,32,256]{3,2,1,0:T(8,128)(2,1)S(1)} %fusion.76), channel_id=1, source_target_pairs={{64,0},{128,64},{192,128},{256,192},{320,256},{384,320},{448,384},... | collective-permute-start | bytes 491528 | tf_op jit(solution)/shard_map/ppermute | solution.py:20
  127.8 6.9 %collective-permute-start.21 = (bf16[1,10,32,256]{3,2,1,0:T(8,128)(2,1)S(1)}, bf16[1,10,32,256]{3,2,1,0:T(8,128)(2,1)S(1)}, u32[]{:S(2)}, u32[]{:S(2)}) collective-permute-start(bf16[1,10,32,256]{3,2,1,0:T(8,128)(2,1)S(1)} %fusion.76), channel_id=1, source_target_pairs={{0,64},{64,128},{128,192},{192,256},{256,320},{320,384},{384,448},... | collective-permute-start | bytes 491528 | tf_op jit(solution)/shard_map/ppermute | solution.py:17
  134.6 1.0 copy-start.5
  136.0 6.7 %collective-permute-start.22 = (bf16[1,8,32,256]{3,2,1,0:T(8,128)(2,1)S(1)}, bf16[1,8,32,256]{3,2,1,0:T(8,128)(2,1)S(1)}, u32[]{:S(2)}, u32[]{:S(2)}) collective-permute-start(bf16[1,8,32,256]{3,2,1,0:T(8,128)(2,1)S(1)} %get-tuple-element.3), channel_id=1, source_target_pairs={{64,0},{128,64},{192,128},{256,192},{320,256},{384,320},{448,384},... | collective-permute-start | bytes 393224 | tf_op jit(solution)/shard_map/ppermute | solution.py:20
  137.3 6.7 %collective-permute-start.23 = (bf16[1,8,32,256]{3,2,1,0:T(8,128)(2,1)S(1)}, bf16[1,8,32,256]{3,2,1,0:T(8,128)(2,1)S(1)}, u32[]{:S(2)}, u32[]{:S(2)}) collective-permute-start(bf16[1,8,32,256]{3,2,1,0:T(8,128)(2,1)S(1)} %get-tuple-element.3), channel_id=1, source_target_pairs={{0,64},{64,128},{128,192},{192,256},{256,320},{320,384},{384,448},... | collective-permute-start | bytes 393224 | tf_op jit(solution)/shard_map/ppermute | solution.py:17
  144.4 9.4 %slice-start.1 = ((bf16[8,1,2,32,256]{4,3,2,0,1:T(8,128)(2,1)}), bf16[7,1,2,32,256]{4,3,2,0,1:T(8,128)(2,1)S(1)}, s32[]{:S(2)}) async-start(bf16[8,1,2,32,256]{4,3,2,0,1:T(8,128)(2,1)} %copy-done.8), calls=%async_computation.4 | async-start | bytes 458752 | tf_op jit(solution)/shard_map/slice | solution.py:209
  144.4 9.4 %slice-start.3 = ((bf16[8,1,2,32,256]{4,3,2,0,1:T(8,128)(2,1)}), bf16[7,1,2,32,256]{4,3,2,0,1:T(8,128)(2,1)S(1)}, s32[]{:S(2)}) async-start(bf16[8,1,2,32,256]{4,3,2,0,1:T(8,128)(2,1)} %copy-done.9), calls=%async_computation.6 | async-start | bytes 458752 | tf_op jit(solution)/shard_map/slice | solution.py:209
  145.9 12.0 %collective-permute-start.24 = (bf16[1,6,32,256]{3,2,1,0:T(8,128)(2,1)}, bf16[1,6,32,256]{3,2,1,0:T(8,128)(2,1)}, u32[]{:S(2)}, u32[]{:S(2)}) collective-permute-start(bf16[1,6,32,256]{3,2,1,0:T(8,128)(2,1)} %get-tuple-element.64), channel_id=1, source_target_pairs={{64,0},{128,64},{192,128},{256,192},{320,256},{384,320},{448,384},... | collective-permute-start | bytes 294920 | tf_op jit(solution)/shard_map/ppermute | solution.py:20
  147.2 10.7 %collective-permute-start.25 = (bf16[1,6,32,256]{3,2,1,0:T(8,128)(2,1)}, bf16[1,6,32,256]{3,2,1,0:T(8,128)(2,1)}, u32[]{:S(2)}, u32[]{:S(2)}) collective-permute-start(bf16[1,6,32,256]{3,2,1,0:T(8,128)(2,1)} %get-tuple-element.64), channel_id=1, source_target_pairs={{0,64},{64,128},{128,192},{192,256},{256,320},{320,384},{384,448},... | collective-permute-start | bytes 294920 | tf_op jit(solution)/shard_map/ppermute | solution.py:17
  156.0 3.8 %copy-start.3 = (bf16[1,9,32,32]{3,2,1,0:T(8,128)(2,1)S(1)}, bf16[1,9,32,32]{3,2,1,0:T(8,128)(2,1)}, u32[]{:S(2)}) copy-start(bf16[1,9,32,32]{3,2,1,0:T(8,128)(2,1)} %get-tuple-element.17) | copy-start | bytes 55300
  156.7 3.0 %copy-start.7 = (bf16[1,6,32,256]{3,2,1,0:T(8,128)(2,1)S(1)}, bf16[1,6,32,256]{3,2,1,0:T(8,128)(2,1)}, u32[]{:S(2)}) copy-start(bf16[1,6,32,256]{3,2,1,0:T(8,128)(2,1)} %get-tuple-element.65) | copy-start | bytes 294916
  156.7 3.1 %copy-start.10 = (f32[1,2,32,256]{3,2,1,0:T(8,128)S(1)}, f32[1,2,32,256]{3,2,1,0:T(8,128)}, u32[]{:S(2)}) copy-start(f32[1,2,32,256]{3,2,1,0:T(8,128)} %slice_bitcast_fusion.2) | copy-start | bytes 196612
  156.7 3.1 %copy-start.12 = (f32[1,1,32,256]{3,2,1,0:T(8,128)S(1)}, f32[1,1,32,256]{3,2,1,0:T(8,128)}, u32[]{:S(2)}) copy-start(f32[1,1,32,256]{3,2,1,0:T(8,128)} %get-tuple-element.75) | copy-start | bytes 98308
  160.7 9.7 %collective-permute-start.26 = (bf16[1,4,32,256]{3,2,1,0:T(8,128)(2,1)}, bf16[1,4,32,256]{3,2,1,0:T(8,128)(2,1)S(1)}, u32[]{:S(2)}, u32[]{:S(2)}) collective-permute-start(bf16[1,4,32,256]{3,2,1,0:T(8,128)(2,1)} %get-tuple-element.66), channel_id=1, source_target_pairs={{64,0},{128,64},{192,128},{256,192},{320,256},{384,320},{448,384},... | collective-permute-start | bytes 196616 | tf_op jit(solution)/shard_map/ppermute | solution.py:20
  162.0 8.4 %collective-permute-start.27 = (bf16[1,4,32,256]{3,2,1,0:T(8,128)(2,1)}, bf16[1,4,32,256]{3,2,1,0:T(8,128)(2,1)}, u32[]{:S(2)}, u32[]{:S(2)}) collective-permute-start(bf16[1,4,32,256]{3,2,1,0:T(8,128)(2,1)} %get-tuple-element.66), channel_id=1, source_target_pairs={{0,64},{64,128},{128,192},{192,256},{256,320},{320,384},{384,448},... | collective-permute-start | bytes 196616 | tf_op jit(solution)/shard_map/ppermute | solution.py:17
  169.5 2.1 copy-start.1
  172.2 58.5 %copy-start.11 = (bf16[1,4,32,256]{3,2,1,0:T(8,128)(2,1)S(1)}, bf16[1,4,32,256]{3,2,1,0:T(8,128)(2,1)}, u32[]{:S(2)}) copy-start(bf16[1,4,32,256]{3,2,1,0:T(8,128)(2,1)} %get-tuple-element.67) | copy-start | bytes 196612
  173.6 51.7 %all-to-all-start.1 = ((f32[512,1,256]{2,1,0:T(1,128)}), f32[512,1,256]{2,1,0:T(1,128)S(1)}, u32[]{:S(2)}, u32[]{:S(2)}) async-start(f32[512,1,256]{2,1,0:T(1,128)} %all_to_all.17), calls=%async_computation.1 | async-start | bytes 1048576 | tf_op jit(solution)/shard_map/all_to_all | solution.py:223
  226.5 14.0 %all-to-all-start.2 = ((f32[64,1,256]{2,1,0:T(1,128)}), f32[64,1,256]{2,1,0:T(1,128)S(1)}, u32[]{:S(2)}, u32[]{:S(2)}) async-start(f32[64,1,256]{2,1,0:T(1,128)} %broadcast_in_dim.22), calls=%async_computation.2 | async-start | bytes 131072 | tf_op jit(solution)/shard_map/all_to_all | solution.py:224
  (2 other events, 1.9 us)

commit v16 on v15

--- a/solution.py
+++ b/solution.py
@@ -187,9 +187,12 @@
         mix_deep = padded_2(grad_mix, (("segment", 0),), 1)
         grad_mid = depth_back(mix_deep, depth_w[layer], zs).astype(jnp.bfloat16)
         rows = grad.shape[1] - 2
-        grad = (
-            grad[:, 1:-1].astype(jnp.float32) + plane_back(grad_mid, plane_w[layer], rows, width)
-        ).astype(jnp.bfloat16)
+        if layer == 0:
+            last = (grad, grad_mid, rows)
+        else:
+            grad = (
+                grad[:, 1:-1].astype(jnp.float32) + plane_back(grad_mid, plane_w[layer], rows, width)
+            ).astype(jnp.bfloat16)
         depth_list[layer] = grad_mix[:, h : h + height]
         plane_list[layer] = grad_mid[:, h : h + height]
 
@@ -221,6 +224,11 @@
     piece = 128 * -(-size // (128 * spread_n))
     flat = jnp.pad(flat, ((0, 0), (0, piece * spread_n - size))).reshape(layers * spread_n, piece)
     part = lax.all_to_all(flat, ("segment", "gy"), 0, 0, tiled=True).sum(axis=0)
+    grad, grad_mid, rows = last
+    part, grad, grad_mid = lax.optimization_barrier((part, grad, grad_mid))
+    grad = (
+        grad[:, 1:-1].astype(jnp.float32) + plane_back(grad_mid, plane_w[0], rows, width)
+    ).astype(jnp.bfloat16)
     whole = lax.all_to_all(jnp.broadcast_to(part, (spread_n, piece)), "gy", 0, 0, tiled=True)
     flat = whole.reshape(-1)[:size][None] * scale
     cut = planes.shape[1]

time: 244 us -> 243 us (level)
  blocking collectives: 0 us -> 51.4 us
  starting transfers between devices: 129 us -> 100 us
  waiting for transfers between devices: 75.5 us -> 53.2 us
    all_to_all x0 -> x1, blocking collectives: none -> 51.4 us  [local(): part = lax.all_to_all(flat, ('segment', 'gy'), 0, 0, tiled=True).sum(axis=0)]
    all_to_all x1 -> x0, starting transfers between devices: 28.9 us -> none  [local(): part = lax.all_to_all(flat, ('segment', 'gy'), 0, 0, tiled=True).sum(axis=0)]
    all_to_all x1 -> x0, waiting for transfers between devices: 22.3 us -> none  [local(): part = lax.all_to_all(flat, ('segment', 'gy'), 0, 0, tiled=True).sum(axis=0)]
  transfers between devices with their start and end apart: 31 -> 30, of which waited for: 19 -> 18; matrix products, arithmetic and copies ran while one was open for 5% -> 5% of each run, Pallas kernels for 0% -> 0%
where the time goes in v16:
time: 243 us; the launch traced here: 242 us
  starting transfers between devices  100 us (41%)
  waiting for transfers between devices  53.2 us (22%)
  blocking collectives  51.4 us (21%)
  local copies, waits for them, and re-layouts  17.7 us (7%)
  matrix products  11.8 us (5%)
  other arithmetic  4.96 us (2%)
    all_to_all x1, blocking collectives, local(): part = lax.all_to_all(flat, ('segment', 'gy'), 0, 0, tiled=True).sum(axis=0)  51.4 us
    ppermute x10, starting transfers between devices, padded_2(): lax.ppermute(lax.slice_in_dim(block, block.shape[dim] - width, None, axis...  44.1 us
    ppermute x8, starting transfers between devices, passed_along(): return lax.ppermute(block, axis, route)  27.5 us
    all_to_all x1, waiting for transfers between devices, local(): got = lax.all_to_all(send, 'segment', 0, 0, tiled=True)  16.2 us
    ppermute x10, starting transfers between devices, padded_2(): lax.ppermute(lax.slice_in_dim(block, 0, width, axis=dim), axis, backward)  13.5 us
    all_to_all x1, starting transfers between devices, local(): got = lax.all_to_all(send, 'segment', 0, 0, tiled=True)  10.9 us
    ppermute x10, waiting for transfers between devices, padded_2(): lax.ppermute(lax.slice_in_dim(block, 0, width, axis=dim), axis, backward)  9.76 us
    ppermute x8, waiting for transfers between devices, passed_along(): return lax.ppermute(block, axis, route)  9.25 us
  transfers between devices with their start and end apart: 30, of which 18 were waited for; matrix products, arithmetic and copies ran while one was open for 5% of the time, Pallas kernels for 0%

profile of v16, /device:TPU:1, one launch (start us, length us, event | category | flops | bytes accessed | tf_op | source)
XLA Modules:
  0.0 241.6 jit_solution(15758369281287497813)
XLA Ops:
  1.7 1.8 pad_maximum_fusion
  3.5 10.9 %all-to-all-start = ((bf16[8,112,256]{2,1,0:T(8,128)(2,1)}), bf16[8,112,256]{2,1,0:T(8,128)(2,1)S(1)}, u32[]{:S(2)}, u32[]{:S(2)}) async-start(bf16[8,112,256]{2,1,0:T(8,128)(2,1)} %pad_maximum_fusion), calls=%async_computation | async-start | bytes 917504 | tf_op jit(solution)/shard_map/all_to_all | solution.py:133
  14.6 16.2 %all-to-all-done = bf16[8,112,256]{2,1,0:T(8,128)(2,1)S(1)} async-done(((bf16[8,112,256]{2,1,0:T(8,128)(2,1)}), bf16[8,112,256]{2,1,0:T(8,128)(2,1)S(1)}, u32[]{:S(2)}, u32[]{:S(2)}) %all-to-all-start) | async-done | bytes 458784 | tf_op jit(solution)/shard_map/all_to_all | solution.py:133
  32.7 3.7 %collective-permute-start = (bf16[8,1,1,32,256]{4,3,2,0,1:T(8,128)(2,1)}, bf16[8,1,1,32,256]{4,3,2,0,1:T(8,128)(2,1)S(1)}, u32[]{:S(2)}, u32[]{:S(2)}) collective-permute-start(bf16[8,1,1,32,256]{4,3,2,0,1:T(8,128)(2,1)} %get-tuple-element.54), channel_id=1, source_target_pairs={{0,1},{1,2},{2,3},{3,4},{4,5},{5,6},{6,7},{7,8},{8,9},{9,10},{10,1... | collective-permute-start | bytes 393224 | tf_op jit(solution)/shard_map/ppermute | solution.py:17
  36.4 1.9 collective-permute-start.1
  39.6 3.3 %collective-permute-done.1 = bf16[8,1,1,32,256]{4,3,2,0,1:T(8,128)(2,1)S(1)} collective-permute-done((bf16[8,1,1,32,256]{4,3,2,0,1:T(8,128)(2,1)}, bf16[8,1,1,32,256]{4,3,2,0,1:T(8,128)(2,1)S(1)}, u32[]{:S(2)}, u32[]{:S(2)}) %collective-permute-start.1) | collective-permute-done | bytes 131104 | tf_op jit(solution)/shard_map/ppermute | solution.py:20
  44.5 2.2 collective-permute-start.2
  46.7 1.3 collective-permute-start.3
  48.8 1.4 collective-permute-done.2
  50.2 4.1 %collective-permute-done.3 = bf16[8,1,2,32,256]{4,3,2,0,1:T(8,128)(2,1)S(1)} collective-permute-done((bf16[8,1,2,32,256]{4,3,2,0,1:T(8,128)(2,1)S(1)}, bf16[8,1,2,32,256]{4,3,2,0,1:T(8,128)(2,1)S(1)}, u32[]{:S(2)}, u32[]{:S(2)}) %collective-permute-start.3) | collective-permute-done | bytes 262176 | tf_op jit(solution)/shard_map/ppermute | solution.py:20
  54.7 5.0 %collective-permute-start.4 = (bf16[5,1,2,32,256]{4,3,2,1,0:T(8,128)(2,1)S(1)}, bf16[5,1,2,32,256]{4,3,2,1,0:T(8,128)(2,1)S(1)}, u32[]{:S(2)}, u32[]{:S(2)}) collective-permute-start(bf16[5,1,2,32,256]{4,3,2,1,0:T(8,128)(2,1)S(1)} %pad_maximum_fusion.4), channel_id=1, source_target_pairs={{0,2},{1,3},{2,4},{3,5},{4,6},{5,7},{6,8},{7,9},{8,10},{9,11},{10,... | collective-permute-start | bytes 491528 | tf_op jit(solution)/shard_map/ppermute | solution.py:28
  59.8 1.3 collective-permute-start.7
  61.1 4.7 %collective-permute-start.5 = (bf16[9,1,2,32,256]{4,3,2,1,0:T(8,128)(2,1)S(1)}, bf16[9,1,2,32,256]{4,3,2,1,0:T(8,128)(2,1)S(1)}, u32[]{:S(2)}, u32[]{:S(2)}) collective-permute-start(bf16[9,1,2,32,256]{4,3,2,1,0:T(8,128)(2,1)S(1)} %pad_maximum_fusion.1), channel_id=1, source_target_pairs={{0,1},{1,2},{2,3},{3,4},{4,5},{5,6},{6,7},{7,8},{8,9},{9,10},{10,1... | collective-permute-start | bytes 884744 | tf_op jit(solution)/shard_map/ppermute | solution.py:28
  65.9 1.9 collective-permute-start.6
  67.9 1.6 collective-permute-done.5
  69.6 4.3 %collective-permute-done.6 = bf16[9,1,2,32,256]{4,3,2,1,0:T(8,128)(2,1)S(1)} collective-permute-done((bf16[9,1,2,32,256]{4,3,2,1,0:T(8,128)(2,1)S(1)}, bf16[9,1,2,32,256]{4,3,2,1,0:T(8,128)(2,1)S(1)}, u32[]{:S(2)}, u32[]{:S(2)}) %collective-permute-start.6) | collective-permute-done | bytes 294944 | tf_op jit(solution)/shard_map/ppermute | solution.py:28
  74.0 1.3 collective-permute-start.8
  75.3 4.0 %collective-permute-start.9 = (bf16[1,10,32,256]{3,2,1,0:T(8,128)(2,1)S(1)}, bf16[1,10,32,256]{3,2,1,0:T(8,128)(2,1)S(1)}, u32[]{:S(2)}, u32[]{:S(2)}) collective-permute-start(bf16[1,10,32,256]{3,2,1,0:T(8,128)(2,1)S(1)} %fusion.75), channel_id=1, source_target_pairs={{0,64},{64,128},{128,192},{192,256},{256,320},{320,384},{384,448},... | collective-permute-start | bytes 491528 | tf_op jit(solution)/shard_map/ppermute | solution.py:17
  80.1 1.5 collective-permute-done.9
  83.0 1.3 collective-permute-start.10
  84.3 4.4 %collective-permute-start.11 = (bf16[1,8,32,256]{3,2,1,0:T(8,128)(2,1)S(1)}, bf16[1,8,32,256]{3,2,1,0:T(8,128)(2,1)S(1)}, u32[]{:S(2)}, u32[]{:S(2)}) collective-permute-start(bf16[1,8,32,256]{3,2,1,0:T(8,128)(2,1)S(1)} %get-tuple-element.11), channel_id=1, source_target_pairs={{0,64},{64,128},{128,192},{192,256},{256,320},{320,384},{384,448},... | collective-permute-start | bytes 393224 | tf_op jit(solution)/shard_map/ppermute | solution.py:17
  89.1 1.5 collective-permute-done.11
  91.9 1.3 collective-permute-start.12
  93.2 4.4 %collective-permute-start.13 = (bf16[1,6,32,256]{3,2,1,0:T(8,128)(2,1)S(1)}, bf16[1,6,32,256]{3,2,1,0:T(8,128)(2,1)S(1)}, u32[]{:S(2)}, u32[]{:S(2)}) collective-permute-start(bf16[1,6,32,256]{3,2,1,0:T(8,128)(2,1)S(1)} %get-tuple-element.66), channel_id=1, source_target_pairs={{0,64},{64,128},{128,192},{192,256},{256,320},{320,384},{384,448},... | collective-permute-start | bytes 294920 | tf_op jit(solution)/shard_map/ppermute | solution.py:17
  97.7 1.6 collective-permute-done.13
  100.3 1.3 collective-permute-start.14
  101.6 4.4 %collective-permute-start.15 = (bf16[1,4,32,256]{3,2,1,0:T(8,128)(2,1)S(1)}, bf16[1,4,32,256]{3,2,1,0:T(8,128)(2,1)S(1)}, u32[]{:S(2)}, u32[]{:S(2)}) collective-permute-start(bf16[1,4,32,256]{3,2,1,0:T(8,128)(2,1)S(1)} %get-tuple-element.68), channel_id=1, source_target_pairs={{0,64},{64,128},{128,192},{192,256},{256,320},{320,384},{384,448},... | collective-permute-start | bytes 196616 | tf_op jit(solution)/shard_map/ppermute | solution.py:17
  108.4 5.3 %collective-permute-start.16 = (bf16[1,2,32,256]{3,2,1,0:T(8,128)(2,1)S(1)}, bf16[1,2,32,256]{3,2,1,0:T(8,128)(2,1)S(1)}, u32[]{:S(2)}, u32[]{:S(2)}) collective-permute-start(bf16[1,2,32,256]{3,2,1,0:T(8,128)(2,1)S(1)} %fusion.39), channel_id=1, source_target_pairs={{0,2},{1,3},{2,4},{3,5},{4,6},{5,7},{6,8},{7,9},{8,10},{9,11},{10,... | collective-permute-start | bytes 98312 | tf_op jit(solution)/shard_map/ppermute | solution.py:28
  113.8 6.0 %collective-permute-start.17 = (bf16[1,2,32,256]{3,2,1,0:T(8,128)(2,1)S(1)}, bf16[1,2,32,256]{3,2,1,0:T(8,128)(2,1)S(1)}, u32[]{:S(2)}, u32[]{:S(2)}) collective-permute-start(bf16[1,2,32,256]{3,2,1,0:T(8,128)(2,1)S(1)} %fusion.39), channel_id=1, source_target_pairs={{0,1},{1,2},{2,3},{3,4},{4,5},{5,6},{6,7},{7,8},{8,9},{9,10},{10,1... | collective-permute-start | bytes 98312 | tf_op jit(solution)/shard_map/ppermute | solution.py:28
  119.8 1.9 collective-permute-start.18
  121.7 1.3 collective-permute-start.19
  123.1 1.9 collective-permute-done.18
  125.0 1.3 collective-permute-done.19
  126.4 1.3 collective-permute-start.20
  127.7 4.6 %collective-permute-start.21 = (bf16[1,10,32,256]{3,2,1,0:T(8,128)(2,1)S(1)}, bf16[1,10,32,256]{3,2,1,0:T(8,128)(2,1)S(1)}, u32[]{:S(2)}, u32[]{:S(2)}) collective-permute-start(bf16[1,10,32,256]{3,2,1,0:T(8,128)(2,1)S(1)} %fusion.76), channel_id=1, source_target_pairs={{0,64},{64,128},{128,192},{192,256},{256,320},{320,384},{384,448},... | collective-permute-start | bytes 491528 | tf_op jit(solution)/shard_map/ppermute | solution.py:17
  132.4 1.2 collective-permute-done.20
  136.0 1.3 collective-permute-start.22
  137.3 4.7 %collective-permute-start.23 = (bf16[1,8,32,256]{3,2,1,0:T(8,128)(2,1)S(1)}, bf16[1,8,32,256]{3,2,1,0:T(8,128)(2,1)S(1)}, u32[]{:S(2)}, u32[]{:S(2)}) collective-permute-start(bf16[1,8,32,256]{3,2,1,0:T(8,128)(2,1)S(1)} %get-tuple-element.9), channel_id=1, source_target_pairs={{0,64},{64,128},{128,192},{192,256},{256,320},{320,384},{384,448},... | collective-permute-start | bytes 393224 | tf_op jit(solution)/shard_map/ppermute | solution.py:17
  142.7 1.3 collective-permute-done.23
  145.9 1.3 collective-permute-start.24
  147.2 5.8 %collective-permute-start.25 = (bf16[1,6,32,256]{3,2,1,0:T(8,128)(2,1)}, bf16[1,6,32,256]{3,2,1,0:T(8,128)(2,1)}, u32[]{:S(2)}, u32[]{:S(2)}) collective-permute-start(bf16[1,6,32,256]{3,2,1,0:T(8,128)(2,1)} %get-tuple-element.70), channel_id=1, source_target_pairs={{0,64},{64,128},{128,192},{192,256},{256,320},{320,384},{384,448},... | collective-permute-start | bytes 294920 | tf_op jit(solution)/shard_map/ppermute | solution.py:17
  156.7 1.2 reshape.760
  157.9 1.2 fusion.34
  160.7 1.3 collective-permute-start.26
  162.0 5.8 %collective-permute-start.27 = (bf16[1,4,32,256]{3,2,1,0:T(8,128)(2,1)}, bf16[1,4,32,256]{3,2,1,0:T(8,128)(2,1)}, u32[]{:S(2)}, u32[]{:S(2)}) collective-permute-start(bf16[1,4,32,256]{3,2,1,0:T(8,128)(2,1)} %get-tuple-element.72), channel_id=1, source_target_pairs={{0,64},{64,128},{128,192},{192,256},{256,320},{320,384},{384,448},... | collective-permute-start | bytes 196616 | tf_op jit(solution)/shard_map/ppermute | solution.py:17
  172.7 51.4 %all_to_all.21 = f32[512,1,256]{2,1,0:T(1,128)S(1)} all-to-all(f32[512,1,256]{2,1,0:T(1,128)S(1)} %all_to_all.17), channel_id=1, replica_groups=mesh['segment'=8,'gy'=64] {'segment','gy'}, dimensions={0} | all-to-all | bytes 1048576 | tf_op jit(solution)/shard_map/all_to_all | solution.py:226
  225.9 4.2 %all-to-all-start.2 = ((f32[64,1,256]{2,1,0:T(1,128)}), f32[64,1,256]{2,1,0:T(1,128)S(1)}, u32[]{:S(2)}, u32[]{:S(2)}) async-start(f32[64,1,256]{2,1,0:T(1,128)} %broadcast_in_dim.22), calls=%async_computation.2 | async-start | bytes 131072 | tf_op jit(solution)/shard_map/all_to_all | solution.py:232
  230.9 9.0 %all-to-all-done.2 = f32[64,1,256]{2,1,0:T(1,128)S(1)} async-done(((f32[64,1,256]{2,1,0:T(1,128)}), f32[64,1,256]{2,1,0:T(1,128)S(1)}, u32[]{:S(2)}, u32[]{:S(2)}) %all-to-all-start.2) | async-done | bytes 65568 | tf_op jit(solution)/shard_map/all_to_all | solution.py:232
  (256 shorter events, 33.2 us)
Async XLA Ops:
  0.6 13.7 %copy-start.14 = (s32[1,12]{1,0:T(1,128)S(1)}, s32[1,12]{1,0:T(1,128)}, u32[]{:S(2)}) copy-start(s32[1,12]{1,0:T(1,128)} %param.9) | copy-start | bytes 148
  3.5 27.3 %all-to-all-start = ((bf16[8,112,256]{2,1,0:T(8,128)(2,1)}), bf16[8,112,256]{2,1,0:T(8,128)(2,1)S(1)}, u32[]{:S(2)}, u32[]{:S(2)}) async-start(bf16[8,112,256]{2,1,0:T(8,128)(2,1)} %pad_maximum_fusion), calls=%async_computation | async-start | bytes 917504 | tf_op jit(solution)/shard_map/all_to_all | solution.py:133
  32.7 6.9 %collective-permute-start = (bf16[8,1,1,32,256]{4,3,2,0,1:T(8,128)(2,1)}, bf16[8,1,1,32,256]{4,3,2,0,1:T(8,128)(2,1)S(1)}, u32[]{:S(2)}, u32[]{:S(2)}) collective-permute-start(bf16[8,1,1,32,256]{4,3,2,0,1:T(8,128)(2,1)} %get-tuple-element.54), channel_id=1, source_target_pairs={{0,1},{1,2},{2,3},{3,4},{4,5},{5,6},{6,7},{7,8},{8,9},{9,10},{10,1... | collective-permute-start | bytes 393224 | tf_op jit(solution)/shard_map/ppermute | solution.py:17
  36.4 6.5 %collective-permute-start.1 = (bf16[8,1,1,32,256]{4,3,2,0,1:T(8,128)(2,1)}, bf16[8,1,1,32,256]{4,3,2,0,1:T(8,128)(2,1)S(1)}, u32[]{:S(2)}, u32[]{:S(2)}) collective-permute-start(bf16[8,1,1,32,256]{4,3,2,0,1:T(8,128)(2,1)} %get-tuple-element.55), channel_id=1, source_target_pairs={{1,0},{2,1},{3,2},{4,3},{5,4},{6,5},{7,6},{8,7},{9,8},{10,9},{11,1... | collective-permute-start | bytes 393224 | tf_op jit(solution)/shard_map/ppermute | solution.py:20
  44.5 5.7 %collective-permute-start.2 = (bf16[8,1,2,32,256]{4,3,2,0,1:T(8,128)(2,1)S(1)}, bf16[8,1,2,32,256]{4,3,2,0,1:T(8,128)(2,1)S(1)}, u32[]{:S(2)}, u32[]{:S(2)}) collective-permute-start(bf16[8,1,2,32,256]{4,3,2,0,1:T(8,128)(2,1)S(1)} %fusion.12), channel_id=1, source_target_pairs={{0,64},{64,128},{128,192},{192,256},{256,320},{320,384},{384,448},... | collective-permute-start | bytes 786440 | tf_op jit(solution)/shard_map/ppermute | solution.py:17
  46.7 7.6 %collective-permute-start.3 = (bf16[8,1,2,32,256]{4,3,2,0,1:T(8,128)(2,1)S(1)}, bf16[8,1,2,32,256]{4,3,2,0,1:T(8,128)(2,1)S(1)}, u32[]{:S(2)}, u32[]{:S(2)}) collective-permute-start(bf16[8,1,2,32,256]{4,3,2,0,1:T(8,128)(2,1)S(1)} %fusion.12), channel_id=1, source_target_pairs={{64,0},{128,64},{192,128},{256,192},{320,256},{384,320},{448,384},... | collective-permute-start | bytes 786440 | tf_op jit(solution)/shard_map/ppermute | solution.py:20
  48.8 5.9 %copy-start.2 = (bf16[1,2,32,256]{3,2,1,0:T(8,128)(2,1)S(1)}, bf16[1,2,32,256]{3,2,1,0:T(8,128)(2,1)}, u32[]{:S(2)}) copy-start(bf16[1,2,32,256]{3,2,1,0:T(8,128)(2,1)} %param.6) | copy-start | bytes 98308
  50.2 56.4 %copy-start.8 = (bf16[8,1,2,32,256]{4,3,2,0,1:T(8,128)(2,1)}, bf16[8,1,2,32,256]{4,3,2,0,1:T(8,128)(2,1)S(1)}, u32[]{:S(2)}) copy-start(bf16[8,1,2,32,256]{4,3,2,0,1:T(8,128)(2,1)S(1)} %collective-permute-done.2) | copy-start | bytes 786436
  54.3 52.3 %copy-start.9 = (bf16[8,1,2,32,256]{4,3,2,0,1:T(8,128)(2,1)}, bf16[8,1,2,32,256]{4,3,2,0,1:T(8,128)(2,1)S(1)}, u32[]{:S(2)}) copy-start(bf16[8,1,2,32,256]{4,3,2,0,1:T(8,128)(2,1)S(1)} %collective-permute-done.3) | copy-start | bytes 786436
  54.7 13.1 %collective-permute-start.4 = (bf16[5,1,2,32,256]{4,3,2,1,0:T(8,128)(2,1)S(1)}, bf16[5,1,2,32,256]{4,3,2,1,0:T(8,128)(2,1)S(1)}, u32[]{:S(2)}, u32[]{:S(2)}) collective-permute-start(bf16[5,1,2,32,256]{4,3,2,1,0:T(8,128)(2,1)S(1)} %pad_maximum_fusion.4), channel_id=1, source_target_pairs={{0,2},{1,3},{2,4},{3,5},{4,6},{5,7},{6,8},{7,9},{8,10},{9,11},{10,... | collective-permute-start | bytes 491528 | tf_op jit(solution)/shard_map/ppermute | solution.py:28
  59.8 8.1 %collective-permute-start.7 = (bf16[5,1,2,32,256]{4,3,2,1,0:T(8,128)(2,1)S(1)}, bf16[5,1,2,32,256]{4,3,2,1,0:T(8,128)(2,1)S(1)}, u32[]{:S(2)}, u32[]{:S(2)}) collective-permute-start(bf16[5,1,2,32,256]{4,3,2,1,0:T(8,128)(2,1)S(1)} %pad_maximum_fusion.4), channel_id=1, source_target_pairs={{2,0},{3,1},{4,2},{5,3},{6,4},{7,5},{8,6},{9,7},{10,8},{11,9},{12,... | collective-permute-start | bytes 491528 | tf_op jit(solution)/shard_map/ppermute | solution.py:28
  61.1 8.4 %collective-permute-start.5 = (bf16[9,1,2,32,256]{4,3,2,1,0:T(8,128)(2,1)S(1)}, bf16[9,1,2,32,256]{4,3,2,1,0:T(8,128)(2,1)S(1)}, u32[]{:S(2)}, u32[]{:S(2)}) collective-permute-start(bf16[9,1,2,32,256]{4,3,2,1,0:T(8,128)(2,1)S(1)} %pad_maximum_fusion.1), channel_id=1, source_target_pairs={{0,1},{1,2},{2,3},{3,4},{4,5},{5,6},{6,7},{7,8},{8,9},{9,10},{10,1... | collective-permute-start | bytes 884744 | tf_op jit(solution)/shard_map/ppermute | solution.py:28
  65.9 8.0 %collective-permute-start.6 = (bf16[9,1,2,32,256]{4,3,2,1,0:T(8,128)(2,1)S(1)}, bf16[9,1,2,32,256]{4,3,2,1,0:T(8,128)(2,1)S(1)}, u32[]{:S(2)}, u32[]{:S(2)}) collective-permute-start(bf16[9,1,2,32,256]{4,3,2,1,0:T(8,128)(2,1)S(1)} %pad_maximum_fusion.1), channel_id=1, source_target_pairs={{1,0},{2,1},{3,2},{4,3},{5,4},{6,5},{7,6},{8,7},{9,8},{10,9},{11,1... | collective-permute-start | bytes 884744 | tf_op jit(solution)/shard_map/ppermute | solution.py:28
  74.0 6.1 %collective-permute-start.8 = (bf16[1,10,32,256]{3,2,1,0:T(8,128)(2,1)S(1)}, bf16[1,10,32,256]{3,2,1,0:T(8,128)(2,1)S(1)}, u32[]{:S(2)}, u32[]{:S(2)}) collective-permute-start(bf16[1,10,32,256]{3,2,1,0:T(8,128)(2,1)S(1)} %fusion.75), channel_id=1, source_target_pairs={{64,0},{128,64},{192,128},{256,192},{320,256},{384,320},{448,384},... | collective-permute-start | bytes 491528 | tf_op jit(solution)/shard_map/ppermute | solution.py:20
  75.3 6.2 %collective-permute-start.9 = (bf16[1,10,32,256]{3,2,1,0:T(8,128)(2,1)S(1)}, bf16[1,10,32,256]{3,2,1,0:T(8,128)(2,1)S(1)}, u32[]{:S(2)}, u32[]{:S(2)}) collective-permute-start(bf16[1,10,32,256]{3,2,1,0:T(8,128)(2,1)S(1)} %fusion.75), channel_id=1, source_target_pairs={{0,64},{64,128},{128,192},{192,256},{256,320},{320,384},{384,448},... | collective-permute-start | bytes 491528 | tf_op jit(solution)/shard_map/ppermute | solution.py:17
  81.6 1.0 copy-start.6
  83.0 6.2 %collective-permute-start.10 = (bf16[1,8,32,256]{3,2,1,0:T(8,128)(2,1)S(1)}, bf16[1,8,32,256]{3,2,1,0:T(8,128)(2,1)S(1)}, u32[]{:S(2)}, u32[]{:S(2)}) collective-permute-start(bf16[1,8,32,256]{3,2,1,0:T(8,128)(2,1)S(1)} %get-tuple-element.11), channel_id=1, source_target_pairs={{64,0},{128,64},{192,128},{256,192},{320,256},{384,320},{448,384},... | collective-permute-start | bytes 393224 | tf_op jit(solution)/shard_map/ppermute | solution.py:20
  84.3 6.4 %collective-permute-start.11 = (bf16[1,8,32,256]{3,2,1,0:T(8,128)(2,1)S(1)}, bf16[1,8,32,256]{3,2,1,0:T(8,128)(2,1)S(1)}, u32[]{:S(2)}, u32[]{:S(2)}) collective-permute-start(bf16[1,8,32,256]{3,2,1,0:T(8,128)(2,1)S(1)} %get-tuple-element.11), channel_id=1, source_target_pairs={{0,64},{64,128},{128,192},{192,256},{256,320},{320,384},{384,448},... | collective-permute-start | bytes 393224 | tf_op jit(solution)/shard_map/ppermute | solution.py:17
  88.8 3.1 %copy-start = (bf16[1,1,2,288,256]{4,3,2,0,1:T(8,128)(2,1)}, bf16[1,1,2,288,256]{4,3,2,0,1:T(8,128)(2,1)S(1)}, u32[]{:S(2)}) copy-start(bf16[1,1,2,288,256]{4,3,2,0,1:T(8,128)(2,1)S(1)} %constant_dynamic-update-slice_fusion.74) | copy-start | bytes 884740
  91.5 8.5 %copy-start.4 = (bf16[1,9,32,32]{3,2,1,0:T(8,128)(2,1)S(1)}, bf16[1,9,32,32]{3,2,1,0:T(8,128)(2,1)}, u32[]{:S(2)}) copy-start(bf16[1,9,32,32]{3,2,1,0:T(8,128)(2,1)} %get-tuple-element.26) | copy-start | bytes 55300
  91.9 5.8 %collective-permute-start.12 = (bf16[1,6,32,256]{3,2,1,0:T(8,128)(2,1)S(1)}, bf16[1,6,32,256]{3,2,1,0:T(8,128)(2,1)S(1)}, u32[]{:S(2)}, u32[]{:S(2)}) collective-permute-start(bf16[1,6,32,256]{3,2,1,0:T(8,128)(2,1)S(1)} %get-tuple-element.66), channel_id=1, source_target_pairs={{64,0},{128,64},{192,128},{256,192},{320,256},{384,320},{448,384},... | collective-permute-start | bytes 294920 | tf_op jit(solution)/shard_map/ppermute | solution.py:20
  93.2 6.0 %collective-permute-start.13 = (bf16[1,6,32,256]{3,2,1,0:T(8,128)(2,1)S(1)}, bf16[1,6,32,256]{3,2,1,0:T(8,128)(2,1)S(1)}, u32[]{:S(2)}, u32[]{:S(2)}) collective-permute-start(bf16[1,6,32,256]{3,2,1,0:T(8,128)(2,1)S(1)} %get-tuple-element.66), channel_id=1, source_target_pairs={{0,64},{64,128},{128,192},{192,256},{256,320},{320,384},{384,448},... | collective-permute-start | bytes 294920 | tf_op jit(solution)/shard_map/ppermute | solution.py:17
  100.3 6.3 %collective-permute-start.14 = (bf16[1,4,32,256]{3,2,1,0:T(8,128)(2,1)S(1)}, bf16[1,4,32,256]{3,2,1,0:T(8,128)(2,1)S(1)}, u32[]{:S(2)}, u32[]{:S(2)}) collective-permute-start(bf16[1,4,32,256]{3,2,1,0:T(8,128)(2,1)S(1)} %get-tuple-element.68), channel_id=1, source_target_pairs={{64,0},{128,64},{192,128},{256,192},{320,256},{384,320},{448,384},... | collective-permute-start | bytes 196616 | tf_op jit(solution)/shard_map/ppermute | solution.py:20
  101.6 5.9 %collective-permute-start.15 = (bf16[1,4,32,256]{3,2,1,0:T(8,128)(2,1)S(1)}, bf16[1,4,32,256]{3,2,1,0:T(8,128)(2,1)S(1)}, u32[]{:S(2)}, u32[]{:S(2)}) collective-permute-start(bf16[1,4,32,256]{3,2,1,0:T(8,128)(2,1)S(1)} %get-tuple-element.68), channel_id=1, source_target_pairs={{0,64},{64,128},{128,192},{192,256},{256,320},{320,384},{384,448},... | collective-permute-start | bytes 196616 | tf_op jit(solution)/shard_map/ppermute | solution.py:17
  106.6 25.7 %slice-start = ((bf16[8,1,2,32,256]{4,3,2,0,1:T(8,128)(2,1)}), bf16[1,1,2,32,256]{4,3,2,0,1:T(8,128)(2,1)S(1)}, s32[]{:S(2)}) async-start(bf16[8,1,2,32,256]{4,3,2,0,1:T(8,128)(2,1)} %copy-done.8), calls=%async_computation.3 | async-start | bytes 65536 | tf_op jit(solution)/shard_map/slice | solution.py:212
  106.6 25.8 %slice-start.2 = ((bf16[8,1,2,32,256]{4,3,2,0,1:T(8,128)(2,1)}), bf16[1,1,2,32,256]{4,3,2,0,1:T(8,128)(2,1)S(1)}, s32[]{:S(2)}) async-start(bf16[8,1,2,32,256]{4,3,2,0,1:T(8,128)(2,1)} %copy-done.9), calls=%async_computation.5 | async-start | bytes 65536 | tf_op jit(solution)/shard_map/slice | solution.py:212
  108.4 14.6 %collective-permute-start.16 = (bf16[1,2,32,256]{3,2,1,0:T(8,128)(2,1)S(1)}, bf16[1,2,32,256]{3,2,1,0:T(8,128)(2,1)S(1)}, u32[]{:S(2)}, u32[]{:S(2)}) collective-permute-start(bf16[1,2,32,256]{3,2,1,0:T(8,128)(2,1)S(1)} %fusion.39), channel_id=1, source_target_pairs={{0,2},{1,3},{2,4},{3,5},{4,6},{5,7},{6,8},{7,9},{8,10},{9,11},{10,... | collective-permute-start | bytes 98312 | tf_op jit(solution)/shard_map/ppermute | solution.py:28
  113.8 9.3 %collective-permute-start.17 = (bf16[1,2,32,256]{3,2,1,0:T(8,128)(2,1)S(1)}, bf16[1,2,32,256]{3,2,1,0:T(8,128)(2,1)S(1)}, u32[]{:S(2)}, u32[]{:S(2)}) collective-permute-start(bf16[1,2,32,256]{3,2,1,0:T(8,128)(2,1)S(1)} %fusion.39), channel_id=1, source_target_pairs={{0,1},{1,2},{2,3},{3,4},{4,5},{5,6},{6,7},{7,8},{8,9},{9,10},{10,1... | collective-permute-start | bytes 98312 | tf_op jit(solution)/shard_map/ppermute | solution.py:28
  119.8 5.2 %collective-permute-start.18 = (bf16[1,2,32,256]{3,2,1,0:T(8,128)(2,1)S(1)}, bf16[1,2,32,256]{3,2,1,0:T(8,128)(2,1)S(1)}, u32[]{:S(2)}, u32[]{:S(2)}) collective-permute-start(bf16[1,2,32,256]{3,2,1,0:T(8,128)(2,1)S(1)} %fusion.39), channel_id=1, source_target_pairs={{1,0},{2,1},{3,2},{4,3},{5,4},{6,5},{7,6},{8,7},{9,8},{10,9},{11,1... | collective-permute-start | bytes 98312 | tf_op jit(solution)/shard_map/ppermute | solution.py:28
  121.7 4.7 %collective-permute-start.19 = (bf16[1,2,32,256]{3,2,1,0:T(8,128)(2,1)S(1)}, bf16[1,2,32,256]{3,2,1,0:T(8,128)(2,1)S(1)}, u32[]{:S(2)}, u32[]{:S(2)}) collective-permute-start(bf16[1,2,32,256]{3,2,1,0:T(8,128)(2,1)S(1)} %fusion.39), channel_id=1, source_target_pairs={{2,0},{3,1},{4,2},{5,3},{6,4},{7,5},{8,6},{9,7},{10,8},{11,9},{12,... | collective-permute-start | bytes 98312 | tf_op jit(solution)/shard_map/ppermute | solution.py:28
  126.4 7.2 %collective-permute-start.20 = (bf16[1,10,32,256]{3,2,1,0:T(8,128)(2,1)S(1)}, bf16[1,10,32,256]{3,2,1,0:T(8,128)(2,1)S(1)}, u32[]{:S(2)}, u32[]{:S(2)}) collective-permute-start(bf16[1,10,32,256]{3,2,1,0:T(8,128)(2,1)S(1)} %fusion.76), channel_id=1, source_target_pairs={{64,0},{128,64},{192,128},{256,192},{320,256},{384,320},{448,384},... | collective-permute-start | bytes 491528 | tf_op jit(solution)/shard_map/ppermute | solution.py:20
  127.7 6.9 %collective-permute-start.21 = (bf16[1,10,32,256]{3,2,1,0:T(8,128)(2,1)S(1)}, bf16[1,10,32,256]{3,2,1,0:T(8,128)(2,1)S(1)}, u32[]{:S(2)}, u32[]{:S(2)}) collective-permute-start(bf16[1,10,32,256]{3,2,1,0:T(8,128)(2,1)S(1)} %fusion.76), channel_id=1, source_target_pairs={{0,64},{64,128},{128,192},{192,256},{256,320},{320,384},{384,448},... | collective-permute-start | bytes 491528 | tf_op jit(solution)/shard_map/ppermute | solution.py:17
  134.6 1.0 copy-start.5
  136.0 6.7 %collective-permute-start.22 = (bf16[1,8,32,256]{3,2,1,0:T(8,128)(2,1)S(1)}, bf16[1,8,32,256]{3,2,1,0:T(8,128)(2,1)S(1)}, u32[]{:S(2)}, u32[]{:S(2)}) collective-permute-start(bf16[1,8,32,256]{3,2,1,0:T(8,128)(2,1)S(1)} %get-tuple-element.9), channel_id=1, source_target_pairs={{64,0},{128,64},{192,128},{256,192},{320,256},{384,320},{448,384},... | collective-permute-start | bytes 393224 | tf_op jit(solution)/shard_map/ppermute | solution.py:20
  137.3 6.7 %collective-permute-start.23 = (bf16[1,8,32,256]{3,2,1,0:T(8,128)(2,1)S(1)}, bf16[1,8,32,256]{3,2,1,0:T(8,128)(2,1)S(1)}, u32[]{:S(2)}, u32[]{:S(2)}) collective-permute-start(bf16[1,8,32,256]{3,2,1,0:T(8,128)(2,1)S(1)} %get-tuple-element.9), channel_id=1, source_target_pairs={{0,64},{64,128},{128,192},{192,256},{256,320},{320,384},{384,448},... | collective-permute-start | bytes 393224 | tf_op jit(solution)/shard_map/ppermute | solution.py:17
  144.4 9.4 %slice-start.1 = ((bf16[8,1,2,32,256]{4,3,2,0,1:T(8,128)(2,1)}), bf16[7,1,2,32,256]{4,3,2,0,1:T(8,128)(2,1)S(1)}, s32[]{:S(2)}) async-start(bf16[8,1,2,32,256]{4,3,2,0,1:T(8,128)(2,1)} %copy-done.8), calls=%async_computation.4 | async-start | bytes 458752 | tf_op jit(solution)/shard_map/slice | solution.py:212
  144.4 9.4 %slice-start.3 = ((bf16[8,1,2,32,256]{4,3,2,0,1:T(8,128)(2,1)}), bf16[7,1,2,32,256]{4,3,2,0,1:T(8,128)(2,1)S(1)}, s32[]{:S(2)}) async-start(bf16[8,1,2,32,256]{4,3,2,0,1:T(8,128)(2,1)} %copy-done.9), calls=%async_computation.6 | async-start | bytes 458752 | tf_op jit(solution)/shard_map/slice | solution.py:212
  145.9 12.0 %collective-permute-start.24 = (bf16[1,6,32,256]{3,2,1,0:T(8,128)(2,1)}, bf16[1,6,32,256]{3,2,1,0:T(8,128)(2,1)}, u32[]{:S(2)}, u32[]{:S(2)}) collective-permute-start(bf16[1,6,32,256]{3,2,1,0:T(8,128)(2,1)} %get-tuple-element.70), channel_id=1, source_target_pairs={{64,0},{128,64},{192,128},{256,192},{320,256},{384,320},{448,384},... | collective-permute-start | bytes 294920 | tf_op jit(solution)/shard_map/ppermute | solution.py:20
  147.2 10.8 %collective-permute-start.25 = (bf16[1,6,32,256]{3,2,1,0:T(8,128)(2,1)}, bf16[1,6,32,256]{3,2,1,0:T(8,128)(2,1)}, u32[]{:S(2)}, u32[]{:S(2)}) collective-permute-start(bf16[1,6,32,256]{3,2,1,0:T(8,128)(2,1)} %get-tuple-element.70), channel_id=1, source_target_pairs={{0,64},{64,128},{128,192},{192,256},{256,320},{320,384},{384,448},... | collective-permute-start | bytes 294920 | tf_op jit(solution)/shard_map/ppermute | solution.py:17
  156.0 3.8 %copy-start.3 = (bf16[1,9,32,32]{3,2,1,0:T(8,128)(2,1)S(1)}, bf16[1,9,32,32]{3,2,1,0:T(8,128)(2,1)}, u32[]{:S(2)}) copy-start(bf16[1,9,32,32]{3,2,1,0:T(8,128)(2,1)} %get-tuple-element.21) | copy-start | bytes 55300
  156.7 3.0 %copy-start.7 = (bf16[1,6,32,256]{3,2,1,0:T(8,128)(2,1)S(1)}, bf16[1,6,32,256]{3,2,1,0:T(8,128)(2,1)}, u32[]{:S(2)}) copy-start(bf16[1,6,32,256]{3,2,1,0:T(8,128)(2,1)} %get-tuple-element.71) | copy-start | bytes 294916
  156.7 3.1 %copy-start.10 = (f32[1,2,32,256]{3,2,1,0:T(8,128)S(1)}, f32[1,2,32,256]{3,2,1,0:T(8,128)}, u32[]{:S(2)}) copy-start(f32[1,2,32,256]{3,2,1,0:T(8,128)} %slice_bitcast_fusion.2) | copy-start | bytes 196612
  156.7 3.1 %copy-start.12 = (f32[1,1,32,256]{3,2,1,0:T(8,128)S(1)}, f32[1,1,32,256]{3,2,1,0:T(8,128)}, u32[]{:S(2)}) copy-start(f32[1,1,32,256]{3,2,1,0:T(8,128)} %get-tuple-element.81) | copy-start | bytes 98308
  160.7 9.7 %collective-permute-start.26 = (bf16[1,4,32,256]{3,2,1,0:T(8,128)(2,1)}, bf16[1,4,32,256]{3,2,1,0:T(8,128)(2,1)S(1)}, u32[]{:S(2)}, u32[]{:S(2)}) collective-permute-start(bf16[1,4,32,256]{3,2,1,0:T(8,128)(2,1)} %get-tuple-element.72), channel_id=1, source_target_pairs={{64,0},{128,64},{192,128},{256,192},{320,256},{384,320},{448,384},... | collective-permute-start | bytes 196616 | tf_op jit(solution)/shard_map/ppermute | solution.py:20
  162.0 8.4 %collective-permute-start.27 = (bf16[1,4,32,256]{3,2,1,0:T(8,128)(2,1)}, bf16[1,4,32,256]{3,2,1,0:T(8,128)(2,1)}, u32[]{:S(2)}, u32[]{:S(2)}) collective-permute-start(bf16[1,4,32,256]{3,2,1,0:T(8,128)(2,1)} %get-tuple-element.72), channel_id=1, source_target_pairs={{0,64},{64,128},{128,192},{192,256},{256,320},{320,384},{384,448},... | collective-permute-start | bytes 196616 | tf_op jit(solution)/shard_map/ppermute | solution.py:17
  169.5 2.0 copy-start.1
  172.1 58.0 %copy-start.11 = (bf16[1,4,32,256]{3,2,1,0:T(8,128)(2,1)S(1)}, bf16[1,4,32,256]{3,2,1,0:T(8,128)(2,1)}, u32[]{:S(2)}) copy-start(bf16[1,4,32,256]{3,2,1,0:T(8,128)(2,1)} %get-tuple-element.6) | copy-start | bytes 196612
  225.9 14.0 %all-to-all-start.2 = ((f32[64,1,256]{2,1,0:T(1,128)}), f32[64,1,256]{2,1,0:T(1,128)S(1)}, u32[]{:S(2)}, u32[]{:S(2)}) async-start(f32[64,1,256]{2,1,0:T(1,128)} %broadcast_in_dim.22), calls=%async_computation.2 | async-start | bytes 131072 | tf_op jit(solution)/shard_map/all_to_all | solution.py:232
  (1 other events, 0.9 us)

commit v17 on v15

--- a/solution.py
+++ b/solution.py
@@ -211,8 +211,8 @@
         depths = depths.reshape(len(chosen), chans, 3, chans).transpose(0, 2, 1, 3)
         return planes.reshape(len(chosen), -1), depths.reshape(len(chosen), -1)
 
-    first_p, first_d = kernel_grads([0])
-    rest_p, rest_d = kernel_grads(list(range(1, layers)))
+    first_p, first_d = kernel_grads([0, 1])
+    rest_p, rest_d = kernel_grads(list(range(2, layers)))
     planes = jnp.concatenate([first_p, rest_p])
     depths = jnp.concatenate([first_d, rest_d])
     flat = jnp.concatenate([planes, depths], axis=1)

time: 244 us -> 241 us (0.988)
  matrix products: 11.8 us -> 8.65 us
  starting transfers between devices: 129 us -> 132 us
  waiting for transfers between devices: 75.5 us -> 72.9 us
    all_to_all x1, starting transfers between devices: 28.9 us -> 31.5 us  [local(): part = lax.all_to_all(flat, ('segment', 'gy'), 0, 0, tiled=True).sum(axis=0)]
    unnamed x132 -> x137, local copies, waits for them, and re-layouts: 5.68 us -> 5.62 us
  transfers between devices with their start and end apart: 31 -> 31, of which waited for: 19 -> 20; matrix products, arithmetic and copies ran while one was open for 5% -> 4% of each run, Pallas kernels for 0% -> 0%
where the time goes in v17:
time: 241 us; the launch traced here: 239 us
  starting transfers between devices  132 us (55%)
  waiting for transfers between devices  72.9 us (30%)
  local copies, waits for them, and re-layouts  17.4 us (7%)
  matrix products  8.65 us (4%)
  other arithmetic  6.19 us (3%)
    ppermute x10, starting transfers between devices, padded_2(): lax.ppermute(lax.slice_in_dim(block, block.shape[dim] - width, None, axis...  44 us
    all_to_all x1, starting transfers between devices, local(): part = lax.all_to_all(flat, ('segment', 'gy'), 0, 0, tiled=True).sum(axis=0)  31.5 us
    ppermute x8, starting transfers between devices, passed_along(): return lax.ppermute(block, axis, route)  27.6 us
    all_to_all x1, waiting for transfers between devices, local(): part = lax.all_to_all(flat, ('segment', 'gy'), 0, 0, tiled=True).sum(axis=0)  22.4 us
    all_to_all x1, waiting for transfers between devices, local(): got = lax.all_to_all(send, 'segment', 0, 0, tiled=True)  16.2 us
    ppermute x10, starting transfers between devices, padded_2(): lax.ppermute(lax.slice_in_dim(block, 0, width, axis=dim), axis, backward)  13.7 us
    all_to_all x1, starting transfers between devices, local(): got = lax.all_to_all(send, 'segment', 0, 0, tiled=True)  10.9 us
    ppermute x10, waiting for transfers between devices, padded_2(): lax.ppermute(lax.slice_in_dim(block, 0, width, axis=dim), axis, backward)  9.14 us
  transfers between devices with their start and end apart: 31, of which 20 were waited for; matrix products, arithmetic and copies ran while one was open for 4% of the time, Pallas kernels for 0%

profile of v17, /device:TPU:1, one launch (start us, length us, event | category | flops | bytes accessed | tf_op | source)
XLA Modules:
  0.0 239.3 jit_solution(13509697922111679915)
XLA Ops:
  1.7 1.8 pad_maximum_fusion
  3.5 10.9 %all-to-all-start = ((bf16[8,112,256]{2,1,0:T(8,128)(2,1)}), bf16[8,112,256]{2,1,0:T(8,128)(2,1)S(1)}, u32[]{:S(2)}, u32[]{:S(2)}) async-start(bf16[8,112,256]{2,1,0:T(8,128)(2,1)} %pad_maximum_fusion), calls=%async_computation | async-start | bytes 917504 | tf_op jit(solution)/shard_map/all_to_all | solution.py:133
  14.6 16.2 %all-to-all-done = bf16[8,112,256]{2,1,0:T(8,128)(2,1)S(1)} async-done(((bf16[8,112,256]{2,1,0:T(8,128)(2,1)}), bf16[8,112,256]{2,1,0:T(8,128)(2,1)S(1)}, u32[]{:S(2)}, u32[]{:S(2)}) %all-to-all-start) | async-done | bytes 458784 | tf_op jit(solution)/shard_map/all_to_all | solution.py:133
  32.7 3.7 %collective-permute-start = (bf16[8,1,1,32,256]{4,3,2,0,1:T(8,128)(2,1)}, bf16[8,1,1,32,256]{4,3,2,0,1:T(8,128)(2,1)S(1)}, u32[]{:S(2)}, u32[]{:S(2)}) collective-permute-start(bf16[8,1,1,32,256]{4,3,2,0,1:T(8,128)(2,1)} %get-tuple-element.48), channel_id=1, source_target_pairs={{0,1},{1,2},{2,3},{3,4},{4,5},{5,6},{6,7},{7,8},{8,9},{9,10},{10,1... | collective-permute-start | bytes 393224 | tf_op jit(solution)/shard_map/ppermute | solution.py:17
  36.4 1.9 collective-permute-start.1
  39.6 3.3 %collective-permute-done.1 = bf16[8,1,1,32,256]{4,3,2,0,1:T(8,128)(2,1)S(1)} collective-permute-done((bf16[8,1,1,32,256]{4,3,2,0,1:T(8,128)(2,1)}, bf16[8,1,1,32,256]{4,3,2,0,1:T(8,128)(2,1)S(1)}, u32[]{:S(2)}, u32[]{:S(2)}) %collective-permute-start.1) | collective-permute-done | bytes 131104 | tf_op jit(solution)/shard_map/ppermute | solution.py:20
  44.5 2.2 collective-permute-start.2
  46.7 1.3 collective-permute-start.3
  50.2 4.1 %collective-permute-done.3 = bf16[8,1,2,32,256]{4,3,2,0,1:T(8,128)(2,1)S(1)} collective-permute-done((bf16[8,1,2,32,256]{4,3,2,0,1:T(8,128)(2,1)S(1)}, bf16[8,1,2,32,256]{4,3,2,0,1:T(8,128)(2,1)S(1)}, u32[]{:S(2)}, u32[]{:S(2)}) %collective-permute-start.3) | collective-permute-done | bytes 262176 | tf_op jit(solution)/shard_map/ppermute | solution.py:20
  54.7 5.0 %collective-permute-start.4 = (bf16[5,1,2,32,256]{4,3,2,1,0:T(8,128)(2,1)S(1)}, bf16[5,1,2,32,256]{4,3,2,1,0:T(8,128)(2,1)S(1)}, u32[]{:S(2)}, u32[]{:S(2)}) collective-permute-start(bf16[5,1,2,32,256]{4,3,2,1,0:T(8,128)(2,1)S(1)} %pad_maximum_fusion.4), channel_id=1, source_target_pairs={{0,2},{1,3},{2,4},{3,5},{4,6},{5,7},{6,8},{7,9},{8,10},{9,11},{10,... | collective-permute-start | bytes 491528 | tf_op jit(solution)/shard_map/ppermute | solution.py:28
  59.8 1.3 collective-permute-start.7
  61.1 4.7 %collective-permute-start.5 = (bf16[9,1,2,32,256]{4,3,2,1,0:T(8,128)(2,1)S(1)}, bf16[9,1,2,32,256]{4,3,2,1,0:T(8,128)(2,1)S(1)}, u32[]{:S(2)}, u32[]{:S(2)}) collective-permute-start(bf16[9,1,2,32,256]{4,3,2,1,0:T(8,128)(2,1)S(1)} %pad_maximum_fusion.1), channel_id=1, source_target_pairs={{0,1},{1,2},{2,3},{3,4},{4,5},{5,6},{6,7},{7,8},{8,9},{9,10},{10,1... | collective-permute-start | bytes 884744 | tf_op jit(solution)/shard_map/ppermute | solution.py:28
  65.9 1.9 collective-permute-start.6
  68.5 1.0 collective-permute-done.5
  70.2 3.7 %collective-permute-done.6 = bf16[9,1,2,32,256]{4,3,2,1,0:T(8,128)(2,1)S(1)} collective-permute-done((bf16[9,1,2,32,256]{4,3,2,1,0:T(8,128)(2,1)S(1)}, bf16[9,1,2,32,256]{4,3,2,1,0:T(8,128)(2,1)S(1)}, u32[]{:S(2)}, u32[]{:S(2)}) %collective-permute-start.6) | collective-permute-done | bytes 294944 | tf_op jit(solution)/shard_map/ppermute | solution.py:28
  74.7 1.3 collective-permute-start.8
  76.0 4.0 %collective-permute-start.9 = (bf16[1,10,32,256]{3,2,1,0:T(8,128)(2,1)S(1)}, bf16[1,10,32,256]{3,2,1,0:T(8,128)(2,1)S(1)}, u32[]{:S(2)}, u32[]{:S(2)}) collective-permute-start(bf16[1,10,32,256]{3,2,1,0:T(8,128)(2,1)S(1)} %fusion.77), channel_id=1, source_target_pairs={{0,64},{64,128},{128,192},{192,256},{256,320},{320,384},{384,448},... | collective-permute-start | bytes 491528 | tf_op jit(solution)/shard_map/ppermute | solution.py:17
  80.7 1.5 collective-permute-done.9
  83.6 1.3 collective-permute-start.10
  84.9 4.4 %collective-permute-start.11 = (bf16[1,8,32,256]{3,2,1,0:T(8,128)(2,1)S(1)}, bf16[1,8,32,256]{3,2,1,0:T(8,128)(2,1)S(1)}, u32[]{:S(2)}, u32[]{:S(2)}) collective-permute-start(bf16[1,8,32,256]{3,2,1,0:T(8,128)(2,1)S(1)} %get-tuple-element.5), channel_id=1, source_target_pairs={{0,64},{64,128},{128,192},{192,256},{256,320},{320,384},{384,448},... | collective-permute-start | bytes 393224 | tf_op jit(solution)/shard_map/ppermute | solution.py:17
  89.7 1.5 collective-permute-done.11
  92.5 1.3 collective-permute-start.12
  93.8 4.4 %collective-permute-start.13 = (bf16[1,6,32,256]{3,2,1,0:T(8,128)(2,1)S(1)}, bf16[1,6,32,256]{3,2,1,0:T(8,128)(2,1)S(1)}, u32[]{:S(2)}, u32[]{:S(2)}) collective-permute-start(bf16[1,6,32,256]{3,2,1,0:T(8,128)(2,1)S(1)} %get-tuple-element.62), channel_id=1, source_target_pairs={{0,64},{64,128},{128,192},{192,256},{256,320},{320,384},{384,448},... | collective-permute-start | bytes 294920 | tf_op jit(solution)/shard_map/ppermute | solution.py:17
  98.3 1.6 collective-permute-done.13
  100.9 1.3 collective-permute-start.14
  102.2 4.4 %collective-permute-start.15 = (bf16[1,4,32,256]{3,2,1,0:T(8,128)(2,1)S(1)}, bf16[1,4,32,256]{3,2,1,0:T(8,128)(2,1)S(1)}, u32[]{:S(2)}, u32[]{:S(2)}) collective-permute-start(bf16[1,4,32,256]{3,2,1,0:T(8,128)(2,1)S(1)} %get-tuple-element.64), channel_id=1, source_target_pairs={{0,64},{64,128},{128,192},{192,256},{256,320},{320,384},{384,448},... | collective-permute-start | bytes 196616 | tf_op jit(solution)/shard_map/ppermute | solution.py:17
  109.0 5.3 %collective-permute-start.16 = (bf16[1,2,32,256]{3,2,1,0:T(8,128)(2,1)S(1)}, bf16[1,2,32,256]{3,2,1,0:T(8,128)(2,1)S(1)}, u32[]{:S(2)}, u32[]{:S(2)}) collective-permute-start(bf16[1,2,32,256]{3,2,1,0:T(8,128)(2,1)S(1)} %fusion.39), channel_id=1, source_target_pairs={{0,2},{1,3},{2,4},{3,5},{4,6},{5,7},{6,8},{7,9},{8,10},{9,11},{10,... | collective-permute-start | bytes 98312 | tf_op jit(solution)/shard_map/ppermute | solution.py:28
  114.3 6.1 %collective-permute-start.17 = (bf16[1,2,32,256]{3,2,1,0:T(8,128)(2,1)S(1)}, bf16[1,2,32,256]{3,2,1,0:T(8,128)(2,1)S(1)}, u32[]{:S(2)}, u32[]{:S(2)}) collective-permute-start(bf16[1,2,32,256]{3,2,1,0:T(8,128)(2,1)S(1)} %fusion.39), channel_id=1, source_target_pairs={{0,1},{1,2},{2,3},{3,4},{4,5},{5,6},{6,7},{7,8},{8,9},{9,10},{10,1... | collective-permute-start | bytes 98312 | tf_op jit(solution)/shard_map/ppermute | solution.py:28
  120.4 1.9 collective-permute-start.18
  122.4 1.3 collective-permute-start.19
  123.7 1.9 collective-permute-done.18
  125.7 1.3 collective-permute-done.19
  127.1 1.3 collective-permute-start.20
  128.4 4.6 %collective-permute-start.21 = (bf16[1,10,32,256]{3,2,1,0:T(8,128)(2,1)S(1)}, bf16[1,10,32,256]{3,2,1,0:T(8,128)(2,1)S(1)}, u32[]{:S(2)}, u32[]{:S(2)}) collective-permute-start(bf16[1,10,32,256]{3,2,1,0:T(8,128)(2,1)S(1)} %fusion.78), channel_id=1, source_target_pairs={{0,64},{64,128},{128,192},{192,256},{256,320},{320,384},{384,448},... | collective-permute-start | bytes 491528 | tf_op jit(solution)/shard_map/ppermute | solution.py:17
  134.3 0.9 collective-permute-done.21
  136.2 1.0 fusion.94
  137.3 1.3 collective-permute-start.22
  138.6 5.4 %collective-permute-start.23 = (bf16[1,8,32,256]{3,2,1,0:T(8,128)(2,1)}, bf16[1,8,32,256]{3,2,1,0:T(8,128)(2,1)}, u32[]{:S(2)}, u32[]{:S(2)}) collective-permute-start(bf16[1,8,32,256]{3,2,1,0:T(8,128)(2,1)} %get-tuple-element.3), channel_id=1, source_target_pairs={{0,64},{64,128},{128,192},{192,256},{256,320},{320,384},{384,448},... | collective-permute-start | bytes 393224 | tf_op jit(solution)/shard_map/ppermute | solution.py:17
  145.6 1.3 fusion.28
  147.9 1.3 collective-permute-start.24
  149.2 5.1 %collective-permute-start.25 = (bf16[1,6,32,256]{3,2,1,0:T(8,128)(2,1)S(1)}, bf16[1,6,32,256]{3,2,1,0:T(8,128)(2,1)S(1)}, u32[]{:S(2)}, u32[]{:S(2)}) collective-permute-start(bf16[1,6,32,256]{3,2,1,0:T(8,128)(2,1)S(1)} %get-tuple-element.66), channel_id=1, source_target_pairs={{0,64},{64,128},{128,192},{192,256},{256,320},{320,384},{384,448},... | collective-permute-start | bytes 294920 | tf_op jit(solution)/shard_map/ppermute | solution.py:17
  157.1 1.5 collective-permute-start.26
  158.6 5.8 %collective-permute-start.27 = (bf16[1,4,32,256]{3,2,1,0:T(8,128)(2,1)S(1)}, bf16[1,4,32,256]{3,2,1,0:T(8,128)(2,1)S(1)}, u32[]{:S(2)}, u32[]{:S(2)}) collective-permute-start(bf16[1,4,32,256]{3,2,1,0:T(8,128)(2,1)S(1)} %get-tuple-element.68), channel_id=1, source_target_pairs={{0,64},{64,128},{128,192},{192,256},{256,320},{320,384},{384,448},... | collective-permute-start | bytes 196616 | tf_op jit(solution)/shard_map/ppermute | solution.py:17
  166.8 1.4 all_to_all.17
  168.2 31.5 %all-to-all-start.1 = ((f32[512,1,256]{2,1,0:T(1,128)}), f32[512,1,256]{2,1,0:T(1,128)S(1)}, u32[]{:S(2)}, u32[]{:S(2)}) async-start(f32[512,1,256]{2,1,0:T(1,128)} %all_to_all.17), calls=%async_computation.1 | async-start | bytes 1048576 | tf_op jit(solution)/shard_map/all_to_all | solution.py:223
  200.0 22.4 %all-to-all-done.1 = f32[512,1,256]{2,1,0:T(1,128)S(1)} async-done(((f32[512,1,256]{2,1,0:T(1,128)}), f32[512,1,256]{2,1,0:T(1,128)S(1)}, u32[]{:S(2)}, u32[]{:S(2)}) %all-to-all-start.1) | async-done | bytes 524320 | tf_op jit(solution)/shard_map/all_to_all | solution.py:223
  223.7 4.2 %all-to-all-start.2 = ((f32[64,1,256]{2,1,0:T(1,128)}), f32[64,1,256]{2,1,0:T(1,128)S(1)}, u32[]{:S(2)}, u32[]{:S(2)}) async-start(f32[64,1,256]{2,1,0:T(1,128)} %broadcast_in_dim.22), calls=%async_computation.2 | async-start | bytes 131072 | tf_op jit(solution)/shard_map/all_to_all | solution.py:224
  228.7 9.0 %all-to-all-done.2 = f32[64,1,256]{2,1,0:T(1,128)S(1)} async-done(((f32[64,1,256]{2,1,0:T(1,128)}), f32[64,1,256]{2,1,0:T(1,128)S(1)}, u32[]{:S(2)}, u32[]{:S(2)}) %all-to-all-start.2) | async-done | bytes 65568 | tf_op jit(solution)/shard_map/all_to_all | solution.py:224
  (268 shorter events, 31.2 us)
Async XLA Ops:
  0.6 13.7 %copy-start.18 = (s32[1,12]{1,0:T(1,128)S(1)}, s32[1,12]{1,0:T(1,128)}, u32[]{:S(2)}) copy-start(s32[1,12]{1,0:T(1,128)} %param.9) | copy-start | bytes 148
  3.5 27.3 %all-to-all-start = ((bf16[8,112,256]{2,1,0:T(8,128)(2,1)}), bf16[8,112,256]{2,1,0:T(8,128)(2,1)S(1)}, u32[]{:S(2)}, u32[]{:S(2)}) async-start(bf16[8,112,256]{2,1,0:T(8,128)(2,1)} %pad_maximum_fusion), calls=%async_computation | async-start | bytes 917504 | tf_op jit(solution)/shard_map/all_to_all | solution.py:133
  32.7 6.9 %collective-permute-start = (bf16[8,1,1,32,256]{4,3,2,0,1:T(8,128)(2,1)}, bf16[8,1,1,32,256]{4,3,2,0,1:T(8,128)(2,1)S(1)}, u32[]{:S(2)}, u32[]{:S(2)}) collective-permute-start(bf16[8,1,1,32,256]{4,3,2,0,1:T(8,128)(2,1)} %get-tuple-element.48), channel_id=1, source_target_pairs={{0,1},{1,2},{2,3},{3,4},{4,5},{5,6},{6,7},{7,8},{8,9},{9,10},{10,1... | collective-permute-start | bytes 393224 | tf_op jit(solution)/shard_map/ppermute | solution.py:17
  36.4 6.5 %collective-permute-start.1 = (bf16[8,1,1,32,256]{4,3,2,0,1:T(8,128)(2,1)}, bf16[8,1,1,32,256]{4,3,2,0,1:T(8,128)(2,1)S(1)}, u32[]{:S(2)}, u32[]{:S(2)}) collective-permute-start(bf16[8,1,1,32,256]{4,3,2,0,1:T(8,128)(2,1)} %get-tuple-element.49), channel_id=1, source_target_pairs={{1,0},{2,1},{3,2},{4,3},{5,4},{6,5},{7,6},{8,7},{9,8},{10,9},{11,1... | collective-permute-start | bytes 393224 | tf_op jit(solution)/shard_map/ppermute | solution.py:20
  44.5 5.7 %collective-permute-start.2 = (bf16[8,1,2,32,256]{4,3,2,0,1:T(8,128)(2,1)S(1)}, bf16[8,1,2,32,256]{4,3,2,0,1:T(8,128)(2,1)S(1)}, u32[]{:S(2)}, u32[]{:S(2)}) collective-permute-start(bf16[8,1,2,32,256]{4,3,2,0,1:T(8,128)(2,1)S(1)} %fusion.12), channel_id=1, source_target_pairs={{0,64},{64,128},{128,192},{192,256},{256,320},{320,384},{384,448},... | collective-permute-start | bytes 786440 | tf_op jit(solution)/shard_map/ppermute | solution.py:17
  46.7 7.6 %collective-permute-start.3 = (bf16[8,1,2,32,256]{4,3,2,0,1:T(8,128)(2,1)S(1)}, bf16[8,1,2,32,256]{4,3,2,0,1:T(8,128)(2,1)S(1)}, u32[]{:S(2)}, u32[]{:S(2)}) collective-permute-start(bf16[8,1,2,32,256]{4,3,2,0,1:T(8,128)(2,1)S(1)} %fusion.12), channel_id=1, source_target_pairs={{64,0},{128,64},{192,128},{256,192},{320,256},{384,320},{448,384},... | collective-permute-start | bytes 786440 | tf_op jit(solution)/shard_map/ppermute | solution.py:20
  49.4 5.3 %copy-start.3 = (bf16[1,2,32,256]{3,2,1,0:T(8,128)(2,1)S(1)}, bf16[1,2,32,256]{3,2,1,0:T(8,128)(2,1)}, u32[]{:S(2)}) copy-start(bf16[1,2,32,256]{3,2,1,0:T(8,128)(2,1)} %param.6) | copy-start | bytes 98308
  50.2 57.0 %copy-start.9 = (bf16[8,1,2,32,256]{4,3,2,0,1:T(8,128)(2,1)}, bf16[8,1,2,32,256]{4,3,2,0,1:T(8,128)(2,1)S(1)}, u32[]{:S(2)}) copy-start(bf16[8,1,2,32,256]{4,3,2,0,1:T(8,128)(2,1)S(1)} %collective-permute-done.2) | copy-start | bytes 786436
  54.3 52.9 %copy-start.10 = (bf16[8,1,2,32,256]{4,3,2,0,1:T(8,128)(2,1)}, bf16[8,1,2,32,256]{4,3,2,0,1:T(8,128)(2,1)S(1)}, u32[]{:S(2)}) copy-start(bf16[8,1,2,32,256]{4,3,2,0,1:T(8,128)(2,1)S(1)} %collective-permute-done.3) | copy-start | bytes 786436
  54.7 13.7 %collective-permute-start.4 = (bf16[5,1,2,32,256]{4,3,2,1,0:T(8,128)(2,1)S(1)}, bf16[5,1,2,32,256]{4,3,2,1,0:T(8,128)(2,1)S(1)}, u32[]{:S(2)}, u32[]{:S(2)}) collective-permute-start(bf16[5,1,2,32,256]{4,3,2,1,0:T(8,128)(2,1)S(1)} %pad_maximum_fusion.4), channel_id=1, source_target_pairs={{0,2},{1,3},{2,4},{3,5},{4,6},{5,7},{6,8},{7,9},{8,10},{9,11},{10,... | collective-permute-start | bytes 491528 | tf_op jit(solution)/shard_map/ppermute | solution.py:28
  59.8 8.7 %collective-permute-start.7 = (bf16[5,1,2,32,256]{4,3,2,1,0:T(8,128)(2,1)S(1)}, bf16[5,1,2,32,256]{4,3,2,1,0:T(8,128)(2,1)S(1)}, u32[]{:S(2)}, u32[]{:S(2)}) collective-permute-start(bf16[5,1,2,32,256]{4,3,2,1,0:T(8,128)(2,1)S(1)} %pad_maximum_fusion.4), channel_id=1, source_target_pairs={{2,0},{3,1},{4,2},{5,3},{6,4},{7,5},{8,6},{9,7},{10,8},{11,9},{12,... | collective-permute-start | bytes 491528 | tf_op jit(solution)/shard_map/ppermute | solution.py:28
  61.1 8.4 %collective-permute-start.5 = (bf16[9,1,2,32,256]{4,3,2,1,0:T(8,128)(2,1)S(1)}, bf16[9,1,2,32,256]{4,3,2,1,0:T(8,128)(2,1)S(1)}, u32[]{:S(2)}, u32[]{:S(2)}) collective-permute-start(bf16[9,1,2,32,256]{4,3,2,1,0:T(8,128)(2,1)S(1)} %pad_maximum_fusion.1), channel_id=1, source_target_pairs={{0,1},{1,2},{2,3},{3,4},{4,5},{5,6},{6,7},{7,8},{8,9},{9,10},{10,1... | collective-permute-start | bytes 884744 | tf_op jit(solution)/shard_map/ppermute | solution.py:28
  65.9 8.0 %collective-permute-start.6 = (bf16[9,1,2,32,256]{4,3,2,1,0:T(8,128)(2,1)S(1)}, bf16[9,1,2,32,256]{4,3,2,1,0:T(8,128)(2,1)S(1)}, u32[]{:S(2)}, u32[]{:S(2)}) collective-permute-start(bf16[9,1,2,32,256]{4,3,2,1,0:T(8,128)(2,1)S(1)} %pad_maximum_fusion.1), channel_id=1, source_target_pairs={{1,0},{2,1},{3,2},{4,3},{5,4},{6,5},{7,6},{8,7},{9,8},{10,9},{11,1... | collective-permute-start | bytes 884744 | tf_op jit(solution)/shard_map/ppermute | solution.py:28
  74.7 6.1 %collective-permute-start.8 = (bf16[1,10,32,256]{3,2,1,0:T(8,128)(2,1)S(1)}, bf16[1,10,32,256]{3,2,1,0:T(8,128)(2,1)S(1)}, u32[]{:S(2)}, u32[]{:S(2)}) collective-permute-start(bf16[1,10,32,256]{3,2,1,0:T(8,128)(2,1)S(1)} %fusion.77), channel_id=1, source_target_pairs={{64,0},{128,64},{192,128},{256,192},{320,256},{384,320},{448,384},... | collective-permute-start | bytes 491528 | tf_op jit(solution)/shard_map/ppermute | solution.py:20
  76.0 6.2 %collective-permute-start.9 = (bf16[1,10,32,256]{3,2,1,0:T(8,128)(2,1)S(1)}, bf16[1,10,32,256]{3,2,1,0:T(8,128)(2,1)S(1)}, u32[]{:S(2)}, u32[]{:S(2)}) collective-permute-start(bf16[1,10,32,256]{3,2,1,0:T(8,128)(2,1)S(1)} %fusion.77), channel_id=1, source_target_pairs={{0,64},{64,128},{128,192},{192,256},{256,320},{320,384},{384,448},... | collective-permute-start | bytes 491528 | tf_op jit(solution)/shard_map/ppermute | solution.py:17
  83.6 6.2 %collective-permute-start.10 = (bf16[1,8,32,256]{3,2,1,0:T(8,128)(2,1)S(1)}, bf16[1,8,32,256]{3,2,1,0:T(8,128)(2,1)S(1)}, u32[]{:S(2)}, u32[]{:S(2)}) collective-permute-start(bf16[1,8,32,256]{3,2,1,0:T(8,128)(2,1)S(1)} %get-tuple-element.5), channel_id=1, source_target_pairs={{64,0},{128,64},{192,128},{256,192},{320,256},{384,320},{448,384},... | collective-permute-start | bytes 393224 | tf_op jit(solution)/shard_map/ppermute | solution.py:20
  84.9 6.4 %collective-permute-start.11 = (bf16[1,8,32,256]{3,2,1,0:T(8,128)(2,1)S(1)}, bf16[1,8,32,256]{3,2,1,0:T(8,128)(2,1)S(1)}, u32[]{:S(2)}, u32[]{:S(2)}) collective-permute-start(bf16[1,8,32,256]{3,2,1,0:T(8,128)(2,1)S(1)} %get-tuple-element.5), channel_id=1, source_target_pairs={{0,64},{64,128},{128,192},{192,256},{256,320},{320,384},{384,448},... | collective-permute-start | bytes 393224 | tf_op jit(solution)/shard_map/ppermute | solution.py:17
  89.4 3.1 %copy-start = (bf16[2,1,2,288,256]{4,3,2,0,1:T(8,128)(2,1)}, bf16[2,1,2,288,256]{4,3,2,0,1:T(8,128)(2,1)S(1)}, u32[]{:S(2)}) copy-start(bf16[2,1,2,288,256]{4,3,2,0,1:T(8,128)(2,1)S(1)} %constant_dynamic-update-slice_fusion.83) | copy-start | bytes 1769476
  92.5 5.8 %collective-permute-start.12 = (bf16[1,6,32,256]{3,2,1,0:T(8,128)(2,1)S(1)}, bf16[1,6,32,256]{3,2,1,0:T(8,128)(2,1)S(1)}, u32[]{:S(2)}, u32[]{:S(2)}) collective-permute-start(bf16[1,6,32,256]{3,2,1,0:T(8,128)(2,1)S(1)} %get-tuple-element.62), channel_id=1, source_target_pairs={{64,0},{128,64},{192,128},{256,192},{320,256},{384,320},{448,384},... | collective-permute-start | bytes 294920 | tf_op jit(solution)/shard_map/ppermute | solution.py:20
  93.8 6.0 %collective-permute-start.13 = (bf16[1,6,32,256]{3,2,1,0:T(8,128)(2,1)S(1)}, bf16[1,6,32,256]{3,2,1,0:T(8,128)(2,1)S(1)}, u32[]{:S(2)}, u32[]{:S(2)}) collective-permute-start(bf16[1,6,32,256]{3,2,1,0:T(8,128)(2,1)S(1)} %get-tuple-element.62), channel_id=1, source_target_pairs={{0,64},{64,128},{128,192},{192,256},{256,320},{320,384},{384,448},... | collective-permute-start | bytes 294920 | tf_op jit(solution)/shard_map/ppermute | solution.py:17
  100.9 6.3 %collective-permute-start.14 = (bf16[1,4,32,256]{3,2,1,0:T(8,128)(2,1)S(1)}, bf16[1,4,32,256]{3,2,1,0:T(8,128)(2,1)S(1)}, u32[]{:S(2)}, u32[]{:S(2)}) collective-permute-start(bf16[1,4,32,256]{3,2,1,0:T(8,128)(2,1)S(1)} %get-tuple-element.64), channel_id=1, source_target_pairs={{64,0},{128,64},{192,128},{256,192},{320,256},{384,320},{448,384},... | collective-permute-start | bytes 196616 | tf_op jit(solution)/shard_map/ppermute | solution.py:20
  102.2 5.9 %collective-permute-start.15 = (bf16[1,4,32,256]{3,2,1,0:T(8,128)(2,1)S(1)}, bf16[1,4,32,256]{3,2,1,0:T(8,128)(2,1)S(1)}, u32[]{:S(2)}, u32[]{:S(2)}) collective-permute-start(bf16[1,4,32,256]{3,2,1,0:T(8,128)(2,1)S(1)} %get-tuple-element.64), channel_id=1, source_target_pairs={{0,64},{64,128},{128,192},{192,256},{256,320},{320,384},{384,448},... | collective-permute-start | bytes 196616 | tf_op jit(solution)/shard_map/ppermute | solution.py:17
  109.0 14.6 %collective-permute-start.16 = (bf16[1,2,32,256]{3,2,1,0:T(8,128)(2,1)S(1)}, bf16[1,2,32,256]{3,2,1,0:T(8,128)(2,1)S(1)}, u32[]{:S(2)}, u32[]{:S(2)}) collective-permute-start(bf16[1,2,32,256]{3,2,1,0:T(8,128)(2,1)S(1)} %fusion.39), channel_id=1, source_target_pairs={{0,2},{1,3},{2,4},{3,5},{4,6},{5,7},{6,8},{7,9},{8,10},{9,11},{10,... | collective-permute-start | bytes 98312 | tf_op jit(solution)/shard_map/ppermute | solution.py:28
  114.3 9.4 %collective-permute-start.17 = (bf16[1,2,32,256]{3,2,1,0:T(8,128)(2,1)S(1)}, bf16[1,2,32,256]{3,2,1,0:T(8,128)(2,1)S(1)}, u32[]{:S(2)}, u32[]{:S(2)}) collective-permute-start(bf16[1,2,32,256]{3,2,1,0:T(8,128)(2,1)S(1)} %fusion.39), channel_id=1, source_target_pairs={{0,1},{1,2},{2,3},{3,4},{4,5},{5,6},{6,7},{7,8},{8,9},{9,10},{10,1... | collective-permute-start | bytes 98312 | tf_op jit(solution)/shard_map/ppermute | solution.py:28
  120.4 5.2 %collective-permute-start.18 = (bf16[1,2,32,256]{3,2,1,0:T(8,128)(2,1)S(1)}, bf16[1,2,32,256]{3,2,1,0:T(8,128)(2,1)S(1)}, u32[]{:S(2)}, u32[]{:S(2)}) collective-permute-start(bf16[1,2,32,256]{3,2,1,0:T(8,128)(2,1)S(1)} %fusion.39), channel_id=1, source_target_pairs={{1,0},{2,1},{3,2},{4,3},{5,4},{6,5},{7,6},{8,7},{9,8},{10,9},{11,1... | collective-permute-start | bytes 98312 | tf_op jit(solution)/shard_map/ppermute | solution.py:28
  122.4 4.7 %collective-permute-start.19 = (bf16[1,2,32,256]{3,2,1,0:T(8,128)(2,1)S(1)}, bf16[1,2,32,256]{3,2,1,0:T(8,128)(2,1)S(1)}, u32[]{:S(2)}, u32[]{:S(2)}) collective-permute-start(bf16[1,2,32,256]{3,2,1,0:T(8,128)(2,1)S(1)} %fusion.39), channel_id=1, source_target_pairs={{2,0},{3,1},{4,2},{5,3},{6,4},{7,5},{8,6},{9,7},{10,8},{11,9},{12,... | collective-permute-start | bytes 98312 | tf_op jit(solution)/shard_map/ppermute | solution.py:28
  127.1 7.2 %collective-permute-start.20 = (bf16[1,10,32,256]{3,2,1,0:T(8,128)(2,1)S(1)}, bf16[1,10,32,256]{3,2,1,0:T(8,128)(2,1)S(1)}, u32[]{:S(2)}, u32[]{:S(2)}) collective-permute-start(bf16[1,10,32,256]{3,2,1,0:T(8,128)(2,1)S(1)} %fusion.78), channel_id=1, source_target_pairs={{64,0},{128,64},{192,128},{256,192},{320,256},{384,320},{448,384},... | collective-permute-start | bytes 491528 | tf_op jit(solution)/shard_map/ppermute | solution.py:20
  128.4 6.9 %collective-permute-start.21 = (bf16[1,10,32,256]{3,2,1,0:T(8,128)(2,1)S(1)}, bf16[1,10,32,256]{3,2,1,0:T(8,128)(2,1)S(1)}, u32[]{:S(2)}, u32[]{:S(2)}) collective-permute-start(bf16[1,10,32,256]{3,2,1,0:T(8,128)(2,1)S(1)} %fusion.78), channel_id=1, source_target_pairs={{0,64},{64,128},{128,192},{192,256},{256,320},{320,384},{384,448},... | collective-permute-start | bytes 491528 | tf_op jit(solution)/shard_map/ppermute | solution.py:17
  136.0 8.8 %slice-start.1 = ((bf16[8,1,2,32,256]{4,3,2,0,1:T(8,128)(2,1)}), bf16[6,1,2,32,256]{4,3,2,0,1:T(8,128)(2,1)S(1)}, s32[]{:S(2)}) async-start(bf16[8,1,2,32,256]{4,3,2,0,1:T(8,128)(2,1)} %copy-done.9), calls=%async_computation.4 | async-start | bytes 393216 | tf_op jit(solution)/shard_map/slice | solution.py:209
  136.0 8.8 %slice-start.3 = ((bf16[8,1,2,32,256]{4,3,2,0,1:T(8,128)(2,1)}), bf16[6,1,2,32,256]{4,3,2,0,1:T(8,128)(2,1)S(1)}, s32[]{:S(2)}) async-start(bf16[8,1,2,32,256]{4,3,2,0,1:T(8,128)(2,1)} %copy-done.10), calls=%async_computation.6 | async-start | bytes 393216 | tf_op jit(solution)/shard_map/slice | solution.py:209
  137.3 8.3 %collective-permute-start.22 = (bf16[1,8,32,256]{3,2,1,0:T(8,128)(2,1)}, bf16[1,8,32,256]{3,2,1,0:T(8,128)(2,1)}, u32[]{:S(2)}, u32[]{:S(2)}) collective-permute-start(bf16[1,8,32,256]{3,2,1,0:T(8,128)(2,1)} %get-tuple-element.3), channel_id=1, source_target_pairs={{64,0},{128,64},{192,128},{256,192},{320,256},{384,320},{448,384},... | collective-permute-start | bytes 393224 | tf_op jit(solution)/shard_map/ppermute | solution.py:20
  138.6 7.0 %collective-permute-start.23 = (bf16[1,8,32,256]{3,2,1,0:T(8,128)(2,1)}, bf16[1,8,32,256]{3,2,1,0:T(8,128)(2,1)}, u32[]{:S(2)}, u32[]{:S(2)}) collective-permute-start(bf16[1,8,32,256]{3,2,1,0:T(8,128)(2,1)} %get-tuple-element.3), channel_id=1, source_target_pairs={{0,64},{64,128},{128,192},{192,256},{256,320},{320,384},{384,448},... | collective-permute-start | bytes 393224 | tf_op jit(solution)/shard_map/ppermute | solution.py:17
  145.4 2.2 copy-start.6
  145.4 2.2 copy-start.7
  145.4 2.2 copy-start.8
  147.9 7.9 %collective-permute-start.24 = (bf16[1,6,32,256]{3,2,1,0:T(8,128)(2,1)S(1)}, bf16[1,6,32,256]{3,2,1,0:T(8,128)(2,1)S(1)}, u32[]{:S(2)}, u32[]{:S(2)}) collective-permute-start(bf16[1,6,32,256]{3,2,1,0:T(8,128)(2,1)S(1)} %get-tuple-element.66), channel_id=1, source_target_pairs={{64,0},{128,64},{192,128},{256,192},{320,256},{384,320},{448,384},... | collective-permute-start | bytes 294920 | tf_op jit(solution)/shard_map/ppermute | solution.py:20
  149.2 6.7 %collective-permute-start.25 = (bf16[1,6,32,256]{3,2,1,0:T(8,128)(2,1)S(1)}, bf16[1,6,32,256]{3,2,1,0:T(8,128)(2,1)S(1)}, u32[]{:S(2)}, u32[]{:S(2)}) collective-permute-start(bf16[1,6,32,256]{3,2,1,0:T(8,128)(2,1)S(1)} %get-tuple-element.66), channel_id=1, source_target_pairs={{0,64},{64,128},{128,192},{192,256},{256,320},{320,384},{384,448},... | collective-permute-start | bytes 294920 | tf_op jit(solution)/shard_map/ppermute | solution.py:17
  155.3 1.5 copy-start.4
  155.9 8.5 %slice-start = ((bf16[8,1,2,32,256]{4,3,2,0,1:T(8,128)(2,1)}), bf16[2,1,2,32,256]{4,3,2,0,1:T(8,128)(2,1)S(1)}, s32[]{:S(2)}) async-start(bf16[8,1,2,32,256]{4,3,2,0,1:T(8,128)(2,1)} %copy-done.9), calls=%async_computation.3 | async-start | bytes 131072 | tf_op jit(solution)/shard_map/slice | solution.py:209
  155.9 8.5 %slice-start.2 = ((bf16[8,1,2,32,256]{4,3,2,0,1:T(8,128)(2,1)}), bf16[2,1,2,32,256]{4,3,2,0,1:T(8,128)(2,1)S(1)}, s32[]{:S(2)}) async-start(bf16[8,1,2,32,256]{4,3,2,0,1:T(8,128)(2,1)} %copy-done.10), calls=%async_computation.5 | async-start | bytes 131072 | tf_op jit(solution)/shard_map/slice | solution.py:209
  155.9 8.5 %copy-start.14 = (bf16[2,1,2,32,256]{4,3,2,0,1:T(8,128)(2,1)S(1)}, bf16[2,1,2,32,256]{4,3,2,0,1:T(8,128)(2,1)}, u32[]{:S(2)}) copy-start(bf16[2,1,2,32,256]{4,3,2,0,1:T(8,128)(2,1)} %slice.1048) | copy-start | bytes 196612
  156.3 9.4 %copy-start.15 = (bf16[1,3,32,32]{3,2,1,0:T(8,128)(2,1)S(1)}, bf16[1,3,32,32]{3,2,1,0:T(8,128)(2,1)}, u32[]{:S(2)}) copy-start(bf16[1,3,32,32]{3,2,1,0:T(8,128)(2,1)} %get-tuple-element.8) | copy-start | bytes 18436
  156.7 9.4 %copy-start.1 = (bf16[2,1,2,288,256]{4,3,2,0,1:T(8,128)(2,1)S(1)}, bf16[2,1,2,288,256]{4,3,2,0,1:T(8,128)(2,1)}, u32[]{:S(2)}) copy-start(bf16[2,1,2,288,256]{4,3,2,0,1:T(8,128)(2,1)} %copy-done) | copy-start | bytes 1769476
  157.1 7.8 %collective-permute-start.26 = (bf16[1,4,32,256]{3,2,1,0:T(8,128)(2,1)S(1)}, bf16[1,4,32,256]{3,2,1,0:T(8,128)(2,1)S(1)}, u32[]{:S(2)}, u32[]{:S(2)}) collective-permute-start(bf16[1,4,32,256]{3,2,1,0:T(8,128)(2,1)S(1)} %get-tuple-element.68), channel_id=1, source_target_pairs={{64,0},{128,64},{192,128},{256,192},{320,256},{384,320},{448,384},... | collective-permute-start | bytes 196616 | tf_op jit(solution)/shard_map/ppermute | solution.py:20
  158.6 7.1 %collective-permute-start.27 = (bf16[1,4,32,256]{3,2,1,0:T(8,128)(2,1)S(1)}, bf16[1,4,32,256]{3,2,1,0:T(8,128)(2,1)S(1)}, u32[]{:S(2)}, u32[]{:S(2)}) collective-permute-start(bf16[1,4,32,256]{3,2,1,0:T(8,128)(2,1)S(1)} %get-tuple-element.68), channel_id=1, source_target_pairs={{0,64},{64,128},{128,192},{192,256},{256,320},{320,384},{384,448},... | collective-permute-start | bytes 196616 | tf_op jit(solution)/shard_map/ppermute | solution.py:17
  166.8 61.1 %copy-start.2 = (bf16[1,9,32,32]{3,2,1,0:T(8,128)(2,1)S(1)}, bf16[1,9,32,32]{3,2,1,0:T(8,128)(2,1)}, u32[]{:S(2)}) copy-start(bf16[1,9,32,32]{3,2,1,0:T(8,128)(2,1)} %get-tuple-element.16) | copy-start | bytes 55300
  168.2 54.2 %all-to-all-start.1 = ((f32[512,1,256]{2,1,0:T(1,128)}), f32[512,1,256]{2,1,0:T(1,128)S(1)}, u32[]{:S(2)}, u32[]{:S(2)}) async-start(f32[512,1,256]{2,1,0:T(1,128)} %all_to_all.17), calls=%async_computation.1 | async-start | bytes 1048576 | tf_op jit(solution)/shard_map/all_to_all | solution.py:223
  223.7 14.0 %all-to-all-start.2 = ((f32[64,1,256]{2,1,0:T(1,128)}), f32[64,1,256]{2,1,0:T(1,128)S(1)}, u32[]{:S(2)}, u32[]{:S(2)}) async-start(f32[64,1,256]{2,1,0:T(1,128)} %broadcast_in_dim.22), calls=%async_computation.2 | async-start | bytes 131072 | tf_op jit(solution)/shard_map/all_to_all | solution.py:224
  (6 other events, 7.2 us)
